TPU v7x, 32 devices: a whole 2x2x4 slice. The times are simulated.
32 devices in a mesh: dp: 8 (over y, x, core), fsdp: 4 (over z).
Axes of the slice: x: 2, y: 2, z: 4, core: 2. Of those that a mesh axis runs over, the one named last changes fastest.
Arguments:
- query_cache: bfloat16 [384, 1024], P('dp', 'fsdp'), may hold values from -8 to 8
- region_cache: bfloat16 [384, 1024], P('dp', 'fsdp'), may hold values from -8 to 8
- positive: int32 [384], P('dp'), may hold values from 0 to 383, each once
- hidden_states: bfloat16 [4096, 4096], P(('dp', 'fsdp')), may hold values from -12 to 12
- segment_ids: int32 [8, 512], P('dp', 'fsdp'), may hold values from 0 to 47, never falling along the last dimension, each value on 1 to 21 neighbouring positions
- norm_gain: bfloat16 [4096], replicated, may hold values from 0.099609375 to 1.8984375
- proj_weight: bfloat16 [4096, 1024], P('fsdp'), may hold values from -1 to 1
Outputs:
- mean_loss: float32 [], replicated
- query_grad: float32 [384, 1024], P('dp', 'fsdp')
- region_grad: float32 [384, 1024], P('dp', 'fsdp')
- hidden_grad: bfloat16 [4096, 4096], P(('dp', 'fsdp'))
- gain_grad: float32 [4096], replicated
- proj_grad: float32 [4096, 1024], P('dp', 'fsdp')
Inputs may be any that keep to these rules, and one draw needn't show every extreme that they name: Each region is the positive of exactly one instruction. `segment_ids`: within a pair group the ids never fall, every instruction has at least one token, and one has exactly 21.
All inputs are finite; a program needn't handle non-finite values.
Results may differ from a plain program's by a relative error of at most 0.0088.
Values may be sent and summed in bfloat16 or wider, within the bound.
No kernel may reach another device: no remote copies, remote signals or barrier semaphores. Data moves between devices by JAX's collectives and lax.ppermute only.
A program may use at most 64 MiB of HBM per device.

v0:
```python
import jax
import jax.numpy as jnp
from jax import lax
from jax.sharding import PartitionSpec as P

E = 1024


EPS = 1e-05


def local(query_cache, region_cache, positive, hidden_states, segment_ids, norm_gain, proj_weight):
    row_count = query_cache.shape[0]
    data_count = lax.axis_size("dp")
    pair_count = row_count * data_count
    logit_scale = float(E) ** (-0.5)
    contract_last = (((1,), (1,)), ((), ()))
    contract_first = (((0,), (0,)), ((), ()))
    region_all, query_all = (
        lax.all_gather(region_cache, "dp", axis=0, tiled=True),
        lax.all_gather(query_cache, "dp", axis=0, tiled=True),
    )
    partial_value = lax.dot_general(
        query_cache, region_all, contract_last, preferred_element_type=jnp.float32
    )
    scores = lax.psum(partial_value, "fsdp") * logit_scale
    row_max = jnp.max(scores, axis=1, keepdims=True)
    log_total = row_max[:, 0] + jnp.log(jnp.sum(jnp.exp(scores - row_max), axis=1))
    columns = lax.broadcasted_iota(jnp.int32, (1, pair_count), 1)
    matched = columns == positive[:, None]
    target_score = jnp.sum(jnp.where(matched, scores, jnp.zeros_like(scores)), axis=1)
    loss_local = jnp.sum(log_total - target_score)
    grad_probs = (jnp.exp(scores - log_total[:, None]) - matched.astype(jnp.float32)).astype(
        jnp.bfloat16
    )
    query_grad = logit_scale * jnp.dot(grad_probs, region_all, preferred_element_type=jnp.float32)
    totals_all, targets_all = (
        lax.all_gather(log_total, "dp", axis=0, tiled=True),
        lax.all_gather(positive.astype(jnp.float32), "dp", axis=0, tiled=True),
    )
    partial_t = lax.dot_general(
        region_cache, query_all, contract_last, preferred_element_type=jnp.float32
    )
    scores_t = lax.psum(partial_t, "fsdp") * logit_scale
    own_rows = (
        lax.axis_index("dp") * row_count + lax.broadcasted_iota(jnp.int32, (row_count, 1), 0)
    ).astype(jnp.float32)
    matched_t = targets_all[None, :] == own_rows
    probs_t = (jnp.exp(scores_t - totals_all[None, :]) - matched_t.astype(jnp.float32)).astype(
        jnp.bfloat16
    )
    region_grad = logit_scale * jnp.dot(probs_t, query_all, preferred_element_type=jnp.float32)
    gain = norm_gain.astype(jnp.float32)
    states = hidden_states.astype(jnp.float32)
    inv_rms = lax.rsqrt(jnp.mean(states * states, axis=1, keepdims=True) + EPS)
    normed = (states * inv_rms * gain).astype(jnp.bfloat16)
    labels = lax.broadcasted_iota(jnp.int32, (row_count, 1), 0)
    member = segment_ids[0][None, :] == labels
    pooled_part = jnp.dot(member.astype(jnp.bfloat16), normed, preferred_element_type=jnp.float32)
    counts_part = jnp.sum(member.astype(jnp.float32), axis=1)
    pooled, counts = lax.psum((pooled_part, counts_part), "fsdp")
    mean_pooled = (pooled / counts[:, None]).astype(jnp.bfloat16)
    grad_low = query_grad.astype(jnp.bfloat16)
    grad_full = lax.all_gather(grad_low, "fsdp", axis=1, tiled=True)
    mean_part = lax.dot_general(
        grad_full, proj_weight, contract_last, preferred_element_type=jnp.float32
    )
    mean_grad = lax.all_gather(mean_part, "fsdp", axis=1, tiled=True)
    pool_grad = mean_grad / counts[:, None]
    normed_grad = lax.dot_general(
        member.astype(jnp.float32),
        pool_grad,
        contract_first,
        precision=lax.Precision.HIGHEST,
        preferred_element_type=jnp.float32,
    )
    gain_part = jnp.sum(normed_grad * states * inv_rms, axis=0)
    scaled = gain * normed_grad
    inner = jnp.mean(scaled * states, axis=1, keepdims=True)
    hidden_grad = (inv_rms * scaled - states * inv_rms**3 * inner).astype(jnp.bfloat16)
    proj_grad = lax.psum_scatter(
        lax.dot_general(mean_pooled, grad_low, contract_first, preferred_element_type=jnp.float32),
        "dp",
        scatter_dimension=0,
        tiled=True,
    )
    loss_total = lax.psum(loss_local, "dp")
    gain_grad = lax.psum(gain_part, ("dp", "fsdp"))
    mean_loss = loss_total / pair_count
    return (mean_loss, query_grad, region_grad, hidden_grad, gain_grad, proj_grad)


def solution(mesh):
    in_specs = (
        P("dp", "fsdp"),
        P("dp", "fsdp"),
        P("dp"),
        P(("dp", "fsdp"), None),
        P("dp", "fsdp"),
        P(),
        P("fsdp", None),
    )
    out_specs = (
        P(),
        P("dp", "fsdp"),
        P("dp", "fsdp"),
        P(("dp", "fsdp"), None),
        P(),
        P("dp", "fsdp"),
    )
    return jax.shard_map(local, mesh=mesh, in_specs=in_specs, out_specs=out_specs, check_vma=False)
```

profile of v0, /device:TPU:0, one launch (start us, length us, event | category | flops | bytes accessed | tf_op | source)
XLA Modules:
  0.0 194.3 jit_solution(16001850921238040908)
XLA Ops:
  7.2 0.0 copy-start
  7.2 0.0 copy-start.1
  7.2 0.0 all-reduce.6.cloned.1.call-start
  7.2 0.0 copy-start.15
  7.2 1.7 fusion
  8.9 0.6 multiply_multiply_fusion
  9.5 0.7 convert_element_type.53
  10.2 10.9 %all_gather.19 = bf16[384,256]{1,0:T(8,128)(2,1)S(1)} all-gather(bf16[48,256]{1,0:T(8,128)(2,1)} %param.7), channel_id=1, replica_groups=mesh['dp'=8,'fsdp'=4] {'dp'}, dimensions={0}, use_global_device_ids=true | all-gather | bytes 221184 | tf_op jit(solution)/shard_map/all_gather | solution.py:21
  21.1 9.0 %all_gather.18 = bf16[384,256]{1,0:T(8,128)(2,1)S(1)} all-gather(bf16[48,256]{1,0:T(8,128)(2,1)} %param.8), channel_id=1, replica_groups=mesh['dp'=8,'fsdp'=4] {'dp'}, dimensions={0}, use_global_device_ids=true | all-gather | bytes 221184 | tf_op jit(solution)/shard_map/all_gather | solution.py:20
  30.2 1.6 fusion.32
  31.7 1.6 fusion.31
  33.3 0.0 copy-done.11
  33.3 0.0 copy-done.1
  33.3 0.0 copy-done.15
  33.3 1.4 fusion.9
  34.7 0.0 all-reduce.6.cloned.1.call-update
  34.7 0.0 reduce-scatter.2.cloned.1.call-start
  34.7 1.2 dynamic-slice
  36.6 1.3 convert_reduce_fusion
  37.9 13.0 %psum.45 = f32[48]{0:T(128)} all-reduce(f32[48]{0:T(128)} %convert_reduce_fusion), channel_id=1, replica_groups=mesh['dp'=8,'fsdp'=4] {'fsdp'}, use_global_device_ids=true, to_apply=%region_9.10 | all-reduce | flops 48 | bytes 384 | tf_op jit(solution)/shard_map/psum | solution.py:61
  51.0 33.7 %all-reduce.6.cloned.1.call-done = (f32[48,384]{1,0:T(8,128)}, f32[48,384]{1,0:T(8,128)}, f32[48,4096]{1,0:T(8,128)}) async-done(((f32[48,384]{1,0:T(8,128)}, f32[48,384]{1,0:T(8,128)}, f32[48,4096]{1,0:T(8,128)}), (f32[48,384]{1,0:T(8,128)}, f32[48,384]{1,0:T(8,128)}, f32[48,4096]{1,0:T(8,128)})) %all-reduce.6.cloned.1.call-update) | async-done | bytes 933904 | tf_op jit(solution)/shard_map/psum | solution.py:26
  84.6 1.0 multiply_reduce_fusion
  85.6 1.6 select_reduce_fusion
  87.2 0.1 fusion.29
  87.3 1.7 fusion.30
  89.0 0.0 copy-done.5
  89.0 0.0 copy-done.8
  89.1 0.6 copy-done.2
  89.7 3.9 %fusion.15 = f32[4096,256]{1,0:T(8,128)} fusion(bf16[48,256]{1,0:T(8,128)(2,1)S(1)} %get-tuple-element.20, f32[48,4096]{1,0:T(8,128)} %get-tuple-element.15, f32[48]{0:T(128)} %psum.45), kind=kOutput, calls=%fused_computation.22 | convolution fusion | flops 101056512 | bytes 5005504 | tf_op jit(solution)/shard_map/dot_general | solution.py:82
  93.6 0.0 copy-start.3
  93.6 0.0 reduce-scatter.2.cloned.1.call-update
  93.6 0.0 copy-start.12
  93.6 0.0 copy-start.13
  93.6 0.0 copy-start.16
  93.7 0.5 copy-done.7
  94.2 0.1 convert_dynamic-update-slice_fusion
  94.3 0.0 copy-done.9
  94.3 0.0 copy-done.14
  94.3 0.6 subtract_reduce_fusion
  94.9 0.0 copy-done.6
  94.9 14.7 %all-reduce.2 = (f32[]{:T(128)}, f32[384]{0:T(512)S(1)}, f32[384]{0:T(512)S(1)}) all-reduce(f32[]{:T(128)} %subtract_reduce_fusion, f32[384]{0:T(512)S(1)} %convert_dynamic-update-slice_fusion, f32[384]{0:T(512)S(1)} %copy-done.6), channel_id=1, replica_groups=mesh['dp'=8,'fsdp'=4] {'dp'}, use_global_device_ids=true, to_apply=%region_5.6 | all-reduce | flops 769 | bytes 6152 | tf_op jit(solution)/shard_map/psum | solution.py:87
  110.2 13.3 %all_gather.22 = bf16[48,1024]{1,0:T(8,128)(2,1)S(1)} all-gather(bf16[48,256]{1,0:T(8,128)(2,1)S(1)} %copy-done.3), channel_id=1, replica_groups=mesh['dp'=8,'fsdp'=4] {'fsdp'}, dimensions={1}, use_global_device_ids=true | all-gather | bytes 122880 | tf_op jit(solution)/shard_map/all_gather | solution.py:64
  123.5 0.7 fusion.33
  124.3 17.2 %all_gather.23 = f32[48,4096]{1,0:T(8,128)S(1)} all-gather(f32[48,1024]{1,0:T(8,128)S(1)} %fusion.33), channel_id=1, replica_groups=mesh['dp'=8,'fsdp'=4] {'fsdp'}, dimensions={1}, use_global_device_ids=true | all-gather | bytes 983040 | tf_op jit(solution)/shard_map/all_gather | solution.py:68
  141.4 2.8 %fusion.6 = (f32[4096]{0:T(1024)S(1)}, f32[128]{0:T(128)S(1)}, f32[128,4096]{1,0:T(8,128)}) fusion(bf16[128,4096]{1,0:T(8,128)(2,1)S(1)} %copy-done.1, f32[128]{0:T(128)S(1)} %copy-done.12, f32[4096]{0:T(1024)S(1)} %convert_element_type.53, f32[48,4096]{1,0:T(8,128)S(1)} %all_gather.23, f32[48]{0:T(128)S(1)} %copy-done.13, s32[128]{0:T(128)S(1)} %bitcast.13), kind=kOutput, calls=%fused_computation.11 | convolution fusion | flops 305858432 | bytes 3966656 | tf_op jit(solution)/shard_map/dot_general | solution.py:70
  144.3 38.1 %psum.46 = f32[4096]{0:T(1024)} all-reduce(f32[4096]{0:T(1024)S(1)} %get-tuple-element.6), channel_id=1, replica_groups=mesh['dp'=8,'fsdp'=4] {'dp','fsdp'}, use_global_device_ids=true, to_apply=%region_12.13 | all-reduce | flops 4096 | bytes 32768 | tf_op jit(solution)/shard_map/psum | solution.py:88
  182.3 0.8 convolution_multiply_fusion
  183.2 3.2 %fusion.3 = bf16[128,4096]{1,0:T(8,128)(2,1)} fusion(bf16[128,4096]{1,0:T(8,128)(2,1)S(1)} %copy-done.1, f32[128,4096]{1,0:T(8,128)} %get-tuple-element.22, f32[128]{0:T(128)S(1)} %broadcast_multiply_fusion, f32[128]{0:T(128)S(1)} %copy-done.10, f32[4096]{0:T(1024)S(1)} %convert_element_type.53, f32[128]{0:T(128)S(1)} %copy-done.12), kind=kLoop, calls=%fused_computation.8 | loop fusion | flops 3670016 | bytes 4212224 | tf_op jit(solution)/shard_map/convert_element_type | solution.py:80
  (22 shorter events, 0.0 us)
Async XLA Ops:
  7.2 116.3 %copy-start = (bf16[1024,1024]{1,0:T(8,128)(2,1)S(1)}, bf16[1024,1024]{1,0:T(8,128)(2,1)}, u32[]{:S(2)}) copy-start(bf16[1024,1024]{1,0:T(8,128)(2,1)} %param.13) | copy-start | bytes 6291460
  7.2 26.1 %copy-start.1 = (bf16[128,4096]{1,0:T(8,128)(2,1)S(1)}, bf16[128,4096]{1,0:T(8,128)(2,1)}, u32[]{:S(2)}) copy-start(bf16[128,4096]{1,0:T(8,128)(2,1)} %param.10) | copy-start | bytes 3145732
  7.2 77.4 %all-reduce.6.cloned.1.call-start = ((), (), s32[]{:S(2)}) async-start(), calls=%async_computation.2 | async-start | bytes 1867776 | tf_op jit(solution)/shard_map/psum | solution.py:26
  7.2 26.1 %copy-start.15 = (s32[1,128]{1,0:T(1,128)S(1)}, s32[1,128]{1,0:T(1,128)}, u32[]{:S(2)}) copy-start(s32[1,128]{1,0:T(1,128)} %param.11) | copy-start | bytes 1540
  9.5 23.8 %copy-start.11 = (f32[128]{0:T(128)}, f32[128]{0:T(128)S(1)}, u32[]{:S(2)}) copy-start(f32[128]{0:T(128)S(1)} %get-tuple-element.19) | copy-start | bytes 1540
  34.7 151.7 %reduce-scatter.2.cloned.1.call-start = ((), (), s32[]{:S(2)}) async-start(), calls=%async_computation.1 | async-start | bytes 4718592 | tf_op jit(solution)/shard_map/reduce_scatter | solution.py:81
  87.3 1.7 copy-start.5
  87.3 1.7 copy-start.8
  89.0 0.6 copy-start.2
  93.6 0.7 copy-start.7
  93.6 0.7 copy-start.9
  93.6 0.7 copy-start.14
  93.6 1.3 copy-start.6
  93.6 16.7 %copy-start.3 = (bf16[48,256]{1,0:T(8,128)(2,1)S(1)}, bf16[48,256]{1,0:T(8,128)(2,1)}, u32[]{:S(2)}) copy-start(bf16[48,256]{1,0:T(8,128)(2,1)} %copy-done.2) | copy-start | bytes 73732
  93.6 47.8 %copy-start.12 = (f32[128]{0:T(128)S(1)}, f32[128]{0:T(128)}, u32[]{:S(2)}) copy-start(f32[128]{0:T(128)} %copy-done.11) | copy-start | bytes 1540
  93.6 47.8 %copy-start.13 = (f32[48]{0:T(128)S(1)}, f32[48]{0:T(128)}, u32[]{:S(2)}) copy-start(f32[48]{0:T(128)} %psum.45) | copy-start | bytes 580
  93.6 47.8 %copy-start.16 = (s32[1,128]{1,0:T(1,128)S(1)}, s32[1,128]{1,0:T(1,128)}, u32[]{:S(2)}) copy-start(s32[1,128]{1,0:T(1,128)} %param.11) | copy-start | bytes 1540
  141.4 40.9 %copy-start.4 = (f32[48,384]{1,0:T(8,128)S(1)}, f32[48,384]{1,0:T(8,128)}, u32[]{:S(2)}) copy-start(f32[48,384]{1,0:T(8,128)} %get-tuple-element.14) | copy-start | bytes 221188
  141.4 41.7 %copy-start.10 = (f32[128]{0:T(128)S(1)}, f32[128]{0:T(128)}, u32[]{:S(2)}) copy-start(f32[128]{0:T(128)} %get-tuple-element.18) | copy-start | bytes 1540
Sparse Core Ops, SparseCore 0:
  34.8 49.7 all-reduce.5
  93.7 50.6 reduce-scatter.1
where the time goes:
time: 195 us; the launch traced here: 194 us
  blocking collectives  116 us (59%)
  waiting for transfers between devices  33.7 us (17%)
  between operations  16.6 us (9%)
  matrix products  14.5 us (7%)
  other arithmetic  10.8 us (6%)
  local copies, waits for them, and re-layouts  2.47 us (1%)
    psum x1, blocking collectives, local(): gain_grad = lax.psum(gain_part, ('dp', 'fsdp'))  38.1 us
    psum x1, waiting for transfers between devices, local(): scores = lax.psum(partial_value, 'fsdp') * logit_scale  33.7 us
    all_gather x1, blocking collectives, local(): mean_grad = lax.all_gather(mean_part, 'fsdp', axis=1, tiled=True)  17.2 us
    psum x1, blocking collectives, local(): loss_total = lax.psum(loss_local, 'dp')  14.7 us
    all_gather x1, blocking collectives, local(): grad_full = lax.all_gather(grad_low, 'fsdp', axis=1, tiled=True)  13.3 us
    psum x1, blocking collectives, local(): pooled, counts = lax.psum((pooled_part, counts_part), 'fsdp')  13 us
    all_gather x1, blocking collectives, local(): lax.all_gather(query_cache, 'dp', axis=0, tiled=True)  10.9 us
    all_gather x1, blocking collectives, local(): lax.all_gather(region_cache, 'dp', axis=0, tiled=True)  9.04 us
  transfers between devices with their start and end apart: 2, of which 1 were waited for; matrix products, arithmetic and copies ran while one was open for 6% of the time, Pallas kernels for 0%

commit v1 on v0

--- a/solution.py
+++ b/solution.py
@@ -9,7 +9,7 @@
 EPS = 1e-05
 
 
-def local(query_cache, region_cache, positive, hidden_states, segment_ids, norm_gain, proj_weight):
+def local_sharded(query_cache, region_cache, positive, hidden_states, segment_ids, norm_gain, proj_weight):
     row_count = query_cache.shape[0]
     data_count = lax.axis_size("dp")
     pair_count = row_count * data_count
@@ -90,6 +90,115 @@
     return (mean_loss, query_grad, region_grad, hidden_grad, gain_grad, proj_grad)
 
 
+def local_small(query_cache, region_cache, positive, hidden_states, segment_ids, norm_gain, proj_weight):
+    rows, width = query_cache.shape
+    data_count = lax.axis_size("dp")
+    feature_count = lax.axis_size("fsdp")
+    pair_count = rows * data_count
+    tokens = segment_ids.shape[1]
+    model_width = hidden_states.shape[1]
+    logit_scale = float(E) ** (-0.5)
+    contract_last = (((1,), (1,)), ((), ()))
+    contract_first = (((0,), (0,)), ((), ()))
+    me_dp = lax.axis_index("dp")
+    me_f = lax.axis_index("fsdp")
+
+    extra = jnp.concatenate(
+        [positive // 64, positive % 64, segment_ids[0]]
+    ).astype(jnp.float32)
+    extra_rows = -(-extra.shape[0] // width)
+    extra = jnp.pad(extra, (0, extra_rows * width - extra.shape[0]))
+    packed = jnp.concatenate(
+        [query_cache, region_cache, extra.reshape(extra_rows, width).astype(jnp.bfloat16)], axis=0
+    )
+    gathered = lax.all_gather(packed, ("dp", "fsdp"), axis=0, tiled=False)
+    gathered = gathered.reshape(data_count, feature_count, 2 * rows + extra_rows, width)
+    query_all = gathered[:, :, :rows].transpose(0, 2, 1, 3).reshape(pair_count, feature_count * width)
+    region_all = gathered[:, :, rows : 2 * rows].transpose(0, 2, 1, 3).reshape(
+        pair_count, feature_count * width
+    )
+    side = gathered[:, :, 2 * rows :].reshape(data_count, feature_count, extra_rows * width)
+    side = side.astype(jnp.float32)
+    positive_all = (side[:, 0, :rows] * 64 + side[:, 0, rows : 2 * rows]).astype(jnp.int32)
+    positive_all = positive_all.reshape(pair_count)
+    group_ids = side[:, :, 2 * rows : 2 * rows + tokens].reshape(data_count, feature_count * tokens)
+    group_ids = lax.dynamic_index_in_dim(group_ids, me_dp, axis=0, keepdims=False).astype(jnp.int32)
+
+    scores = (
+        lax.dot_general(query_all, region_all, contract_last, preferred_element_type=jnp.float32)
+        * logit_scale
+    )
+    row_max = jnp.max(scores, axis=1, keepdims=True)
+    log_total = row_max[:, 0] + jnp.log(jnp.sum(jnp.exp(scores - row_max), axis=1))
+    columns = lax.broadcasted_iota(jnp.int32, (1, pair_count), 1)
+    matched = columns == positive_all[:, None]
+    target_score = jnp.sum(jnp.where(matched, scores, jnp.zeros_like(scores)), axis=1)
+    mean_loss = jnp.sum(log_total - target_score) / pair_count
+    grad_probs = (jnp.exp(scores - log_total[:, None]) - matched.astype(jnp.float32)).astype(
+        jnp.bfloat16
+    )
+    query_grad_all = logit_scale * jnp.dot(grad_probs, region_all, preferred_element_type=jnp.float32)
+    query_grad = lax.dynamic_slice(query_grad_all, (me_dp * rows, me_f * width), (rows, width))
+    grad_low = lax.dynamic_slice(query_grad_all, (me_dp * rows, 0), (rows, feature_count * width))
+    grad_low = grad_low.astype(jnp.bfloat16)
+    grad_low_cols = lax.dynamic_slice(query_grad_all, (0, me_f * width), (pair_count, width))
+    grad_low_cols = grad_low_cols.astype(jnp.bfloat16)
+    probs_cols = lax.dynamic_slice(grad_probs, (0, me_dp * rows), (pair_count, rows))
+    query_cols = lax.dynamic_slice(query_all, (0, me_f * width), (pair_count, width))
+    region_grad = logit_scale * lax.dot_general(
+        probs_cols, query_cols, contract_first, preferred_element_type=jnp.float32
+    )
+
+    gain = norm_gain.astype(jnp.float32)
+    states = hidden_states.astype(jnp.float32)
+    inv_rms = lax.rsqrt(jnp.mean(states * states, axis=1, keepdims=True) + EPS)
+    normed = (states * inv_rms * gain).astype(jnp.bfloat16)
+    labels = lax.broadcasted_iota(jnp.int32, (rows, 1), 0)
+    member = segment_ids[0][None, :] == labels
+    pooled_part = jnp.dot(member.astype(jnp.bfloat16), normed, preferred_element_type=jnp.float32)
+    counts = jnp.sum((group_ids[None, :] == labels).astype(jnp.float32), axis=1)
+    pooled = lax.psum(pooled_part, "fsdp")
+    mean_pooled = (pooled / counts[:, None]).astype(jnp.bfloat16)
+
+    slice_width = model_width // data_count
+    pieces = mean_pooled.reshape(rows, data_count, slice_width).transpose(1, 0, 2)
+    pieces = lax.all_to_all(pieces, "dp", 0, 0, tiled=True)
+    pooled_cols = pieces.reshape(pair_count, slice_width)
+    proj_grad = lax.dot_general(
+        pooled_cols, grad_low_cols, contract_first, preferred_element_type=jnp.float32
+    )
+
+    mean_part = lax.dot_general(
+        grad_low, proj_weight, contract_last, preferred_element_type=jnp.float32
+    )
+    mean_grad = lax.all_gather(mean_part, "fsdp", axis=1, tiled=True)
+    pool_grad = mean_grad / counts[:, None]
+    normed_grad = lax.dot_general(
+        member.astype(jnp.float32),
+        pool_grad,
+        contract_first,
+        precision=lax.Precision.HIGHEST,
+        preferred_element_type=jnp.float32,
+    )
+    gain_part = jnp.sum(normed_grad * states * inv_rms, axis=0)
+    scaled = gain * normed_grad
+    inner = jnp.mean(scaled * states, axis=1, keepdims=True)
+    hidden_grad = (inv_rms * scaled - states * inv_rms**3 * inner).astype(jnp.bfloat16)
+    gain_grad = lax.psum(gain_part, ("dp", "fsdp"))
+    return (mean_loss, query_grad, region_grad, hidden_grad, gain_grad, proj_grad)
+
+
+SMALL_PAIRS = 1024
+
+
+def local(query_cache, region_cache, positive, hidden_states, segment_ids, norm_gain, proj_weight):
+    pair_count = query_cache.shape[0] * lax.axis_size("dp")
+    args = (query_cache, region_cache, positive, hidden_states, segment_ids, norm_gain, proj_weight)
+    if pair_count <= SMALL_PAIRS:
+        return local_small(*args)
+    return local_sharded(*args)
+
+
 def solution(mesh):
     in_specs = (
         P("dp", "fsdp"),

time: 195 us -> 171 us (0.88)
  blocking collectives: 116 us -> 58.4 us
  waiting for transfers between devices: 33.7 us -> 59 us
  local copies, waits for them, and re-layouts: 2.47 us -> 8.7 us
  starting transfers between devices: 0.08 us -> 3.53 us
  matrix products: 14.5 us -> 11.8 us
    all_gather x0 -> x1, waiting for transfers between devices: none -> 59 us  [local_small(): gathered = lax.all_gather(packed, ('dp', 'fsdp'), axis=0, tiled=False)]
    psum x1, waiting for transfers between devices: 33.7 us -> 0.01 us  [local_small(): pooled = lax.psum(pooled_part, 'fsdp')]
    all_gather x4 -> x1, blocking collectives: 50.3 us -> 19 us  [local_small(): mean_grad = lax.all_gather(mean_part, 'fsdp', axis=1, tiled=True)]
    psum x3 -> x1, blocking collectives: 65.8 us -> 39.4 us  [local_small(): gain_grad = lax.psum(gain_part, ('dp', 'fsdp'))]
    all_to_all x0 -> x1, starting transfers between devices: none -> 3.45 us  [local_small(): pieces = lax.all_to_all(pieces, 'dp', 0, 0, tiled=True)]
    reduce_sum x4, other arithmetic: 5.16 us -> 2.42 us  [the longest x1 1.52 us: local_small(): inv_rms = lax.rsqrt(jnp.mean(states * states, axis=1, keepdims=True) + EPS)]
    dot_general x8 -> x7, matrix products: 14.5 us -> 11.8 us  [the longest x1 3.36 us: local_small(): lax.dot_general(member.astype(jnp.float32), pool_grad, contract_first, pr...]
    unnamed x37 -> x27, local copies, waits for them, and re-layouts: 2.47 us -> 4.91 us
  transfers between devices with their start and end apart: 2 -> 3, of which waited for: 1 -> 1; matrix products, arithmetic and copies ran while one was open for 6% -> 12% of each run, Pallas kernels for 0% -> 0%
where the time goes in v1:
time: 171 us; the launch traced here: 169 us
  waiting for transfers between devices  59 us (35%)
  blocking collectives  58.4 us (34%)
  between operations  17.5 us (10%)
  matrix products  11.8 us (7%)
  other arithmetic  10.6 us (6%)
  local copies, waits for them, and re-layouts  8.7 us (5%)
  starting transfers between devices  3.53 us (2%)
    all_gather x1, waiting for transfers between devices, local_small(): gathered = lax.all_gather(packed, ('dp', 'fsdp'), axis=0, tiled=False)  59 us
    psum x1, blocking collectives, local_small(): gain_grad = lax.psum(gain_part, ('dp', 'fsdp'))  39.4 us
    all_gather x1, blocking collectives, local_small(): mean_grad = lax.all_gather(mean_part, 'fsdp', axis=1, tiled=True)  19 us
    unnamed x27, local copies, waits for them, and re-layouts  4.91 us
    all_to_all x1, starting transfers between devices, local_small(): pieces = lax.all_to_all(pieces, 'dp', 0, 0, tiled=True)  3.45 us
  transfers between devices with their start and end apart: 3, of which 1 were waited for; matrix products, arithmetic and copies ran while one was open for 12% of the time, Pallas kernels for 0%

profile of v1, /device:TPU:0, one launch (start us, length us, event | category | flops | bytes accessed | tf_op | source)
XLA Modules:
  0.0 169.5 jit_solution(11992886837285464235)
XLA Ops:
  8.0 0.0 copy-start
  8.0 0.0 all-gather.4.cloned.1.call-start
  8.1 0.8 and_select_fusion.1
  8.9 0.7 fusion.27
  9.6 1.4 maximum_bitcast_fusion
  11.0 0.0 all-gather.4.cloned.1.call-update
  11.0 0.0 all-reduce.3.cloned.1.call-start
  11.1 0.7 convert_element_type.70
  11.8 1.5 fusion
  13.3 0.5 multiply_multiply_fusion
  13.8 0.5 copy-done.8
  14.3 2.6 %fusion.9 = f32[48,4096]{1,0:T(8,128)} fusion(bf16[128,4096]{1,0:T(8,128)(2,1)} %param.10, f32[4096]{0:T(1024)S(1)} %convert_element_type.70, f32[128]{0:T(128)S(1)} %get-tuple-element.15, s32[128]{0:T(128)} %bitcast.50), kind=kOutput, calls=%fused_computation.17 | convolution fusion | flops 52434944 | bytes 1852416 | tf_op jit(solution)/shard_map/dot_general | solution.py:158
  16.9 0.0 all-reduce.3.cloned.1.call-update
  17.0 59.0 %all-gather.4.cloned.1.call-done = bf16[32,97,256]{2,1,0:T(8,128)(2,1)} async-done(((bf16[1,97,256]{2,1,0:T(8,128)(2,1)}), bf16[32,97,256]{2,1,0:T(8,128)(2,1)}) %all-gather.4.cloned.1.call-update) | async-done | bytes 1589264 | tf_op jit(solution)/shard_map/all_gather | solution.py:114
  76.0 0.9 slice_convert_fusion
  76.9 1.5 fusion.28
  78.4 0.1 fusion.23
  78.5 0.1 slice_bitcast_fusion
  78.6 0.4 copy.24
  79.0 1.0 copy.27
  80.0 0.1 convert_element_type.66
  80.2 0.1 convert_reduce_fusion
  80.3 0.4 copy.23
  80.7 0.2 copy.26
  80.9 0.4 copy-done.2
  81.3 0.6 fusion.29
  81.9 0.2 select_reduce_fusion
  82.0 0.6 subtract_reduce_fusion
  82.7 0.2 subtract_convert_fusion
  82.8 0.7 copy-done.4
  83.5 0.6 convolution_multiply_fusion
  84.2 1.1 copy-done.3
  85.3 0.7 fusion.18
  86.0 0.0 copy-start.1
  86.1 19.0 %all_gather.11 = f32[48,4096]{1,0:T(8,128)} all-gather(f32[48,1024]{1,0:T(8,128)S(1)} %fusion.18), channel_id=1, replica_groups=mesh['dp'=8,'fsdp'=4] {'fsdp'}, dimensions={1}, use_global_device_ids=true | all-gather | bytes 983040 | tf_op jit(solution)/shard_map/all_gather | solution.py:174
  105.1 1.3 divide_convert_fusion
  106.3 0.8 copy.32
  107.1 3.5 %all-to-all-start = ((bf16[8,48,512]{2,1,0:T(8,128)(2,1)}), bf16[8,48,512]{2,1,0:T(8,128)(2,1)S(1)}, u32[]{:S(2)}, u32[]{:S(2)}) async-start(bf16[8,48,512]{2,1,0:T(8,128)(2,1)} %bitcast.32), calls=%async_computation | async-start | bytes 786432 | tf_op jit(solution)/shard_map/all_to_all | solution.py:165
  110.5 0.0 copy-done.1
  110.6 0.0 copy-start.7
  110.6 0.0 copy-start.9
  110.6 3.4 %fusion.6 = (f32[4096]{0:T(1024)}, f32[128]{0:T(128)S(1)}, f32[128,4096]{1,0:T(8,128)S(1)}) fusion(bf16[128,4096]{1,0:T(8,128)(2,1)S(1)} %copy-done.1, f32[128]{0:T(128)} %copy-done.8, f32[4096]{0:T(1024)S(1)} %convert_element_type.70, f32[48,4096]{1,0:T(8,128)} %all_gather.11, f32[48]{0:T(128)} %copy-done.6, s32[128]{0:T(128)} %bitcast.51), kind=kOutput, calls=%fused_computation.11 | convolution fusion | flops 305858432 | bytes 3966656 | tf_op jit(solution)/shard_map/dot_general | solution.py:176
  114.0 1.6 fusion.3
  115.6 1.4 dynamic_slice.19
  117.7 39.4 %psum.14 = f32[4096]{0:T(1024)} all-reduce(f32[4096]{0:T(1024)} %get-tuple-element.6), channel_id=1, replica_groups=mesh['dp'=8,'fsdp'=4] {'dp','fsdp'}, use_global_device_ids=true, to_apply=%region_8.9 | all-reduce | flops 4096 | bytes 32768 | tf_op jit(solution)/shard_map/psum | solution.py:187
  157.1 1.7 %convolution_multiply_fusion.2 = f32[48,256]{1,0:T(8,128)} fusion(bf16[384,1024]{1,0:T(8,128)(2,1)} %bitcast.44, s32[]{:T(128)S(6)} %select_n.34, bf16[384,384]{0,1:T(8,128)(2,1)} %copy-done.4, s32[]{:T(128)S(6)} %select_n.33), kind=kOutput, calls=%fused_computation.16 | convolution fusion | flops 9449472 | bytes 282632 | tf_op jit(solution)/shard_map/dot_general | solution.py:148
  158.8 0.0 all-to-all-done
  158.8 2.1 %fusion.16 = f32[512,256]{1,0:T(8,128)} fusion(bf16[384,512]{1,0:T(8,128)(2,1)S(1)} %bitcast.39, f32[384,1024]{1,0:T(8,128)} %copy-done.3, s32[]{:T(128)S(6)} %select_n.34), kind=kOutput, calls=%fused_computation.30 | convolution fusion | flops 100663296 | bytes 1114116 | tf_op jit(solution)/shard_map/dot_general | solution.py:167
  (18 shorter events, 0.1 us)
Async XLA Ops:
  8.0 77.3 %copy-start = (bf16[1024,1024]{1,0:T(8,128)(2,1)S(1)}, bf16[1024,1024]{1,0:T(8,128)(2,1)}, u32[]{:S(2)}) copy-start(bf16[1024,1024]{1,0:T(8,128)(2,1)} %param.13) | copy-start | bytes 6291460
  8.0 67.9 %all-gather.4.cloned.1.call-start = ((), (), s32[]{:S(2)}) async-start(), calls=%async_computation.2 | async-start | bytes 1757184 | tf_op jit(solution)/shard_map/all_gather | solution.py:114
  11.0 94.0 %all-reduce.3.cloned.1.call-start = ((), (), s32[]{:S(2)}) async-start(), calls=%async_computation.1 | async-start | bytes 1572864 | tf_op jit(solution)/shard_map/psum | solution.py:160
  13.8 0.5 copy-start.8
  80.1 1.1 copy-start.2
  80.3 24.8 %copy-start.6 = (f32[48]{0:T(128)}, f32[48]{0:T(128)S(1)}, u32[]{:S(2)}) copy-start(f32[48]{0:T(128)S(1)} %convert_reduce_fusion) | copy-start | bytes 580
  80.9 2.0 %copy-start.5 = (bf16[48,8,4,256]{3,1,2,0:T(8,128)(2,1)}, bf16[48,8,4,256]{3,1,2,0:T(8,128)(2,1)S(1)}, u32[]{:S(2)}) copy-start(bf16[48,8,4,256]{3,1,2,0:T(8,128)(2,1)S(1)} %copy.26) | copy-start | bytes 2359300
  82.8 0.7 copy-start.4
  84.1 1.2 copy-start.3
  86.0 24.5 %copy-start.1 = (bf16[128,4096]{1,0:T(8,128)(2,1)S(1)}, bf16[128,4096]{1,0:T(8,128)(2,1)}, u32[]{:S(2)}) copy-start(bf16[128,4096]{1,0:T(8,128)(2,1)} %param.10) | copy-start | bytes 3145732
  107.1 51.7 %all-to-all-start = ((bf16[8,48,512]{2,1,0:T(8,128)(2,1)}), bf16[8,48,512]{2,1,0:T(8,128)(2,1)S(1)}, u32[]{:S(2)}, u32[]{:S(2)}) async-start(bf16[8,48,512]{2,1,0:T(8,128)(2,1)} %bitcast.32), calls=%async_computation | async-start | bytes 786432 | tf_op jit(solution)/shard_map/all_to_all | solution.py:165
  110.6 3.4 %copy-start.7 = (f32[128]{0:T(128)S(1)}, f32[128]{0:T(128)}, u32[]{:S(2)}) copy-start(f32[128]{0:T(128)} %get-tuple-element.14) | copy-start | bytes 1540
  110.6 3.4 %copy-start.9 = (f32[128]{0:T(128)S(1)}, f32[128]{0:T(128)}, u32[]{:S(2)}) copy-start(f32[128]{0:T(128)} %copy-done.8) | copy-start | bytes 1540
Sparse Core Ops, SparseCore 0:
  12.3 63.6 all-gather.3
Sparse Core Ops, SparseCore 1:
  17.0 47.7 all-reduce.2

commit v2 on v1

--- a/solution.py
+++ b/solution.py
@@ -90,6 +90,20 @@
     return (mean_loss, query_grad, region_grad, hidden_grad, gain_grad, proj_grad)
 
 
+def gather_blocks(x, axis):
+    n = lax.axis_size(axis)
+    copies = [x] + [
+        lax.ppermute(x, axis, [(i, (i + s) % n) for i in range(n)]) for s in range(1, n)
+    ]
+    stack = jnp.stack(copies)
+    order = (lax.axis_index(axis) - jnp.arange(n)) % n
+    return jnp.take(stack, order, axis=0)
+
+
+def sum_blocks(x, axis):
+    return jnp.sum(gather_blocks(x, axis), axis=0)
+
+
 def local_small(query_cache, region_cache, positive, hidden_states, segment_ids, norm_gain, proj_weight):
     rows, width = query_cache.shape
     data_count = lax.axis_size("dp")
@@ -111,7 +125,7 @@
     packed = jnp.concatenate(
         [query_cache, region_cache, extra.reshape(extra_rows, width).astype(jnp.bfloat16)], axis=0
     )
-    gathered = lax.all_gather(packed, ("dp", "fsdp"), axis=0, tiled=False)
+    gathered = gather_blocks(gather_blocks(packed, "fsdp"), "dp")
     gathered = gathered.reshape(data_count, feature_count, 2 * rows + extra_rows, width)
     query_all = gathered[:, :, :rows].transpose(0, 2, 1, 3).reshape(pair_count, feature_count * width)
     region_all = gathered[:, :, rows : 2 * rows].transpose(0, 2, 1, 3).reshape(
@@ -157,7 +171,7 @@
     member = segment_ids[0][None, :] == labels
     pooled_part = jnp.dot(member.astype(jnp.bfloat16), normed, preferred_element_type=jnp.float32)
     counts = jnp.sum((group_ids[None, :] == labels).astype(jnp.float32), axis=1)
-    pooled = lax.psum(pooled_part, "fsdp")
+    pooled = sum_blocks(pooled_part, "fsdp")
     mean_pooled = (pooled / counts[:, None]).astype(jnp.bfloat16)
 
     slice_width = model_width // data_count
@@ -184,7 +198,7 @@
     scaled = gain * normed_grad
     inner = jnp.mean(scaled * states, axis=1, keepdims=True)
     hidden_grad = (inv_rms * scaled - states * inv_rms**3 * inner).astype(jnp.bfloat16)
-    gain_grad = lax.psum(gain_part, ("dp", "fsdp"))
+    gain_grad = sum_blocks(sum_blocks(gain_part, "dp"), "fsdp")
     return (mean_loss, query_grad, region_grad, hidden_grad, gain_grad, proj_grad)
 
 

time: 171 us -> 142 us (0.83)
  blocking collectives: 58.4 us -> 18 us
  starting transfers between devices: 3.53 us -> 25 us
  between operations: 17.5 us -> 2.74 us
  local copies, waits for them, and re-layouts: 8.7 us -> 20.6 us
  waiting for transfers between devices: 59 us -> 49.9 us
  other arithmetic: 10.6 us -> 16.1 us
  matrix products: 11.8 us -> 9.12 us
    all_gather x1 -> x0, waiting for transfers between devices: 59 us -> none  [local_small(): gathered = lax.all_gather(packed, ('dp', 'fsdp'), axis=0, tiled=False)]
    ppermute x0 -> x23, waiting for transfers between devices: none -> 43 us  [gather_blocks(): lax.ppermute(x, axis, [(i, (i + s) % n) for i in range(n)])]
    psum x1 -> x0, blocking collectives: 39.4 us -> none  [local_small(): gain_grad = lax.psum(gain_part, ('dp', 'fsdp'))]
    ppermute x0 -> x23, starting transfers between devices: none -> 21.5 us  [gather_blocks(): lax.ppermute(x, axis, [(i, (i + s) % n) for i in range(n)])]
    gather x0 -> x5, local copies, waits for them, and re-layouts: none -> 9.34 us  [gather_blocks(): return jnp.take(stack, order, axis=0)]
    all_to_all x1, waiting for transfers between devices: 0.01 us -> 6.86 us  [local_small(): pieces = lax.all_to_all(pieces, 'dp', 0, 0, tiled=True)]
    another operation x1 -> x4, other arithmetic: 0.73 us -> 4.37 us  [the longest x3 3.63 us: gather_blocks(): stack = jnp.stack(copies)]
    reduce_sum x0 -> x3, other arithmetic: none -> 3.16 us  [sum_blocks(): return jnp.sum(gather_blocks(x, axis), axis=0)]
  transfers between devices with their start and end apart: 3 -> 24, of which waited for: 1 -> 12; matrix products, arithmetic and copies ran while one was open for 12% -> 28% of each run, Pallas kernels for 0% -> 0%
where the time goes in v2:
time: 142 us; the launch traced here: 141 us
  waiting for transfers between devices  49.9 us (35%)
  starting transfers between devices  25 us (18%)
  local copies, waits for them, and re-layouts  20.6 us (15%)
  blocking collectives  18 us (13%)
  other arithmetic  16.1 us (11%)
  matrix products  9.12 us (6%)
  between operations  2.74 us (2%)
    ppermute x23, waiting for transfers between devices, gather_blocks(): lax.ppermute(x, axis, [(i, (i + s) % n) for i in range(n)])  43 us
    ppermute x23, starting transfers between devices, gather_blocks(): lax.ppermute(x, axis, [(i, (i + s) % n) for i in range(n)])  21.5 us
    all_gather x1, blocking collectives, local_small(): mean_grad = lax.all_gather(mean_part, 'fsdp', axis=1, tiled=True)  18 us
    gather x5, local copies, waits for them, and re-layouts, gather_blocks(): return jnp.take(stack, order, axis=0)  9.34 us
    unnamed x24, local copies, waits for them, and re-layouts  7.87 us
    all_to_all x1, waiting for transfers between devices, local_small(): pieces = lax.all_to_all(pieces, 'dp', 0, 0, tiled=True)  6.86 us
    another operation x3, other arithmetic, gather_blocks(): stack = jnp.stack(copies)  3.63 us
    all_to_all x1, starting transfers between devices, local_small(): pieces = lax.all_to_all(pieces, 'dp', 0, 0, tiled=True)  3.45 us
  transfers between devices with their start and end apart: 24, of which 12 were waited for; matrix products, arithmetic and copies ran while one was open for 28% of the time, Pallas kernels for 0%

profile of v2, /device:TPU:0, one launch (start us, length us, event | category | flops | bytes accessed | tf_op | source)
XLA Modules:
  0.0 141.4 jit_solution(17586023122076792498)
XLA Ops:
  0.6 0.8 and_select_fusion.3
  1.5 0.7 constant_dynamic-update-slice_fusion.2
  2.2 0.7 fusion.29
  2.9 0.7 constant_dynamic-update-slice_fusion.1
  3.7 5.0 %collective-permute-start.2 = (bf16[97,256]{1,0:T(8,128)(2,1)S(1)}, bf16[97,256]{1,0:T(8,128)(2,1)S(1)}, u32[]{:S(2)}, u32[]{:S(2)}) collective-permute-start(bf16[97,256]{1,0:T(8,128)(2,1)S(1)} %constant_dynamic-update-slice_fusion), channel_id=1, source_target_pairs={{0,3},{1,0},{2,1},{3,2},{4,7},{5,4},{6,5},{7,6},{8,11},{9,8},{10,9... | collective-permute-start | bytes 149000 | tf_op jit(solution)/shard_map/ppermute | solution.py:96
  8.7 1.0 collective-permute-start
  9.8 1.5 %fusion = f32[128]{0:T(128)S(1)} fusion(bf16[128,4096]{1,0:T(8,128)(2,1)} %param.10), kind=kLoop, calls=%fused_computation.12 | loop fusion | flops 1572736 | bytes 1049088 | tf_op jit(solution)/shard_map/reduce_sum | solution.py:168
  11.3 0.7 convert_element_type.71
  12.0 2.6 %fusion.9 = f32[48,4096]{1,0:T(8,128)} fusion(bf16[128,4096]{1,0:T(8,128)(2,1)} %param.10, f32[4096]{0:T(1024)S(1)} %convert_element_type.71, f32[128]{0:T(128)S(1)} %get-tuple-element.15, s32[128]{0:T(128)} %bitcast.106), kind=kOutput, calls=%fused_computation.25 | convolution fusion | flops 52434944 | bytes 1852416 | tf_op jit(solution)/shard_map/dot_general | solution.py:172
  14.6 2.8 %collective-permute-start.22 = (f32[48,4096]{1,0:T(8,128)}, f32[48,4096]{1,0:T(8,128)}, u32[]{:S(2)}, u32[]{:S(2)}) collective-permute-start(f32[48,4096]{1,0:T(8,128)} %fusion.9), channel_id=1, source_target_pairs={{0,3},{1,0},{2,1},{3,2},{4,7},{5,4},{6,5},{7,6},{8,11},{9,8},{10,9... | collective-permute-start | bytes 2359304 | tf_op jit(solution)/shard_map/ppermute | solution.py:96
  17.4 1.1 collective-permute-start.21
  19.9 2.0 %collective-permute-start.8 = (bf16[4,97,256]{2,1,0:T(8,128)(2,1)S(1)}, bf16[4,97,256]{2,1,0:T(8,128)(2,1)S(1)}, u32[]{:S(2)}, u32[]{:S(2)}) collective-permute-start(bf16[4,97,256]{2,1,0:T(8,128)(2,1)S(1)} %broadcast_select_fusion.1), channel_id=1, source_target_pairs={{0,24},{4,28},{8,0},{12,4},{16,8},{20,12},{24,16},{28,20},{1,25},{... | collective-permute-start | bytes 595976 | tf_op jit(solution)/shard_map/ppermute | solution.py:96
  22.1 0.8 fusion.17
  22.9 9.7 %collective-permute-done.3 = bf16[4,97,256]{2,1,0:T(8,128)(2,1)S(1)} collective-permute-done((bf16[4,97,256]{2,1,0:T(8,128)(2,1)S(1)}, bf16[4,97,256]{2,1,0:T(8,128)(2,1)S(1)}, u32[]{:S(2)}, u32[]{:S(2)}) %collective-permute-start.3) | collective-permute-done | bytes 198688 | tf_op jit(solution)/shard_map/ppermute | solution.py:96
  32.6 0.7 bitcast_dynamic-update-slice_fusion.6
  33.3 6.0 %collective-permute-done.4 = bf16[4,97,256]{2,1,0:T(8,128)(2,1)S(1)} collective-permute-done((bf16[4,97,256]{2,1,0:T(8,128)(2,1)S(1)}, bf16[4,97,256]{2,1,0:T(8,128)(2,1)S(1)}, u32[]{:S(2)}, u32[]{:S(2)}) %collective-permute-start.4) | collective-permute-done | bytes 198688 | tf_op jit(solution)/shard_map/ppermute | solution.py:96
  39.3 0.7 bitcast_dynamic-update-slice_fusion.5
  40.0 5.5 %collective-permute-done.5 = bf16[4,97,256]{2,1,0:T(8,128)(2,1)S(1)} collective-permute-done((bf16[4,97,256]{2,1,0:T(8,128)(2,1)S(1)}, bf16[4,97,256]{2,1,0:T(8,128)(2,1)S(1)}, u32[]{:S(2)}, u32[]{:S(2)}) %collective-permute-start.5) | collective-permute-done | bytes 198688 | tf_op jit(solution)/shard_map/ppermute | solution.py:96
  46.8 4.6 %collective-permute-done.6 = bf16[4,97,256]{2,1,0:T(8,128)(2,1)S(1)} collective-permute-done((bf16[4,97,256]{2,1,0:T(8,128)(2,1)S(1)}, bf16[4,97,256]{2,1,0:T(8,128)(2,1)S(1)}, u32[]{:S(2)}, u32[]{:S(2)}) %collective-permute-start.6) | collective-permute-done | bytes 198688 | tf_op jit(solution)/shard_map/ppermute | solution.py:96
  52.1 4.6 %collective-permute-done.7 = bf16[4,97,256]{2,1,0:T(8,128)(2,1)S(1)} collective-permute-done((bf16[4,97,256]{2,1,0:T(8,128)(2,1)S(1)}, bf16[4,97,256]{2,1,0:T(8,128)(2,1)S(1)}, u32[]{:S(2)}, u32[]{:S(2)}) %collective-permute-start.7) | collective-permute-done | bytes 198688 | tf_op jit(solution)/shard_map/ppermute | solution.py:96
  56.7 0.7 bitcast_dynamic-update-slice_fusion.2
  57.4 0.7 bitcast_dynamic-update-slice_fusion.1
  58.8 3.3 %gather_fusion.1 = bf16[8,4,97,256]{3,2,1,0:T(8,128)(2,1)} fusion(bf16[8,4,97,256]{3,2,1,0:T(8,128)(2,1)} %bitcast_dynamic-update-slice_fusion, s32[1024]{0:T(1024)S(1)} %pad_clamp_fusion), kind=kCustom, calls=%fused_computation.1 | custom fusion | bytes 3178528 | tf_op jit(solution)/shard_map/jit(_take)/gather | solution.py:100
  62.1 1.7 %broadcast_select_fusion = bf16[8,4,97,256]{3,2,1,0:T(8,128)(2,1)S(1)} fusion(bf16[8,4,97,256]{3,2,1,0:T(8,128)(2,1)} %gather_fusion.1, pred[8]{0:T(512)(128)(4,1)S(1)} %compare_and_fusion.1), kind=kLoop, calls=%fused_computation.21 | loop fusion | flops 794624 | bytes 3178504 | tf_op jit(solution)/shard_map/jit(_take)/select_n | solution.py:100
  64.5 1.0 copy.26
  69.0 0.7 fusion.20
  69.7 18.0 %all_gather.3 = f32[48,4096]{1,0:T(8,128)S(1)} all-gather(f32[48,1024]{1,0:T(8,128)S(1)} %fusion.20), channel_id=1, replica_groups=mesh['dp'=8,'fsdp'=4] {'fsdp'}, dimensions={1}, use_global_device_ids=true | all-gather | bytes 983040 | tf_op jit(solution)/shard_map/all_gather | solution.py:188
  87.8 1.6 %fusion.6 = (f32[4096]{0:T(1024)S(1)}, f32[128]{0:T(128)S(1)}, f32[128,4096]{1,0:T(8,128)S(1)}) fusion(bf16[128,4096]{1,0:T(8,128)(2,1)S(1)} %copy-done.1, f32[128]{0:T(128)S(1)} %get-tuple-element.15, f32[4096]{0:T(1024)S(1)} %convert_element_type.71, f32[48,4096]{1,0:T(8,128)S(1)} %all_gather.3, f32[48]{0:T(128)S(1)} %convert_reduce_fusion, ...), kind=kOutput, calls=%fused_computation.18 | convolution fusion | flops 305858432 | bytes 3966656 | tf_op jit(solution)/shard_map/dot_general | solution.py:190
  89.4 1.6 %collective-permute-start.16 = (f32[4096]{0:T(1024)S(1)}, f32[4096]{0:T(1024)S(1)}, u32[]{:S(2)}, u32[]{:S(2)}) collective-permute-start(f32[4096]{0:T(1024)S(1)} %get-tuple-element.6), channel_id=1, source_target_pairs={{0,28},{4,0},{8,4},{12,8},{16,12},{20,16},{24,20},{28,24},{1,29},{... | collective-permute-start | bytes 49160 | tf_op jit(solution)/shard_map/ppermute | solution.py:96
  91.0 0.7 collective-permute-start.15
  92.4 2.3 %collective-permute-done.15 = f32[4096]{0:T(1024)S(1)} collective-permute-done((f32[4096]{0:T(1024)S(1)}, f32[4096]{0:T(1024)S(1)}, u32[]{:S(2)}, u32[]{:S(2)}) %collective-permute-start.15) | collective-permute-done | bytes 16416 | tf_op jit(solution)/shard_map/ppermute | solution.py:96
  94.7 1.1 collective-permute-start.13
  95.9 1.6 %fusion.3 = bf16[128,4096]{1,0:T(8,128)(2,1)} fusion(bf16[128,4096]{1,0:T(8,128)(2,1)S(1)} %copy-done.1, f32[128,4096]{1,0:T(8,128)S(1)} %get-tuple-element.20, f32[128]{0:T(128)S(1)} %broadcast_multiply_fusion, f32[128]{0:T(128)S(1)} %get-tuple-element.14, f32[4096]{0:T(1024)S(1)} %convert_element_type.71, f32[128]{0:T(128)S(1)} %get-tuple-element.15), kind=kLoop, calls=%fused_computation.15 | loop fusion | flops 3670016 | bytes 4212224 | tf_op jit(solution)/shard_map/convert_element_type | solution.py:200
  97.5 1.0 collective-permute-done.13
  98.5 1.0 collective-permute-start.11
  99.6 0.8 convolution_multiply_fusion.2
  101.7 1.5 %collective-permute-done.11 = f32[4096]{0:T(1024)S(1)} collective-permute-done((f32[4096]{0:T(1024)S(1)}, f32[4096]{0:T(1024)S(1)}, u32[]{:S(2)}, u32[]{:S(2)}) %collective-permute-start.11) | collective-permute-done | bytes 16416 | tf_op jit(solution)/shard_map/ppermute | solution.py:96
  104.4 2.2 %collective-permute-start.19 = (f32[4096]{0:T(1024)S(1)}, f32[4096]{0:T(1024)S(1)}, u32[]{:S(2)}, u32[]{:S(2)}) collective-permute-start(f32[4096]{0:T(1024)S(1)} %select_reduce_fusion.2), channel_id=1, source_target_pairs={{0,3},{1,0},{2,1},{3,2},{4,7},{5,4},{6,5},{7,6},{8,11},{9,8},{10,9... | collective-permute-start | bytes 49160 | tf_op jit(solution)/shard_map/ppermute | solution.py:96
  106.6 0.9 collective-permute-start.17
  107.5 7.3 %collective-permute-done.20 = f32[48,4096]{1,0:T(8,128)S(1)} collective-permute-done((f32[48,4096]{1,0:T(8,128)}, f32[48,4096]{1,0:T(8,128)S(1)}, u32[]{:S(2)}, u32[]{:S(2)}) %collective-permute-start.20) | collective-permute-done | bytes 786464 | tf_op jit(solution)/shard_map/ppermute | solution.py:96
  114.8 3.5 %pad_maximum_fusion = f32[4,48,4096]{2,1,0:T(8,128)} fusion(f32[1,48,4096]{2,1,0:T(8,128)} %bitcast.33, f32[1,48,4096]{2,1,0:T(8,128)} %bitcast.32, f32[1,48,4096]{2,1,0:T(8,128)S(1)} %bitcast.84, f32[1,48,4096]{2,1,0:T(8,128)} %bitcast.30), kind=kLoop, calls=%fused_computation.10 | loop fusion | flops 2359296 | bytes 6291456 | tf_op jit(solution)/shard_map/stack | solution.py:98
  118.3 4.3 %gather_fusion.4 = f32[4,48,4096]{2,1,0:T(8,128)} fusion(f32[4,48,4096]{2,1,0:T(8,128)} %pad_maximum_fusion, s32[1024]{0:T(1024)S(1)} %pad_clamp_fusion.1), kind=kCustom, calls=%fused_computation.4 | custom fusion | bytes 6291472 | tf_op jit(solution)/shard_map/jit(_take)/gather | solution.py:100
  122.7 2.3 %select_reduce_fusion = f32[48,4096]{1,0:T(8,128)S(1)} fusion(f32[4,48,4096]{2,1,0:T(8,128)} %gather_fusion.4, pred[4]{0:T(512)(128)(4,1)S(1)} %compare_and_fusion), kind=kLoop, calls=%fused_computation.11 | loop fusion | flops 1376256 | bytes 3932164 | tf_op jit(solution)/shard_map/reduce_sum | solution.py:104
  125.6 0.9 copy.23
  126.4 3.5 %all-to-all-start = ((bf16[8,48,512]{2,1,0:T(8,128)(2,1)}), bf16[8,48,512]{2,1,0:T(8,128)(2,1)S(1)}, u32[]{:S(2)}, u32[]{:S(2)}) async-start(bf16[8,48,512]{2,1,0:T(8,128)(2,1)} %copy.23), calls=%async_computation | async-start | bytes 786432 | tf_op jit(solution)/shard_map/all_to_all | solution.py:179
  130.6 0.7 select_reduce_fusion.3
  131.3 6.9 %all-to-all-done = bf16[8,48,512]{2,1,0:T(8,128)(2,1)S(1)} async-done(((bf16[8,48,512]{2,1,0:T(8,128)(2,1)}), bf16[8,48,512]{2,1,0:T(8,128)(2,1)S(1)}, u32[]{:S(2)}, u32[]{:S(2)}) %all-to-all-start) | async-done | bytes 393248 | tf_op jit(solution)/shard_map/all_to_all | solution.py:179
  138.2 2.1 %fusion.18 = f32[512,256]{1,0:T(8,128)} fusion(bf16[384,512]{1,0:T(8,128)(2,1)S(1)} %bitcast.80, f32[384,1024]{1,0:T(8,128)} %copy-done.3, s32[]{:T(128)S(6)} %select_n.152), kind=kOutput, calls=%fused_computation.51 | convolution fusion | flops 100663296 | bytes 1114116 | tf_op jit(solution)/shard_map/dot_general | solution.py:181
  (77 shorter events, 12.2 us)
Async XLA Ops:
  0.6 68.3 %copy-start = (bf16[1024,1024]{1,0:T(8,128)(2,1)S(1)}, bf16[1024,1024]{1,0:T(8,128)(2,1)}, u32[]{:S(2)}) copy-start(bf16[1024,1024]{1,0:T(8,128)(2,1)} %param.13) | copy-start | bytes 6291460
  3.7 15.0 %collective-permute-start.2 = (bf16[97,256]{1,0:T(8,128)(2,1)S(1)}, bf16[97,256]{1,0:T(8,128)(2,1)S(1)}, u32[]{:S(2)}, u32[]{:S(2)}) collective-permute-start(bf16[97,256]{1,0:T(8,128)(2,1)S(1)} %constant_dynamic-update-slice_fusion), channel_id=1, source_target_pairs={{0,3},{1,0},{2,1},{3,2},{4,7},{5,4},{6,5},{7,6},{8,11},{9,8},{10,9... | collective-permute-start | bytes 149000 | tf_op jit(solution)/shard_map/ppermute | solution.py:96
  8.7 9.9 %collective-permute-start.1 = (bf16[97,256]{1,0:T(8,128)(2,1)S(1)}, bf16[97,256]{1,0:T(8,128)(2,1)S(1)}, u32[]{:S(2)}, u32[]{:S(2)}) collective-permute-start(bf16[97,256]{1,0:T(8,128)(2,1)S(1)} %constant_dynamic-update-slice_fusion), channel_id=1, source_target_pairs={{0,2},{1,3},{2,0},{3,1},{4,6},{5,7},{6,4},{7,5},{8,10},{9,11},{10,... | collective-permute-start | bytes 149000 | tf_op jit(solution)/shard_map/ppermute | solution.py:96
  8.7 9.9 %collective-permute-start = (bf16[97,256]{1,0:T(8,128)(2,1)S(1)}, bf16[97,256]{1,0:T(8,128)(2,1)S(1)}, u32[]{:S(2)}, u32[]{:S(2)}) collective-permute-start(bf16[97,256]{1,0:T(8,128)(2,1)S(1)} %constant_dynamic-update-slice_fusion), channel_id=1, source_target_pairs={{0,1},{1,2},{2,3},{3,0},{4,5},{5,6},{6,7},{7,4},{8,9},{9,10},{10,1... | collective-permute-start | bytes 149000 | tf_op jit(solution)/shard_map/ppermute | solution.py:96
  14.6 92.0 %collective-permute-start.22 = (f32[48,4096]{1,0:T(8,128)}, f32[48,4096]{1,0:T(8,128)}, u32[]{:S(2)}, u32[]{:S(2)}) collective-permute-start(f32[48,4096]{1,0:T(8,128)} %fusion.9), channel_id=1, source_target_pairs={{0,3},{1,0},{2,1},{3,2},{4,7},{5,4},{6,5},{7,6},{8,11},{9,8},{10,9... | collective-permute-start | bytes 2359304 | tf_op jit(solution)/shard_map/ppermute | solution.py:96
  17.4 90.1 %collective-permute-start.21 = (f32[48,4096]{1,0:T(8,128)}, f32[48,4096]{1,0:T(8,128)}, u32[]{:S(2)}, u32[]{:S(2)}) collective-permute-start(f32[48,4096]{1,0:T(8,128)} %fusion.9), channel_id=1, source_target_pairs={{0,2},{1,3},{2,0},{3,1},{4,6},{5,7},{6,4},{7,5},{8,10},{9,11},{10,... | collective-permute-start | bytes 2359304 | tf_op jit(solution)/shard_map/ppermute | solution.py:96
  19.4 38.7 %collective-permute-start.9 = (bf16[4,97,256]{2,1,0:T(8,128)(2,1)S(1)}, bf16[4,97,256]{2,1,0:T(8,128)(2,1)S(1)}, u32[]{:S(2)}, u32[]{:S(2)}) collective-permute-start(bf16[4,97,256]{2,1,0:T(8,128)(2,1)S(1)} %broadcast_select_fusion.1), channel_id=1, source_target_pairs={{0,28},{4,0},{8,4},{12,8},{16,12},{20,16},{24,20},{28,24},{1,29},{... | collective-permute-start | bytes 595976 | tf_op jit(solution)/shard_map/ppermute | solution.py:96
  19.9 37.4 %collective-permute-start.8 = (bf16[4,97,256]{2,1,0:T(8,128)(2,1)S(1)}, bf16[4,97,256]{2,1,0:T(8,128)(2,1)S(1)}, u32[]{:S(2)}, u32[]{:S(2)}) collective-permute-start(bf16[4,97,256]{2,1,0:T(8,128)(2,1)S(1)} %broadcast_select_fusion.1), channel_id=1, source_target_pairs={{0,24},{4,28},{8,0},{12,4},{16,8},{20,12},{24,16},{28,20},{1,25},{... | collective-permute-start | bytes 595976 | tf_op jit(solution)/shard_map/ppermute | solution.py:96
  22.0 10.6 %collective-permute-start.3 = (bf16[4,97,256]{2,1,0:T(8,128)(2,1)S(1)}, bf16[4,97,256]{2,1,0:T(8,128)(2,1)S(1)}, u32[]{:S(2)}, u32[]{:S(2)}) collective-permute-start(bf16[4,97,256]{2,1,0:T(8,128)(2,1)S(1)} %broadcast_select_fusion.1), channel_id=1, source_target_pairs={{0,4},{4,8},{8,12},{12,16},{16,20},{20,24},{24,28},{28,0},{1,5},{5... | collective-permute-start | bytes 595976 | tf_op jit(solution)/shard_map/ppermute | solution.py:96
  32.6 6.7 %collective-permute-start.4 = (bf16[4,97,256]{2,1,0:T(8,128)(2,1)S(1)}, bf16[4,97,256]{2,1,0:T(8,128)(2,1)S(1)}, u32[]{:S(2)}, u32[]{:S(2)}) collective-permute-start(bf16[4,97,256]{2,1,0:T(8,128)(2,1)S(1)} %broadcast_select_fusion.1), channel_id=1, source_target_pairs={{0,8},{4,12},{8,16},{12,20},{16,24},{20,28},{24,0},{28,4},{1,9},{5... | collective-permute-start | bytes 595976 | tf_op jit(solution)/shard_map/ppermute | solution.py:96
  39.3 6.2 %collective-permute-start.5 = (bf16[4,97,256]{2,1,0:T(8,128)(2,1)S(1)}, bf16[4,97,256]{2,1,0:T(8,128)(2,1)S(1)}, u32[]{:S(2)}, u32[]{:S(2)}) collective-permute-start(bf16[4,97,256]{2,1,0:T(8,128)(2,1)S(1)} %broadcast_select_fusion.1), channel_id=1, source_target_pairs={{0,12},{4,16},{8,20},{12,24},{16,28},{20,0},{24,4},{28,8},{1,13},{... | collective-permute-start | bytes 595976 | tf_op jit(solution)/shard_map/ppermute | solution.py:96
  45.6 5.8 %collective-permute-start.6 = (bf16[4,97,256]{2,1,0:T(8,128)(2,1)S(1)}, bf16[4,97,256]{2,1,0:T(8,128)(2,1)S(1)}, u32[]{:S(2)}, u32[]{:S(2)}) collective-permute-start(bf16[4,97,256]{2,1,0:T(8,128)(2,1)S(1)} %broadcast_select_fusion.1), channel_id=1, source_target_pairs={{0,16},{4,20},{8,24},{12,28},{16,0},{20,4},{24,8},{28,12},{1,17},{... | collective-permute-start | bytes 595976 | tf_op jit(solution)/shard_map/ppermute | solution.py:96
  51.4 5.3 %collective-permute-start.7 = (bf16[4,97,256]{2,1,0:T(8,128)(2,1)S(1)}, bf16[4,97,256]{2,1,0:T(8,128)(2,1)S(1)}, u32[]{:S(2)}, u32[]{:S(2)}) collective-permute-start(bf16[4,97,256]{2,1,0:T(8,128)(2,1)S(1)} %broadcast_select_fusion.1), channel_id=1, source_target_pairs={{0,20},{4,24},{8,28},{12,0},{16,4},{20,8},{24,12},{28,16},{1,21},{... | collective-permute-start | bytes 595976 | tf_op jit(solution)/shard_map/ppermute | solution.py:96
  65.6 1.1 copy-start.2
  68.9 31.4 %copy-start.3 = (f32[384,1024]{1,0:T(8,128)}, f32[384,1024]{1,0:T(8,128)S(1)}, u32[]{:S(2)}) copy-start(f32[384,1024]{1,0:T(8,128)S(1)} %convolution_multiply_fusion) | copy-start | bytes 4718596
  68.9 18.8 %copy-start.1 = (bf16[128,4096]{1,0:T(8,128)(2,1)S(1)}, bf16[128,4096]{1,0:T(8,128)(2,1)}, u32[]{:S(2)}) copy-start(bf16[128,4096]{1,0:T(8,128)(2,1)} %param.10) | copy-start | bytes 3145732
  69.0 18.8 %copy-start.4 = (s32[1,128]{1,0:T(1,128)S(1)}, s32[1,128]{1,0:T(1,128)}, u32[]{:S(2)}) copy-start(s32[1,128]{1,0:T(1,128)} %param.11) | copy-start | bytes 1540
  89.4 3.0 %collective-permute-start.16 = (f32[4096]{0:T(1024)S(1)}, f32[4096]{0:T(1024)S(1)}, u32[]{:S(2)}, u32[]{:S(2)}) collective-permute-start(f32[4096]{0:T(1024)S(1)} %get-tuple-element.6), channel_id=1, source_target_pairs={{0,28},{4,0},{8,4},{12,8},{16,12},{20,16},{24,20},{28,24},{1,29},{... | collective-permute-start | bytes 49160 | tf_op jit(solution)/shard_map/ppermute | solution.py:96
  91.0 3.8 %collective-permute-start.15 = (f32[4096]{0:T(1024)S(1)}, f32[4096]{0:T(1024)S(1)}, u32[]{:S(2)}, u32[]{:S(2)}) collective-permute-start(f32[4096]{0:T(1024)S(1)} %get-tuple-element.6), channel_id=1, source_target_pairs={{0,24},{4,28},{8,0},{12,4},{16,8},{20,12},{24,16},{28,20},{1,25},{... | collective-permute-start | bytes 49160 | tf_op jit(solution)/shard_map/ppermute | solution.py:96
  91.7 4.2 %collective-permute-start.14 = (f32[4096]{0:T(1024)S(1)}, f32[4096]{0:T(1024)S(1)}, u32[]{:S(2)}, u32[]{:S(2)}) collective-permute-start(f32[4096]{0:T(1024)S(1)} %get-tuple-element.6), channel_id=1, source_target_pairs={{0,20},{4,24},{8,28},{12,0},{16,4},{20,8},{24,12},{28,16},{1,21},{... | collective-permute-start | bytes 49160 | tf_op jit(solution)/shard_map/ppermute | solution.py:96
  92.4 22.4 %collective-permute-start.20 = (f32[48,4096]{1,0:T(8,128)}, f32[48,4096]{1,0:T(8,128)S(1)}, u32[]{:S(2)}, u32[]{:S(2)}) collective-permute-start(f32[48,4096]{1,0:T(8,128)} %fusion.9), channel_id=1, source_target_pairs={{0,1},{1,2},{2,3},{3,0},{4,5},{5,6},{6,7},{7,4},{8,9},{9,10},{10,1... | collective-permute-start | bytes 2359304 | tf_op jit(solution)/shard_map/ppermute | solution.py:96
  94.7 3.7 %collective-permute-start.13 = (f32[4096]{0:T(1024)S(1)}, f32[4096]{0:T(1024)S(1)}, u32[]{:S(2)}, u32[]{:S(2)}) collective-permute-start(f32[4096]{0:T(1024)S(1)} %get-tuple-element.6), channel_id=1, source_target_pairs={{0,16},{4,20},{8,24},{12,28},{16,0},{20,4},{24,8},{28,12},{1,17},{... | collective-permute-start | bytes 49160 | tf_op jit(solution)/shard_map/ppermute | solution.py:96
  95.9 3.6 %collective-permute-start.12 = (f32[4096]{0:T(1024)S(1)}, f32[4096]{0:T(1024)S(1)}, u32[]{:S(2)}, u32[]{:S(2)}) collective-permute-start(f32[4096]{0:T(1024)S(1)} %get-tuple-element.6), channel_id=1, source_target_pairs={{0,12},{4,16},{8,20},{12,24},{16,28},{20,0},{24,4},{28,8},{1,13},{... | collective-permute-start | bytes 49160 | tf_op jit(solution)/shard_map/ppermute | solution.py:96
  98.5 4.6 %collective-permute-start.11 = (f32[4096]{0:T(1024)S(1)}, f32[4096]{0:T(1024)S(1)}, u32[]{:S(2)}, u32[]{:S(2)}) collective-permute-start(f32[4096]{0:T(1024)S(1)} %get-tuple-element.6), channel_id=1, source_target_pairs={{0,8},{4,12},{8,16},{12,20},{16,24},{20,28},{24,0},{28,4},{1,9},{5... | collective-permute-start | bytes 49160 | tf_op jit(solution)/shard_map/ppermute | solution.py:96
  99.4 4.1 %collective-permute-start.10 = (f32[4096]{0:T(1024)S(1)}, f32[4096]{0:T(1024)S(1)}, u32[]{:S(2)}, u32[]{:S(2)}) collective-permute-start(f32[4096]{0:T(1024)S(1)} %get-tuple-element.6), channel_id=1, source_target_pairs={{0,4},{4,8},{8,12},{12,16},{16,20},{20,24},{24,28},{28,0},{1,5},{5... | collective-permute-start | bytes 49160 | tf_op jit(solution)/shard_map/ppermute | solution.py:96
  104.4 25.5 %collective-permute-start.19 = (f32[4096]{0:T(1024)S(1)}, f32[4096]{0:T(1024)S(1)}, u32[]{:S(2)}, u32[]{:S(2)}) collective-permute-start(f32[4096]{0:T(1024)S(1)} %select_reduce_fusion.2), channel_id=1, source_target_pairs={{0,3},{1,0},{2,1},{3,2},{4,7},{5,4},{6,5},{7,6},{8,11},{9,8},{10,9... | collective-permute-start | bytes 49160 | tf_op jit(solution)/shard_map/ppermute | solution.py:96
  106.6 23.3 %collective-permute-start.18 = (f32[4096]{0:T(1024)S(1)}, f32[4096]{0:T(1024)S(1)}, u32[]{:S(2)}, u32[]{:S(2)}) collective-permute-start(f32[4096]{0:T(1024)S(1)} %select_reduce_fusion.2), channel_id=1, source_target_pairs={{0,2},{1,3},{2,0},{3,1},{4,6},{5,7},{6,4},{7,5},{8,10},{9,11},{10,... | collective-permute-start | bytes 49160 | tf_op jit(solution)/shard_map/ppermute | solution.py:96
  106.6 23.3 %collective-permute-start.17 = (f32[4096]{0:T(1024)S(1)}, f32[4096]{0:T(1024)S(1)}, u32[]{:S(2)}, u32[]{:S(2)}) collective-permute-start(f32[4096]{0:T(1024)S(1)} %select_reduce_fusion.2), channel_id=1, source_target_pairs={{0,1},{1,2},{2,3},{3,0},{4,5},{5,6},{6,7},{7,4},{8,9},{9,10},{10,1... | collective-permute-start | bytes 49160 | tf_op jit(solution)/shard_map/ppermute | solution.py:96
  126.4 11.7 %all-to-all-start = ((bf16[8,48,512]{2,1,0:T(8,128)(2,1)}), bf16[8,48,512]{2,1,0:T(8,128)(2,1)S(1)}, u32[]{:S(2)}, u32[]{:S(2)}) async-start(bf16[8,48,512]{2,1,0:T(8,128)(2,1)} %copy.23), calls=%async_computation | async-start | bytes 786432 | tf_op jit(solution)/shard_map/all_to_all | solution.py:179

commit v3 on v2

--- a/solution.py
+++ b/solution.py
@@ -104,6 +104,17 @@
     return jnp.sum(gather_blocks(x, axis), axis=0)
 
 
+def scatter_sum(chunks, axis):
+    n = lax.axis_size(axis)
+    me = lax.axis_index(axis)
+    copies = [lax.dynamic_index_in_dim(chunks, me, axis=0, keepdims=False)]
+    for s in range(1, n):
+        piece = lax.dynamic_index_in_dim(chunks, (me + s) % n, axis=0, keepdims=False)
+        copies.append(lax.ppermute(piece, axis, [(i, (i + s) % n) for i in range(n)]))
+    order = (me - jnp.arange(n)) % n
+    return jnp.sum(jnp.take(jnp.stack(copies), order, axis=0), axis=0)
+
+
 def local_small(query_cache, region_cache, positive, hidden_states, segment_ids, norm_gain, proj_weight):
     rows, width = query_cache.shape
     data_count = lax.axis_size("dp")
@@ -125,8 +136,33 @@
     packed = jnp.concatenate(
         [query_cache, region_cache, extra.reshape(extra_rows, width).astype(jnp.bfloat16)], axis=0
     )
-    gathered = gather_blocks(gather_blocks(packed, "fsdp"), "dp")
-    gathered = gathered.reshape(data_count, feature_count, 2 * rows + extra_rows, width)
+    group_blocks = gather_blocks(packed, "fsdp")
+    group_side = group_blocks[:, 2 * rows :].reshape(feature_count, extra_rows * width)
+    group_ids = group_side[:, 2 * rows : 2 * rows + tokens].reshape(feature_count * tokens)
+    group_ids = group_ids.astype(jnp.int32)
+
+    gain = norm_gain.astype(jnp.float32)
+    states = hidden_states.astype(jnp.float32)
+    inv_rms = lax.rsqrt(jnp.mean(states * states, axis=1, keepdims=True) + EPS)
+    normed = (states * inv_rms * gain).astype(jnp.bfloat16)
+    labels = lax.broadcasted_iota(jnp.int32, (rows, 1), 0)
+    member = segment_ids[0][None, :] == labels
+    pooled_part = jnp.dot(member.astype(jnp.bfloat16), normed, preferred_element_type=jnp.float32)
+    counts = jnp.sum((group_ids[None, :] == labels).astype(jnp.float32), axis=1)
+    chunk = model_width // feature_count
+    pooled_chunk = scatter_sum(
+        pooled_part.reshape(rows, feature_count, chunk).transpose(1, 0, 2), "fsdp"
+    )
+    mean_chunk = (pooled_chunk / counts[:, None]).astype(jnp.bfloat16)
+    mean_pooled = gather_blocks(mean_chunk, "fsdp").transpose(1, 0, 2).reshape(rows, model_width)
+
+    gathered = gather_blocks(group_blocks, "dp")
+    mean_pooled, gathered = lax.optimization_barrier((mean_pooled, gathered))
+    slice_width = model_width // data_count
+    pieces = mean_pooled.reshape(rows, data_count, slice_width).transpose(1, 0, 2)
+    pieces = lax.all_to_all(pieces, "dp", 0, 0, tiled=True)
+    pooled_cols = pieces.reshape(pair_count, slice_width)
+
     query_all = gathered[:, :, :rows].transpose(0, 2, 1, 3).reshape(pair_count, feature_count * width)
     region_all = gathered[:, :, rows : 2 * rows].transpose(0, 2, 1, 3).reshape(
         pair_count, feature_count * width
@@ -135,8 +171,6 @@
     side = side.astype(jnp.float32)
     positive_all = (side[:, 0, :rows] * 64 + side[:, 0, rows : 2 * rows]).astype(jnp.int32)
     positive_all = positive_all.reshape(pair_count)
-    group_ids = side[:, :, 2 * rows : 2 * rows + tokens].reshape(data_count, feature_count * tokens)
-    group_ids = lax.dynamic_index_in_dim(group_ids, me_dp, axis=0, keepdims=False).astype(jnp.int32)
 
     scores = (
         lax.dot_general(query_all, region_all, contract_last, preferred_element_type=jnp.float32)
@@ -163,27 +197,12 @@
         probs_cols, query_cols, contract_first, preferred_element_type=jnp.float32
     )
 
-    gain = norm_gain.astype(jnp.float32)
-    states = hidden_states.astype(jnp.float32)
-    inv_rms = lax.rsqrt(jnp.mean(states * states, axis=1, keepdims=True) + EPS)
-    normed = (states * inv_rms * gain).astype(jnp.bfloat16)
-    labels = lax.broadcasted_iota(jnp.int32, (rows, 1), 0)
-    member = segment_ids[0][None, :] == labels
-    pooled_part = jnp.dot(member.astype(jnp.bfloat16), normed, preferred_element_type=jnp.float32)
-    counts = jnp.sum((group_ids[None, :] == labels).astype(jnp.float32), axis=1)
-    pooled = sum_blocks(pooled_part, "fsdp")
-    mean_pooled = (pooled / counts[:, None]).astype(jnp.bfloat16)
-
-    slice_width = model_width // data_count
-    pieces = mean_pooled.reshape(rows, data_count, slice_width).transpose(1, 0, 2)
-    pieces = lax.all_to_all(pieces, "dp", 0, 0, tiled=True)
-    pooled_cols = pieces.reshape(pair_count, slice_width)
+    mean_part = lax.dot_general(
+        grad_low, proj_weight, contract_last, preferred_element_type=jnp.float32
+    )
+    mean_part, pooled_cols = lax.optimization_barrier((mean_part, pooled_cols))
     proj_grad = lax.dot_general(
         pooled_cols, grad_low_cols, contract_first, preferred_element_type=jnp.float32
-    )
-
-    mean_part = lax.dot_general(
-        grad_low, proj_weight, contract_last, preferred_element_type=jnp.float32
     )
     mean_grad = lax.all_gather(mean_part, "fsdp", axis=1, tiled=True)
     pool_grad = mean_grad / counts[:, None]

time: 142 us -> 137 us (0.965)
  waiting for transfers between devices: 49.9 us -> 14.3 us
  starting transfers between devices: 25 us -> 38 us
  local copies, waits for them, and re-layouts: 20.6 us -> 30.4 us
  matrix products: 9.12 us -> 14.7 us
    ppermute x23, waiting for transfers between devices: 43 us -> 2.87 us  [gather_blocks(): lax.ppermute(x, axis, [(i, (i + s) % n) for i in range(n)])]
    ppermute x0 -> x3, waiting for transfers between devices: none -> 9.32 us  [scatter_sum(): lax.ppermute(piece, axis, [(i, (i + s) % n) for i in range(n)])]
    ppermute x23, starting transfers between devices: 21.5 us -> 28.2 us  [gather_blocks(): lax.ppermute(x, axis, [(i, (i + s) % n) for i in range(n)])]
    unnamed x24 -> x60, local copies, waits for them, and re-layouts: 7.87 us -> 14.3 us
    all_to_all x1, waiting for transfers between devices: 6.86 us -> 2.09 us  [local_small(): pieces = lax.all_to_all(pieces, 'dp', 0, 0, tiled=True)]
    ppermute x0 -> x3, starting transfers between devices: none -> 4 us  [scatter_sum(): lax.ppermute(piece, axis, [(i, (i + s) % n) for i in range(n)])]
    gather x5, local copies, waits for them, and re-layouts: 9.34 us -> 5.85 us  [gather_blocks(): return jnp.take(stack, order, axis=0)]
    another operation x3, other arithmetic: 3.63 us -> 1.04 us  [gather_blocks(): stack = jnp.stack(copies)]
  transfers between devices with their start and end apart: 24 -> 27, of which waited for: 12 -> 5; matrix products, arithmetic and copies ran while one was open for 28% -> 29% of each run, Pallas kernels for 0% -> 0%
where the time goes in v3:
time: 137 us; the launch traced here: 136 us
  starting transfers between devices  38 us (28%)
  local copies, waits for them, and re-layouts  30.4 us (22%)
  blocking collectives  18.6 us (14%)
  other arithmetic  17 us (12%)
  matrix products  14.7 us (11%)
  waiting for transfers between devices  14.3 us (10%)
  between operations  2.91 us (2%)
    ppermute x23, starting transfers between devices, gather_blocks(): lax.ppermute(x, axis, [(i, (i + s) % n) for i in range(n)])  28.2 us
    all_gather x1, blocking collectives, local_small(): mean_grad = lax.all_gather(mean_part, 'fsdp', axis=1, tiled=True)  18.6 us
    unnamed x60, local copies, waits for them, and re-layouts  14.3 us
    ppermute x3, waiting for transfers between devices, scatter_sum(): lax.ppermute(piece, axis, [(i, (i + s) % n) for i in range(n)])  9.32 us
    gather x5, local copies, waits for them, and re-layouts, gather_blocks(): return jnp.take(stack, order, axis=0)  5.85 us
    all_to_all x1, starting transfers between devices, local_small(): pieces = lax.all_to_all(pieces, 'dp', 0, 0, tiled=True)  5.81 us
    ppermute x3, starting transfers between devices, scatter_sum(): lax.ppermute(piece, axis, [(i, (i + s) % n) for i in range(n)])  4 us
    select_n x4, other arithmetic, gather_blocks(): return jnp.take(stack, order, axis=0)  2.99 us
  transfers between devices with their start and end apart: 27, of which 5 were waited for; matrix products, arithmetic and copies ran while one was open for 29% of the time, Pallas kernels for 0%

profile of v3, /device:TPU:0, one launch (start us, length us, event | category | flops | bytes accessed | tf_op | source)
XLA Modules:
  0.0 136.0 jit_solution(12294122701298600128)
XLA Ops:
  0.6 0.9 constant_dynamic-update-slice_fusion.2
  3.7 5.1 %collective-permute-start.5 = (bf16[97,256]{1,0:T(8,128)(2,1)S(1)}, bf16[97,256]{1,0:T(8,128)(2,1)S(1)}, u32[]{:S(2)}, u32[]{:S(2)}) collective-permute-start(bf16[97,256]{1,0:T(8,128)(2,1)S(1)} %constant_dynamic-update-slice_fusion), channel_id=1, source_target_pairs={{0,3},{1,0},{2,1},{3,2},{4,7},{5,4},{6,5},{7,6},{8,11},{9,8},{10,9... | collective-permute-start | bytes 149000 | tf_op jit(solution)/shard_map/ppermute | solution.py:96
  8.8 1.0 collective-permute-start.3
  10.5 1.5 %fusion = f32[128]{0:T(128)S(1)} fusion(bf16[128,4096]{1,0:T(8,128)(2,1)} %param.10), kind=kLoop, calls=%fused_computation.11 | loop fusion | flops 1572736 | bytes 1049088 | tf_op jit(solution)/shard_map/reduce_sum | solution.py:146
  12.6 2.6 %fusion.9 = f32[48,4096]{1,0:T(8,128)} fusion(bf16[128,4096]{1,0:T(8,128)(2,1)} %param.10, f32[4096]{0:T(1024)S(1)} %convert_element_type.77, f32[128]{0:T(128)S(1)} %get-tuple-element.27, s32[128]{0:T(128)} %bitcast.132), kind=kOutput, calls=%fused_computation.24 | convolution fusion | flops 52434944 | bytes 1852416 | tf_op jit(solution)/shard_map/dot_general | solution.py:150
  15.2 1.7 %reshape.237 = f32[48,4,1024]{2,1,0:T(4,128)S(1)} reshape(f32[48,4096]{1,0:T(8,128)} %fusion.9) | data formatting | bytes 1572864 | tf_op jit(solution)/shard_map/reshape | solution.py:154
  18.4 2.8 %collective-permute-start.2 = (f32[48,1024]{1,0:T(8,128)}, f32[48,1024]{1,0:T(8,128)S(1)}, u32[]{:S(2)}, u32[]{:S(2)}) collective-permute-start(f32[48,1024]{1,0:T(8,128)} %bitcast.94), channel_id=1, source_target_pairs={{0,3},{1,0},{2,1},{3,2},{4,7},{5,4},{6,5},{7,6},{8,11},{9,8},{10,9... | collective-permute-start | bytes 589832 | tf_op jit(solution)/shard_map/ppermute | solution.py:113
  21.9 1.1 collective-permute-start.1
  24.8 1.5 %collective-permute-start.10 = (bf16[4,97,256]{2,1,0:T(8,128)(2,1)S(1)}, bf16[4,97,256]{2,1,0:T(8,128)(2,1)S(1)}, u32[]{:S(2)}, u32[]{:S(2)}) collective-permute-start(bf16[4,97,256]{2,1,0:T(8,128)(2,1)S(1)} %broadcast_select_fusion.1), channel_id=1, source_target_pairs={{0,8},{4,12},{8,16},{12,20},{16,24},{20,28},{24,0},{28,4},{1,9},{5... | collective-permute-start | bytes 595976 | tf_op jit(solution)/shard_map/ppermute | solution.py:96
  27.4 2.4 %collective-permute-start.11 = (bf16[4,97,256]{2,1,0:T(8,128)(2,1)S(1)}, bf16[4,97,256]{2,1,0:T(8,128)(2,1)}, u32[]{:S(2)}, u32[]{:S(2)}) collective-permute-start(bf16[4,97,256]{2,1,0:T(8,128)(2,1)S(1)} %broadcast_select_fusion.1), channel_id=1, source_target_pairs={{0,12},{4,16},{8,20},{12,24},{16,28},{20,0},{24,4},{28,8},{1,13},{... | collective-permute-start | bytes 595976 | tf_op jit(solution)/shard_map/ppermute | solution.py:96
  29.7 9.3 %collective-permute-done.1 = f32[48,1024]{1,0:T(8,128)} collective-permute-done((f32[48,1024]{1,0:T(8,128)}, f32[48,1024]{1,0:T(8,128)}, u32[]{:S(2)}, u32[]{:S(2)}) %collective-permute-start.1) | collective-permute-done | bytes 196640 | tf_op jit(solution)/shard_map/ppermute | solution.py:113
  39.0 1.5 %collective-permute-start.12 = (bf16[4,97,256]{2,1,0:T(8,128)(2,1)S(1)}, bf16[4,97,256]{2,1,0:T(8,128)(2,1)}, u32[]{:S(2)}, u32[]{:S(2)}) collective-permute-start(bf16[4,97,256]{2,1,0:T(8,128)(2,1)S(1)} %broadcast_select_fusion.1), channel_id=1, source_target_pairs={{0,16},{4,20},{8,24},{12,28},{16,0},{20,4},{24,8},{28,12},{1,17},{... | collective-permute-start | bytes 595976 | tf_op jit(solution)/shard_map/ppermute | solution.py:96
  40.6 1.2 pad_maximum_fusion
  41.8 1.5 %gather_fusion = f32[4,48,1024]{2,1,0:T(8,128)} fusion(f32[4,48,1024]{2,1,0:T(8,128)S(1)} %pad_maximum_fusion, s32[1024]{0:T(1024)S(1)} %pad_clamp_fusion.1), kind=kCustom, calls=%fused_computation | custom fusion | bytes 1572880 | tf_op jit(solution)/shard_map/jit(_take)/gather | solution.py:115
  43.2 1.3 select_reduce_fusion
  44.7 1.5 %collective-permute-start.14 = (bf16[4,97,256]{2,1,0:T(8,128)(2,1)S(1)}, bf16[4,97,256]{2,1,0:T(8,128)(2,1)S(1)}, u32[]{:S(2)}, u32[]{:S(2)}) collective-permute-start(bf16[4,97,256]{2,1,0:T(8,128)(2,1)S(1)} %broadcast_select_fusion.1), channel_id=1, source_target_pairs={{0,24},{4,28},{8,0},{12,4},{16,8},{20,12},{24,16},{28,20},{1,25},{... | collective-permute-start | bytes 595976 | tf_op jit(solution)/shard_map/ppermute | solution.py:96
  46.2 1.6 %bitcast_dynamic-update-slice_fusion.6 = bf16[8,4,97,256]{3,2,1,0:T(8,128)(2,1)} fusion(bf16[8,4,97,256]{3,2,1,0:T(8,128)(2,1)} %fusion.16, bf16[4,97,256]{2,1,0:T(8,128)(2,1)} %collective-permute-done.9), kind=kLoop, calls=%fused_computation.49 | loop fusion | bytes 425984
  47.8 2.4 %collective-permute-start.15 = (bf16[4,97,256]{2,1,0:T(8,128)(2,1)S(1)}, bf16[4,97,256]{2,1,0:T(8,128)(2,1)S(1)}, u32[]{:S(2)}, u32[]{:S(2)}) collective-permute-start(bf16[4,97,256]{2,1,0:T(8,128)(2,1)S(1)} %broadcast_select_fusion.1), channel_id=1, source_target_pairs={{0,28},{4,0},{8,4},{12,8},{16,12},{20,16},{24,20},{28,24},{1,29},{... | collective-permute-start | bytes 595976 | tf_op jit(solution)/shard_map/ppermute | solution.py:96
  51.0 1.6 %bitcast_dynamic-update-slice_fusion.4 = bf16[8,4,97,256]{3,2,1,0:T(8,128)(2,1)} fusion(bf16[8,4,97,256]{3,2,1,0:T(8,128)(2,1)} %bitcast_dynamic-update-slice_fusion.5, bf16[4,97,256]{2,1,0:T(8,128)(2,1)} %collective-permute-done.11), kind=kLoop, calls=%fused_computation.47 | loop fusion | bytes 425984
  53.1 1.6 %bitcast_dynamic-update-slice_fusion.3 = bf16[8,4,97,256]{3,2,1,0:T(8,128)(2,1)} fusion(bf16[8,4,97,256]{3,2,1,0:T(8,128)(2,1)} %bitcast_dynamic-update-slice_fusion.4, bf16[4,97,256]{2,1,0:T(8,128)(2,1)} %collective-permute-done.12), kind=kLoop, calls=%fused_computation.46 | loop fusion | bytes 425984
  54.8 2.0 %collective-permute-start.6 = (bf16[48,1024]{1,0:T(8,128)(2,1)S(1)}, bf16[48,1024]{1,0:T(8,128)(2,1)S(1)}, u32[]{:S(2)}, u32[]{:S(2)}) collective-permute-start(bf16[48,1024]{1,0:T(8,128)(2,1)S(1)} %divide_convert_fusion), channel_id=1, source_target_pairs={{0,1},{1,2},{2,3},{3,0},{4,5},{5,6},{6,7},{7,4},{8,9},{9,10},{10,1... | collective-permute-start | bytes 294920 | tf_op jit(solution)/shard_map/ppermute | solution.py:96
  56.8 1.6 %bitcast_dynamic-update-slice_fusion.2 = bf16[8,4,97,256]{3,2,1,0:T(8,128)(2,1)} fusion(bf16[8,4,97,256]{3,2,1,0:T(8,128)(2,1)} %bitcast_dynamic-update-slice_fusion.3, bf16[4,97,256]{2,1,0:T(8,128)(2,1)} %collective-permute-done.13), kind=kLoop, calls=%fused_computation.45 | loop fusion | bytes 425984
  59.9 3.3 %gather_fusion.3 = bf16[8,4,97,256]{3,2,1,0:T(8,128)(2,1)} fusion(bf16[8,4,97,256]{3,2,1,0:T(8,128)(2,1)} %bitcast_dynamic-update-slice_fusion, s32[1024]{0:T(1024)S(1)} %pad_clamp_fusion), kind=kCustom, calls=%fused_computation.3 | custom fusion | bytes 3178528 | tf_op jit(solution)/shard_map/jit(_take)/gather | solution.py:100
  63.2 2.9 %broadcast_select_fusion = bf16[8,4,97,256]{3,2,1,0:T(8,128)(2,1)} fusion(bf16[8,4,97,256]{3,2,1,0:T(8,128)(2,1)} %gather_fusion.3, pred[8]{0:T(512)(128)(4,1)S(1)} %compare_and_fusion), kind=kLoop, calls=%fused_computation.20 | loop fusion | flops 794624 | bytes 3178504 | tf_op jit(solution)/shard_map/jit(_take)/select_n | solution.py:100
  66.7 0.9 pad_maximum_fusion.1
  68.4 1.5 %slice_bitcast_fusion = (bf16[8,48,4,256]{3,1,2,0:T(8,128)(2,1)S(1)}, bf16[8,48,4,256]{3,1,2,0:T(8,128)(2,1)S(1)}) fusion(bf16[8,4,97,256]{3,2,1,0:T(8,128)(2,1)} %broadcast_select_fusion), kind=kLoop, calls=%fused_computation.30 | loop fusion | bytes 3145728 | tf_op jit(solution)/shard_map/transpose | solution.py:167
  69.9 0.9 slice_convert_fusion
  71.2 1.0 copy.32
  73.0 1.7 %fusion.37 = (f32[384]{0:T(512)S(1)}, f32[384,384]{0,1:T(8,128)S(1)}) fusion(bf16[384,1024]{1,0:T(8,128)(2,1)} %bitcast.106, bf16[384,1024]{1,0:T(8,128)(2,1)S(1)} %bitcast.102), kind=kOutput, calls=%fused_computation.130 | convolution fusion | flops 302284416 | bytes 2164224 | tf_op jit(solution)/shard_map/dot_general | solution.py:176
  75.7 1.8 %convolution_multiply_fusion = f32[384,1024]{1,0:T(8,128)} fusion(bf16[384,384]{0,1:T(8,128)(2,1)S(1)} %subtract_convert_fusion, bf16[384,1024]{1,0:T(8,128)(2,1)S(1)} %bitcast.103), kind=kOutput, calls=%fused_computation.21 | convolution fusion | flops 302383104 | bytes 2654208 | tf_op jit(solution)/shard_map/dot_general | solution.py:188
  78.3 5.8 %all-to-all-start = ((bf16[8,48,512]{2,1,0:T(8,128)(2,1)}), bf16[8,48,512]{2,1,0:T(8,128)(2,1)S(1)}, u32[]{:S(2)}, u32[]{:S(2)}) async-start(bf16[8,48,512]{2,1,0:T(8,128)(2,1)} %bitcast.93), calls=%async_computation | async-start | bytes 786432 | tf_op jit(solution)/shard_map/all_to_all | solution.py:163
  84.8 1.4 %dynamic_slice.23 = f32[48,256]{1,0:T(8,128)} dynamic-slice(f32[384,1024]{1,0:T(8,128)} %convolution_multiply_fusion, s32[]{:T(128)S(6)} %select_n.196, s32[]{:T(128)S(6)} %select_n.197), dynamic_slice_sizes={48,256} | dynamic-slice | bytes 98308 | tf_op jit(solution)/shard_map/dynamic_slice | solution.py:189
  86.2 1.7 %convolution_multiply_fusion.2 = f32[48,256]{1,0:T(8,128)} fusion(bf16[384,1024]{1,0:T(8,128)(2,1)} %bitcast.107, s32[]{:T(128)S(6)} %select_n.197, bf16[384,384]{0,1:T(8,128)(2,1)} %copy-done.2, s32[]{:T(128)S(6)} %select_n.196), kind=kOutput, calls=%fused_computation.23 | convolution fusion | flops 9449472 | bytes 282632 | tf_op jit(solution)/shard_map/dot_general | solution.py:196
  87.9 2.4 %fusion.20 = f32[48,1024]{1,0:T(8,128)} fusion(bf16[1024,1024]{1,0:T(8,128)(2,1)S(1)} %copy-done, f32[384,1024]{1,0:T(8,128)} %convolution_multiply_fusion, s32[]{:T(128)S(6)} %select_n.196), kind=kOutput, calls=%fused_computation.64 | convolution fusion | flops 100663296 | bytes 2392068 | tf_op jit(solution)/shard_map/dot_general | solution.py:200
  90.4 2.1 %all-to-all-done = bf16[8,48,512]{2,1,0:T(8,128)(2,1)S(1)} async-done(((bf16[8,48,512]{2,1,0:T(8,128)(2,1)}), bf16[8,48,512]{2,1,0:T(8,128)(2,1)S(1)}, u32[]{:S(2)}, u32[]{:S(2)}) %all-to-all-start) | async-done | bytes 393248 | tf_op jit(solution)/shard_map/all_to_all | solution.py:163
  92.4 18.6 %all_gather.3 = f32[48,4096]{1,0:T(8,128)S(1)} all-gather(f32[48,1024]{1,0:T(8,128)} %fusion.20), channel_id=1, replica_groups=mesh['dp'=8,'fsdp'=4] {'fsdp'}, dimensions={1}, use_global_device_ids=true | all-gather | bytes 983040 | tf_op jit(solution)/shard_map/all_gather | solution.py:207
  111.0 2.3 %fusion.8 = (f32[4096]{0:T(1024)S(1)}, f32[128]{0:T(128)S(1)}, f32[128,4096]{1,0:T(8,128)S(1)}) fusion(bf16[128,4096]{1,0:T(8,128)(2,1)S(1)} %copy-done.1, f32[128]{0:T(128)} %copy-done.20, f32[4096]{0:T(1024)S(1)} %convert_element_type.77, f32[48,4096]{1,0:T(8,128)S(1)} %all_gather.3, f32[48]{0:T(128)} %copy-done.17, s32[128]{0:T(128)} %bitcast.133), kind=kOutput, calls=%fused_computation.19 | convolution fusion | flops 305858432 | bytes 3966656 | tf_op jit(solution)/shard_map/dot_general | solution.py:209
  114.2 1.6 %collective-permute-start.18 = (f32[4096]{0:T(1024)S(1)}, f32[4096]{0:T(1024)S(1)}, u32[]{:S(2)}, u32[]{:S(2)}) collective-permute-start(f32[4096]{0:T(1024)S(1)} %get-tuple-element.14), channel_id=1, source_target_pairs={{0,12},{4,16},{8,20},{12,24},{16,28},{20,0},{24,4},{28,8},{1,13},{... | collective-permute-start | bytes 49160 | tf_op jit(solution)/shard_map/ppermute | solution.py:96
  115.9 1.2 collective-permute-start.19
  117.5 1.9 %collective-permute-start.21 = (f32[4096]{0:T(1024)S(1)}, f32[4096]{0:T(1024)S(1)}, u32[]{:S(2)}, u32[]{:S(2)}) collective-permute-start(f32[4096]{0:T(1024)S(1)} %get-tuple-element.14), channel_id=1, source_target_pairs={{0,24},{4,28},{8,0},{12,4},{16,8},{20,12},{24,16},{28,20},{1,25},{... | collective-permute-start | bytes 49160 | tf_op jit(solution)/shard_map/ppermute | solution.py:96
  119.3 1.6 %collective-permute-start.22 = (f32[4096]{0:T(1024)S(1)}, f32[4096]{0:T(1024)S(1)}, u32[]{:S(2)}, u32[]{:S(2)}) collective-permute-start(f32[4096]{0:T(1024)S(1)} %get-tuple-element.14), channel_id=1, source_target_pairs={{0,28},{4,0},{8,4},{12,8},{16,12},{20,16},{24,20},{28,24},{1,29},{... | collective-permute-start | bytes 49160 | tf_op jit(solution)/shard_map/ppermute | solution.py:96
  121.0 1.6 %fusion.5 = bf16[128,4096]{1,0:T(8,128)(2,1)} fusion(bf16[128,4096]{1,0:T(8,128)(2,1)S(1)} %copy-done.1, f32[128,4096]{1,0:T(8,128)S(1)} %get-tuple-element.32, f32[128]{0:T(128)S(1)} %broadcast_multiply_fusion, f32[128]{0:T(128)S(1)} %copy-done.19, f32[4096]{0:T(1024)S(1)} %convert_element_type.77, f32[128]{0:T(128)S(1)} %copy-done.21), kind=kLoop, calls=%fused_computation.16 | loop fusion | flops 3670016 | bytes 4212224 | tf_op jit(solution)/shard_map/convert_element_type | solution.py:219
  123.3 1.0 stack.137
  125.8 2.0 %collective-permute-start.25 = (f32[4096]{0:T(1024)S(1)}, f32[4096]{0:T(1024)S(1)}, u32[]{:S(2)}, u32[]{:S(2)}) collective-permute-start(f32[4096]{0:T(1024)S(1)} %select_reduce_fusion.2), channel_id=1, source_target_pairs={{0,3},{1,0},{2,1},{3,2},{4,7},{5,4},{6,5},{7,6},{8,11},{9,8},{10,9... | collective-permute-start | bytes 49160 | tf_op jit(solution)/shard_map/ppermute | solution.py:96
  127.8 0.9 collective-permute-start.23
  128.7 2.1 %fusion.17 = f32[512,256]{1,0:T(8,128)} fusion(bf16[384,512]{1,0:T(8,128)(2,1)S(1)} %bitcast.105, f32[384,1024]{1,0:T(8,128)} %convolution_multiply_fusion, s32[]{:T(128)S(6)} %select_n.197), kind=kOutput, calls=%fused_computation.53 | convolution fusion | flops 100663296 | bytes 1114116 | tf_op jit(solution)/shard_map/dot_general | solution.py:204
  130.9 1.6 %collective-permute-done.24 = f32[4096]{0:T(1024)S(1)} collective-permute-done((f32[4096]{0:T(1024)S(1)}, f32[4096]{0:T(1024)S(1)}, u32[]{:S(2)}, u32[]{:S(2)}) %collective-permute-start.24) | collective-permute-done | bytes 16416 | tf_op jit(solution)/shard_map/ppermute | solution.py:96
  132.4 0.9 collective-permute-done.23
  (127 shorter events, 20.3 us)
Async XLA Ops:
  0.6 87.3 %copy-start = (bf16[1024,1024]{1,0:T(8,128)(2,1)S(1)}, bf16[1024,1024]{1,0:T(8,128)(2,1)}, u32[]{:S(2)}) copy-start(bf16[1024,1024]{1,0:T(8,128)(2,1)} %param.13) | copy-start | bytes 6291460
  3.7 20.3 %collective-permute-start.5 = (bf16[97,256]{1,0:T(8,128)(2,1)S(1)}, bf16[97,256]{1,0:T(8,128)(2,1)S(1)}, u32[]{:S(2)}, u32[]{:S(2)}) collective-permute-start(bf16[97,256]{1,0:T(8,128)(2,1)S(1)} %constant_dynamic-update-slice_fusion), channel_id=1, source_target_pairs={{0,3},{1,0},{2,1},{3,2},{4,7},{5,4},{6,5},{7,6},{8,11},{9,8},{10,9... | collective-permute-start | bytes 149000 | tf_op jit(solution)/shard_map/ppermute | solution.py:96
  8.8 15.3 %collective-permute-start.4 = (bf16[97,256]{1,0:T(8,128)(2,1)S(1)}, bf16[97,256]{1,0:T(8,128)(2,1)S(1)}, u32[]{:S(2)}, u32[]{:S(2)}) collective-permute-start(bf16[97,256]{1,0:T(8,128)(2,1)S(1)} %constant_dynamic-update-slice_fusion), channel_id=1, source_target_pairs={{0,2},{1,3},{2,0},{3,1},{4,6},{5,7},{6,4},{7,5},{8,10},{9,11},{10,... | collective-permute-start | bytes 149000 | tf_op jit(solution)/shard_map/ppermute | solution.py:96
  8.8 15.3 %collective-permute-start.3 = (bf16[97,256]{1,0:T(8,128)(2,1)S(1)}, bf16[97,256]{1,0:T(8,128)(2,1)S(1)}, u32[]{:S(2)}, u32[]{:S(2)}) collective-permute-start(bf16[97,256]{1,0:T(8,128)(2,1)S(1)} %constant_dynamic-update-slice_fusion), channel_id=1, source_target_pairs={{0,1},{1,2},{2,3},{3,0},{4,5},{5,6},{6,7},{7,4},{8,9},{9,10},{10,1... | collective-permute-start | bytes 149000 | tf_op jit(solution)/shard_map/ppermute | solution.py:96
  12.6 4.3 %copy-start.20 = (f32[128]{0:T(128)}, f32[128]{0:T(128)S(1)}, u32[]{:S(2)}) copy-start(f32[128]{0:T(128)S(1)} %get-tuple-element.27) | copy-start | bytes 1540
  18.4 9.0 %collective-permute-start.2 = (f32[48,1024]{1,0:T(8,128)}, f32[48,1024]{1,0:T(8,128)S(1)}, u32[]{:S(2)}, u32[]{:S(2)}) collective-permute-start(f32[48,1024]{1,0:T(8,128)} %bitcast.94), channel_id=1, source_target_pairs={{0,3},{1,0},{2,1},{3,2},{4,7},{5,4},{6,5},{7,6},{8,11},{9,8},{10,9... | collective-permute-start | bytes 589832 | tf_op jit(solution)/shard_map/ppermute | solution.py:113
  21.9 17.1 %collective-permute-start.1 = (f32[48,1024]{1,0:T(8,128)}, f32[48,1024]{1,0:T(8,128)}, u32[]{:S(2)}, u32[]{:S(2)}) collective-permute-start(f32[48,1024]{1,0:T(8,128)} %bitcast.95), channel_id=1, source_target_pairs={{0,2},{1,3},{2,0},{3,1},{4,6},{5,7},{6,4},{7,5},{8,10},{9,11},{10,... | collective-permute-start | bytes 589832 | tf_op jit(solution)/shard_map/ppermute | solution.py:113
  23.1 45.2 %copy-start.13 = (pred[4]{0:T(512)(128)(4,1)}, pred[4]{0:T(512)(128)(4,1)S(1)}, u32[]{:S(2)}) copy-start(pred[4]{0:T(512)(128)(4,1)S(1)} %compare_and_fusion.1) | copy-start | bytes 16
  23.1 44.6 %copy-start.15 = (s32[1024]{0:T(1024)}, s32[1024]{0:T(1024)S(1)}, u32[]{:S(2)}) copy-start(s32[1024]{0:T(1024)S(1)} %pad_clamp_fusion.1) | copy-start | bytes 12292
  23.1 36.7 %copy-start.16 = (s32[1024]{0:T(1024)}, s32[1024]{0:T(1024)S(1)}, u32[]{:S(2)}) copy-start(s32[1024]{0:T(1024)S(1)} %pad_clamp_fusion) | copy-start | bytes 12292
  23.2 40.0 %copy-start.18 = (pred[8]{0:T(512)(128)(4,1)}, pred[8]{0:T(512)(128)(4,1)S(1)}, u32[]{:S(2)}) copy-start(pred[8]{0:T(512)(128)(4,1)S(1)} %compare_and_fusion) | copy-start | bytes 28
  24.0 16.6 %collective-permute-start = (f32[48,1024]{1,0:T(8,128)}, f32[48,1024]{1,0:T(8,128)}, u32[]{:S(2)}, u32[]{:S(2)}) collective-permute-start(f32[48,1024]{1,0:T(8,128)} %bitcast.96), channel_id=1, source_target_pairs={{0,1},{1,2},{2,3},{3,0},{4,5},{5,6},{6,7},{7,4},{8,9},{9,10},{10,1... | collective-permute-start | bytes 589832 | tf_op jit(solution)/shard_map/ppermute | solution.py:113
  24.8 19.9 %collective-permute-start.9 = (bf16[4,97,256]{2,1,0:T(8,128)(2,1)S(1)}, bf16[4,97,256]{2,1,0:T(8,128)(2,1)}, u32[]{:S(2)}, u32[]{:S(2)}) collective-permute-start(bf16[4,97,256]{2,1,0:T(8,128)(2,1)S(1)} %broadcast_select_fusion.1), channel_id=1, source_target_pairs={{0,4},{4,8},{8,12},{12,16},{16,20},{20,24},{24,28},{28,0},{1,5},{5... | collective-permute-start | bytes 595976 | tf_op jit(solution)/shard_map/ppermute | solution.py:96
  24.8 23.0 %collective-permute-start.10 = (bf16[4,97,256]{2,1,0:T(8,128)(2,1)S(1)}, bf16[4,97,256]{2,1,0:T(8,128)(2,1)S(1)}, u32[]{:S(2)}, u32[]{:S(2)}) collective-permute-start(bf16[4,97,256]{2,1,0:T(8,128)(2,1)S(1)} %broadcast_select_fusion.1), channel_id=1, source_target_pairs={{0,8},{4,12},{8,16},{12,20},{16,24},{20,28},{24,0},{28,4},{1,9},{5... | collective-permute-start | bytes 595976 | tf_op jit(solution)/shard_map/ppermute | solution.py:96
  26.6 18.0 %copy-start.17 = (f32[48]{0:T(128)}, f32[48]{0:T(128)S(1)}, u32[]{:S(2)}) copy-start(f32[48]{0:T(128)S(1)} %convert_reduce_fusion) | copy-start | bytes 580
  27.4 13.2 %copy-start.3 = (f32[48,1024]{1,0:T(8,128)}, f32[48,1024]{1,0:T(8,128)S(1)}, u32[]{:S(2)}) copy-start(f32[48,1024]{1,0:T(8,128)S(1)} %collective-permute-done.2) | copy-start | bytes 589828
  27.4 23.6 %collective-permute-start.11 = (bf16[4,97,256]{2,1,0:T(8,128)(2,1)S(1)}, bf16[4,97,256]{2,1,0:T(8,128)(2,1)}, u32[]{:S(2)}, u32[]{:S(2)}) collective-permute-start(bf16[4,97,256]{2,1,0:T(8,128)(2,1)S(1)} %broadcast_select_fusion.1), channel_id=1, source_target_pairs={{0,12},{4,16},{8,20},{12,24},{16,28},{20,0},{24,4},{28,8},{1,13},{... | collective-permute-start | bytes 595976 | tf_op jit(solution)/shard_map/ppermute | solution.py:96
  39.0 13.5 %collective-permute-start.12 = (bf16[4,97,256]{2,1,0:T(8,128)(2,1)S(1)}, bf16[4,97,256]{2,1,0:T(8,128)(2,1)}, u32[]{:S(2)}, u32[]{:S(2)}) collective-permute-start(bf16[4,97,256]{2,1,0:T(8,128)(2,1)S(1)} %broadcast_select_fusion.1), channel_id=1, source_target_pairs={{0,16},{4,20},{8,24},{12,28},{16,0},{20,4},{24,8},{28,12},{1,17},{... | collective-permute-start | bytes 595976 | tf_op jit(solution)/shard_map/ppermute | solution.py:96
  40.6 14.2 %collective-permute-start.13 = (bf16[4,97,256]{2,1,0:T(8,128)(2,1)S(1)}, bf16[4,97,256]{2,1,0:T(8,128)(2,1)}, u32[]{:S(2)}, u32[]{:S(2)}) collective-permute-start(bf16[4,97,256]{2,1,0:T(8,128)(2,1)S(1)} %broadcast_select_fusion.1), channel_id=1, source_target_pairs={{0,20},{4,24},{8,28},{12,0},{16,4},{20,8},{24,12},{28,16},{1,21},{... | collective-permute-start | bytes 595976 | tf_op jit(solution)/shard_map/ppermute | solution.py:96
  44.7 13.7 %collective-permute-start.14 = (bf16[4,97,256]{2,1,0:T(8,128)(2,1)S(1)}, bf16[4,97,256]{2,1,0:T(8,128)(2,1)S(1)}, u32[]{:S(2)}, u32[]{:S(2)}) collective-permute-start(bf16[4,97,256]{2,1,0:T(8,128)(2,1)S(1)} %broadcast_select_fusion.1), channel_id=1, source_target_pairs={{0,24},{4,28},{8,0},{12,4},{16,8},{20,12},{24,16},{28,20},{1,25},{... | collective-permute-start | bytes 595976 | tf_op jit(solution)/shard_map/ppermute | solution.py:96
  47.8 11.3 %collective-permute-start.15 = (bf16[4,97,256]{2,1,0:T(8,128)(2,1)S(1)}, bf16[4,97,256]{2,1,0:T(8,128)(2,1)S(1)}, u32[]{:S(2)}, u32[]{:S(2)}) collective-permute-start(bf16[4,97,256]{2,1,0:T(8,128)(2,1)S(1)} %broadcast_select_fusion.1), channel_id=1, source_target_pairs={{0,28},{4,0},{8,4},{12,8},{16,12},{20,16},{24,20},{28,24},{1,29},{... | collective-permute-start | bytes 595976 | tf_op jit(solution)/shard_map/ppermute | solution.py:96
  51.0 15.1 %collective-permute-start.8 = (bf16[48,1024]{1,0:T(8,128)(2,1)S(1)}, bf16[48,1024]{1,0:T(8,128)(2,1)S(1)}, u32[]{:S(2)}, u32[]{:S(2)}) collective-permute-start(bf16[48,1024]{1,0:T(8,128)(2,1)S(1)} %divide_convert_fusion), channel_id=1, source_target_pairs={{0,3},{1,0},{2,1},{3,2},{4,7},{5,4},{6,5},{7,6},{8,11},{9,8},{10,9... | collective-permute-start | bytes 294920 | tf_op jit(solution)/shard_map/ppermute | solution.py:96
  52.6 13.5 %collective-permute-start.7 = (bf16[48,1024]{1,0:T(8,128)(2,1)S(1)}, bf16[48,1024]{1,0:T(8,128)(2,1)S(1)}, u32[]{:S(2)}, u32[]{:S(2)}) collective-permute-start(bf16[48,1024]{1,0:T(8,128)(2,1)S(1)} %divide_convert_fusion), channel_id=1, source_target_pairs={{0,2},{1,3},{2,0},{3,1},{4,6},{5,7},{6,4},{7,5},{8,10},{9,11},{10,... | collective-permute-start | bytes 294920 | tf_op jit(solution)/shard_map/ppermute | solution.py:96
  54.8 11.3 %collective-permute-start.6 = (bf16[48,1024]{1,0:T(8,128)(2,1)S(1)}, bf16[48,1024]{1,0:T(8,128)(2,1)S(1)}, u32[]{:S(2)}, u32[]{:S(2)}) collective-permute-start(bf16[48,1024]{1,0:T(8,128)(2,1)S(1)} %divide_convert_fusion), channel_id=1, source_target_pairs={{0,1},{1,2},{2,3},{3,0},{4,5},{5,6},{6,7},{7,4},{8,9},{9,10},{10,1... | collective-permute-start | bytes 294920 | tf_op jit(solution)/shard_map/ppermute | solution.py:96
  66.0 0.6 copy-start.4
  75.7 2.6 %copy-start.2 = (bf16[384,384]{0,1:T(8,128)(2,1)}, bf16[384,384]{0,1:T(8,128)(2,1)S(1)}, u32[]{:S(2)}) copy-start(bf16[384,384]{0,1:T(8,128)(2,1)S(1)} %subtract_convert_fusion) | copy-start | bytes 884740
  78.3 14.2 %all-to-all-start = ((bf16[8,48,512]{2,1,0:T(8,128)(2,1)}), bf16[8,48,512]{2,1,0:T(8,128)(2,1)S(1)}, u32[]{:S(2)}, u32[]{:S(2)}) async-start(bf16[8,48,512]{2,1,0:T(8,128)(2,1)} %bitcast.93), calls=%async_computation | async-start | bytes 786432 | tf_op jit(solution)/shard_map/all_to_all | solution.py:163
  87.9 23.1 %copy-start.1 = (bf16[128,4096]{1,0:T(8,128)(2,1)S(1)}, bf16[128,4096]{1,0:T(8,128)(2,1)}, u32[]{:S(2)}) copy-start(bf16[128,4096]{1,0:T(8,128)(2,1)} %param.10) | copy-start | bytes 3145732
  111.0 9.9 %copy-start.19 = (f32[128]{0:T(128)S(1)}, f32[128]{0:T(128)}, u32[]{:S(2)}) copy-start(f32[128]{0:T(128)} %get-tuple-element.26) | copy-start | bytes 1540
  111.0 9.9 %copy-start.21 = (f32[128]{0:T(128)S(1)}, f32[128]{0:T(128)}, u32[]{:S(2)}) copy-start(f32[128]{0:T(128)} %copy-done.20) | copy-start | bytes 1540
  113.3 9.3 %copy-start.5 = (f32[4096]{0:T(1024)}, f32[4096]{0:T(1024)S(1)}, u32[]{:S(2)}) copy-start(f32[4096]{0:T(1024)S(1)} %get-tuple-element.14) | copy-start | bytes 49156
  113.3 4.1 %collective-permute-start.16 = (f32[4096]{0:T(1024)S(1)}, f32[4096]{0:T(1024)S(1)}, u32[]{:S(2)}, u32[]{:S(2)}) collective-permute-start(f32[4096]{0:T(1024)S(1)} %get-tuple-element.14), channel_id=1, source_target_pairs={{0,4},{4,8},{8,12},{12,16},{16,20},{20,24},{24,28},{28,0},{1,5},{5... | collective-permute-start | bytes 49160 | tf_op jit(solution)/shard_map/ppermute | solution.py:96
  113.4 5.9 %collective-permute-start.17 = (f32[4096]{0:T(1024)S(1)}, f32[4096]{0:T(1024)S(1)}, u32[]{:S(2)}, u32[]{:S(2)}) collective-permute-start(f32[4096]{0:T(1024)S(1)} %get-tuple-element.14), channel_id=1, source_target_pairs={{0,8},{4,12},{8,16},{12,20},{16,24},{20,28},{24,0},{28,4},{1,9},{5... | collective-permute-start | bytes 49160 | tf_op jit(solution)/shard_map/ppermute | solution.py:96
  114.2 8.4 %collective-permute-start.18 = (f32[4096]{0:T(1024)S(1)}, f32[4096]{0:T(1024)S(1)}, u32[]{:S(2)}, u32[]{:S(2)}) collective-permute-start(f32[4096]{0:T(1024)S(1)} %get-tuple-element.14), channel_id=1, source_target_pairs={{0,12},{4,16},{8,20},{12,24},{16,28},{20,0},{24,4},{28,8},{1,13},{... | collective-permute-start | bytes 49160 | tf_op jit(solution)/shard_map/ppermute | solution.py:96
  115.9 6.7 %collective-permute-start.19 = (f32[4096]{0:T(1024)S(1)}, f32[4096]{0:T(1024)S(1)}, u32[]{:S(2)}, u32[]{:S(2)}) collective-permute-start(f32[4096]{0:T(1024)S(1)} %get-tuple-element.14), channel_id=1, source_target_pairs={{0,16},{4,20},{8,24},{12,28},{16,0},{20,4},{24,8},{28,12},{1,17},{... | collective-permute-start | bytes 49160 | tf_op jit(solution)/shard_map/ppermute | solution.py:96
  117.1 5.5 %collective-permute-start.20 = (f32[4096]{0:T(1024)S(1)}, f32[4096]{0:T(1024)S(1)}, u32[]{:S(2)}, u32[]{:S(2)}) collective-permute-start(f32[4096]{0:T(1024)S(1)} %get-tuple-element.14), channel_id=1, source_target_pairs={{0,20},{4,24},{8,28},{12,0},{16,4},{20,8},{24,12},{28,16},{1,21},{... | collective-permute-start | bytes 49160 | tf_op jit(solution)/shard_map/ppermute | solution.py:96
  117.5 5.1 %copy-start.6 = (f32[4096]{0:T(1024)}, f32[4096]{0:T(1024)S(1)}, u32[]{:S(2)}) copy-start(f32[4096]{0:T(1024)S(1)} %collective-permute-done.16) | copy-start | bytes 49156
  117.5 5.2 %collective-permute-start.21 = (f32[4096]{0:T(1024)S(1)}, f32[4096]{0:T(1024)S(1)}, u32[]{:S(2)}, u32[]{:S(2)}) collective-permute-start(f32[4096]{0:T(1024)S(1)} %get-tuple-element.14), channel_id=1, source_target_pairs={{0,24},{4,28},{8,0},{12,4},{16,8},{20,12},{24,16},{28,20},{1,25},{... | collective-permute-start | bytes 49160 | tf_op jit(solution)/shard_map/ppermute | solution.py:96
  119.3 3.3 %copy-start.7 = (f32[4096]{0:T(1024)}, f32[4096]{0:T(1024)S(1)}, u32[]{:S(2)}) copy-start(f32[4096]{0:T(1024)S(1)} %collective-permute-done.17) | copy-start | bytes 49156
  119.3 3.4 %collective-permute-start.22 = (f32[4096]{0:T(1024)S(1)}, f32[4096]{0:T(1024)S(1)}, u32[]{:S(2)}, u32[]{:S(2)}) collective-permute-start(f32[4096]{0:T(1024)S(1)} %get-tuple-element.14), channel_id=1, source_target_pairs={{0,28},{4,0},{8,4},{12,8},{16,12},{20,16},{24,20},{28,24},{1,29},{... | collective-permute-start | bytes 49160 | tf_op jit(solution)/shard_map/ppermute | solution.py:96
  122.6 0.6 copy-start.9
  122.6 0.6 copy-start.10
  122.7 0.6 copy-start.11
  122.7 0.6 copy-start.12
  123.3 10.8 %copy-start.14 = (pred[4]{0:T(512)(128)(4,1)S(1)}, pred[4]{0:T(512)(128)(4,1)}, u32[]{:S(2)}) copy-start(pred[4]{0:T(512)(128)(4,1)} %copy-done.13) | copy-start | bytes 16
  125.8 5.0 %collective-permute-start.25 = (f32[4096]{0:T(1024)S(1)}, f32[4096]{0:T(1024)S(1)}, u32[]{:S(2)}, u32[]{:S(2)}) collective-permute-start(f32[4096]{0:T(1024)S(1)} %select_reduce_fusion.2), channel_id=1, source_target_pairs={{0,3},{1,0},{2,1},{3,2},{4,7},{5,4},{6,5},{7,6},{8,11},{9,8},{10,9... | collective-permute-start | bytes 49160 | tf_op jit(solution)/shard_map/ppermute | solution.py:96
  127.8 4.6 %collective-permute-start.24 = (f32[4096]{0:T(1024)S(1)}, f32[4096]{0:T(1024)S(1)}, u32[]{:S(2)}, u32[]{:S(2)}) collective-permute-start(f32[4096]{0:T(1024)S(1)} %select_reduce_fusion.2), channel_id=1, source_target_pairs={{0,2},{1,3},{2,0},{3,1},{4,6},{5,7},{6,4},{7,5},{8,10},{9,11},{10,... | collective-permute-start | bytes 49160 | tf_op jit(solution)/shard_map/ppermute | solution.py:96
  127.8 5.5 %collective-permute-start.23 = (f32[4096]{0:T(1024)S(1)}, f32[4096]{0:T(1024)S(1)}, u32[]{:S(2)}, u32[]{:S(2)}) collective-permute-start(f32[4096]{0:T(1024)S(1)} %select_reduce_fusion.2), channel_id=1, source_target_pairs={{0,1},{1,2},{2,3},{3,0},{4,5},{5,6},{6,7},{7,4},{8,9},{9,10},{10,1... | collective-permute-start | bytes 49160 | tf_op jit(solution)/shard_map/ppermute | solution.py:96
  (1 other events, 0.6 us)

commit v4 on v3

--- a/solution.py
+++ b/solution.py
@@ -149,10 +149,16 @@
     member = segment_ids[0][None, :] == labels
     pooled_part = jnp.dot(member.astype(jnp.bfloat16), normed, preferred_element_type=jnp.float32)
     counts = jnp.sum((group_ids[None, :] == labels).astype(jnp.float32), axis=1)
+    scaled_part = lax.dot_general(
+        member.astype(jnp.float32),
+        states * inv_rms,
+        (((1,), (0,)), ((), ())),
+        precision=lax.Precision.HIGHEST,
+        preferred_element_type=jnp.float32,
+    )
     chunk = model_width // feature_count
-    pooled_chunk = scatter_sum(
-        pooled_part.reshape(rows, feature_count, chunk).transpose(1, 0, 2), "fsdp"
-    )
+    both = jnp.stack([pooled_part, scaled_part]).reshape(2, rows, feature_count, chunk)
+    pooled_chunk, scaled_chunk = scatter_sum(both.transpose(2, 0, 1, 3), "fsdp")
     mean_chunk = (pooled_chunk / counts[:, None]).astype(jnp.bfloat16)
     mean_pooled = gather_blocks(mean_chunk, "fsdp").transpose(1, 0, 2).reshape(rows, model_width)
 
@@ -204,7 +210,10 @@
     proj_grad = lax.dot_general(
         pooled_cols, grad_low_cols, contract_first, preferred_element_type=jnp.float32
     )
-    mean_grad = lax.all_gather(mean_part, "fsdp", axis=1, tiled=True)
+    gain_slice = jnp.sum((mean_part / counts[:, None]) * scaled_chunk, axis=0)
+    both = jnp.concatenate([mean_part, gain_slice[None, :]], axis=0)
+    both = lax.all_gather(both, "fsdp", axis=1, tiled=True)
+    mean_grad = both[:rows]
     pool_grad = mean_grad / counts[:, None]
     normed_grad = lax.dot_general(
         member.astype(jnp.float32),
@@ -213,11 +222,10 @@
         precision=lax.Precision.HIGHEST,
         preferred_element_type=jnp.float32,
     )
-    gain_part = jnp.sum(normed_grad * states * inv_rms, axis=0)
     scaled = gain * normed_grad
     inner = jnp.mean(scaled * states, axis=1, keepdims=True)
     hidden_grad = (inv_rms * scaled - states * inv_rms**3 * inner).astype(jnp.bfloat16)
-    gain_grad = sum_blocks(sum_blocks(gain_part, "dp"), "fsdp")
+    gain_grad = sum_blocks(both[rows], "dp")
     return (mean_loss, query_grad, region_grad, hidden_grad, gain_grad, proj_grad)
 
 

time: 137 us -> 181 us (1.32)
  waiting for transfers between devices: 14.3 us -> 43.3 us
  local copies, waits for them, and re-layouts: 30.4 us -> 48.3 us
  starting transfers between devices: 38 us -> 27.4 us
  other arithmetic: 17 us -> 23.7 us
    ppermute x23 -> x20, waiting for transfers between devices: 2.87 us -> 43.3 us  [gather_blocks(): lax.ppermute(x, axis, [(i, (i + s) % n) for i in range(n)])]
    another operation x1 -> x4, local copies, waits for them, and re-layouts: 0.81 us -> 13.1 us  [the longest x3 7.17 us: local_small(): jnp.stack([pooled_part, scaled_part]).reshape(2, rows, feature_count, chunk)]
    ppermute x23 -> x20, starting transfers between devices: 28.2 us -> 18.3 us  [gather_blocks(): lax.ppermute(x, axis, [(i, (i + s) % n) for i in range(n)])]
    ppermute x3, waiting for transfers between devices: 9.32 us -> 0.01 us  [scatter_sum(): lax.ppermute(piece, axis, [(i, (i + s) % n) for i in range(n)])]
    dot_general x0 -> x1, matrix products: none -> 2.61 us  [local_small(): lax.dot_general(member.astype(jnp.float32), states * inv_rms, (((1,), (0,...]
    transpose x2, local copies, waits for them, and re-layouts: 1.89 us -> 4.21 us  [local_small(): gathered[:, :, rows:2 * rows].transpose(0, 2, 1, 3)]
    all_to_all x1, waiting for transfers between devices: 2.09 us -> 0.01 us  [local_small(): pieces = lax.all_to_all(pieces, 'dp', 0, 0, tiled=True)]
    gather x5 -> x4, local copies, waits for them, and re-layouts: 5.85 us -> 7.82 us  [gather_blocks(): return jnp.take(stack, order, axis=0)]
  transfers between devices with their start and end apart: 27 -> 24, of which waited for: 5 -> 10; matrix products, arithmetic and copies ran while one was open for 29% -> 34% of each run, Pallas kernels for 0% -> 0%
where the time goes in v4:
time: 181 us; the launch traced here: 180 us
  local copies, waits for them, and re-layouts  48.3 us (27%)
  waiting for transfers between devices  43.3 us (24%)
  starting transfers between devices  27.4 us (15%)
  other arithmetic  23.7 us (13%)
  blocking collectives  20.2 us (11%)
  matrix products  14.1 us (8%)
  between operations  2.73 us (2%)
    ppermute x20, waiting for transfers between devices, gather_blocks(): lax.ppermute(x, axis, [(i, (i + s) % n) for i in range(n)])  43.3 us
    all_gather x1, blocking collectives, local_small(): both = lax.all_gather(both, 'fsdp', axis=1, tiled=True)  20.2 us
    ppermute x20, starting transfers between devices, gather_blocks(): lax.ppermute(x, axis, [(i, (i + s) % n) for i in range(n)])  18.3 us
    unnamed x55, local copies, waits for them, and re-layouts  14.6 us
    gather x4, local copies, waits for them, and re-layouts, gather_blocks(): return jnp.take(stack, order, axis=0)  7.82 us
    another operation x3, local copies, waits for them, and re-layouts, local_small(): jnp.stack([pooled_part, scaled_part]).reshape(2, rows, feature_count, chunk)  7.17 us
    another operation x1, local copies, waits for them, and re-layouts  5.9 us
    ppermute x3, starting transfers between devices, scatter_sum(): lax.ppermute(piece, axis, [(i, (i + s) % n) for i in range(n)])  4.84 us
  transfers between devices with their start and end apart: 24, of which 10 were waited for; matrix products, arithmetic and copies ran while one was open for 34% of the time, Pallas kernels for 0%

profile of v4, /device:TPU:0, one launch (start us, length us, event | category | flops | bytes accessed | tf_op | source)
XLA Modules:
  0.0 179.7 jit_solution(88381625418877228)
XLA Ops:
  1.5 1.4 constant_dynamic-update-slice_fusion.4
  3.6 1.4 constant_dynamic-update-slice_fusion.3
  5.6 5.0 %collective-permute-start.5 = (bf16[97,256]{1,0:T(8,128)(2,1)}, bf16[97,256]{1,0:T(8,128)(2,1)}, u32[]{:S(2)}, u32[]{:S(2)}) collective-permute-start(bf16[97,256]{1,0:T(8,128)(2,1)} %constant_dynamic-update-slice_fusion.2), channel_id=1, source_target_pairs={{0,3},{1,0},{2,1},{3,2},{4,7},{5,4},{6,5},{7,6},{8,11},{9,8},{10,9... | collective-permute-start | bytes 149000 | tf_op jit(solution)/shard_map/ppermute | solution.py:96
  11.6 1.5 fusion.3
  14.5 2.6 %fusion = f32[48,4096]{1,0:T(8,128)} fusion(bf16[128,4096]{1,0:T(8,128)(2,1)S(1)} %copy-done.1, f32[128]{0:T(128)S(1)} %get-tuple-element.25, s32[128]{0:T(128)} %bitcast.134), kind=kOutput, calls=%fused_computation.10 | convolution fusion | flops 303044608 | bytes 1836032 | tf_op jit(solution)/shard_map/dot_general | solution.py:152
  17.1 1.4 fusion.8
  18.4 2.5 %stack.99 = f32[1,48,4,1024]{3,2,1,0:T(4,128)} reshape(f32[48,4096]{1,0:T(8,128)} %fusion.8) | data formatting | bytes 1572864 | tf_op jit(solution)/shard_map/stack | solution.py:160
  21.0 2.1 %constant_dynamic-update-slice_fusion.1 = f32[2,48,4,1024]{3,2,1,0:T(4,128)} fusion(f32[1,48,4,1024]{3,2,1,0:T(4,128)} %stack.99), kind=kLoop, calls=%fused_computation.73 | loop fusion | bytes 1572864
  23.0 2.5 %stack.100 = f32[1,48,4,1024]{3,2,1,0:T(4,128)} reshape(f32[48,4096]{1,0:T(8,128)} %fusion) | data formatting | bytes 1572864 | tf_op jit(solution)/shard_map/stack | solution.py:160
  25.6 2.1 %constant_dynamic-update-slice_fusion = f32[2,48,4,1024]{3,2,1,0:T(4,128)} fusion(f32[2,48,4,1024]{3,2,1,0:T(4,128)} %constant_dynamic-update-slice_fusion.1, f32[1,48,4,1024]{3,2,1,0:T(4,128)} %stack.100), kind=kLoop, calls=%fused_computation.72 | loop fusion | bytes 1572864 | tf_op jit(solution)/shard_map/stack | solution.py:160
  27.7 5.9 %constant_dynamic-slice_fusion.3 = (f32[2,48,1,1024]{3,2,1,0:T(1,128)}, f32[2,48,1,1024]{3,2,1,0:T(1,128)S(1)}, f32[2,48,1,1024]{3,2,1,0:T(1,128)S(1)}, f32[2,48,1,1024]{3,2,1,0:T(1,128)S(1)}) fusion(f32[2,48,4,1024]{3,2,1,0:T(4,128)} %constant_dynamic-update-slice_fusion, s32[]{:T(128)S(6)} %select_n.166, s32[]{:T(128)S(6)} %select_n.172, ...), kind=kLoop, calls=%fused_computation.108 | loop fusion | bytes 3145744 | tf_op jit(solution)/shard_map/dynamic-slice
  34.4 2.5 %collective-permute-start = (f32[2,48,1024]{2,1,0:T(8,128)}, f32[2,48,1024]{2,1,0:T(8,128)}, u32[]{:S(2)}, u32[]{:S(2)}) collective-permute-start(f32[2,48,1024]{2,1,0:T(8,128)} %bitcast.99), channel_id=1, source_target_pairs={{0,1},{1,2},{2,3},{3,0},{4,5},{5,6},{6,7},{7,4},{8,9},{9,10},{10,1... | collective-permute-start | bytes 1179656 | tf_op jit(solution)/shard_map/ppermute | solution.py:113
  39.2 1.8 %copy.42 = f32[2,48,1,1024]{3,1,2,0:T(8,128)} copy(f32[2,48,1,1024]{3,2,1,0:T(1,128)} %get-tuple-element.20) | data formatting | bytes 786432
  41.9 1.5 collective-permute-start.2
  43.4 1.6 pad_maximum_fusion.3
  44.9 1.5 gather_fusion.1
  48.1 7.1 %collective-permute-done.9 = bf16[4,97,256]{2,1,0:T(8,128)(2,1)S(1)} collective-permute-done((bf16[4,97,256]{2,1,0:T(8,128)(2,1)S(1)}, bf16[4,97,256]{2,1,0:T(8,128)(2,1)S(1)}, u32[]{:S(2)}, u32[]{:S(2)}) %collective-permute-start.9) | collective-permute-done | bytes 198688 | tf_op jit(solution)/shard_map/ppermute | solution.py:96
  55.9 6.0 %collective-permute-done.10 = bf16[4,97,256]{2,1,0:T(8,128)(2,1)S(1)} collective-permute-done((bf16[4,97,256]{2,1,0:T(8,128)(2,1)S(1)}, bf16[4,97,256]{2,1,0:T(8,128)(2,1)S(1)}, u32[]{:S(2)}, u32[]{:S(2)}) %collective-permute-start.10) | collective-permute-done | bytes 198688 | tf_op jit(solution)/shard_map/ppermute | solution.py:96
  62.6 5.5 %collective-permute-done.11 = bf16[4,97,256]{2,1,0:T(8,128)(2,1)S(1)} collective-permute-done((bf16[4,97,256]{2,1,0:T(8,128)(2,1)S(1)}, bf16[4,97,256]{2,1,0:T(8,128)(2,1)S(1)}, u32[]{:S(2)}, u32[]{:S(2)}) %collective-permute-start.11) | collective-permute-done | bytes 198688 | tf_op jit(solution)/shard_map/ppermute | solution.py:96
  69.3 4.6 %collective-permute-done.12 = bf16[4,97,256]{2,1,0:T(8,128)(2,1)S(1)} collective-permute-done((bf16[4,97,256]{2,1,0:T(8,128)(2,1)S(1)}, bf16[4,97,256]{2,1,0:T(8,128)(2,1)S(1)}, u32[]{:S(2)}, u32[]{:S(2)}) %collective-permute-start.12) | collective-permute-done | bytes 198688 | tf_op jit(solution)/shard_map/ppermute | solution.py:96
  74.6 4.6 %collective-permute-done.13 = bf16[4,97,256]{2,1,0:T(8,128)(2,1)S(1)} collective-permute-done((bf16[4,97,256]{2,1,0:T(8,128)(2,1)S(1)}, bf16[4,97,256]{2,1,0:T(8,128)(2,1)S(1)}, u32[]{:S(2)}, u32[]{:S(2)}) %collective-permute-start.13) | collective-permute-done | bytes 198688 | tf_op jit(solution)/shard_map/ppermute | solution.py:96
  79.2 1.8 %collective-permute-start.14 = (bf16[4,97,256]{2,1,0:T(8,128)(2,1)S(1)}, bf16[4,97,256]{2,1,0:T(8,128)(2,1)S(1)}, u32[]{:S(2)}, u32[]{:S(2)}) collective-permute-start(bf16[4,97,256]{2,1,0:T(8,128)(2,1)S(1)} %broadcast_select_fusion.1), channel_id=1, source_target_pairs={{0,24},{4,28},{8,0},{12,4},{16,8},{20,12},{24,16},{28,20},{1,25},{... | collective-permute-start | bytes 595976 | tf_op jit(solution)/shard_map/ppermute | solution.py:96
  81.7 5.5 %collective-permute-done.14 = bf16[4,97,256]{2,1,0:T(8,128)(2,1)S(1)} collective-permute-done((bf16[4,97,256]{2,1,0:T(8,128)(2,1)S(1)}, bf16[4,97,256]{2,1,0:T(8,128)(2,1)S(1)}, u32[]{:S(2)}, u32[]{:S(2)}) %collective-permute-start.14) | collective-permute-done | bytes 198688 | tf_op jit(solution)/shard_map/ppermute | solution.py:96
  88.7 3.3 %gather_fusion.3 = bf16[8,4,97,256]{3,2,1,0:T(8,128)(2,1)} fusion(bf16[8,4,97,256]{3,2,1,0:T(8,128)(2,1)} %bitcast_dynamic-update-slice_fusion, s32[1024]{0:T(1024)S(1)} %pad_clamp_fusion), kind=kCustom, calls=%fused_computation.3 | custom fusion | bytes 3178528 | tf_op jit(solution)/shard_map/jit(_take)/gather | solution.py:100
  92.0 2.9 %broadcast_select_fusion = bf16[8,4,97,256]{3,2,1,0:T(8,128)(2,1)} fusion(bf16[8,4,97,256]{3,2,1,0:T(8,128)(2,1)} %gather_fusion.3, pred[8]{0:T(512)(128)(4,1)S(1)} %copy-done.14), kind=kLoop, calls=%fused_computation.18 | loop fusion | flops 794624 | bytes 3178504 | tf_op jit(solution)/shard_map/jit(_take)/select_n | solution.py:100
  94.9 2.6 %pad_maximum_fusion = f32[4,2,48,1024]{3,2,1,0:T(8,128)} fusion(f32[1,2,48,1024]{3,2,1,0:T(8,128)} %bitcast.3, f32[1,2,48,1024]{3,2,1,0:T(8,128)} %bitcast.2, f32[1,2,48,1024]{3,2,1,0:T(8,128)} %bitcast.1, f32[1,2,48,1024]{3,2,1,0:T(8,128)S(1)} %bitcast.107), kind=kLoop, calls=%fused_computation.19 | loop fusion | flops 1179648 | bytes 3145728 | tf_op jit(solution)/shard_map/stack | solution.py:115
  97.5 3.2 %gather_fusion = f32[4,2,48,1024]{3,2,1,0:T(8,128)} fusion(f32[4,2,48,1024]{3,2,1,0:T(8,128)} %pad_maximum_fusion, s32[1024]{0:T(1024)S(1)} %pad_clamp_fusion.1), kind=kCustom, calls=%fused_computation | custom fusion | bytes 3145744 | tf_op jit(solution)/shard_map/jit(_take)/gather | solution.py:115
  100.7 1.7 select_reduce_fusion
  102.5 2.0 %collective-permute-start.8 = (bf16[48,1024]{1,0:T(8,128)(2,1)S(1)}, bf16[48,1024]{1,0:T(8,128)(2,1)S(1)}, u32[]{:S(2)}, u32[]{:S(2)}) collective-permute-start(bf16[48,1024]{1,0:T(8,128)(2,1)S(1)} %fusion.18), channel_id=1, source_target_pairs={{0,3},{1,0},{2,1},{3,2},{4,7},{5,4},{6,5},{7,6},{8,11},{9,8},{10,9... | collective-permute-start | bytes 294920 | tf_op jit(solution)/shard_map/ppermute | solution.py:96
  105.6 2.1 %collective-permute-done.8 = bf16[48,1024]{1,0:T(8,128)(2,1)S(1)} collective-permute-done((bf16[48,1024]{1,0:T(8,128)(2,1)S(1)}, bf16[48,1024]{1,0:T(8,128)(2,1)S(1)}, u32[]{:S(2)}, u32[]{:S(2)}) %collective-permute-start.8) | collective-permute-done | bytes 98336 | tf_op jit(solution)/shard_map/ppermute | solution.py:96
  107.7 6.1 %collective-permute-done.7 = bf16[48,1024]{1,0:T(8,128)(2,1)S(1)} collective-permute-done((bf16[48,1024]{1,0:T(8,128)(2,1)S(1)}, bf16[48,1024]{1,0:T(8,128)(2,1)S(1)}, u32[]{:S(2)}, u32[]{:S(2)}) %collective-permute-start.7) | collective-permute-done | bytes 98336 | tf_op jit(solution)/shard_map/ppermute | solution.py:96
  114.6 2.3 %gather_fusion.2 = bf16[4,48,1024]{2,1,0:T(8,128)(2,1)} fusion(bf16[4,48,1024]{2,1,0:T(8,128)(2,1)} %pad_maximum_fusion.1, s32[1024]{0:T(1024)S(1)} %pad_clamp_fusion.1), kind=kCustom, calls=%fused_computation.2 | custom fusion | bytes 786448 | tf_op jit(solution)/shard_map/jit(_take)/gather | solution.py:100
  118.0 1.5 slice_convert_fusion
  119.6 2.7 %slice_bitcast_fusion = (bf16[8,48,4,256]{3,1,2,0:T(8,128)(2,1)}, bf16[8,48,4,256]{3,1,2,0:T(8,128)(2,1)}) fusion(bf16[8,4,97,256]{3,2,1,0:T(8,128)(2,1)} %broadcast_select_fusion), kind=kLoop, calls=%fused_computation.29 | loop fusion | bytes 3145728 | tf_op jit(solution)/shard_map/transpose | solution.py:173
  123.0 4.3 %all-to-all-start = ((bf16[8,48,512]{2,1,0:T(8,128)(2,1)}), bf16[8,48,512]{2,1,0:T(8,128)(2,1)}, u32[]{:S(2)}, u32[]{:S(2)}) async-start(bf16[8,48,512]{2,1,0:T(8,128)(2,1)} %bitcast.108), calls=%async_computation | async-start | bytes 786432 | tf_op jit(solution)/shard_map/all_to_all | solution.py:169
  127.3 1.5 copy.19
  130.1 1.6 copy.18
  133.5 1.8 convolution_multiply_fusion.1
  135.9 1.4 dynamic_slice.23
  137.3 1.7 convolution_multiply_fusion.3
  139.1 2.4 %fusion.20 = f32[48,1024]{1,0:T(8,128)} fusion(bf16[1024,1024]{1,0:T(8,128)(2,1)S(1)} %copy-done, f32[384,1024]{1,0:T(8,128)} %convolution_multiply_fusion.1, s32[]{:T(128)S(6)} %select_n.188), kind=kOutput, calls=%fused_computation.66 | convolution fusion | flops 100663296 | bytes 2392068 | tf_op jit(solution)/shard_map/dot_general | solution.py:206
  143.4 20.2 %all_gather.3 = f32[49,4096]{1,0:T(8,128)S(1)} all-gather(f32[49,1024]{1,0:T(8,128)S(1)} %pad_maximum_fusion.2), channel_id=1, replica_groups=mesh['dp'=8,'fsdp'=4] {'fsdp'}, dimensions={1}, use_global_device_ids=true | all-gather | bytes 1003520 | tf_op jit(solution)/shard_map/all_gather | solution.py:215
  164.9 1.5 collective-permute-start.21
  166.7 1.5 collective-permute-start.19
  168.4 1.4 fusion.7
  169.8 1.6 fusion.6
  171.4 1.5 collective-permute-start.17
  172.8 2.2 %fusion.15 = f32[512,256]{1,0:T(8,128)} fusion(bf16[384,512]{1,0:T(8,128)(2,1)} %bitcast.27, f32[384,1024]{1,0:T(8,128)} %convolution_multiply_fusion.1, s32[]{:T(128)S(6)} %select_n.189), kind=kOutput, calls=%fused_computation.56 | convolution fusion | flops 100663296 | bytes 1114116 | tf_op jit(solution)/shard_map/dot_general | solution.py:210
  (119 shorter events, 29.8 us)
Async XLA Ops:
  0.6 138.4 %copy-start = (bf16[1024,1024]{1,0:T(8,128)(2,1)S(1)}, bf16[1024,1024]{1,0:T(8,128)(2,1)}, u32[]{:S(2)}) copy-start(bf16[1024,1024]{1,0:T(8,128)(2,1)} %param.13) | copy-start | bytes 6291460
  0.6 16.4 %copy-start.16 = (s32[1,128]{1,0:T(1,128)S(1)}, s32[1,128]{1,0:T(1,128)}, u32[]{:S(2)}) copy-start(s32[1,128]{1,0:T(1,128)} %param.11) | copy-start | bytes 1540
  0.7 13.8 %copy-start.1 = (bf16[128,4096]{1,0:T(8,128)(2,1)S(1)}, bf16[128,4096]{1,0:T(8,128)(2,1)}, u32[]{:S(2)}) copy-start(bf16[128,4096]{1,0:T(8,128)(2,1)} %param.10) | copy-start | bytes 3145732
  5.6 36.3 %collective-permute-start.5 = (bf16[97,256]{1,0:T(8,128)(2,1)}, bf16[97,256]{1,0:T(8,128)(2,1)}, u32[]{:S(2)}, u32[]{:S(2)}) collective-permute-start(bf16[97,256]{1,0:T(8,128)(2,1)} %constant_dynamic-update-slice_fusion.2), channel_id=1, source_target_pairs={{0,3},{1,0},{2,1},{3,2},{4,7},{5,4},{6,5},{7,6},{8,11},{9,8},{10,9... | collective-permute-start | bytes 149000 | tf_op jit(solution)/shard_map/ppermute | solution.py:96
  10.6 32.7 %collective-permute-start.4 = (bf16[97,256]{1,0:T(8,128)(2,1)}, bf16[97,256]{1,0:T(8,128)(2,1)}, u32[]{:S(2)}, u32[]{:S(2)}) collective-permute-start(bf16[97,256]{1,0:T(8,128)(2,1)} %constant_dynamic-update-slice_fusion.2), channel_id=1, source_target_pairs={{0,2},{1,3},{2,0},{3,1},{4,6},{5,7},{6,4},{7,5},{8,10},{9,11},{10,... | collective-permute-start | bytes 149000 | tf_op jit(solution)/shard_map/ppermute | solution.py:96
  10.6 32.7 %collective-permute-start.3 = (bf16[97,256]{1,0:T(8,128)(2,1)}, bf16[97,256]{1,0:T(8,128)(2,1)}, u32[]{:S(2)}, u32[]{:S(2)}) collective-permute-start(bf16[97,256]{1,0:T(8,128)(2,1)} %constant_dynamic-update-slice_fusion.2), channel_id=1, source_target_pairs={{0,1},{1,2},{2,3},{3,0},{4,5},{5,6},{6,7},{7,4},{8,9},{9,10},{10,1... | collective-permute-start | bytes 149000 | tf_op jit(solution)/shard_map/ppermute | solution.py:96
  13.7 3.3 %copy-start.12 = (f32[128]{0:T(128)}, f32[128]{0:T(128)S(1)}, u32[]{:S(2)}) copy-start(f32[128]{0:T(128)S(1)} %get-tuple-element.25) | copy-start | bytes 1540
  14.4 2.6 %copy-start.7 = (f32[4096]{0:T(1024)}, f32[4096]{0:T(1024)S(1)}, u32[]{:S(2)}) copy-start(f32[4096]{0:T(1024)S(1)} %convert_element_type.72) | copy-start | bytes 49156
  34.4 60.5 %collective-permute-start = (f32[2,48,1024]{2,1,0:T(8,128)}, f32[2,48,1024]{2,1,0:T(8,128)}, u32[]{:S(2)}, u32[]{:S(2)}) collective-permute-start(f32[2,48,1024]{2,1,0:T(8,128)} %bitcast.99), channel_id=1, source_target_pairs={{0,1},{1,2},{2,3},{3,0},{4,5},{5,6},{6,7},{7,4},{8,9},{9,10},{10,1... | collective-permute-start | bytes 1179656 | tf_op jit(solution)/shard_map/ppermute | solution.py:113
  37.7 57.2 %collective-permute-start.1 = (f32[2,48,1024]{2,1,0:T(8,128)}, f32[2,48,1024]{2,1,0:T(8,128)}, u32[]{:S(2)}, u32[]{:S(2)}) collective-permute-start(f32[2,48,1024]{2,1,0:T(8,128)} %bitcast.98), channel_id=1, source_target_pairs={{0,2},{1,3},{2,0},{3,1},{4,6},{5,7},{6,4},{7,5},{8,10},{9,11},{10,... | collective-permute-start | bytes 1179656 | tf_op jit(solution)/shard_map/ppermute | solution.py:113
  38.7 50.0 %copy-start.11 = (s32[1024]{0:T(1024)}, s32[1024]{0:T(1024)S(1)}, u32[]{:S(2)}) copy-start(s32[1024]{0:T(1024)S(1)} %pad_clamp_fusion) | copy-start | bytes 12292
  41.9 53.0 %collective-permute-start.2 = (f32[2,48,1024]{2,1,0:T(8,128)}, f32[2,48,1024]{2,1,0:T(8,128)}, u32[]{:S(2)}, u32[]{:S(2)}) collective-permute-start(f32[2,48,1024]{2,1,0:T(8,128)} %bitcast.112), channel_id=1, source_target_pairs={{0,3},{1,0},{2,1},{3,2},{4,7},{5,4},{6,5},{7,6},{8,11},{9,8},{10,9... | collective-permute-start | bytes 1179656 | tf_op jit(solution)/shard_map/ppermute | solution.py:113
  46.5 41.4 %collective-permute-start.15 = (bf16[4,97,256]{2,1,0:T(8,128)(2,1)S(1)}, bf16[4,97,256]{2,1,0:T(8,128)(2,1)S(1)}, u32[]{:S(2)}, u32[]{:S(2)}) collective-permute-start(bf16[4,97,256]{2,1,0:T(8,128)(2,1)S(1)} %broadcast_select_fusion.1), channel_id=1, source_target_pairs={{0,28},{4,0},{8,4},{12,8},{16,12},{20,16},{24,20},{28,24},{1,29},{... | collective-permute-start | bytes 595976 | tf_op jit(solution)/shard_map/ppermute | solution.py:96
  47.1 8.1 %collective-permute-start.9 = (bf16[4,97,256]{2,1,0:T(8,128)(2,1)S(1)}, bf16[4,97,256]{2,1,0:T(8,128)(2,1)S(1)}, u32[]{:S(2)}, u32[]{:S(2)}) collective-permute-start(bf16[4,97,256]{2,1,0:T(8,128)(2,1)S(1)} %broadcast_select_fusion.1), channel_id=1, source_target_pairs={{0,4},{4,8},{8,12},{12,16},{16,20},{20,24},{24,28},{28,0},{1,5},{5... | collective-permute-start | bytes 595976 | tf_op jit(solution)/shard_map/ppermute | solution.py:96
  47.3 58.2 %copy-start.9 = (f32[48]{0:T(128)}, f32[48]{0:T(128)S(1)}, u32[]{:S(2)}) copy-start(f32[48]{0:T(128)S(1)} %convert_reduce_fusion) | copy-start | bytes 580
  55.2 6.7 %collective-permute-start.10 = (bf16[4,97,256]{2,1,0:T(8,128)(2,1)S(1)}, bf16[4,97,256]{2,1,0:T(8,128)(2,1)S(1)}, u32[]{:S(2)}, u32[]{:S(2)}) collective-permute-start(bf16[4,97,256]{2,1,0:T(8,128)(2,1)S(1)} %broadcast_select_fusion.1), channel_id=1, source_target_pairs={{0,8},{4,12},{8,16},{12,20},{16,24},{20,28},{24,0},{28,4},{1,9},{5... | collective-permute-start | bytes 595976 | tf_op jit(solution)/shard_map/ppermute | solution.py:96
  61.9 6.2 %collective-permute-start.11 = (bf16[4,97,256]{2,1,0:T(8,128)(2,1)S(1)}, bf16[4,97,256]{2,1,0:T(8,128)(2,1)S(1)}, u32[]{:S(2)}, u32[]{:S(2)}) collective-permute-start(bf16[4,97,256]{2,1,0:T(8,128)(2,1)S(1)} %broadcast_select_fusion.1), channel_id=1, source_target_pairs={{0,12},{4,16},{8,20},{12,24},{16,28},{20,0},{24,4},{28,8},{1,13},{... | collective-permute-start | bytes 595976 | tf_op jit(solution)/shard_map/ppermute | solution.py:96
  68.1 5.8 %collective-permute-start.12 = (bf16[4,97,256]{2,1,0:T(8,128)(2,1)S(1)}, bf16[4,97,256]{2,1,0:T(8,128)(2,1)S(1)}, u32[]{:S(2)}, u32[]{:S(2)}) collective-permute-start(bf16[4,97,256]{2,1,0:T(8,128)(2,1)S(1)} %broadcast_select_fusion.1), channel_id=1, source_target_pairs={{0,16},{4,20},{8,24},{12,28},{16,0},{20,4},{24,8},{28,12},{1,17},{... | collective-permute-start | bytes 595976 | tf_op jit(solution)/shard_map/ppermute | solution.py:96
  73.9 5.3 %collective-permute-start.13 = (bf16[4,97,256]{2,1,0:T(8,128)(2,1)S(1)}, bf16[4,97,256]{2,1,0:T(8,128)(2,1)S(1)}, u32[]{:S(2)}, u32[]{:S(2)}) collective-permute-start(bf16[4,97,256]{2,1,0:T(8,128)(2,1)S(1)} %broadcast_select_fusion.1), channel_id=1, source_target_pairs={{0,20},{4,24},{8,28},{12,0},{16,4},{20,8},{24,12},{28,16},{1,21},{... | collective-permute-start | bytes 595976 | tf_op jit(solution)/shard_map/ppermute | solution.py:96
  79.2 8.1 %collective-permute-start.14 = (bf16[4,97,256]{2,1,0:T(8,128)(2,1)S(1)}, bf16[4,97,256]{2,1,0:T(8,128)(2,1)S(1)}, u32[]{:S(2)}, u32[]{:S(2)}) collective-permute-start(bf16[4,97,256]{2,1,0:T(8,128)(2,1)S(1)} %broadcast_select_fusion.1), channel_id=1, source_target_pairs={{0,24},{4,28},{8,0},{12,4},{16,8},{20,12},{24,16},{28,20},{1,25},{... | collective-permute-start | bytes 595976 | tf_op jit(solution)/shard_map/ppermute | solution.py:96
  88.7 3.3 %copy-start.14 = (pred[8]{0:T(512)(128)(4,1)S(1)}, pred[8]{0:T(512)(128)(4,1)}, u32[]{:S(2)}) copy-start(pred[8]{0:T(512)(128)(4,1)} %compare_and_fusion) | copy-start | bytes 28
  92.0 2.9 %copy-start.3 = (f32[2,48,1,1024]{3,1,2,0:T(8,128)S(1)}, f32[2,48,1,1024]{3,1,2,0:T(8,128)}, u32[]{:S(2)}) copy-start(f32[2,48,1,1024]{3,1,2,0:T(8,128)} %copy.42) | copy-start | bytes 1179652
  102.5 5.2 %collective-permute-start.8 = (bf16[48,1024]{1,0:T(8,128)(2,1)S(1)}, bf16[48,1024]{1,0:T(8,128)(2,1)S(1)}, u32[]{:S(2)}, u32[]{:S(2)}) collective-permute-start(bf16[48,1024]{1,0:T(8,128)(2,1)S(1)} %fusion.18), channel_id=1, source_target_pairs={{0,3},{1,0},{2,1},{3,2},{4,7},{5,4},{6,5},{7,6},{8,11},{9,8},{10,9... | collective-permute-start | bytes 294920 | tf_op jit(solution)/shard_map/ppermute | solution.py:96
  104.5 9.3 %collective-permute-start.7 = (bf16[48,1024]{1,0:T(8,128)(2,1)S(1)}, bf16[48,1024]{1,0:T(8,128)(2,1)S(1)}, u32[]{:S(2)}, u32[]{:S(2)}) collective-permute-start(bf16[48,1024]{1,0:T(8,128)(2,1)S(1)} %fusion.18), channel_id=1, source_target_pairs={{0,2},{1,3},{2,0},{3,1},{4,6},{5,7},{6,4},{7,5},{8,10},{9,11},{10,... | collective-permute-start | bytes 294920 | tf_op jit(solution)/shard_map/ppermute | solution.py:96
  104.5 9.2 %collective-permute-start.6 = (bf16[48,1024]{1,0:T(8,128)(2,1)S(1)}, bf16[48,1024]{1,0:T(8,128)(2,1)S(1)}, u32[]{:S(2)}, u32[]{:S(2)}) collective-permute-start(bf16[48,1024]{1,0:T(8,128)(2,1)S(1)} %fusion.18), channel_id=1, source_target_pairs={{0,1},{1,2},{2,3},{3,0},{4,5},{5,6},{6,7},{7,4},{8,9},{9,10},{10,1... | collective-permute-start | bytes 294920 | tf_op jit(solution)/shard_map/ppermute | solution.py:96
  123.0 18.4 %all-to-all-start = ((bf16[8,48,512]{2,1,0:T(8,128)(2,1)}), bf16[8,48,512]{2,1,0:T(8,128)(2,1)}, u32[]{:S(2)}, u32[]{:S(2)}) async-start(bf16[8,48,512]{2,1,0:T(8,128)(2,1)} %bitcast.108), calls=%async_computation | async-start | bytes 786432 | tf_op jit(solution)/shard_map/all_to_all | solution.py:169
  127.3 2.6 %copy-start.6 = (f32[8,4,1,256]{3,2,1,0:T(1,128)S(1)}, f32[8,4,1,256]{3,2,1,0:T(1,128)}, u32[]{:S(2)}) copy-start(f32[8,4,1,256]{3,2,1,0:T(1,128)} %slice_convert_fusion) | copy-start | bytes 98308
  130.1 1.8 copy-start.2
  131.9 1.6 copy-start.5
  133.5 1.8 %copy-start.4 = (bf16[384,384]{0,1:T(8,128)(2,1)}, bf16[384,384]{0,1:T(8,128)(2,1)S(1)}, u32[]{:S(2)}) copy-start(bf16[384,384]{0,1:T(8,128)(2,1)S(1)} %subtract_convert_fusion) | copy-start | bytes 884740
  139.1 29.3 %copy-start.8 = (f32[4096]{0:T(1024)S(1)}, f32[4096]{0:T(1024)}, u32[]{:S(2)}) copy-start(f32[4096]{0:T(1024)} %copy-done.7) | copy-start | bytes 49156
  141.4 26.9 %copy-start.10 = (f32[48]{0:T(128)S(1)}, f32[48]{0:T(128)}, u32[]{:S(2)}) copy-start(f32[48]{0:T(128)} %copy-done.9) | copy-start | bytes 580
  141.4 26.9 %copy-start.17 = (s32[1,128]{1,0:T(1,128)S(1)}, s32[1,128]{1,0:T(1,128)}, u32[]{:S(2)}) copy-start(s32[1,128]{1,0:T(1,128)} %param.11) | copy-start | bytes 1540
  163.6 6.2 %copy-start.13 = (f32[128]{0:T(128)S(1)}, f32[128]{0:T(128)}, u32[]{:S(2)}) copy-start(f32[128]{0:T(128)} %copy-done.12) | copy-start | bytes 1540
  163.6 6.2 %copy-start.18 = (f32[128]{0:T(128)S(1)}, f32[128]{0:T(128)}, u32[]{:S(2)}) copy-start(f32[128]{0:T(128)} %get-tuple-element.24) | copy-start | bytes 1540
  163.6 7.7 %collective-permute-start.22 = (f32[4096]{0:T(1024)S(1)}, f32[4096]{0:T(1024)S(1)}, u32[]{:S(2)}, u32[]{:S(2)}) collective-permute-start(f32[4096]{0:T(1024)S(1)} %bitcast.116), channel_id=1, source_target_pairs={{0,28},{4,0},{8,4},{12,8},{16,12},{20,16},{24,20},{28,24},{1,29},{... | collective-permute-start | bytes 49160 | tf_op jit(solution)/shard_map/ppermute | solution.py:96
  164.9 8.0 %collective-permute-start.21 = (f32[4096]{0:T(1024)S(1)}, f32[4096]{0:T(1024)S(1)}, u32[]{:S(2)}, u32[]{:S(2)}) collective-permute-start(f32[4096]{0:T(1024)S(1)} %bitcast.117), channel_id=1, source_target_pairs={{0,24},{4,28},{8,0},{12,4},{16,8},{20,12},{24,16},{28,20},{1,25},{... | collective-permute-start | bytes 49160 | tf_op jit(solution)/shard_map/ppermute | solution.py:96
  166.3 8.8 %collective-permute-start.20 = (f32[4096]{0:T(1024)S(1)}, f32[4096]{0:T(1024)S(1)}, u32[]{:S(2)}, u32[]{:S(2)}) collective-permute-start(f32[4096]{0:T(1024)S(1)} %bitcast.118), channel_id=1, source_target_pairs={{0,20},{4,24},{8,28},{12,0},{16,4},{20,8},{24,12},{28,16},{1,21},{... | collective-permute-start | bytes 49160 | tf_op jit(solution)/shard_map/ppermute | solution.py:96
  166.7 8.4 %collective-permute-start.19 = (f32[4096]{0:T(1024)S(1)}, f32[4096]{0:T(1024)S(1)}, u32[]{:S(2)}, u32[]{:S(2)}) collective-permute-start(f32[4096]{0:T(1024)S(1)} %bitcast.119), channel_id=1, source_target_pairs={{0,16},{4,20},{8,24},{12,28},{16,0},{20,4},{24,8},{28,12},{1,17},{... | collective-permute-start | bytes 49160 | tf_op jit(solution)/shard_map/ppermute | solution.py:96
  168.1 7.0 %collective-permute-start.18 = (f32[4096]{0:T(1024)S(1)}, f32[4096]{0:T(1024)S(1)}, u32[]{:S(2)}, u32[]{:S(2)}) collective-permute-start(f32[4096]{0:T(1024)S(1)} %bitcast.120), channel_id=1, source_target_pairs={{0,12},{4,16},{8,20},{12,24},{16,28},{20,0},{24,4},{28,8},{1,13},{... | collective-permute-start | bytes 49160 | tf_op jit(solution)/shard_map/ppermute | solution.py:96
  171.4 6.5 %copy-start.15 = (pred[8]{0:T(512)(128)(4,1)S(1)}, pred[8]{0:T(512)(128)(4,1)}, u32[]{:S(2)}) copy-start(pred[8]{0:T(512)(128)(4,1)} %compare_and_fusion) | copy-start | bytes 28
  171.4 4.6 %collective-permute-start.17 = (f32[4096]{0:T(1024)S(1)}, f32[4096]{0:T(1024)S(1)}, u32[]{:S(2)}, u32[]{:S(2)}) collective-permute-start(f32[4096]{0:T(1024)S(1)} %bitcast.121), channel_id=1, source_target_pairs={{0,8},{4,12},{8,16},{12,20},{16,24},{20,28},{24,0},{28,4},{1,9},{5... | collective-permute-start | bytes 49160 | tf_op jit(solution)/shard_map/ppermute | solution.py:96
  172.8 4.1 %collective-permute-start.16 = (f32[4096]{0:T(1024)S(1)}, f32[4096]{0:T(1024)S(1)}, u32[]{:S(2)}, u32[]{:S(2)}) collective-permute-start(f32[4096]{0:T(1024)S(1)} %bitcast.122), channel_id=1, source_target_pairs={{0,4},{4,8},{8,12},{12,16},{16,20},{20,24},{24,28},{28,0},{1,5},{5... | collective-permute-start | bytes 49160 | tf_op jit(solution)/shard_map/ppermute | solution.py:96

commit v5 on v3

--- a/solution.py
+++ b/solution.py
@@ -100,6 +100,22 @@
     return jnp.take(stack, order, axis=0)
 
 
+def gather_grouped(x, axis, inner):
+    n = lax.axis_size(axis)
+    outer = n // inner
+    me = lax.axis_index(axis)
+    copies = [x] + [
+        lax.ppermute(x, axis, [(i, i - i % inner + (i % inner + s) % inner) for i in range(n)])
+        for s in range(1, inner)
+    ]
+    near = jnp.take(jnp.stack(copies), (me % inner - jnp.arange(inner)) % inner, axis=0)
+    copies = [near] + [
+        lax.ppermute(near, axis, [(i, (i + inner * s) % n) for i in range(n)]) for s in range(1, outer)
+    ]
+    far = jnp.take(jnp.stack(copies), (me // inner - jnp.arange(outer)) % outer, axis=0)
+    return far.reshape((n,) + x.shape)
+
+
 def sum_blocks(x, axis):
     return jnp.sum(gather_blocks(x, axis), axis=0)
 
@@ -156,7 +172,7 @@
     mean_chunk = (pooled_chunk / counts[:, None]).astype(jnp.bfloat16)
     mean_pooled = gather_blocks(mean_chunk, "fsdp").transpose(1, 0, 2).reshape(rows, model_width)
 
-    gathered = gather_blocks(group_blocks, "dp")
+    gathered = gather_grouped(group_blocks, "dp", CORES)
     mean_pooled, gathered = lax.optimization_barrier((mean_pooled, gathered))
     slice_width = model_width // data_count
     pieces = mean_pooled.reshape(rows, data_count, slice_width).transpose(1, 0, 2)
@@ -217,11 +233,12 @@
     scaled = gain * normed_grad
     inner = jnp.mean(scaled * states, axis=1, keepdims=True)
     hidden_grad = (inv_rms * scaled - states * inv_rms**3 * inner).astype(jnp.bfloat16)
-    gain_grad = sum_blocks(sum_blocks(gain_part, "dp"), "fsdp")
+    gain_grad = sum_blocks(jnp.sum(gather_grouped(gain_part, "dp", CORES), axis=0), "fsdp")
     return (mean_loss, query_grad, region_grad, hidden_grad, gain_grad, proj_grad)
 
 
 SMALL_PAIRS = 1024
+CORES = 2
 
 
 def local(query_cache, region_cache, positive, hidden_states, segment_ids, norm_gain, proj_weight):

time: 137 us -> 145 us (1.058)
  waiting for transfers between devices: 14.3 us -> 28.5 us
  other arithmetic: 17 us -> 26.3 us
  starting transfers between devices: 38 us -> 29.6 us
  local copies, waits for them, and re-layouts: 30.4 us -> 23.3 us
    ppermute x0 -> x8, waiting for transfers between devices: none -> 18.9 us  [the longest x6 18.9 us: gather_grouped(): lax.ppermute(near, axis, [(i, (i + inner * s) % n) for i in range(n)])]
    ppermute x23 -> x9, starting transfers between devices: 28.2 us -> 13.7 us  [gather_blocks(): lax.ppermute(x, axis, [(i, (i + s) % n) for i in range(n)])]
    unnamed x60 -> x43, local copies, waits for them, and re-layouts: 14.3 us -> 6.46 us
    ppermute x0 -> x8, starting transfers between devices: none -> 7.63 us  [the longest x6 7.56 us: gather_grouped(): lax.ppermute(near, axis, [(i, (i + inner * s) % n) for i in range(n)])]
    select_n x0 -> x7, other arithmetic: none -> 6.13 us  [the longest x5 3.8 us: gather_grouped(): jnp.take(jnp.stack(copies), (me % inner - jnp.arange(inner)) % inner, axi...]
    gather x0 -> x4, local copies, waits for them, and re-layouts: none -> 5.63 us  [the longest x2 4.24 us: gather_grouped(): jnp.take(jnp.stack(copies), (me // inner - jnp.arange(outer)) % outer, ax...]
    gather x5 -> x3, local copies, waits for them, and re-layouts: 5.85 us -> 1.96 us  [gather_blocks(): return jnp.take(stack, order, axis=0)]
    another operation x1 -> x5, other arithmetic: 0.73 us -> 4.5 us  [the longest x4 3.76 us: gather_grouped(): jnp.stack(copies)]
  transfers between devices with their start and end apart: 27 -> 21, of which waited for: 5 -> 9; matrix products, arithmetic and copies ran while one was open for 29% -> 28% of each run, Pallas kernels for 0% -> 0%
where the time goes in v5:
time: 145 us; the launch traced here: 144 us
  starting transfers between devices  29.6 us (20%)
  waiting for transfers between devices  28.5 us (20%)
  other arithmetic  26.3 us (18%)
  local copies, waits for them, and re-layouts  23.3 us (16%)
  blocking collectives  20 us (14%)
  matrix products  13.5 us (9%)
  between operations  2.9 us (2%)
    all_gather x1, blocking collectives, local_small(): mean_grad = lax.all_gather(mean_part, 'fsdp', axis=1, tiled=True)  20 us
    ppermute x6, waiting for transfers between devices, gather_grouped(): lax.ppermute(near, axis, [(i, (i + inner * s) % n) for i in range(n)])  18.9 us
    ppermute x9, starting transfers between devices, gather_blocks(): lax.ppermute(x, axis, [(i, (i + s) % n) for i in range(n)])  13.7 us
    ppermute x6, starting transfers between devices, gather_grouped(): lax.ppermute(near, axis, [(i, (i + inner * s) % n) for i in range(n)])  7.56 us
    unnamed x43, local copies, waits for them, and re-layouts  6.46 us
    ppermute x3, waiting for transfers between devices, scatter_sum(): lax.ppermute(piece, axis, [(i, (i + s) % n) for i in range(n)])  5.6 us
    ppermute x3, starting transfers between devices, scatter_sum(): lax.ppermute(piece, axis, [(i, (i + s) % n) for i in range(n)])  4.84 us
    gather x2, local copies, waits for them, and re-layouts, gather_grouped(): jnp.take(jnp.stack(copies), (me // inner - jnp.arange(outer)) % outer, ax...  4.24 us
  transfers between devices with their start and end apart: 21, of which 9 were waited for; matrix products, arithmetic and copies ran while one was open for 28% of the time, Pallas kernels for 0%

profile of v5, /device:TPU:0, one launch (start us, length us, event | category | flops | bytes accessed | tf_op | source)
XLA Modules:
  0.0 144.1 jit_solution(10237097122672443739)
XLA Ops:
  0.6 0.8 and_select_fusion.5
  3.7 5.0 %collective-permute-start.5 = (bf16[97,256]{1,0:T(8,128)(2,1)S(1)}, bf16[97,256]{1,0:T(8,128)(2,1)}, u32[]{:S(2)}, u32[]{:S(2)}) collective-permute-start(bf16[97,256]{1,0:T(8,128)(2,1)S(1)} %constant_dynamic-update-slice_fusion), channel_id=1, source_target_pairs={{0,3},{1,0},{2,1},{3,2},{4,7},{5,4},{6,5},{7,6},{8,11},{9,8},{10,9... | collective-permute-start | bytes 149000 | tf_op jit(solution)/shard_map/ppermute | solution.py:96
  8.7 1.0 collective-permute-start.3
  9.8 1.5 %fusion = f32[128]{0:T(128)S(1)} fusion(bf16[128,4096]{1,0:T(8,128)(2,1)} %param.10), kind=kLoop, calls=%fused_computation.13 | loop fusion | flops 1572736 | bytes 1049088 | tf_op jit(solution)/shard_map/reduce_sum | solution.py:162
  13.2 2.6 %fusion.9 = f32[48,4096]{1,0:T(8,128)} fusion(bf16[128,4096]{1,0:T(8,128)(2,1)} %param.10, f32[4096]{0:T(1024)S(1)} %convert_element_type.77, f32[128]{0:T(128)S(1)} %get-tuple-element.27, s32[128]{0:T(128)} %bitcast.117), kind=kOutput, calls=%fused_computation.27 | convolution fusion | flops 52434944 | bytes 1852416 | tf_op jit(solution)/shard_map/dot_general | solution.py:166
  15.8 1.7 %reshape.332 = f32[48,4,1024]{2,1,0:T(4,128)S(1)} reshape(f32[48,4096]{1,0:T(8,128)} %fusion.9) | data formatting | bytes 1572864 | tf_op jit(solution)/shard_map/reshape | solution.py:170
  17.5 0.8 constant_dynamic-slice_fusion.3
  19.0 2.5 %collective-permute-start = (f32[48,1024]{1,0:T(8,128)}, f32[48,1024]{1,0:T(8,128)S(1)}, u32[]{:S(2)}, u32[]{:S(2)}) collective-permute-start(f32[48,1024]{1,0:T(8,128)} %bitcast.87), channel_id=1, source_target_pairs={{0,1},{1,2},{2,3},{3,0},{4,5},{5,6},{6,7},{7,4},{8,9},{9,10},{10,1... | collective-permute-start | bytes 589832 | tf_op jit(solution)/shard_map/ppermute | solution.py:129
  22.2 0.9 collective-permute-start.1
  26.5 1.5 %collective-permute-start.2 = (f32[48,1024]{1,0:T(8,128)}, f32[48,1024]{1,0:T(8,128)S(1)}, u32[]{:S(2)}, u32[]{:S(2)}) collective-permute-start(f32[48,1024]{1,0:T(8,128)} %bitcast.85), channel_id=1, source_target_pairs={{0,3},{1,0},{2,1},{3,2},{4,7},{5,4},{6,5},{7,6},{8,11},{9,8},{10,9... | collective-permute-start | bytes 589832 | tf_op jit(solution)/shard_map/ppermute | solution.py:129
  27.9 0.9 pad_maximum_fusion.4
  29.4 0.8 broadcast_select_fusion.1
  31.2 4.3 %collective-permute-done.1 = f32[48,1024]{1,0:T(8,128)} collective-permute-done((f32[48,1024]{1,0:T(8,128)}, f32[48,1024]{1,0:T(8,128)}, u32[]{:S(2)}, u32[]{:S(2)}) %collective-permute-start.1) | collective-permute-done | bytes 196640 | tf_op jit(solution)/shard_map/ppermute | solution.py:129
  35.5 1.3 collective-permute-done.2
  37.5 1.2 pad_maximum_fusion.1
  38.6 1.5 %gather_fusion = f32[4,48,1024]{2,1,0:T(8,128)} fusion(f32[4,48,1024]{2,1,0:T(8,128)S(1)} %pad_maximum_fusion.1, s32[1024]{0:T(1024)S(1)} %pad_clamp_fusion.2), kind=kCustom, calls=%fused_computation | custom fusion | bytes 1572880 | tf_op jit(solution)/shard_map/jit(_take)/gather | solution.py:131
  40.1 1.3 select_reduce_fusion
  42.1 4.1 %collective-permute-start.8 = (bf16[48,1024]{1,0:T(8,128)(2,1)}, bf16[48,1024]{1,0:T(8,128)(2,1)S(1)}, u32[]{:S(2)}, u32[]{:S(2)}) collective-permute-start(bf16[48,1024]{1,0:T(8,128)(2,1)} %divide_convert_fusion), channel_id=1, source_target_pairs={{0,3},{1,0},{2,1},{3,2},{4,7},{5,4},{6,5},{7,6},{8,11},{9,8},{10,9... | collective-permute-start | bytes 294920 | tf_op jit(solution)/shard_map/ppermute | solution.py:96
  47.0 1.0 pad_maximum_fusion.2
  48.7 1.5 %broadcast_select_fusion = bf16[2,4,97,256]{3,2,1,0:T(8,128)(2,1)} fusion(bf16[2,4,97,256]{3,2,1,0:T(8,128)(2,1)S(1)} %gather_fusion.3, pred[2]{0:T(512)(128)(4,1)} %compare_and_fusion), kind=kLoop, calls=%fused_computation.40 | loop fusion | flops 198656 | bytes 794626 | tf_op jit(solution)/shard_map/jit(_take)/select_n | solution.py:111
  50.2 2.4 %collective-permute-start.12 = (bf16[2,4,97,256]{3,2,1,0:T(8,128)(2,1)}, bf16[2,4,97,256]{3,2,1,0:T(8,128)(2,1)}, u32[]{:S(2)}, u32[]{:S(2)}) collective-permute-start(bf16[2,4,97,256]{3,2,1,0:T(8,128)(2,1)} %broadcast_select_fusion), channel_id=1, source_target_pairs={{0,24},{4,28},{8,0},{12,4},{16,8},{20,12},{24,16},{28,20},{1,25},{... | collective-permute-start | bytes 1191944 | tf_op jit(solution)/shard_map/ppermute | solution.py:113
  53.7 0.8 bitcast_select_fusion
  54.5 1.6 %collective-permute-done.7 = bf16[48,1024]{1,0:T(8,128)(2,1)S(1)} collective-permute-done((bf16[48,1024]{1,0:T(8,128)(2,1)}, bf16[48,1024]{1,0:T(8,128)(2,1)S(1)}, u32[]{:S(2)}, u32[]{:S(2)}) %collective-permute-start.7) | collective-permute-done | bytes 98336 | tf_op jit(solution)/shard_map/ppermute | solution.py:96
  57.6 5.7 %collective-permute-done.12 = bf16[2,4,97,256]{3,2,1,0:T(8,128)(2,1)} collective-permute-done((bf16[2,4,97,256]{3,2,1,0:T(8,128)(2,1)}, bf16[2,4,97,256]{3,2,1,0:T(8,128)(2,1)}, u32[]{:S(2)}, u32[]{:S(2)}) %collective-permute-start.12) | collective-permute-done | bytes 397344 | tf_op jit(solution)/shard_map/ppermute | solution.py:113
  63.3 9.7 %collective-permute-done.11 = bf16[2,4,97,256]{3,2,1,0:T(8,128)(2,1)} collective-permute-done((bf16[2,4,97,256]{3,2,1,0:T(8,128)(2,1)}, bf16[2,4,97,256]{3,2,1,0:T(8,128)(2,1)}, u32[]{:S(2)}, u32[]{:S(2)}) %collective-permute-start.11) | collective-permute-done | bytes 397344 | tf_op jit(solution)/shard_map/ppermute | solution.py:113
  73.0 2.7 %pad_maximum_fusion = bf16[4,2,4,97,256]{4,3,2,1,0:T(8,128)(2,1)} fusion(bf16[1,2,4,97,256]{4,3,2,1,0:T(8,128)(2,1)} %bitcast.21, bf16[1,2,4,97,256]{4,3,2,1,0:T(8,128)(2,1)} %bitcast.20, bf16[1,2,4,97,256]{4,3,2,1,0:T(8,128)(2,1)} %bitcast.19, bf16[1,2,4,97,256]{4,3,2,1,0:T(8,128)(2,1)S(1)} %bitcast_select_fusion), kind=kLoop, calls=%fused_computation.22 | loop fusion | flops 2383872 | bytes 3178496 | tf_op jit(solution)/shard_map/stack | solution.py:115
  75.7 3.4 %gather_fusion.4 = bf16[4,2,4,97,256]{4,3,2,1,0:T(8,128)(2,1)} fusion(bf16[4,2,4,97,256]{4,3,2,1,0:T(8,128)(2,1)} %pad_maximum_fusion, s32[1024]{0:T(1024)} %pad_clamp_fusion), kind=kCustom, calls=%fused_computation.4 | custom fusion | bytes 3178512 | tf_op jit(solution)/shard_map/jit(_take)/gather | solution.py:115
  79.1 2.3 %copy_select_fusion = bf16[8,4,97,256]{3,1,2,0:T(4,128)(2,1)S(1)} fusion(bf16[8,4,97,256]{3,2,1,0:T(8,128)(2,1)} %bitcast.90, pred[8]{0:T(512)(128)(4,1)S(1)} %copy-done.16), kind=kLoop, calls=%fused_computation.23 | loop fusion | flops 794624 | bytes 3178504 | tf_op jit(solution)/shard_map/jit(_take)/select_n | solution.py:115
  81.4 1.6 %fusion.39 = (bf16[8,4,48,256]{3,1,2,0:T(4,128)(2,1)}, bf16[8,4,48,256]{3,1,2,0:T(4,128)(2,1)S(1)}) fusion(bf16[8,4,97,256]{3,1,2,0:T(4,128)(2,1)S(1)} %copy_select_fusion), kind=kLoop, calls=%fused_computation.142 | loop fusion | bytes 3145728 | tf_op jit(solution)/shard_map/slice | solution.py:183
  83.1 0.8 copy.37
  83.9 3.5 %all-to-all-start = ((bf16[8,48,512]{2,1,0:T(8,128)(2,1)}), bf16[8,48,512]{2,1,0:T(8,128)(2,1)S(1)}, u32[]{:S(2)}, u32[]{:S(2)}) async-start(bf16[8,48,512]{2,1,0:T(8,128)(2,1)} %bitcast.84), calls=%async_computation | async-start | bytes 786432 | tf_op jit(solution)/shard_map/all_to_all | solution.py:179
  87.5 1.3 copy.29
  90.5 1.8 %convolution_multiply_fusion = f32[384,1024]{1,0:T(8,128)} fusion(bf16[384,384]{0,1:T(8,128)(2,1)S(1)} %subtract_convert_fusion, bf16[384,1024]{1,0:T(8,128)(2,1)S(1)} %bitcast.94), kind=kOutput, calls=%fused_computation.24 | convolution fusion | flops 302383104 | bytes 2654208 | tf_op jit(solution)/shard_map/dot_general | solution.py:204
  93.1 1.4 dynamic_slice.23
  94.5 1.7 %convolution_multiply_fusion.2 = f32[48,256]{1,0:T(8,128)} fusion(bf16[384,1024]{1,0:T(8,128)(2,1)} %bitcast.98, s32[]{:T(128)S(6)} %select_n.279, bf16[384,384]{0,1:T(8,128)(2,1)} %copy-done.2, s32[]{:T(128)S(6)} %select_n.278), kind=kOutput, calls=%fused_computation.26 | convolution fusion | flops 9449472 | bytes 282632 | tf_op jit(solution)/shard_map/dot_general | solution.py:212
  96.2 2.3 %fusion.19 = f32[48,1024]{1,0:T(8,128)} fusion(bf16[1024,1024]{1,0:T(8,128)(2,1)S(1)} %copy-done, f32[384,1024]{1,0:T(8,128)} %convolution_multiply_fusion, s32[]{:T(128)S(6)} %select_n.278), kind=kOutput, calls=%fused_computation.61 | convolution fusion | flops 100663296 | bytes 2392068 | tf_op jit(solution)/shard_map/dot_general | solution.py:216
  98.6 20.0 %all_gather.3 = f32[48,4096]{1,0:T(8,128)S(1)} all-gather(f32[48,1024]{1,0:T(8,128)} %fusion.19), channel_id=1, replica_groups=mesh['dp'=8,'fsdp'=4] {'fsdp'}, dimensions={1}, use_global_device_ids=true | all-gather | bytes 983040 | tf_op jit(solution)/shard_map/all_gather | solution.py:223
  118.5 2.4 %fusion.8 = (f32[4096]{0:T(1024)S(1)}, f32[128]{0:T(128)S(1)}, f32[128,4096]{1,0:T(8,128)S(1)}) fusion(bf16[128,4096]{1,0:T(8,128)(2,1)S(1)} %copy-done.1, f32[128]{0:T(128)} %copy-done.14, f32[4096]{0:T(1024)S(1)} %copy-done.7, f32[48,4096]{1,0:T(8,128)S(1)} %all_gather.3, f32[48]{0:T(128)} %copy-done.11, s32[128]{0:T(128)} %bitcast.118), kind=kOutput, calls=%fused_computation.21 | convolution fusion | flops 305858432 | bytes 3966656 | tf_op jit(solution)/shard_map/dot_general | solution.py:225
  121.0 1.6 %fusion.5 = bf16[128,4096]{1,0:T(8,128)(2,1)} fusion(bf16[128,4096]{1,0:T(8,128)(2,1)S(1)} %copy-done.1, f32[128,4096]{1,0:T(8,128)S(1)} %get-tuple-element.32, f32[128]{0:T(128)S(1)} %broadcast_multiply_fusion, f32[128]{0:T(128)S(1)} %copy-done.13, f32[4096]{0:T(1024)S(1)} %copy-done.7, f32[128]{0:T(128)S(1)} %copy-done.15), kind=kLoop, calls=%fused_computation.18 | loop fusion | flops 3670016 | bytes 4212224 | tf_op jit(solution)/shard_map/convert_element_type | solution.py:235
  124.1 2.9 %collective-permute-start.16 = (f32[2,4096]{1,0:T(2,128)S(1)}, f32[2,4096]{1,0:T(2,128)S(1)}, u32[]{:S(2)}, u32[]{:S(2)}) collective-permute-start(f32[2,4096]{1,0:T(2,128)S(1)} %broadcast_select_fusion.2), channel_id=1, source_target_pairs={{0,24},{4,28},{8,0},{12,4},{16,8},{20,12},{24,16},{28,20},{1,25},{... | collective-permute-start | bytes 98312 | tf_op jit(solution)/shard_map/ppermute | solution.py:113
  128.9 2.0 %collective-permute-done.15 = f32[2,4096]{1,0:T(2,128)S(1)} collective-permute-done((f32[2,4096]{1,0:T(2,128)S(1)}, f32[2,4096]{1,0:T(2,128)S(1)}, u32[]{:S(2)}, u32[]{:S(2)}) %collective-permute-start.15) | collective-permute-done | bytes 32800 | tf_op jit(solution)/shard_map/ppermute | solution.py:113
  130.9 1.4 collective-permute-done.14
  132.5 0.8 gather_fusion.6
  134.0 1.9 %collective-permute-start.19 = (f32[4096]{0:T(1024)S(1)}, f32[4096]{0:T(1024)S(1)}, u32[]{:S(2)}, u32[]{:S(2)}) collective-permute-start(f32[4096]{0:T(1024)S(1)} %select_reduce_fusion.2), channel_id=1, source_target_pairs={{0,3},{1,0},{2,1},{3,2},{4,7},{5,4},{6,5},{7,6},{8,11},{9,8},{10,9... | collective-permute-start | bytes 49160 | tf_op jit(solution)/shard_map/ppermute | solution.py:96
  135.9 1.0 collective-permute-start.17
  136.9 2.1 %fusion.16 = f32[512,256]{1,0:T(8,128)} fusion(bf16[384,512]{1,0:T(8,128)(2,1)S(1)} %bitcast.96, f32[384,1024]{1,0:T(8,128)} %convolution_multiply_fusion, s32[]{:T(128)S(6)} %select_n.279), kind=kOutput, calls=%fused_computation.49 | convolution fusion | flops 100663296 | bytes 1114116 | tf_op jit(solution)/shard_map/dot_general | solution.py:220
  139.1 1.5 %collective-permute-done.18 = f32[4096]{0:T(1024)S(1)} collective-permute-done((f32[4096]{0:T(1024)S(1)}, f32[4096]{0:T(1024)S(1)}, u32[]{:S(2)}, u32[]{:S(2)}) %collective-permute-start.18) | collective-permute-done | bytes 16416 | tf_op jit(solution)/shard_map/ppermute | solution.py:96
  140.6 0.9 collective-permute-done.17
  (108 shorter events, 23.5 us)
Async XLA Ops:
  0.6 95.6 %copy-start = (bf16[1024,1024]{1,0:T(8,128)(2,1)S(1)}, bf16[1024,1024]{1,0:T(8,128)(2,1)}, u32[]{:S(2)}) copy-start(bf16[1024,1024]{1,0:T(8,128)(2,1)} %param.13) | copy-start | bytes 6291460
  3.7 22.8 %collective-permute-start.5 = (bf16[97,256]{1,0:T(8,128)(2,1)S(1)}, bf16[97,256]{1,0:T(8,128)(2,1)}, u32[]{:S(2)}, u32[]{:S(2)}) collective-permute-start(bf16[97,256]{1,0:T(8,128)(2,1)S(1)} %constant_dynamic-update-slice_fusion), channel_id=1, source_target_pairs={{0,3},{1,0},{2,1},{3,2},{4,7},{5,4},{6,5},{7,6},{8,11},{9,8},{10,9... | collective-permute-start | bytes 149000 | tf_op jit(solution)/shard_map/ppermute | solution.py:96
  8.7 19.2 %collective-permute-start.4 = (bf16[97,256]{1,0:T(8,128)(2,1)S(1)}, bf16[97,256]{1,0:T(8,128)(2,1)}, u32[]{:S(2)}, u32[]{:S(2)}) collective-permute-start(bf16[97,256]{1,0:T(8,128)(2,1)S(1)} %constant_dynamic-update-slice_fusion), channel_id=1, source_target_pairs={{0,2},{1,3},{2,0},{3,1},{4,6},{5,7},{6,4},{7,5},{8,10},{9,11},{10,... | collective-permute-start | bytes 149000 | tf_op jit(solution)/shard_map/ppermute | solution.py:96
  8.7 19.2 %collective-permute-start.3 = (bf16[97,256]{1,0:T(8,128)(2,1)S(1)}, bf16[97,256]{1,0:T(8,128)(2,1)}, u32[]{:S(2)}, u32[]{:S(2)}) collective-permute-start(bf16[97,256]{1,0:T(8,128)(2,1)S(1)} %constant_dynamic-update-slice_fusion), channel_id=1, source_target_pairs={{0,1},{1,2},{2,3},{3,0},{4,5},{5,6},{6,7},{7,4},{8,9},{9,10},{10,1... | collective-permute-start | bytes 149000 | tf_op jit(solution)/shard_map/ppermute | solution.py:96
  11.9 0.7 copy-start.14
  12.6 0.6 copy-start.6
  19.0 12.2 %collective-permute-start = (f32[48,1024]{1,0:T(8,128)}, f32[48,1024]{1,0:T(8,128)S(1)}, u32[]{:S(2)}, u32[]{:S(2)}) collective-permute-start(f32[48,1024]{1,0:T(8,128)} %bitcast.87), channel_id=1, source_target_pairs={{0,1},{1,2},{2,3},{3,0},{4,5},{5,6},{6,7},{7,4},{8,9},{9,10},{10,1... | collective-permute-start | bytes 589832 | tf_op jit(solution)/shard_map/ppermute | solution.py:129
  22.2 13.3 %collective-permute-start.1 = (f32[48,1024]{1,0:T(8,128)}, f32[48,1024]{1,0:T(8,128)}, u32[]{:S(2)}, u32[]{:S(2)}) collective-permute-start(f32[48,1024]{1,0:T(8,128)} %bitcast.86), channel_id=1, source_target_pairs={{0,2},{1,3},{2,0},{3,1},{4,6},{5,7},{6,4},{7,5},{8,10},{9,11},{10,... | collective-permute-start | bytes 589832 | tf_op jit(solution)/shard_map/ppermute | solution.py:129
  23.2 3.3 %copy-start.12 = (pred[4]{0:T(512)(128)(4,1)}, pred[4]{0:T(512)(128)(4,1)S(1)}, u32[]{:S(2)}) copy-start(pred[4]{0:T(512)(128)(4,1)S(1)} %get-tuple-element.33) | copy-start | bytes 16
  23.2 16.9 %copy-start.8 = (pred[4]{0:T(512)(128)(4,1)}, pred[4]{0:T(512)(128)(4,1)S(1)}, u32[]{:S(2)}) copy-start(pred[4]{0:T(512)(128)(4,1)S(1)} %get-tuple-element.34) | copy-start | bytes 16
  23.2 16.9 %copy-start.10 = (s32[1024]{0:T(1024)}, s32[1024]{0:T(1024)S(1)}, u32[]{:S(2)}) copy-start(s32[1024]{0:T(1024)S(1)} %pad_clamp_fusion.2) | copy-start | bytes 12292
  26.5 10.3 %collective-permute-start.2 = (f32[48,1024]{1,0:T(8,128)}, f32[48,1024]{1,0:T(8,128)S(1)}, u32[]{:S(2)}, u32[]{:S(2)}) collective-permute-start(f32[48,1024]{1,0:T(8,128)} %bitcast.85), channel_id=1, source_target_pairs={{0,3},{1,0},{2,1},{3,2},{4,7},{5,4},{6,5},{7,6},{8,11},{9,8},{10,9... | collective-permute-start | bytes 589832 | tf_op jit(solution)/shard_map/ppermute | solution.py:129
  30.9 16.1 %collective-permute-start.9 = (bf16[4,97,256]{2,1,0:T(8,128)(2,1)}, bf16[4,97,256]{2,1,0:T(8,128)(2,1)}, u32[]{:S(2)}, u32[]{:S(2)}) collective-permute-start(bf16[4,97,256]{2,1,0:T(8,128)(2,1)} %broadcast_select_fusion.1), channel_id=1, source_target_pairs={{0,4},{4,0},{8,12},{12,8},{16,20},{20,16},{24,28},{28,24},{1,5},{5... | collective-permute-start | bytes 595976 | tf_op jit(solution)/shard_map/ppermute | solution.py:108
  31.1 15.8 %copy-start.11 = (f32[48]{0:T(128)}, f32[48]{0:T(128)S(1)}, u32[]{:S(2)}) copy-start(f32[48]{0:T(128)S(1)} %convert_reduce_fusion) | copy-start | bytes 580
  31.2 5.6 %copy-start.4 = (f32[48,1024]{1,0:T(8,128)}, f32[48,1024]{1,0:T(8,128)S(1)}, u32[]{:S(2)}) copy-start(f32[48,1024]{1,0:T(8,128)S(1)} %collective-permute-done) | copy-start | bytes 589828
  36.8 0.7 copy-start.5
  42.1 11.0 %collective-permute-start.8 = (bf16[48,1024]{1,0:T(8,128)(2,1)}, bf16[48,1024]{1,0:T(8,128)(2,1)S(1)}, u32[]{:S(2)}, u32[]{:S(2)}) collective-permute-start(bf16[48,1024]{1,0:T(8,128)(2,1)} %divide_convert_fusion), channel_id=1, source_target_pairs={{0,3},{1,0},{2,1},{3,2},{4,7},{5,4},{6,5},{7,6},{8,11},{9,8},{10,9... | collective-permute-start | bytes 294920 | tf_op jit(solution)/shard_map/ppermute | solution.py:96
  46.2 9.9 %collective-permute-start.7 = (bf16[48,1024]{1,0:T(8,128)(2,1)}, bf16[48,1024]{1,0:T(8,128)(2,1)S(1)}, u32[]{:S(2)}, u32[]{:S(2)}) collective-permute-start(bf16[48,1024]{1,0:T(8,128)(2,1)} %divide_convert_fusion), channel_id=1, source_target_pairs={{0,2},{1,3},{2,0},{3,1},{4,6},{5,7},{6,4},{7,5},{8,10},{9,11},{10,... | collective-permute-start | bytes 294920 | tf_op jit(solution)/shard_map/ppermute | solution.py:96
  46.9 9.2 %collective-permute-start.6 = (bf16[48,1024]{1,0:T(8,128)(2,1)}, bf16[48,1024]{1,0:T(8,128)(2,1)S(1)}, u32[]{:S(2)}, u32[]{:S(2)}) collective-permute-start(bf16[48,1024]{1,0:T(8,128)(2,1)} %divide_convert_fusion), channel_id=1, source_target_pairs={{0,1},{1,2},{2,3},{3,0},{4,5},{5,6},{6,7},{7,4},{8,9},{9,10},{10,1... | collective-permute-start | bytes 294920 | tf_op jit(solution)/shard_map/ppermute | solution.py:96
  50.2 13.1 %collective-permute-start.12 = (bf16[2,4,97,256]{3,2,1,0:T(8,128)(2,1)}, bf16[2,4,97,256]{3,2,1,0:T(8,128)(2,1)}, u32[]{:S(2)}, u32[]{:S(2)}) collective-permute-start(bf16[2,4,97,256]{3,2,1,0:T(8,128)(2,1)} %broadcast_select_fusion), channel_id=1, source_target_pairs={{0,24},{4,28},{8,0},{12,4},{16,8},{20,12},{24,16},{28,20},{1,25},{... | collective-permute-start | bytes 1191944 | tf_op jit(solution)/shard_map/ppermute | solution.py:113
  52.6 20.3 %collective-permute-start.11 = (bf16[2,4,97,256]{3,2,1,0:T(8,128)(2,1)}, bf16[2,4,97,256]{3,2,1,0:T(8,128)(2,1)}, u32[]{:S(2)}, u32[]{:S(2)}) collective-permute-start(bf16[2,4,97,256]{3,2,1,0:T(8,128)(2,1)} %broadcast_select_fusion), channel_id=1, source_target_pairs={{0,16},{4,20},{8,24},{12,28},{16,0},{20,4},{24,8},{28,12},{1,17},{... | collective-permute-start | bytes 1191944 | tf_op jit(solution)/shard_map/ppermute | solution.py:113
  53.2 19.8 %collective-permute-start.10 = (bf16[2,4,97,256]{3,2,1,0:T(8,128)(2,1)}, bf16[2,4,97,256]{3,2,1,0:T(8,128)(2,1)}, u32[]{:S(2)}, u32[]{:S(2)}) collective-permute-start(bf16[2,4,97,256]{3,2,1,0:T(8,128)(2,1)} %broadcast_select_fusion), channel_id=1, source_target_pairs={{0,8},{4,12},{8,16},{12,20},{16,24},{20,28},{24,0},{28,4},{1,9},{5... | collective-permute-start | bytes 1191944 | tf_op jit(solution)/shard_map/ppermute | solution.py:113
  75.7 3.4 %copy-start.16 = (pred[8]{0:T(512)(128)(4,1)S(1)}, pred[8]{0:T(512)(128)(4,1)}, u32[]{:S(2)}) copy-start(pred[8]{0:T(512)(128)(4,1)} %broadcast_in_dim.112) | copy-start | bytes 28
  83.9 14.7 %all-to-all-start = ((bf16[8,48,512]{2,1,0:T(8,128)(2,1)}), bf16[8,48,512]{2,1,0:T(8,128)(2,1)S(1)}, u32[]{:S(2)}, u32[]{:S(2)}) async-start(bf16[8,48,512]{2,1,0:T(8,128)(2,1)} %bitcast.84), calls=%async_computation | async-start | bytes 786432 | tf_op jit(solution)/shard_map/all_to_all | solution.py:179
  89.0 3.4 %copy-start.3 = (bf16[48,8,4,256]{3,1,2,0:T(8,128)(2,1)}, bf16[48,8,4,256]{3,1,2,0:T(8,128)(2,1)S(1)}, u32[]{:S(2)}) copy-start(bf16[48,8,4,256]{3,1,2,0:T(8,128)(2,1)S(1)} %copy.28) | copy-start | bytes 2359300
  90.5 1.8 %copy-start.2 = (bf16[384,384]{0,1:T(8,128)(2,1)}, bf16[384,384]{0,1:T(8,128)(2,1)S(1)}, u32[]{:S(2)}) copy-start(bf16[384,384]{0,1:T(8,128)(2,1)S(1)} %subtract_convert_fusion) | copy-start | bytes 884740
  92.3 26.2 %copy-start.1 = (bf16[128,4096]{1,0:T(8,128)(2,1)S(1)}, bf16[128,4096]{1,0:T(8,128)(2,1)}, u32[]{:S(2)}) copy-start(bf16[128,4096]{1,0:T(8,128)(2,1)} %param.10) | copy-start | bytes 3145732
  92.3 26.2 %copy-start.7 = (f32[4096]{0:T(1024)S(1)}, f32[4096]{0:T(1024)}, u32[]{:S(2)}) copy-start(f32[4096]{0:T(1024)} %copy-done.6) | copy-start | bytes 49156
  118.5 2.5 %copy-start.13 = (f32[128]{0:T(128)S(1)}, f32[128]{0:T(128)}, u32[]{:S(2)}) copy-start(f32[128]{0:T(128)} %get-tuple-element.26) | copy-start | bytes 1540
  118.5 2.5 %copy-start.15 = (f32[128]{0:T(128)S(1)}, f32[128]{0:T(128)}, u32[]{:S(2)}) copy-start(f32[128]{0:T(128)} %copy-done.14) | copy-start | bytes 1540
  120.9 1.7 %collective-permute-start.13 = (f32[4096]{0:T(1024)S(1)}, f32[4096]{0:T(1024)S(1)}, u32[]{:S(2)}, u32[]{:S(2)}) collective-permute-start(f32[4096]{0:T(1024)S(1)} %get-tuple-element.14), channel_id=1, source_target_pairs={{0,4},{4,0},{8,12},{12,8},{16,20},{20,16},{24,28},{28,24},{1,5},{5... | collective-permute-start | bytes 49160 | tf_op jit(solution)/shard_map/ppermute | solution.py:108
  122.6 19.6 %copy-start.9 = (pred[4]{0:T(512)(128)(4,1)S(1)}, pred[4]{0:T(512)(128)(4,1)}, u32[]{:S(2)}) copy-start(pred[4]{0:T(512)(128)(4,1)} %copy-done.8) | copy-start | bytes 16
  124.1 4.8 %collective-permute-start.16 = (f32[2,4096]{1,0:T(2,128)S(1)}, f32[2,4096]{1,0:T(2,128)S(1)}, u32[]{:S(2)}, u32[]{:S(2)}) collective-permute-start(f32[2,4096]{1,0:T(2,128)S(1)} %broadcast_select_fusion.2), channel_id=1, source_target_pairs={{0,24},{4,28},{8,0},{12,4},{16,8},{20,12},{24,16},{28,20},{1,25},{... | collective-permute-start | bytes 98312 | tf_op jit(solution)/shard_map/ppermute | solution.py:113
  127.0 3.9 %collective-permute-start.15 = (f32[2,4096]{1,0:T(2,128)S(1)}, f32[2,4096]{1,0:T(2,128)S(1)}, u32[]{:S(2)}, u32[]{:S(2)}) collective-permute-start(f32[2,4096]{1,0:T(2,128)S(1)} %broadcast_select_fusion.2), channel_id=1, source_target_pairs={{0,16},{4,20},{8,24},{12,28},{16,0},{20,4},{24,8},{28,12},{1,17},{... | collective-permute-start | bytes 98312 | tf_op jit(solution)/shard_map/ppermute | solution.py:113
  127.6 4.8 %collective-permute-start.14 = (f32[2,4096]{1,0:T(2,128)S(1)}, f32[2,4096]{1,0:T(2,128)S(1)}, u32[]{:S(2)}, u32[]{:S(2)}) collective-permute-start(f32[2,4096]{1,0:T(2,128)S(1)} %broadcast_select_fusion.2), channel_id=1, source_target_pairs={{0,8},{4,12},{8,16},{12,20},{16,24},{20,28},{24,0},{28,4},{1,9},{5... | collective-permute-start | bytes 98312 | tf_op jit(solution)/shard_map/ppermute | solution.py:113
  134.0 5.0 %collective-permute-start.19 = (f32[4096]{0:T(1024)S(1)}, f32[4096]{0:T(1024)S(1)}, u32[]{:S(2)}, u32[]{:S(2)}) collective-permute-start(f32[4096]{0:T(1024)S(1)} %select_reduce_fusion.2), channel_id=1, source_target_pairs={{0,3},{1,0},{2,1},{3,2},{4,7},{5,4},{6,5},{7,6},{8,11},{9,8},{10,9... | collective-permute-start | bytes 49160 | tf_op jit(solution)/shard_map/ppermute | solution.py:96
  135.9 4.6 %collective-permute-start.18 = (f32[4096]{0:T(1024)S(1)}, f32[4096]{0:T(1024)S(1)}, u32[]{:S(2)}, u32[]{:S(2)}) collective-permute-start(f32[4096]{0:T(1024)S(1)} %select_reduce_fusion.2), channel_id=1, source_target_pairs={{0,2},{1,3},{2,0},{3,1},{4,6},{5,7},{6,4},{7,5},{8,10},{9,11},{10,... | collective-permute-start | bytes 49160 | tf_op jit(solution)/shard_map/ppermute | solution.py:96
  135.9 5.5 %collective-permute-start.17 = (f32[4096]{0:T(1024)S(1)}, f32[4096]{0:T(1024)S(1)}, u32[]{:S(2)}, u32[]{:S(2)}) collective-permute-start(f32[4096]{0:T(1024)S(1)} %select_reduce_fusion.2), channel_id=1, source_target_pairs={{0,1},{1,2},{2,3},{3,0},{4,5},{5,6},{6,7},{7,4},{8,9},{9,10},{10,1... | collective-permute-start | bytes 49160 | tf_op jit(solution)/shard_map/ppermute | solution.py:96

commit v6 on v3

--- a/solution.py
+++ b/solution.py
@@ -150,14 +150,14 @@
     pooled_part = jnp.dot(member.astype(jnp.bfloat16), normed, preferred_element_type=jnp.float32)
     counts = jnp.sum((group_ids[None, :] == labels).astype(jnp.float32), axis=1)
     chunk = model_width // feature_count
+    gathered = gather_blocks(group_blocks, "dp")
+    pooled_part, gathered = lax.optimization_barrier((pooled_part, gathered))
     pooled_chunk = scatter_sum(
         pooled_part.reshape(rows, feature_count, chunk).transpose(1, 0, 2), "fsdp"
     )
     mean_chunk = (pooled_chunk / counts[:, None]).astype(jnp.bfloat16)
     mean_pooled = gather_blocks(mean_chunk, "fsdp").transpose(1, 0, 2).reshape(rows, model_width)
 
-    gathered = gather_blocks(group_blocks, "dp")
-    mean_pooled, gathered = lax.optimization_barrier((mean_pooled, gathered))
     slice_width = model_width // data_count
     pieces = mean_pooled.reshape(rows, data_count, slice_width).transpose(1, 0, 2)
     pieces = lax.all_to_all(pieces, "dp", 0, 0, tiled=True)

time: 137 us -> 148 us (1.080)
  waiting for transfers between devices: 14.3 us -> 36.9 us
  local copies, waits for them, and re-layouts: 30.4 us -> 24.5 us
  other arithmetic: 17 us -> 14 us
    ppermute x23, waiting for transfers between devices: 2.87 us -> 17.8 us  [gather_blocks(): lax.ppermute(x, axis, [(i, (i + s) % n) for i in range(n)])]
    ppermute x3, waiting for transfers between devices: 9.32 us -> 14.9 us  [scatter_sum(): lax.ppermute(piece, axis, [(i, (i + s) % n) for i in range(n)])]
    unnamed x60, local copies, waits for them, and re-layouts: 14.3 us -> 9.89 us
    all_to_all x1, starting transfers between devices: 5.81 us -> 3.45 us  [local_small(): pieces = lax.all_to_all(pieces, 'dp', 0, 0, tiled=True)]
    all_to_all x1, waiting for transfers between devices: 2.09 us -> 4.13 us  [local_small(): pieces = lax.all_to_all(pieces, 'dp', 0, 0, tiled=True)]
    ppermute x23, starting transfers between devices: 28.2 us -> 30.3 us  [gather_blocks(): lax.ppermute(x, axis, [(i, (i + s) % n) for i in range(n)])]
    select_n x4 -> x5, other arithmetic: 2.99 us -> 1.9 us  [gather_blocks(): return jnp.take(stack, order, axis=0)]
  transfers between devices with their start and end apart: 27 -> 27, of which waited for: 5 -> 10; matrix products, arithmetic and copies ran while one was open for 29% -> 15% of each run, Pallas kernels for 0% -> 0%
where the time goes in v6:
time: 148 us; the launch traced here: 147 us
  starting transfers between devices  37.7 us (25%)
  waiting for transfers between devices  36.9 us (25%)
  local copies, waits for them, and re-layouts  24.5 us (17%)
  blocking collectives  17.2 us (12%)
  other arithmetic  14 us (9%)
  matrix products  13.7 us (9%)
  between operations  2.95 us (2%)
    ppermute x23, starting transfers between devices, gather_blocks(): lax.ppermute(x, axis, [(i, (i + s) % n) for i in range(n)])  30.3 us
    ppermute x23, waiting for transfers between devices, gather_blocks(): lax.ppermute(x, axis, [(i, (i + s) % n) for i in range(n)])  17.8 us
    all_gather x1, blocking collectives, local_small(): mean_grad = lax.all_gather(mean_part, 'fsdp', axis=1, tiled=True)  17.2 us
    ppermute x3, waiting for transfers between devices, scatter_sum(): lax.ppermute(piece, axis, [(i, (i + s) % n) for i in range(n)])  14.9 us
    unnamed x60, local copies, waits for them, and re-layouts  9.89 us
    gather x5, local copies, waits for them, and re-layouts, gather_blocks(): return jnp.take(stack, order, axis=0)  5.85 us
    all_to_all x1, waiting for transfers between devices, local_small(): pieces = lax.all_to_all(pieces, 'dp', 0, 0, tiled=True)  4.13 us
    ppermute x3, starting transfers between devices, scatter_sum(): lax.ppermute(piece, axis, [(i, (i + s) % n) for i in range(n)])  3.95 us
  transfers between devices with their start and end apart: 27, of which 10 were waited for; matrix products, arithmetic and copies ran while one was open for 15% of the time, Pallas kernels for 0%

profile of v6, /device:TPU:0, one launch (start us, length us, event | category | flops | bytes accessed | tf_op | source)
XLA Modules:
  0.0 146.9 jit_solution(4782453382318751615)
XLA Ops:
  0.6 0.9 constant_dynamic-update-slice_fusion.2
  2.2 0.7 constant_dynamic-update-slice_fusion.1
  2.9 0.7 fusion.30
  3.7 5.1 %collective-permute-start.2 = (bf16[97,256]{1,0:T(8,128)(2,1)S(1)}, bf16[97,256]{1,0:T(8,128)(2,1)S(1)}, u32[]{:S(2)}, u32[]{:S(2)}) collective-permute-start(bf16[97,256]{1,0:T(8,128)(2,1)S(1)} %constant_dynamic-update-slice_fusion), channel_id=1, source_target_pairs={{0,3},{1,0},{2,1},{3,2},{4,7},{5,4},{6,5},{7,6},{8,11},{9,8},{10,9... | collective-permute-start | bytes 149000 | tf_op jit(solution)/shard_map/ppermute | solution.py:96
  8.8 1.0 collective-permute-start
  10.5 1.5 %fusion = f32[128]{0:T(128)S(1)} fusion(bf16[128,4096]{1,0:T(8,128)(2,1)} %param.10), kind=kLoop, calls=%fused_computation.11 | loop fusion | flops 1572736 | bytes 1049088 | tf_op jit(solution)/shard_map/reduce_sum | solution.py:146
  12.7 2.6 %fusion.9 = f32[48,4096]{1,0:T(8,128)} fusion(bf16[128,4096]{1,0:T(8,128)(2,1)} %param.10, f32[4096]{0:T(1024)S(1)} %convert_element_type.77, f32[128]{0:T(128)S(1)} %get-tuple-element.27, s32[128]{0:T(128)} %bitcast.123), kind=kOutput, calls=%fused_computation.24 | convolution fusion | flops 52434944 | bytes 1852416 | tf_op jit(solution)/shard_map/dot_general | solution.py:150
  16.2 1.5 %collective-permute-start.4 = (bf16[4,97,256]{2,1,0:T(8,128)(2,1)S(1)}, bf16[4,97,256]{2,1,0:T(8,128)(2,1)S(1)}, u32[]{:S(2)}, u32[]{:S(2)}) collective-permute-start(bf16[4,97,256]{2,1,0:T(8,128)(2,1)S(1)} %broadcast_select_fusion.1), channel_id=1, source_target_pairs={{0,8},{4,12},{8,16},{12,20},{16,24},{20,28},{24,0},{28,4},{1,9},{5... | collective-permute-start | bytes 595976 | tf_op jit(solution)/shard_map/ppermute | solution.py:96
  17.7 2.4 %collective-permute-start.5 = (bf16[4,97,256]{2,1,0:T(8,128)(2,1)S(1)}, bf16[4,97,256]{2,1,0:T(8,128)(2,1)S(1)}, u32[]{:S(2)}, u32[]{:S(2)}) collective-permute-start(bf16[4,97,256]{2,1,0:T(8,128)(2,1)S(1)} %broadcast_select_fusion.1), channel_id=1, source_target_pairs={{0,12},{4,16},{8,20},{12,24},{16,28},{20,0},{24,4},{28,8},{1,13},{... | collective-permute-start | bytes 595976 | tf_op jit(solution)/shard_map/ppermute | solution.py:96
  20.9 0.8 fusion.16
  21.7 2.4 %collective-permute-done.3 = bf16[4,97,256]{2,1,0:T(8,128)(2,1)S(1)} collective-permute-done((bf16[4,97,256]{2,1,0:T(8,128)(2,1)S(1)}, bf16[4,97,256]{2,1,0:T(8,128)(2,1)S(1)}, u32[]{:S(2)}, u32[]{:S(2)}) %collective-permute-start.3) | collective-permute-done | bytes 198688 | tf_op jit(solution)/shard_map/ppermute | solution.py:96
  24.1 1.4 collective-permute-start.8
  26.3 3.6 %collective-permute-start.9 = (bf16[4,97,256]{2,1,0:T(8,128)(2,1)S(1)}, bf16[4,97,256]{2,1,0:T(8,128)(2,1)S(1)}, u32[]{:S(2)}, u32[]{:S(2)}) collective-permute-start(bf16[4,97,256]{2,1,0:T(8,128)(2,1)S(1)} %broadcast_select_fusion.1), channel_id=1, source_target_pairs={{0,28},{4,0},{8,4},{12,8},{16,12},{20,16},{24,20},{28,24},{1,29},{... | collective-permute-start | bytes 595976 | tf_op jit(solution)/shard_map/ppermute | solution.py:96
  30.6 3.1 %collective-permute-done.5 = bf16[4,97,256]{2,1,0:T(8,128)(2,1)S(1)} collective-permute-done((bf16[4,97,256]{2,1,0:T(8,128)(2,1)S(1)}, bf16[4,97,256]{2,1,0:T(8,128)(2,1)S(1)}, u32[]{:S(2)}, u32[]{:S(2)}) %collective-permute-start.5) | collective-permute-done | bytes 198688 | tf_op jit(solution)/shard_map/ppermute | solution.py:96
  35.1 2.3 %collective-permute-done.7 = bf16[4,97,256]{2,1,0:T(8,128)(2,1)S(1)} collective-permute-done((bf16[4,97,256]{2,1,0:T(8,128)(2,1)S(1)}, bf16[4,97,256]{2,1,0:T(8,128)(2,1)S(1)}, u32[]{:S(2)}, u32[]{:S(2)}) %collective-permute-start.7) | collective-permute-done | bytes 198688 | tf_op jit(solution)/shard_map/ppermute | solution.py:96
  39.5 3.3 %gather_fusion.1 = bf16[8,4,97,256]{3,2,1,0:T(8,128)(2,1)} fusion(bf16[8,4,97,256]{3,2,1,0:T(8,128)(2,1)} %bitcast_dynamic-update-slice_fusion, s32[1024]{0:T(1024)S(1)} %pad_clamp_fusion), kind=kCustom, calls=%fused_computation.1 | custom fusion | bytes 3178528 | tf_op jit(solution)/shard_map/jit(_take)/gather | solution.py:100
  42.8 1.7 %broadcast_select_fusion = bf16[8,4,97,256]{3,2,1,0:T(8,128)(2,1)S(1)} fusion(bf16[8,4,97,256]{3,2,1,0:T(8,128)(2,1)} %gather_fusion.1, pred[8]{0:T(512)(128)(4,1)S(1)} %compare_and_fusion.1), kind=kLoop, calls=%fused_computation.20 | loop fusion | flops 794624 | bytes 3178504 | tf_op jit(solution)/shard_map/jit(_take)/select_n | solution.py:100
  45.1 1.0 copy.34
  46.9 1.8 %fusion.37 = (f32[384]{0:T(512)S(1)}, f32[384,384]{0,1:T(8,128)S(1)}) fusion(bf16[384,1024]{1,0:T(8,128)(2,1)} %bitcast.98, bf16[384,1024]{1,0:T(8,128)(2,1)S(1)} %bitcast.94), kind=kOutput, calls=%fused_computation.129 | convolution fusion | flops 302284416 | bytes 2164224 | tf_op jit(solution)/shard_map/dot_general | solution.py:176
  49.7 1.7 %reshape.233 = f32[48,4,1024]{2,1,0:T(4,128)S(1)} reshape(f32[48,4096]{1,0:T(8,128)} %fusion.9) | data formatting | bytes 1572864 | tf_op jit(solution)/shard_map/reshape | solution.py:156
  51.3 0.8 constant_dynamic-slice_fusion.3
  52.9 2.8 %collective-permute-start.12 = (f32[48,1024]{1,0:T(8,128)}, f32[48,1024]{1,0:T(8,128)}, u32[]{:S(2)}, u32[]{:S(2)}) collective-permute-start(f32[48,1024]{1,0:T(8,128)} %bitcast.86), channel_id=1, source_target_pairs={{0,3},{1,0},{2,1},{3,2},{4,7},{5,4},{6,5},{7,6},{8,11},{9,8},{10,9... | collective-permute-start | bytes 589832 | tf_op jit(solution)/shard_map/ppermute | solution.py:113
  56.4 1.1 collective-permute-start.11
  61.0 14.2 %collective-permute-done.11 = f32[48,1024]{1,0:T(8,128)} collective-permute-done((f32[48,1024]{1,0:T(8,128)}, f32[48,1024]{1,0:T(8,128)}, u32[]{:S(2)}, u32[]{:S(2)}) %collective-permute-start.11) | collective-permute-done | bytes 196640 | tf_op jit(solution)/shard_map/ppermute | solution.py:113
  75.2 1.2 pad_maximum_fusion
  76.4 1.5 %gather_fusion.2 = f32[4,48,1024]{2,1,0:T(8,128)} fusion(f32[4,48,1024]{2,1,0:T(8,128)S(1)} %pad_maximum_fusion, s32[1024]{0:T(1024)S(1)} %pad_clamp_fusion.1), kind=kCustom, calls=%fused_computation.2 | custom fusion | bytes 1572880 | tf_op jit(solution)/shard_map/jit(_take)/gather | solution.py:115
  77.9 1.3 select_reduce_fusion
  79.3 2.2 %collective-permute-start.14 = (bf16[48,1024]{1,0:T(8,128)(2,1)S(1)}, bf16[48,1024]{1,0:T(8,128)(2,1)S(1)}, u32[]{:S(2)}, u32[]{:S(2)}) collective-permute-start(bf16[48,1024]{1,0:T(8,128)(2,1)S(1)} %divide_convert_fusion), channel_id=1, source_target_pairs={{0,2},{1,3},{2,0},{3,1},{4,6},{5,7},{6,4},{7,5},{8,10},{9,11},{10,... | collective-permute-start | bytes 294920 | tf_op jit(solution)/shard_map/ppermute | solution.py:96
  81.5 1.9 %collective-permute-start.13 = (bf16[48,1024]{1,0:T(8,128)(2,1)S(1)}, bf16[48,1024]{1,0:T(8,128)(2,1)S(1)}, u32[]{:S(2)}, u32[]{:S(2)}) collective-permute-start(bf16[48,1024]{1,0:T(8,128)(2,1)S(1)} %divide_convert_fusion), channel_id=1, source_target_pairs={{0,1},{1,2},{2,3},{3,0},{4,5},{5,6},{6,7},{7,4},{8,9},{9,10},{10,1... | collective-permute-start | bytes 294920 | tf_op jit(solution)/shard_map/ppermute | solution.py:96
  84.3 6.6 %collective-permute-done.14 = bf16[48,1024]{1,0:T(8,128)(2,1)S(1)} collective-permute-done((bf16[48,1024]{1,0:T(8,128)(2,1)S(1)}, bf16[48,1024]{1,0:T(8,128)(2,1)S(1)}, u32[]{:S(2)}, u32[]{:S(2)}) %collective-permute-start.14) | collective-permute-done | bytes 98336 | tf_op jit(solution)/shard_map/ppermute | solution.py:96
  92.0 0.9 copy.27
  92.9 3.5 %all-to-all-start = ((bf16[8,48,512]{2,1,0:T(8,128)(2,1)}), bf16[8,48,512]{2,1,0:T(8,128)(2,1)S(1)}, u32[]{:S(2)}, u32[]{:S(2)}) async-start(bf16[8,48,512]{2,1,0:T(8,128)(2,1)} %copy.27), calls=%async_computation | async-start | bytes 786432 | tf_op jit(solution)/shard_map/all_to_all | solution.py:163
  96.4 1.7 %convolution_multiply_fusion.2 = f32[48,256]{1,0:T(8,128)} fusion(bf16[384,1024]{1,0:T(8,128)(2,1)} %bitcast.99, s32[]{:T(128)S(6)} %select_n.187, bf16[384,384]{0,1:T(8,128)(2,1)S(1)} %subtract_convert_fusion, s32[]{:T(128)S(6)} %select_n.186), kind=kOutput, calls=%fused_computation.23 | convolution fusion | flops 9449472 | bytes 282632 | tf_op jit(solution)/shard_map/dot_general | solution.py:196
  98.1 2.4 %fusion.20 = f32[48,1024]{1,0:T(8,128)} fusion(bf16[1024,1024]{1,0:T(8,128)(2,1)S(1)} %copy-done, f32[384,1024]{1,0:T(8,128)} %copy-done.4, s32[]{:T(128)S(6)} %select_n.186), kind=kOutput, calls=%fused_computation.63 | convolution fusion | flops 100663296 | bytes 2392068 | tf_op jit(solution)/shard_map/dot_general | solution.py:200
  100.5 4.1 %all-to-all-done = bf16[8,48,512]{2,1,0:T(8,128)(2,1)S(1)} async-done(((bf16[8,48,512]{2,1,0:T(8,128)(2,1)}), bf16[8,48,512]{2,1,0:T(8,128)(2,1)S(1)}, u32[]{:S(2)}, u32[]{:S(2)}) %all-to-all-start) | async-done | bytes 393248 | tf_op jit(solution)/shard_map/all_to_all | solution.py:163
  104.6 17.2 %all_gather.3 = f32[48,4096]{1,0:T(8,128)S(1)} all-gather(f32[48,1024]{1,0:T(8,128)} %fusion.20), channel_id=1, replica_groups=mesh['dp'=8,'fsdp'=4] {'fsdp'}, dimensions={1}, use_global_device_ids=true | all-gather | bytes 983040 | tf_op jit(solution)/shard_map/all_gather | solution.py:207
  121.9 2.4 %fusion.8 = (f32[4096]{0:T(1024)S(1)}, f32[128]{0:T(128)S(1)}, f32[128,4096]{1,0:T(8,128)S(1)}) fusion(bf16[128,4096]{1,0:T(8,128)(2,1)S(1)} %copy-done.1, f32[128]{0:T(128)} %copy-done.20, f32[4096]{0:T(1024)S(1)} %convert_element_type.77, f32[48,4096]{1,0:T(8,128)S(1)} %all_gather.3, f32[48]{0:T(128)} %copy-done.17, s32[128]{0:T(128)} %bitcast.124), kind=kOutput, calls=%fused_computation.19 | convolution fusion | flops 305858432 | bytes 3966656 | tf_op jit(solution)/shard_map/dot_general | solution.py:209
  124.3 1.3 collective-permute-start.17
  125.6 1.5 collective-permute-start.18
  127.0 1.4 collective-permute-start.19
  128.5 1.8 %collective-permute-start.21 = (f32[4096]{0:T(1024)S(1)}, f32[4096]{0:T(1024)S(1)}, u32[]{:S(2)}, u32[]{:S(2)}) collective-permute-start(f32[4096]{0:T(1024)S(1)} %get-tuple-element.14), channel_id=1, source_target_pairs={{0,24},{4,28},{8,0},{12,4},{16,8},{20,12},{24,16},{28,20},{1,25},{... | collective-permute-start | bytes 49160 | tf_op jit(solution)/shard_map/ppermute | solution.py:96
  130.2 1.4 collective-permute-start.22
  131.7 1.6 %fusion.5 = bf16[128,4096]{1,0:T(8,128)(2,1)} fusion(bf16[128,4096]{1,0:T(8,128)(2,1)S(1)} %copy-done.1, f32[128,4096]{1,0:T(8,128)S(1)} %get-tuple-element.32, f32[128]{0:T(128)S(1)} %broadcast_multiply_fusion, f32[128]{0:T(128)S(1)} %copy-done.19, f32[4096]{0:T(1024)S(1)} %convert_element_type.77, f32[128]{0:T(128)S(1)} %copy-done.21), kind=kLoop, calls=%fused_computation.16 | loop fusion | flops 3670016 | bytes 4212224 | tf_op jit(solution)/shard_map/convert_element_type | solution.py:219
  134.0 1.0 stack.137
  136.5 2.2 %collective-permute-start.25 = (f32[4096]{0:T(1024)S(1)}, f32[4096]{0:T(1024)S(1)}, u32[]{:S(2)}, u32[]{:S(2)}) collective-permute-start(f32[4096]{0:T(1024)S(1)} %select_reduce_fusion.2), channel_id=1, source_target_pairs={{0,3},{1,0},{2,1},{3,2},{4,7},{5,4},{6,5},{7,6},{8,11},{9,8},{10,9... | collective-permute-start | bytes 49160 | tf_op jit(solution)/shard_map/ppermute | solution.py:96
  139.4 2.1 %fusion.17 = f32[512,256]{1,0:T(8,128)} fusion(bf16[384,512]{1,0:T(8,128)(2,1)S(1)} %bitcast.97, f32[384,1024]{1,0:T(8,128)} %copy-done.4, s32[]{:T(128)S(6)} %select_n.187), kind=kOutput, calls=%fused_computation.52 | convolution fusion | flops 100663296 | bytes 1114116 | tf_op jit(solution)/shard_map/dot_general | solution.py:204
  141.5 1.8 %collective-permute-done.24 = f32[4096]{0:T(1024)S(1)} collective-permute-done((f32[4096]{0:T(1024)S(1)}, f32[4096]{0:T(1024)S(1)}, u32[]{:S(2)}, u32[]{:S(2)}) %collective-permute-start.24) | collective-permute-done | bytes 16416 | tf_op jit(solution)/shard_map/ppermute | solution.py:96
  143.3 0.9 collective-permute-done.23
  (128 shorter events, 21.5 us)
Async XLA Ops:
  0.6 97.4 %copy-start = (bf16[1024,1024]{1,0:T(8,128)(2,1)S(1)}, bf16[1024,1024]{1,0:T(8,128)(2,1)}, u32[]{:S(2)}) copy-start(bf16[1024,1024]{1,0:T(8,128)(2,1)} %param.13) | copy-start | bytes 6291460
  3.7 11.7 %collective-permute-start.2 = (bf16[97,256]{1,0:T(8,128)(2,1)S(1)}, bf16[97,256]{1,0:T(8,128)(2,1)S(1)}, u32[]{:S(2)}, u32[]{:S(2)}) collective-permute-start(bf16[97,256]{1,0:T(8,128)(2,1)S(1)} %constant_dynamic-update-slice_fusion), channel_id=1, source_target_pairs={{0,3},{1,0},{2,1},{3,2},{4,7},{5,4},{6,5},{7,6},{8,11},{9,8},{10,9... | collective-permute-start | bytes 149000 | tf_op jit(solution)/shard_map/ppermute | solution.py:96
  8.8 6.6 %collective-permute-start.1 = (bf16[97,256]{1,0:T(8,128)(2,1)S(1)}, bf16[97,256]{1,0:T(8,128)(2,1)S(1)}, u32[]{:S(2)}, u32[]{:S(2)}) collective-permute-start(bf16[97,256]{1,0:T(8,128)(2,1)S(1)} %constant_dynamic-update-slice_fusion), channel_id=1, source_target_pairs={{0,2},{1,3},{2,0},{3,1},{4,6},{5,7},{6,4},{7,5},{8,10},{9,11},{10,... | collective-permute-start | bytes 149000 | tf_op jit(solution)/shard_map/ppermute | solution.py:96
  8.8 6.6 %collective-permute-start = (bf16[97,256]{1,0:T(8,128)(2,1)S(1)}, bf16[97,256]{1,0:T(8,128)(2,1)S(1)}, u32[]{:S(2)}, u32[]{:S(2)}) collective-permute-start(bf16[97,256]{1,0:T(8,128)(2,1)S(1)} %constant_dynamic-update-slice_fusion), channel_id=1, source_target_pairs={{0,1},{1,2},{2,3},{3,0},{4,5},{5,6},{6,7},{7,4},{8,9},{9,10},{10,1... | collective-permute-start | bytes 149000 | tf_op jit(solution)/shard_map/ppermute | solution.py:96
  9.8 81.7 %copy-start.13 = (pred[4]{0:T(512)(128)(4,1)}, pred[4]{0:T(512)(128)(4,1)S(1)}, u32[]{:S(2)}) copy-start(pred[4]{0:T(512)(128)(4,1)S(1)} %compare_and_fusion) | copy-start | bytes 16
  12.6 8.1 %copy-start.20 = (f32[128]{0:T(128)}, f32[128]{0:T(128)S(1)}, u32[]{:S(2)}) copy-start(f32[128]{0:T(128)S(1)} %get-tuple-element.27) | copy-start | bytes 1540
  12.7 78.3 %copy-start.15 = (s32[1024]{0:T(1024)}, s32[1024]{0:T(1024)S(1)}, u32[]{:S(2)}) copy-start(s32[1024]{0:T(1024)S(1)} %pad_clamp_fusion.1) | copy-start | bytes 12292
  12.7 26.8 %copy-start.16 = (s32[1024]{0:T(1024)}, s32[1024]{0:T(1024)S(1)}, u32[]{:S(2)}) copy-start(s32[1024]{0:T(1024)S(1)} %pad_clamp_fusion) | copy-start | bytes 12292
  15.3 27.5 %copy-start.18 = (pred[8]{0:T(512)(128)(4,1)}, pred[8]{0:T(512)(128)(4,1)S(1)}, u32[]{:S(2)}) copy-start(pred[8]{0:T(512)(128)(4,1)S(1)} %compare_and_fusion.1) | copy-start | bytes 28
  16.1 8.0 %collective-permute-start.3 = (bf16[4,97,256]{2,1,0:T(8,128)(2,1)S(1)}, bf16[4,97,256]{2,1,0:T(8,128)(2,1)S(1)}, u32[]{:S(2)}, u32[]{:S(2)}) collective-permute-start(bf16[4,97,256]{2,1,0:T(8,128)(2,1)S(1)} %broadcast_select_fusion.1), channel_id=1, source_target_pairs={{0,4},{4,8},{8,12},{12,16},{16,20},{20,24},{24,28},{28,0},{1,5},{5... | collective-permute-start | bytes 595976 | tf_op jit(solution)/shard_map/ppermute | solution.py:96
  16.2 10.1 %collective-permute-start.4 = (bf16[4,97,256]{2,1,0:T(8,128)(2,1)S(1)}, bf16[4,97,256]{2,1,0:T(8,128)(2,1)S(1)}, u32[]{:S(2)}, u32[]{:S(2)}) collective-permute-start(bf16[4,97,256]{2,1,0:T(8,128)(2,1)S(1)} %broadcast_select_fusion.1), channel_id=1, source_target_pairs={{0,8},{4,12},{8,16},{12,20},{16,24},{20,28},{24,0},{28,4},{1,9},{5... | collective-permute-start | bytes 595976 | tf_op jit(solution)/shard_map/ppermute | solution.py:96
  17.7 15.9 %collective-permute-start.5 = (bf16[4,97,256]{2,1,0:T(8,128)(2,1)S(1)}, bf16[4,97,256]{2,1,0:T(8,128)(2,1)S(1)}, u32[]{:S(2)}, u32[]{:S(2)}) collective-permute-start(bf16[4,97,256]{2,1,0:T(8,128)(2,1)S(1)} %broadcast_select_fusion.1), channel_id=1, source_target_pairs={{0,12},{4,16},{8,20},{12,24},{16,28},{20,0},{24,4},{28,8},{1,13},{... | collective-permute-start | bytes 595976 | tf_op jit(solution)/shard_map/ppermute | solution.py:96
  20.1 14.3 %collective-permute-start.6 = (bf16[4,97,256]{2,1,0:T(8,128)(2,1)S(1)}, bf16[4,97,256]{2,1,0:T(8,128)(2,1)S(1)}, u32[]{:S(2)}, u32[]{:S(2)}) collective-permute-start(bf16[4,97,256]{2,1,0:T(8,128)(2,1)S(1)} %broadcast_select_fusion.1), channel_id=1, source_target_pairs={{0,16},{4,20},{8,24},{12,28},{16,0},{20,4},{24,8},{28,12},{1,17},{... | collective-permute-start | bytes 595976 | tf_op jit(solution)/shard_map/ppermute | solution.py:96
  20.6 16.8 %collective-permute-start.7 = (bf16[4,97,256]{2,1,0:T(8,128)(2,1)S(1)}, bf16[4,97,256]{2,1,0:T(8,128)(2,1)S(1)}, u32[]{:S(2)}, u32[]{:S(2)}) collective-permute-start(bf16[4,97,256]{2,1,0:T(8,128)(2,1)S(1)} %broadcast_select_fusion.1), channel_id=1, source_target_pairs={{0,20},{4,24},{8,28},{12,0},{16,4},{20,8},{24,12},{28,16},{1,21},{... | collective-permute-start | bytes 595976 | tf_op jit(solution)/shard_map/ppermute | solution.py:96
  20.9 62.5 %copy-start.17 = (f32[48]{0:T(128)}, f32[48]{0:T(128)S(1)}, u32[]{:S(2)}) copy-start(f32[48]{0:T(128)S(1)} %convert_reduce_fusion) | copy-start | bytes 580
  24.1 13.9 %collective-permute-start.8 = (bf16[4,97,256]{2,1,0:T(8,128)(2,1)S(1)}, bf16[4,97,256]{2,1,0:T(8,128)(2,1)S(1)}, u32[]{:S(2)}, u32[]{:S(2)}) collective-permute-start(bf16[4,97,256]{2,1,0:T(8,128)(2,1)S(1)} %broadcast_select_fusion.1), channel_id=1, source_target_pairs={{0,24},{4,28},{8,0},{12,4},{16,8},{20,12},{24,16},{28,20},{1,25},{... | collective-permute-start | bytes 595976 | tf_op jit(solution)/shard_map/ppermute | solution.py:96
  26.3 12.5 %collective-permute-start.9 = (bf16[4,97,256]{2,1,0:T(8,128)(2,1)S(1)}, bf16[4,97,256]{2,1,0:T(8,128)(2,1)S(1)}, u32[]{:S(2)}, u32[]{:S(2)}) collective-permute-start(bf16[4,97,256]{2,1,0:T(8,128)(2,1)S(1)} %broadcast_select_fusion.1), channel_id=1, source_target_pairs={{0,28},{4,0},{8,4},{12,8},{16,12},{20,16},{24,20},{28,24},{1,29},{... | collective-permute-start | bytes 595976 | tf_op jit(solution)/shard_map/ppermute | solution.py:96
  46.7 2.8 %copy-start.2 = (bf16[48,8,4,256]{3,1,2,0:T(8,128)(2,1)}, bf16[48,8,4,256]{3,1,2,0:T(8,128)(2,1)S(1)}, u32[]{:S(2)}) copy-start(bf16[48,8,4,256]{3,1,2,0:T(8,128)(2,1)S(1)} %copy.35) | copy-start | bytes 2359300
  52.2 6.8 %copy-start.3 = (bf16[48,8,4,256]{3,1,2,0:T(8,128)(2,1)S(1)}, bf16[48,8,4,256]{3,1,2,0:T(8,128)(2,1)}, u32[]{:S(2)}) copy-start(bf16[48,8,4,256]{3,1,2,0:T(8,128)(2,1)} %copy-done.2) | copy-start | bytes 2359300
  52.9 8.1 %collective-permute-start.12 = (f32[48,1024]{1,0:T(8,128)}, f32[48,1024]{1,0:T(8,128)}, u32[]{:S(2)}, u32[]{:S(2)}) collective-permute-start(f32[48,1024]{1,0:T(8,128)} %bitcast.86), channel_id=1, source_target_pairs={{0,3},{1,0},{2,1},{3,2},{4,7},{5,4},{6,5},{7,6},{8,11},{9,8},{10,9... | collective-permute-start | bytes 589832 | tf_op jit(solution)/shard_map/ppermute | solution.py:113
  56.4 18.8 %collective-permute-start.11 = (f32[48,1024]{1,0:T(8,128)}, f32[48,1024]{1,0:T(8,128)}, u32[]{:S(2)}, u32[]{:S(2)}) collective-permute-start(f32[48,1024]{1,0:T(8,128)} %bitcast.87), channel_id=1, source_target_pairs={{0,2},{1,3},{2,0},{3,1},{4,6},{5,7},{6,4},{7,5},{8,10},{9,11},{10,... | collective-permute-start | bytes 589832 | tf_op jit(solution)/shard_map/ppermute | solution.py:113
  58.3 16.9 %collective-permute-start.10 = (f32[48,1024]{1,0:T(8,128)}, f32[48,1024]{1,0:T(8,128)}, u32[]{:S(2)}, u32[]{:S(2)}) collective-permute-start(f32[48,1024]{1,0:T(8,128)} %bitcast.88), channel_id=1, source_target_pairs={{0,1},{1,2},{2,3},{3,0},{4,5},{5,6},{6,7},{7,4},{8,9},{9,10},{10,1... | collective-permute-start | bytes 589832 | tf_op jit(solution)/shard_map/ppermute | solution.py:113
  59.6 15.6 %copy-start.4 = (f32[384,1024]{1,0:T(8,128)}, f32[384,1024]{1,0:T(8,128)S(1)}, u32[]{:S(2)}) copy-start(f32[384,1024]{1,0:T(8,128)S(1)} %convolution_multiply_fusion) | copy-start | bytes 4718596
  79.2 5.0 %collective-permute-start.15 = (bf16[48,1024]{1,0:T(8,128)(2,1)S(1)}, bf16[48,1024]{1,0:T(8,128)(2,1)S(1)}, u32[]{:S(2)}, u32[]{:S(2)}) collective-permute-start(bf16[48,1024]{1,0:T(8,128)(2,1)S(1)} %divide_convert_fusion), channel_id=1, source_target_pairs={{0,3},{1,0},{2,1},{3,2},{4,7},{5,4},{6,5},{7,6},{8,11},{9,8},{10,9... | collective-permute-start | bytes 294920 | tf_op jit(solution)/shard_map/ppermute | solution.py:96
  79.3 11.5 %collective-permute-start.14 = (bf16[48,1024]{1,0:T(8,128)(2,1)S(1)}, bf16[48,1024]{1,0:T(8,128)(2,1)S(1)}, u32[]{:S(2)}, u32[]{:S(2)}) collective-permute-start(bf16[48,1024]{1,0:T(8,128)(2,1)S(1)} %divide_convert_fusion), channel_id=1, source_target_pairs={{0,2},{1,3},{2,0},{3,1},{4,6},{5,7},{6,4},{7,5},{8,10},{9,11},{10,... | collective-permute-start | bytes 294920 | tf_op jit(solution)/shard_map/ppermute | solution.py:96
  81.5 9.3 %collective-permute-start.13 = (bf16[48,1024]{1,0:T(8,128)(2,1)S(1)}, bf16[48,1024]{1,0:T(8,128)(2,1)S(1)}, u32[]{:S(2)}, u32[]{:S(2)}) collective-permute-start(bf16[48,1024]{1,0:T(8,128)(2,1)S(1)} %divide_convert_fusion), channel_id=1, source_target_pairs={{0,1},{1,2},{2,3},{3,0},{4,5},{5,6},{6,7},{7,4},{8,9},{9,10},{10,1... | collective-permute-start | bytes 294920 | tf_op jit(solution)/shard_map/ppermute | solution.py:96
  92.9 11.7 %all-to-all-start = ((bf16[8,48,512]{2,1,0:T(8,128)(2,1)}), bf16[8,48,512]{2,1,0:T(8,128)(2,1)S(1)}, u32[]{:S(2)}, u32[]{:S(2)}) async-start(bf16[8,48,512]{2,1,0:T(8,128)(2,1)} %copy.27), calls=%async_computation | async-start | bytes 786432 | tf_op jit(solution)/shard_map/all_to_all | solution.py:163
  98.1 23.8 %copy-start.1 = (bf16[128,4096]{1,0:T(8,128)(2,1)S(1)}, bf16[128,4096]{1,0:T(8,128)(2,1)}, u32[]{:S(2)}) copy-start(bf16[128,4096]{1,0:T(8,128)(2,1)} %param.10) | copy-start | bytes 3145732
  121.9 9.8 %copy-start.19 = (f32[128]{0:T(128)S(1)}, f32[128]{0:T(128)}, u32[]{:S(2)}) copy-start(f32[128]{0:T(128)} %get-tuple-element.26) | copy-start | bytes 1540
  121.9 9.8 %copy-start.21 = (f32[128]{0:T(128)S(1)}, f32[128]{0:T(128)}, u32[]{:S(2)}) copy-start(f32[128]{0:T(128)} %copy-done.20) | copy-start | bytes 1540
  124.2 9.1 %copy-start.5 = (f32[4096]{0:T(1024)}, f32[4096]{0:T(1024)S(1)}, u32[]{:S(2)}) copy-start(f32[4096]{0:T(1024)S(1)} %get-tuple-element.14) | copy-start | bytes 49156
  124.2 4.2 %collective-permute-start.16 = (f32[4096]{0:T(1024)S(1)}, f32[4096]{0:T(1024)S(1)}, u32[]{:S(2)}, u32[]{:S(2)}) collective-permute-start(f32[4096]{0:T(1024)S(1)} %get-tuple-element.14), channel_id=1, source_target_pairs={{0,4},{4,8},{8,12},{12,16},{16,20},{20,24},{24,28},{28,0},{1,5},{5... | collective-permute-start | bytes 49160 | tf_op jit(solution)/shard_map/ppermute | solution.py:96
  124.3 5.9 %collective-permute-start.17 = (f32[4096]{0:T(1024)S(1)}, f32[4096]{0:T(1024)S(1)}, u32[]{:S(2)}, u32[]{:S(2)}) collective-permute-start(f32[4096]{0:T(1024)S(1)} %get-tuple-element.14), channel_id=1, source_target_pairs={{0,8},{4,12},{8,16},{12,20},{16,24},{20,28},{24,0},{28,4},{1,9},{5... | collective-permute-start | bytes 49160 | tf_op jit(solution)/shard_map/ppermute | solution.py:96
  125.6 7.7 %collective-permute-start.18 = (f32[4096]{0:T(1024)S(1)}, f32[4096]{0:T(1024)S(1)}, u32[]{:S(2)}, u32[]{:S(2)}) collective-permute-start(f32[4096]{0:T(1024)S(1)} %get-tuple-element.14), channel_id=1, source_target_pairs={{0,12},{4,16},{8,20},{12,24},{16,28},{20,0},{24,4},{28,8},{1,13},{... | collective-permute-start | bytes 49160 | tf_op jit(solution)/shard_map/ppermute | solution.py:96
  127.0 6.3 %collective-permute-start.19 = (f32[4096]{0:T(1024)S(1)}, f32[4096]{0:T(1024)S(1)}, u32[]{:S(2)}, u32[]{:S(2)}) collective-permute-start(f32[4096]{0:T(1024)S(1)} %get-tuple-element.14), channel_id=1, source_target_pairs={{0,16},{4,20},{8,24},{12,28},{16,0},{20,4},{24,8},{28,12},{1,17},{... | collective-permute-start | bytes 49160 | tf_op jit(solution)/shard_map/ppermute | solution.py:96
  128.4 4.9 %collective-permute-start.20 = (f32[4096]{0:T(1024)S(1)}, f32[4096]{0:T(1024)S(1)}, u32[]{:S(2)}, u32[]{:S(2)}) collective-permute-start(f32[4096]{0:T(1024)S(1)} %get-tuple-element.14), channel_id=1, source_target_pairs={{0,20},{4,24},{8,28},{12,0},{16,4},{20,8},{24,12},{28,16},{1,21},{... | collective-permute-start | bytes 49160 | tf_op jit(solution)/shard_map/ppermute | solution.py:96
  128.5 4.9 %copy-start.6 = (f32[4096]{0:T(1024)}, f32[4096]{0:T(1024)S(1)}, u32[]{:S(2)}) copy-start(f32[4096]{0:T(1024)S(1)} %collective-permute-done.16) | copy-start | bytes 49156
  128.5 4.9 %collective-permute-start.21 = (f32[4096]{0:T(1024)S(1)}, f32[4096]{0:T(1024)S(1)}, u32[]{:S(2)}, u32[]{:S(2)}) collective-permute-start(f32[4096]{0:T(1024)S(1)} %get-tuple-element.14), channel_id=1, source_target_pairs={{0,24},{4,28},{8,0},{12,4},{16,8},{20,12},{24,16},{28,20},{1,25},{... | collective-permute-start | bytes 49160 | tf_op jit(solution)/shard_map/ppermute | solution.py:96
  130.2 3.1 %copy-start.7 = (f32[4096]{0:T(1024)}, f32[4096]{0:T(1024)S(1)}, u32[]{:S(2)}) copy-start(f32[4096]{0:T(1024)S(1)} %collective-permute-done.17) | copy-start | bytes 49156
  130.2 3.2 %collective-permute-start.22 = (f32[4096]{0:T(1024)S(1)}, f32[4096]{0:T(1024)S(1)}, u32[]{:S(2)}, u32[]{:S(2)}) collective-permute-start(f32[4096]{0:T(1024)S(1)} %get-tuple-element.14), channel_id=1, source_target_pairs={{0,28},{4,0},{8,4},{12,8},{16,12},{20,16},{24,20},{28,24},{1,29},{... | collective-permute-start | bytes 49160 | tf_op jit(solution)/shard_map/ppermute | solution.py:96
  133.3 0.6 copy-start.8
  133.4 0.6 copy-start.9
  133.4 0.6 copy-start.10
  133.4 0.6 copy-start.11
  134.0 11.0 %copy-start.14 = (pred[4]{0:T(512)(128)(4,1)S(1)}, pred[4]{0:T(512)(128)(4,1)}, u32[]{:S(2)}) copy-start(pred[4]{0:T(512)(128)(4,1)} %copy-done.13) | copy-start | bytes 16
  136.5 5.0 %collective-permute-start.25 = (f32[4096]{0:T(1024)S(1)}, f32[4096]{0:T(1024)S(1)}, u32[]{:S(2)}, u32[]{:S(2)}) collective-permute-start(f32[4096]{0:T(1024)S(1)} %select_reduce_fusion.2), channel_id=1, source_target_pairs={{0,3},{1,0},{2,1},{3,2},{4,7},{5,4},{6,5},{7,6},{8,11},{9,8},{10,9... | collective-permute-start | bytes 49160 | tf_op jit(solution)/shard_map/ppermute | solution.py:96
  138.7 4.6 %collective-permute-start.24 = (f32[4096]{0:T(1024)S(1)}, f32[4096]{0:T(1024)S(1)}, u32[]{:S(2)}, u32[]{:S(2)}) collective-permute-start(f32[4096]{0:T(1024)S(1)} %select_reduce_fusion.2), channel_id=1, source_target_pairs={{0,2},{1,3},{2,0},{3,1},{4,6},{5,7},{6,4},{7,5},{8,10},{9,11},{10,... | collective-permute-start | bytes 49160 | tf_op jit(solution)/shard_map/ppermute | solution.py:96
  138.7 5.5 %collective-permute-start.23 = (f32[4096]{0:T(1024)S(1)}, f32[4096]{0:T(1024)S(1)}, u32[]{:S(2)}, u32[]{:S(2)}) collective-permute-start(f32[4096]{0:T(1024)S(1)} %select_reduce_fusion.2), channel_id=1, source_target_pairs={{0,1},{1,2},{2,3},{3,0},{4,5},{5,6},{6,7},{7,4},{8,9},{9,10},{10,1... | collective-permute-start | bytes 49160 | tf_op jit(solution)/shard_map/ppermute | solution.py:96
  (1 other events, 0.6 us)

commit v7 on v6

--- a/solution.py
+++ b/solution.py
@@ -200,7 +200,6 @@
     mean_part = lax.dot_general(
         grad_low, proj_weight, contract_last, preferred_element_type=jnp.float32
     )
-    mean_part, pooled_cols = lax.optimization_barrier((mean_part, pooled_cols))
     proj_grad = lax.dot_general(
         pooled_cols, grad_low_cols, contract_first, preferred_element_type=jnp.float32
     )

time: 148 us -> 143 us (0.966)
  waiting for transfers between devices: 36.9 us -> 25.7 us
  starting transfers between devices: 37.7 us -> 41.1 us
  blocking collectives: 17.2 us -> 19.1 us
  other arithmetic: 14 us -> 15.5 us
    ppermute x3, waiting for transfers between devices: 14.9 us -> 7.14 us  [scatter_sum(): lax.ppermute(piece, axis, [(i, (i + s) % n) for i in range(n)])]
    ppermute x23, waiting for transfers between devices: 17.8 us -> 11.8 us  [gather_blocks(): lax.ppermute(x, axis, [(i, (i + s) % n) for i in range(n)])]
    ppermute x23, starting transfers between devices: 30.3 us -> 34.7 us  [gather_blocks(): lax.ppermute(x, axis, [(i, (i + s) % n) for i in range(n)])]
    all_to_all x1, waiting for transfers between devices: 4.13 us -> 6.74 us  [local_small(): pieces = lax.all_to_all(pieces, 'dp', 0, 0, tiled=True)]
    all_gather x1, blocking collectives: 17.2 us -> 19.1 us  [local_small(): mean_grad = lax.all_gather(mean_part, 'fsdp', axis=1, tiled=True)]
    dot_general x1, matrix products: 2.44 us -> 0.75 us  [local_small(): lax.dot_general(grad_low, proj_weight, contract_last, preferred_element_t...]
    convert_element_type x1, other arithmetic: 1.63 us -> 3.28 us  [local_small(): (inv_rms * scaled - states * inv_rms ** 3 * inner).astype(jnp.bfloat16)]
    unnamed x60 -> x48, local copies, waits for them, and re-layouts: 9.89 us -> 9.95 us
  transfers between devices with their start and end apart: 27 -> 27, of which waited for: 10 -> 7; matrix products, arithmetic and copies ran while one was open for 15% -> 22% of each run, Pallas kernels for 0% -> 0%
where the time goes in v7:
time: 143 us; the launch traced here: 142 us
  starting transfers between devices  41.1 us (29%)
  waiting for transfers between devices  25.7 us (18%)
  local copies, waits for them, and re-layouts  25.6 us (18%)
  blocking collectives  19.1 us (13%)
  other arithmetic  15.5 us (11%)
  matrix products  12.3 us (9%)
  between operations  2.91 us (2%)
    ppermute x23, starting transfers between devices, gather_blocks(): lax.ppermute(x, axis, [(i, (i + s) % n) for i in range(n)])  34.7 us
    all_gather x1, blocking collectives, local_small(): mean_grad = lax.all_gather(mean_part, 'fsdp', axis=1, tiled=True)  19.1 us
    ppermute x23, waiting for transfers between devices, gather_blocks(): lax.ppermute(x, axis, [(i, (i + s) % n) for i in range(n)])  11.8 us
    unnamed x48, local copies, waits for them, and re-layouts  9.95 us
    ppermute x3, waiting for transfers between devices, scatter_sum(): lax.ppermute(piece, axis, [(i, (i + s) % n) for i in range(n)])  7.14 us
    all_to_all x1, waiting for transfers between devices, local_small(): pieces = lax.all_to_all(pieces, 'dp', 0, 0, tiled=True)  6.74 us
    gather x5, local copies, waits for them, and re-layouts, gather_blocks(): return jnp.take(stack, order, axis=0)  5.97 us
    all_to_all x1, starting transfers between devices, local_small(): pieces = lax.all_to_all(pieces, 'dp', 0, 0, tiled=True)  3.45 us
  transfers between devices with their start and end apart: 27, of which 7 were waited for; matrix products, arithmetic and copies ran while one was open for 22% of the time, Pallas kernels for 0%

profile of v7, /device:TPU:0, one launch (start us, length us, event | category | flops | bytes accessed | tf_op | source)
XLA Modules:
  0.0 142.2 jit_solution(7879704769377036548)
XLA Ops:
  0.6 0.9 constant_dynamic-update-slice_fusion.2
  2.2 0.7 constant_dynamic-update-slice_fusion.1
  2.9 0.7 fusion.30
  3.7 5.1 %collective-permute-start.2 = (bf16[97,256]{1,0:T(8,128)(2,1)S(1)}, bf16[97,256]{1,0:T(8,128)(2,1)S(1)}, u32[]{:S(2)}, u32[]{:S(2)}) collective-permute-start(bf16[97,256]{1,0:T(8,128)(2,1)S(1)} %constant_dynamic-update-slice_fusion), channel_id=1, source_target_pairs={{0,3},{1,0},{2,1},{3,2},{4,7},{5,4},{6,5},{7,6},{8,11},{9,8},{10,9... | collective-permute-start | bytes 149000 | tf_op jit(solution)/shard_map/ppermute | solution.py:96
  8.8 1.0 collective-permute-start
  10.5 1.5 %fusion = f32[128]{0:T(128)S(1)} fusion(bf16[128,4096]{1,0:T(8,128)(2,1)} %param.10), kind=kLoop, calls=%fused_computation.11 | loop fusion | flops 1572736 | bytes 1049088 | tf_op jit(solution)/shard_map/reduce_sum | solution.py:146
  12.7 2.6 %fusion.9 = f32[48,4096]{1,0:T(8,128)} fusion(bf16[128,4096]{1,0:T(8,128)(2,1)} %param.10, f32[4096]{0:T(1024)S(1)} %convert_element_type.77, f32[128]{0:T(128)S(1)} %get-tuple-element.23, s32[128]{0:T(128)} %bitcast.125), kind=kOutput, calls=%fused_computation.24 | convolution fusion | flops 52434944 | bytes 1852416 | tf_op jit(solution)/shard_map/dot_general | solution.py:150
  16.1 1.5 %collective-permute-start.4 = (bf16[4,97,256]{2,1,0:T(8,128)(2,1)S(1)}, bf16[4,97,256]{2,1,0:T(8,128)(2,1)S(1)}, u32[]{:S(2)}, u32[]{:S(2)}) collective-permute-start(bf16[4,97,256]{2,1,0:T(8,128)(2,1)S(1)} %broadcast_select_fusion.1), channel_id=1, source_target_pairs={{0,8},{4,12},{8,16},{12,20},{16,24},{20,28},{24,0},{28,4},{1,9},{5... | collective-permute-start | bytes 595976 | tf_op jit(solution)/shard_map/ppermute | solution.py:96
  17.7 2.4 %collective-permute-start.5 = (bf16[4,97,256]{2,1,0:T(8,128)(2,1)S(1)}, bf16[4,97,256]{2,1,0:T(8,128)(2,1)S(1)}, u32[]{:S(2)}, u32[]{:S(2)}) collective-permute-start(bf16[4,97,256]{2,1,0:T(8,128)(2,1)S(1)} %broadcast_select_fusion.1), channel_id=1, source_target_pairs={{0,12},{4,16},{8,20},{12,24},{16,28},{20,0},{24,4},{28,8},{1,13},{... | collective-permute-start | bytes 595976 | tf_op jit(solution)/shard_map/ppermute | solution.py:96
  20.9 0.8 fusion.16
  21.7 2.4 %collective-permute-done.3 = bf16[4,97,256]{2,1,0:T(8,128)(2,1)S(1)} collective-permute-done((bf16[4,97,256]{2,1,0:T(8,128)(2,1)S(1)}, bf16[4,97,256]{2,1,0:T(8,128)(2,1)S(1)}, u32[]{:S(2)}, u32[]{:S(2)}) %collective-permute-start.3) | collective-permute-done | bytes 198688 | tf_op jit(solution)/shard_map/ppermute | solution.py:96
  24.1 1.4 %collective-permute-start.8 = (bf16[4,97,256]{2,1,0:T(8,128)(2,1)S(1)}, bf16[4,97,256]{2,1,0:T(8,128)(2,1)S(1)}, u32[]{:S(2)}, u32[]{:S(2)}) collective-permute-start(bf16[4,97,256]{2,1,0:T(8,128)(2,1)S(1)} %broadcast_select_fusion.1), channel_id=1, source_target_pairs={{0,24},{4,28},{8,0},{12,4},{16,8},{20,12},{24,16},{28,20},{1,25},{... | collective-permute-start | bytes 595976 | tf_op jit(solution)/shard_map/ppermute | solution.py:96
  26.2 3.6 %collective-permute-start.9 = (bf16[4,97,256]{2,1,0:T(8,128)(2,1)S(1)}, bf16[4,97,256]{2,1,0:T(8,128)(2,1)S(1)}, u32[]{:S(2)}, u32[]{:S(2)}) collective-permute-start(bf16[4,97,256]{2,1,0:T(8,128)(2,1)S(1)} %broadcast_select_fusion.1), channel_id=1, source_target_pairs={{0,28},{4,0},{8,4},{12,8},{16,12},{20,16},{24,20},{28,24},{1,29},{... | collective-permute-start | bytes 595976 | tf_op jit(solution)/shard_map/ppermute | solution.py:96
  30.5 3.1 %collective-permute-done.5 = bf16[4,97,256]{2,1,0:T(8,128)(2,1)S(1)} collective-permute-done((bf16[4,97,256]{2,1,0:T(8,128)(2,1)S(1)}, bf16[4,97,256]{2,1,0:T(8,128)(2,1)S(1)}, u32[]{:S(2)}, u32[]{:S(2)}) %collective-permute-start.5) | collective-permute-done | bytes 198688 | tf_op jit(solution)/shard_map/ppermute | solution.py:96
  35.0 2.3 %collective-permute-done.7 = bf16[4,97,256]{2,1,0:T(8,128)(2,1)S(1)} collective-permute-done((bf16[4,97,256]{2,1,0:T(8,128)(2,1)S(1)}, bf16[4,97,256]{2,1,0:T(8,128)(2,1)S(1)}, u32[]{:S(2)}, u32[]{:S(2)}) %collective-permute-start.7) | collective-permute-done | bytes 198688 | tf_op jit(solution)/shard_map/ppermute | solution.py:96
  39.4 3.3 %gather_fusion.1 = bf16[8,4,97,256]{3,2,1,0:T(8,128)(2,1)} fusion(bf16[8,4,97,256]{3,2,1,0:T(8,128)(2,1)} %bitcast_dynamic-update-slice_fusion, s32[1024]{0:T(1024)S(1)} %pad_clamp_fusion), kind=kCustom, calls=%fused_computation.1 | custom fusion | bytes 3178528 | tf_op jit(solution)/shard_map/jit(_take)/gather | solution.py:100
  42.7 1.7 %broadcast_select_fusion = bf16[8,4,97,256]{3,2,1,0:T(8,128)(2,1)S(1)} fusion(bf16[8,4,97,256]{3,2,1,0:T(8,128)(2,1)} %gather_fusion.1, pred[8]{0:T(512)(128)(4,1)S(1)} %compare_and_fusion.1), kind=kLoop, calls=%fused_computation.20 | loop fusion | flops 794624 | bytes 3178504 | tf_op jit(solution)/shard_map/jit(_take)/select_n | solution.py:100
  45.0 1.0 copy.34
  46.8 1.7 %fusion.37 = (f32[384]{0:T(512)S(1)}, f32[384,384]{0,1:T(8,128)S(1)}) fusion(bf16[384,1024]{1,0:T(8,128)(2,1)} %bitcast.98, bf16[384,1024]{1,0:T(8,128)(2,1)S(1)} %bitcast.94), kind=kOutput, calls=%fused_computation.129 | convolution fusion | flops 302284416 | bytes 2164224 | tf_op jit(solution)/shard_map/dot_general | solution.py:176
  50.1 0.7 fusion.20
  50.9 19.1 %all_gather.3 = f32[48,4096]{1,0:T(8,128)S(1)} all-gather(f32[48,1024]{1,0:T(8,128)S(1)} %fusion.20), channel_id=1, replica_groups=mesh['dp'=8,'fsdp'=4] {'fsdp'}, dimensions={1}, use_global_device_ids=true | all-gather | bytes 983040 | tf_op jit(solution)/shard_map/all_gather | solution.py:206
  70.0 2.8 %fusion.8 = (f32[4096]{0:T(1024)S(1)}, f32[128]{0:T(128)S(1)}, f32[128,4096]{1,0:T(8,128)}) fusion(bf16[128,4096]{1,0:T(8,128)(2,1)S(1)} %copy-done.1, f32[128]{0:T(128)S(1)} %get-tuple-element.23, f32[4096]{0:T(1024)S(1)} %convert_element_type.77, f32[48,4096]{1,0:T(8,128)S(1)} %all_gather.3, f32[48]{0:T(128)S(1)} %convert_reduce_fusion, s32[128]{0:T(128)S(1)} %bitcast.126), kind=kOutput, calls=%fused_computation.19 | convolution fusion | flops 305858432 | bytes 3966656 | tf_op jit(solution)/shard_map/dot_general | solution.py:208
  72.9 1.7 %collective-permute-start.11 = (f32[4096]{0:T(1024)S(1)}, f32[4096]{0:T(1024)S(1)}, u32[]{:S(2)}, u32[]{:S(2)}) collective-permute-start(f32[4096]{0:T(1024)S(1)} %get-tuple-element.10), channel_id=1, source_target_pairs={{0,8},{4,12},{8,16},{12,20},{16,24},{20,28},{24,0},{28,4},{1,9},{5... | collective-permute-start | bytes 49160 | tf_op jit(solution)/shard_map/ppermute | solution.py:96
  74.7 1.8 %collective-permute-start.12 = (f32[4096]{0:T(1024)S(1)}, f32[4096]{0:T(1024)S(1)}, u32[]{:S(2)}, u32[]{:S(2)}) collective-permute-start(f32[4096]{0:T(1024)S(1)} %get-tuple-element.10), channel_id=1, source_target_pairs={{0,12},{4,16},{8,20},{12,24},{16,28},{20,0},{24,4},{28,8},{1,13},{... | collective-permute-start | bytes 49160 | tf_op jit(solution)/shard_map/ppermute | solution.py:96
  76.4 1.1 collective-permute-start.13
  78.1 2.6 %reshape.233 = f32[48,4,1024]{2,1,0:T(4,128)} reshape(f32[48,4096]{1,0:T(8,128)} %fusion.9) | data formatting | bytes 1572864 | tf_op jit(solution)/shard_map/reshape | solution.py:156
  80.6 3.3 %fusion.5 = bf16[128,4096]{1,0:T(8,128)(2,1)} fusion(bf16[128,4096]{1,0:T(8,128)(2,1)S(1)} %copy-done.1, f32[128,4096]{1,0:T(8,128)} %get-tuple-element.28, f32[128]{0:T(128)} %broadcast_multiply_fusion, f32[128]{0:T(128)} %get-tuple-element.22, f32[4096]{0:T(1024)S(1)} %convert_element_type.77, f32[128]{0:T(128)} %copy-done.14), kind=kLoop, calls=%fused_computation.16 | loop fusion | flops 3670016 | bytes 4212224 | tf_op jit(solution)/shard_map/convert_element_type | solution.py:218
  83.9 0.8 constant_dynamic-slice_fusion.3
  86.9 1.2 collective-permute-start.15
  88.1 1.5 %collective-permute-start.16 = (f32[4096]{0:T(1024)S(1)}, f32[4096]{0:T(1024)S(1)}, u32[]{:S(2)}, u32[]{:S(2)}) collective-permute-start(f32[4096]{0:T(1024)S(1)} %get-tuple-element.10), channel_id=1, source_target_pairs={{0,28},{4,0},{8,4},{12,8},{16,12},{20,16},{24,20},{28,24},{1,29},{... | collective-permute-start | bytes 49160 | tf_op jit(solution)/shard_map/ppermute | solution.py:96
  89.6 2.3 %collective-permute-start.22 = (f32[48,1024]{1,0:T(8,128)}, f32[48,1024]{1,0:T(8,128)S(1)}, u32[]{:S(2)}, u32[]{:S(2)}) collective-permute-start(f32[48,1024]{1,0:T(8,128)} %bitcast.86), channel_id=1, source_target_pairs={{0,3},{1,0},{2,1},{3,2},{4,7},{5,4},{6,5},{7,6},{8,11},{9,8},{10,9... | collective-permute-start | bytes 589832 | tf_op jit(solution)/shard_map/ppermute | solution.py:113
  92.5 1.7 %convolution_multiply_fusion.2 = f32[48,256]{1,0:T(8,128)} fusion(bf16[384,1024]{1,0:T(8,128)(2,1)} %bitcast.99, s32[]{:T(128)S(6)} %select_n.187, bf16[384,384]{0,1:T(8,128)(2,1)S(1)} %subtract_convert_fusion, s32[]{:T(128)S(6)} %select_n.186), kind=kOutput, calls=%fused_computation.23 | convolution fusion | flops 9449472 | bytes 282632 | tf_op jit(solution)/shard_map/dot_general | solution.py:196
  94.2 1.4 dynamic_slice.22
  97.4 3.3 %collective-permute-start.19 = (f32[4096]{0:T(1024)S(1)}, f32[4096]{0:T(1024)S(1)}, u32[]{:S(2)}, u32[]{:S(2)}) collective-permute-start(f32[4096]{0:T(1024)S(1)} %select_reduce_fusion.2), channel_id=1, source_target_pairs={{0,3},{1,0},{2,1},{3,2},{4,7},{5,4},{6,5},{7,6},{8,11},{9,8},{10,9... | collective-permute-start | bytes 49160 | tf_op jit(solution)/shard_map/ppermute | solution.py:96
  100.7 1.1 collective-permute-start.18
  101.8 7.1 %collective-permute-done.21 = f32[48,1024]{1,0:T(8,128)S(1)} collective-permute-done((f32[48,1024]{1,0:T(8,128)}, f32[48,1024]{1,0:T(8,128)S(1)}, u32[]{:S(2)}, u32[]{:S(2)}) %collective-permute-start.21) | collective-permute-done | bytes 196640 | tf_op jit(solution)/shard_map/ppermute | solution.py:113
  109.6 1.2 pad_maximum_fusion
  110.8 1.6 %gather_fusion.4 = f32[4,48,1024]{2,1,0:T(8,128)} fusion(f32[4,48,1024]{2,1,0:T(8,128)S(1)} %pad_maximum_fusion, s32[1024]{0:T(1024)} %copy-done.8), kind=kCustom, calls=%fused_computation.4 | custom fusion | bytes 1572880 | tf_op jit(solution)/shard_map/jit(_take)/gather | solution.py:115
  112.4 1.3 select_reduce_fusion
  114.1 2.4 %collective-permute-start.24 = (bf16[48,1024]{1,0:T(8,128)(2,1)S(1)}, bf16[48,1024]{1,0:T(8,128)(2,1)S(1)}, u32[]{:S(2)}, u32[]{:S(2)}) collective-permute-start(bf16[48,1024]{1,0:T(8,128)(2,1)S(1)} %divide_convert_fusion), channel_id=1, source_target_pairs={{0,2},{1,3},{2,0},{3,1},{4,6},{5,7},{6,4},{7,5},{8,10},{9,11},{10,... | collective-permute-start | bytes 294920 | tf_op jit(solution)/shard_map/ppermute | solution.py:96
  116.5 1.9 %collective-permute-start.23 = (bf16[48,1024]{1,0:T(8,128)(2,1)S(1)}, bf16[48,1024]{1,0:T(8,128)(2,1)S(1)}, u32[]{:S(2)}, u32[]{:S(2)}) collective-permute-start(bf16[48,1024]{1,0:T(8,128)(2,1)S(1)} %divide_convert_fusion), channel_id=1, source_target_pairs={{0,1},{1,2},{2,3},{3,0},{4,5},{5,6},{6,7},{7,4},{8,9},{9,10},{10,1... | collective-permute-start | bytes 294920 | tf_op jit(solution)/shard_map/ppermute | solution.py:96
  118.6 0.8 collective-permute-done.25
  119.4 2.5 %collective-permute-start.17 = (f32[4096]{0:T(1024)S(1)}, f32[4096]{0:T(1024)S(1)}, u32[]{:S(2)}, u32[]{:S(2)}) collective-permute-start(f32[4096]{0:T(1024)S(1)} %select_reduce_fusion.2), channel_id=1, source_target_pairs={{0,1},{1,2},{2,3},{3,0},{4,5},{5,6},{6,7},{7,4},{8,9},{9,10},{10,1... | collective-permute-start | bytes 49160 | tf_op jit(solution)/shard_map/ppermute | solution.py:96
  121.9 3.2 %collective-permute-done.24 = bf16[48,1024]{1,0:T(8,128)(2,1)S(1)} collective-permute-done((bf16[48,1024]{1,0:T(8,128)(2,1)S(1)}, bf16[48,1024]{1,0:T(8,128)(2,1)S(1)}, u32[]{:S(2)}, u32[]{:S(2)}) %collective-permute-start.24) | collective-permute-done | bytes 98336 | tf_op jit(solution)/shard_map/ppermute | solution.py:96
  126.4 0.9 copy.27
  127.2 3.5 %all-to-all-start = ((bf16[8,48,512]{2,1,0:T(8,128)(2,1)}), bf16[8,48,512]{2,1,0:T(8,128)(2,1)S(1)}, u32[]{:S(2)}, u32[]{:S(2)}) async-start(bf16[8,48,512]{2,1,0:T(8,128)(2,1)} %copy.27), calls=%async_computation | async-start | bytes 786432 | tf_op jit(solution)/shard_map/all_to_all | solution.py:163
  132.2 6.7 %all-to-all-done = bf16[8,48,512]{2,1,0:T(8,128)(2,1)S(1)} async-done(((bf16[8,48,512]{2,1,0:T(8,128)(2,1)}), bf16[8,48,512]{2,1,0:T(8,128)(2,1)S(1)}, u32[]{:S(2)}, u32[]{:S(2)}) %all-to-all-start) | async-done | bytes 393248 | tf_op jit(solution)/shard_map/all_to_all | solution.py:163
  139.0 2.1 %fusion.17 = f32[512,256]{1,0:T(8,128)} fusion(bf16[384,512]{1,0:T(8,128)(2,1)S(1)} %bitcast.97, f32[384,1024]{1,0:T(8,128)} %copy-done.3, s32[]{:T(128)S(6)} %select_n.187), kind=kOutput, calls=%fused_computation.52 | convolution fusion | flops 100663296 | bytes 1114116 | tf_op jit(solution)/shard_map/dot_general | solution.py:203
  (116 shorter events, 19.8 us)
Async XLA Ops:
  0.6 49.5 %copy-start = (bf16[1024,1024]{1,0:T(8,128)(2,1)S(1)}, bf16[1024,1024]{1,0:T(8,128)(2,1)}, u32[]{:S(2)}) copy-start(bf16[1024,1024]{1,0:T(8,128)(2,1)} %param.13) | copy-start | bytes 6291460
  3.7 11.6 %collective-permute-start.2 = (bf16[97,256]{1,0:T(8,128)(2,1)S(1)}, bf16[97,256]{1,0:T(8,128)(2,1)S(1)}, u32[]{:S(2)}, u32[]{:S(2)}) collective-permute-start(bf16[97,256]{1,0:T(8,128)(2,1)S(1)} %constant_dynamic-update-slice_fusion), channel_id=1, source_target_pairs={{0,3},{1,0},{2,1},{3,2},{4,7},{5,4},{6,5},{7,6},{8,11},{9,8},{10,9... | collective-permute-start | bytes 149000 | tf_op jit(solution)/shard_map/ppermute | solution.py:96
  8.8 6.6 %collective-permute-start.1 = (bf16[97,256]{1,0:T(8,128)(2,1)S(1)}, bf16[97,256]{1,0:T(8,128)(2,1)S(1)}, u32[]{:S(2)}, u32[]{:S(2)}) collective-permute-start(bf16[97,256]{1,0:T(8,128)(2,1)S(1)} %constant_dynamic-update-slice_fusion), channel_id=1, source_target_pairs={{0,2},{1,3},{2,0},{3,1},{4,6},{5,7},{6,4},{7,5},{8,10},{9,11},{10,... | collective-permute-start | bytes 149000 | tf_op jit(solution)/shard_map/ppermute | solution.py:96
  8.8 6.6 %collective-permute-start = (bf16[97,256]{1,0:T(8,128)(2,1)S(1)}, bf16[97,256]{1,0:T(8,128)(2,1)S(1)}, u32[]{:S(2)}, u32[]{:S(2)}) collective-permute-start(bf16[97,256]{1,0:T(8,128)(2,1)S(1)} %constant_dynamic-update-slice_fusion), channel_id=1, source_target_pairs={{0,1},{1,2},{2,3},{3,0},{4,5},{5,6},{6,7},{7,4},{8,9},{9,10},{10,1... | collective-permute-start | bytes 149000 | tf_op jit(solution)/shard_map/ppermute | solution.py:96
  9.8 11.0 %copy-start.6 = (pred[4]{0:T(512)(128)(4,1)}, pred[4]{0:T(512)(128)(4,1)S(1)}, u32[]{:S(2)}) copy-start(pred[4]{0:T(512)(128)(4,1)S(1)} %compare_and_fusion) | copy-start | bytes 16
  12.6 57.4 %copy-start.14 = (f32[128]{0:T(128)}, f32[128]{0:T(128)S(1)}, u32[]{:S(2)}) copy-start(f32[128]{0:T(128)S(1)} %get-tuple-element.23) | copy-start | bytes 1540
  12.6 8.1 %copy-start.8 = (s32[1024]{0:T(1024)}, s32[1024]{0:T(1024)S(1)}, u32[]{:S(2)}) copy-start(s32[1024]{0:T(1024)S(1)} %pad_clamp_fusion.1) | copy-start | bytes 12292
  12.6 26.8 %copy-start.9 = (s32[1024]{0:T(1024)}, s32[1024]{0:T(1024)S(1)}, u32[]{:S(2)}) copy-start(s32[1024]{0:T(1024)S(1)} %pad_clamp_fusion) | copy-start | bytes 12292
  15.3 27.4 %copy-start.12 = (pred[8]{0:T(512)(128)(4,1)}, pred[8]{0:T(512)(128)(4,1)S(1)}, u32[]{:S(2)}) copy-start(pred[8]{0:T(512)(128)(4,1)S(1)} %compare_and_fusion.1) | copy-start | bytes 28
  16.1 8.0 %collective-permute-start.3 = (bf16[4,97,256]{2,1,0:T(8,128)(2,1)S(1)}, bf16[4,97,256]{2,1,0:T(8,128)(2,1)S(1)}, u32[]{:S(2)}, u32[]{:S(2)}) collective-permute-start(bf16[4,97,256]{2,1,0:T(8,128)(2,1)S(1)} %broadcast_select_fusion.1), channel_id=1, source_target_pairs={{0,4},{4,8},{8,12},{12,16},{16,20},{20,24},{24,28},{28,0},{1,5},{5... | collective-permute-start | bytes 595976 | tf_op jit(solution)/shard_map/ppermute | solution.py:96
  16.1 10.1 %collective-permute-start.4 = (bf16[4,97,256]{2,1,0:T(8,128)(2,1)S(1)}, bf16[4,97,256]{2,1,0:T(8,128)(2,1)S(1)}, u32[]{:S(2)}, u32[]{:S(2)}) collective-permute-start(bf16[4,97,256]{2,1,0:T(8,128)(2,1)S(1)} %broadcast_select_fusion.1), channel_id=1, source_target_pairs={{0,8},{4,12},{8,16},{12,20},{16,24},{20,28},{24,0},{28,4},{1,9},{5... | collective-permute-start | bytes 595976 | tf_op jit(solution)/shard_map/ppermute | solution.py:96
  17.7 15.9 %collective-permute-start.5 = (bf16[4,97,256]{2,1,0:T(8,128)(2,1)S(1)}, bf16[4,97,256]{2,1,0:T(8,128)(2,1)S(1)}, u32[]{:S(2)}, u32[]{:S(2)}) collective-permute-start(bf16[4,97,256]{2,1,0:T(8,128)(2,1)S(1)} %broadcast_select_fusion.1), channel_id=1, source_target_pairs={{0,12},{4,16},{8,20},{12,24},{16,28},{20,0},{24,4},{28,8},{1,13},{... | collective-permute-start | bytes 595976 | tf_op jit(solution)/shard_map/ppermute | solution.py:96
  20.0 14.3 %collective-permute-start.6 = (bf16[4,97,256]{2,1,0:T(8,128)(2,1)S(1)}, bf16[4,97,256]{2,1,0:T(8,128)(2,1)S(1)}, u32[]{:S(2)}, u32[]{:S(2)}) collective-permute-start(bf16[4,97,256]{2,1,0:T(8,128)(2,1)S(1)} %broadcast_select_fusion.1), channel_id=1, source_target_pairs={{0,16},{4,20},{8,24},{12,28},{16,0},{20,4},{24,8},{28,12},{1,17},{... | collective-permute-start | bytes 595976 | tf_op jit(solution)/shard_map/ppermute | solution.py:96
  20.5 16.8 %collective-permute-start.7 = (bf16[4,97,256]{2,1,0:T(8,128)(2,1)S(1)}, bf16[4,97,256]{2,1,0:T(8,128)(2,1)S(1)}, u32[]{:S(2)}, u32[]{:S(2)}) collective-permute-start(bf16[4,97,256]{2,1,0:T(8,128)(2,1)S(1)} %broadcast_select_fusion.1), channel_id=1, source_target_pairs={{0,20},{4,24},{8,28},{12,0},{16,4},{20,8},{24,12},{28,16},{1,21},{... | collective-permute-start | bytes 595976 | tf_op jit(solution)/shard_map/ppermute | solution.py:96
  20.9 49.1 %copy-start.10 = (f32[48]{0:T(128)}, f32[48]{0:T(128)S(1)}, u32[]{:S(2)}) copy-start(f32[48]{0:T(128)S(1)} %convert_reduce_fusion) | copy-start | bytes 580
  24.1 13.9 %collective-permute-start.8 = (bf16[4,97,256]{2,1,0:T(8,128)(2,1)S(1)}, bf16[4,97,256]{2,1,0:T(8,128)(2,1)S(1)}, u32[]{:S(2)}, u32[]{:S(2)}) collective-permute-start(bf16[4,97,256]{2,1,0:T(8,128)(2,1)S(1)} %broadcast_select_fusion.1), channel_id=1, source_target_pairs={{0,24},{4,28},{8,0},{12,4},{16,8},{20,12},{24,16},{28,20},{1,25},{... | collective-permute-start | bytes 595976 | tf_op jit(solution)/shard_map/ppermute | solution.py:96
  26.2 12.5 %collective-permute-start.9 = (bf16[4,97,256]{2,1,0:T(8,128)(2,1)S(1)}, bf16[4,97,256]{2,1,0:T(8,128)(2,1)S(1)}, u32[]{:S(2)}, u32[]{:S(2)}) collective-permute-start(bf16[4,97,256]{2,1,0:T(8,128)(2,1)S(1)} %broadcast_select_fusion.1), channel_id=1, source_target_pairs={{0,28},{4,0},{8,4},{12,8},{16,12},{20,16},{24,20},{28,24},{1,29},{... | collective-permute-start | bytes 595976 | tf_op jit(solution)/shard_map/ppermute | solution.py:96
  50.1 22.7 %copy-start.3 = (f32[384,1024]{1,0:T(8,128)}, f32[384,1024]{1,0:T(8,128)S(1)}, u32[]{:S(2)}) copy-start(f32[384,1024]{1,0:T(8,128)S(1)} %convolution_multiply_fusion) | copy-start | bytes 4718596
  50.1 19.9 %copy-start.1 = (bf16[128,4096]{1,0:T(8,128)(2,1)S(1)}, bf16[128,4096]{1,0:T(8,128)(2,1)}, u32[]{:S(2)}) copy-start(bf16[128,4096]{1,0:T(8,128)(2,1)} %param.10) | copy-start | bytes 3145732
  50.1 19.9 %copy-start.15 = (s32[1,128]{1,0:T(1,128)S(1)}, s32[1,128]{1,0:T(1,128)}, u32[]{:S(2)}) copy-start(s32[1,128]{1,0:T(1,128)} %param.11) | copy-start | bytes 1540
  72.8 14.1 %collective-permute-start.10 = (f32[4096]{0:T(1024)S(1)}, f32[4096]{0:T(1024)S(1)}, u32[]{:S(2)}, u32[]{:S(2)}) collective-permute-start(f32[4096]{0:T(1024)S(1)} %get-tuple-element.10), channel_id=1, source_target_pairs={{0,4},{4,8},{8,12},{12,16},{16,20},{20,24},{24,28},{28,0},{1,5},{5... | collective-permute-start | bytes 49160 | tf_op jit(solution)/shard_map/ppermute | solution.py:96
  72.9 15.1 %collective-permute-start.11 = (f32[4096]{0:T(1024)S(1)}, f32[4096]{0:T(1024)S(1)}, u32[]{:S(2)}, u32[]{:S(2)}) collective-permute-start(f32[4096]{0:T(1024)S(1)} %get-tuple-element.10), channel_id=1, source_target_pairs={{0,8},{4,12},{8,16},{12,20},{16,24},{20,28},{24,0},{28,4},{1,9},{5... | collective-permute-start | bytes 49160 | tf_op jit(solution)/shard_map/ppermute | solution.py:96
  74.7 14.9 %collective-permute-start.12 = (f32[4096]{0:T(1024)S(1)}, f32[4096]{0:T(1024)S(1)}, u32[]{:S(2)}, u32[]{:S(2)}) collective-permute-start(f32[4096]{0:T(1024)S(1)} %get-tuple-element.10), channel_id=1, source_target_pairs={{0,12},{4,16},{8,20},{12,24},{16,28},{20,0},{24,4},{28,8},{1,13},{... | collective-permute-start | bytes 49160 | tf_op jit(solution)/shard_map/ppermute | solution.py:96
  76.4 15.5 %collective-permute-start.13 = (f32[4096]{0:T(1024)S(1)}, f32[4096]{0:T(1024)S(1)}, u32[]{:S(2)}, u32[]{:S(2)}) collective-permute-start(f32[4096]{0:T(1024)S(1)} %get-tuple-element.10), channel_id=1, source_target_pairs={{0,16},{4,20},{8,24},{12,28},{16,0},{20,4},{24,8},{28,12},{1,17},{... | collective-permute-start | bytes 49160 | tf_op jit(solution)/shard_map/ppermute | solution.py:96
  77.6 14.3 %collective-permute-start.14 = (f32[4096]{0:T(1024)S(1)}, f32[4096]{0:T(1024)S(1)}, u32[]{:S(2)}, u32[]{:S(2)}) collective-permute-start(f32[4096]{0:T(1024)S(1)} %get-tuple-element.10), channel_id=1, source_target_pairs={{0,20},{4,24},{8,28},{12,0},{16,4},{20,8},{24,12},{28,16},{1,21},{... | collective-permute-start | bytes 49160 | tf_op jit(solution)/shard_map/ppermute | solution.py:96
  80.6 3.3 %copy-start.2 = (f32[48,4,1024]{2,1,0:T(4,128)S(1)}, f32[48,4,1024]{2,1,0:T(4,128)}, u32[]{:S(2)}) copy-start(f32[48,4,1024]{2,1,0:T(4,128)} %reshape.233) | copy-start | bytes 2359300
  84.7 12.5 %copy-start.13 = (pred[8]{0:T(512)(128)(4,1)S(1)}, pred[8]{0:T(512)(128)(4,1)}, u32[]{:S(2)}) copy-start(pred[8]{0:T(512)(128)(4,1)} %copy-done.12) | copy-start | bytes 28
  86.9 9.4 %collective-permute-start.15 = (f32[4096]{0:T(1024)S(1)}, f32[4096]{0:T(1024)S(1)}, u32[]{:S(2)}, u32[]{:S(2)}) collective-permute-start(f32[4096]{0:T(1024)S(1)} %get-tuple-element.10), channel_id=1, source_target_pairs={{0,24},{4,28},{8,0},{12,4},{16,8},{20,12},{24,16},{28,20},{1,25},{... | collective-permute-start | bytes 49160 | tf_op jit(solution)/shard_map/ppermute | solution.py:96
  88.1 8.3 %collective-permute-start.16 = (f32[4096]{0:T(1024)S(1)}, f32[4096]{0:T(1024)S(1)}, u32[]{:S(2)}, u32[]{:S(2)}) collective-permute-start(f32[4096]{0:T(1024)S(1)} %get-tuple-element.10), channel_id=1, source_target_pairs={{0,28},{4,0},{8,4},{12,8},{16,12},{20,16},{24,20},{28,24},{1,29},{... | collective-permute-start | bytes 49160 | tf_op jit(solution)/shard_map/ppermute | solution.py:96
  89.6 12.2 %collective-permute-start.22 = (f32[48,1024]{1,0:T(8,128)}, f32[48,1024]{1,0:T(8,128)S(1)}, u32[]{:S(2)}, u32[]{:S(2)}) collective-permute-start(f32[48,1024]{1,0:T(8,128)} %bitcast.86), channel_id=1, source_target_pairs={{0,3},{1,0},{2,1},{3,2},{4,7},{5,4},{6,5},{7,6},{8,11},{9,8},{10,9... | collective-permute-start | bytes 589832 | tf_op jit(solution)/shard_map/ppermute | solution.py:113
  91.9 17.0 %collective-permute-start.21 = (f32[48,1024]{1,0:T(8,128)}, f32[48,1024]{1,0:T(8,128)S(1)}, u32[]{:S(2)}, u32[]{:S(2)}) collective-permute-start(f32[48,1024]{1,0:T(8,128)} %bitcast.87), channel_id=1, source_target_pairs={{0,2},{1,3},{2,0},{3,1},{4,6},{5,7},{6,4},{7,5},{8,10},{9,11},{10,... | collective-permute-start | bytes 589832 | tf_op jit(solution)/shard_map/ppermute | solution.py:113
  91.9 17.0 %collective-permute-start.20 = (f32[48,1024]{1,0:T(8,128)}, f32[48,1024]{1,0:T(8,128)}, u32[]{:S(2)}, u32[]{:S(2)}) collective-permute-start(f32[48,1024]{1,0:T(8,128)} %bitcast.88), channel_id=1, source_target_pairs={{0,1},{1,2},{2,3},{3,0},{4,5},{5,6},{6,7},{7,4},{8,9},{9,10},{10,1... | collective-permute-start | bytes 589832 | tf_op jit(solution)/shard_map/ppermute | solution.py:113
  97.3 15.1 %copy-start.7 = (pred[4]{0:T(512)(128)(4,1)S(1)}, pred[4]{0:T(512)(128)(4,1)}, u32[]{:S(2)}) copy-start(pred[4]{0:T(512)(128)(4,1)} %copy-done.6) | copy-start | bytes 16
  97.4 33.3 %collective-permute-start.19 = (f32[4096]{0:T(1024)S(1)}, f32[4096]{0:T(1024)S(1)}, u32[]{:S(2)}, u32[]{:S(2)}) collective-permute-start(f32[4096]{0:T(1024)S(1)} %select_reduce_fusion.2), channel_id=1, source_target_pairs={{0,3},{1,0},{2,1},{3,2},{4,7},{5,4},{6,5},{7,6},{8,11},{9,8},{10,9... | collective-permute-start | bytes 49160 | tf_op jit(solution)/shard_map/ppermute | solution.py:96
  100.7 30.0 %collective-permute-start.18 = (f32[4096]{0:T(1024)S(1)}, f32[4096]{0:T(1024)S(1)}, u32[]{:S(2)}, u32[]{:S(2)}) collective-permute-start(f32[4096]{0:T(1024)S(1)} %select_reduce_fusion.2), channel_id=1, source_target_pairs={{0,2},{1,3},{2,0},{3,1},{4,6},{5,7},{6,4},{7,5},{8,10},{9,11},{10,... | collective-permute-start | bytes 49160 | tf_op jit(solution)/shard_map/ppermute | solution.py:96
  101.8 7.1 %copy-start.4 = (f32[48,1024]{1,0:T(8,128)}, f32[48,1024]{1,0:T(8,128)S(1)}, u32[]{:S(2)}) copy-start(f32[48,1024]{1,0:T(8,128)S(1)} %collective-permute-done.22) | copy-start | bytes 589828
  108.9 0.7 copy-start.5
  109.6 4.1 %copy-start.11 = (f32[48]{0:T(128)S(1)}, f32[48]{0:T(128)}, u32[]{:S(2)}) copy-start(f32[48]{0:T(128)} %copy-done.10) | copy-start | bytes 580
  113.8 5.6 %collective-permute-start.25 = (bf16[48,1024]{1,0:T(8,128)(2,1)S(1)}, bf16[48,1024]{1,0:T(8,128)(2,1)S(1)}, u32[]{:S(2)}, u32[]{:S(2)}) collective-permute-start(bf16[48,1024]{1,0:T(8,128)(2,1)S(1)} %divide_convert_fusion), channel_id=1, source_target_pairs={{0,3},{1,0},{2,1},{3,2},{4,7},{5,4},{6,5},{7,6},{8,11},{9,8},{10,9... | collective-permute-start | bytes 294920 | tf_op jit(solution)/shard_map/ppermute | solution.py:96
  114.1 10.9 %collective-permute-start.24 = (bf16[48,1024]{1,0:T(8,128)(2,1)S(1)}, bf16[48,1024]{1,0:T(8,128)(2,1)S(1)}, u32[]{:S(2)}, u32[]{:S(2)}) collective-permute-start(bf16[48,1024]{1,0:T(8,128)(2,1)S(1)} %divide_convert_fusion), channel_id=1, source_target_pairs={{0,2},{1,3},{2,0},{3,1},{4,6},{5,7},{6,4},{7,5},{8,10},{9,11},{10,... | collective-permute-start | bytes 294920 | tf_op jit(solution)/shard_map/ppermute | solution.py:96
  116.5 8.5 %collective-permute-start.23 = (bf16[48,1024]{1,0:T(8,128)(2,1)S(1)}, bf16[48,1024]{1,0:T(8,128)(2,1)S(1)}, u32[]{:S(2)}, u32[]{:S(2)}) collective-permute-start(bf16[48,1024]{1,0:T(8,128)(2,1)S(1)} %divide_convert_fusion), channel_id=1, source_target_pairs={{0,1},{1,2},{2,3},{3,0},{4,5},{5,6},{6,7},{7,4},{8,9},{9,10},{10,1... | collective-permute-start | bytes 294920 | tf_op jit(solution)/shard_map/ppermute | solution.py:96
  119.4 11.3 %collective-permute-start.17 = (f32[4096]{0:T(1024)S(1)}, f32[4096]{0:T(1024)S(1)}, u32[]{:S(2)}, u32[]{:S(2)}) collective-permute-start(f32[4096]{0:T(1024)S(1)} %select_reduce_fusion.2), channel_id=1, source_target_pairs={{0,1},{1,2},{2,3},{3,0},{4,5},{5,6},{6,7},{7,4},{8,9},{9,10},{10,1... | collective-permute-start | bytes 49160 | tf_op jit(solution)/shard_map/ppermute | solution.py:96
  127.2 11.7 %all-to-all-start = ((bf16[8,48,512]{2,1,0:T(8,128)(2,1)}), bf16[8,48,512]{2,1,0:T(8,128)(2,1)S(1)}, u32[]{:S(2)}, u32[]{:S(2)}) async-start(bf16[8,48,512]{2,1,0:T(8,128)(2,1)} %copy.27), calls=%async_computation | async-start | bytes 786432 | tf_op jit(solution)/shard_map/all_to_all | solution.py:163

commit v8 on v4

--- a/solution.py
+++ b/solution.py
@@ -157,13 +157,13 @@
         preferred_element_type=jnp.float32,
     )
     chunk = model_width // feature_count
+    gathered = gather_blocks(group_blocks, "dp")
     both = jnp.stack([pooled_part, scaled_part]).reshape(2, rows, feature_count, chunk)
+    both, gathered = lax.optimization_barrier((both, gathered))
     pooled_chunk, scaled_chunk = scatter_sum(both.transpose(2, 0, 1, 3), "fsdp")
     mean_chunk = (pooled_chunk / counts[:, None]).astype(jnp.bfloat16)
     mean_pooled = gather_blocks(mean_chunk, "fsdp").transpose(1, 0, 2).reshape(rows, model_width)
 
-    gathered = gather_blocks(group_blocks, "dp")
-    mean_pooled, gathered = lax.optimization_barrier((mean_pooled, gathered))
     slice_width = model_width // data_count
     pieces = mean_pooled.reshape(rows, data_count, slice_width).transpose(1, 0, 2)
     pieces = lax.all_to_all(pieces, "dp", 0, 0, tiled=True)
@@ -206,7 +206,6 @@
     mean_part = lax.dot_general(
         grad_low, proj_weight, contract_last, preferred_element_type=jnp.float32
     )
-    mean_part, pooled_cols = lax.optimization_barrier((mean_part, pooled_cols))
     proj_grad = lax.dot_general(
         pooled_cols, grad_low_cols, contract_first, preferred_element_type=jnp.float32
     )

time: 181 us -> 175 us (0.967)
  local copies, waits for them, and re-layouts: 48.3 us -> 35.8 us
  starting transfers between devices: 27.4 us -> 33.9 us
  matrix products: 14.1 us -> 16.1 us
    ppermute x20, waiting for transfers between devices: 43.3 us -> 15.5 us  [gather_blocks(): lax.ppermute(x, axis, [(i, (i + s) % n) for i in range(n)])]
    ppermute x3, waiting for transfers between devices: 0.01 us -> 27.5 us  [scatter_sum(): lax.ppermute(piece, axis, [(i, (i + s) % n) for i in range(n)])]
    ppermute x20, starting transfers between devices: 18.3 us -> 26 us  [gather_blocks(): lax.ppermute(x, axis, [(i, (i + s) % n) for i in range(n)])]
    transpose x2, local copies, waits for them, and re-layouts: 4.21 us -> 0.56 us  [local_small(): gathered[:, :, rows:2 * rows].transpose(0, 2, 1, 3)]
    another operation x1 -> x2, local copies, waits for them, and re-layouts: 5.9 us -> 2.45 us
    another operation x1 -> x2, other arithmetic: 0.73 us -> 3.69 us  [the longest x1 2.96 us: local_small(): jnp.stack([pooled_part, scaled_part]).reshape(2, rows, feature_count, chunk)]
    unnamed x55 -> x48, local copies, waits for them, and re-layouts: 14.6 us -> 12.3 us
    another operation x3 -> x2, local copies, waits for them, and re-layouts: 7.17 us -> 5.13 us  [local_small(): jnp.stack([pooled_part, scaled_part]).reshape(2, rows, feature_count, chunk)]
  transfers between devices with their start and end apart: 24 -> 24, of which waited for: 10 -> 8; matrix products, arithmetic and copies ran while one was open for 34% -> 22% of each run, Pallas kernels for 0% -> 0%
where the time goes in v8:
time: 175 us; the launch traced here: 174 us
  waiting for transfers between devices  43 us (25%)
  local copies, waits for them, and re-layouts  35.8 us (20%)
  starting transfers between devices  33.9 us (19%)
  other arithmetic  22.7 us (13%)
  blocking collectives  19.8 us (11%)
  matrix products  16.1 us (9%)
  between operations  2.79 us (2%)
    ppermute x3, waiting for transfers between devices, scatter_sum(): lax.ppermute(piece, axis, [(i, (i + s) % n) for i in range(n)])  27.5 us
    ppermute x20, starting transfers between devices, gather_blocks(): lax.ppermute(x, axis, [(i, (i + s) % n) for i in range(n)])  26 us
    all_gather x1, blocking collectives, local_small(): both = lax.all_gather(both, 'fsdp', axis=1, tiled=True)  19.8 us
    ppermute x20, waiting for transfers between devices, gather_blocks(): lax.ppermute(x, axis, [(i, (i + s) % n) for i in range(n)])  15.5 us
    unnamed x48, local copies, waits for them, and re-layouts  12.3 us
    gather x4, local copies, waits for them, and re-layouts, gather_blocks(): return jnp.take(stack, order, axis=0)  6.94 us
    another operation x2, local copies, waits for them, and re-layouts, local_small(): jnp.stack([pooled_part, scaled_part]).reshape(2, rows, feature_count, chunk)  5.13 us
    ppermute x3, starting transfers between devices, scatter_sum(): lax.ppermute(piece, axis, [(i, (i + s) % n) for i in range(n)])  3.94 us
  transfers between devices with their start and end apart: 24, of which 8 were waited for; matrix products, arithmetic and copies ran while one was open for 22% of the time, Pallas kernels for 0%

profile of v8, /device:TPU:0, one launch (start us, length us, event | category | flops | bytes accessed | tf_op | source)
XLA Modules:
  0.0 174.1 jit_solution(8601981076457233212)
XLA Ops:
  3.8 5.1 %collective-permute-start.2 = (bf16[97,256]{1,0:T(8,128)(2,1)S(1)}, bf16[97,256]{1,0:T(8,128)(2,1)S(1)}, u32[]{:S(2)}, u32[]{:S(2)}) collective-permute-start(bf16[97,256]{1,0:T(8,128)(2,1)S(1)} %constant_dynamic-update-slice_fusion), channel_id=1, source_target_pairs={{0,3},{1,0},{2,1},{3,2},{4,7},{5,4},{6,5},{7,6},{8,11},{9,8},{10,9... | collective-permute-start | bytes 149000 | tf_op jit(solution)/shard_map/ppermute | solution.py:96
  9.9 1.5 fusion.3
  12.0 2.7 %fusion = f32[48,4096]{1,0:T(8,128)} fusion(bf16[128,4096]{1,0:T(8,128)(2,1)S(1)} %copy-done.1, f32[128]{0:T(128)S(1)} %get-tuple-element.23, s32[128]{0:T(128)} %bitcast.124), kind=kOutput, calls=%fused_computation.10 | convolution fusion | flops 303044608 | bytes 1836032 | tf_op jit(solution)/shard_map/dot_general | solution.py:152
  14.7 2.6 %stack.100 = f32[1,48,4,1024]{3,2,1,0:T(4,128)} reshape(f32[48,4096]{1,0:T(8,128)} %fusion) | data formatting | bytes 1572864 | tf_op jit(solution)/shard_map/stack | solution.py:161
  17.3 1.4 fusion.8
  18.6 2.6 %stack.99 = f32[1,48,4,1024]{3,2,1,0:T(4,128)} reshape(f32[48,4096]{1,0:T(8,128)} %fusion.8) | data formatting | bytes 1572864 | tf_op jit(solution)/shard_map/stack | solution.py:161
  21.3 3.0 %pad_maximum_fusion = f32[2,48,4,1024]{3,2,1,0:T(4,128)} fusion(f32[1,48,4,1024]{3,2,1,0:T(4,128)} %stack.100, f32[1,48,4,1024]{3,2,1,0:T(4,128)} %stack.99), kind=kLoop, calls=%fused_computation.19 | loop fusion | flops 393216 | bytes 3145728 | tf_op jit(solution)/shard_map/stack | solution.py:161
  25.0 1.5 gather_fusion
  26.7 1.5 collective-permute-start.4
  28.2 2.4 %collective-permute-start.5 = (bf16[4,97,256]{2,1,0:T(8,128)(2,1)S(1)}, bf16[4,97,256]{2,1,0:T(8,128)(2,1)S(1)}, u32[]{:S(2)}, u32[]{:S(2)}) collective-permute-start(bf16[4,97,256]{2,1,0:T(8,128)(2,1)S(1)} %broadcast_select_fusion.1), channel_id=1, source_target_pairs={{0,12},{4,16},{8,20},{12,24},{16,28},{20,0},{24,4},{28,8},{1,13},{... | collective-permute-start | bytes 595976 | tf_op jit(solution)/shard_map/ppermute | solution.py:96
  32.7 1.9 %collective-permute-done.3 = bf16[4,97,256]{2,1,0:T(8,128)(2,1)S(1)} collective-permute-done((bf16[4,97,256]{2,1,0:T(8,128)(2,1)S(1)}, bf16[4,97,256]{2,1,0:T(8,128)(2,1)S(1)}, u32[]{:S(2)}, u32[]{:S(2)}) %collective-permute-start.3) | collective-permute-done | bytes 198688 | tf_op jit(solution)/shard_map/ppermute | solution.py:96
  34.7 1.4 collective-permute-start.8
  36.8 3.6 %collective-permute-start.9 = (bf16[4,97,256]{2,1,0:T(8,128)(2,1)S(1)}, bf16[4,97,256]{2,1,0:T(8,128)(2,1)S(1)}, u32[]{:S(2)}, u32[]{:S(2)}) collective-permute-start(bf16[4,97,256]{2,1,0:T(8,128)(2,1)S(1)} %broadcast_select_fusion.1), channel_id=1, source_target_pairs={{0,28},{4,0},{8,4},{12,8},{16,12},{20,16},{24,20},{28,24},{1,29},{... | collective-permute-start | bytes 595976 | tf_op jit(solution)/shard_map/ppermute | solution.py:96
  41.1 3.1 %collective-permute-done.5 = bf16[4,97,256]{2,1,0:T(8,128)(2,1)S(1)} collective-permute-done((bf16[4,97,256]{2,1,0:T(8,128)(2,1)S(1)}, bf16[4,97,256]{2,1,0:T(8,128)(2,1)S(1)}, u32[]{:S(2)}, u32[]{:S(2)}) %collective-permute-start.5) | collective-permute-done | bytes 198688 | tf_op jit(solution)/shard_map/ppermute | solution.py:96
  45.6 2.3 %collective-permute-done.7 = bf16[4,97,256]{2,1,0:T(8,128)(2,1)S(1)} collective-permute-done((bf16[4,97,256]{2,1,0:T(8,128)(2,1)S(1)}, bf16[4,97,256]{2,1,0:T(8,128)(2,1)S(1)}, u32[]{:S(2)}, u32[]{:S(2)}) %collective-permute-start.7) | collective-permute-done | bytes 198688 | tf_op jit(solution)/shard_map/ppermute | solution.py:96
  50.0 3.3 %gather_fusion.1 = bf16[8,4,97,256]{3,2,1,0:T(8,128)(2,1)} fusion(bf16[8,4,97,256]{3,2,1,0:T(8,128)(2,1)} %bitcast_dynamic-update-slice_fusion, s32[1024]{0:T(1024)S(1)} %pad_clamp_fusion), kind=kCustom, calls=%fused_computation.1 | custom fusion | bytes 3178528 | tf_op jit(solution)/shard_map/jit(_take)/gather | solution.py:100
  53.3 1.7 broadcast_select_fusion
  55.6 1.0 copy.31
  57.0 1.1 copy.32
  58.3 2.1 %fusion.38 = (f32[384]{0:T(512)S(1)}, f32[384,384]{0,1:T(8,128)S(1)}) fusion(bf16[384,1024]{1,0:T(8,128)(2,1)} %bitcast.102, bf16[384,1024]{1,0:T(8,128)(2,1)} %bitcast.97), kind=kOutput, calls=%fused_computation.131 | convolution fusion | flops 302284416 | bytes 2164224 | tf_op jit(solution)/shard_map/dot_general | solution.py:182
  62.0 1.6 constant_dynamic-slice_fusion.3
  64.5 2.8 %collective-permute-start.12 = (f32[2,48,1024]{2,1,0:T(8,128)}, f32[2,48,1024]{2,1,0:T(8,128)}, u32[]{:S(2)}, u32[]{:S(2)}) collective-permute-start(f32[2,48,1024]{2,1,0:T(8,128)} %bitcast.89), channel_id=1, source_target_pairs={{0,3},{1,0},{2,1},{3,2},{4,7},{5,4},{6,5},{7,6},{8,11},{9,8},{10,9... | collective-permute-start | bytes 1179656 | tf_op jit(solution)/shard_map/ppermute | solution.py:113
  68.1 1.1 collective-permute-start.11
  70.8 1.8 %convolution_multiply_fusion.1 = f32[384,1024]{1,0:T(8,128)S(1)} fusion(bf16[384,384]{0,1:T(8,128)(2,1)} %subtract_convert_fusion, bf16[384,1024]{1,0:T(8,128)(2,1)} %bitcast.98), kind=kOutput, calls=%fused_computation.22 | convolution fusion | flops 302383104 | bytes 2654208 | tf_op jit(solution)/shard_map/dot_general | solution.py:194
  72.6 1.1 copy-done.3
  74.4 1.7 convolution_multiply_fusion.3
  76.9 26.8 %collective-permute-done.11 = f32[2,48,1024]{2,1,0:T(8,128)} collective-permute-done((f32[2,48,1024]{2,1,0:T(8,128)}, f32[2,48,1024]{2,1,0:T(8,128)}, u32[]{:S(2)}, u32[]{:S(2)}) %collective-permute-start.11) | collective-permute-done | bytes 393248 | tf_op jit(solution)/shard_map/ppermute | solution.py:113
  103.7 2.6 %pad_maximum_fusion.1 = f32[4,2,48,1024]{3,2,1,0:T(8,128)} fusion(f32[1,2,48,1024]{3,2,1,0:T(8,128)} %bitcast.20, f32[1,2,48,1024]{3,2,1,0:T(8,128)} %bitcast.19, f32[1,2,48,1024]{3,2,1,0:T(8,128)} %bitcast.18, f32[1,2,48,1024]{3,2,1,0:T(8,128)S(1)} %bitcast.99), kind=kLoop, calls=%fused_computation.20 | loop fusion | flops 1179648 | bytes 3145728 | tf_op jit(solution)/shard_map/stack | solution.py:115
  106.2 3.3 %gather_fusion.2 = f32[4,2,48,1024]{3,2,1,0:T(8,128)} fusion(f32[4,2,48,1024]{3,2,1,0:T(8,128)} %pad_maximum_fusion.1, s32[1024]{0:T(1024)} %copy-done.9), kind=kCustom, calls=%fused_computation.2 | custom fusion | bytes 3145744 | tf_op jit(solution)/shard_map/jit(_take)/gather | solution.py:115
  109.6 1.7 select_reduce_fusion
  111.3 1.7 fusion.18
  113.0 19.8 %all_gather.3 = f32[49,4096]{1,0:T(8,128)S(1)} all-gather(f32[49,1024]{1,0:T(8,128)S(1)} %pad_maximum_fusion.3), channel_id=1, replica_groups=mesh['dp'=8,'fsdp'=4] {'fsdp'}, dimensions={1}, use_global_device_ids=true | all-gather | bytes 1003520 | tf_op jit(solution)/shard_map/all_gather | solution.py:214
  132.8 2.6 %fusion.7 = (f32[128]{0:T(128)S(1)}, f32[128,4096]{1,0:T(8,128)}) fusion(bf16[128,4096]{1,0:T(8,128)(2,1)S(1)} %copy-done.1, f32[49,4096]{1,0:T(8,128)S(1)} %all_gather.3, f32[48]{0:T(128)S(1)} %copy-done.13, s32[128]{0:T(128)S(1)} %bitcast.126, f32[4096]{0:T(1024)S(1)} %convert_element_type.72), kind=kOutput, calls=%fused_computation.17 | convolution fusion | flops 304289664 | bytes 3950080 | tf_op jit(solution)/shard_map/dot_general | solution.py:217
  135.5 1.9 %collective-permute-start.14 = (f32[4096]{0:T(1024)S(1)}, f32[4096]{0:T(1024)}, u32[]{:S(2)}, u32[]{:S(2)}) collective-permute-start(f32[4096]{0:T(1024)S(1)} %bitcast.109), channel_id=1, source_target_pairs={{0,8},{4,12},{8,16},{12,20},{16,24},{20,28},{24,0},{28,4},{1,9},{5... | collective-permute-start | bytes 49160 | tf_op jit(solution)/shard_map/ppermute | solution.py:96
  137.5 1.6 collective-permute-start.22
  139.0 1.3 collective-permute-start.20
  140.9 1.3 collective-permute-done.22
  143.0 5.6 %collective-permute-done.21 = bf16[48,1024]{1,0:T(8,128)(2,1)S(1)} collective-permute-done((bf16[48,1024]{1,0:T(8,128)(2,1)S(1)}, bf16[48,1024]{1,0:T(8,128)(2,1)S(1)}, u32[]{:S(2)}, u32[]{:S(2)}) %collective-permute-start.21) | collective-permute-done | bytes 98336 | tf_op jit(solution)/shard_map/ppermute | solution.py:96
  148.6 1.3 collective-permute-start.16
  149.9 1.4 gather_fusion.4
  151.4 1.1 select_bitcast_fusion
  153.6 1.9 %copy.24 = bf16[8,48,512]{2,1,0:T(8,128)(2,1)} copy(bf16[8,48,512]{2,0,1:T(8,128)(2,1)} %bitcast.100) | data formatting | bytes 786432 | tf_op jit(solution)/shard_map/transpose | solution.py:168
  155.5 3.9 %all-to-all-start = ((bf16[8,48,512]{2,1,0:T(8,128)(2,1)}), bf16[8,48,512]{2,1,0:T(8,128)(2,1)S(1)}, u32[]{:S(2)}, u32[]{:S(2)}) async-start(bf16[8,48,512]{2,1,0:T(8,128)(2,1)} %copy.24), calls=%async_computation | async-start | bytes 786432 | tf_op jit(solution)/shard_map/all_to_all | solution.py:169
  159.4 2.9 %collective-permute-start.18 = (f32[4096]{0:T(1024)S(1)}, f32[4096]{0:T(1024)S(1)}, u32[]{:S(2)}, u32[]{:S(2)}) collective-permute-start(f32[4096]{0:T(1024)S(1)} %bitcast.113), channel_id=1, source_target_pairs={{0,24},{4,28},{8,0},{12,4},{16,8},{20,12},{24,16},{28,20},{1,25},{... | collective-permute-start | bytes 49160 | tf_op jit(solution)/shard_map/ppermute | solution.py:96
  162.8 3.1 %fusion.6 = bf16[128,4096]{1,0:T(8,128)(2,1)} fusion(bf16[128,4096]{1,0:T(8,128)(2,1)S(1)} %copy-done.1, f32[128,4096]{1,0:T(8,128)} %get-tuple-element.30, f32[128]{0:T(128)} %broadcast_multiply_fusion, f32[128]{0:T(128)} %get-tuple-element.22, f32[128]{0:T(128)} %copy-done.12), kind=kLoop, calls=%fused_computation.16 | loop fusion | flops 3145728 | bytes 4195840 | tf_op jit(solution)/shard_map/convert_element_type | solution.py:226
  165.9 1.3 collective-permute-done.18
  169.5 1.3 select_reduce_fusion.2
  170.8 2.1 %fusion.15 = f32[512,256]{1,0:T(8,128)} fusion(bf16[384,512]{1,0:T(8,128)(2,1)S(1)} %bitcast.101, f32[384,1024]{1,0:T(8,128)} %copy-done.3, s32[]{:T(128)S(6)} %select_n.179), kind=kOutput, calls=%fused_computation.56 | convolution fusion | flops 100663296 | bytes 1114116 | tf_op jit(solution)/shard_map/dot_general | solution.py:209
  (111 shorter events, 24.9 us)
Async XLA Ops:
  0.6 110.6 %copy-start = (bf16[1024,1024]{1,0:T(8,128)(2,1)S(1)}, bf16[1024,1024]{1,0:T(8,128)(2,1)}, u32[]{:S(2)}) copy-start(bf16[1024,1024]{1,0:T(8,128)(2,1)} %param.13) | copy-start | bytes 6291460
  0.6 11.4 %copy-start.1 = (bf16[128,4096]{1,0:T(8,128)(2,1)S(1)}, bf16[128,4096]{1,0:T(8,128)(2,1)}, u32[]{:S(2)}) copy-start(bf16[128,4096]{1,0:T(8,128)(2,1)} %param.10) | copy-start | bytes 3145732
  3.8 20.5 %collective-permute-start.2 = (bf16[97,256]{1,0:T(8,128)(2,1)S(1)}, bf16[97,256]{1,0:T(8,128)(2,1)S(1)}, u32[]{:S(2)}, u32[]{:S(2)}) collective-permute-start(bf16[97,256]{1,0:T(8,128)(2,1)S(1)} %constant_dynamic-update-slice_fusion), channel_id=1, source_target_pairs={{0,3},{1,0},{2,1},{3,2},{4,7},{5,4},{6,5},{7,6},{8,11},{9,8},{10,9... | collective-permute-start | bytes 149000 | tf_op jit(solution)/shard_map/ppermute | solution.py:96
  8.9 15.5 %collective-permute-start.1 = (bf16[97,256]{1,0:T(8,128)(2,1)S(1)}, bf16[97,256]{1,0:T(8,128)(2,1)S(1)}, u32[]{:S(2)}, u32[]{:S(2)}) collective-permute-start(bf16[97,256]{1,0:T(8,128)(2,1)S(1)} %constant_dynamic-update-slice_fusion), channel_id=1, source_target_pairs={{0,2},{1,3},{2,0},{3,1},{4,6},{5,7},{6,4},{7,5},{8,10},{9,11},{10,... | collective-permute-start | bytes 149000 | tf_op jit(solution)/shard_map/ppermute | solution.py:96
  8.9 15.5 %collective-permute-start = (bf16[97,256]{1,0:T(8,128)(2,1)S(1)}, bf16[97,256]{1,0:T(8,128)(2,1)S(1)}, u32[]{:S(2)}, u32[]{:S(2)}) collective-permute-start(bf16[97,256]{1,0:T(8,128)(2,1)S(1)} %constant_dynamic-update-slice_fusion), channel_id=1, source_target_pairs={{0,1},{1,2},{2,3},{3,0},{4,5},{5,6},{6,7},{7,4},{8,9},{9,10},{10,1... | collective-permute-start | bytes 149000 | tf_op jit(solution)/shard_map/ppermute | solution.py:96
  9.9 22.1 %copy-start.7 = (pred[4]{0:T(512)(128)(4,1)}, pred[4]{0:T(512)(128)(4,1)S(1)}, u32[]{:S(2)}) copy-start(pred[4]{0:T(512)(128)(4,1)S(1)} %compare_and_fusion) | copy-start | bytes 16
  12.0 5.2 %copy-start.12 = (f32[128]{0:T(128)}, f32[128]{0:T(128)S(1)}, u32[]{:S(2)}) copy-start(f32[128]{0:T(128)S(1)} %get-tuple-element.23) | copy-start | bytes 1540
  12.0 5.2 %copy-start.6 = (bf16[4096]{0:T(1024)(128)(2,1)S(1)}, bf16[4096]{0:T(1024)(128)(2,1)}, u32[]{:S(2)}) copy-start(bf16[4096]{0:T(1024)(128)(2,1)} %param.12) | copy-start | bytes 24580
  12.0 5.2 %copy-start.14 = (s32[1,128]{1,0:T(1,128)S(1)}, s32[1,128]{1,0:T(1,128)}, u32[]{:S(2)}) copy-start(s32[1,128]{1,0:T(1,128)} %param.11) | copy-start | bytes 1540
  21.2 3.8 %copy-start.9 = (s32[1024]{0:T(1024)}, s32[1024]{0:T(1024)S(1)}, u32[]{:S(2)}) copy-start(s32[1024]{0:T(1024)S(1)} %pad_clamp_fusion.1) | copy-start | bytes 12292
  21.3 28.7 %copy-start.10 = (s32[1024]{0:T(1024)}, s32[1024]{0:T(1024)S(1)}, u32[]{:S(2)}) copy-start(s32[1024]{0:T(1024)S(1)} %pad_clamp_fusion) | copy-start | bytes 12292
  24.2 29.0 %copy-start.11 = (pred[8]{0:T(512)(128)(4,1)}, pred[8]{0:T(512)(128)(4,1)S(1)}, u32[]{:S(2)}) copy-start(pred[8]{0:T(512)(128)(4,1)S(1)} %compare_and_fusion.1) | copy-start | bytes 28
  26.6 8.0 %collective-permute-start.3 = (bf16[4,97,256]{2,1,0:T(8,128)(2,1)S(1)}, bf16[4,97,256]{2,1,0:T(8,128)(2,1)S(1)}, u32[]{:S(2)}, u32[]{:S(2)}) collective-permute-start(bf16[4,97,256]{2,1,0:T(8,128)(2,1)S(1)} %broadcast_select_fusion.1), channel_id=1, source_target_pairs={{0,4},{4,8},{8,12},{12,16},{16,20},{20,24},{24,28},{28,0},{1,5},{5... | collective-permute-start | bytes 595976 | tf_op jit(solution)/shard_map/ppermute | solution.py:96
  26.7 10.1 %collective-permute-start.4 = (bf16[4,97,256]{2,1,0:T(8,128)(2,1)S(1)}, bf16[4,97,256]{2,1,0:T(8,128)(2,1)S(1)}, u32[]{:S(2)}, u32[]{:S(2)}) collective-permute-start(bf16[4,97,256]{2,1,0:T(8,128)(2,1)S(1)} %broadcast_select_fusion.1), channel_id=1, source_target_pairs={{0,8},{4,12},{8,16},{12,20},{16,24},{20,28},{24,0},{28,4},{1,9},{5... | collective-permute-start | bytes 595976 | tf_op jit(solution)/shard_map/ppermute | solution.py:96
  28.2 15.9 %collective-permute-start.5 = (bf16[4,97,256]{2,1,0:T(8,128)(2,1)S(1)}, bf16[4,97,256]{2,1,0:T(8,128)(2,1)S(1)}, u32[]{:S(2)}, u32[]{:S(2)}) collective-permute-start(bf16[4,97,256]{2,1,0:T(8,128)(2,1)S(1)} %broadcast_select_fusion.1), channel_id=1, source_target_pairs={{0,12},{4,16},{8,20},{12,24},{16,28},{20,0},{24,4},{28,8},{1,13},{... | collective-permute-start | bytes 595976 | tf_op jit(solution)/shard_map/ppermute | solution.py:96
  30.6 14.3 %collective-permute-start.6 = (bf16[4,97,256]{2,1,0:T(8,128)(2,1)S(1)}, bf16[4,97,256]{2,1,0:T(8,128)(2,1)S(1)}, u32[]{:S(2)}, u32[]{:S(2)}) collective-permute-start(bf16[4,97,256]{2,1,0:T(8,128)(2,1)S(1)} %broadcast_select_fusion.1), channel_id=1, source_target_pairs={{0,16},{4,20},{8,24},{12,28},{16,0},{20,4},{24,8},{28,12},{1,17},{... | collective-permute-start | bytes 595976 | tf_op jit(solution)/shard_map/ppermute | solution.py:96
  31.1 16.8 %collective-permute-start.7 = (bf16[4,97,256]{2,1,0:T(8,128)(2,1)S(1)}, bf16[4,97,256]{2,1,0:T(8,128)(2,1)S(1)}, u32[]{:S(2)}, u32[]{:S(2)}) collective-permute-start(bf16[4,97,256]{2,1,0:T(8,128)(2,1)S(1)} %broadcast_select_fusion.1), channel_id=1, source_target_pairs={{0,20},{4,24},{8,28},{12,0},{16,4},{20,8},{24,12},{28,16},{1,21},{... | collective-permute-start | bytes 595976 | tf_op jit(solution)/shard_map/ppermute | solution.py:96
  34.7 13.9 %collective-permute-start.8 = (bf16[4,97,256]{2,1,0:T(8,128)(2,1)S(1)}, bf16[4,97,256]{2,1,0:T(8,128)(2,1)S(1)}, u32[]{:S(2)}, u32[]{:S(2)}) collective-permute-start(bf16[4,97,256]{2,1,0:T(8,128)(2,1)S(1)} %broadcast_select_fusion.1), channel_id=1, source_target_pairs={{0,24},{4,28},{8,0},{12,4},{16,8},{20,12},{24,16},{28,20},{1,25},{... | collective-permute-start | bytes 595976 | tf_op jit(solution)/shard_map/ppermute | solution.py:96
  36.8 12.5 %collective-permute-start.9 = (bf16[4,97,256]{2,1,0:T(8,128)(2,1)S(1)}, bf16[4,97,256]{2,1,0:T(8,128)(2,1)S(1)}, u32[]{:S(2)}, u32[]{:S(2)}) collective-permute-start(bf16[4,97,256]{2,1,0:T(8,128)(2,1)S(1)} %broadcast_select_fusion.1), channel_id=1, source_target_pairs={{0,28},{4,0},{8,4},{12,8},{16,12},{20,16},{24,20},{28,24},{1,29},{... | collective-permute-start | bytes 595976 | tf_op jit(solution)/shard_map/ppermute | solution.py:96
  58.3 3.8 %copy-start.2 = (f32[2,48,4,1024]{3,2,1,0:T(4,128)S(1)}, f32[2,48,4,1024]{3,2,1,0:T(4,128)}, u32[]{:S(2)}) copy-start(f32[2,48,4,1024]{3,2,1,0:T(4,128)} %pad_maximum_fusion) | copy-start | bytes 4718596
  64.5 12.4 %collective-permute-start.12 = (f32[2,48,1024]{2,1,0:T(8,128)}, f32[2,48,1024]{2,1,0:T(8,128)}, u32[]{:S(2)}, u32[]{:S(2)}) collective-permute-start(f32[2,48,1024]{2,1,0:T(8,128)} %bitcast.89), channel_id=1, source_target_pairs={{0,3},{1,0},{2,1},{3,2},{4,7},{5,4},{6,5},{7,6},{8,11},{9,8},{10,9... | collective-permute-start | bytes 1179656 | tf_op jit(solution)/shard_map/ppermute | solution.py:113
  68.1 35.5 %collective-permute-start.11 = (f32[2,48,1024]{2,1,0:T(8,128)}, f32[2,48,1024]{2,1,0:T(8,128)}, u32[]{:S(2)}, u32[]{:S(2)}) collective-permute-start(f32[2,48,1024]{2,1,0:T(8,128)} %bitcast.90), channel_id=1, source_target_pairs={{0,2},{1,3},{2,0},{3,1},{4,6},{5,7},{6,4},{7,5},{8,10},{9,11},{10,... | collective-permute-start | bytes 1179656 | tf_op jit(solution)/shard_map/ppermute | solution.py:113
  70.1 33.6 %collective-permute-start.10 = (f32[2,48,1024]{2,1,0:T(8,128)}, f32[2,48,1024]{2,1,0:T(8,128)}, u32[]{:S(2)}, u32[]{:S(2)}) collective-permute-start(f32[2,48,1024]{2,1,0:T(8,128)} %bitcast.91), channel_id=1, source_target_pairs={{0,1},{1,2},{2,3},{3,0},{4,5},{5,6},{6,7},{7,4},{8,9},{9,10},{10,1... | collective-permute-start | bytes 1179656 | tf_op jit(solution)/shard_map/ppermute | solution.py:113
  72.6 1.2 copy-start.3
  106.2 3.3 %copy-start.8 = (pred[4]{0:T(512)(128)(4,1)S(1)}, pred[4]{0:T(512)(128)(4,1)}, u32[]{:S(2)}) copy-start(pred[4]{0:T(512)(128)(4,1)} %copy-done.7) | copy-start | bytes 16
  109.6 1.7 copy-start.13
  111.3 21.5 %copy-start.15 = (s32[1,128]{1,0:T(1,128)S(1)}, s32[1,128]{1,0:T(1,128)}, u32[]{:S(2)}) copy-start(s32[1,128]{1,0:T(1,128)} %param.11) | copy-start | bytes 1540
  135.4 23.9 %collective-permute-start.13 = (f32[4096]{0:T(1024)S(1)}, f32[4096]{0:T(1024)}, u32[]{:S(2)}, u32[]{:S(2)}) collective-permute-start(f32[4096]{0:T(1024)S(1)} %bitcast.108), channel_id=1, source_target_pairs={{0,4},{4,8},{8,12},{12,16},{16,20},{20,24},{24,28},{28,0},{1,5},{5... | collective-permute-start | bytes 49160 | tf_op jit(solution)/shard_map/ppermute | solution.py:96
  135.5 26.8 %collective-permute-start.14 = (f32[4096]{0:T(1024)S(1)}, f32[4096]{0:T(1024)}, u32[]{:S(2)}, u32[]{:S(2)}) collective-permute-start(f32[4096]{0:T(1024)S(1)} %bitcast.109), channel_id=1, source_target_pairs={{0,8},{4,12},{8,16},{12,20},{16,24},{20,28},{24,0},{28,4},{1,9},{5... | collective-permute-start | bytes 49160 | tf_op jit(solution)/shard_map/ppermute | solution.py:96
  137.5 4.8 %collective-permute-start.22 = (bf16[48,1024]{1,0:T(8,128)(2,1)S(1)}, bf16[48,1024]{1,0:T(8,128)(2,1)S(1)}, u32[]{:S(2)}, u32[]{:S(2)}) collective-permute-start(bf16[48,1024]{1,0:T(8,128)(2,1)S(1)} %get-tuple-element.20), channel_id=1, source_target_pairs={{0,3},{1,0},{2,1},{3,2},{4,7},{5,4},{6,5},{7,6},{8,11},{9,8},{10,9... | collective-permute-start | bytes 294920 | tf_op jit(solution)/shard_map/ppermute | solution.py:96
  139.0 9.5 %collective-permute-start.21 = (bf16[48,1024]{1,0:T(8,128)(2,1)S(1)}, bf16[48,1024]{1,0:T(8,128)(2,1)S(1)}, u32[]{:S(2)}, u32[]{:S(2)}) collective-permute-start(bf16[48,1024]{1,0:T(8,128)(2,1)S(1)} %get-tuple-element.20), channel_id=1, source_target_pairs={{0,2},{1,3},{2,0},{3,1},{4,6},{5,7},{6,4},{7,5},{8,10},{9,11},{10,... | collective-permute-start | bytes 294920 | tf_op jit(solution)/shard_map/ppermute | solution.py:96
  139.0 10.8 %collective-permute-start.20 = (bf16[48,1024]{1,0:T(8,128)(2,1)S(1)}, bf16[48,1024]{1,0:T(8,128)(2,1)S(1)}, u32[]{:S(2)}, u32[]{:S(2)}) collective-permute-start(bf16[48,1024]{1,0:T(8,128)(2,1)S(1)} %get-tuple-element.20), channel_id=1, source_target_pairs={{0,1},{1,2},{2,3},{3,0},{4,5},{5,6},{6,7},{7,4},{8,9},{9,10},{10,1... | collective-permute-start | bytes 294920 | tf_op jit(solution)/shard_map/ppermute | solution.py:96
  142.3 23.6 %collective-permute-start.15 = (f32[4096]{0:T(1024)S(1)}, f32[4096]{0:T(1024)}, u32[]{:S(2)}, u32[]{:S(2)}) collective-permute-start(f32[4096]{0:T(1024)S(1)} %bitcast.110), channel_id=1, source_target_pairs={{0,12},{4,16},{8,20},{12,24},{16,28},{20,0},{24,4},{28,8},{1,13},{... | collective-permute-start | bytes 49160 | tf_op jit(solution)/shard_map/ppermute | solution.py:96
  148.6 17.4 %collective-permute-start.16 = (f32[4096]{0:T(1024)S(1)}, f32[4096]{0:T(1024)}, u32[]{:S(2)}, u32[]{:S(2)}) collective-permute-start(f32[4096]{0:T(1024)S(1)} %bitcast.111), channel_id=1, source_target_pairs={{0,16},{4,20},{8,24},{12,28},{16,0},{20,4},{24,8},{28,12},{1,17},{... | collective-permute-start | bytes 49160 | tf_op jit(solution)/shard_map/ppermute | solution.py:96
  149.9 16.0 %collective-permute-start.17 = (f32[4096]{0:T(1024)S(1)}, f32[4096]{0:T(1024)}, u32[]{:S(2)}, u32[]{:S(2)}) collective-permute-start(f32[4096]{0:T(1024)S(1)} %bitcast.112), channel_id=1, source_target_pairs={{0,20},{4,24},{8,28},{12,0},{16,4},{20,8},{24,12},{28,16},{1,21},{... | collective-permute-start | bytes 49160 | tf_op jit(solution)/shard_map/ppermute | solution.py:96
  155.5 15.4 %all-to-all-start = ((bf16[8,48,512]{2,1,0:T(8,128)(2,1)}), bf16[8,48,512]{2,1,0:T(8,128)(2,1)S(1)}, u32[]{:S(2)}, u32[]{:S(2)}) async-start(bf16[8,48,512]{2,1,0:T(8,128)(2,1)} %copy.24), calls=%async_computation | async-start | bytes 786432 | tf_op jit(solution)/shard_map/all_to_all | solution.py:169
  159.4 7.8 %collective-permute-start.18 = (f32[4096]{0:T(1024)S(1)}, f32[4096]{0:T(1024)S(1)}, u32[]{:S(2)}, u32[]{:S(2)}) collective-permute-start(f32[4096]{0:T(1024)S(1)} %bitcast.113), channel_id=1, source_target_pairs={{0,24},{4,28},{8,0},{12,4},{16,8},{20,12},{24,16},{28,20},{1,25},{... | collective-permute-start | bytes 49160 | tf_op jit(solution)/shard_map/ppermute | solution.py:96
  162.3 4.9 %collective-permute-start.19 = (f32[4096]{0:T(1024)S(1)}, f32[4096]{0:T(1024)S(1)}, u32[]{:S(2)}, u32[]{:S(2)}) collective-permute-start(f32[4096]{0:T(1024)S(1)} %bitcast.114), channel_id=1, source_target_pairs={{0,28},{4,0},{8,4},{12,8},{16,12},{20,16},{24,20},{28,24},{1,29},{... | collective-permute-start | bytes 49160 | tf_op jit(solution)/shard_map/ppermute | solution.py:96
  167.2 0.6 copy-start.4
  167.2 0.6 copy-start.5

commit v9 on v5

--- a/solution.py
+++ b/solution.py
@@ -172,7 +172,7 @@
     mean_chunk = (pooled_chunk / counts[:, None]).astype(jnp.bfloat16)
     mean_pooled = gather_blocks(mean_chunk, "fsdp").transpose(1, 0, 2).reshape(rows, model_width)
 
-    gathered = gather_grouped(group_blocks, "dp", CORES)
+    gathered = gather_blocks(group_blocks, "dp")
     mean_pooled, gathered = lax.optimization_barrier((mean_pooled, gathered))
     slice_width = model_width // data_count
     pieces = mean_pooled.reshape(rows, data_count, slice_width).transpose(1, 0, 2)

time: 145 us -> 136 us (0.938)
  waiting for transfers between devices: 28.5 us -> 15.1 us
  local copies, waits for them, and re-layouts: 23.3 us -> 30.5 us
  other arithmetic: 26.3 us -> 20.9 us
  starting transfers between devices: 29.6 us -> 32.6 us
  blocking collectives: 20 us -> 18.5 us
    ppermute x6 -> x3, waiting for transfers between devices: 18.9 us -> 3.55 us  [gather_grouped(): lax.ppermute(near, axis, [(i, (i + inner * s) % n) for i in range(n)])]
    unnamed x43 -> x40, local copies, waits for them, and re-layouts: 6.46 us -> 14.6 us
    ppermute x9 -> x16, starting transfers between devices: 13.7 us -> 20.9 us  [gather_blocks(): lax.ppermute(x, axis, [(i, (i + s) % n) for i in range(n)])]
    ppermute x6 -> x3, starting transfers between devices: 7.56 us -> 2.82 us  [gather_grouped(): lax.ppermute(near, axis, [(i, (i + inner * s) % n) for i in range(n)])]
    another operation x4 -> x2, other arithmetic: 3.76 us -> 0.09 us  [gather_grouped(): jnp.stack(copies)]
    gather x2 -> x1, local copies, waits for them, and re-layouts: 4.24 us -> 0.81 us  [gather_grouped(): jnp.take(jnp.stack(copies), (me // inner - jnp.arange(outer)) % outer, ax...]
    gather x3 -> x4, local copies, waits for them, and re-layouts: 1.96 us -> 5.13 us  [gather_blocks(): return jnp.take(stack, order, axis=0)]
    select_n x2 -> x1, other arithmetic: 2.32 us -> 0.01 us  [gather_grouped(): jnp.take(jnp.stack(copies), (me // inner - jnp.arange(outer)) % outer, ax...]
  transfers between devices with their start and end apart: 21 -> 24, of which waited for: 9 -> 7; matrix products, arithmetic and copies ran while one was open for 28% -> 33% of each run, Pallas kernels for 0% -> 0%
where the time goes in v9:
time: 136 us; the launch traced here: 135 us
  starting transfers between devices  32.6 us (24%)
  local copies, waits for them, and re-layouts  30.5 us (22%)
  other arithmetic  20.9 us (15%)
  blocking collectives  18.5 us (14%)
  waiting for transfers between devices  15.1 us (11%)
  matrix products  14.7 us (11%)
  between operations  2.87 us (2%)
    ppermute x16, starting transfers between devices, gather_blocks(): lax.ppermute(x, axis, [(i, (i + s) % n) for i in range(n)])  20.9 us
    all_gather x1, blocking collectives, local_small(): mean_grad = lax.all_gather(mean_part, 'fsdp', axis=1, tiled=True)  18.5 us
    unnamed x40, local copies, waits for them, and re-layouts  14.6 us
    ppermute x3, waiting for transfers between devices, scatter_sum(): lax.ppermute(piece, axis, [(i, (i + s) % n) for i in range(n)])  6.99 us
    gather x4, local copies, waits for them, and re-layouts, gather_blocks(): return jnp.take(stack, order, axis=0)  5.13 us
    all_to_all x1, starting transfers between devices, local_small(): pieces = lax.all_to_all(pieces, 'dp', 0, 0, tiled=True)  4.82 us
    ppermute x3, starting transfers between devices, scatter_sum(): lax.ppermute(piece, axis, [(i, (i + s) % n) for i in range(n)])  3.99 us
    ppermute x3, waiting for transfers between devices, gather_grouped(): lax.ppermute(near, axis, [(i, (i + inner * s) % n) for i in range(n)])  3.55 us
  transfers between devices with their start and end apart: 24, of which 7 were waited for; matrix products, arithmetic and copies ran while one was open for 33% of the time, Pallas kernels for 0%

profile of v9, /device:TPU:0, one launch (start us, length us, event | category | flops | bytes accessed | tf_op | source)
XLA Modules:
  0.0 135.3 jit_solution(8014286048004674429)
XLA Ops:
  0.6 0.9 constant_dynamic-update-slice_fusion.2
  3.7 5.1 %collective-permute-start.5 = (bf16[97,256]{1,0:T(8,128)(2,1)S(1)}, bf16[97,256]{1,0:T(8,128)(2,1)S(1)}, u32[]{:S(2)}, u32[]{:S(2)}) collective-permute-start(bf16[97,256]{1,0:T(8,128)(2,1)S(1)} %constant_dynamic-update-slice_fusion), channel_id=1, source_target_pairs={{0,3},{1,0},{2,1},{3,2},{4,7},{5,4},{6,5},{7,6},{8,11},{9,8},{10,9... | collective-permute-start | bytes 149000 | tf_op jit(solution)/shard_map/ppermute | solution.py:96
  8.8 1.0 collective-permute-start.3
  10.5 1.5 %fusion = f32[128]{0:T(128)S(1)} fusion(bf16[128,4096]{1,0:T(8,128)(2,1)} %param.10), kind=kLoop, calls=%fused_computation.12 | loop fusion | flops 1572736 | bytes 1049088 | tf_op jit(solution)/shard_map/reduce_sum | solution.py:162
  12.6 2.6 %fusion.9 = f32[48,4096]{1,0:T(8,128)} fusion(bf16[128,4096]{1,0:T(8,128)(2,1)} %param.10, f32[4096]{0:T(1024)S(1)} %convert_element_type.77, f32[128]{0:T(128)S(1)} %get-tuple-element.27, s32[128]{0:T(128)} %bitcast.133), kind=kOutput, calls=%fused_computation.25 | convolution fusion | flops 52434944 | bytes 1852416 | tf_op jit(solution)/shard_map/dot_general | solution.py:166
  15.2 1.7 %reshape.376 = f32[48,4,1024]{2,1,0:T(4,128)S(1)} reshape(f32[48,4096]{1,0:T(8,128)} %fusion.9) | data formatting | bytes 1572864 | tf_op jit(solution)/shard_map/reshape | solution.py:170
  18.5 2.8 %collective-permute-start.2 = (f32[48,1024]{1,0:T(8,128)}, f32[48,1024]{1,0:T(8,128)S(1)}, u32[]{:S(2)}, u32[]{:S(2)}) collective-permute-start(f32[48,1024]{1,0:T(8,128)} %bitcast.97), channel_id=1, source_target_pairs={{0,3},{1,0},{2,1},{3,2},{4,7},{5,4},{6,5},{7,6},{8,11},{9,8},{10,9... | collective-permute-start | bytes 589832 | tf_op jit(solution)/shard_map/ppermute | solution.py:129
  22.0 1.1 collective-permute-start.1
  27.2 1.5 %collective-permute-start.10 = (bf16[4,97,256]{2,1,0:T(8,128)(2,1)S(1)}, bf16[4,97,256]{2,1,0:T(8,128)(2,1)}, u32[]{:S(2)}, u32[]{:S(2)}) collective-permute-start(bf16[4,97,256]{2,1,0:T(8,128)(2,1)S(1)} %broadcast_select_fusion.1), channel_id=1, source_target_pairs={{0,8},{4,12},{8,16},{12,20},{16,24},{20,28},{24,0},{28,4},{1,9},{5... | collective-permute-start | bytes 595976 | tf_op jit(solution)/shard_map/ppermute | solution.py:96
  29.8 2.4 %collective-permute-start.11 = (bf16[4,97,256]{2,1,0:T(8,128)(2,1)S(1)}, bf16[4,97,256]{2,1,0:T(8,128)(2,1)}, u32[]{:S(2)}, u32[]{:S(2)}) collective-permute-start(bf16[4,97,256]{2,1,0:T(8,128)(2,1)S(1)} %broadcast_select_fusion.1), channel_id=1, source_target_pairs={{0,12},{4,16},{8,20},{12,24},{16,28},{20,0},{24,4},{28,8},{1,13},{... | collective-permute-start | bytes 595976 | tf_op jit(solution)/shard_map/ppermute | solution.py:96
  32.1 7.0 %collective-permute-done.1 = f32[48,1024]{1,0:T(8,128)} collective-permute-done((f32[48,1024]{1,0:T(8,128)}, f32[48,1024]{1,0:T(8,128)}, u32[]{:S(2)}, u32[]{:S(2)}) %collective-permute-start.1) | collective-permute-done | bytes 196640 | tf_op jit(solution)/shard_map/ppermute | solution.py:129
  39.1 1.5 %collective-permute-start.12 = (bf16[4,97,256]{2,1,0:T(8,128)(2,1)S(1)}, bf16[4,97,256]{2,1,0:T(8,128)(2,1)}, u32[]{:S(2)}, u32[]{:S(2)}) collective-permute-start(bf16[4,97,256]{2,1,0:T(8,128)(2,1)S(1)} %broadcast_select_fusion.1), channel_id=1, source_target_pairs={{0,16},{4,20},{8,24},{12,28},{16,0},{20,4},{24,8},{28,12},{1,17},{... | collective-permute-start | bytes 595976 | tf_op jit(solution)/shard_map/ppermute | solution.py:96
  40.7 1.1 pad_maximum_fusion
  41.7 1.5 %gather_fusion = f32[4,48,1024]{2,1,0:T(8,128)} fusion(f32[4,48,1024]{2,1,0:T(8,128)S(1)} %pad_maximum_fusion, s32[1024]{0:T(1024)S(1)} %pad_clamp_fusion.3), kind=kCustom, calls=%fused_computation | custom fusion | bytes 1572880 | tf_op jit(solution)/shard_map/jit(_take)/gather | solution.py:131
  43.2 1.3 select_reduce_fusion
  44.7 1.5 %collective-permute-start.14 = (bf16[4,97,256]{2,1,0:T(8,128)(2,1)S(1)}, bf16[4,97,256]{2,1,0:T(8,128)(2,1)S(1)}, u32[]{:S(2)}, u32[]{:S(2)}) collective-permute-start(bf16[4,97,256]{2,1,0:T(8,128)(2,1)S(1)} %broadcast_select_fusion.1), channel_id=1, source_target_pairs={{0,24},{4,28},{8,0},{12,4},{16,8},{20,12},{24,16},{28,20},{1,25},{... | collective-permute-start | bytes 595976 | tf_op jit(solution)/shard_map/ppermute | solution.py:96
  46.2 1.6 %bitcast_dynamic-update-slice_fusion.6 = bf16[8,4,97,256]{3,2,1,0:T(8,128)(2,1)} fusion(bf16[8,4,97,256]{3,2,1,0:T(8,128)(2,1)} %fusion.16, bf16[4,97,256]{2,1,0:T(8,128)(2,1)} %collective-permute-done.9), kind=kLoop, calls=%fused_computation.50 | loop fusion | bytes 425984
  47.8 2.4 %collective-permute-start.15 = (bf16[4,97,256]{2,1,0:T(8,128)(2,1)S(1)}, bf16[4,97,256]{2,1,0:T(8,128)(2,1)S(1)}, u32[]{:S(2)}, u32[]{:S(2)}) collective-permute-start(bf16[4,97,256]{2,1,0:T(8,128)(2,1)S(1)} %broadcast_select_fusion.1), channel_id=1, source_target_pairs={{0,28},{4,0},{8,4},{12,8},{16,12},{20,16},{24,20},{28,24},{1,29},{... | collective-permute-start | bytes 595976 | tf_op jit(solution)/shard_map/ppermute | solution.py:96
  50.2 1.6 %bitcast_dynamic-update-slice_fusion.5 = bf16[8,4,97,256]{3,2,1,0:T(8,128)(2,1)} fusion(bf16[8,4,97,256]{3,2,1,0:T(8,128)(2,1)} %bitcast_dynamic-update-slice_fusion.6, bf16[4,97,256]{2,1,0:T(8,128)(2,1)} %collective-permute-done.10), kind=kLoop, calls=%fused_computation.49 | loop fusion | bytes 425984
  51.9 1.6 %bitcast_dynamic-update-slice_fusion.4 = bf16[8,4,97,256]{3,2,1,0:T(8,128)(2,1)} fusion(bf16[8,4,97,256]{3,2,1,0:T(8,128)(2,1)} %bitcast_dynamic-update-slice_fusion.5, bf16[4,97,256]{2,1,0:T(8,128)(2,1)} %collective-permute-done.11), kind=kLoop, calls=%fused_computation.48 | loop fusion | bytes 425984
  54.0 1.6 %bitcast_dynamic-update-slice_fusion.3 = bf16[8,4,97,256]{3,2,1,0:T(8,128)(2,1)} fusion(bf16[8,4,97,256]{3,2,1,0:T(8,128)(2,1)} %bitcast_dynamic-update-slice_fusion.4, bf16[4,97,256]{2,1,0:T(8,128)(2,1)} %collective-permute-done.12), kind=kLoop, calls=%fused_computation.47 | loop fusion | bytes 425984
  55.7 2.0 %collective-permute-start.6 = (bf16[48,1024]{1,0:T(8,128)(2,1)S(1)}, bf16[48,1024]{1,0:T(8,128)(2,1)S(1)}, u32[]{:S(2)}, u32[]{:S(2)}) collective-permute-start(bf16[48,1024]{1,0:T(8,128)(2,1)S(1)} %divide_convert_fusion), channel_id=1, source_target_pairs={{0,1},{1,2},{2,3},{3,0},{4,5},{5,6},{6,7},{7,4},{8,9},{9,10},{10,1... | collective-permute-start | bytes 294920 | tf_op jit(solution)/shard_map/ppermute | solution.py:96
  57.7 1.6 %bitcast_dynamic-update-slice_fusion.2 = bf16[8,4,97,256]{3,2,1,0:T(8,128)(2,1)} fusion(bf16[8,4,97,256]{3,2,1,0:T(8,128)(2,1)} %bitcast_dynamic-update-slice_fusion.3, bf16[4,97,256]{2,1,0:T(8,128)(2,1)} %collective-permute-done.13), kind=kLoop, calls=%fused_computation.46 | loop fusion | bytes 425984
  60.7 3.3 %gather_fusion.3 = bf16[8,4,97,256]{3,2,1,0:T(8,128)(2,1)} fusion(bf16[8,4,97,256]{3,2,1,0:T(8,128)(2,1)} %bitcast_dynamic-update-slice_fusion, s32[1024]{0:T(1024)S(1)} %pad_clamp_fusion.2), kind=kCustom, calls=%fused_computation.3 | custom fusion | bytes 3178528 | tf_op jit(solution)/shard_map/jit(_take)/gather | solution.py:100
  64.0 2.9 %broadcast_select_fusion = bf16[8,4,97,256]{3,2,1,0:T(8,128)(2,1)} fusion(bf16[8,4,97,256]{3,2,1,0:T(8,128)(2,1)} %gather_fusion.3, pred[8]{0:T(512)(128)(4,1)S(1)} %compare_and_fusion.2), kind=kLoop, calls=%fused_computation.21 | loop fusion | flops 794624 | bytes 3178504 | tf_op jit(solution)/shard_map/jit(_take)/select_n | solution.py:100
  67.5 0.9 pad_maximum_fusion.1
  69.2 1.5 %slice_bitcast_fusion = (bf16[8,48,4,256]{3,1,2,0:T(8,128)(2,1)S(1)}, bf16[8,48,4,256]{3,1,2,0:T(8,128)(2,1)S(1)}) fusion(bf16[8,4,97,256]{3,2,1,0:T(8,128)(2,1)} %broadcast_select_fusion), kind=kLoop, calls=%fused_computation.31 | loop fusion | bytes 3145728 | tf_op jit(solution)/shard_map/transpose | solution.py:183
  70.7 0.9 slice_convert_fusion
  72.0 1.0 copy.32
  73.9 1.7 %fusion.43 = (f32[384]{0:T(512)S(1)}, f32[384,384]{0,1:T(8,128)S(1)}) fusion(bf16[384,1024]{1,0:T(8,128)(2,1)} %bitcast.109, bf16[384,1024]{1,0:T(8,128)(2,1)S(1)} %bitcast.105), kind=kOutput, calls=%fused_computation.161 | convolution fusion | flops 302284416 | bytes 2164224 | tf_op jit(solution)/shard_map/dot_general | solution.py:192
  76.6 1.8 %convolution_multiply_fusion = f32[384,1024]{1,0:T(8,128)} fusion(bf16[384,384]{0,1:T(8,128)(2,1)S(1)} %subtract_convert_fusion, bf16[384,1024]{1,0:T(8,128)(2,1)S(1)} %bitcast.106), kind=kOutput, calls=%fused_computation.22 | convolution fusion | flops 302383104 | bytes 2654208 | tf_op jit(solution)/shard_map/dot_general | solution.py:204
  79.1 4.8 %all-to-all-start = ((bf16[8,48,512]{2,1,0:T(8,128)(2,1)}), bf16[8,48,512]{2,1,0:T(8,128)(2,1)S(1)}, u32[]{:S(2)}, u32[]{:S(2)}) async-start(bf16[8,48,512]{2,1,0:T(8,128)(2,1)} %bitcast.96), calls=%async_computation | async-start | bytes 786432 | tf_op jit(solution)/shard_map/all_to_all | solution.py:179
  84.6 1.4 %dynamic_slice.23 = f32[48,256]{1,0:T(8,128)} dynamic-slice(f32[384,1024]{1,0:T(8,128)} %convolution_multiply_fusion, s32[]{:T(128)S(6)} %select_n.278, s32[]{:T(128)S(6)} %select_n.279), dynamic_slice_sizes={48,256} | dynamic-slice | bytes 98308 | tf_op jit(solution)/shard_map/dynamic_slice | solution.py:205
  86.0 1.7 %convolution_multiply_fusion.2 = f32[48,256]{1,0:T(8,128)} fusion(bf16[384,1024]{1,0:T(8,128)(2,1)} %bitcast.110, s32[]{:T(128)S(6)} %select_n.279, bf16[384,384]{0,1:T(8,128)(2,1)} %copy-done.2, s32[]{:T(128)S(6)} %select_n.278), kind=kOutput, calls=%fused_computation.24 | convolution fusion | flops 9449472 | bytes 282632 | tf_op jit(solution)/shard_map/dot_general | solution.py:212
  87.7 2.4 %fusion.20 = f32[48,1024]{1,0:T(8,128)} fusion(bf16[1024,1024]{1,0:T(8,128)(2,1)S(1)} %copy-done, f32[384,1024]{1,0:T(8,128)} %convolution_multiply_fusion, s32[]{:T(128)S(6)} %select_n.278), kind=kOutput, calls=%fused_computation.66 | convolution fusion | flops 100663296 | bytes 2392068 | tf_op jit(solution)/shard_map/dot_general | solution.py:216
  90.2 2.1 %all-to-all-done = bf16[8,48,512]{2,1,0:T(8,128)(2,1)S(1)} async-done(((bf16[8,48,512]{2,1,0:T(8,128)(2,1)}), bf16[8,48,512]{2,1,0:T(8,128)(2,1)S(1)}, u32[]{:S(2)}, u32[]{:S(2)}) %all-to-all-start) | async-done | bytes 393248 | tf_op jit(solution)/shard_map/all_to_all | solution.py:179
  92.3 18.5 %all_gather.3 = f32[48,4096]{1,0:T(8,128)S(1)} all-gather(f32[48,1024]{1,0:T(8,128)} %fusion.20), channel_id=1, replica_groups=mesh['dp'=8,'fsdp'=4] {'fsdp'}, dimensions={1}, use_global_device_ids=true | all-gather | bytes 983040 | tf_op jit(solution)/shard_map/all_gather | solution.py:223
  110.8 2.3 %fusion.8 = (f32[4096]{0:T(1024)S(1)}, f32[128]{0:T(128)S(1)}, f32[128,4096]{1,0:T(8,128)S(1)}) fusion(bf16[128,4096]{1,0:T(8,128)(2,1)S(1)} %copy-done.1, f32[128]{0:T(128)} %copy-done.10, f32[4096]{0:T(1024)S(1)} %convert_element_type.77, f32[48,4096]{1,0:T(8,128)S(1)} %all_gather.3, f32[48]{0:T(128)} %copy-done.8, s32[128]{0:T(128)} %bitcast.134), kind=kOutput, calls=%fused_computation.20 | convolution fusion | flops 305858432 | bytes 3966656 | tf_op jit(solution)/shard_map/dot_general | solution.py:225
  113.2 1.6 %fusion.5 = bf16[128,4096]{1,0:T(8,128)(2,1)} fusion(bf16[128,4096]{1,0:T(8,128)(2,1)S(1)} %copy-done.1, f32[128,4096]{1,0:T(8,128)S(1)} %get-tuple-element.32, f32[128]{0:T(128)S(1)} %broadcast_multiply_fusion, f32[128]{0:T(128)S(1)} %copy-done.9, f32[4096]{0:T(1024)S(1)} %convert_element_type.77, f32[128]{0:T(128)S(1)} %copy-done.11), kind=kLoop, calls=%fused_computation.17 | loop fusion | flops 3670016 | bytes 4212224 | tf_op jit(solution)/shard_map/convert_element_type | solution.py:235
  116.4 1.1 collective-permute-start.19
  117.5 1.2 collective-permute-start.18
  120.3 1.1 collective-permute-done.18
  121.4 2.1 %collective-permute-done.17 = f32[2,4096]{1,0:T(2,128)S(1)} collective-permute-done((f32[2,4096]{1,0:T(2,128)S(1)}, f32[2,4096]{1,0:T(2,128)S(1)}, u32[]{:S(2)}, u32[]{:S(2)}) %collective-permute-start.17) | collective-permute-done | bytes 32800 | tf_op jit(solution)/shard_map/ppermute | solution.py:113
  125.1 2.0 %collective-permute-start.22 = (f32[4096]{0:T(1024)S(1)}, f32[4096]{0:T(1024)S(1)}, u32[]{:S(2)}, u32[]{:S(2)}) collective-permute-start(f32[4096]{0:T(1024)S(1)} %select_reduce_fusion.2), channel_id=1, source_target_pairs={{0,3},{1,0},{2,1},{3,2},{4,7},{5,4},{6,5},{7,6},{8,11},{9,8},{10,9... | collective-permute-start | bytes 49160 | tf_op jit(solution)/shard_map/ppermute | solution.py:96
  127.1 0.9 collective-permute-start.20
  128.0 2.1 %fusion.17 = f32[512,256]{1,0:T(8,128)} fusion(bf16[384,512]{1,0:T(8,128)(2,1)S(1)} %bitcast.108, f32[384,1024]{1,0:T(8,128)} %convolution_multiply_fusion, s32[]{:T(128)S(6)} %select_n.279), kind=kOutput, calls=%fused_computation.54 | convolution fusion | flops 100663296 | bytes 1114116 | tf_op jit(solution)/shard_map/dot_general | solution.py:220
  130.2 1.6 %collective-permute-done.21 = f32[4096]{0:T(1024)S(1)} collective-permute-done((f32[4096]{0:T(1024)S(1)}, f32[4096]{0:T(1024)S(1)}, u32[]{:S(2)}, u32[]{:S(2)}) %collective-permute-start.21) | collective-permute-done | bytes 16416 | tf_op jit(solution)/shard_map/ppermute | solution.py:96
  131.7 0.9 collective-permute-done.20
  (110 shorter events, 23.4 us)
Async XLA Ops:
  0.6 87.1 %copy-start = (bf16[1024,1024]{1,0:T(8,128)(2,1)S(1)}, bf16[1024,1024]{1,0:T(8,128)(2,1)}, u32[]{:S(2)}) copy-start(bf16[1024,1024]{1,0:T(8,128)(2,1)} %param.13) | copy-start | bytes 6291460
  3.7 22.7 %collective-permute-start.5 = (bf16[97,256]{1,0:T(8,128)(2,1)S(1)}, bf16[97,256]{1,0:T(8,128)(2,1)S(1)}, u32[]{:S(2)}, u32[]{:S(2)}) collective-permute-start(bf16[97,256]{1,0:T(8,128)(2,1)S(1)} %constant_dynamic-update-slice_fusion), channel_id=1, source_target_pairs={{0,3},{1,0},{2,1},{3,2},{4,7},{5,4},{6,5},{7,6},{8,11},{9,8},{10,9... | collective-permute-start | bytes 149000 | tf_op jit(solution)/shard_map/ppermute | solution.py:96
  8.8 17.7 %collective-permute-start.4 = (bf16[97,256]{1,0:T(8,128)(2,1)S(1)}, bf16[97,256]{1,0:T(8,128)(2,1)S(1)}, u32[]{:S(2)}, u32[]{:S(2)}) collective-permute-start(bf16[97,256]{1,0:T(8,128)(2,1)S(1)} %constant_dynamic-update-slice_fusion), channel_id=1, source_target_pairs={{0,2},{1,3},{2,0},{3,1},{4,6},{5,7},{6,4},{7,5},{8,10},{9,11},{10,... | collective-permute-start | bytes 149000 | tf_op jit(solution)/shard_map/ppermute | solution.py:96
  8.8 17.7 %collective-permute-start.3 = (bf16[97,256]{1,0:T(8,128)(2,1)S(1)}, bf16[97,256]{1,0:T(8,128)(2,1)S(1)}, u32[]{:S(2)}, u32[]{:S(2)}) collective-permute-start(bf16[97,256]{1,0:T(8,128)(2,1)S(1)} %constant_dynamic-update-slice_fusion), channel_id=1, source_target_pairs={{0,1},{1,2},{2,3},{3,0},{4,5},{5,6},{6,7},{7,4},{8,9},{9,10},{10,1... | collective-permute-start | bytes 149000 | tf_op jit(solution)/shard_map/ppermute | solution.py:96
  12.6 4.3 %copy-start.10 = (f32[128]{0:T(128)}, f32[128]{0:T(128)S(1)}, u32[]{:S(2)}) copy-start(f32[128]{0:T(128)S(1)} %get-tuple-element.27) | copy-start | bytes 1540
  18.5 11.3 %collective-permute-start.2 = (f32[48,1024]{1,0:T(8,128)}, f32[48,1024]{1,0:T(8,128)S(1)}, u32[]{:S(2)}, u32[]{:S(2)}) collective-permute-start(f32[48,1024]{1,0:T(8,128)} %bitcast.97), channel_id=1, source_target_pairs={{0,3},{1,0},{2,1},{3,2},{4,7},{5,4},{6,5},{7,6},{8,11},{9,8},{10,9... | collective-permute-start | bytes 589832 | tf_op jit(solution)/shard_map/ppermute | solution.py:129
  22.0 17.1 %collective-permute-start.1 = (f32[48,1024]{1,0:T(8,128)}, f32[48,1024]{1,0:T(8,128)}, u32[]{:S(2)}, u32[]{:S(2)}) collective-permute-start(f32[48,1024]{1,0:T(8,128)} %bitcast.98), channel_id=1, source_target_pairs={{0,2},{1,3},{2,0},{3,1},{4,6},{5,7},{6,4},{7,5},{8,10},{9,11},{10,... | collective-permute-start | bytes 589832 | tf_op jit(solution)/shard_map/ppermute | solution.py:129
  23.7 45.3 %copy-start.5 = (pred[4]{0:T(512)(128)(4,1)}, pred[4]{0:T(512)(128)(4,1)S(1)}, u32[]{:S(2)}) copy-start(pred[4]{0:T(512)(128)(4,1)S(1)} %get-tuple-element.34) | copy-start | bytes 16
  23.7 44.7 %copy-start.7 = (s32[1024]{0:T(1024)}, s32[1024]{0:T(1024)S(1)}, u32[]{:S(2)}) copy-start(s32[1024]{0:T(1024)S(1)} %pad_clamp_fusion.3) | copy-start | bytes 12292
  26.4 14.3 %collective-permute-start = (f32[48,1024]{1,0:T(8,128)}, f32[48,1024]{1,0:T(8,128)S(1)}, u32[]{:S(2)}, u32[]{:S(2)}) collective-permute-start(f32[48,1024]{1,0:T(8,128)} %bitcast.99), channel_id=1, source_target_pairs={{0,1},{1,2},{2,3},{3,0},{4,5},{5,6},{6,7},{7,4},{8,9},{9,10},{10,1... | collective-permute-start | bytes 589832 | tf_op jit(solution)/shard_map/ppermute | solution.py:129
  27.2 17.5 %collective-permute-start.9 = (bf16[4,97,256]{2,1,0:T(8,128)(2,1)S(1)}, bf16[4,97,256]{2,1,0:T(8,128)(2,1)}, u32[]{:S(2)}, u32[]{:S(2)}) collective-permute-start(bf16[4,97,256]{2,1,0:T(8,128)(2,1)S(1)} %broadcast_select_fusion.1), channel_id=1, source_target_pairs={{0,4},{4,8},{8,12},{12,16},{16,20},{20,24},{24,28},{28,0},{1,5},{5... | collective-permute-start | bytes 595976 | tf_op jit(solution)/shard_map/ppermute | solution.py:96
  27.2 20.6 %collective-permute-start.10 = (bf16[4,97,256]{2,1,0:T(8,128)(2,1)S(1)}, bf16[4,97,256]{2,1,0:T(8,128)(2,1)}, u32[]{:S(2)}, u32[]{:S(2)}) collective-permute-start(bf16[4,97,256]{2,1,0:T(8,128)(2,1)S(1)} %broadcast_select_fusion.1), channel_id=1, source_target_pairs={{0,8},{4,12},{8,16},{12,20},{16,24},{20,28},{24,0},{28,4},{1,9},{5... | collective-permute-start | bytes 595976 | tf_op jit(solution)/shard_map/ppermute | solution.py:96
  29.0 15.6 %copy-start.8 = (f32[48]{0:T(128)}, f32[48]{0:T(128)S(1)}, u32[]{:S(2)}) copy-start(f32[48]{0:T(128)S(1)} %convert_reduce_fusion) | copy-start | bytes 580
  29.8 10.9 %copy-start.3 = (f32[48,1024]{1,0:T(8,128)}, f32[48,1024]{1,0:T(8,128)S(1)}, u32[]{:S(2)}) copy-start(f32[48,1024]{1,0:T(8,128)S(1)} %collective-permute-done.2) | copy-start | bytes 589828
  29.8 22.1 %collective-permute-start.11 = (bf16[4,97,256]{2,1,0:T(8,128)(2,1)S(1)}, bf16[4,97,256]{2,1,0:T(8,128)(2,1)}, u32[]{:S(2)}, u32[]{:S(2)}) collective-permute-start(bf16[4,97,256]{2,1,0:T(8,128)(2,1)S(1)} %broadcast_select_fusion.1), channel_id=1, source_target_pairs={{0,12},{4,16},{8,20},{12,24},{16,28},{20,0},{24,4},{28,8},{1,13},{... | collective-permute-start | bytes 595976 | tf_op jit(solution)/shard_map/ppermute | solution.py:96
  39.1 14.4 %collective-permute-start.12 = (bf16[4,97,256]{2,1,0:T(8,128)(2,1)S(1)}, bf16[4,97,256]{2,1,0:T(8,128)(2,1)}, u32[]{:S(2)}, u32[]{:S(2)}) collective-permute-start(bf16[4,97,256]{2,1,0:T(8,128)(2,1)S(1)} %broadcast_select_fusion.1), channel_id=1, source_target_pairs={{0,16},{4,20},{8,24},{12,28},{16,0},{20,4},{24,8},{28,12},{1,17},{... | collective-permute-start | bytes 595976 | tf_op jit(solution)/shard_map/ppermute | solution.py:96
  40.6 15.0 %collective-permute-start.13 = (bf16[4,97,256]{2,1,0:T(8,128)(2,1)S(1)}, bf16[4,97,256]{2,1,0:T(8,128)(2,1)}, u32[]{:S(2)}, u32[]{:S(2)}) collective-permute-start(bf16[4,97,256]{2,1,0:T(8,128)(2,1)S(1)} %broadcast_select_fusion.1), channel_id=1, source_target_pairs={{0,20},{4,24},{8,28},{12,0},{16,4},{20,8},{24,12},{28,16},{1,21},{... | collective-permute-start | bytes 595976 | tf_op jit(solution)/shard_map/ppermute | solution.py:96
  44.7 14.6 %collective-permute-start.14 = (bf16[4,97,256]{2,1,0:T(8,128)(2,1)S(1)}, bf16[4,97,256]{2,1,0:T(8,128)(2,1)S(1)}, u32[]{:S(2)}, u32[]{:S(2)}) collective-permute-start(bf16[4,97,256]{2,1,0:T(8,128)(2,1)S(1)} %broadcast_select_fusion.1), channel_id=1, source_target_pairs={{0,24},{4,28},{8,0},{12,4},{16,8},{20,12},{24,16},{28,20},{1,25},{... | collective-permute-start | bytes 595976 | tf_op jit(solution)/shard_map/ppermute | solution.py:96
  47.8 12.2 %collective-permute-start.15 = (bf16[4,97,256]{2,1,0:T(8,128)(2,1)S(1)}, bf16[4,97,256]{2,1,0:T(8,128)(2,1)S(1)}, u32[]{:S(2)}, u32[]{:S(2)}) collective-permute-start(bf16[4,97,256]{2,1,0:T(8,128)(2,1)S(1)} %broadcast_select_fusion.1), channel_id=1, source_target_pairs={{0,28},{4,0},{8,4},{12,8},{16,12},{20,16},{24,20},{28,24},{1,29},{... | collective-permute-start | bytes 595976 | tf_op jit(solution)/shard_map/ppermute | solution.py:96
  51.9 15.0 %collective-permute-start.8 = (bf16[48,1024]{1,0:T(8,128)(2,1)S(1)}, bf16[48,1024]{1,0:T(8,128)(2,1)S(1)}, u32[]{:S(2)}, u32[]{:S(2)}) collective-permute-start(bf16[48,1024]{1,0:T(8,128)(2,1)S(1)} %divide_convert_fusion), channel_id=1, source_target_pairs={{0,3},{1,0},{2,1},{3,2},{4,7},{5,4},{6,5},{7,6},{8,11},{9,8},{10,9... | collective-permute-start | bytes 294920 | tf_op jit(solution)/shard_map/ppermute | solution.py:96
  53.5 13.4 %collective-permute-start.7 = (bf16[48,1024]{1,0:T(8,128)(2,1)S(1)}, bf16[48,1024]{1,0:T(8,128)(2,1)S(1)}, u32[]{:S(2)}, u32[]{:S(2)}) collective-permute-start(bf16[48,1024]{1,0:T(8,128)(2,1)S(1)} %divide_convert_fusion), channel_id=1, source_target_pairs={{0,2},{1,3},{2,0},{3,1},{4,6},{5,7},{6,4},{7,5},{8,10},{9,11},{10,... | collective-permute-start | bytes 294920 | tf_op jit(solution)/shard_map/ppermute | solution.py:96
  55.7 11.2 %collective-permute-start.6 = (bf16[48,1024]{1,0:T(8,128)(2,1)S(1)}, bf16[48,1024]{1,0:T(8,128)(2,1)S(1)}, u32[]{:S(2)}, u32[]{:S(2)}) collective-permute-start(bf16[48,1024]{1,0:T(8,128)(2,1)S(1)} %divide_convert_fusion), channel_id=1, source_target_pairs={{0,1},{1,2},{2,3},{3,0},{4,5},{5,6},{6,7},{7,4},{8,9},{9,10},{10,1... | collective-permute-start | bytes 294920 | tf_op jit(solution)/shard_map/ppermute | solution.py:96
  66.9 0.6 copy-start.4
  76.5 2.6 %copy-start.2 = (bf16[384,384]{0,1:T(8,128)(2,1)}, bf16[384,384]{0,1:T(8,128)(2,1)S(1)}, u32[]{:S(2)}) copy-start(bf16[384,384]{0,1:T(8,128)(2,1)S(1)} %subtract_convert_fusion) | copy-start | bytes 884740
  79.1 13.2 %all-to-all-start = ((bf16[8,48,512]{2,1,0:T(8,128)(2,1)}), bf16[8,48,512]{2,1,0:T(8,128)(2,1)S(1)}, u32[]{:S(2)}, u32[]{:S(2)}) async-start(bf16[8,48,512]{2,1,0:T(8,128)(2,1)} %bitcast.96), calls=%async_computation | async-start | bytes 786432 | tf_op jit(solution)/shard_map/all_to_all | solution.py:179
  87.7 23.1 %copy-start.1 = (bf16[128,4096]{1,0:T(8,128)(2,1)S(1)}, bf16[128,4096]{1,0:T(8,128)(2,1)}, u32[]{:S(2)}) copy-start(bf16[128,4096]{1,0:T(8,128)(2,1)} %param.10) | copy-start | bytes 3145732
  110.8 2.4 %copy-start.9 = (f32[128]{0:T(128)S(1)}, f32[128]{0:T(128)}, u32[]{:S(2)}) copy-start(f32[128]{0:T(128)} %get-tuple-element.26) | copy-start | bytes 1540
  110.8 2.4 %copy-start.11 = (f32[128]{0:T(128)S(1)}, f32[128]{0:T(128)}, u32[]{:S(2)}) copy-start(f32[128]{0:T(128)} %copy-done.10) | copy-start | bytes 1540
  113.1 1.7 %collective-permute-start.16 = (f32[4096]{0:T(1024)S(1)}, f32[4096]{0:T(1024)S(1)}, u32[]{:S(2)}, u32[]{:S(2)}) collective-permute-start(f32[4096]{0:T(1024)S(1)} %get-tuple-element.14), channel_id=1, source_target_pairs={{0,4},{4,0},{8,12},{12,8},{16,20},{20,16},{24,28},{28,24},{1,5},{5... | collective-permute-start | bytes 49160 | tf_op jit(solution)/shard_map/ppermute | solution.py:108
  114.9 18.6 %copy-start.6 = (pred[4]{0:T(512)(128)(4,1)S(1)}, pred[4]{0:T(512)(128)(4,1)}, u32[]{:S(2)}) copy-start(pred[4]{0:T(512)(128)(4,1)} %copy-done.5) | copy-start | bytes 16
  116.4 4.0 %collective-permute-start.19 = (f32[2,4096]{1,0:T(2,128)S(1)}, f32[2,4096]{1,0:T(2,128)S(1)}, u32[]{:S(2)}, u32[]{:S(2)}) collective-permute-start(f32[2,4096]{1,0:T(2,128)S(1)} %broadcast_select_fusion.2), channel_id=1, source_target_pairs={{0,24},{4,28},{8,0},{12,4},{16,8},{20,12},{24,16},{28,20},{1,25},{... | collective-permute-start | bytes 98312 | tf_op jit(solution)/shard_map/ppermute | solution.py:113
  117.5 3.9 %collective-permute-start.18 = (f32[2,4096]{1,0:T(2,128)S(1)}, f32[2,4096]{1,0:T(2,128)S(1)}, u32[]{:S(2)}, u32[]{:S(2)}) collective-permute-start(f32[2,4096]{1,0:T(2,128)S(1)} %broadcast_select_fusion.2), channel_id=1, source_target_pairs={{0,16},{4,20},{8,24},{12,28},{16,0},{20,4},{24,8},{28,12},{1,17},{... | collective-permute-start | bytes 98312 | tf_op jit(solution)/shard_map/ppermute | solution.py:113
  118.7 4.8 %collective-permute-start.17 = (f32[2,4096]{1,0:T(2,128)S(1)}, f32[2,4096]{1,0:T(2,128)S(1)}, u32[]{:S(2)}, u32[]{:S(2)}) collective-permute-start(f32[2,4096]{1,0:T(2,128)S(1)} %broadcast_select_fusion.2), channel_id=1, source_target_pairs={{0,8},{4,12},{8,16},{12,20},{16,24},{20,28},{24,0},{28,4},{1,9},{5... | collective-permute-start | bytes 98312 | tf_op jit(solution)/shard_map/ppermute | solution.py:113
  125.1 5.0 %collective-permute-start.22 = (f32[4096]{0:T(1024)S(1)}, f32[4096]{0:T(1024)S(1)}, u32[]{:S(2)}, u32[]{:S(2)}) collective-permute-start(f32[4096]{0:T(1024)S(1)} %select_reduce_fusion.2), channel_id=1, source_target_pairs={{0,3},{1,0},{2,1},{3,2},{4,7},{5,4},{6,5},{7,6},{8,11},{9,8},{10,9... | collective-permute-start | bytes 49160 | tf_op jit(solution)/shard_map/ppermute | solution.py:96
  127.1 4.6 %collective-permute-start.21 = (f32[4096]{0:T(1024)S(1)}, f32[4096]{0:T(1024)S(1)}, u32[]{:S(2)}, u32[]{:S(2)}) collective-permute-start(f32[4096]{0:T(1024)S(1)} %select_reduce_fusion.2), channel_id=1, source_target_pairs={{0,2},{1,3},{2,0},{3,1},{4,6},{5,7},{6,4},{7,5},{8,10},{9,11},{10,... | collective-permute-start | bytes 49160 | tf_op jit(solution)/shard_map/ppermute | solution.py:96
  127.1 5.5 %collective-permute-start.20 = (f32[4096]{0:T(1024)S(1)}, f32[4096]{0:T(1024)S(1)}, u32[]{:S(2)}, u32[]{:S(2)}) collective-permute-start(f32[4096]{0:T(1024)S(1)} %select_reduce_fusion.2), channel_id=1, source_target_pairs={{0,1},{1,2},{2,3},{3,0},{4,5},{5,6},{6,7},{7,4},{8,9},{9,10},{10,1... | collective-permute-start | bytes 49160 | tf_op jit(solution)/shard_map/ppermute | solution.py:96

commit v10 on v3

--- a/solution.py
+++ b/solution.py
@@ -115,6 +115,25 @@
     return jnp.sum(jnp.take(jnp.stack(copies), order, axis=0), axis=0)
 
 
+def spread_with_sum(total, pieces, axis):
+    n = lax.axis_size(axis)
+    me = lax.axis_index(axis)
+    size = total.shape[0]
+    sums = [total]
+    got = [lax.dynamic_index_in_dim(pieces, me, axis=0, keepdims=False)]
+    for s in range(1, n):
+        piece = lax.dynamic_index_in_dim(pieces, (me + s) % n, axis=0, keepdims=False)
+        payload = jnp.concatenate([total, piece.reshape(-1)])
+        arrived = lax.ppermute(payload, axis, [(i, (i + s) % n) for i in range(n)])
+        sums.append(arrived[:size])
+        got.append(arrived[size:].reshape(piece.shape))
+    order = (me - jnp.arange(n)) % n
+    return (
+        jnp.sum(jnp.take(jnp.stack(sums), order, axis=0), axis=0),
+        jnp.take(jnp.stack(got), order, axis=0),
+    )
+
+
 def local_small(query_cache, region_cache, positive, hidden_states, segment_ids, norm_gain, proj_weight):
     rows, width = query_cache.shape
     data_count = lax.axis_size("dp")
@@ -160,8 +179,6 @@
     mean_pooled, gathered = lax.optimization_barrier((mean_pooled, gathered))
     slice_width = model_width // data_count
     pieces = mean_pooled.reshape(rows, data_count, slice_width).transpose(1, 0, 2)
-    pieces = lax.all_to_all(pieces, "dp", 0, 0, tiled=True)
-    pooled_cols = pieces.reshape(pair_count, slice_width)
 
     query_all = gathered[:, :, :rows].transpose(0, 2, 1, 3).reshape(pair_count, feature_count * width)
     region_all = gathered[:, :, rows : 2 * rows].transpose(0, 2, 1, 3).reshape(
@@ -200,10 +217,6 @@
     mean_part = lax.dot_general(
         grad_low, proj_weight, contract_last, preferred_element_type=jnp.float32
     )
-    mean_part, pooled_cols = lax.optimization_barrier((mean_part, pooled_cols))
-    proj_grad = lax.dot_general(
-        pooled_cols, grad_low_cols, contract_first, preferred_element_type=jnp.float32
-    )
     mean_grad = lax.all_gather(mean_part, "fsdp", axis=1, tiled=True)
     pool_grad = mean_grad / counts[:, None]
     normed_grad = lax.dot_general(
@@ -217,7 +230,12 @@
     scaled = gain * normed_grad
     inner = jnp.mean(scaled * states, axis=1, keepdims=True)
     hidden_grad = (inv_rms * scaled - states * inv_rms**3 * inner).astype(jnp.bfloat16)
-    gain_grad = sum_blocks(sum_blocks(gain_part, "dp"), "fsdp")
+    gain_dp, pieces = spread_with_sum(gain_part, pieces.astype(jnp.float32), "dp")
+    gain_grad = sum_blocks(gain_dp, "fsdp")
+    pooled_cols = pieces.reshape(pair_count, slice_width).astype(jnp.bfloat16)
+    proj_grad = lax.dot_general(
+        pooled_cols, grad_low_cols, contract_first, preferred_element_type=jnp.float32
+    )
     return (mean_loss, query_grad, region_grad, hidden_grad, gain_grad, proj_grad)
 
 

time: 137 us -> 129 us (0.942)
  local copies, waits for them, and re-layouts: 30.4 us -> 37.2 us
  waiting for transfers between devices: 14.3 us -> 9.21 us
  starting transfers between devices: 38 us -> 33.1 us
  matrix products: 14.7 us -> 11.2 us
    ppermute x0 -> x7, starting transfers between devices: none -> 8.26 us  [spread_with_sum(): arrived = lax.ppermute(payload, axis, [(i, (i + s) % n) for i in range(n)])]
    ppermute x23 -> x16, starting transfers between devices: 28.2 us -> 20.9 us  [gather_blocks(): lax.ppermute(x, axis, [(i, (i + s) % n) for i in range(n)])]
    slice x0 -> x14, local copies, waits for them, and re-layouts: none -> 6.51 us  [the longest x7 3.62 us: spread_with_sum(): got.append(arrived[size:].reshape(piece.shape))]
    all_to_all x1 -> x0, starting transfers between devices: 5.81 us -> none  [local_small(): pieces = lax.all_to_all(pieces, 'dp', 0, 0, tiled=True)]
    ppermute x23 -> x16, waiting for transfers between devices: 2.87 us -> 0.04 us  [gather_blocks(): lax.ppermute(x, axis, [(i, (i + s) % n) for i in range(n)])]
    all_to_all x1 -> x0, waiting for transfers between devices: 2.09 us -> none  [local_small(): pieces = lax.all_to_all(pieces, 'dp', 0, 0, tiled=True)]
    dot_general x1, matrix products: 2.44 us -> 0.74 us  [local_small(): lax.dot_general(grad_low, proj_weight, contract_last, preferred_element_t...]
    unnamed x60 -> x38, local copies, waits for them, and re-layouts: 14.3 us -> 15.4 us
  transfers between devices with their start and end apart: 27 -> 26, of which waited for: 5 -> 1; matrix products, arithmetic and copies ran while one was open for 29% -> 35% of each run, Pallas kernels for 0% -> 0%
where the time goes in v10:
time: 129 us; the launch traced here: 128 us
  local copies, waits for them, and re-layouts  37.2 us (29%)
  starting transfers between devices  33.1 us (26%)
  blocking collectives  18.1 us (14%)
  other arithmetic  15.9 us (12%)
  matrix products  11.2 us (9%)
  waiting for transfers between devices  9.21 us (7%)
  between operations  3.06 us (2%)
    ppermute x16, starting transfers between devices, gather_blocks(): lax.ppermute(x, axis, [(i, (i + s) % n) for i in range(n)])  20.9 us
    all_gather x1, blocking collectives, local_small(): mean_grad = lax.all_gather(mean_part, 'fsdp', axis=1, tiled=True)  18.1 us
    unnamed x38, local copies, waits for them, and re-layouts  15.4 us
    ppermute x3, waiting for transfers between devices, scatter_sum(): lax.ppermute(piece, axis, [(i, (i + s) % n) for i in range(n)])  9.15 us
    ppermute x7, starting transfers between devices, spread_with_sum(): arrived = lax.ppermute(payload, axis, [(i, (i + s) % n) for i in range(n)])  8.26 us
    gather x4, local copies, waits for them, and re-layouts, gather_blocks(): return jnp.take(stack, order, axis=0)  5 us
    ppermute x3, starting transfers between devices, scatter_sum(): lax.ppermute(piece, axis, [(i, (i + s) % n) for i in range(n)])  3.99 us
    slice x7, local copies, waits for them, and re-layouts, spread_with_sum(): got.append(arrived[size:].reshape(piece.shape))  3.62 us
  transfers between devices with their start and end apart: 26, of which 1 were waited for; matrix products, arithmetic and copies ran while one was open for 35% of the time, Pallas kernels for 0%

profile of v10, /device:TPU:0, one launch (start us, length us, event | category | flops | bytes accessed | tf_op | source)
XLA Modules:
  0.0 127.8 jit_solution(12851066517247688018)
XLA Ops:
  0.6 0.9 constant_dynamic-update-slice_fusion.2
  3.7 5.1 %collective-permute-start.5 = (bf16[97,256]{1,0:T(8,128)(2,1)S(1)}, bf16[97,256]{1,0:T(8,128)(2,1)S(1)}, u32[]{:S(2)}, u32[]{:S(2)}) collective-permute-start(bf16[97,256]{1,0:T(8,128)(2,1)S(1)} %constant_dynamic-update-slice_fusion), channel_id=1, source_target_pairs={{0,3},{1,0},{2,1},{3,2},{4,7},{5,4},{6,5},{7,6},{8,11},{9,8},{10,9... | collective-permute-start | bytes 149000 | tf_op jit(solution)/shard_map/ppermute | solution.py:96
  8.8 1.0 collective-permute-start.3
  10.5 1.5 %fusion = f32[128]{0:T(128)S(1)} fusion(bf16[128,4096]{1,0:T(8,128)(2,1)} %param.10), kind=kLoop, calls=%fused_computation.12 | loop fusion | flops 1572736 | bytes 1049088 | tf_op jit(solution)/shard_map/reduce_sum | solution.py:165
  12.0 2.6 %fusion.9 = f32[48,4096]{1,0:T(8,128)} fusion(bf16[128,4096]{1,0:T(8,128)(2,1)} %param.10, f32[4096]{0:T(1024)S(1)} %convert_element_type.87, f32[128]{0:T(128)S(1)} %get-tuple-element.37, s32[128]{0:T(128)} %bitcast.151), kind=kOutput, calls=%fused_computation.25 | convolution fusion | flops 52434944 | bytes 1852416 | tf_op jit(solution)/shard_map/dot_general | solution.py:169
  14.6 1.7 %reshape.280 = f32[48,4,1024]{2,1,0:T(4,128)S(1)} reshape(f32[48,4096]{1,0:T(8,128)} %fusion.9) | data formatting | bytes 1572864 | tf_op jit(solution)/shard_map/reshape | solution.py:173
  16.3 0.8 constant_dynamic-slice_fusion.11
  17.9 2.8 %collective-permute-start.2 = (f32[48,1024]{1,0:T(8,128)}, f32[48,1024]{1,0:T(8,128)S(1)}, u32[]{:S(2)}, u32[]{:S(2)}) collective-permute-start(f32[48,1024]{1,0:T(8,128)} %bitcast.104), channel_id=1, source_target_pairs={{0,3},{1,0},{2,1},{3,2},{4,7},{5,4},{6,5},{7,6},{8,11},{9,8},{10,9... | collective-permute-start | bytes 589832 | tf_op jit(solution)/shard_map/ppermute | solution.py:113
  21.4 1.1 collective-permute-start.1
  24.5 1.5 %collective-permute-start.10 = (bf16[4,97,256]{2,1,0:T(8,128)(2,1)S(1)}, bf16[4,97,256]{2,1,0:T(8,128)(2,1)}, u32[]{:S(2)}, u32[]{:S(2)}) collective-permute-start(bf16[4,97,256]{2,1,0:T(8,128)(2,1)S(1)} %broadcast_select_fusion.1), channel_id=1, source_target_pairs={{0,8},{4,12},{8,16},{12,20},{16,24},{20,28},{24,0},{28,4},{1,9},{5... | collective-permute-start | bytes 595976 | tf_op jit(solution)/shard_map/ppermute | solution.py:96
  26.2 0.8 fusion.17
  27.0 2.4 %collective-permute-start.11 = (bf16[4,97,256]{2,1,0:T(8,128)(2,1)S(1)}, bf16[4,97,256]{2,1,0:T(8,128)(2,1)}, u32[]{:S(2)}, u32[]{:S(2)}) collective-permute-start(bf16[4,97,256]{2,1,0:T(8,128)(2,1)S(1)} %broadcast_select_fusion.1), channel_id=1, source_target_pairs={{0,12},{4,16},{8,20},{12,24},{16,28},{20,0},{24,4},{28,8},{1,13},{... | collective-permute-start | bytes 595976 | tf_op jit(solution)/shard_map/ppermute | solution.py:96
  29.4 9.1 %collective-permute-done.1 = f32[48,1024]{1,0:T(8,128)} collective-permute-done((f32[48,1024]{1,0:T(8,128)}, f32[48,1024]{1,0:T(8,128)}, u32[]{:S(2)}, u32[]{:S(2)}) %collective-permute-start.1) | collective-permute-done | bytes 196640 | tf_op jit(solution)/shard_map/ppermute | solution.py:113
  38.5 1.5 %collective-permute-start.12 = (bf16[4,97,256]{2,1,0:T(8,128)(2,1)S(1)}, bf16[4,97,256]{2,1,0:T(8,128)(2,1)}, u32[]{:S(2)}, u32[]{:S(2)}) collective-permute-start(bf16[4,97,256]{2,1,0:T(8,128)(2,1)S(1)} %broadcast_select_fusion.1), channel_id=1, source_target_pairs={{0,16},{4,20},{8,24},{12,28},{16,0},{20,4},{24,8},{28,12},{1,17},{... | collective-permute-start | bytes 595976 | tf_op jit(solution)/shard_map/ppermute | solution.py:96
  40.1 1.1 pad_maximum_fusion
  41.1 1.5 %gather_fusion = f32[4,48,1024]{2,1,0:T(8,128)} fusion(f32[4,48,1024]{2,1,0:T(8,128)S(1)} %pad_maximum_fusion, s32[1024]{0:T(1024)S(1)} %pad_clamp_fusion.1), kind=kCustom, calls=%fused_computation | custom fusion | bytes 1572880 | tf_op jit(solution)/shard_map/jit(_take)/gather | solution.py:115
  42.6 1.3 %select_reduce_fusion = f32[48,1024]{1,0:T(8,128)S(1)} fusion(f32[4,48,1024]{2,1,0:T(8,128)} %gather_fusion, pred[4]{0:T(512)(128)(4,1)S(1)} %compare_and_fusion.1), kind=kLoop, calls=%fused_computation.35 | loop fusion | flops 344064 | bytes 983044 | tf_op jit(solution)/shard_map/reduce_sum | solution.py:115
  44.1 1.5 %collective-permute-start.14 = (bf16[4,97,256]{2,1,0:T(8,128)(2,1)S(1)}, bf16[4,97,256]{2,1,0:T(8,128)(2,1)S(1)}, u32[]{:S(2)}, u32[]{:S(2)}) collective-permute-start(bf16[4,97,256]{2,1,0:T(8,128)(2,1)S(1)} %broadcast_select_fusion.1), channel_id=1, source_target_pairs={{0,24},{4,28},{8,0},{12,4},{16,8},{20,12},{24,16},{28,20},{1,25},{... | collective-permute-start | bytes 595976 | tf_op jit(solution)/shard_map/ppermute | solution.py:96
  45.6 1.6 %bitcast_dynamic-update-slice_fusion.6 = bf16[8,4,97,256]{3,2,1,0:T(8,128)(2,1)} fusion(bf16[8,4,97,256]{3,2,1,0:T(8,128)(2,1)} %fusion.17, bf16[4,97,256]{2,1,0:T(8,128)(2,1)} %collective-permute-done.9), kind=kLoop, calls=%fused_computation.58 | loop fusion | bytes 425984
  47.2 2.4 %collective-permute-start.15 = (bf16[4,97,256]{2,1,0:T(8,128)(2,1)S(1)}, bf16[4,97,256]{2,1,0:T(8,128)(2,1)S(1)}, u32[]{:S(2)}, u32[]{:S(2)}) collective-permute-start(bf16[4,97,256]{2,1,0:T(8,128)(2,1)S(1)} %broadcast_select_fusion.1), channel_id=1, source_target_pairs={{0,28},{4,0},{8,4},{12,8},{16,12},{20,16},{24,20},{28,24},{1,29},{... | collective-permute-start | bytes 595976 | tf_op jit(solution)/shard_map/ppermute | solution.py:96
  49.6 1.6 %bitcast_dynamic-update-slice_fusion.5 = bf16[8,4,97,256]{3,2,1,0:T(8,128)(2,1)} fusion(bf16[8,4,97,256]{3,2,1,0:T(8,128)(2,1)} %bitcast_dynamic-update-slice_fusion.6, bf16[4,97,256]{2,1,0:T(8,128)(2,1)} %collective-permute-done.10), kind=kLoop, calls=%fused_computation.57 | loop fusion | bytes 425984
  51.2 1.6 %bitcast_dynamic-update-slice_fusion.4 = bf16[8,4,97,256]{3,2,1,0:T(8,128)(2,1)} fusion(bf16[8,4,97,256]{3,2,1,0:T(8,128)(2,1)} %bitcast_dynamic-update-slice_fusion.5, bf16[4,97,256]{2,1,0:T(8,128)(2,1)} %collective-permute-done.11), kind=kLoop, calls=%fused_computation.56 | loop fusion | bytes 425984
  53.3 1.6 %bitcast_dynamic-update-slice_fusion.3 = bf16[8,4,97,256]{3,2,1,0:T(8,128)(2,1)} fusion(bf16[8,4,97,256]{3,2,1,0:T(8,128)(2,1)} %bitcast_dynamic-update-slice_fusion.4, bf16[4,97,256]{2,1,0:T(8,128)(2,1)} %collective-permute-done.12), kind=kLoop, calls=%fused_computation.55 | loop fusion | bytes 425984
  55.0 2.0 %collective-permute-start.6 = (bf16[48,1024]{1,0:T(8,128)(2,1)S(1)}, bf16[48,1024]{1,0:T(8,128)(2,1)S(1)}, u32[]{:S(2)}, u32[]{:S(2)}) collective-permute-start(bf16[48,1024]{1,0:T(8,128)(2,1)S(1)} %divide_convert_fusion), channel_id=1, source_target_pairs={{0,1},{1,2},{2,3},{3,0},{4,5},{5,6},{6,7},{7,4},{8,9},{9,10},{10,1... | collective-permute-start | bytes 294920 | tf_op jit(solution)/shard_map/ppermute | solution.py:96
  57.0 1.6 %bitcast_dynamic-update-slice_fusion.2 = bf16[8,4,97,256]{3,2,1,0:T(8,128)(2,1)} fusion(bf16[8,4,97,256]{3,2,1,0:T(8,128)(2,1)} %bitcast_dynamic-update-slice_fusion.3, bf16[4,97,256]{2,1,0:T(8,128)(2,1)} %collective-permute-done.13), kind=kLoop, calls=%fused_computation.54 | loop fusion | bytes 425984
  60.0 3.3 %gather_fusion.3 = bf16[8,4,97,256]{3,2,1,0:T(8,128)(2,1)} fusion(bf16[8,4,97,256]{3,2,1,0:T(8,128)(2,1)} %bitcast_dynamic-update-slice_fusion, s32[1024]{0:T(1024)S(1)} %pad_clamp_fusion), kind=kCustom, calls=%fused_computation.3 | custom fusion | bytes 3178528 | tf_op jit(solution)/shard_map/jit(_take)/gather | solution.py:100
  63.3 2.9 %broadcast_select_fusion = bf16[8,4,97,256]{3,2,1,0:T(8,128)(2,1)} fusion(bf16[8,4,97,256]{3,2,1,0:T(8,128)(2,1)} %gather_fusion.3, pred[8]{0:T(512)(128)(4,1)S(1)} %compare_and_fusion), kind=kLoop, calls=%fused_computation.21 | loop fusion | flops 794624 | bytes 3178504 | tf_op jit(solution)/shard_map/jit(_take)/select_n | solution.py:100
  66.8 0.9 pad_maximum_fusion.1
  68.5 1.5 %slice_bitcast_fusion = (bf16[8,48,4,256]{3,1,2,0:T(8,128)(2,1)S(1)}, bf16[8,48,4,256]{3,1,2,0:T(8,128)(2,1)S(1)}) fusion(bf16[8,4,97,256]{3,2,1,0:T(8,128)(2,1)} %broadcast_select_fusion), kind=kLoop, calls=%fused_computation.33 | loop fusion | bytes 3145728 | tf_op jit(solution)/shard_map/transpose | solution.py:184
  70.0 0.9 slice_convert_fusion
  71.3 1.1 copy.32
  73.1 1.7 %fusion.39 = (f32[384]{0:T(512)S(1)}, f32[384,384]{0,1:T(8,128)S(1)}) fusion(bf16[384,1024]{1,0:T(8,128)(2,1)} %bitcast.117, bf16[384,1024]{1,0:T(8,128)(2,1)S(1)} %bitcast.114), kind=kOutput, calls=%fused_computation.156 | convolution fusion | flops 302284416 | bytes 2164224 | tf_op jit(solution)/shard_map/dot_general | solution.py:193
  77.9 18.1 %all_gather.3 = f32[48,4096]{1,0:T(8,128)S(1)} all-gather(f32[48,1024]{1,0:T(8,128)S(1)} %fusion.21), channel_id=1, replica_groups=mesh['dp'=8,'fsdp'=4] {'fsdp'}, dimensions={1}, use_global_device_ids=true | all-gather | bytes 983040 | tf_op jit(solution)/shard_map/all_gather | solution.py:220
  96.1 1.6 %fusion.8 = (f32[4096]{0:T(1024)S(1)}, f32[128]{0:T(128)S(1)}, f32[128,4096]{1,0:T(8,128)S(1)}) fusion(bf16[128,4096]{1,0:T(8,128)(2,1)S(1)} %copy-done.1, f32[128]{0:T(128)S(1)} %get-tuple-element.37, f32[4096]{0:T(1024)S(1)} %convert_element_type.87, f32[48,4096]{1,0:T(8,128)S(1)} %all_gather.3, f32[48]{0:T(128)S(1)} %convert_reduce_fusion, ...), kind=kOutput, calls=%fused_computation.20 | convolution fusion | flops 305858432 | bytes 3966656 | tf_op jit(solution)/shard_map/dot_general | solution.py:222
  98.7 1.6 %collective-permute-start.17 = (f32[28672]{0:T(1024)S(1)}, f32[28672]{0:T(1024)S(1)}, u32[]{:S(2)}, u32[]{:S(2)}) collective-permute-start(f32[28672]{0:T(1024)S(1)} %get-tuple-element.30), channel_id=1, source_target_pairs={{0,8},{4,12},{8,16},{12,20},{16,24},{20,28},{24,0},{28,4},{1,9},{5... | collective-permute-start | bytes 344072 | tf_op jit(solution)/shard_map/ppermute | solution.py:127
  100.2 1.5 %collective-permute-start.18 = (f32[28672]{0:T(1024)S(1)}, f32[28672]{0:T(1024)}, u32[]{:S(2)}, u32[]{:S(2)}) collective-permute-start(f32[28672]{0:T(1024)S(1)} %get-tuple-element.31), channel_id=1, source_target_pairs={{0,12},{4,16},{8,20},{12,24},{16,28},{20,0},{24,4},{28,8},{1,13},{... | collective-permute-start | bytes 344072 | tf_op jit(solution)/shard_map/ppermute | solution.py:127
  101.7 1.3 %collective-permute-start.19 = (f32[28672]{0:T(1024)S(1)}, f32[28672]{0:T(1024)}, u32[]{:S(2)}, u32[]{:S(2)}) collective-permute-start(f32[28672]{0:T(1024)S(1)} %get-tuple-element.32), channel_id=1, source_target_pairs={{0,16},{4,20},{8,24},{12,28},{16,0},{20,4},{24,8},{28,12},{1,17},{... | collective-permute-start | bytes 344072 | tf_op jit(solution)/shard_map/ppermute | solution.py:127
  103.0 1.6 %fusion.5 = bf16[128,4096]{1,0:T(8,128)(2,1)} fusion(bf16[128,4096]{1,0:T(8,128)(2,1)S(1)} %copy-done.1, f32[128,4096]{1,0:T(8,128)S(1)} %get-tuple-element.42, f32[128]{0:T(128)S(1)} %broadcast_multiply_fusion, f32[128]{0:T(128)S(1)} %get-tuple-element.36, f32[4096]{0:T(1024)S(1)} %convert_element_type.87, f32[128]{0:T(128)S(1)} %get-tuple-element.37), kind=kLoop, calls=%fused_computation.17 | loop fusion | flops 3670016 | bytes 4212224 | tf_op jit(solution)/shard_map/convert_element_type | solution.py:232
  104.7 1.6 %collective-permute-start.21 = (f32[28672]{0:T(1024)S(1)}, f32[28672]{0:T(1024)S(1)}, u32[]{:S(2)}, u32[]{:S(2)}) collective-permute-start(f32[28672]{0:T(1024)S(1)} %get-tuple-element.34), channel_id=1, source_target_pairs={{0,24},{4,28},{8,0},{12,4},{16,8},{20,12},{24,16},{28,20},{1,25},{... | collective-permute-start | bytes 344072 | tf_op jit(solution)/shard_map/ppermute | solution.py:127
  106.3 2.3 %collective-permute-start.22 = (f32[28672]{0:T(1024)S(1)}, f32[28672]{0:T(1024)}, u32[]{:S(2)}, u32[]{:S(2)}) collective-permute-start(f32[28672]{0:T(1024)S(1)} %get-tuple-element.29), channel_id=1, source_target_pairs={{0,28},{4,0},{8,4},{12,8},{16,12},{20,16},{24,20},{28,24},{1,29},{... | collective-permute-start | bytes 344072 | tf_op jit(solution)/shard_map/ppermute | solution.py:127
  109.9 1.7 %convolution_multiply_fusion.2 = f32[48,256]{1,0:T(8,128)} fusion(bf16[384,1024]{1,0:T(8,128)(2,1)} %bitcast.118, s32[]{:T(128)S(6)} %select_n.257, bf16[384,384]{0,1:T(8,128)(2,1)} %copy-done.3, s32[]{:T(128)S(6)} %select_n.256), kind=kOutput, calls=%fused_computation.24 | convolution fusion | flops 9449472 | bytes 282632 | tf_op jit(solution)/shard_map/dot_general | solution.py:213
  115.5 1.9 %collective-permute-start.25 = (f32[4096]{0:T(1024)S(1)}, f32[4096]{0:T(1024)S(1)}, u32[]{:S(2)}, u32[]{:S(2)}) collective-permute-start(f32[4096]{0:T(1024)S(1)} %select_reduce_fusion.2), channel_id=1, source_target_pairs={{0,3},{1,0},{2,1},{3,2},{4,7},{5,4},{6,5},{7,6},{8,11},{9,8},{10,9... | collective-permute-start | bytes 49160 | tf_op jit(solution)/shard_map/ppermute | solution.py:96
  117.3 1.0 collective-permute-start.23
  118.5 0.9 slice.111
  119.4 0.9 slice.112
  120.4 0.9 slice.113
  121.4 0.9 slice.115
  123.2 2.1 %fusion.18 = f32[512,256]{1,0:T(8,128)} fusion(bf16[384,512]{1,0:T(8,128)(2,1)S(1)} %fusion.13, f32[384,1024]{1,0:T(8,128)} %copy-done.2, s32[]{:T(128)S(6)} %select_n.257), kind=kOutput, calls=%fused_computation.62 | convolution fusion | flops 100663296 | bytes 1114116 | tf_op jit(solution)/shard_map/dot_general | solution.py:236
  (131 shorter events, 21.8 us)
Async XLA Ops:
  0.6 76.5 %copy-start = (bf16[1024,1024]{1,0:T(8,128)(2,1)S(1)}, bf16[1024,1024]{1,0:T(8,128)(2,1)}, u32[]{:S(2)}) copy-start(bf16[1024,1024]{1,0:T(8,128)(2,1)} %param.13) | copy-start | bytes 6291460
  3.7 19.9 %collective-permute-start.5 = (bf16[97,256]{1,0:T(8,128)(2,1)S(1)}, bf16[97,256]{1,0:T(8,128)(2,1)S(1)}, u32[]{:S(2)}, u32[]{:S(2)}) collective-permute-start(bf16[97,256]{1,0:T(8,128)(2,1)S(1)} %constant_dynamic-update-slice_fusion), channel_id=1, source_target_pairs={{0,3},{1,0},{2,1},{3,2},{4,7},{5,4},{6,5},{7,6},{8,11},{9,8},{10,9... | collective-permute-start | bytes 149000 | tf_op jit(solution)/shard_map/ppermute | solution.py:96
  8.8 14.9 %collective-permute-start.4 = (bf16[97,256]{1,0:T(8,128)(2,1)S(1)}, bf16[97,256]{1,0:T(8,128)(2,1)S(1)}, u32[]{:S(2)}, u32[]{:S(2)}) collective-permute-start(bf16[97,256]{1,0:T(8,128)(2,1)S(1)} %constant_dynamic-update-slice_fusion), channel_id=1, source_target_pairs={{0,2},{1,3},{2,0},{3,1},{4,6},{5,7},{6,4},{7,5},{8,10},{9,11},{10,... | collective-permute-start | bytes 149000 | tf_op jit(solution)/shard_map/ppermute | solution.py:96
  8.8 14.9 %collective-permute-start.3 = (bf16[97,256]{1,0:T(8,128)(2,1)S(1)}, bf16[97,256]{1,0:T(8,128)(2,1)S(1)}, u32[]{:S(2)}, u32[]{:S(2)}) collective-permute-start(bf16[97,256]{1,0:T(8,128)(2,1)S(1)} %constant_dynamic-update-slice_fusion), channel_id=1, source_target_pairs={{0,1},{1,2},{2,3},{3,0},{4,5},{5,6},{6,7},{7,4},{8,9},{9,10},{10,1... | collective-permute-start | bytes 149000 | tf_op jit(solution)/shard_map/ppermute | solution.py:96
  17.9 9.2 %collective-permute-start.2 = (f32[48,1024]{1,0:T(8,128)}, f32[48,1024]{1,0:T(8,128)S(1)}, u32[]{:S(2)}, u32[]{:S(2)}) collective-permute-start(f32[48,1024]{1,0:T(8,128)} %bitcast.104), channel_id=1, source_target_pairs={{0,3},{1,0},{2,1},{3,2},{4,7},{5,4},{6,5},{7,6},{8,11},{9,8},{10,9... | collective-permute-start | bytes 589832 | tf_op jit(solution)/shard_map/ppermute | solution.py:113
  21.4 17.1 %collective-permute-start.1 = (f32[48,1024]{1,0:T(8,128)}, f32[48,1024]{1,0:T(8,128)}, u32[]{:S(2)}, u32[]{:S(2)}) collective-permute-start(f32[48,1024]{1,0:T(8,128)} %bitcast.105), channel_id=1, source_target_pairs={{0,2},{1,3},{2,0},{3,1},{4,6},{5,7},{6,4},{7,5},{8,10},{9,11},{10,... | collective-permute-start | bytes 589832 | tf_op jit(solution)/shard_map/ppermute | solution.py:113
  23.6 16.4 %collective-permute-start = (f32[48,1024]{1,0:T(8,128)}, f32[48,1024]{1,0:T(8,128)S(1)}, u32[]{:S(2)}, u32[]{:S(2)}) collective-permute-start(f32[48,1024]{1,0:T(8,128)} %bitcast.106), channel_id=1, source_target_pairs={{0,1},{1,2},{2,3},{3,0},{4,5},{5,6},{6,7},{7,4},{8,9},{9,10},{10,1... | collective-permute-start | bytes 589832 | tf_op jit(solution)/shard_map/ppermute | solution.py:113
  24.4 19.7 %collective-permute-start.9 = (bf16[4,97,256]{2,1,0:T(8,128)(2,1)S(1)}, bf16[4,97,256]{2,1,0:T(8,128)(2,1)}, u32[]{:S(2)}, u32[]{:S(2)}) collective-permute-start(bf16[4,97,256]{2,1,0:T(8,128)(2,1)S(1)} %broadcast_select_fusion.1), channel_id=1, source_target_pairs={{0,4},{4,8},{8,12},{12,16},{16,20},{20,24},{24,28},{28,0},{1,5},{5... | collective-permute-start | bytes 595976 | tf_op jit(solution)/shard_map/ppermute | solution.py:96
  24.5 22.7 %collective-permute-start.10 = (bf16[4,97,256]{2,1,0:T(8,128)(2,1)S(1)}, bf16[4,97,256]{2,1,0:T(8,128)(2,1)}, u32[]{:S(2)}, u32[]{:S(2)}) collective-permute-start(bf16[4,97,256]{2,1,0:T(8,128)(2,1)S(1)} %broadcast_select_fusion.1), channel_id=1, source_target_pairs={{0,8},{4,12},{8,16},{12,20},{16,24},{20,28},{24,0},{28,4},{1,9},{5... | collective-permute-start | bytes 595976 | tf_op jit(solution)/shard_map/ppermute | solution.py:96
  27.0 13.0 %copy-start.4 = (f32[48,1024]{1,0:T(8,128)}, f32[48,1024]{1,0:T(8,128)S(1)}, u32[]{:S(2)}) copy-start(f32[48,1024]{1,0:T(8,128)S(1)} %collective-permute-done.2) | copy-start | bytes 589828
  27.0 24.2 %collective-permute-start.11 = (bf16[4,97,256]{2,1,0:T(8,128)(2,1)S(1)}, bf16[4,97,256]{2,1,0:T(8,128)(2,1)}, u32[]{:S(2)}, u32[]{:S(2)}) collective-permute-start(bf16[4,97,256]{2,1,0:T(8,128)(2,1)S(1)} %broadcast_select_fusion.1), channel_id=1, source_target_pairs={{0,12},{4,16},{8,20},{12,24},{16,28},{20,0},{24,4},{28,8},{1,13},{... | collective-permute-start | bytes 595976 | tf_op jit(solution)/shard_map/ppermute | solution.py:96
  38.5 14.4 %collective-permute-start.12 = (bf16[4,97,256]{2,1,0:T(8,128)(2,1)S(1)}, bf16[4,97,256]{2,1,0:T(8,128)(2,1)}, u32[]{:S(2)}, u32[]{:S(2)}) collective-permute-start(bf16[4,97,256]{2,1,0:T(8,128)(2,1)S(1)} %broadcast_select_fusion.1), channel_id=1, source_target_pairs={{0,16},{4,20},{8,24},{12,28},{16,0},{20,4},{24,8},{28,12},{1,17},{... | collective-permute-start | bytes 595976 | tf_op jit(solution)/shard_map/ppermute | solution.py:96
  40.0 14.9 %collective-permute-start.13 = (bf16[4,97,256]{2,1,0:T(8,128)(2,1)S(1)}, bf16[4,97,256]{2,1,0:T(8,128)(2,1)}, u32[]{:S(2)}, u32[]{:S(2)}) collective-permute-start(bf16[4,97,256]{2,1,0:T(8,128)(2,1)S(1)} %broadcast_select_fusion.1), channel_id=1, source_target_pairs={{0,20},{4,24},{8,28},{12,0},{16,4},{20,8},{24,12},{28,16},{1,21},{... | collective-permute-start | bytes 595976 | tf_op jit(solution)/shard_map/ppermute | solution.py:96
  44.1 14.5 %collective-permute-start.14 = (bf16[4,97,256]{2,1,0:T(8,128)(2,1)S(1)}, bf16[4,97,256]{2,1,0:T(8,128)(2,1)S(1)}, u32[]{:S(2)}, u32[]{:S(2)}) collective-permute-start(bf16[4,97,256]{2,1,0:T(8,128)(2,1)S(1)} %broadcast_select_fusion.1), channel_id=1, source_target_pairs={{0,24},{4,28},{8,0},{12,4},{16,8},{20,12},{24,16},{28,20},{1,25},{... | collective-permute-start | bytes 595976 | tf_op jit(solution)/shard_map/ppermute | solution.py:96
  47.2 12.1 %collective-permute-start.15 = (bf16[4,97,256]{2,1,0:T(8,128)(2,1)S(1)}, bf16[4,97,256]{2,1,0:T(8,128)(2,1)S(1)}, u32[]{:S(2)}, u32[]{:S(2)}) collective-permute-start(bf16[4,97,256]{2,1,0:T(8,128)(2,1)S(1)} %broadcast_select_fusion.1), channel_id=1, source_target_pairs={{0,28},{4,0},{8,4},{12,8},{16,12},{20,16},{24,20},{28,24},{1,29},{... | collective-permute-start | bytes 595976 | tf_op jit(solution)/shard_map/ppermute | solution.py:96
  51.2 14.9 %collective-permute-start.8 = (bf16[48,1024]{1,0:T(8,128)(2,1)S(1)}, bf16[48,1024]{1,0:T(8,128)(2,1)S(1)}, u32[]{:S(2)}, u32[]{:S(2)}) collective-permute-start(bf16[48,1024]{1,0:T(8,128)(2,1)S(1)} %divide_convert_fusion), channel_id=1, source_target_pairs={{0,3},{1,0},{2,1},{3,2},{4,7},{5,4},{6,5},{7,6},{8,11},{9,8},{10,9... | collective-permute-start | bytes 294920 | tf_op jit(solution)/shard_map/ppermute | solution.py:96
  52.9 13.3 %collective-permute-start.7 = (bf16[48,1024]{1,0:T(8,128)(2,1)S(1)}, bf16[48,1024]{1,0:T(8,128)(2,1)S(1)}, u32[]{:S(2)}, u32[]{:S(2)}) collective-permute-start(bf16[48,1024]{1,0:T(8,128)(2,1)S(1)} %divide_convert_fusion), channel_id=1, source_target_pairs={{0,2},{1,3},{2,0},{3,1},{4,6},{5,7},{6,4},{7,5},{8,10},{9,11},{10,... | collective-permute-start | bytes 294920 | tf_op jit(solution)/shard_map/ppermute | solution.py:96
  55.0 11.2 %collective-permute-start.6 = (bf16[48,1024]{1,0:T(8,128)(2,1)S(1)}, bf16[48,1024]{1,0:T(8,128)(2,1)S(1)}, u32[]{:S(2)}, u32[]{:S(2)}) collective-permute-start(bf16[48,1024]{1,0:T(8,128)(2,1)S(1)} %divide_convert_fusion), channel_id=1, source_target_pairs={{0,1},{1,2},{2,3},{3,0},{4,5},{5,6},{6,7},{7,4},{8,9},{9,10},{10,1... | collective-permute-start | bytes 294920 | tf_op jit(solution)/shard_map/ppermute | solution.py:96
  66.2 0.6 copy-start.5
  75.8 0.7 copy-start.3
  77.2 31.5 %copy-start.2 = (f32[384,1024]{1,0:T(8,128)}, f32[384,1024]{1,0:T(8,128)S(1)}, u32[]{:S(2)}) copy-start(f32[384,1024]{1,0:T(8,128)S(1)} %convolution_multiply_fusion) | copy-start | bytes 4718596
  77.2 18.9 %copy-start.1 = (bf16[128,4096]{1,0:T(8,128)(2,1)S(1)}, bf16[128,4096]{1,0:T(8,128)(2,1)}, u32[]{:S(2)}) copy-start(bf16[128,4096]{1,0:T(8,128)(2,1)} %param.10) | copy-start | bytes 3145732
  77.2 18.9 %copy-start.6 = (s32[1,128]{1,0:T(1,128)S(1)}, s32[1,128]{1,0:T(1,128)}, u32[]{:S(2)}) copy-start(s32[1,128]{1,0:T(1,128)} %param.11) | copy-start | bytes 1540
  98.6 6.1 %collective-permute-start.16 = (f32[28672]{0:T(1024)S(1)}, f32[28672]{0:T(1024)S(1)}, u32[]{:S(2)}, u32[]{:S(2)}) collective-permute-start(f32[28672]{0:T(1024)S(1)} %get-tuple-element.35), channel_id=1, source_target_pairs={{0,4},{4,8},{8,12},{12,16},{16,20},{20,24},{24,28},{28,0},{1,5},{5... | collective-permute-start | bytes 344072 | tf_op jit(solution)/shard_map/ppermute | solution.py:127
  98.7 7.7 %collective-permute-start.17 = (f32[28672]{0:T(1024)S(1)}, f32[28672]{0:T(1024)S(1)}, u32[]{:S(2)}, u32[]{:S(2)}) collective-permute-start(f32[28672]{0:T(1024)S(1)} %get-tuple-element.30), channel_id=1, source_target_pairs={{0,8},{4,12},{8,16},{12,20},{16,24},{20,28},{24,0},{28,4},{1,9},{5... | collective-permute-start | bytes 344072 | tf_op jit(solution)/shard_map/ppermute | solution.py:127
  100.2 11.4 %collective-permute-start.18 = (f32[28672]{0:T(1024)S(1)}, f32[28672]{0:T(1024)}, u32[]{:S(2)}, u32[]{:S(2)}) collective-permute-start(f32[28672]{0:T(1024)S(1)} %get-tuple-element.31), channel_id=1, source_target_pairs={{0,12},{4,16},{8,20},{12,24},{16,28},{20,0},{24,4},{28,8},{1,13},{... | collective-permute-start | bytes 344072 | tf_op jit(solution)/shard_map/ppermute | solution.py:127
  101.7 10.7 %collective-permute-start.19 = (f32[28672]{0:T(1024)S(1)}, f32[28672]{0:T(1024)}, u32[]{:S(2)}, u32[]{:S(2)}) collective-permute-start(f32[28672]{0:T(1024)S(1)} %get-tuple-element.32), channel_id=1, source_target_pairs={{0,16},{4,20},{8,24},{12,28},{16,0},{20,4},{24,8},{28,12},{1,17},{... | collective-permute-start | bytes 344072 | tf_op jit(solution)/shard_map/ppermute | solution.py:127
  103.0 10.1 %collective-permute-start.20 = (f32[28672]{0:T(1024)S(1)}, f32[28672]{0:T(1024)}, u32[]{:S(2)}, u32[]{:S(2)}) collective-permute-start(f32[28672]{0:T(1024)S(1)} %get-tuple-element.33), channel_id=1, source_target_pairs={{0,20},{4,24},{8,28},{12,0},{16,4},{20,8},{24,12},{28,16},{1,21},{... | collective-permute-start | bytes 344072 | tf_op jit(solution)/shard_map/ppermute | solution.py:127
  104.7 9.1 %collective-permute-start.21 = (f32[28672]{0:T(1024)S(1)}, f32[28672]{0:T(1024)S(1)}, u32[]{:S(2)}, u32[]{:S(2)}) collective-permute-start(f32[28672]{0:T(1024)S(1)} %get-tuple-element.34), channel_id=1, source_target_pairs={{0,24},{4,28},{8,0},{12,4},{16,8},{20,12},{24,16},{28,20},{1,25},{... | collective-permute-start | bytes 344072 | tf_op jit(solution)/shard_map/ppermute | solution.py:127
  106.3 7.5 %collective-permute-start.22 = (f32[28672]{0:T(1024)S(1)}, f32[28672]{0:T(1024)}, u32[]{:S(2)}, u32[]{:S(2)}) collective-permute-start(f32[28672]{0:T(1024)S(1)} %get-tuple-element.29), channel_id=1, source_target_pairs={{0,28},{4,0},{8,4},{12,8},{16,12},{20,16},{24,20},{28,24},{1,29},{... | collective-permute-start | bytes 344072 | tf_op jit(solution)/shard_map/ppermute | solution.py:127
  115.5 9.8 %collective-permute-start.25 = (f32[4096]{0:T(1024)S(1)}, f32[4096]{0:T(1024)S(1)}, u32[]{:S(2)}, u32[]{:S(2)}) collective-permute-start(f32[4096]{0:T(1024)S(1)} %select_reduce_fusion.2), channel_id=1, source_target_pairs={{0,3},{1,0},{2,1},{3,2},{4,7},{5,4},{6,5},{7,6},{8,11},{9,8},{10,9... | collective-permute-start | bytes 49160 | tf_op jit(solution)/shard_map/ppermute | solution.py:96
  117.3 8.0 %collective-permute-start.24 = (f32[4096]{0:T(1024)S(1)}, f32[4096]{0:T(1024)S(1)}, u32[]{:S(2)}, u32[]{:S(2)}) collective-permute-start(f32[4096]{0:T(1024)S(1)} %select_reduce_fusion.2), channel_id=1, source_target_pairs={{0,2},{1,3},{2,0},{3,1},{4,6},{5,7},{6,4},{7,5},{8,10},{9,11},{10,... | collective-permute-start | bytes 49160 | tf_op jit(solution)/shard_map/ppermute | solution.py:96
  117.3 8.0 %collective-permute-start.23 = (f32[4096]{0:T(1024)S(1)}, f32[4096]{0:T(1024)S(1)}, u32[]{:S(2)}, u32[]{:S(2)}) collective-permute-start(f32[4096]{0:T(1024)S(1)} %select_reduce_fusion.2), channel_id=1, source_target_pairs={{0,1},{1,2},{2,3},{3,0},{4,5},{5,6},{6,7},{7,4},{8,9},{9,10},{10,1... | collective-permute-start | bytes 49160 | tf_op jit(solution)/shard_map/ppermute | solution.py:96

commit v11 on v10

--- a/solution.py
+++ b/solution.py
@@ -90,14 +90,21 @@
     return (mean_loss, query_grad, region_grad, hidden_grad, gain_grad, proj_grad)
 
 
+def arrange(copies, me):
+    n = len(copies)
+    source = ((me - jnp.arange(n)) % n).reshape((n,) + (1,) * copies[0].ndim)
+    out = jnp.broadcast_to(copies[0][None], (n,) + copies[0].shape)
+    for s in range(1, n):
+        out = jnp.where(source == s, copies[s][None], out)
+    return out
+
+
 def gather_blocks(x, axis):
     n = lax.axis_size(axis)
     copies = [x] + [
         lax.ppermute(x, axis, [(i, (i + s) % n) for i in range(n)]) for s in range(1, n)
     ]
-    stack = jnp.stack(copies)
-    order = (lax.axis_index(axis) - jnp.arange(n)) % n
-    return jnp.take(stack, order, axis=0)
+    return arrange(copies, lax.axis_index(axis))
 
 
 def sum_blocks(x, axis):
@@ -111,8 +118,7 @@
     for s in range(1, n):
         piece = lax.dynamic_index_in_dim(chunks, (me + s) % n, axis=0, keepdims=False)
         copies.append(lax.ppermute(piece, axis, [(i, (i + s) % n) for i in range(n)]))
-    order = (me - jnp.arange(n)) % n
-    return jnp.sum(jnp.take(jnp.stack(copies), order, axis=0), axis=0)
+    return jnp.sum(arrange(copies, me), axis=0)
 
 
 def spread_with_sum(total, pieces, axis):
@@ -127,11 +133,7 @@
         arrived = lax.ppermute(payload, axis, [(i, (i + s) % n) for i in range(n)])
         sums.append(arrived[:size])
         got.append(arrived[size:].reshape(piece.shape))
-    order = (me - jnp.arange(n)) % n
-    return (
-        jnp.sum(jnp.take(jnp.stack(sums), order, axis=0), axis=0),
-        jnp.take(jnp.stack(got), order, axis=0),
-    )
+    return jnp.sum(arrange(sums, me), axis=0), arrange(got, me)
 
 
 def local_small(query_cache, region_cache, positive, hidden_states, segment_ids, norm_gain, proj_weight):

time: 129 us -> 118 us (0.915)
  local copies, waits for them, and re-layouts: 37.2 us -> 22.9 us
  starting transfers between devices: 33.1 us -> 36.1 us
  waiting for transfers between devices: 9.21 us -> 7.52 us
    broadcast_in_dim x2 -> x18, local copies, waits for them, and re-layouts: 0.16 us -> 9.74 us  [the longest x17 9.63 us: arrange(): out = jnp.where(source == s, copies[s][None], out)]
    ppermute x3, waiting for transfers between devices: 9.15 us -> 0.01 us  [scatter_sum(): lax.ppermute(piece, axis, [(i, (i + s) % n) for i in range(n)])]
    unnamed x38 -> x90, local copies, waits for them, and re-layouts: 15.4 us -> 6.5 us
    gather x7 -> x0, local copies, waits for them, and re-layouts: 7.65 us -> none  [the longest x4 5 us: gather_blocks(): return jnp.take(stack, order, axis=0)]
    ppermute x16, waiting for transfers between devices: 0.04 us -> 7.5 us  [gather_blocks(): lax.ppermute(x, axis, [(i, (i + s) % n) for i in range(n)])]
    ppermute x16, starting transfers between devices: 20.9 us -> 23.9 us  [gather_blocks(): lax.ppermute(x, axis, [(i, (i + s) % n) for i in range(n)])]
    select_n x4 -> x3, other arithmetic: 2.97 us -> 5.56 us  [arrange(): out = jnp.where(source == s, copies[s][None], out)]
    slice x7 -> x14, local copies, waits for them, and re-layouts: 3.62 us -> 1.24 us  [spread_with_sum(): got.append(arrived[size:].reshape(piece.shape))]
  transfers between devices with their start and end apart: 26 -> 26, of which waited for: 1 -> 4; matrix products, arithmetic and copies ran while one was open for 35% -> 31% of each run, Pallas kernels for 0% -> 0%
where the time goes in v11:
time: 118 us; the launch traced here: 117 us
  starting transfers between devices  36.1 us (31%)
  local copies, waits for them, and re-layouts  22.9 us (19%)
  blocking collectives  19.2 us (16%)
  other arithmetic  17.1 us (14%)
  matrix products  11.2 us (9%)
  waiting for transfers between devices  7.52 us (6%)
  between operations  3.34 us (3%)
    ppermute x16, starting transfers between devices, gather_blocks(): lax.ppermute(x, axis, [(i, (i + s) % n) for i in range(n)])  23.9 us
    all_gather x1, blocking collectives, local_small(): mean_grad = lax.all_gather(mean_part, 'fsdp', axis=1, tiled=True)  19.2 us
    broadcast_in_dim x17, local copies, waits for them, and re-layouts, arrange(): out = jnp.where(source == s, copies[s][None], out)  9.63 us
    ppermute x7, starting transfers between devices, spread_with_sum(): arrived = lax.ppermute(payload, axis, [(i, (i + s) % n) for i in range(n)])  8.3 us
    ppermute x16, waiting for transfers between devices, gather_blocks(): lax.ppermute(x, axis, [(i, (i + s) % n) for i in range(n)])  7.5 us
    unnamed x90, local copies, waits for them, and re-layouts  6.5 us
    select_n x3, other arithmetic, arrange(): out = jnp.where(source == s, copies[s][None], out)  5.56 us
    ppermute x3, starting transfers between devices, scatter_sum(): lax.ppermute(piece, axis, [(i, (i + s) % n) for i in range(n)])  3.96 us
  transfers between devices with their start and end apart: 26, of which 4 were waited for; matrix products, arithmetic and copies ran while one was open for 31% of the time, Pallas kernels for 0%

profile of v11, /device:TPU:0, one launch (start us, length us, event | category | flops | bytes accessed | tf_op | source)
XLA Modules:
  0.0 117.4 jit_solution(6419315046204050385)
XLA Ops:
  0.6 0.9 constant_dynamic-update-slice_fusion.2
  2.2 0.7 constant_dynamic-update-slice_fusion.1
  2.9 0.7 fusion.35
  3.7 3.1 %collective-permute-start.5 = (bf16[97,256]{1,0:T(8,128)(2,1)S(1)}, bf16[97,256]{1,0:T(8,128)(2,1)}, u32[]{:S(2)}, u32[]{:S(2)}) collective-permute-start(bf16[97,256]{1,0:T(8,128)(2,1)S(1)} %constant_dynamic-update-slice_fusion), channel_id=1, source_target_pairs={{0,1},{1,2},{2,3},{3,0},{4,5},{5,6},{6,7},{7,4},{8,9},{9,10},{10,1... | collective-permute-start | bytes 149000 | tf_op jit(solution)/shard_map/ppermute | solution.py:105
  6.8 2.6 %collective-permute-start.4 = (bf16[97,256]{1,0:T(8,128)(2,1)S(1)}, bf16[97,256]{1,0:T(8,128)(2,1)}, u32[]{:S(2)}, u32[]{:S(2)}) collective-permute-start(bf16[97,256]{1,0:T(8,128)(2,1)S(1)} %constant_dynamic-update-slice_fusion), channel_id=1, source_target_pairs={{0,2},{1,3},{2,0},{3,1},{4,6},{5,7},{6,4},{7,5},{8,10},{9,11},{10,... | collective-permute-start | bytes 149000 | tf_op jit(solution)/shard_map/ppermute | solution.py:105
  9.4 1.3 %collective-permute-start.3 = (bf16[97,256]{1,0:T(8,128)(2,1)S(1)}, bf16[97,256]{1,0:T(8,128)(2,1)}, u32[]{:S(2)}, u32[]{:S(2)}) collective-permute-start(bf16[97,256]{1,0:T(8,128)(2,1)S(1)} %constant_dynamic-update-slice_fusion), channel_id=1, source_target_pairs={{0,3},{1,0},{2,1},{3,2},{4,7},{5,4},{6,5},{7,6},{8,11},{9,8},{10,9... | collective-permute-start | bytes 149000 | tf_op jit(solution)/shard_map/ppermute | solution.py:105
  10.7 0.7 convert_element_type.82
  11.4 1.5 %fusion = f32[128]{0:T(128)S(1)} fusion(bf16[128,4096]{1,0:T(8,128)(2,1)} %param.10), kind=kLoop, calls=%fused_computation.5 | loop fusion | flops 1572736 | bytes 1049088 | tf_op jit(solution)/shard_map/reduce_sum | solution.py:167
  14.0 2.6 %fusion.9 = f32[48,4096]{1,0:T(8,128)} fusion(bf16[128,4096]{1,0:T(8,128)(2,1)} %param.10, f32[4096]{0:T(1024)S(1)} %convert_element_type.82, f32[128]{0:T(128)S(1)} %get-tuple-element.37, s32[128]{0:T(128)} %bitcast.136), kind=kOutput, calls=%fused_computation.18 | convolution fusion | flops 52434944 | bytes 1852416 | tf_op jit(solution)/shard_map/dot_general | solution.py:171
  16.6 1.7 %reshape.432 = f32[48,4,1024]{2,1,0:T(4,128)S(1)} reshape(f32[48,4096]{1,0:T(8,128)} %fusion.9) | data formatting | bytes 1572864 | tf_op jit(solution)/shard_map/reshape | solution.py:175
  18.2 0.8 constant_dynamic-slice_fusion.11
  19.1 0.7 collective-permute-start.2
  27.0 0.7 broadcast_in_dim.610
  29.5 0.7 broadcast_in_dim.600
  33.6 2.8 %collective-permute-start = (f32[48,1024]{1,0:T(8,128)S(1)}, f32[48,1024]{1,0:T(8,128)S(1)}, u32[]{:S(2)}, u32[]{:S(2)}) collective-permute-start(f32[48,1024]{1,0:T(8,128)S(1)} %bitcast.130), channel_id=1, source_target_pairs={{0,3},{1,0},{2,1},{3,2},{4,7},{5,4},{6,5},{7,6},{8,11},{9,8},{10,9... | collective-permute-start | bytes 589832 | tf_op jit(solution)/shard_map/ppermute | solution.py:120
  36.4 1.1 select_select_fusion.2
  37.6 1.5 %collective-permute-start.14 = (bf16[4,97,256]{2,0,1:T(4,128)(2,1)S(1)}, bf16[4,97,256]{2,0,1:T(4,128)(2,1)S(1)}, u32[]{:S(2)}, u32[]{:S(2)}) collective-permute-start(bf16[4,97,256]{2,0,1:T(4,128)(2,1)S(1)} %select_select_fusion.2), channel_id=1, source_target_pairs={{0,8},{4,12},{8,16},{12,20},{16,24},{20,28},{24,0},{28,4},{1,9},{5... | collective-permute-start | bytes 595976 | tf_op jit(solution)/shard_map/ppermute | solution.py:105
  39.4 2.4 %collective-permute-start.13 = (bf16[4,97,256]{2,0,1:T(4,128)(2,1)S(1)}, bf16[4,97,256]{2,0,1:T(4,128)(2,1)S(1)}, u32[]{:S(2)}, u32[]{:S(2)}) collective-permute-start(bf16[4,97,256]{2,0,1:T(4,128)(2,1)S(1)} %select_select_fusion.2), channel_id=1, source_target_pairs={{0,12},{4,16},{8,20},{12,24},{16,28},{20,0},{24,4},{28,8},{1,13},{... | collective-permute-start | bytes 595976 | tf_op jit(solution)/shard_map/ppermute | solution.py:105
  42.4 0.9 select_reduce_fusion
  43.3 2.0 %collective-permute-done.15 = bf16[4,97,256]{2,0,1:T(4,128)(2,1)S(1)} collective-permute-done((bf16[4,97,256]{2,0,1:T(4,128)(2,1)S(1)}, bf16[4,97,256]{2,0,1:T(4,128)(2,1)S(1)}, u32[]{:S(2)}, u32[]{:S(2)}) %collective-permute-start.15) | collective-permute-done | bytes 198688 | tf_op jit(solution)/shard_map/ppermute | solution.py:105
  45.3 1.4 %collective-permute-start.10 = (bf16[4,97,256]{2,0,1:T(4,128)(2,1)S(1)}, bf16[4,97,256]{2,0,1:T(4,128)(2,1)S(1)}, u32[]{:S(2)}, u32[]{:S(2)}) collective-permute-start(bf16[4,97,256]{2,0,1:T(4,128)(2,1)S(1)} %select_select_fusion.2), channel_id=1, source_target_pairs={{0,24},{4,28},{8,0},{12,4},{16,8},{20,12},{24,16},{28,20},{1,25},{... | collective-permute-start | bytes 595976 | tf_op jit(solution)/shard_map/ppermute | solution.py:105
  46.7 4.0 %collective-permute-start.9 = (bf16[4,97,256]{2,0,1:T(4,128)(2,1)S(1)}, bf16[4,97,256]{2,0,1:T(4,128)(2,1)S(1)}, u32[]{:S(2)}, u32[]{:S(2)}) collective-permute-start(bf16[4,97,256]{2,0,1:T(4,128)(2,1)S(1)} %select_select_fusion.2), channel_id=1, source_target_pairs={{0,28},{4,0},{8,4},{12,8},{16,12},{20,16},{24,20},{28,24},{1,29},{... | collective-permute-start | bytes 595976 | tf_op jit(solution)/shard_map/ppermute | solution.py:105
  51.1 3.1 %collective-permute-done.13 = bf16[4,97,256]{2,0,1:T(4,128)(2,1)S(1)} collective-permute-done((bf16[4,97,256]{2,0,1:T(4,128)(2,1)S(1)}, bf16[4,97,256]{2,0,1:T(4,128)(2,1)S(1)}, u32[]{:S(2)}, u32[]{:S(2)}) %collective-permute-start.13) | collective-permute-done | bytes 198688 | tf_op jit(solution)/shard_map/ppermute | solution.py:105
  54.2 1.2 %collective-permute-start.6 = (bf16[48,1024]{1,0:T(8,128)(2,1)S(1)}, bf16[48,1024]{1,0:T(8,128)(2,1)S(1)}, u32[]{:S(2)}, u32[]{:S(2)}) collective-permute-start(bf16[48,1024]{1,0:T(8,128)(2,1)S(1)} %divide_convert_fusion), channel_id=1, source_target_pairs={{0,3},{1,0},{2,1},{3,2},{4,7},{5,4},{6,5},{7,6},{8,11},{9,8},{10,9... | collective-permute-start | bytes 294920 | tf_op jit(solution)/shard_map/ppermute | solution.py:105
  55.4 1.0 collective-permute-start.7
  56.4 1.2 %collective-permute-done.11 = bf16[4,97,256]{2,0,1:T(4,128)(2,1)S(1)} collective-permute-done((bf16[4,97,256]{2,0,1:T(4,128)(2,1)S(1)}, bf16[4,97,256]{2,0,1:T(4,128)(2,1)S(1)}, u32[]{:S(2)}, u32[]{:S(2)}) %collective-permute-start.11) | collective-permute-done | bytes 198688 | tf_op jit(solution)/shard_map/ppermute | solution.py:105
  58.3 4.3 %select_select_fusion = bf16[8,4,97,256]{3,1,2,0:T(4,128)(2,1)S(1)} fusion(pred[8]{0:T(512)(128)(4,1)S(1)} %copy-done.12, pred[8]{0:T(512)(128)(4,1)S(1)} %copy-done.14, pred[8]{0:T(512)(128)(4,1)S(1)} %copy-done.16, pred[8]{0:T(512)(128)(4,1)S(1)} %copy-done.18, pred[8]{0:T(512)(128)(4,1)S(1)} %copy-done.20, pred[8]{0:T(512)(128)(4,1)S(1)} %copy-done.22, ...), kind=kLoop, calls=%fused_computation.14 | loop fusion | flops 5562368 | bytes 3178552 | tf_op jit(solution)/shard_map/jit(_where)/select_n | solution.py:98
  63.1 1.2 collective-permute-done.8
  64.7 0.7 fusion.38
  65.4 1.0 copy.25
  66.8 1.7 %fusion.39 = (f32[384]{0:T(512)S(1)}, f32[384,384]{0,1:T(8,128)S(1)}) fusion(bf16[384,1024]{1,0:T(8,128)(2,1)} %bitcast.118, bf16[384,1024]{1,0:T(8,128)(2,1)S(1)} %bitcast.107), kind=kOutput, calls=%fused_computation.128 | convolution fusion | flops 302284416 | bytes 2164224 | tf_op jit(solution)/shard_map/dot_general | solution.py:195
  69.5 0.7 copy-done.3
  70.9 0.7 fusion.25
  71.6 19.2 %all_gather.3 = f32[48,4096]{1,0:T(8,128)S(1)} all-gather(f32[48,1024]{1,0:T(8,128)S(1)} %fusion.25), channel_id=1, replica_groups=mesh['dp'=8,'fsdp'=4] {'fsdp'}, dimensions={1}, use_global_device_ids=true | all-gather | bytes 983040 | tf_op jit(solution)/shard_map/all_gather | solution.py:222
  90.8 1.6 %fusion.8 = (f32[4096]{0:T(1024)S(1)}, f32[128]{0:T(128)S(1)}, f32[128,4096]{1,0:T(8,128)S(1)}) fusion(bf16[128,4096]{1,0:T(8,128)(2,1)S(1)} %copy-done.1, f32[128]{0:T(128)S(1)} %copy-done.26, f32[4096]{0:T(1024)S(1)} %convert_element_type.82, f32[48,4096]{1,0:T(8,128)S(1)} %all_gather.3, f32[48]{0:T(128)S(1)} %convert_reduce_fusion, s32[128]{0:T(128)S(1)} %bitcast.137), kind=kOutput, calls=%fused_computation.13 | convolution fusion | flops 305858432 | bytes 3966656 | tf_op jit(solution)/shard_map/dot_general | solution.py:224
  93.4 1.9 %collective-permute-start.21 = (f32[28672]{0:T(1024)S(1)}, f32[28672]{0:T(1024)S(1)}, u32[]{:S(2)}, u32[]{:S(2)}) collective-permute-start(f32[28672]{0:T(1024)S(1)} %get-tuple-element.34), channel_id=1, source_target_pairs={{0,8},{4,12},{8,16},{12,20},{16,24},{20,28},{24,0},{28,4},{1,9},{5... | collective-permute-start | bytes 344072 | tf_op jit(solution)/shard_map/ppermute | solution.py:133
  95.3 1.6 %collective-permute-start.20 = (f32[28672]{0:T(1024)S(1)}, f32[28672]{0:T(1024)S(1)}, u32[]{:S(2)}, u32[]{:S(2)}) collective-permute-start(f32[28672]{0:T(1024)S(1)} %get-tuple-element.33), channel_id=1, source_target_pairs={{0,12},{4,16},{8,20},{12,24},{16,28},{20,0},{24,4},{28,8},{1,13},{... | collective-permute-start | bytes 344072 | tf_op jit(solution)/shard_map/ppermute | solution.py:133
  96.9 1.3 %collective-permute-start.19 = (f32[28672]{0:T(1024)S(1)}, f32[28672]{0:T(1024)S(1)}, u32[]{:S(2)}, u32[]{:S(2)}) collective-permute-start(f32[28672]{0:T(1024)S(1)} %get-tuple-element.32), channel_id=1, source_target_pairs={{0,16},{4,20},{8,24},{12,28},{16,0},{20,4},{24,8},{28,12},{1,17},{... | collective-permute-start | bytes 344072 | tf_op jit(solution)/shard_map/ppermute | solution.py:133
  98.2 1.6 %fusion.5 = bf16[128,4096]{1,0:T(8,128)(2,1)} fusion(bf16[128,4096]{1,0:T(8,128)(2,1)S(1)} %copy-done.1, f32[128,4096]{1,0:T(8,128)S(1)} %get-tuple-element.42, f32[128]{0:T(128)S(1)} %broadcast_multiply_fusion, f32[128]{0:T(128)S(1)} %copy-done.24, f32[4096]{0:T(1024)S(1)} %convert_element_type.82, f32[128]{0:T(128)S(1)} %copy-done.26), kind=kLoop, calls=%fused_computation.10 | loop fusion | flops 3670016 | bytes 4212224 | tf_op jit(solution)/shard_map/convert_element_type | solution.py:234
  99.9 1.2 %collective-permute-start.17 = (f32[28672]{0:T(1024)S(1)}, f32[28672]{0:T(1024)S(1)}, u32[]{:S(2)}, u32[]{:S(2)}) collective-permute-start(f32[28672]{0:T(1024)S(1)} %get-tuple-element.30), channel_id=1, source_target_pairs={{0,24},{4,28},{8,0},{12,4},{16,8},{20,12},{24,16},{28,20},{1,25},{... | collective-permute-start | bytes 344072 | tf_op jit(solution)/shard_map/ppermute | solution.py:133
  101.1 2.3 %collective-permute-start.16 = (f32[28672]{0:T(1024)S(1)}, f32[28672]{0:T(1024)}, u32[]{:S(2)}, u32[]{:S(2)}) collective-permute-start(f32[28672]{0:T(1024)S(1)} %get-tuple-element.29), channel_id=1, source_target_pairs={{0,28},{4,0},{8,4},{12,8},{16,12},{20,16},{24,20},{28,24},{1,29},{... | collective-permute-start | bytes 344072 | tf_op jit(solution)/shard_map/ppermute | solution.py:133
  104.8 1.7 %convolution_multiply_fusion.2 = f32[48,256]{1,0:T(8,128)} fusion(bf16[384,1024]{1,0:T(8,128)(2,1)} %bitcast.119, s32[]{:T(128)S(6)} %select_n.374, bf16[384,384]{0,1:T(8,128)(2,1)} %copy-done.3, s32[]{:T(128)S(6)} %select_n.373), kind=kOutput, calls=%fused_computation.17 | convolution fusion | flops 9449472 | bytes 282632 | tf_op jit(solution)/shard_map/dot_general | solution.py:215
  106.6 0.7 slice.151
  107.6 2.4 %collective-permute-start.24 = (f32[4096]{0:T(1024)S(1)}, f32[4096]{0:T(1024)S(1)}, u32[]{:S(2)}, u32[]{:S(2)}) collective-permute-start(f32[4096]{0:T(1024)S(1)} %select_reduce_fusion.2), channel_id=1, source_target_pairs={{0,2},{1,3},{2,0},{3,1},{4,6},{5,7},{6,4},{7,5},{8,10},{9,11},{10,... | collective-permute-start | bytes 49160 | tf_op jit(solution)/shard_map/ppermute | solution.py:105
  110.1 1.5 %collective-permute-start.23 = (f32[4096]{0:T(1024)S(1)}, f32[4096]{0:T(1024)S(1)}, u32[]{:S(2)}, u32[]{:S(2)}) collective-permute-start(f32[4096]{0:T(1024)S(1)} %select_reduce_fusion.2), channel_id=1, source_target_pairs={{0,3},{1,0},{2,1},{3,2},{4,7},{5,4},{6,5},{7,6},{8,11},{9,8},{10,9... | collective-permute-start | bytes 49160 | tf_op jit(solution)/shard_map/ppermute | solution.py:105
  111.9 0.9 slice.158
  113.4 2.1 %fusion.23 = f32[512,256]{1,0:T(8,128)} fusion(bf16[384,512]{1,0:T(8,128)(2,1)S(1)} %fusion.19, f32[384,1024]{1,0:T(8,128)} %copy-done.2, s32[]{:T(128)S(6)} %select_n.374), kind=kOutput, calls=%fused_computation.47 | convolution fusion | flops 100663296 | bytes 1114116 | tf_op jit(solution)/shard_map/dot_general | solution.py:238
  115.6 0.7 select_reduce_fusion.3
  (180 shorter events, 21.4 us)
Async XLA Ops:
  0.6 70.2 %copy-start = (bf16[1024,1024]{1,0:T(8,128)(2,1)S(1)}, bf16[1024,1024]{1,0:T(8,128)(2,1)}, u32[]{:S(2)}) copy-start(bf16[1024,1024]{1,0:T(8,128)(2,1)} %param.13) | copy-start | bytes 6291460
  3.7 29.9 %collective-permute-start.5 = (bf16[97,256]{1,0:T(8,128)(2,1)S(1)}, bf16[97,256]{1,0:T(8,128)(2,1)}, u32[]{:S(2)}, u32[]{:S(2)}) collective-permute-start(bf16[97,256]{1,0:T(8,128)(2,1)S(1)} %constant_dynamic-update-slice_fusion), channel_id=1, source_target_pairs={{0,1},{1,2},{2,3},{3,0},{4,5},{5,6},{6,7},{7,4},{8,9},{9,10},{10,1... | collective-permute-start | bytes 149000 | tf_op jit(solution)/shard_map/ppermute | solution.py:105
  6.8 29.7 %collective-permute-start.4 = (bf16[97,256]{1,0:T(8,128)(2,1)S(1)}, bf16[97,256]{1,0:T(8,128)(2,1)}, u32[]{:S(2)}, u32[]{:S(2)}) collective-permute-start(bf16[97,256]{1,0:T(8,128)(2,1)S(1)} %constant_dynamic-update-slice_fusion), channel_id=1, source_target_pairs={{0,2},{1,3},{2,0},{3,1},{4,6},{5,7},{6,4},{7,5},{8,10},{9,11},{10,... | collective-permute-start | bytes 149000 | tf_op jit(solution)/shard_map/ppermute | solution.py:105
  9.4 27.1 %collective-permute-start.3 = (bf16[97,256]{1,0:T(8,128)(2,1)S(1)}, bf16[97,256]{1,0:T(8,128)(2,1)}, u32[]{:S(2)}, u32[]{:S(2)}) collective-permute-start(bf16[97,256]{1,0:T(8,128)(2,1)S(1)} %constant_dynamic-update-slice_fusion), channel_id=1, source_target_pairs={{0,3},{1,0},{2,1},{3,2},{4,7},{5,4},{6,5},{7,6},{8,11},{9,8},{10,9... | collective-permute-start | bytes 149000 | tf_op jit(solution)/shard_map/ppermute | solution.py:105
  19.1 20.3 %collective-permute-start.2 = (f32[48,1024]{1,0:T(8,128)S(1)}, f32[48,1024]{1,0:T(8,128)S(1)}, u32[]{:S(2)}, u32[]{:S(2)}) collective-permute-start(f32[48,1024]{1,0:T(8,128)S(1)} %bitcast.129), channel_id=1, source_target_pairs={{0,1},{1,2},{2,3},{3,0},{4,5},{5,6},{6,7},{7,4},{8,9},{9,10},{10,1... | collective-permute-start | bytes 589832 | tf_op jit(solution)/shard_map/ppermute | solution.py:120
  19.9 21.9 %collective-permute-start.1 = (f32[48,1024]{1,0:T(8,128)S(1)}, f32[48,1024]{1,0:T(8,128)S(1)}, u32[]{:S(2)}, u32[]{:S(2)}) collective-permute-start(f32[48,1024]{1,0:T(8,128)S(1)} %bitcast.128), channel_id=1, source_target_pairs={{0,2},{1,3},{2,0},{3,1},{4,6},{5,7},{6,4},{7,5},{8,10},{9,11},{10,... | collective-permute-start | bytes 589832 | tf_op jit(solution)/shard_map/ppermute | solution.py:120
  23.5 34.7 %copy-start.10 = (pred[8]{0:T(512)(128)(4,1)S(1)}, pred[8]{0:T(512)(128)(4,1)}, u32[]{:S(2)}) copy-start(pred[8]{0:T(512)(128)(4,1)} %get-tuple-element.45) | copy-start | bytes 28
  23.5 34.7 %copy-start.12 = (pred[8]{0:T(512)(128)(4,1)S(1)}, pred[8]{0:T(512)(128)(4,1)}, u32[]{:S(2)}) copy-start(pred[8]{0:T(512)(128)(4,1)} %get-tuple-element.46) | copy-start | bytes 28
  23.5 34.7 %copy-start.14 = (pred[8]{0:T(512)(128)(4,1)S(1)}, pred[8]{0:T(512)(128)(4,1)}, u32[]{:S(2)}) copy-start(pred[8]{0:T(512)(128)(4,1)} %get-tuple-element.47) | copy-start | bytes 28
  23.5 34.7 %copy-start.16 = (pred[8]{0:T(512)(128)(4,1)S(1)}, pred[8]{0:T(512)(128)(4,1)}, u32[]{:S(2)}) copy-start(pred[8]{0:T(512)(128)(4,1)} %get-tuple-element.48) | copy-start | bytes 28
  23.6 34.7 %copy-start.18 = (pred[8]{0:T(512)(128)(4,1)S(1)}, pred[8]{0:T(512)(128)(4,1)}, u32[]{:S(2)}) copy-start(pred[8]{0:T(512)(128)(4,1)} %get-tuple-element.49) | copy-start | bytes 28
  23.6 34.7 %copy-start.20 = (pred[8]{0:T(512)(128)(4,1)S(1)}, pred[8]{0:T(512)(128)(4,1)}, u32[]{:S(2)}) copy-start(pred[8]{0:T(512)(128)(4,1)} %get-tuple-element.50) | copy-start | bytes 28
  23.6 34.7 %copy-start.22 = (pred[8]{0:T(512)(128)(4,1)S(1)}, pred[8]{0:T(512)(128)(4,1)}, u32[]{:S(2)}) copy-start(pred[8]{0:T(512)(128)(4,1)} %broadcast_compare_fusion.6) | copy-start | bytes 28
  33.6 8.7 %collective-permute-start = (f32[48,1024]{1,0:T(8,128)S(1)}, f32[48,1024]{1,0:T(8,128)S(1)}, u32[]{:S(2)}, u32[]{:S(2)}) collective-permute-start(f32[48,1024]{1,0:T(8,128)S(1)} %bitcast.130), channel_id=1, source_target_pairs={{0,3},{1,0},{2,1},{3,2},{4,7},{5,4},{6,5},{7,6},{8,11},{9,8},{10,9... | collective-permute-start | bytes 589832 | tf_op jit(solution)/shard_map/ppermute | solution.py:120
  37.6 7.7 %collective-permute-start.15 = (bf16[4,97,256]{2,0,1:T(4,128)(2,1)S(1)}, bf16[4,97,256]{2,0,1:T(4,128)(2,1)S(1)}, u32[]{:S(2)}, u32[]{:S(2)}) collective-permute-start(bf16[4,97,256]{2,0,1:T(4,128)(2,1)S(1)} %select_select_fusion.2), channel_id=1, source_target_pairs={{0,4},{4,8},{8,12},{12,16},{16,20},{20,24},{24,28},{28,0},{1,5},{5... | collective-permute-start | bytes 595976 | tf_op jit(solution)/shard_map/ppermute | solution.py:105
  37.6 9.1 %collective-permute-start.14 = (bf16[4,97,256]{2,0,1:T(4,128)(2,1)S(1)}, bf16[4,97,256]{2,0,1:T(4,128)(2,1)S(1)}, u32[]{:S(2)}, u32[]{:S(2)}) collective-permute-start(bf16[4,97,256]{2,0,1:T(4,128)(2,1)S(1)} %select_select_fusion.2), channel_id=1, source_target_pairs={{0,8},{4,12},{8,16},{12,20},{16,24},{20,28},{24,0},{28,4},{1,9},{5... | collective-permute-start | bytes 595976 | tf_op jit(solution)/shard_map/ppermute | solution.py:105
  39.4 14.8 %collective-permute-start.13 = (bf16[4,97,256]{2,0,1:T(4,128)(2,1)S(1)}, bf16[4,97,256]{2,0,1:T(4,128)(2,1)S(1)}, u32[]{:S(2)}, u32[]{:S(2)}) collective-permute-start(bf16[4,97,256]{2,0,1:T(4,128)(2,1)S(1)} %select_select_fusion.2), channel_id=1, source_target_pairs={{0,12},{4,16},{8,20},{12,24},{16,28},{20,0},{24,4},{28,8},{1,13},{... | collective-permute-start | bytes 595976 | tf_op jit(solution)/shard_map/ppermute | solution.py:105
  41.8 13.6 %collective-permute-start.12 = (bf16[4,97,256]{2,0,1:T(4,128)(2,1)S(1)}, bf16[4,97,256]{2,0,1:T(4,128)(2,1)S(1)}, u32[]{:S(2)}, u32[]{:S(2)}) collective-permute-start(bf16[4,97,256]{2,0,1:T(4,128)(2,1)S(1)} %select_select_fusion.2), channel_id=1, source_target_pairs={{0,16},{4,20},{8,24},{12,28},{16,0},{20,4},{24,8},{28,12},{1,17},{... | collective-permute-start | bytes 595976 | tf_op jit(solution)/shard_map/ppermute | solution.py:105
  42.3 15.3 %collective-permute-start.11 = (bf16[4,97,256]{2,0,1:T(4,128)(2,1)S(1)}, bf16[4,97,256]{2,0,1:T(4,128)(2,1)S(1)}, u32[]{:S(2)}, u32[]{:S(2)}) collective-permute-start(bf16[4,97,256]{2,0,1:T(4,128)(2,1)S(1)} %select_select_fusion.2), channel_id=1, source_target_pairs={{0,20},{4,24},{8,28},{12,0},{16,4},{20,8},{24,12},{28,16},{1,21},{... | collective-permute-start | bytes 595976 | tf_op jit(solution)/shard_map/ppermute | solution.py:105
  45.3 12.9 %collective-permute-start.10 = (bf16[4,97,256]{2,0,1:T(4,128)(2,1)S(1)}, bf16[4,97,256]{2,0,1:T(4,128)(2,1)S(1)}, u32[]{:S(2)}, u32[]{:S(2)}) collective-permute-start(bf16[4,97,256]{2,0,1:T(4,128)(2,1)S(1)} %select_select_fusion.2), channel_id=1, source_target_pairs={{0,24},{4,28},{8,0},{12,4},{16,8},{20,12},{24,16},{28,20},{1,25},{... | collective-permute-start | bytes 595976 | tf_op jit(solution)/shard_map/ppermute | solution.py:105
  46.7 11.5 %collective-permute-start.9 = (bf16[4,97,256]{2,0,1:T(4,128)(2,1)S(1)}, bf16[4,97,256]{2,0,1:T(4,128)(2,1)S(1)}, u32[]{:S(2)}, u32[]{:S(2)}) collective-permute-start(bf16[4,97,256]{2,0,1:T(4,128)(2,1)S(1)} %select_select_fusion.2), channel_id=1, source_target_pairs={{0,28},{4,0},{8,4},{12,8},{16,12},{20,16},{24,20},{28,24},{1,29},{... | collective-permute-start | bytes 595976 | tf_op jit(solution)/shard_map/ppermute | solution.py:105
  54.2 8.4 %collective-permute-start.6 = (bf16[48,1024]{1,0:T(8,128)(2,1)S(1)}, bf16[48,1024]{1,0:T(8,128)(2,1)S(1)}, u32[]{:S(2)}, u32[]{:S(2)}) collective-permute-start(bf16[48,1024]{1,0:T(8,128)(2,1)S(1)} %divide_convert_fusion), channel_id=1, source_target_pairs={{0,3},{1,0},{2,1},{3,2},{4,7},{5,4},{6,5},{7,6},{8,11},{9,8},{10,9... | collective-permute-start | bytes 294920 | tf_op jit(solution)/shard_map/ppermute | solution.py:105
  55.4 7.4 %collective-permute-start.7 = (bf16[48,1024]{1,0:T(8,128)(2,1)S(1)}, bf16[48,1024]{1,0:T(8,128)(2,1)S(1)}, u32[]{:S(2)}, u32[]{:S(2)}) collective-permute-start(bf16[48,1024]{1,0:T(8,128)(2,1)S(1)} %divide_convert_fusion), channel_id=1, source_target_pairs={{0,2},{1,3},{2,0},{3,1},{4,6},{5,7},{6,4},{7,5},{8,10},{9,11},{10,... | collective-permute-start | bytes 294920 | tf_op jit(solution)/shard_map/ppermute | solution.py:105
  57.6 6.7 %collective-permute-start.8 = (bf16[48,1024]{1,0:T(8,128)(2,1)S(1)}, bf16[48,1024]{1,0:T(8,128)(2,1)S(1)}, u32[]{:S(2)}, u32[]{:S(2)}) collective-permute-start(bf16[48,1024]{1,0:T(8,128)(2,1)S(1)} %divide_convert_fusion), channel_id=1, source_target_pairs={{0,1},{1,2},{2,3},{3,0},{4,5},{5,6},{6,7},{7,4},{8,9},{9,10},{10,1... | collective-permute-start | bytes 294920 | tf_op jit(solution)/shard_map/ppermute | solution.py:105
  70.8 32.7 %copy-start.2 = (f32[384,1024]{1,0:T(8,128)}, f32[384,1024]{1,0:T(8,128)S(1)}, u32[]{:S(2)}) copy-start(f32[384,1024]{1,0:T(8,128)S(1)} %convolution_multiply_fusion) | copy-start | bytes 4718596
  70.8 19.9 %copy-start.1 = (bf16[128,4096]{1,0:T(8,128)(2,1)S(1)}, bf16[128,4096]{1,0:T(8,128)(2,1)}, u32[]{:S(2)}) copy-start(bf16[128,4096]{1,0:T(8,128)(2,1)} %param.10) | copy-start | bytes 3145732
  70.8 19.9 %copy-start.26 = (f32[128]{0:T(128)S(1)}, f32[128]{0:T(128)}, u32[]{:S(2)}) copy-start(f32[128]{0:T(128)} %copy-done.25) | copy-start | bytes 1540
  70.8 19.9 %copy-start.27 = (s32[1,128]{1,0:T(1,128)S(1)}, s32[1,128]{1,0:T(1,128)}, u32[]{:S(2)}) copy-start(s32[1,128]{1,0:T(1,128)} %param.11) | copy-start | bytes 1540
  93.3 6.5 %collective-permute-start.22 = (f32[28672]{0:T(1024)S(1)}, f32[28672]{0:T(1024)S(1)}, u32[]{:S(2)}, u32[]{:S(2)}) collective-permute-start(f32[28672]{0:T(1024)S(1)} %get-tuple-element.35), channel_id=1, source_target_pairs={{0,4},{4,8},{8,12},{12,16},{16,20},{20,24},{24,28},{28,0},{1,5},{5... | collective-permute-start | bytes 344072 | tf_op jit(solution)/shard_map/ppermute | solution.py:133
  93.4 7.7 %collective-permute-start.21 = (f32[28672]{0:T(1024)S(1)}, f32[28672]{0:T(1024)S(1)}, u32[]{:S(2)}, u32[]{:S(2)}) collective-permute-start(f32[28672]{0:T(1024)S(1)} %get-tuple-element.34), channel_id=1, source_target_pairs={{0,8},{4,12},{8,16},{12,20},{16,24},{20,28},{24,0},{28,4},{1,9},{5... | collective-permute-start | bytes 344072 | tf_op jit(solution)/shard_map/ppermute | solution.py:133
  95.3 11.3 %collective-permute-start.20 = (f32[28672]{0:T(1024)S(1)}, f32[28672]{0:T(1024)S(1)}, u32[]{:S(2)}, u32[]{:S(2)}) collective-permute-start(f32[28672]{0:T(1024)S(1)} %get-tuple-element.33), channel_id=1, source_target_pairs={{0,12},{4,16},{8,20},{12,24},{16,28},{20,0},{24,4},{28,8},{1,13},{... | collective-permute-start | bytes 344072 | tf_op jit(solution)/shard_map/ppermute | solution.py:133
  96.9 9.7 %collective-permute-start.19 = (f32[28672]{0:T(1024)S(1)}, f32[28672]{0:T(1024)S(1)}, u32[]{:S(2)}, u32[]{:S(2)}) collective-permute-start(f32[28672]{0:T(1024)S(1)} %get-tuple-element.32), channel_id=1, source_target_pairs={{0,16},{4,20},{8,24},{12,28},{16,0},{20,4},{24,8},{28,12},{1,17},{... | collective-permute-start | bytes 344072 | tf_op jit(solution)/shard_map/ppermute | solution.py:133
  98.1 8.5 %collective-permute-start.18 = (f32[28672]{0:T(1024)S(1)}, f32[28672]{0:T(1024)S(1)}, u32[]{:S(2)}, u32[]{:S(2)}) collective-permute-start(f32[28672]{0:T(1024)S(1)} %get-tuple-element.31), channel_id=1, source_target_pairs={{0,20},{4,24},{8,28},{12,0},{16,4},{20,8},{24,12},{28,16},{1,21},{... | collective-permute-start | bytes 344072 | tf_op jit(solution)/shard_map/ppermute | solution.py:133
  99.8 13.1 %copy-start.28 = (pred[384]{0:T(512)(128)(4,1)S(1)}, pred[384]{0:T(512)(128)(4,1)}, u32[]{:S(2)}) copy-start(pred[384]{0:T(512)(128)(4,1)} %broadcast_in_dim.621) | copy-start | bytes 1156
  99.8 13.1 %copy-start.29 = (pred[384]{0:T(512)(128)(4,1)S(1)}, pred[384]{0:T(512)(128)(4,1)}, u32[]{:S(2)}) copy-start(pred[384]{0:T(512)(128)(4,1)} %broadcast_in_dim.616) | copy-start | bytes 1156
  99.8 13.1 %copy-start.30 = (pred[384]{0:T(512)(128)(4,1)S(1)}, pred[384]{0:T(512)(128)(4,1)}, u32[]{:S(2)}) copy-start(pred[384]{0:T(512)(128)(4,1)} %broadcast_in_dim.611) | copy-start | bytes 1156
  99.8 13.1 %copy-start.31 = (pred[384]{0:T(512)(128)(4,1)S(1)}, pred[384]{0:T(512)(128)(4,1)}, u32[]{:S(2)}) copy-start(pred[384]{0:T(512)(128)(4,1)} %broadcast_in_dim.606) | copy-start | bytes 1156
  99.8 13.1 %copy-start.32 = (pred[384]{0:T(512)(128)(4,1)S(1)}, pred[384]{0:T(512)(128)(4,1)}, u32[]{:S(2)}) copy-start(pred[384]{0:T(512)(128)(4,1)} %broadcast_in_dim.601) | copy-start | bytes 1156
  99.8 13.1 %copy-start.33 = (pred[384]{0:T(512)(128)(4,1)S(1)}, pred[384]{0:T(512)(128)(4,1)}, u32[]{:S(2)}) copy-start(pred[384]{0:T(512)(128)(4,1)} %broadcast_in_dim.596) | copy-start | bytes 1156
  99.8 13.1 %copy-start.34 = (pred[384]{0:T(512)(128)(4,1)S(1)}, pred[384]{0:T(512)(128)(4,1)}, u32[]{:S(2)}) copy-start(pred[384]{0:T(512)(128)(4,1)} %broadcast_in_dim.591) | copy-start | bytes 1156
  99.9 6.8 %collective-permute-start.17 = (f32[28672]{0:T(1024)S(1)}, f32[28672]{0:T(1024)S(1)}, u32[]{:S(2)}, u32[]{:S(2)}) collective-permute-start(f32[28672]{0:T(1024)S(1)} %get-tuple-element.30), channel_id=1, source_target_pairs={{0,24},{4,28},{8,0},{12,4},{16,8},{20,12},{24,16},{28,20},{1,25},{... | collective-permute-start | bytes 344072 | tf_op jit(solution)/shard_map/ppermute | solution.py:133
  101.1 5.5 %collective-permute-start.16 = (f32[28672]{0:T(1024)S(1)}, f32[28672]{0:T(1024)}, u32[]{:S(2)}, u32[]{:S(2)}) collective-permute-start(f32[28672]{0:T(1024)S(1)} %get-tuple-element.29), channel_id=1, source_target_pairs={{0,28},{4,0},{8,4},{12,8},{16,12},{20,16},{24,20},{28,24},{1,29},{... | collective-permute-start | bytes 344072 | tf_op jit(solution)/shard_map/ppermute | solution.py:133
  103.5 12.0 %copy-start.5 = (pred[4]{0:T(512)(128)(4,1)S(1)}, pred[4]{0:T(512)(128)(4,1)}, u32[]{:S(2)}) copy-start(pred[4]{0:T(512)(128)(4,1)} %copy-done.4) | copy-start | bytes 16
  103.5 12.0 %copy-start.7 = (pred[4]{0:T(512)(128)(4,1)S(1)}, pred[4]{0:T(512)(128)(4,1)}, u32[]{:S(2)}) copy-start(pred[4]{0:T(512)(128)(4,1)} %copy-done.6) | copy-start | bytes 16
  103.5 12.0 %copy-start.9 = (pred[4]{0:T(512)(128)(4,1)S(1)}, pred[4]{0:T(512)(128)(4,1)}, u32[]{:S(2)}) copy-start(pred[4]{0:T(512)(128)(4,1)} %copy-done.8) | copy-start | bytes 16
  107.6 7.9 %collective-permute-start.25 = (f32[4096]{0:T(1024)S(1)}, f32[4096]{0:T(1024)S(1)}, u32[]{:S(2)}, u32[]{:S(2)}) collective-permute-start(f32[4096]{0:T(1024)S(1)} %select_reduce_fusion.2), channel_id=1, source_target_pairs={{0,1},{1,2},{2,3},{3,0},{4,5},{5,6},{6,7},{7,4},{8,9},{9,10},{10,1... | collective-permute-start | bytes 49160 | tf_op jit(solution)/shard_map/ppermute | solution.py:105
  107.6 7.9 %collective-permute-start.24 = (f32[4096]{0:T(1024)S(1)}, f32[4096]{0:T(1024)S(1)}, u32[]{:S(2)}, u32[]{:S(2)}) collective-permute-start(f32[4096]{0:T(1024)S(1)} %select_reduce_fusion.2), channel_id=1, source_target_pairs={{0,2},{1,3},{2,0},{3,1},{4,6},{5,7},{6,4},{7,5},{8,10},{9,11},{10,... | collective-permute-start | bytes 49160 | tf_op jit(solution)/shard_map/ppermute | solution.py:105
  110.1 5.5 %collective-permute-start.23 = (f32[4096]{0:T(1024)S(1)}, f32[4096]{0:T(1024)S(1)}, u32[]{:S(2)}, u32[]{:S(2)}) collective-permute-start(f32[4096]{0:T(1024)S(1)} %select_reduce_fusion.2), channel_id=1, source_target_pairs={{0,3},{1,0},{2,1},{3,2},{4,7},{5,4},{6,5},{7,6},{8,11},{9,8},{10,9... | collective-permute-start | bytes 49160 | tf_op jit(solution)/shard_map/ppermute | solution.py:105
  (13 other events, 80.9 us)

commit v12 on v11

--- a/solution.py
+++ b/solution.py
@@ -234,9 +234,11 @@
     hidden_grad = (inv_rms * scaled - states * inv_rms**3 * inner).astype(jnp.bfloat16)
     gain_dp, pieces = spread_with_sum(gain_part, pieces.astype(jnp.float32), "dp")
     gain_grad = sum_blocks(gain_dp, "fsdp")
-    pooled_cols = pieces.reshape(pair_count, slice_width).astype(jnp.bfloat16)
     proj_grad = lax.dot_general(
-        pooled_cols, grad_low_cols, contract_first, preferred_element_type=jnp.float32
+        pieces.astype(jnp.bfloat16),
+        grad_low_cols.reshape(data_count, rows, width),
+        (((0, 1), (0, 1)), ((), ())),
+        preferred_element_type=jnp.float32,
     )
     return (mean_loss, query_grad, region_grad, hidden_grad, gain_grad, proj_grad)
 

time: 118 us -> 121 us (1.025)
  waiting for transfers between devices: 7.52 us -> 14.6 us
  local copies, waits for them, and re-layouts: 22.9 us -> 18.6 us
  starting transfers between devices: 36.1 us -> 38.7 us
  matrix products: 11.2 us -> 9.19 us
    broadcast_in_dim x17 -> x3, local copies, waits for them, and re-layouts: 9.63 us -> 0.33 us  [arrange(): out = jnp.where(source == s, copies[s][None], out)]
    ppermute x3, waiting for transfers between devices: 0.01 us -> 5.37 us  [scatter_sum(): lax.ppermute(piece, axis, [(i, (i + s) % n) for i in range(n)])]
    ppermute x7, waiting for transfers between devices: 0.02 us -> 4.12 us  [spread_with_sum(): arrived = lax.ppermute(payload, axis, [(i, (i + s) % n) for i in range(n)])]
    ppermute x7, starting transfers between devices: 8.3 us -> 12.4 us  [spread_with_sum(): arrived = lax.ppermute(payload, axis, [(i, (i + s) % n) for i in range(n)])]
    slice x14, local copies, waits for them, and re-layouts: 1.24 us -> 4.8 us  [spread_with_sum(): got.append(arrived[size:].reshape(piece.shape))]
    slice x7, local copies, waits for them, and re-layouts: 0.74 us -> 3.6 us  [spread_with_sum(): sums.append(arrived[:size])]
    unnamed x90 -> x74, local copies, waits for them, and re-layouts: 6.5 us -> 4.09 us
    ppermute x16, waiting for transfers between devices: 7.5 us -> 5.11 us  [gather_blocks(): lax.ppermute(x, axis, [(i, (i + s) % n) for i in range(n)])]
  transfers between devices with their start and end apart: 26 -> 26, of which waited for: 4 -> 7; matrix products, arithmetic and copies ran while one was open for 31% -> 26% of each run, Pallas kernels for 0% -> 0%
where the time goes in v12:
time: 121 us; the launch traced here: 120 us
  starting transfers between devices  38.7 us (32%)
  blocking collectives  18.7 us (15%)
  local copies, waits for them, and re-layouts  18.6 us (15%)
  other arithmetic  16.9 us (14%)
  waiting for transfers between devices  14.6 us (12%)
  matrix products  9.19 us (8%)
  between operations  3.18 us (3%)
    ppermute x16, starting transfers between devices, gather_blocks(): lax.ppermute(x, axis, [(i, (i + s) % n) for i in range(n)])  22.1 us
    all_gather x1, blocking collectives, local_small(): mean_grad = lax.all_gather(mean_part, 'fsdp', axis=1, tiled=True)  18.7 us
    ppermute x7, starting transfers between devices, spread_with_sum(): arrived = lax.ppermute(payload, axis, [(i, (i + s) % n) for i in range(n)])  12.4 us
    select_n x3, other arithmetic, arrange(): out = jnp.where(source == s, copies[s][None], out)  5.56 us
    ppermute x3, waiting for transfers between devices, scatter_sum(): lax.ppermute(piece, axis, [(i, (i + s) % n) for i in range(n)])  5.37 us
    ppermute x16, waiting for transfers between devices, gather_blocks(): lax.ppermute(x, axis, [(i, (i + s) % n) for i in range(n)])  5.11 us
    slice x14, local copies, waits for them, and re-layouts, spread_with_sum(): got.append(arrived[size:].reshape(piece.shape))  4.8 us
    ppermute x3, starting transfers between devices, scatter_sum(): lax.ppermute(piece, axis, [(i, (i + s) % n) for i in range(n)])  4.18 us
  transfers between devices with their start and end apart: 26, of which 7 were waited for; matrix products, arithmetic and copies ran while one was open for 26% of the time, Pallas kernels for 0%

profile of v12, /device:TPU:0, one launch (start us, length us, event | category | flops | bytes accessed | tf_op | source)
XLA Modules:
  0.0 119.7 jit_solution(15250093123395121282)
XLA Ops:
  0.6 0.8 and_select_fusion.2
  1.5 0.7 constant_dynamic-update-slice_fusion.2
  2.9 0.7 constant_dynamic-update-slice_fusion.1
  3.7 3.0 %collective-permute-start.5 = (bf16[97,256]{1,0:T(8,128)(2,1)S(1)}, bf16[97,256]{1,0:T(8,128)(2,1)}, u32[]{:S(2)}, u32[]{:S(2)}) collective-permute-start(bf16[97,256]{1,0:T(8,128)(2,1)S(1)} %constant_dynamic-update-slice_fusion), channel_id=1, source_target_pairs={{0,1},{1,2},{2,3},{3,0},{4,5},{5,6},{6,7},{7,4},{8,9},{9,10},{10,1... | collective-permute-start | bytes 149000 | tf_op jit(solution)/shard_map/ppermute | solution.py:105
  6.7 2.6 %collective-permute-start.4 = (bf16[97,256]{1,0:T(8,128)(2,1)S(1)}, bf16[97,256]{1,0:T(8,128)(2,1)}, u32[]{:S(2)}, u32[]{:S(2)}) collective-permute-start(bf16[97,256]{1,0:T(8,128)(2,1)S(1)} %constant_dynamic-update-slice_fusion), channel_id=1, source_target_pairs={{0,2},{1,3},{2,0},{3,1},{4,6},{5,7},{6,4},{7,5},{8,10},{9,11},{10,... | collective-permute-start | bytes 149000 | tf_op jit(solution)/shard_map/ppermute | solution.py:105
  9.3 1.3 %collective-permute-start.3 = (bf16[97,256]{1,0:T(8,128)(2,1)S(1)}, bf16[97,256]{1,0:T(8,128)(2,1)}, u32[]{:S(2)}, u32[]{:S(2)}) collective-permute-start(bf16[97,256]{1,0:T(8,128)(2,1)S(1)} %constant_dynamic-update-slice_fusion), channel_id=1, source_target_pairs={{0,3},{1,0},{2,1},{3,2},{4,7},{5,4},{6,5},{7,6},{8,11},{9,8},{10,9... | collective-permute-start | bytes 149000 | tf_op jit(solution)/shard_map/ppermute | solution.py:105
  10.7 1.5 %fusion = f32[128]{0:T(128)S(1)} fusion(bf16[128,4096]{1,0:T(8,128)(2,1)} %param.10), kind=kLoop, calls=%fused_computation.5 | loop fusion | flops 1572736 | bytes 1049088 | tf_op jit(solution)/shard_map/reduce_sum | solution.py:167
  13.4 2.6 %fusion.9 = f32[48,4096]{1,0:T(8,128)} fusion(bf16[128,4096]{1,0:T(8,128)(2,1)} %param.10, f32[4096]{0:T(1024)S(1)} %convert_element_type.82, f32[128]{0:T(128)S(1)} %get-tuple-element.37, s32[128]{0:T(128)} %bitcast.110), kind=kOutput, calls=%fused_computation.19 | convolution fusion | flops 52434944 | bytes 1852416 | tf_op jit(solution)/shard_map/dot_general | solution.py:171
  16.0 1.7 %reshape.419 = f32[48,4,1024]{2,1,0:T(4,128)S(1)} reshape(f32[48,4096]{1,0:T(8,128)} %fusion.9) | data formatting | bytes 1572864 | tf_op jit(solution)/shard_map/reshape | solution.py:175
  17.7 0.8 constant_dynamic-slice_fusion.11
  18.8 0.9 collective-permute-start.2
  22.5 3.0 %collective-permute-start = (f32[48,1024]{1,0:T(8,128)S(1)}, f32[48,1024]{1,0:T(8,128)S(1)}, u32[]{:S(2)}, u32[]{:S(2)}) collective-permute-start(f32[48,1024]{1,0:T(8,128)S(1)} %bitcast.104), channel_id=1, source_target_pairs={{0,3},{1,0},{2,1},{3,2},{4,7},{5,4},{6,5},{7,6},{8,11},{9,8},{10,9... | collective-permute-start | bytes 589832 | tf_op jit(solution)/shard_map/ppermute | solution.py:120
  25.6 1.1 select_select_fusion.2
  26.8 1.7 %collective-permute-start.14 = (bf16[4,97,256]{2,0,1:T(4,128)(2,1)S(1)}, bf16[4,97,256]{2,0,1:T(4,128)(2,1)S(1)}, u32[]{:S(2)}, u32[]{:S(2)}) collective-permute-start(bf16[4,97,256]{2,0,1:T(4,128)(2,1)S(1)} %select_select_fusion.2), channel_id=1, source_target_pairs={{0,8},{4,12},{8,16},{12,20},{16,24},{20,28},{24,0},{28,4},{1,9},{5... | collective-permute-start | bytes 595976 | tf_op jit(solution)/shard_map/ppermute | solution.py:105
  28.7 5.3 %collective-permute-done.1 = f32[48,1024]{1,0:T(8,128)S(1)} collective-permute-done((f32[48,1024]{1,0:T(8,128)S(1)}, f32[48,1024]{1,0:T(8,128)S(1)}, u32[]{:S(2)}, u32[]{:S(2)}) %collective-permute-start.1) | collective-permute-done | bytes 196640 | tf_op jit(solution)/shard_map/ppermute | solution.py:120
  34.0 0.8 collective-permute-start.13
  34.8 1.5 %collective-permute-start.12 = (bf16[4,97,256]{2,0,1:T(4,128)(2,1)S(1)}, bf16[4,97,256]{2,0,1:T(4,128)(2,1)S(1)}, u32[]{:S(2)}, u32[]{:S(2)}) collective-permute-start(bf16[4,97,256]{2,0,1:T(4,128)(2,1)S(1)} %select_select_fusion.2), channel_id=1, source_target_pairs={{0,16},{4,20},{8,24},{12,28},{16,0},{20,4},{24,8},{28,12},{1,17},{... | collective-permute-start | bytes 595976 | tf_op jit(solution)/shard_map/ppermute | solution.py:105
  37.0 0.9 select_reduce_fusion
  37.9 1.9 %collective-permute-start.10 = (bf16[4,97,256]{2,0,1:T(4,128)(2,1)S(1)}, bf16[4,97,256]{2,0,1:T(4,128)(2,1)S(1)}, u32[]{:S(2)}, u32[]{:S(2)}) collective-permute-start(bf16[4,97,256]{2,0,1:T(4,128)(2,1)S(1)} %select_select_fusion.2), channel_id=1, source_target_pairs={{0,24},{4,28},{8,0},{12,4},{16,8},{20,12},{24,16},{28,20},{1,25},{... | collective-permute-start | bytes 595976 | tf_op jit(solution)/shard_map/ppermute | solution.py:105
  39.8 1.4 %collective-permute-start.9 = (bf16[4,97,256]{2,0,1:T(4,128)(2,1)S(1)}, bf16[4,97,256]{2,0,1:T(4,128)(2,1)S(1)}, u32[]{:S(2)}, u32[]{:S(2)}) collective-permute-start(bf16[4,97,256]{2,0,1:T(4,128)(2,1)S(1)} %select_select_fusion.2), channel_id=1, source_target_pairs={{0,28},{4,0},{8,4},{12,8},{16,12},{20,16},{24,20},{28,24},{1,29},{... | collective-permute-start | bytes 595976 | tf_op jit(solution)/shard_map/ppermute | solution.py:105
  41.5 0.9 collective-permute-done.13
  42.4 1.4 %collective-permute-start.8 = (bf16[48,1024]{1,0:T(8,128)(2,1)S(1)}, bf16[48,1024]{1,0:T(8,128)(2,1)S(1)}, u32[]{:S(2)}, u32[]{:S(2)}) collective-permute-start(bf16[48,1024]{1,0:T(8,128)(2,1)S(1)} %divide_convert_fusion), channel_id=1, source_target_pairs={{0,1},{1,2},{2,3},{3,0},{4,5},{5,6},{6,7},{7,4},{8,9},{9,10},{10,1... | collective-permute-start | bytes 294920 | tf_op jit(solution)/shard_map/ppermute | solution.py:105
  43.8 0.8 collective-permute-done.12
  44.5 0.9 collective-permute-start.7
  45.4 1.5 %collective-permute-done.11 = bf16[4,97,256]{2,0,1:T(4,128)(2,1)S(1)} collective-permute-done((bf16[4,97,256]{2,0,1:T(4,128)(2,1)S(1)}, bf16[4,97,256]{2,0,1:T(4,128)(2,1)S(1)}, u32[]{:S(2)}, u32[]{:S(2)}) %collective-permute-start.11) | collective-permute-done | bytes 198688 | tf_op jit(solution)/shard_map/ppermute | solution.py:105
  46.9 1.0 collective-permute-start.6
  48.0 4.3 %select_select_fusion = bf16[8,4,97,256]{3,1,2,0:T(4,128)(2,1)S(1)} fusion(pred[8]{0:T(512)(128)(4,1)S(1)} %copy-done.19, pred[8]{0:T(512)(128)(4,1)S(1)} %copy-done.9, pred[8]{0:T(512)(128)(4,1)S(1)} %copy-done.11, pred[8]{0:T(512)(128)(4,1)S(1)} %copy-done.13, pred[8]{0:T(512)(128)(4,1)S(1)} %copy-done.15, pred[8]{0:T(512)(128)(4,1)S(1)} %copy-done.21, ...), kind=kLoop, calls=%fused_computation.14 | loop fusion | flops 5562368 | bytes 3178552 | tf_op jit(solution)/shard_map/jit(_where)/select_n | solution.py:98
  52.3 1.9 %collective-permute-done.6 = bf16[48,1024]{1,0:T(8,128)(2,1)S(1)} collective-permute-done((bf16[48,1024]{1,0:T(8,128)(2,1)S(1)}, bf16[48,1024]{1,0:T(8,128)(2,1)S(1)}, u32[]{:S(2)}, u32[]{:S(2)}) %collective-permute-start.6) | collective-permute-done | bytes 98336 | tf_op jit(solution)/shard_map/ppermute | solution.py:105
  55.2 1.6 %fusion.44 = (bf16[8,4,48,256]{3,1,2,0:T(4,128)(2,1)}, bf16[8,4,48,256]{3,1,2,0:T(4,128)(2,1)S(1)}) fusion(bf16[8,4,97,256]{3,1,2,0:T(4,128)(2,1)S(1)} %select_select_fusion), kind=kLoop, calls=%fused_computation.134 | loop fusion | bytes 3145728 | tf_op jit(solution)/shard_map/slice | solution.py:186
  57.0 1.3 %copy.26 = bf16[48,8,4,256]{3,1,2,0:T(8,128)(2,1)S(1)} copy(bf16[48,8,4,256]{3,2,1,0:T(4,128)(2,1)} %bitcast.79) | data formatting | bytes 1572864
  60.8 0.7 fusion.32
  61.6 18.7 %all_gather.3 = f32[48,4096]{1,0:T(8,128)S(1)} all-gather(f32[48,1024]{1,0:T(8,128)S(1)} %fusion.32), channel_id=1, replica_groups=mesh['dp'=8,'fsdp'=4] {'fsdp'}, dimensions={1}, use_global_device_ids=true | all-gather | bytes 983040 | tf_op jit(solution)/shard_map/all_gather | solution.py:222
  80.2 1.6 %fusion.8 = (f32[4096]{0:T(1024)S(1)}, f32[128]{0:T(128)S(1)}, f32[128,4096]{1,0:T(8,128)S(1)}) fusion(bf16[128,4096]{1,0:T(8,128)(2,1)S(1)} %copy-done.1, f32[128]{0:T(128)S(1)} %copy-done.25, f32[4096]{0:T(1024)S(1)} %convert_element_type.82, f32[48,4096]{1,0:T(8,128)S(1)} %all_gather.3, f32[48]{0:T(128)S(1)} %convert_reduce_fusion, s32[128]{0:T(128)S(1)} %bitcast.111), kind=kOutput, calls=%fused_computation.13 | convolution fusion | flops 305858432 | bytes 3966656 | tf_op jit(solution)/shard_map/dot_general | solution.py:224
  82.7 6.2 %collective-permute-start.16 = (f32[28672]{0:T(1024)S(1)}, f32[28672]{0:T(1024)S(1)}, u32[]{:S(2)}, u32[]{:S(2)}) collective-permute-start(f32[28672]{0:T(1024)S(1)} %get-tuple-element.29), channel_id=1, source_target_pairs={{0,28},{4,0},{8,4},{12,8},{16,12},{20,16},{24,20},{28,24},{1,29},{... | collective-permute-start | bytes 344072 | tf_op jit(solution)/shard_map/ppermute | solution.py:133
  88.8 3.1 %collective-permute-start.17 = (f32[28672]{0:T(1024)S(1)}, f32[28672]{0:T(1024)S(1)}, u32[]{:S(2)}, u32[]{:S(2)}) collective-permute-start(f32[28672]{0:T(1024)S(1)} %get-tuple-element.30), channel_id=1, source_target_pairs={{0,24},{4,28},{8,0},{12,4},{16,8},{20,12},{24,16},{28,20},{1,25},{... | collective-permute-start | bytes 344072 | tf_op jit(solution)/shard_map/ppermute | solution.py:133
  92.0 1.8 %collective-permute-start.19 = (f32[28672]{0:T(1024)S(1)}, f32[28672]{0:T(1024)}, u32[]{:S(2)}, u32[]{:S(2)}) collective-permute-start(f32[28672]{0:T(1024)S(1)} %get-tuple-element.32), channel_id=1, source_target_pairs={{0,16},{4,20},{8,24},{12,28},{16,0},{20,4},{24,8},{28,12},{1,17},{... | collective-permute-start | bytes 344072 | tf_op jit(solution)/shard_map/ppermute | solution.py:133
  93.8 1.6 %fusion.5 = bf16[128,4096]{1,0:T(8,128)(2,1)} fusion(bf16[128,4096]{1,0:T(8,128)(2,1)S(1)} %copy-done.1, f32[128,4096]{1,0:T(8,128)S(1)} %get-tuple-element.42, f32[128]{0:T(128)S(1)} %broadcast_multiply_fusion, f32[128]{0:T(128)S(1)} %copy-done.23, f32[4096]{0:T(1024)S(1)} %convert_element_type.82, f32[128]{0:T(128)S(1)} %copy-done.25), kind=kLoop, calls=%fused_computation.10 | loop fusion | flops 3670016 | bytes 4212224 | tf_op jit(solution)/shard_map/convert_element_type | solution.py:234
  95.5 1.3 %collective-permute-start.21 = (f32[28672]{0:T(1024)S(1)}, f32[28672]{0:T(1024)}, u32[]{:S(2)}, u32[]{:S(2)}) collective-permute-start(f32[28672]{0:T(1024)S(1)} %get-tuple-element.34), channel_id=1, source_target_pairs={{0,8},{4,12},{8,16},{12,20},{16,24},{20,28},{24,0},{28,4},{1,9},{5... | collective-permute-start | bytes 344072 | tf_op jit(solution)/shard_map/ppermute | solution.py:133
  98.1 1.7 %convolution_multiply_fusion.2 = f32[48,256]{1,0:T(8,128)} fusion(bf16[384,1024]{1,0:T(8,128)(2,1)} %bitcast.92, s32[]{:T(128)S(6)} %select_n.367, bf16[384,384]{0,1:T(8,128)(2,1)S(1)} %subtract_convert_fusion, s32[]{:T(128)S(6)} %select_n.366), kind=kOutput, calls=%fused_computation.18 | convolution fusion | flops 9449472 | bytes 282632 | tf_op jit(solution)/shard_map/dot_general | solution.py:215
  100.6 4.1 %collective-permute-done.19 = f32[28672]{0:T(1024)} collective-permute-done((f32[28672]{0:T(1024)S(1)}, f32[28672]{0:T(1024)}, u32[]{:S(2)}, u32[]{:S(2)}) %collective-permute-start.19) | collective-permute-done | bytes 114720 | tf_op jit(solution)/shard_map/ppermute | solution.py:133
  107.9 2.3 %collective-permute-start.24 = (f32[4096]{0:T(1024)S(1)}, f32[4096]{0:T(1024)S(1)}, u32[]{:S(2)}, u32[]{:S(2)}) collective-permute-start(f32[4096]{0:T(1024)S(1)} %select_reduce_fusion.2), channel_id=1, source_target_pairs={{0,2},{1,3},{2,0},{3,1},{4,6},{5,7},{6,4},{7,5},{8,10},{9,11},{10,... | collective-permute-start | bytes 49160 | tf_op jit(solution)/shard_map/ppermute | solution.py:105
  110.2 1.5 %collective-permute-start.23 = (f32[4096]{0:T(1024)S(1)}, f32[4096]{0:T(1024)S(1)}, u32[]{:S(2)}, u32[]{:S(2)}) collective-permute-start(f32[4096]{0:T(1024)S(1)} %select_reduce_fusion.2), channel_id=1, source_target_pairs={{0,3},{1,0},{2,1},{3,2},{4,7},{5,4},{6,5},{7,6},{8,11},{9,8},{10,9... | collective-permute-start | bytes 49160 | tf_op jit(solution)/shard_map/ppermute | solution.py:105
  111.8 0.9 slice.160
  112.7 0.9 slice.161
  113.7 0.9 slice.162
  114.6 0.9 slice.163
  115.6 0.9 slice.164
  116.5 1.3 %convolution_bitcast_fusion = f32[512,256]{1,0:T(8,128)} fusion(bf16[8,48,256]{2,1,0:T(8,128)(2,1)S(1)} %bitcast.103, bf16[48,512]{1,0:T(8,128)(2,1)S(1)} %bitcast.105, bf16[48,512]{1,0:T(8,128)(2,1)S(1)} %slice.146, bf16[48,512]{1,0:T(8,128)(2,1)S(1)} %slice.144, bf16[48,512]{1,0:T(8,128)(2,1)S(1)} %slice.142, bf16[48,512]{1,0:T(8,128)(2,1)S(1)} %slice.140, ...), kind=kOutput, calls=%fused_computation.17 | convolution fusion | flops 102039552 | bytes 1114168 | tf_op jit(solution)/shard_map/dot_general | solution.py:237
  (150 shorter events, 16.2 us)
Async XLA Ops:
  0.6 60.1 %copy-start = (bf16[1024,1024]{1,0:T(8,128)(2,1)S(1)}, bf16[1024,1024]{1,0:T(8,128)(2,1)}, u32[]{:S(2)}) copy-start(bf16[1024,1024]{1,0:T(8,128)(2,1)} %param.13) | copy-start | bytes 6291460
  3.7 18.8 %collective-permute-start.5 = (bf16[97,256]{1,0:T(8,128)(2,1)S(1)}, bf16[97,256]{1,0:T(8,128)(2,1)}, u32[]{:S(2)}, u32[]{:S(2)}) collective-permute-start(bf16[97,256]{1,0:T(8,128)(2,1)S(1)} %constant_dynamic-update-slice_fusion), channel_id=1, source_target_pairs={{0,1},{1,2},{2,3},{3,0},{4,5},{5,6},{6,7},{7,4},{8,9},{9,10},{10,1... | collective-permute-start | bytes 149000 | tf_op jit(solution)/shard_map/ppermute | solution.py:105
  6.7 18.9 %collective-permute-start.4 = (bf16[97,256]{1,0:T(8,128)(2,1)S(1)}, bf16[97,256]{1,0:T(8,128)(2,1)}, u32[]{:S(2)}, u32[]{:S(2)}) collective-permute-start(bf16[97,256]{1,0:T(8,128)(2,1)S(1)} %constant_dynamic-update-slice_fusion), channel_id=1, source_target_pairs={{0,2},{1,3},{2,0},{3,1},{4,6},{5,7},{6,4},{7,5},{8,10},{9,11},{10,... | collective-permute-start | bytes 149000 | tf_op jit(solution)/shard_map/ppermute | solution.py:105
  9.3 16.3 %collective-permute-start.3 = (bf16[97,256]{1,0:T(8,128)(2,1)S(1)}, bf16[97,256]{1,0:T(8,128)(2,1)}, u32[]{:S(2)}, u32[]{:S(2)}) collective-permute-start(bf16[97,256]{1,0:T(8,128)(2,1)S(1)} %constant_dynamic-update-slice_fusion), channel_id=1, source_target_pairs={{0,3},{1,0},{2,1},{3,2},{4,7},{5,4},{6,5},{7,6},{8,11},{9,8},{10,9... | collective-permute-start | bytes 149000 | tf_op jit(solution)/shard_map/ppermute | solution.py:105
  18.6 15.4 %collective-permute-start.1 = (f32[48,1024]{1,0:T(8,128)S(1)}, f32[48,1024]{1,0:T(8,128)S(1)}, u32[]{:S(2)}, u32[]{:S(2)}) collective-permute-start(f32[48,1024]{1,0:T(8,128)S(1)} %bitcast.102), channel_id=1, source_target_pairs={{0,2},{1,3},{2,0},{3,1},{4,6},{5,7},{6,4},{7,5},{8,10},{9,11},{10,... | collective-permute-start | bytes 589832 | tf_op jit(solution)/shard_map/ppermute | solution.py:120
  18.8 15.9 %collective-permute-start.2 = (f32[48,1024]{1,0:T(8,128)S(1)}, f32[48,1024]{1,0:T(8,128)S(1)}, u32[]{:S(2)}, u32[]{:S(2)}) collective-permute-start(f32[48,1024]{1,0:T(8,128)S(1)} %bitcast.101), channel_id=1, source_target_pairs={{0,1},{1,2},{2,3},{3,0},{4,5},{5,6},{6,7},{7,4},{8,9},{9,10},{10,1... | collective-permute-start | bytes 589832 | tf_op jit(solution)/shard_map/ppermute | solution.py:120
  19.7 2.6 %copy-start.3 = (pred[4]{0:T(512)(128)(4,1)}, pred[4]{0:T(512)(128)(4,1)S(1)}, u32[]{:S(2)}) copy-start(pred[4]{0:T(512)(128)(4,1)S(1)} %broadcast_compare_fusion.9) | copy-start | bytes 16
  19.8 2.6 %copy-start.7 = (pred[4]{0:T(512)(128)(4,1)}, pred[4]{0:T(512)(128)(4,1)S(1)}, u32[]{:S(2)}) copy-start(pred[4]{0:T(512)(128)(4,1)S(1)} %get-tuple-element.44) | copy-start | bytes 16
  22.4 25.5 %copy-start.9 = (pred[8]{0:T(512)(128)(4,1)S(1)}, pred[8]{0:T(512)(128)(4,1)}, u32[]{:S(2)}) copy-start(pred[8]{0:T(512)(128)(4,1)} %get-tuple-element.47) | copy-start | bytes 28
  22.4 25.5 %copy-start.11 = (pred[8]{0:T(512)(128)(4,1)S(1)}, pred[8]{0:T(512)(128)(4,1)}, u32[]{:S(2)}) copy-start(pred[8]{0:T(512)(128)(4,1)} %get-tuple-element.48) | copy-start | bytes 28
  22.4 25.5 %copy-start.13 = (pred[8]{0:T(512)(128)(4,1)S(1)}, pred[8]{0:T(512)(128)(4,1)}, u32[]{:S(2)}) copy-start(pred[8]{0:T(512)(128)(4,1)} %get-tuple-element.49) | copy-start | bytes 28
  22.5 25.5 %copy-start.15 = (pred[8]{0:T(512)(128)(4,1)S(1)}, pred[8]{0:T(512)(128)(4,1)}, u32[]{:S(2)}) copy-start(pred[8]{0:T(512)(128)(4,1)} %get-tuple-element.50) | copy-start | bytes 28
  22.5 25.5 %copy-start.17 = (pred[8]{0:T(512)(128)(4,1)S(1)}, pred[8]{0:T(512)(128)(4,1)}, u32[]{:S(2)}) copy-start(pred[8]{0:T(512)(128)(4,1)} %get-tuple-element.45) | copy-start | bytes 28
  22.5 25.5 %copy-start.19 = (pred[8]{0:T(512)(128)(4,1)S(1)}, pred[8]{0:T(512)(128)(4,1)}, u32[]{:S(2)}) copy-start(pred[8]{0:T(512)(128)(4,1)} %get-tuple-element.46) | copy-start | bytes 28
  22.5 25.5 %copy-start.21 = (pred[8]{0:T(512)(128)(4,1)S(1)}, pred[8]{0:T(512)(128)(4,1)}, u32[]{:S(2)}) copy-start(pred[8]{0:T(512)(128)(4,1)} %broadcast_compare_fusion.6) | copy-start | bytes 28
  22.5 13.8 %collective-permute-start = (f32[48,1024]{1,0:T(8,128)S(1)}, f32[48,1024]{1,0:T(8,128)S(1)}, u32[]{:S(2)}, u32[]{:S(2)}) collective-permute-start(f32[48,1024]{1,0:T(8,128)S(1)} %bitcast.104), channel_id=1, source_target_pairs={{0,3},{1,0},{2,1},{3,2},{4,7},{5,4},{6,5},{7,6},{8,11},{9,8},{10,9... | collective-permute-start | bytes 589832 | tf_op jit(solution)/shard_map/ppermute | solution.py:120
  26.7 11.1 %collective-permute-start.15 = (bf16[4,97,256]{2,0,1:T(4,128)(2,1)S(1)}, bf16[4,97,256]{2,0,1:T(4,128)(2,1)S(1)}, u32[]{:S(2)}, u32[]{:S(2)}) collective-permute-start(bf16[4,97,256]{2,0,1:T(4,128)(2,1)S(1)} %select_select_fusion.2), channel_id=1, source_target_pairs={{0,4},{4,8},{8,12},{12,16},{16,20},{20,24},{24,28},{28,0},{1,5},{5... | collective-permute-start | bytes 595976 | tf_op jit(solution)/shard_map/ppermute | solution.py:105
  26.8 13.0 %collective-permute-start.14 = (bf16[4,97,256]{2,0,1:T(4,128)(2,1)S(1)}, bf16[4,97,256]{2,0,1:T(4,128)(2,1)S(1)}, u32[]{:S(2)}, u32[]{:S(2)}) collective-permute-start(bf16[4,97,256]{2,0,1:T(4,128)(2,1)S(1)} %select_select_fusion.2), channel_id=1, source_target_pairs={{0,8},{4,12},{8,16},{12,20},{16,24},{20,28},{24,0},{28,4},{1,9},{5... | collective-permute-start | bytes 595976 | tf_op jit(solution)/shard_map/ppermute | solution.py:105
  34.0 8.4 %collective-permute-start.13 = (bf16[4,97,256]{2,0,1:T(4,128)(2,1)S(1)}, bf16[4,97,256]{2,0,1:T(4,128)(2,1)S(1)}, u32[]{:S(2)}, u32[]{:S(2)}) collective-permute-start(bf16[4,97,256]{2,0,1:T(4,128)(2,1)S(1)} %select_select_fusion.2), channel_id=1, source_target_pairs={{0,12},{4,16},{8,20},{12,24},{16,28},{20,0},{24,4},{28,8},{1,13},{... | collective-permute-start | bytes 595976 | tf_op jit(solution)/shard_map/ppermute | solution.py:105
  34.8 9.7 %collective-permute-start.12 = (bf16[4,97,256]{2,0,1:T(4,128)(2,1)S(1)}, bf16[4,97,256]{2,0,1:T(4,128)(2,1)S(1)}, u32[]{:S(2)}, u32[]{:S(2)}) collective-permute-start(bf16[4,97,256]{2,0,1:T(4,128)(2,1)S(1)} %select_select_fusion.2), channel_id=1, source_target_pairs={{0,16},{4,20},{8,24},{12,28},{16,0},{20,4},{24,8},{28,12},{1,17},{... | collective-permute-start | bytes 595976 | tf_op jit(solution)/shard_map/ppermute | solution.py:105
  36.4 10.5 %collective-permute-start.11 = (bf16[4,97,256]{2,0,1:T(4,128)(2,1)S(1)}, bf16[4,97,256]{2,0,1:T(4,128)(2,1)S(1)}, u32[]{:S(2)}, u32[]{:S(2)}) collective-permute-start(bf16[4,97,256]{2,0,1:T(4,128)(2,1)S(1)} %select_select_fusion.2), channel_id=1, source_target_pairs={{0,20},{4,24},{8,28},{12,0},{16,4},{20,8},{24,12},{28,16},{1,21},{... | collective-permute-start | bytes 595976 | tf_op jit(solution)/shard_map/ppermute | solution.py:105
  37.9 10.1 %collective-permute-start.10 = (bf16[4,97,256]{2,0,1:T(4,128)(2,1)S(1)}, bf16[4,97,256]{2,0,1:T(4,128)(2,1)S(1)}, u32[]{:S(2)}, u32[]{:S(2)}) collective-permute-start(bf16[4,97,256]{2,0,1:T(4,128)(2,1)S(1)} %select_select_fusion.2), channel_id=1, source_target_pairs={{0,24},{4,28},{8,0},{12,4},{16,8},{20,12},{24,16},{28,20},{1,25},{... | collective-permute-start | bytes 595976 | tf_op jit(solution)/shard_map/ppermute | solution.py:105
  39.8 8.2 %collective-permute-start.9 = (bf16[4,97,256]{2,0,1:T(4,128)(2,1)S(1)}, bf16[4,97,256]{2,0,1:T(4,128)(2,1)S(1)}, u32[]{:S(2)}, u32[]{:S(2)}) collective-permute-start(bf16[4,97,256]{2,0,1:T(4,128)(2,1)S(1)} %select_select_fusion.2), channel_id=1, source_target_pairs={{0,28},{4,0},{8,4},{12,8},{16,12},{20,16},{24,20},{28,24},{1,29},{... | collective-permute-start | bytes 595976 | tf_op jit(solution)/shard_map/ppermute | solution.py:105
  42.4 12.4 %collective-permute-start.8 = (bf16[48,1024]{1,0:T(8,128)(2,1)S(1)}, bf16[48,1024]{1,0:T(8,128)(2,1)S(1)}, u32[]{:S(2)}, u32[]{:S(2)}) collective-permute-start(bf16[48,1024]{1,0:T(8,128)(2,1)S(1)} %divide_convert_fusion), channel_id=1, source_target_pairs={{0,1},{1,2},{2,3},{3,0},{4,5},{5,6},{6,7},{7,4},{8,9},{9,10},{10,1... | collective-permute-start | bytes 294920 | tf_op jit(solution)/shard_map/ppermute | solution.py:105
  44.5 10.0 %collective-permute-start.7 = (bf16[48,1024]{1,0:T(8,128)(2,1)S(1)}, bf16[48,1024]{1,0:T(8,128)(2,1)S(1)}, u32[]{:S(2)}, u32[]{:S(2)}) collective-permute-start(bf16[48,1024]{1,0:T(8,128)(2,1)S(1)} %divide_convert_fusion), channel_id=1, source_target_pairs={{0,2},{1,3},{2,0},{3,1},{4,6},{5,7},{6,4},{7,5},{8,10},{9,11},{10,... | collective-permute-start | bytes 294920 | tf_op jit(solution)/shard_map/ppermute | solution.py:105
  46.9 7.3 %collective-permute-start.6 = (bf16[48,1024]{1,0:T(8,128)(2,1)S(1)}, bf16[48,1024]{1,0:T(8,128)(2,1)S(1)}, u32[]{:S(2)}, u32[]{:S(2)}) collective-permute-start(bf16[48,1024]{1,0:T(8,128)(2,1)S(1)} %divide_convert_fusion), channel_id=1, source_target_pairs={{0,3},{1,0},{2,1},{3,2},{4,7},{5,4},{6,5},{7,6},{8,11},{9,8},{10,9... | collective-permute-start | bytes 294920 | tf_op jit(solution)/shard_map/ppermute | solution.py:105
  60.8 19.4 %copy-start.1 = (bf16[128,4096]{1,0:T(8,128)(2,1)S(1)}, bf16[128,4096]{1,0:T(8,128)(2,1)}, u32[]{:S(2)}) copy-start(bf16[128,4096]{1,0:T(8,128)(2,1)} %param.10) | copy-start | bytes 3145732
  60.8 19.4 %copy-start.25 = (f32[128]{0:T(128)S(1)}, f32[128]{0:T(128)}, u32[]{:S(2)}) copy-start(f32[128]{0:T(128)} %copy-done.24) | copy-start | bytes 1540
  60.8 19.4 %copy-start.26 = (s32[1,128]{1,0:T(1,128)S(1)}, s32[1,128]{1,0:T(1,128)}, u32[]{:S(2)}) copy-start(s32[1,128]{1,0:T(1,128)} %param.11) | copy-start | bytes 1540
  81.9 11.9 %copy-start.23 = (f32[128]{0:T(128)S(1)}, f32[128]{0:T(128)}, u32[]{:S(2)}) copy-start(f32[128]{0:T(128)} %get-tuple-element.36) | copy-start | bytes 1540
  82.7 12.8 %collective-permute-start.16 = (f32[28672]{0:T(1024)S(1)}, f32[28672]{0:T(1024)S(1)}, u32[]{:S(2)}, u32[]{:S(2)}) collective-permute-start(f32[28672]{0:T(1024)S(1)} %get-tuple-element.29), channel_id=1, source_target_pairs={{0,28},{4,0},{8,4},{12,8},{16,12},{20,16},{24,20},{28,24},{1,29},{... | collective-permute-start | bytes 344072 | tf_op jit(solution)/shard_map/ppermute | solution.py:133
  88.8 7.9 %collective-permute-start.17 = (f32[28672]{0:T(1024)S(1)}, f32[28672]{0:T(1024)S(1)}, u32[]{:S(2)}, u32[]{:S(2)}) collective-permute-start(f32[28672]{0:T(1024)S(1)} %get-tuple-element.30), channel_id=1, source_target_pairs={{0,24},{4,28},{8,0},{12,4},{16,8},{20,12},{24,16},{28,20},{1,25},{... | collective-permute-start | bytes 344072 | tf_op jit(solution)/shard_map/ppermute | solution.py:133
  92.0 7.9 %collective-permute-start.18 = (f32[28672]{0:T(1024)S(1)}, f32[28672]{0:T(1024)}, u32[]{:S(2)}, u32[]{:S(2)}) collective-permute-start(f32[28672]{0:T(1024)S(1)} %get-tuple-element.31), channel_id=1, source_target_pairs={{0,20},{4,24},{8,28},{12,0},{16,4},{20,8},{24,12},{28,16},{1,21},{... | collective-permute-start | bytes 344072 | tf_op jit(solution)/shard_map/ppermute | solution.py:133
  92.0 12.7 %collective-permute-start.19 = (f32[28672]{0:T(1024)S(1)}, f32[28672]{0:T(1024)}, u32[]{:S(2)}, u32[]{:S(2)}) collective-permute-start(f32[28672]{0:T(1024)S(1)} %get-tuple-element.32), channel_id=1, source_target_pairs={{0,16},{4,20},{8,24},{12,28},{16,0},{20,4},{24,8},{28,12},{1,17},{... | collective-permute-start | bytes 344072 | tf_op jit(solution)/shard_map/ppermute | solution.py:133
  93.8 11.7 %collective-permute-start.20 = (f32[28672]{0:T(1024)S(1)}, f32[28672]{0:T(1024)}, u32[]{:S(2)}, u32[]{:S(2)}) collective-permute-start(f32[28672]{0:T(1024)S(1)} %get-tuple-element.33), channel_id=1, source_target_pairs={{0,12},{4,16},{8,20},{12,24},{16,28},{20,0},{24,4},{28,8},{1,13},{... | collective-permute-start | bytes 344072 | tf_op jit(solution)/shard_map/ppermute | solution.py:133
  93.8 13.8 %copy-start.10 = (pred[8]{0:T(512)(128)(4,1)S(1)}, pred[8]{0:T(512)(128)(4,1)}, u32[]{:S(2)}) copy-start(pred[8]{0:T(512)(128)(4,1)} %get-tuple-element.47) | copy-start | bytes 28
  93.8 13.8 %copy-start.12 = (pred[8]{0:T(512)(128)(4,1)S(1)}, pred[8]{0:T(512)(128)(4,1)}, u32[]{:S(2)}) copy-start(pred[8]{0:T(512)(128)(4,1)} %get-tuple-element.48) | copy-start | bytes 28
  93.8 13.8 %copy-start.14 = (pred[8]{0:T(512)(128)(4,1)S(1)}, pred[8]{0:T(512)(128)(4,1)}, u32[]{:S(2)}) copy-start(pred[8]{0:T(512)(128)(4,1)} %get-tuple-element.49) | copy-start | bytes 28
  93.8 13.8 %copy-start.16 = (pred[8]{0:T(512)(128)(4,1)S(1)}, pred[8]{0:T(512)(128)(4,1)}, u32[]{:S(2)}) copy-start(pred[8]{0:T(512)(128)(4,1)} %get-tuple-element.50) | copy-start | bytes 28
  93.8 13.8 %copy-start.18 = (pred[8]{0:T(512)(128)(4,1)S(1)}, pred[8]{0:T(512)(128)(4,1)}, u32[]{:S(2)}) copy-start(pred[8]{0:T(512)(128)(4,1)} %get-tuple-element.45) | copy-start | bytes 28
  93.8 13.8 %copy-start.20 = (pred[8]{0:T(512)(128)(4,1)S(1)}, pred[8]{0:T(512)(128)(4,1)}, u32[]{:S(2)}) copy-start(pred[8]{0:T(512)(128)(4,1)} %get-tuple-element.46) | copy-start | bytes 28
  93.8 13.8 %copy-start.22 = (pred[8]{0:T(512)(128)(4,1)S(1)}, pred[8]{0:T(512)(128)(4,1)}, u32[]{:S(2)}) copy-start(pred[8]{0:T(512)(128)(4,1)} %broadcast_compare_fusion.6) | copy-start | bytes 28
  95.5 10.7 %collective-permute-start.21 = (f32[28672]{0:T(1024)S(1)}, f32[28672]{0:T(1024)}, u32[]{:S(2)}, u32[]{:S(2)}) collective-permute-start(f32[28672]{0:T(1024)S(1)} %get-tuple-element.34), channel_id=1, source_target_pairs={{0,8},{4,12},{8,16},{12,20},{16,24},{20,28},{24,0},{28,4},{1,9},{5... | collective-permute-start | bytes 344072 | tf_op jit(solution)/shard_map/ppermute | solution.py:133
  96.8 10.1 %collective-permute-start.22 = (f32[28672]{0:T(1024)S(1)}, f32[28672]{0:T(1024)}, u32[]{:S(2)}, u32[]{:S(2)}) collective-permute-start(f32[28672]{0:T(1024)S(1)} %get-tuple-element.35), channel_id=1, source_target_pairs={{0,4},{4,8},{8,12},{12,16},{16,20},{20,24},{24,28},{28,0},{1,5},{5... | collective-permute-start | bytes 344072 | tf_op jit(solution)/shard_map/ppermute | solution.py:133
  107.8 10.0 %collective-permute-start.25 = (f32[4096]{0:T(1024)S(1)}, f32[4096]{0:T(1024)S(1)}, u32[]{:S(2)}, u32[]{:S(2)}) collective-permute-start(f32[4096]{0:T(1024)S(1)} %select_reduce_fusion.2), channel_id=1, source_target_pairs={{0,1},{1,2},{2,3},{3,0},{4,5},{5,6},{6,7},{7,4},{8,9},{9,10},{10,1... | collective-permute-start | bytes 49160 | tf_op jit(solution)/shard_map/ppermute | solution.py:105
  107.9 10.0 %collective-permute-start.24 = (f32[4096]{0:T(1024)S(1)}, f32[4096]{0:T(1024)S(1)}, u32[]{:S(2)}, u32[]{:S(2)}) collective-permute-start(f32[4096]{0:T(1024)S(1)} %select_reduce_fusion.2), channel_id=1, source_target_pairs={{0,2},{1,3},{2,0},{3,1},{4,6},{5,7},{6,4},{7,5},{8,10},{9,11},{10,... | collective-permute-start | bytes 49160 | tf_op jit(solution)/shard_map/ppermute | solution.py:105
  110.2 7.7 %collective-permute-start.23 = (f32[4096]{0:T(1024)S(1)}, f32[4096]{0:T(1024)S(1)}, u32[]{:S(2)}, u32[]{:S(2)}) collective-permute-start(f32[4096]{0:T(1024)S(1)} %select_reduce_fusion.2), channel_id=1, source_target_pairs={{0,3},{1,0},{2,1},{3,2},{4,7},{5,4},{6,5},{7,6},{8,11},{9,8},{10,9... | collective-permute-start | bytes 49160 | tf_op jit(solution)/shard_map/ppermute | solution.py:105
  115.6 2.3 %copy-start.4 = (pred[4]{0:T(512)(128)(4,1)S(1)}, pred[4]{0:T(512)(128)(4,1)}, u32[]{:S(2)}) copy-start(pred[4]{0:T(512)(128)(4,1)} %copy-done.3) | copy-start | bytes 16
  (5 other events, 8.8 us)

commit v13 on v11

--- a/solution.py
+++ b/solution.py
@@ -133,7 +133,7 @@
         arrived = lax.ppermute(payload, axis, [(i, (i + s) % n) for i in range(n)])
         sums.append(arrived[:size])
         got.append(arrived[size:].reshape(piece.shape))
-    return jnp.sum(arrange(sums, me), axis=0), arrange(got, me)
+    return jnp.sum(arrange(sums, me), axis=0), lax.optimization_barrier(arrange(got, me))
 
 
 def local_small(query_cache, region_cache, positive, hidden_states, segment_ids, norm_gain, proj_weight):

time: 118 us -> 111 us (0.941)
  local copies, waits for them, and re-layouts: 22.9 us -> 13.7 us
  starting transfers between devices: 36.1 us -> 38 us
    broadcast_in_dim x17 -> x3, local copies, waits for them, and re-layouts: 9.63 us -> 0.33 us  [arrange(): out = jnp.where(source == s, copies[s][None], out)]
    ppermute x3, waiting for transfers between devices: 0.01 us -> 2.8 us  [scatter_sum(): lax.ppermute(piece, axis, [(i, (i + s) % n) for i in range(n)])]
    ppermute x7, starting transfers between devices: 8.3 us -> 10.9 us  [spread_with_sum(): arrived = lax.ppermute(payload, axis, [(i, (i + s) % n) for i in range(n)])]
    ppermute x16, waiting for transfers between devices: 7.5 us -> 5.34 us  [gather_blocks(): lax.ppermute(x, axis, [(i, (i + s) % n) for i in range(n)])]
    select_n x3 -> x4, other arithmetic: 5.56 us -> 5.79 us  [arrange(): out = jnp.where(source == s, copies[s][None], out)]
    unnamed x90 -> x76, local copies, waits for them, and re-layouts: 6.5 us -> 6.52 us
  transfers between devices with their start and end apart: 26 -> 26, of which waited for: 4 -> 4; matrix products, arithmetic and copies ran while one was open for 31% -> 24% of each run, Pallas kernels for 0% -> 0%
where the time goes in v13:
time: 111 us; the launch traced here: 110 us
  starting transfers between devices  38 us (34%)
  blocking collectives  19.1 us (17%)
  other arithmetic  17 us (15%)
  local copies, waits for them, and re-layouts  13.7 us (12%)
  matrix products  11.2 us (10%)
  waiting for transfers between devices  8.16 us (7%)
  between operations  3.25 us (3%)
    ppermute x16, starting transfers between devices, gather_blocks(): lax.ppermute(x, axis, [(i, (i + s) % n) for i in range(n)])  23.2 us
    all_gather x1, blocking collectives, local_small(): mean_grad = lax.all_gather(mean_part, 'fsdp', axis=1, tiled=True)  19.1 us
    ppermute x7, starting transfers between devices, spread_with_sum(): arrived = lax.ppermute(payload, axis, [(i, (i + s) % n) for i in range(n)])  10.9 us
    unnamed x76, local copies, waits for them, and re-layouts  6.52 us
    select_n x4, other arithmetic, arrange(): out = jnp.where(source == s, copies[s][None], out)  5.79 us
    ppermute x16, waiting for transfers between devices, gather_blocks(): lax.ppermute(x, axis, [(i, (i + s) % n) for i in range(n)])  5.34 us
    ppermute x3, starting transfers between devices, scatter_sum(): lax.ppermute(piece, axis, [(i, (i + s) % n) for i in range(n)])  3.96 us
    ppermute x3, waiting for transfers between devices, scatter_sum(): lax.ppermute(piece, axis, [(i, (i + s) % n) for i in range(n)])  2.8 us
  transfers between devices with their start and end apart: 26, of which 4 were waited for; matrix products, arithmetic and copies ran while one was open for 24% of the time, Pallas kernels for 0%

profile of v13, /device:TPU:0, one launch (start us, length us, event | category | flops | bytes accessed | tf_op | source)
XLA Modules:
  0.0 110.4 jit_solution(12107135868925955201)
XLA Ops:
  0.6 0.9 constant_dynamic-update-slice_fusion.2
  2.2 0.7 constant_dynamic-update-slice_fusion.1
  2.9 0.7 fusion.28
  3.7 3.1 %collective-permute-start.5 = (bf16[97,256]{1,0:T(8,128)(2,1)S(1)}, bf16[97,256]{1,0:T(8,128)(2,1)}, u32[]{:S(2)}, u32[]{:S(2)}) collective-permute-start(bf16[97,256]{1,0:T(8,128)(2,1)S(1)} %constant_dynamic-update-slice_fusion), channel_id=1, source_target_pairs={{0,1},{1,2},{2,3},{3,0},{4,5},{5,6},{6,7},{7,4},{8,9},{9,10},{10,1... | collective-permute-start | bytes 149000 | tf_op jit(solution)/shard_map/ppermute | solution.py:105
  6.8 2.6 %collective-permute-start.4 = (bf16[97,256]{1,0:T(8,128)(2,1)S(1)}, bf16[97,256]{1,0:T(8,128)(2,1)}, u32[]{:S(2)}, u32[]{:S(2)}) collective-permute-start(bf16[97,256]{1,0:T(8,128)(2,1)S(1)} %constant_dynamic-update-slice_fusion), channel_id=1, source_target_pairs={{0,2},{1,3},{2,0},{3,1},{4,6},{5,7},{6,4},{7,5},{8,10},{9,11},{10,... | collective-permute-start | bytes 149000 | tf_op jit(solution)/shard_map/ppermute | solution.py:105
  9.4 1.3 %collective-permute-start.3 = (bf16[97,256]{1,0:T(8,128)(2,1)S(1)}, bf16[97,256]{1,0:T(8,128)(2,1)}, u32[]{:S(2)}, u32[]{:S(2)}) collective-permute-start(bf16[97,256]{1,0:T(8,128)(2,1)S(1)} %constant_dynamic-update-slice_fusion), channel_id=1, source_target_pairs={{0,3},{1,0},{2,1},{3,2},{4,7},{5,4},{6,5},{7,6},{8,11},{9,8},{10,9... | collective-permute-start | bytes 149000 | tf_op jit(solution)/shard_map/ppermute | solution.py:105
  10.7 0.7 convert_element_type.85
  11.4 1.5 %fusion = f32[128]{0:T(128)S(1)} fusion(bf16[128,4096]{1,0:T(8,128)(2,1)} %param.10), kind=kLoop, calls=%fused_computation.5 | loop fusion | flops 1572736 | bytes 1049088 | tf_op jit(solution)/shard_map/reduce_sum | solution.py:167
  14.0 2.6 %fusion.9 = f32[48,4096]{1,0:T(8,128)} fusion(bf16[128,4096]{1,0:T(8,128)(2,1)} %param.10, f32[4096]{0:T(1024)S(1)} %convert_element_type.85, f32[128]{0:T(128)S(1)} %get-tuple-element.37, s32[128]{0:T(128)} %bitcast.108), kind=kOutput, calls=%fused_computation.18 | convolution fusion | flops 52434944 | bytes 1852416 | tf_op jit(solution)/shard_map/dot_general | solution.py:171
  16.6 1.7 %reshape.418 = f32[48,4,1024]{2,1,0:T(4,128)S(1)} reshape(f32[48,4096]{1,0:T(8,128)} %fusion.9) | data formatting | bytes 1572864 | tf_op jit(solution)/shard_map/reshape | solution.py:175
  18.2 0.8 constant_dynamic-slice_fusion.11
  19.1 0.7 collective-permute-start.2
  24.4 2.8 %collective-permute-start = (f32[48,1024]{1,0:T(8,128)S(1)}, f32[48,1024]{1,0:T(8,128)S(1)}, u32[]{:S(2)}, u32[]{:S(2)}) collective-permute-start(f32[48,1024]{1,0:T(8,128)S(1)} %bitcast.102), channel_id=1, source_target_pairs={{0,3},{1,0},{2,1},{3,2},{4,7},{5,4},{6,5},{7,6},{8,11},{9,8},{10,9... | collective-permute-start | bytes 589832 | tf_op jit(solution)/shard_map/ppermute | solution.py:120
  27.2 1.1 %select_select_fusion.3 = bf16[4,97,256]{2,0,1:T(4,128)(2,1)S(1)} fusion(pred[4]{0:T(512)(128)(4,1)} %copy-done.6, pred[4]{0:T(512)(128)(4,1)} %copy-done.8, pred[4]{0:T(512)(128)(4,1)} %copy-done.4, bf16[97,256]{1,0:T(8,128)(2,1)S(1)} %constant_dynamic-update-slice_fusion, bf16[97,256]{1,0:T(8,128)(2,1)} %collective-permute-done.5, ...), kind=kLoop, calls=%fused_computation.39 | loop fusion | flops 297984 | bytes 397324 | tf_op jit(solution)/shard_map/jit(_where)/select_n | solution.py:98
  28.4 1.5 %collective-permute-start.14 = (bf16[4,97,256]{2,0,1:T(4,128)(2,1)S(1)}, bf16[4,97,256]{2,0,1:T(4,128)(2,1)S(1)}, u32[]{:S(2)}, u32[]{:S(2)}) collective-permute-start(bf16[4,97,256]{2,0,1:T(4,128)(2,1)S(1)} %select_select_fusion.3), channel_id=1, source_target_pairs={{0,8},{4,12},{8,16},{12,20},{16,24},{20,28},{24,0},{28,4},{1,9},{5... | collective-permute-start | bytes 595976 | tf_op jit(solution)/shard_map/ppermute | solution.py:105
  30.2 2.4 %collective-permute-start.13 = (bf16[4,97,256]{2,0,1:T(4,128)(2,1)S(1)}, bf16[4,97,256]{2,0,1:T(4,128)(2,1)S(1)}, u32[]{:S(2)}, u32[]{:S(2)}) collective-permute-start(bf16[4,97,256]{2,0,1:T(4,128)(2,1)S(1)} %select_select_fusion.3), channel_id=1, source_target_pairs={{0,12},{4,16},{8,20},{12,24},{16,28},{20,0},{24,4},{28,8},{1,13},{... | collective-permute-start | bytes 595976 | tf_op jit(solution)/shard_map/ppermute | solution.py:105
  32.6 2.8 %collective-permute-done.1 = f32[48,1024]{1,0:T(8,128)S(1)} collective-permute-done((f32[48,1024]{1,0:T(8,128)S(1)}, f32[48,1024]{1,0:T(8,128)S(1)}, u32[]{:S(2)}, u32[]{:S(2)}) %collective-permute-start.1) | collective-permute-done | bytes 196640 | tf_op jit(solution)/shard_map/ppermute | solution.py:120
  35.4 1.5 %collective-permute-start.12 = (bf16[4,97,256]{2,0,1:T(4,128)(2,1)S(1)}, bf16[4,97,256]{2,0,1:T(4,128)(2,1)S(1)}, u32[]{:S(2)}, u32[]{:S(2)}) collective-permute-start(bf16[4,97,256]{2,0,1:T(4,128)(2,1)S(1)} %select_select_fusion.3), channel_id=1, source_target_pairs={{0,16},{4,20},{8,24},{12,28},{16,0},{20,4},{24,8},{28,12},{1,17},{... | collective-permute-start | bytes 595976 | tf_op jit(solution)/shard_map/ppermute | solution.py:105
  36.9 0.9 select_reduce_fusion
  37.8 1.5 %collective-permute-start.10 = (bf16[4,97,256]{2,0,1:T(4,128)(2,1)S(1)}, bf16[4,97,256]{2,0,1:T(4,128)(2,1)S(1)}, u32[]{:S(2)}, u32[]{:S(2)}) collective-permute-start(bf16[4,97,256]{2,0,1:T(4,128)(2,1)S(1)} %select_select_fusion.3), channel_id=1, source_target_pairs={{0,24},{4,28},{8,0},{12,4},{16,8},{20,12},{24,16},{28,20},{1,25},{... | collective-permute-start | bytes 595976 | tf_op jit(solution)/shard_map/ppermute | solution.py:105
  39.3 2.4 %collective-permute-start.9 = (bf16[4,97,256]{2,0,1:T(4,128)(2,1)S(1)}, bf16[4,97,256]{2,0,1:T(4,128)(2,1)S(1)}, u32[]{:S(2)}, u32[]{:S(2)}) collective-permute-start(bf16[4,97,256]{2,0,1:T(4,128)(2,1)S(1)} %select_select_fusion.3), channel_id=1, source_target_pairs={{0,28},{4,0},{8,4},{12,8},{16,12},{20,16},{24,20},{28,24},{1,29},{... | collective-permute-start | bytes 595976 | tf_op jit(solution)/shard_map/ppermute | solution.py:105
  42.0 3.0 %collective-permute-done.13 = bf16[4,97,256]{2,0,1:T(4,128)(2,1)S(1)} collective-permute-done((bf16[4,97,256]{2,0,1:T(4,128)(2,1)S(1)}, bf16[4,97,256]{2,0,1:T(4,128)(2,1)S(1)}, u32[]{:S(2)}, u32[]{:S(2)}) %collective-permute-start.13) | collective-permute-done | bytes 198688 | tf_op jit(solution)/shard_map/ppermute | solution.py:105
  45.0 0.8 collective-permute-start.6
  45.7 1.4 %collective-permute-start.7 = (bf16[48,1024]{1,0:T(8,128)(2,1)S(1)}, bf16[48,1024]{1,0:T(8,128)(2,1)S(1)}, u32[]{:S(2)}, u32[]{:S(2)}) collective-permute-start(bf16[48,1024]{1,0:T(8,128)(2,1)S(1)} %divide_convert_fusion), channel_id=1, source_target_pairs={{0,2},{1,3},{2,0},{3,1},{4,6},{5,7},{6,4},{7,5},{8,10},{9,11},{10,... | collective-permute-start | bytes 294920 | tf_op jit(solution)/shard_map/ppermute | solution.py:105
  47.2 1.2 %collective-permute-done.11 = bf16[4,97,256]{2,0,1:T(4,128)(2,1)S(1)} collective-permute-done((bf16[4,97,256]{2,0,1:T(4,128)(2,1)S(1)}, bf16[4,97,256]{2,0,1:T(4,128)(2,1)S(1)}, u32[]{:S(2)}, u32[]{:S(2)}) %collective-permute-start.11) | collective-permute-done | bytes 198688 | tf_op jit(solution)/shard_map/ppermute | solution.py:105
  49.1 4.3 %select_select_fusion = bf16[8,4,97,256]{3,1,2,0:T(4,128)(2,1)S(1)} fusion(pred[8]{0:T(512)(128)(4,1)S(1)} %copy-done.12, pred[8]{0:T(512)(128)(4,1)S(1)} %copy-done.14, pred[8]{0:T(512)(128)(4,1)S(1)} %copy-done.16, pred[8]{0:T(512)(128)(4,1)S(1)} %copy-done.18, pred[8]{0:T(512)(128)(4,1)S(1)} %copy-done.20, pred[8]{0:T(512)(128)(4,1)S(1)} %copy-done.22, ...), kind=kLoop, calls=%fused_computation.14 | loop fusion | flops 5562368 | bytes 3178552 | tf_op jit(solution)/shard_map/jit(_where)/select_n | solution.py:98
  53.9 1.2 %collective-permute-done.8 = bf16[48,1024]{1,0:T(8,128)(2,1)S(1)} collective-permute-done((bf16[48,1024]{1,0:T(8,128)(2,1)S(1)}, bf16[48,1024]{1,0:T(8,128)(2,1)S(1)}, u32[]{:S(2)}, u32[]{:S(2)}) %collective-permute-start.8) | collective-permute-done | bytes 98336 | tf_op jit(solution)/shard_map/ppermute | solution.py:105
  55.5 0.7 fusion.31
  56.2 1.1 copy.25
  57.6 1.7 %fusion.32 = (f32[384]{0:T(512)S(1)}, f32[384,384]{0,1:T(8,128)S(1)}) fusion(bf16[384,1024]{1,0:T(8,128)(2,1)} %bitcast.90, bf16[384,1024]{1,0:T(8,128)(2,1)S(1)} %bitcast.78), kind=kOutput, calls=%fused_computation.121 | convolution fusion | flops 302284416 | bytes 2164224 | tf_op jit(solution)/shard_map/dot_general | solution.py:195
  60.3 0.7 copy-done.3
  61.7 0.7 fusion.18
  62.5 19.1 %all_gather.3 = f32[48,4096]{1,0:T(8,128)S(1)} all-gather(f32[48,1024]{1,0:T(8,128)S(1)} %fusion.18), channel_id=1, replica_groups=mesh['dp'=8,'fsdp'=4] {'fsdp'}, dimensions={1}, use_global_device_ids=true | all-gather | bytes 983040 | tf_op jit(solution)/shard_map/all_gather | solution.py:222
  81.6 1.6 %fusion.8 = (f32[4096]{0:T(1024)S(1)}, f32[128]{0:T(128)S(1)}, f32[128,4096]{1,0:T(8,128)S(1)}) fusion(bf16[128,4096]{1,0:T(8,128)(2,1)S(1)} %copy-done.1, f32[128]{0:T(128)S(1)} %copy-done.26, f32[4096]{0:T(1024)S(1)} %convert_element_type.85, f32[48,4096]{1,0:T(8,128)S(1)} %all_gather.3, f32[48]{0:T(128)S(1)} %convert_reduce_fusion, s32[128]{0:T(128)S(1)} %bitcast.109), kind=kOutput, calls=%fused_computation.13 | convolution fusion | flops 305858432 | bytes 3966656 | tf_op jit(solution)/shard_map/dot_general | solution.py:224
  83.4 0.7 constant_dynamic-slice_fusion.7
  84.2 5.0 %collective-permute-start.21 = (f32[28672]{0:T(1024)S(1)}, f32[28672]{0:T(1024)S(1)}, u32[]{:S(2)}, u32[]{:S(2)}) collective-permute-start(f32[28672]{0:T(1024)S(1)} %get-tuple-element.34), channel_id=1, source_target_pairs={{0,8},{4,12},{8,16},{12,20},{16,24},{20,28},{24,0},{28,4},{1,9},{5... | collective-permute-start | bytes 344072 | tf_op jit(solution)/shard_map/ppermute | solution.py:133
  89.2 1.9 %collective-permute-start.20 = (f32[28672]{0:T(1024)S(1)}, f32[28672]{0:T(1024)S(1)}, u32[]{:S(2)}, u32[]{:S(2)}) collective-permute-start(f32[28672]{0:T(1024)S(1)} %get-tuple-element.33), channel_id=1, source_target_pairs={{0,12},{4,16},{8,20},{12,24},{16,28},{20,0},{24,4},{28,8},{1,13},{... | collective-permute-start | bytes 344072 | tf_op jit(solution)/shard_map/ppermute | solution.py:133
  91.1 0.9 collective-permute-start.19
  92.1 1.6 %fusion.5 = bf16[128,4096]{1,0:T(8,128)(2,1)} fusion(bf16[128,4096]{1,0:T(8,128)(2,1)S(1)} %copy-done.1, f32[128,4096]{1,0:T(8,128)S(1)} %get-tuple-element.42, f32[128]{0:T(128)S(1)} %broadcast_multiply_fusion, f32[128]{0:T(128)S(1)} %copy-done.24, f32[4096]{0:T(1024)S(1)} %convert_element_type.85, f32[128]{0:T(128)S(1)} %copy-done.26), kind=kLoop, calls=%fused_computation.10 | loop fusion | flops 3670016 | bytes 4212224 | tf_op jit(solution)/shard_map/convert_element_type | solution.py:234
  93.7 1.2 %collective-permute-start.17 = (f32[28672]{0:T(1024)S(1)}, f32[28672]{0:T(1024)S(1)}, u32[]{:S(2)}, u32[]{:S(2)}) collective-permute-start(f32[28672]{0:T(1024)S(1)} %get-tuple-element.30), channel_id=1, source_target_pairs={{0,24},{4,28},{8,0},{12,4},{16,8},{20,12},{24,16},{28,20},{1,25},{... | collective-permute-start | bytes 344072 | tf_op jit(solution)/shard_map/ppermute | solution.py:133
  94.9 1.8 %collective-permute-start.16 = (f32[28672]{0:T(1024)S(1)}, f32[28672]{0:T(1024)}, u32[]{:S(2)}, u32[]{:S(2)}) collective-permute-start(f32[28672]{0:T(1024)S(1)} %get-tuple-element.29), channel_id=1, source_target_pairs={{0,28},{4,0},{8,4},{12,8},{16,12},{20,16},{24,20},{28,24},{1,29},{... | collective-permute-start | bytes 344072 | tf_op jit(solution)/shard_map/ppermute | solution.py:133
  98.1 1.7 %convolution_multiply_fusion.2 = f32[48,256]{1,0:T(8,128)} fusion(bf16[384,1024]{1,0:T(8,128)(2,1)} %bitcast.91, s32[]{:T(128)S(6)} %select_n.367, bf16[384,384]{0,1:T(8,128)(2,1)} %copy-done.3, s32[]{:T(128)S(6)} %select_n.366), kind=kOutput, calls=%fused_computation.17 | convolution fusion | flops 9449472 | bytes 282632 | tf_op jit(solution)/shard_map/dot_general | solution.py:215
  100.0 0.7 slice.151
  101.0 2.0 %collective-permute-start.24 = (f32[4096]{0:T(1024)S(1)}, f32[4096]{0:T(1024)S(1)}, u32[]{:S(2)}, u32[]{:S(2)}) collective-permute-start(f32[4096]{0:T(1024)S(1)} %select_reduce_fusion.2), channel_id=1, source_target_pairs={{0,2},{1,3},{2,0},{3,1},{4,6},{5,7},{6,4},{7,5},{8,10},{9,11},{10,... | collective-permute-start | bytes 49160 | tf_op jit(solution)/shard_map/ppermute | solution.py:105
  103.0 1.8 %collective-permute-start.23 = (f32[4096]{0:T(1024)S(1)}, f32[4096]{0:T(1024)S(1)}, u32[]{:S(2)}, u32[]{:S(2)}) collective-permute-start(f32[4096]{0:T(1024)S(1)} %select_reduce_fusion.2), channel_id=1, source_target_pairs={{0,3},{1,0},{2,1},{3,2},{4,7},{5,4},{6,5},{7,6},{8,11},{9,8},{10,9... | collective-permute-start | bytes 49160 | tf_op jit(solution)/shard_map/ppermute | solution.py:105
  105.1 0.9 slice.158
  106.3 2.1 %fusion.16 = f32[512,256]{1,0:T(8,128)} fusion(bf16[384,512]{1,0:T(8,128)(2,1)S(1)} %bitcast.84, f32[384,1024]{1,0:T(8,128)} %copy-done.2, s32[]{:T(128)S(6)} %select_n.367), kind=kOutput, calls=%fused_computation.40 | convolution fusion | flops 100663296 | bytes 1114116 | tf_op jit(solution)/shard_map/dot_general | solution.py:238
  108.5 0.7 select_reduce_fusion.3
  (152 shorter events, 12.1 us)
Async XLA Ops:
  0.6 61.0 %copy-start = (bf16[1024,1024]{1,0:T(8,128)(2,1)S(1)}, bf16[1024,1024]{1,0:T(8,128)(2,1)}, u32[]{:S(2)}) copy-start(bf16[1024,1024]{1,0:T(8,128)(2,1)} %param.13) | copy-start | bytes 6291460
  3.7 20.7 %collective-permute-start.5 = (bf16[97,256]{1,0:T(8,128)(2,1)S(1)}, bf16[97,256]{1,0:T(8,128)(2,1)}, u32[]{:S(2)}, u32[]{:S(2)}) collective-permute-start(bf16[97,256]{1,0:T(8,128)(2,1)S(1)} %constant_dynamic-update-slice_fusion), channel_id=1, source_target_pairs={{0,1},{1,2},{2,3},{3,0},{4,5},{5,6},{6,7},{7,4},{8,9},{9,10},{10,1... | collective-permute-start | bytes 149000 | tf_op jit(solution)/shard_map/ppermute | solution.py:105
  6.8 20.5 %collective-permute-start.4 = (bf16[97,256]{1,0:T(8,128)(2,1)S(1)}, bf16[97,256]{1,0:T(8,128)(2,1)}, u32[]{:S(2)}, u32[]{:S(2)}) collective-permute-start(bf16[97,256]{1,0:T(8,128)(2,1)S(1)} %constant_dynamic-update-slice_fusion), channel_id=1, source_target_pairs={{0,2},{1,3},{2,0},{3,1},{4,6},{5,7},{6,4},{7,5},{8,10},{9,11},{10,... | collective-permute-start | bytes 149000 | tf_op jit(solution)/shard_map/ppermute | solution.py:105
  9.4 17.9 %collective-permute-start.3 = (bf16[97,256]{1,0:T(8,128)(2,1)S(1)}, bf16[97,256]{1,0:T(8,128)(2,1)}, u32[]{:S(2)}, u32[]{:S(2)}) collective-permute-start(bf16[97,256]{1,0:T(8,128)(2,1)S(1)} %constant_dynamic-update-slice_fusion), channel_id=1, source_target_pairs={{0,3},{1,0},{2,1},{3,2},{4,7},{5,4},{6,5},{7,6},{8,11},{9,8},{10,9... | collective-permute-start | bytes 149000 | tf_op jit(solution)/shard_map/ppermute | solution.py:105
  19.1 11.1 %collective-permute-start.2 = (f32[48,1024]{1,0:T(8,128)S(1)}, f32[48,1024]{1,0:T(8,128)S(1)}, u32[]{:S(2)}, u32[]{:S(2)}) collective-permute-start(f32[48,1024]{1,0:T(8,128)S(1)} %bitcast.101), channel_id=1, source_target_pairs={{0,1},{1,2},{2,3},{3,0},{4,5},{5,6},{6,7},{7,4},{8,9},{9,10},{10,1... | collective-permute-start | bytes 589832 | tf_op jit(solution)/shard_map/ppermute | solution.py:120
  19.9 15.5 %collective-permute-start.1 = (f32[48,1024]{1,0:T(8,128)S(1)}, f32[48,1024]{1,0:T(8,128)S(1)}, u32[]{:S(2)}, u32[]{:S(2)}) collective-permute-start(f32[48,1024]{1,0:T(8,128)S(1)} %bitcast.100), channel_id=1, source_target_pairs={{0,2},{1,3},{2,0},{3,1},{4,6},{5,7},{6,4},{7,5},{8,10},{9,11},{10,... | collective-permute-start | bytes 589832 | tf_op jit(solution)/shard_map/ppermute | solution.py:120
  23.6 25.4 %copy-start.10 = (pred[8]{0:T(512)(128)(4,1)S(1)}, pred[8]{0:T(512)(128)(4,1)}, u32[]{:S(2)}) copy-start(pred[8]{0:T(512)(128)(4,1)} %get-tuple-element.45) | copy-start | bytes 28
  23.6 25.4 %copy-start.12 = (pred[8]{0:T(512)(128)(4,1)S(1)}, pred[8]{0:T(512)(128)(4,1)}, u32[]{:S(2)}) copy-start(pred[8]{0:T(512)(128)(4,1)} %get-tuple-element.46) | copy-start | bytes 28
  23.6 25.4 %copy-start.14 = (pred[8]{0:T(512)(128)(4,1)S(1)}, pred[8]{0:T(512)(128)(4,1)}, u32[]{:S(2)}) copy-start(pred[8]{0:T(512)(128)(4,1)} %get-tuple-element.47) | copy-start | bytes 28
  23.6 25.4 %copy-start.16 = (pred[8]{0:T(512)(128)(4,1)S(1)}, pred[8]{0:T(512)(128)(4,1)}, u32[]{:S(2)}) copy-start(pred[8]{0:T(512)(128)(4,1)} %get-tuple-element.48) | copy-start | bytes 28
  23.6 25.4 %copy-start.18 = (pred[8]{0:T(512)(128)(4,1)S(1)}, pred[8]{0:T(512)(128)(4,1)}, u32[]{:S(2)}) copy-start(pred[8]{0:T(512)(128)(4,1)} %get-tuple-element.49) | copy-start | bytes 28
  23.7 25.4 %copy-start.20 = (pred[8]{0:T(512)(128)(4,1)S(1)}, pred[8]{0:T(512)(128)(4,1)}, u32[]{:S(2)}) copy-start(pred[8]{0:T(512)(128)(4,1)} %get-tuple-element.50) | copy-start | bytes 28
  23.7 25.4 %copy-start.22 = (pred[8]{0:T(512)(128)(4,1)S(1)}, pred[8]{0:T(512)(128)(4,1)}, u32[]{:S(2)}) copy-start(pred[8]{0:T(512)(128)(4,1)} %broadcast_compare_fusion.6) | copy-start | bytes 28
  24.4 12.5 %collective-permute-start = (f32[48,1024]{1,0:T(8,128)S(1)}, f32[48,1024]{1,0:T(8,128)S(1)}, u32[]{:S(2)}, u32[]{:S(2)}) collective-permute-start(f32[48,1024]{1,0:T(8,128)S(1)} %bitcast.102), channel_id=1, source_target_pairs={{0,3},{1,0},{2,1},{3,2},{4,7},{5,4},{6,5},{7,6},{8,11},{9,8},{10,9... | collective-permute-start | bytes 589832 | tf_op jit(solution)/shard_map/ppermute | solution.py:120
  28.4 9.4 %collective-permute-start.15 = (bf16[4,97,256]{2,0,1:T(4,128)(2,1)S(1)}, bf16[4,97,256]{2,0,1:T(4,128)(2,1)S(1)}, u32[]{:S(2)}, u32[]{:S(2)}) collective-permute-start(bf16[4,97,256]{2,0,1:T(4,128)(2,1)S(1)} %select_select_fusion.3), channel_id=1, source_target_pairs={{0,4},{4,8},{8,12},{12,16},{16,20},{20,24},{24,28},{28,0},{1,5},{5... | collective-permute-start | bytes 595976 | tf_op jit(solution)/shard_map/ppermute | solution.py:105
  28.4 10.8 %collective-permute-start.14 = (bf16[4,97,256]{2,0,1:T(4,128)(2,1)S(1)}, bf16[4,97,256]{2,0,1:T(4,128)(2,1)S(1)}, u32[]{:S(2)}, u32[]{:S(2)}) collective-permute-start(bf16[4,97,256]{2,0,1:T(4,128)(2,1)S(1)} %select_select_fusion.3), channel_id=1, source_target_pairs={{0,8},{4,12},{8,16},{12,20},{16,24},{20,28},{24,0},{28,4},{1,9},{5... | collective-permute-start | bytes 595976 | tf_op jit(solution)/shard_map/ppermute | solution.py:105
  30.2 14.8 %collective-permute-start.13 = (bf16[4,97,256]{2,0,1:T(4,128)(2,1)S(1)}, bf16[4,97,256]{2,0,1:T(4,128)(2,1)S(1)}, u32[]{:S(2)}, u32[]{:S(2)}) collective-permute-start(bf16[4,97,256]{2,0,1:T(4,128)(2,1)S(1)} %select_select_fusion.3), channel_id=1, source_target_pairs={{0,12},{4,16},{8,20},{12,24},{16,28},{20,0},{24,4},{28,8},{1,13},{... | collective-permute-start | bytes 595976 | tf_op jit(solution)/shard_map/ppermute | solution.py:105
  35.4 10.4 %collective-permute-start.12 = (bf16[4,97,256]{2,0,1:T(4,128)(2,1)S(1)}, bf16[4,97,256]{2,0,1:T(4,128)(2,1)S(1)}, u32[]{:S(2)}, u32[]{:S(2)}) collective-permute-start(bf16[4,97,256]{2,0,1:T(4,128)(2,1)S(1)} %select_select_fusion.3), channel_id=1, source_target_pairs={{0,16},{4,20},{8,24},{12,28},{16,0},{20,4},{24,8},{28,12},{1,17},{... | collective-permute-start | bytes 595976 | tf_op jit(solution)/shard_map/ppermute | solution.py:105
  36.9 11.5 %collective-permute-start.11 = (bf16[4,97,256]{2,0,1:T(4,128)(2,1)S(1)}, bf16[4,97,256]{2,0,1:T(4,128)(2,1)S(1)}, u32[]{:S(2)}, u32[]{:S(2)}) collective-permute-start(bf16[4,97,256]{2,0,1:T(4,128)(2,1)S(1)} %select_select_fusion.3), channel_id=1, source_target_pairs={{0,20},{4,24},{8,28},{12,0},{16,4},{20,8},{24,12},{28,16},{1,21},{... | collective-permute-start | bytes 595976 | tf_op jit(solution)/shard_map/ppermute | solution.py:105
  37.8 11.2 %collective-permute-start.10 = (bf16[4,97,256]{2,0,1:T(4,128)(2,1)S(1)}, bf16[4,97,256]{2,0,1:T(4,128)(2,1)S(1)}, u32[]{:S(2)}, u32[]{:S(2)}) collective-permute-start(bf16[4,97,256]{2,0,1:T(4,128)(2,1)S(1)} %select_select_fusion.3), channel_id=1, source_target_pairs={{0,24},{4,28},{8,0},{12,4},{16,8},{20,12},{24,16},{28,20},{1,25},{... | collective-permute-start | bytes 595976 | tf_op jit(solution)/shard_map/ppermute | solution.py:105
  39.3 9.8 %collective-permute-start.9 = (bf16[4,97,256]{2,0,1:T(4,128)(2,1)S(1)}, bf16[4,97,256]{2,0,1:T(4,128)(2,1)S(1)}, u32[]{:S(2)}, u32[]{:S(2)}) collective-permute-start(bf16[4,97,256]{2,0,1:T(4,128)(2,1)S(1)} %select_select_fusion.3), channel_id=1, source_target_pairs={{0,28},{4,0},{8,4},{12,8},{16,12},{20,16},{24,20},{28,24},{1,29},{... | collective-permute-start | bytes 595976 | tf_op jit(solution)/shard_map/ppermute | solution.py:105
  45.0 8.4 %collective-permute-start.6 = (bf16[48,1024]{1,0:T(8,128)(2,1)S(1)}, bf16[48,1024]{1,0:T(8,128)(2,1)S(1)}, u32[]{:S(2)}, u32[]{:S(2)}) collective-permute-start(bf16[48,1024]{1,0:T(8,128)(2,1)S(1)} %divide_convert_fusion), channel_id=1, source_target_pairs={{0,3},{1,0},{2,1},{3,2},{4,7},{5,4},{6,5},{7,6},{8,11},{9,8},{10,9... | collective-permute-start | bytes 294920 | tf_op jit(solution)/shard_map/ppermute | solution.py:105
  45.7 7.9 %collective-permute-start.7 = (bf16[48,1024]{1,0:T(8,128)(2,1)S(1)}, bf16[48,1024]{1,0:T(8,128)(2,1)S(1)}, u32[]{:S(2)}, u32[]{:S(2)}) collective-permute-start(bf16[48,1024]{1,0:T(8,128)(2,1)S(1)} %divide_convert_fusion), channel_id=1, source_target_pairs={{0,2},{1,3},{2,0},{3,1},{4,6},{5,7},{6,4},{7,5},{8,10},{9,11},{10,... | collective-permute-start | bytes 294920 | tf_op jit(solution)/shard_map/ppermute | solution.py:105
  48.4 6.7 %collective-permute-start.8 = (bf16[48,1024]{1,0:T(8,128)(2,1)S(1)}, bf16[48,1024]{1,0:T(8,128)(2,1)S(1)}, u32[]{:S(2)}, u32[]{:S(2)}) collective-permute-start(bf16[48,1024]{1,0:T(8,128)(2,1)S(1)} %divide_convert_fusion), channel_id=1, source_target_pairs={{0,1},{1,2},{2,3},{3,0},{4,5},{5,6},{6,7},{7,4},{8,9},{9,10},{10,1... | collective-permute-start | bytes 294920 | tf_op jit(solution)/shard_map/ppermute | solution.py:105
  61.7 35.1 %copy-start.2 = (f32[384,1024]{1,0:T(8,128)}, f32[384,1024]{1,0:T(8,128)S(1)}, u32[]{:S(2)}) copy-start(f32[384,1024]{1,0:T(8,128)S(1)} %convolution_multiply_fusion) | copy-start | bytes 4718596
  61.7 19.9 %copy-start.1 = (bf16[128,4096]{1,0:T(8,128)(2,1)S(1)}, bf16[128,4096]{1,0:T(8,128)(2,1)}, u32[]{:S(2)}) copy-start(bf16[128,4096]{1,0:T(8,128)(2,1)} %param.10) | copy-start | bytes 3145732
  61.7 19.9 %copy-start.26 = (f32[128]{0:T(128)S(1)}, f32[128]{0:T(128)}, u32[]{:S(2)}) copy-start(f32[128]{0:T(128)} %copy-done.25) | copy-start | bytes 1540
  61.7 19.9 %copy-start.27 = (s32[1,128]{1,0:T(1,128)S(1)}, s32[1,128]{1,0:T(1,128)}, u32[]{:S(2)}) copy-start(s32[1,128]{1,0:T(1,128)} %param.11) | copy-start | bytes 1540
  83.2 8.9 %copy-start.24 = (f32[128]{0:T(128)S(1)}, f32[128]{0:T(128)}, u32[]{:S(2)}) copy-start(f32[128]{0:T(128)} %get-tuple-element.36) | copy-start | bytes 1540
  84.1 9.6 %collective-permute-start.22 = (f32[28672]{0:T(1024)S(1)}, f32[28672]{0:T(1024)S(1)}, u32[]{:S(2)}, u32[]{:S(2)}) collective-permute-start(f32[28672]{0:T(1024)S(1)} %get-tuple-element.35), channel_id=1, source_target_pairs={{0,4},{4,8},{8,12},{12,16},{16,20},{20,24},{24,28},{28,0},{1,5},{5... | collective-permute-start | bytes 344072 | tf_op jit(solution)/shard_map/ppermute | solution.py:133
  84.2 10.7 %collective-permute-start.21 = (f32[28672]{0:T(1024)S(1)}, f32[28672]{0:T(1024)S(1)}, u32[]{:S(2)}, u32[]{:S(2)}) collective-permute-start(f32[28672]{0:T(1024)S(1)} %get-tuple-element.34), channel_id=1, source_target_pairs={{0,8},{4,12},{8,16},{12,20},{16,24},{20,28},{24,0},{28,4},{1,9},{5... | collective-permute-start | bytes 344072 | tf_op jit(solution)/shard_map/ppermute | solution.py:133
  89.2 10.7 %collective-permute-start.20 = (f32[28672]{0:T(1024)S(1)}, f32[28672]{0:T(1024)S(1)}, u32[]{:S(2)}, u32[]{:S(2)}) collective-permute-start(f32[28672]{0:T(1024)S(1)} %get-tuple-element.33), channel_id=1, source_target_pairs={{0,12},{4,16},{8,20},{12,24},{16,28},{20,0},{24,4},{28,8},{1,13},{... | collective-permute-start | bytes 344072 | tf_op jit(solution)/shard_map/ppermute | solution.py:133
  91.1 8.8 %collective-permute-start.19 = (f32[28672]{0:T(1024)S(1)}, f32[28672]{0:T(1024)S(1)}, u32[]{:S(2)}, u32[]{:S(2)}) collective-permute-start(f32[28672]{0:T(1024)S(1)} %get-tuple-element.32), channel_id=1, source_target_pairs={{0,16},{4,20},{8,24},{12,28},{16,0},{20,4},{24,8},{28,12},{1,17},{... | collective-permute-start | bytes 344072 | tf_op jit(solution)/shard_map/ppermute | solution.py:133
  92.1 7.9 %collective-permute-start.18 = (f32[28672]{0:T(1024)S(1)}, f32[28672]{0:T(1024)S(1)}, u32[]{:S(2)}, u32[]{:S(2)}) collective-permute-start(f32[28672]{0:T(1024)S(1)} %get-tuple-element.31), channel_id=1, source_target_pairs={{0,20},{4,24},{8,28},{12,0},{16,4},{20,8},{24,12},{28,16},{1,21},{... | collective-permute-start | bytes 344072 | tf_op jit(solution)/shard_map/ppermute | solution.py:133
  92.1 8.6 %copy-start.11 = (pred[8]{0:T(512)(128)(4,1)S(1)}, pred[8]{0:T(512)(128)(4,1)}, u32[]{:S(2)}) copy-start(pred[8]{0:T(512)(128)(4,1)} %get-tuple-element.45) | copy-start | bytes 28
  92.1 8.6 %copy-start.13 = (pred[8]{0:T(512)(128)(4,1)S(1)}, pred[8]{0:T(512)(128)(4,1)}, u32[]{:S(2)}) copy-start(pred[8]{0:T(512)(128)(4,1)} %get-tuple-element.46) | copy-start | bytes 28
  92.1 8.6 %copy-start.15 = (pred[8]{0:T(512)(128)(4,1)S(1)}, pred[8]{0:T(512)(128)(4,1)}, u32[]{:S(2)}) copy-start(pred[8]{0:T(512)(128)(4,1)} %get-tuple-element.47) | copy-start | bytes 28
  92.1 8.6 %copy-start.17 = (pred[8]{0:T(512)(128)(4,1)S(1)}, pred[8]{0:T(512)(128)(4,1)}, u32[]{:S(2)}) copy-start(pred[8]{0:T(512)(128)(4,1)} %get-tuple-element.48) | copy-start | bytes 28
  92.1 8.6 %copy-start.19 = (pred[8]{0:T(512)(128)(4,1)S(1)}, pred[8]{0:T(512)(128)(4,1)}, u32[]{:S(2)}) copy-start(pred[8]{0:T(512)(128)(4,1)} %get-tuple-element.49) | copy-start | bytes 28
  92.1 8.6 %copy-start.21 = (pred[8]{0:T(512)(128)(4,1)S(1)}, pred[8]{0:T(512)(128)(4,1)}, u32[]{:S(2)}) copy-start(pred[8]{0:T(512)(128)(4,1)} %get-tuple-element.50) | copy-start | bytes 28
  93.7 6.2 %collective-permute-start.17 = (f32[28672]{0:T(1024)S(1)}, f32[28672]{0:T(1024)S(1)}, u32[]{:S(2)}, u32[]{:S(2)}) collective-permute-start(f32[28672]{0:T(1024)S(1)} %get-tuple-element.30), channel_id=1, source_target_pairs={{0,24},{4,28},{8,0},{12,4},{16,8},{20,12},{24,16},{28,20},{1,25},{... | collective-permute-start | bytes 344072 | tf_op jit(solution)/shard_map/ppermute | solution.py:133
  94.9 5.0 %collective-permute-start.16 = (f32[28672]{0:T(1024)S(1)}, f32[28672]{0:T(1024)}, u32[]{:S(2)}, u32[]{:S(2)}) collective-permute-start(f32[28672]{0:T(1024)S(1)} %get-tuple-element.29), channel_id=1, source_target_pairs={{0,28},{4,0},{8,4},{12,8},{16,12},{20,16},{24,20},{28,24},{1,29},{... | collective-permute-start | bytes 344072 | tf_op jit(solution)/shard_map/ppermute | solution.py:133
  96.8 11.7 %copy-start.5 = (pred[4]{0:T(512)(128)(4,1)S(1)}, pred[4]{0:T(512)(128)(4,1)}, u32[]{:S(2)}) copy-start(pred[4]{0:T(512)(128)(4,1)} %copy-done.4) | copy-start | bytes 16
  96.8 11.7 %copy-start.7 = (pred[4]{0:T(512)(128)(4,1)S(1)}, pred[4]{0:T(512)(128)(4,1)}, u32[]{:S(2)}) copy-start(pred[4]{0:T(512)(128)(4,1)} %copy-done.6) | copy-start | bytes 16
  96.8 11.7 %copy-start.9 = (pred[4]{0:T(512)(128)(4,1)S(1)}, pred[4]{0:T(512)(128)(4,1)}, u32[]{:S(2)}) copy-start(pred[4]{0:T(512)(128)(4,1)} %copy-done.8) | copy-start | bytes 16
  100.9 7.6 %collective-permute-start.25 = (f32[4096]{0:T(1024)S(1)}, f32[4096]{0:T(1024)S(1)}, u32[]{:S(2)}, u32[]{:S(2)}) collective-permute-start(f32[4096]{0:T(1024)S(1)} %select_reduce_fusion.2), channel_id=1, source_target_pairs={{0,1},{1,2},{2,3},{3,0},{4,5},{5,6},{6,7},{7,4},{8,9},{9,10},{10,1... | collective-permute-start | bytes 49160 | tf_op jit(solution)/shard_map/ppermute | solution.py:105
  101.0 7.5 %collective-permute-start.24 = (f32[4096]{0:T(1024)S(1)}, f32[4096]{0:T(1024)S(1)}, u32[]{:S(2)}, u32[]{:S(2)}) collective-permute-start(f32[4096]{0:T(1024)S(1)} %select_reduce_fusion.2), channel_id=1, source_target_pairs={{0,2},{1,3},{2,0},{3,1},{4,6},{5,7},{6,4},{7,5},{8,10},{9,11},{10,... | collective-permute-start | bytes 49160 | tf_op jit(solution)/shard_map/ppermute | solution.py:105
  103.0 5.5 %collective-permute-start.23 = (f32[4096]{0:T(1024)S(1)}, f32[4096]{0:T(1024)S(1)}, u32[]{:S(2)}, u32[]{:S(2)}) collective-permute-start(f32[4096]{0:T(1024)S(1)} %select_reduce_fusion.2), channel_id=1, source_target_pairs={{0,3},{1,0},{2,1},{3,2},{4,7},{5,4},{6,5},{7,6},{8,11},{9,8},{10,9... | collective-permute-start | bytes 49160 | tf_op jit(solution)/shard_map/ppermute | solution.py:105
  (6 other events, 19.5 us)

commit v14 on v13

--- a/solution.py
+++ b/solution.py
@@ -111,12 +111,13 @@
     return jnp.sum(gather_blocks(x, axis), axis=0)
 
 
-def scatter_sum(chunks, axis):
+def scatter_sum(whole, axis):
     n = lax.axis_size(axis)
     me = lax.axis_index(axis)
-    copies = [lax.dynamic_index_in_dim(chunks, me, axis=0, keepdims=False)]
+    chunk = whole.shape[1] // n
+    copies = [lax.dynamic_slice_in_dim(whole, me * chunk, chunk, axis=1)]
     for s in range(1, n):
-        piece = lax.dynamic_index_in_dim(chunks, (me + s) % n, axis=0, keepdims=False)
+        piece = lax.dynamic_slice_in_dim(whole, (me + s) % n * chunk, chunk, axis=1)
         copies.append(lax.ppermute(piece, axis, [(i, (i + s) % n) for i in range(n)]))
     return jnp.sum(arrange(copies, me), axis=0)
 
@@ -171,11 +172,10 @@
     pooled_part = jnp.dot(member.astype(jnp.bfloat16), normed, preferred_element_type=jnp.float32)
     counts = jnp.sum((group_ids[None, :] == labels).astype(jnp.float32), axis=1)
     chunk = model_width // feature_count
-    pooled_chunk = scatter_sum(
-        pooled_part.reshape(rows, feature_count, chunk).transpose(1, 0, 2), "fsdp"
-    )
+    pooled_chunk = scatter_sum(pooled_part, "fsdp")
     mean_chunk = (pooled_chunk / counts[:, None]).astype(jnp.bfloat16)
-    mean_pooled = gather_blocks(mean_chunk, "fsdp").transpose(1, 0, 2).reshape(rows, model_width)
+    mean_blocks = lax.optimization_barrier(gather_blocks(mean_chunk, "fsdp"))
+    mean_pooled = mean_blocks.transpose(1, 0, 2).reshape(rows, model_width)
 
     gathered = gather_blocks(group_blocks, "dp")
     mean_pooled, gathered = lax.optimization_barrier((mean_pooled, gathered))

time: 111 us -> 110 us (level)
  local copies, waits for them, and re-layouts: 13.7 us -> 8.89 us
  starting transfers between devices: 38 us -> 41.7 us
  waiting for transfers between devices: 8.16 us -> 11 us
  other arithmetic: 17 us -> 15 us
    ppermute x3, waiting for transfers between devices: 2.8 us -> 9.34 us  [scatter_sum(): lax.ppermute(piece, axis, [(i, (i + s) % n) for i in range(n)])]
    ppermute x7, starting transfers between devices: 10.9 us -> 14.7 us  [spread_with_sum(): arrived = lax.ppermute(payload, axis, [(i, (i + s) % n) for i in range(n)])]
    ppermute x16, waiting for transfers between devices: 5.34 us -> 1.68 us  [gather_blocks(): lax.ppermute(x, axis, [(i, (i + s) % n) for i in range(n)])]
    unnamed x76 -> x51, local copies, waits for them, and re-layouts: 6.52 us -> 3.91 us
    eq x6, other arithmetic: 2.37 us -> 0.08 us  [arrange(): out = jnp.where(source == s, copies[s][None], out)]
    reshape x1 -> x0, local copies, waits for them, and re-layouts: 1.66 us -> none  [local_small(): pooled_part.reshape(rows, feature_count, chunk).transpose(1, 0, 2)]
  transfers between devices with their start and end apart: 26 -> 26, of which waited for: 4 -> 5; matrix products, arithmetic and copies ran while one was open for 24% -> 18% of each run, Pallas kernels for 0% -> 0%
where the time goes in v14:
time: 110 us; the launch traced here: 109 us
  starting transfers between devices  41.7 us (38%)
  blocking collectives  19 us (17%)
  other arithmetic  15 us (14%)
  waiting for transfers between devices  11 us (10%)
  matrix products  10.3 us (9%)
  local copies, waits for them, and re-layouts  8.89 us (8%)
  between operations  3.2 us (3%)
    ppermute x16, starting transfers between devices, gather_blocks(): lax.ppermute(x, axis, [(i, (i + s) % n) for i in range(n)])  23.1 us
    all_gather x1, blocking collectives, local_small(): mean_grad = lax.all_gather(mean_part, 'fsdp', axis=1, tiled=True)  19 us
    ppermute x7, starting transfers between devices, spread_with_sum(): arrived = lax.ppermute(payload, axis, [(i, (i + s) % n) for i in range(n)])  14.7 us
    ppermute x3, waiting for transfers between devices, scatter_sum(): lax.ppermute(piece, axis, [(i, (i + s) % n) for i in range(n)])  9.34 us
    select_n x4, other arithmetic, arrange(): out = jnp.where(source == s, copies[s][None], out)  6.1 us
    unnamed x51, local copies, waits for them, and re-layouts  3.91 us
    ppermute x3, starting transfers between devices, scatter_sum(): lax.ppermute(piece, axis, [(i, (i + s) % n) for i in range(n)])  3.88 us
  transfers between devices with their start and end apart: 26, of which 5 were waited for; matrix products, arithmetic and copies ran while one was open for 18% of the time, Pallas kernels for 0%

profile of v14, /device:TPU:0, one launch (start us, length us, event | category | flops | bytes accessed | tf_op | source)
XLA Modules:
  0.0 109.1 jit_solution(16302946568854262447)
XLA Ops:
  0.6 0.9 constant_dynamic-update-slice_fusion.2
  1.5 0.7 and_select_fusion.2
  2.2 0.7 constant_dynamic-update-slice_fusion.1
  2.9 0.7 fusion.28
  3.7 3.1 %collective-permute-start.5 = (bf16[97,256]{1,0:T(8,128)(2,1)S(1)}, bf16[97,256]{1,0:T(8,128)(2,1)}, u32[]{:S(2)}, u32[]{:S(2)}) collective-permute-start(bf16[97,256]{1,0:T(8,128)(2,1)S(1)} %constant_dynamic-update-slice_fusion), channel_id=1, source_target_pairs={{0,1},{1,2},{2,3},{3,0},{4,5},{5,6},{6,7},{7,4},{8,9},{9,10},{10,1... | collective-permute-start | bytes 149000 | tf_op jit(solution)/shard_map/ppermute | solution.py:105
  6.8 2.6 %collective-permute-start.4 = (bf16[97,256]{1,0:T(8,128)(2,1)S(1)}, bf16[97,256]{1,0:T(8,128)(2,1)}, u32[]{:S(2)}, u32[]{:S(2)}) collective-permute-start(bf16[97,256]{1,0:T(8,128)(2,1)S(1)} %constant_dynamic-update-slice_fusion), channel_id=1, source_target_pairs={{0,2},{1,3},{2,0},{3,1},{4,6},{5,7},{6,4},{7,5},{8,10},{9,11},{10,... | collective-permute-start | bytes 149000 | tf_op jit(solution)/shard_map/ppermute | solution.py:105
  9.4 1.3 %collective-permute-start.3 = (bf16[97,256]{1,0:T(8,128)(2,1)S(1)}, bf16[97,256]{1,0:T(8,128)(2,1)}, u32[]{:S(2)}, u32[]{:S(2)}) collective-permute-start(bf16[97,256]{1,0:T(8,128)(2,1)S(1)} %constant_dynamic-update-slice_fusion), channel_id=1, source_target_pairs={{0,3},{1,0},{2,1},{3,2},{4,7},{5,4},{6,5},{7,6},{8,11},{9,8},{10,9... | collective-permute-start | bytes 149000 | tf_op jit(solution)/shard_map/ppermute | solution.py:105
  10.7 0.7 convert_element_type.85
  11.4 1.5 %fusion = f32[128]{0:T(128)S(1)} fusion(bf16[128,4096]{1,0:T(8,128)(2,1)} %param.10), kind=kLoop, calls=%fused_computation.5 | loop fusion | flops 1572736 | bytes 1049088 | tf_op jit(solution)/shard_map/reduce_sum | solution.py:168
  13.4 1.7 %fusion.9 = f32[48,4096]{1,0:T(8,128)S(1)} fusion(bf16[128,4096]{1,0:T(8,128)(2,1)} %param.10, f32[4096]{0:T(1024)S(1)} %convert_element_type.85, f32[128]{0:T(128)S(1)} %get-tuple-element.37, s32[128]{0:T(128)} %bitcast.62), kind=kOutput, calls=%fused_computation.18 | convolution fusion | flops 52434944 | bytes 1852416 | tf_op jit(solution)/shard_map/dot_general | solution.py:172
  15.2 0.8 constant_dynamic-slice_fusion.11
  16.0 0.7 collective-permute-start.2
  17.3 2.9 %collective-permute-start = (f32[48,1024]{1,0:T(8,128)S(1)}, f32[48,1024]{1,0:T(8,128)S(1)}, u32[]{:S(2)}, u32[]{:S(2)}) collective-permute-start(f32[48,1024]{1,0:T(8,128)S(1)} %get-tuple-element.25), channel_id=1, source_target_pairs={{0,3},{1,0},{2,1},{3,2},{4,7},{5,4},{6,5},{7,6},{8,11},{9,8},{10,9... | collective-permute-start | bytes 589832 | tf_op jit(solution)/shard_map/ppermute | solution.py:121
  20.1 1.1 %select_select_fusion.3 = bf16[4,97,256]{2,0,1:T(4,128)(2,1)S(1)} fusion(pred[4]{0:T(512)(128)(4,1)S(1)} %get-tuple-element.50, pred[4]{0:T(512)(128)(4,1)S(1)} %broadcast_compare_fusion.9, pred[4]{0:T(512)(128)(4,1)S(1)} %get-tuple-element.49, bf16[97,256]{1,0:T(8,128)(2,1)S(1)} %constant_dynamic-update-slice_fusion, ...), kind=kLoop, calls=%fused_computation.39 | loop fusion | flops 297984 | bytes 397324 | tf_op jit(solution)/shard_map/jit(_where)/select_n | solution.py:98
  21.3 1.5 %collective-permute-start.14 = (bf16[4,97,256]{2,0,1:T(4,128)(2,1)S(1)}, bf16[4,97,256]{2,0,1:T(4,128)(2,1)S(1)}, u32[]{:S(2)}, u32[]{:S(2)}) collective-permute-start(bf16[4,97,256]{2,0,1:T(4,128)(2,1)S(1)} %select_select_fusion.3), channel_id=1, source_target_pairs={{0,8},{4,12},{8,16},{12,20},{16,24},{20,28},{24,0},{28,4},{1,9},{5... | collective-permute-start | bytes 595976 | tf_op jit(solution)/shard_map/ppermute | solution.py:105
  23.1 2.8 %collective-permute-done.2 = f32[48,1024]{1,0:T(8,128)S(1)} collective-permute-done((f32[48,1024]{1,0:T(8,128)}, f32[48,1024]{1,0:T(8,128)S(1)}, u32[]{:S(2)}, u32[]{:S(2)}) %collective-permute-start.2) | collective-permute-done | bytes 196640 | tf_op jit(solution)/shard_map/ppermute | solution.py:121
  25.9 6.5 %collective-permute-done.1 = f32[48,1024]{1,0:T(8,128)S(1)} collective-permute-done((f32[48,1024]{1,0:T(8,128)S(1)}, f32[48,1024]{1,0:T(8,128)S(1)}, u32[]{:S(2)}, u32[]{:S(2)}) %collective-permute-start.1) | collective-permute-done | bytes 196640 | tf_op jit(solution)/shard_map/ppermute | solution.py:121
  32.4 1.5 %collective-permute-start.12 = (bf16[4,97,256]{2,0,1:T(4,128)(2,1)S(1)}, bf16[4,97,256]{2,0,1:T(4,128)(2,1)S(1)}, u32[]{:S(2)}, u32[]{:S(2)}) collective-permute-start(bf16[4,97,256]{2,0,1:T(4,128)(2,1)S(1)} %select_select_fusion.3), channel_id=1, source_target_pairs={{0,16},{4,20},{8,24},{12,28},{16,0},{20,4},{24,8},{28,12},{1,17},{... | collective-permute-start | bytes 595976 | tf_op jit(solution)/shard_map/ppermute | solution.py:105
  33.9 0.8 select_reduce_fusion
  34.8 1.5 %collective-permute-start.10 = (bf16[4,97,256]{2,0,1:T(4,128)(2,1)S(1)}, bf16[4,97,256]{2,0,1:T(4,128)(2,1)S(1)}, u32[]{:S(2)}, u32[]{:S(2)}) collective-permute-start(bf16[4,97,256]{2,0,1:T(4,128)(2,1)S(1)} %select_select_fusion.3), channel_id=1, source_target_pairs={{0,24},{4,28},{8,0},{12,4},{16,8},{20,12},{24,16},{28,20},{1,25},{... | collective-permute-start | bytes 595976 | tf_op jit(solution)/shard_map/ppermute | solution.py:105
  36.2 2.4 %collective-permute-start.9 = (bf16[4,97,256]{2,0,1:T(4,128)(2,1)S(1)}, bf16[4,97,256]{2,0,1:T(4,128)(2,1)S(1)}, u32[]{:S(2)}, u32[]{:S(2)}) collective-permute-start(bf16[4,97,256]{2,0,1:T(4,128)(2,1)S(1)} %select_select_fusion.3), channel_id=1, source_target_pairs={{0,28},{4,0},{8,4},{12,8},{16,12},{20,16},{24,20},{28,24},{1,29},{... | collective-permute-start | bytes 595976 | tf_op jit(solution)/shard_map/ppermute | solution.py:105
  38.8 2.4 %collective-permute-start.8 = (bf16[48,1024]{1,0:T(8,128)(2,1)S(1)}, bf16[48,1024]{1,0:T(8,128)(2,1)S(1)}, u32[]{:S(2)}, u32[]{:S(2)}) collective-permute-start(bf16[48,1024]{1,0:T(8,128)(2,1)S(1)} %divide_convert_fusion), channel_id=1, source_target_pairs={{0,1},{1,2},{2,3},{3,0},{4,5},{5,6},{6,7},{7,4},{8,9},{9,10},{10,1... | collective-permute-start | bytes 294920 | tf_op jit(solution)/shard_map/ppermute | solution.py:105
  41.2 1.8 %collective-permute-start.7 = (bf16[48,1024]{1,0:T(8,128)(2,1)S(1)}, bf16[48,1024]{1,0:T(8,128)(2,1)S(1)}, u32[]{:S(2)}, u32[]{:S(2)}) collective-permute-start(bf16[48,1024]{1,0:T(8,128)(2,1)S(1)} %divide_convert_fusion), channel_id=1, source_target_pairs={{0,2},{1,3},{2,0},{3,1},{4,6},{5,7},{6,4},{7,5},{8,10},{9,11},{10,... | collective-permute-start | bytes 294920 | tf_op jit(solution)/shard_map/ppermute | solution.py:105
  43.0 1.0 collective-permute-start.6
  44.4 4.2 %select_select_fusion = bf16[8,4,97,256]{3,1,2,0:T(4,128)(2,1)S(1)} fusion(pred[8]{0:T(512)(128)(4,1)S(1)} %get-tuple-element.44, pred[8]{0:T(512)(128)(4,1)S(1)} %get-tuple-element.45, pred[8]{0:T(512)(128)(4,1)S(1)} %get-tuple-element.46, pred[8]{0:T(512)(128)(4,1)S(1)} %get-tuple-element.47, pred[8]{0:T(512)(128)(4,1)S(1)} %get-tuple-element.48, ...), kind=kLoop, calls=%fused_computation.14 | loop fusion | flops 5562368 | bytes 3178552 | tf_op jit(solution)/shard_map/jit(_where)/select_n | solution.py:98
  49.2 0.7 collective-permute-done.6
  50.6 0.7 fusion.31
  51.3 1.1 copy.15
  52.7 1.7 %fusion.32 = (f32[384]{0:T(512)S(1)}, f32[384,384]{0,1:T(8,128)S(1)}) fusion(bf16[384,1024]{1,0:T(8,128)(2,1)} %bitcast.51, bf16[384,1024]{1,0:T(8,128)(2,1)S(1)} %bitcast.46), kind=kOutput, calls=%fused_computation.111 | convolution fusion | flops 302284416 | bytes 2164224 | tf_op jit(solution)/shard_map/dot_general | solution.py:195
  54.6 0.6 subtract_reduce_fusion
  55.4 0.7 copy-done.3
  56.8 0.7 fusion.18
  57.5 19.0 %all_gather.3 = f32[48,4096]{1,0:T(8,128)S(1)} all-gather(f32[48,1024]{1,0:T(8,128)S(1)} %fusion.18), channel_id=1, replica_groups=mesh['dp'=8,'fsdp'=4] {'fsdp'}, dimensions={1}, use_global_device_ids=true | all-gather | bytes 983040 | tf_op jit(solution)/shard_map/all_gather | solution.py:222
  76.5 1.6 %fusion.8 = (f32[4096]{0:T(1024)S(1)}, f32[128]{0:T(128)S(1)}, f32[128,4096]{1,0:T(8,128)S(1)}) fusion(bf16[128,4096]{1,0:T(8,128)(2,1)S(1)} %copy-done.1, f32[128]{0:T(128)S(1)} %copy-done.20, f32[4096]{0:T(1024)S(1)} %convert_element_type.85, f32[48,4096]{1,0:T(8,128)S(1)} %all_gather.3, f32[48]{0:T(128)S(1)} %convert_reduce_fusion, s32[128]{0:T(128)S(1)} %bitcast.63), kind=kOutput, calls=%fused_computation.13 | convolution fusion | flops 305858432 | bytes 3966656 | tf_op jit(solution)/shard_map/dot_general | solution.py:224
  78.3 0.7 constant_dynamic-slice_fusion.7
  79.2 8.1 %collective-permute-start.21 = (f32[28672]{0:T(1024)S(1)}, f32[28672]{0:T(1024)S(1)}, u32[]{:S(2)}, u32[]{:S(2)}) collective-permute-start(f32[28672]{0:T(1024)S(1)} %get-tuple-element.34), channel_id=1, source_target_pairs={{0,8},{4,12},{8,16},{12,20},{16,24},{20,28},{24,0},{28,4},{1,9},{5... | collective-permute-start | bytes 344072 | tf_op jit(solution)/shard_map/ppermute | solution.py:134
  87.2 2.7 %collective-permute-start.20 = (f32[28672]{0:T(1024)S(1)}, f32[28672]{0:T(1024)S(1)}, u32[]{:S(2)}, u32[]{:S(2)}) collective-permute-start(f32[28672]{0:T(1024)S(1)} %get-tuple-element.33), channel_id=1, source_target_pairs={{0,12},{4,16},{8,20},{12,24},{16,28},{20,0},{24,4},{28,8},{1,13},{... | collective-permute-start | bytes 344072 | tf_op jit(solution)/shard_map/ppermute | solution.py:134
  90.6 1.6 %fusion.5 = bf16[128,4096]{1,0:T(8,128)(2,1)} fusion(bf16[128,4096]{1,0:T(8,128)(2,1)S(1)} %copy-done.1, f32[128,4096]{1,0:T(8,128)S(1)} %get-tuple-element.42, f32[128]{0:T(128)S(1)} %broadcast_multiply_fusion, f32[128]{0:T(128)S(1)} %copy-done.18, f32[4096]{0:T(1024)S(1)} %convert_element_type.85, f32[128]{0:T(128)S(1)} %copy-done.20), kind=kLoop, calls=%fused_computation.10 | loop fusion | flops 3670016 | bytes 4212224 | tf_op jit(solution)/shard_map/convert_element_type | solution.py:234
  92.2 1.2 %collective-permute-start.17 = (f32[28672]{0:T(1024)S(1)}, f32[28672]{0:T(1024)S(1)}, u32[]{:S(2)}, u32[]{:S(2)}) collective-permute-start(f32[28672]{0:T(1024)S(1)} %get-tuple-element.30), channel_id=1, source_target_pairs={{0,24},{4,28},{8,0},{12,4},{16,8},{20,12},{24,16},{28,20},{1,25},{... | collective-permute-start | bytes 344072 | tf_op jit(solution)/shard_map/ppermute | solution.py:134
  93.4 2.1 %collective-permute-start.16 = (f32[28672]{0:T(1024)S(1)}, f32[28672]{0:T(1024)}, u32[]{:S(2)}, u32[]{:S(2)}) collective-permute-start(f32[28672]{0:T(1024)S(1)} %get-tuple-element.29), channel_id=1, source_target_pairs={{0,28},{4,0},{8,4},{12,8},{16,12},{20,16},{24,20},{28,24},{1,29},{... | collective-permute-start | bytes 344072 | tf_op jit(solution)/shard_map/ppermute | solution.py:134
  95.6 0.6 dynamic_slice.40
  96.9 1.7 %convolution_multiply_fusion.2 = f32[48,256]{1,0:T(8,128)} fusion(bf16[384,1024]{1,0:T(8,128)(2,1)} %bitcast.52, s32[]{:T(128)S(6)} %select_n.360, bf16[384,384]{0,1:T(8,128)(2,1)} %copy-done.3, s32[]{:T(128)S(6)} %select_n.359), kind=kOutput, calls=%fused_computation.17 | convolution fusion | flops 9449472 | bytes 282632 | tf_op jit(solution)/shard_map/dot_general | solution.py:215
  98.7 0.7 slice.151
  99.7 2.3 %collective-permute-start.24 = (f32[4096]{0:T(1024)S(1)}, f32[4096]{0:T(1024)S(1)}, u32[]{:S(2)}, u32[]{:S(2)}) collective-permute-start(f32[4096]{0:T(1024)S(1)} %select_reduce_fusion.2), channel_id=1, source_target_pairs={{0,2},{1,3},{2,0},{3,1},{4,6},{5,7},{6,4},{7,5},{8,10},{9,11},{10,... | collective-permute-start | bytes 49160 | tf_op jit(solution)/shard_map/ppermute | solution.py:105
  102.0 1.6 %collective-permute-start.23 = (f32[4096]{0:T(1024)S(1)}, f32[4096]{0:T(1024)S(1)}, u32[]{:S(2)}, u32[]{:S(2)}) collective-permute-start(f32[4096]{0:T(1024)S(1)} %select_reduce_fusion.2), channel_id=1, source_target_pairs={{0,3},{1,0},{2,1},{3,2},{4,7},{5,4},{6,5},{7,6},{8,11},{9,8},{10,9... | collective-permute-start | bytes 49160 | tf_op jit(solution)/shard_map/ppermute | solution.py:105
  103.9 0.9 slice.158
  105.1 2.1 %fusion.16 = f32[512,256]{1,0:T(8,128)} fusion(bf16[384,512]{1,0:T(8,128)(2,1)S(1)} %bitcast.50, f32[384,1024]{1,0:T(8,128)} %copy-done.2, s32[]{:T(128)S(6)} %select_n.360), kind=kOutput, calls=%fused_computation.40 | convolution fusion | flops 100663296 | bytes 1114116 | tf_op jit(solution)/shard_map/dot_general | solution.py:238
  107.2 0.7 select_reduce_fusion.3
  (122 shorter events, 6.0 us)
Async XLA Ops:
  0.6 56.1 %copy-start = (bf16[1024,1024]{1,0:T(8,128)(2,1)S(1)}, bf16[1024,1024]{1,0:T(8,128)(2,1)}, u32[]{:S(2)}) copy-start(bf16[1024,1024]{1,0:T(8,128)(2,1)} %param.13) | copy-start | bytes 6291460
  3.7 13.6 %collective-permute-start.5 = (bf16[97,256]{1,0:T(8,128)(2,1)S(1)}, bf16[97,256]{1,0:T(8,128)(2,1)}, u32[]{:S(2)}, u32[]{:S(2)}) collective-permute-start(bf16[97,256]{1,0:T(8,128)(2,1)S(1)} %constant_dynamic-update-slice_fusion), channel_id=1, source_target_pairs={{0,1},{1,2},{2,3},{3,0},{4,5},{5,6},{6,7},{7,4},{8,9},{9,10},{10,1... | collective-permute-start | bytes 149000 | tf_op jit(solution)/shard_map/ppermute | solution.py:105
  6.8 13.4 %collective-permute-start.4 = (bf16[97,256]{1,0:T(8,128)(2,1)S(1)}, bf16[97,256]{1,0:T(8,128)(2,1)}, u32[]{:S(2)}, u32[]{:S(2)}) collective-permute-start(bf16[97,256]{1,0:T(8,128)(2,1)S(1)} %constant_dynamic-update-slice_fusion), channel_id=1, source_target_pairs={{0,2},{1,3},{2,0},{3,1},{4,6},{5,7},{6,4},{7,5},{8,10},{9,11},{10,... | collective-permute-start | bytes 149000 | tf_op jit(solution)/shard_map/ppermute | solution.py:105
  9.4 10.8 %collective-permute-start.3 = (bf16[97,256]{1,0:T(8,128)(2,1)S(1)}, bf16[97,256]{1,0:T(8,128)(2,1)}, u32[]{:S(2)}, u32[]{:S(2)}) collective-permute-start(bf16[97,256]{1,0:T(8,128)(2,1)S(1)} %constant_dynamic-update-slice_fusion), channel_id=1, source_target_pairs={{0,3},{1,0},{2,1},{3,2},{4,7},{5,4},{6,5},{7,6},{8,11},{9,8},{10,9... | collective-permute-start | bytes 149000 | tf_op jit(solution)/shard_map/ppermute | solution.py:105
  13.4 1.7 %copy-start.19 = (f32[128]{0:T(128)}, f32[128]{0:T(128)S(1)}, u32[]{:S(2)}) copy-start(f32[128]{0:T(128)S(1)} %get-tuple-element.37) | copy-start | bytes 1540
  16.0 9.9 %collective-permute-start.2 = (f32[48,1024]{1,0:T(8,128)}, f32[48,1024]{1,0:T(8,128)S(1)}, u32[]{:S(2)}, u32[]{:S(2)}) collective-permute-start(f32[48,1024]{1,0:T(8,128)} %get-tuple-element.27), channel_id=1, source_target_pairs={{0,1},{1,2},{2,3},{3,0},{4,5},{5,6},{6,7},{7,4},{8,9},{9,10},{10,1... | collective-permute-start | bytes 589832 | tf_op jit(solution)/shard_map/ppermute | solution.py:121
  16.6 15.8 %collective-permute-start.1 = (f32[48,1024]{1,0:T(8,128)S(1)}, f32[48,1024]{1,0:T(8,128)S(1)}, u32[]{:S(2)}, u32[]{:S(2)}) collective-permute-start(f32[48,1024]{1,0:T(8,128)S(1)} %get-tuple-element.28), channel_id=1, source_target_pairs={{0,2},{1,3},{2,0},{3,1},{4,6},{5,7},{6,4},{7,5},{8,10},{9,11},{10,... | collective-permute-start | bytes 589832 | tf_op jit(solution)/shard_map/ppermute | solution.py:121
  17.0 31.7 %copy-start.4 = (pred[8]{0:T(512)(128)(4,1)}, pred[8]{0:T(512)(128)(4,1)S(1)}, u32[]{:S(2)}) copy-start(pred[8]{0:T(512)(128)(4,1)S(1)} %get-tuple-element.43) | copy-start | bytes 28
  17.0 31.7 %copy-start.6 = (pred[8]{0:T(512)(128)(4,1)}, pred[8]{0:T(512)(128)(4,1)S(1)}, u32[]{:S(2)}) copy-start(pred[8]{0:T(512)(128)(4,1)S(1)} %get-tuple-element.44) | copy-start | bytes 28
  17.1 31.6 %copy-start.8 = (pred[8]{0:T(512)(128)(4,1)}, pred[8]{0:T(512)(128)(4,1)S(1)}, u32[]{:S(2)}) copy-start(pred[8]{0:T(512)(128)(4,1)S(1)} %get-tuple-element.45) | copy-start | bytes 28
  17.1 31.6 %copy-start.10 = (pred[8]{0:T(512)(128)(4,1)}, pred[8]{0:T(512)(128)(4,1)S(1)}, u32[]{:S(2)}) copy-start(pred[8]{0:T(512)(128)(4,1)S(1)} %get-tuple-element.46) | copy-start | bytes 28
  17.1 31.6 %copy-start.12 = (pred[8]{0:T(512)(128)(4,1)}, pred[8]{0:T(512)(128)(4,1)S(1)}, u32[]{:S(2)}) copy-start(pred[8]{0:T(512)(128)(4,1)S(1)} %get-tuple-element.47) | copy-start | bytes 28
  17.1 31.6 %copy-start.14 = (pred[8]{0:T(512)(128)(4,1)}, pred[8]{0:T(512)(128)(4,1)S(1)}, u32[]{:S(2)}) copy-start(pred[8]{0:T(512)(128)(4,1)S(1)} %get-tuple-element.48) | copy-start | bytes 28
  17.1 31.6 %copy-start.16 = (pred[8]{0:T(512)(128)(4,1)}, pred[8]{0:T(512)(128)(4,1)S(1)}, u32[]{:S(2)}) copy-start(pred[8]{0:T(512)(128)(4,1)S(1)} %broadcast_compare_fusion.6) | copy-start | bytes 28
  17.3 16.7 %collective-permute-start = (f32[48,1024]{1,0:T(8,128)S(1)}, f32[48,1024]{1,0:T(8,128)S(1)}, u32[]{:S(2)}, u32[]{:S(2)}) collective-permute-start(f32[48,1024]{1,0:T(8,128)S(1)} %get-tuple-element.25), channel_id=1, source_target_pairs={{0,3},{1,0},{2,1},{3,2},{4,7},{5,4},{6,5},{7,6},{8,11},{9,8},{10,9... | collective-permute-start | bytes 589832 | tf_op jit(solution)/shard_map/ppermute | solution.py:121
  21.3 13.5 %collective-permute-start.15 = (bf16[4,97,256]{2,0,1:T(4,128)(2,1)S(1)}, bf16[4,97,256]{2,0,1:T(4,128)(2,1)S(1)}, u32[]{:S(2)}, u32[]{:S(2)}) collective-permute-start(bf16[4,97,256]{2,0,1:T(4,128)(2,1)S(1)} %select_select_fusion.3), channel_id=1, source_target_pairs={{0,4},{4,8},{8,12},{12,16},{16,20},{20,24},{24,28},{28,0},{1,5},{5... | collective-permute-start | bytes 595976 | tf_op jit(solution)/shard_map/ppermute | solution.py:105
  21.3 14.9 %collective-permute-start.14 = (bf16[4,97,256]{2,0,1:T(4,128)(2,1)S(1)}, bf16[4,97,256]{2,0,1:T(4,128)(2,1)S(1)}, u32[]{:S(2)}, u32[]{:S(2)}) collective-permute-start(bf16[4,97,256]{2,0,1:T(4,128)(2,1)S(1)} %select_select_fusion.3), channel_id=1, source_target_pairs={{0,8},{4,12},{8,16},{12,20},{16,24},{20,28},{24,0},{28,4},{1,9},{5... | collective-permute-start | bytes 595976 | tf_op jit(solution)/shard_map/ppermute | solution.py:105
  25.9 12.8 %collective-permute-start.13 = (bf16[4,97,256]{2,0,1:T(4,128)(2,1)S(1)}, bf16[4,97,256]{2,0,1:T(4,128)(2,1)S(1)}, u32[]{:S(2)}, u32[]{:S(2)}) collective-permute-start(bf16[4,97,256]{2,0,1:T(4,128)(2,1)S(1)} %select_select_fusion.3), channel_id=1, source_target_pairs={{0,12},{4,16},{8,20},{12,24},{16,28},{20,0},{24,4},{28,8},{1,13},{... | collective-permute-start | bytes 595976 | tf_op jit(solution)/shard_map/ppermute | solution.py:105
  32.4 8.8 %collective-permute-start.12 = (bf16[4,97,256]{2,0,1:T(4,128)(2,1)S(1)}, bf16[4,97,256]{2,0,1:T(4,128)(2,1)S(1)}, u32[]{:S(2)}, u32[]{:S(2)}) collective-permute-start(bf16[4,97,256]{2,0,1:T(4,128)(2,1)S(1)} %select_select_fusion.3), channel_id=1, source_target_pairs={{0,16},{4,20},{8,24},{12,28},{16,0},{20,4},{24,8},{28,12},{1,17},{... | collective-permute-start | bytes 595976 | tf_op jit(solution)/shard_map/ppermute | solution.py:105
  33.9 9.0 %collective-permute-start.11 = (bf16[4,97,256]{2,0,1:T(4,128)(2,1)S(1)}, bf16[4,97,256]{2,0,1:T(4,128)(2,1)S(1)}, u32[]{:S(2)}, u32[]{:S(2)}) collective-permute-start(bf16[4,97,256]{2,0,1:T(4,128)(2,1)S(1)} %select_select_fusion.3), channel_id=1, source_target_pairs={{0,20},{4,24},{8,28},{12,0},{16,4},{20,8},{24,12},{28,16},{1,21},{... | collective-permute-start | bytes 595976 | tf_op jit(solution)/shard_map/ppermute | solution.py:105
  34.8 9.2 %collective-permute-start.10 = (bf16[4,97,256]{2,0,1:T(4,128)(2,1)S(1)}, bf16[4,97,256]{2,0,1:T(4,128)(2,1)S(1)}, u32[]{:S(2)}, u32[]{:S(2)}) collective-permute-start(bf16[4,97,256]{2,0,1:T(4,128)(2,1)S(1)} %select_select_fusion.3), channel_id=1, source_target_pairs={{0,24},{4,28},{8,0},{12,4},{16,8},{20,12},{24,16},{28,20},{1,25},{... | collective-permute-start | bytes 595976 | tf_op jit(solution)/shard_map/ppermute | solution.py:105
  36.2 8.2 %collective-permute-start.9 = (bf16[4,97,256]{2,0,1:T(4,128)(2,1)S(1)}, bf16[4,97,256]{2,0,1:T(4,128)(2,1)S(1)}, u32[]{:S(2)}, u32[]{:S(2)}) collective-permute-start(bf16[4,97,256]{2,0,1:T(4,128)(2,1)S(1)} %select_select_fusion.3), channel_id=1, source_target_pairs={{0,28},{4,0},{8,4},{12,8},{16,12},{20,16},{24,20},{28,24},{1,29},{... | collective-permute-start | bytes 595976 | tf_op jit(solution)/shard_map/ppermute | solution.py:105
  38.8 10.0 %collective-permute-start.8 = (bf16[48,1024]{1,0:T(8,128)(2,1)S(1)}, bf16[48,1024]{1,0:T(8,128)(2,1)S(1)}, u32[]{:S(2)}, u32[]{:S(2)}) collective-permute-start(bf16[48,1024]{1,0:T(8,128)(2,1)S(1)} %divide_convert_fusion), channel_id=1, source_target_pairs={{0,1},{1,2},{2,3},{3,0},{4,5},{5,6},{6,7},{7,4},{8,9},{9,10},{10,1... | collective-permute-start | bytes 294920 | tf_op jit(solution)/shard_map/ppermute | solution.py:105
  41.2 8.0 %collective-permute-start.7 = (bf16[48,1024]{1,0:T(8,128)(2,1)S(1)}, bf16[48,1024]{1,0:T(8,128)(2,1)S(1)}, u32[]{:S(2)}, u32[]{:S(2)}) collective-permute-start(bf16[48,1024]{1,0:T(8,128)(2,1)S(1)} %divide_convert_fusion), channel_id=1, source_target_pairs={{0,2},{1,3},{2,0},{3,1},{4,6},{5,7},{6,4},{7,5},{8,10},{9,11},{10,... | collective-permute-start | bytes 294920 | tf_op jit(solution)/shard_map/ppermute | solution.py:105
  43.0 7.0 %collective-permute-start.6 = (bf16[48,1024]{1,0:T(8,128)(2,1)S(1)}, bf16[48,1024]{1,0:T(8,128)(2,1)S(1)}, u32[]{:S(2)}, u32[]{:S(2)}) collective-permute-start(bf16[48,1024]{1,0:T(8,128)(2,1)S(1)} %divide_convert_fusion), channel_id=1, source_target_pairs={{0,3},{1,0},{2,1},{3,2},{4,7},{5,4},{6,5},{7,6},{8,11},{9,8},{10,9... | collective-permute-start | bytes 294920 | tf_op jit(solution)/shard_map/ppermute | solution.py:105
  55.4 0.7 copy-start.3
  56.7 38.8 %copy-start.2 = (f32[384,1024]{1,0:T(8,128)}, f32[384,1024]{1,0:T(8,128)S(1)}, u32[]{:S(2)}) copy-start(f32[384,1024]{1,0:T(8,128)S(1)} %convolution_multiply_fusion) | copy-start | bytes 4718596
  56.7 19.8 %copy-start.1 = (bf16[128,4096]{1,0:T(8,128)(2,1)S(1)}, bf16[128,4096]{1,0:T(8,128)(2,1)}, u32[]{:S(2)}) copy-start(bf16[128,4096]{1,0:T(8,128)(2,1)} %param.10) | copy-start | bytes 3145732
  56.8 19.8 %copy-start.20 = (f32[128]{0:T(128)S(1)}, f32[128]{0:T(128)}, u32[]{:S(2)}) copy-start(f32[128]{0:T(128)} %copy-done.19) | copy-start | bytes 1540
  56.8 19.7 %copy-start.21 = (s32[1,128]{1,0:T(1,128)S(1)}, s32[1,128]{1,0:T(1,128)}, u32[]{:S(2)}) copy-start(s32[1,128]{1,0:T(1,128)} %param.11) | copy-start | bytes 1540
  78.2 12.4 %copy-start.18 = (f32[128]{0:T(128)S(1)}, f32[128]{0:T(128)}, u32[]{:S(2)}) copy-start(f32[128]{0:T(128)} %get-tuple-element.36) | copy-start | bytes 1540
  79.1 13.1 %collective-permute-start.22 = (f32[28672]{0:T(1024)S(1)}, f32[28672]{0:T(1024)S(1)}, u32[]{:S(2)}, u32[]{:S(2)}) collective-permute-start(f32[28672]{0:T(1024)S(1)} %get-tuple-element.35), channel_id=1, source_target_pairs={{0,4},{4,8},{8,12},{12,16},{16,20},{20,24},{24,28},{28,0},{1,5},{5... | collective-permute-start | bytes 344072 | tf_op jit(solution)/shard_map/ppermute | solution.py:134
  79.2 14.2 %collective-permute-start.21 = (f32[28672]{0:T(1024)S(1)}, f32[28672]{0:T(1024)S(1)}, u32[]{:S(2)}, u32[]{:S(2)}) collective-permute-start(f32[28672]{0:T(1024)S(1)} %get-tuple-element.34), channel_id=1, source_target_pairs={{0,8},{4,12},{8,16},{12,20},{16,24},{20,28},{24,0},{28,4},{1,9},{5... | collective-permute-start | bytes 344072 | tf_op jit(solution)/shard_map/ppermute | solution.py:134
  87.2 11.4 %collective-permute-start.20 = (f32[28672]{0:T(1024)S(1)}, f32[28672]{0:T(1024)S(1)}, u32[]{:S(2)}, u32[]{:S(2)}) collective-permute-start(f32[28672]{0:T(1024)S(1)} %get-tuple-element.33), channel_id=1, source_target_pairs={{0,12},{4,16},{8,20},{12,24},{16,28},{20,0},{24,4},{28,8},{1,13},{... | collective-permute-start | bytes 344072 | tf_op jit(solution)/shard_map/ppermute | solution.py:134
  89.9 8.7 %collective-permute-start.19 = (f32[28672]{0:T(1024)S(1)}, f32[28672]{0:T(1024)S(1)}, u32[]{:S(2)}, u32[]{:S(2)}) collective-permute-start(f32[28672]{0:T(1024)S(1)} %get-tuple-element.32), channel_id=1, source_target_pairs={{0,16},{4,20},{8,24},{12,28},{16,0},{20,4},{24,8},{28,12},{1,17},{... | collective-permute-start | bytes 344072 | tf_op jit(solution)/shard_map/ppermute | solution.py:134
  90.1 8.6 %collective-permute-start.18 = (f32[28672]{0:T(1024)S(1)}, f32[28672]{0:T(1024)S(1)}, u32[]{:S(2)}, u32[]{:S(2)}) collective-permute-start(f32[28672]{0:T(1024)S(1)} %get-tuple-element.31), channel_id=1, source_target_pairs={{0,20},{4,24},{8,28},{12,0},{16,4},{20,8},{24,12},{28,16},{1,21},{... | collective-permute-start | bytes 344072 | tf_op jit(solution)/shard_map/ppermute | solution.py:134
  90.5 8.9 %copy-start.5 = (pred[8]{0:T(512)(128)(4,1)S(1)}, pred[8]{0:T(512)(128)(4,1)}, u32[]{:S(2)}) copy-start(pred[8]{0:T(512)(128)(4,1)} %copy-done.4) | copy-start | bytes 28
  90.5 8.9 %copy-start.7 = (pred[8]{0:T(512)(128)(4,1)S(1)}, pred[8]{0:T(512)(128)(4,1)}, u32[]{:S(2)}) copy-start(pred[8]{0:T(512)(128)(4,1)} %copy-done.6) | copy-start | bytes 28
  90.5 8.9 %copy-start.9 = (pred[8]{0:T(512)(128)(4,1)S(1)}, pred[8]{0:T(512)(128)(4,1)}, u32[]{:S(2)}) copy-start(pred[8]{0:T(512)(128)(4,1)} %copy-done.8) | copy-start | bytes 28
  90.6 8.9 %copy-start.11 = (pred[8]{0:T(512)(128)(4,1)S(1)}, pred[8]{0:T(512)(128)(4,1)}, u32[]{:S(2)}) copy-start(pred[8]{0:T(512)(128)(4,1)} %copy-done.10) | copy-start | bytes 28
  90.6 8.9 %copy-start.13 = (pred[8]{0:T(512)(128)(4,1)S(1)}, pred[8]{0:T(512)(128)(4,1)}, u32[]{:S(2)}) copy-start(pred[8]{0:T(512)(128)(4,1)} %copy-done.12) | copy-start | bytes 28
  90.6 8.9 %copy-start.15 = (pred[8]{0:T(512)(128)(4,1)S(1)}, pred[8]{0:T(512)(128)(4,1)}, u32[]{:S(2)}) copy-start(pred[8]{0:T(512)(128)(4,1)} %copy-done.14) | copy-start | bytes 28
  90.6 8.9 %copy-start.17 = (pred[8]{0:T(512)(128)(4,1)S(1)}, pred[8]{0:T(512)(128)(4,1)}, u32[]{:S(2)}) copy-start(pred[8]{0:T(512)(128)(4,1)} %copy-done.16) | copy-start | bytes 28
  92.2 6.5 %collective-permute-start.17 = (f32[28672]{0:T(1024)S(1)}, f32[28672]{0:T(1024)S(1)}, u32[]{:S(2)}, u32[]{:S(2)}) collective-permute-start(f32[28672]{0:T(1024)S(1)} %get-tuple-element.30), channel_id=1, source_target_pairs={{0,24},{4,28},{8,0},{12,4},{16,8},{20,12},{24,16},{28,20},{1,25},{... | collective-permute-start | bytes 344072 | tf_op jit(solution)/shard_map/ppermute | solution.py:134
  93.4 5.3 %collective-permute-start.16 = (f32[28672]{0:T(1024)S(1)}, f32[28672]{0:T(1024)}, u32[]{:S(2)}, u32[]{:S(2)}) collective-permute-start(f32[28672]{0:T(1024)S(1)} %get-tuple-element.29), channel_id=1, source_target_pairs={{0,28},{4,0},{8,4},{12,8},{16,12},{20,16},{24,20},{28,24},{1,29},{... | collective-permute-start | bytes 344072 | tf_op jit(solution)/shard_map/ppermute | solution.py:134
  99.6 7.6 %collective-permute-start.25 = (f32[4096]{0:T(1024)S(1)}, f32[4096]{0:T(1024)S(1)}, u32[]{:S(2)}, u32[]{:S(2)}) collective-permute-start(f32[4096]{0:T(1024)S(1)} %select_reduce_fusion.2), channel_id=1, source_target_pairs={{0,1},{1,2},{2,3},{3,0},{4,5},{5,6},{6,7},{7,4},{8,9},{9,10},{10,1... | collective-permute-start | bytes 49160 | tf_op jit(solution)/shard_map/ppermute | solution.py:105
  99.7 7.5 %collective-permute-start.24 = (f32[4096]{0:T(1024)S(1)}, f32[4096]{0:T(1024)S(1)}, u32[]{:S(2)}, u32[]{:S(2)}) collective-permute-start(f32[4096]{0:T(1024)S(1)} %select_reduce_fusion.2), channel_id=1, source_target_pairs={{0,2},{1,3},{2,0},{3,1},{4,6},{5,7},{6,4},{7,5},{8,10},{9,11},{10,... | collective-permute-start | bytes 49160 | tf_op jit(solution)/shard_map/ppermute | solution.py:105
  102.0 5.3 %collective-permute-start.23 = (f32[4096]{0:T(1024)S(1)}, f32[4096]{0:T(1024)S(1)}, u32[]{:S(2)}, u32[]{:S(2)}) collective-permute-start(f32[4096]{0:T(1024)S(1)} %select_reduce_fusion.2), channel_id=1, source_target_pairs={{0,3},{1,0},{2,1},{3,2},{4,7},{5,4},{6,5},{7,6},{8,11},{9,8},{10,9... | collective-permute-start | bytes 49160 | tf_op jit(solution)/shard_map/ppermute | solution.py:105

commit v15 on v14

--- a/solution.py
+++ b/solution.py
@@ -232,8 +232,9 @@
     scaled = gain * normed_grad
     inner = jnp.mean(scaled * states, axis=1, keepdims=True)
     hidden_grad = (inv_rms * scaled - states * inv_rms**3 * inner).astype(jnp.bfloat16)
-    gain_dp, pieces = spread_with_sum(gain_part, pieces.astype(jnp.float32), "dp")
-    gain_grad = sum_blocks(gain_dp, "fsdp")
+    gain_grad, pieces = spread_with_sum(
+        sum_blocks(gain_part, "fsdp"), pieces.astype(jnp.float32), "dp"
+    )
     pooled_cols = pieces.reshape(pair_count, slice_width).astype(jnp.bfloat16)
     proj_grad = lax.dot_general(
         pooled_cols, grad_low_cols, contract_first, preferred_element_type=jnp.float32

time: 110 us -> 116 us (1.055)
  the two profiles are of different devices: /device:TPU:0 before, /device:TPU:11 now
where the time goes in v15:
time: 116 us; the launch traced here: 115 us
  starting transfers between devices  36.1 us (31%)
  waiting for transfers between devices  22.6 us (19%)
  blocking collectives  16.2 us (14%)
  other arithmetic  15 us (13%)
  local copies, waits for them, and re-layouts  12.1 us (10%)
  matrix products  10.3 us (9%)
  between operations  3.22 us (3%)
    ppermute x16, starting transfers between devices, gather_blocks(): lax.ppermute(x, axis, [(i, (i + s) % n) for i in range(n)])  22.2 us
    all_gather x1, blocking collectives, local_small(): mean_grad = lax.all_gather(mean_part, 'fsdp', axis=1, tiled=True)  16.2 us
    ppermute x7, starting transfers between devices, spread_with_sum(): arrived = lax.ppermute(payload, axis, [(i, (i + s) % n) for i in range(n)])  10.6 us
    ppermute x16, waiting for transfers between devices, gather_blocks(): lax.ppermute(x, axis, [(i, (i + s) % n) for i in range(n)])  9.99 us
    ppermute x3, waiting for transfers between devices, scatter_sum(): lax.ppermute(piece, axis, [(i, (i + s) % n) for i in range(n)])  7.98 us
    select_n x4, other arithmetic, arrange(): out = jnp.where(source == s, copies[s][None], out)  6.11 us
    ppermute x7, waiting for transfers between devices, spread_with_sum(): arrived = lax.ppermute(payload, axis, [(i, (i + s) % n) for i in range(n)])  4.6 us
    unnamed x51, local copies, waits for them, and re-layouts  3.91 us
  transfers between devices with their start and end apart: 26, of which 6 were waited for; matrix products, arithmetic and copies ran while one was open for 16% of the time, Pallas kernels for 0%

profile of v15, /device:TPU:11, one launch (start us, length us, event | category | flops | bytes accessed | tf_op | source)
XLA Modules:
  0.0 115.5 jit_solution(13625048102058368553)
XLA Ops:
  0.6 0.9 constant_dynamic-update-slice_fusion.2
  2.2 0.7 constant_dynamic-update-slice_fusion.1
  2.9 0.7 fusion.28
  3.7 1.3 %collective-permute-start.5 = (bf16[97,256]{1,0:T(8,128)(2,1)S(1)}, bf16[97,256]{1,0:T(8,128)(2,1)}, u32[]{:S(2)}, u32[]{:S(2)}) collective-permute-start(bf16[97,256]{1,0:T(8,128)(2,1)S(1)} %constant_dynamic-update-slice_fusion), channel_id=1, source_target_pairs={{0,1},{1,2},{2,3},{3,0},{4,5},{5,6},{6,7},{7,4},{8,9},{9,10},{10,1... | collective-permute-start | bytes 149000 | tf_op jit(solution)/shard_map/ppermute | solution.py:105
  5.0 1.1 collective-permute-start.4
  6.1 1.4 %collective-permute-start.3 = (bf16[97,256]{1,0:T(8,128)(2,1)S(1)}, bf16[97,256]{1,0:T(8,128)(2,1)}, u32[]{:S(2)}, u32[]{:S(2)}) collective-permute-start(bf16[97,256]{1,0:T(8,128)(2,1)S(1)} %constant_dynamic-update-slice_fusion), channel_id=1, source_target_pairs={{0,3},{1,0},{2,1},{3,2},{4,7},{5,4},{6,5},{7,6},{8,11},{9,8},{10,9... | collective-permute-start | bytes 149000 | tf_op jit(solution)/shard_map/ppermute | solution.py:105
  8.2 1.5 %fusion = f32[128]{0:T(128)S(1)} fusion(bf16[128,4096]{1,0:T(8,128)(2,1)} %param.10), kind=kLoop, calls=%fused_computation.5 | loop fusion | flops 1572736 | bytes 1049088 | tf_op jit(solution)/shard_map/reduce_sum | solution.py:168
  10.3 1.7 %fusion.9 = f32[48,4096]{1,0:T(8,128)S(1)} fusion(bf16[128,4096]{1,0:T(8,128)(2,1)} %param.10, f32[4096]{0:T(1024)S(1)} %convert_element_type.85, f32[128]{0:T(128)S(1)} %get-tuple-element.37, s32[128]{0:T(128)} %bitcast.62), kind=kOutput, calls=%fused_computation.18 | convolution fusion | flops 52434944 | bytes 1852416 | tf_op jit(solution)/shard_map/dot_general | solution.py:172
  12.0 0.8 constant_dynamic-slice_fusion.11
  12.9 3.1 %collective-permute-start.1 = (f32[48,1024]{1,0:T(8,128)S(1)}, f32[48,1024]{1,0:T(8,128)S(1)}, u32[]{:S(2)}, u32[]{:S(2)}) collective-permute-start(f32[48,1024]{1,0:T(8,128)S(1)} %get-tuple-element.28), channel_id=1, source_target_pairs={{0,2},{1,3},{2,0},{3,1},{4,6},{5,7},{6,4},{7,5},{8,10},{9,11},{10,... | collective-permute-start | bytes 589832 | tf_op jit(solution)/shard_map/ppermute | solution.py:121
  16.3 1.1 select_select_fusion.3
  17.4 3.2 %collective-permute-start.15 = (bf16[4,97,256]{2,0,1:T(4,128)(2,1)S(1)}, bf16[4,97,256]{2,0,1:T(4,128)(2,1)S(1)}, u32[]{:S(2)}, u32[]{:S(2)}) collective-permute-start(bf16[4,97,256]{2,0,1:T(4,128)(2,1)S(1)} %select_select_fusion.3), channel_id=1, source_target_pairs={{0,4},{4,8},{8,12},{12,16},{16,20},{20,24},{24,28},{28,0},{1,5},{5... | collective-permute-start | bytes 595976 | tf_op jit(solution)/shard_map/ppermute | solution.py:105
  20.7 1.2 %collective-permute-start.14 = (bf16[4,97,256]{2,0,1:T(4,128)(2,1)S(1)}, bf16[4,97,256]{2,0,1:T(4,128)(2,1)S(1)}, u32[]{:S(2)}, u32[]{:S(2)}) collective-permute-start(bf16[4,97,256]{2,0,1:T(4,128)(2,1)S(1)} %select_select_fusion.3), channel_id=1, source_target_pairs={{0,8},{4,12},{8,16},{12,20},{16,24},{20,28},{24,0},{28,4},{1,9},{5... | collective-permute-start | bytes 595976 | tf_op jit(solution)/shard_map/ppermute | solution.py:105
  22.1 1.4 %collective-permute-start.13 = (bf16[4,97,256]{2,0,1:T(4,128)(2,1)S(1)}, bf16[4,97,256]{2,0,1:T(4,128)(2,1)S(1)}, u32[]{:S(2)}, u32[]{:S(2)}) collective-permute-start(bf16[4,97,256]{2,0,1:T(4,128)(2,1)S(1)} %select_select_fusion.3), channel_id=1, source_target_pairs={{0,12},{4,16},{8,20},{12,24},{16,28},{20,0},{24,4},{28,8},{1,13},{... | collective-permute-start | bytes 595976 | tf_op jit(solution)/shard_map/ppermute | solution.py:105
  23.5 5.6 %collective-permute-done.1 = f32[48,1024]{1,0:T(8,128)S(1)} collective-permute-done((f32[48,1024]{1,0:T(8,128)S(1)}, f32[48,1024]{1,0:T(8,128)S(1)}, u32[]{:S(2)}, u32[]{:S(2)}) %collective-permute-start.1) | collective-permute-done | bytes 196640 | tf_op jit(solution)/shard_map/ppermute | solution.py:121
  29.1 1.2 %collective-permute-start.12 = (bf16[4,97,256]{2,0,1:T(4,128)(2,1)S(1)}, bf16[4,97,256]{2,0,1:T(4,128)(2,1)S(1)}, u32[]{:S(2)}, u32[]{:S(2)}) collective-permute-start(bf16[4,97,256]{2,0,1:T(4,128)(2,1)S(1)} %select_select_fusion.3), channel_id=1, source_target_pairs={{0,16},{4,20},{8,24},{12,28},{16,0},{20,4},{24,8},{28,12},{1,17},{... | collective-permute-start | bytes 595976 | tf_op jit(solution)/shard_map/ppermute | solution.py:105
  30.3 2.4 %collective-permute-done = f32[48,1024]{1,0:T(8,128)S(1)} collective-permute-done((f32[48,1024]{1,0:T(8,128)S(1)}, f32[48,1024]{1,0:T(8,128)S(1)}, u32[]{:S(2)}, u32[]{:S(2)}) %collective-permute-start) | collective-permute-done | bytes 196640 | tf_op jit(solution)/shard_map/ppermute | solution.py:121
  32.7 1.4 %collective-permute-start.11 = (bf16[4,97,256]{2,0,1:T(4,128)(2,1)S(1)}, bf16[4,97,256]{2,0,1:T(4,128)(2,1)S(1)}, u32[]{:S(2)}, u32[]{:S(2)}) collective-permute-start(bf16[4,97,256]{2,0,1:T(4,128)(2,1)S(1)} %select_select_fusion.3), channel_id=1, source_target_pairs={{0,20},{4,24},{8,28},{12,0},{16,4},{20,8},{24,12},{28,16},{1,21},{... | collective-permute-start | bytes 595976 | tf_op jit(solution)/shard_map/ppermute | solution.py:105
  34.1 0.8 select_reduce_fusion
  34.9 2.2 %collective-permute-start.10 = (bf16[4,97,256]{2,0,1:T(4,128)(2,1)S(1)}, bf16[4,97,256]{2,0,1:T(4,128)(2,1)S(1)}, u32[]{:S(2)}, u32[]{:S(2)}) collective-permute-start(bf16[4,97,256]{2,0,1:T(4,128)(2,1)S(1)} %select_select_fusion.3), channel_id=1, source_target_pairs={{0,24},{4,28},{8,0},{12,4},{16,8},{20,12},{24,16},{28,20},{1,25},{... | collective-permute-start | bytes 595976 | tf_op jit(solution)/shard_map/ppermute | solution.py:105
  37.9 9.1 %collective-permute-done.11 = bf16[4,97,256]{2,0,1:T(4,128)(2,1)S(1)} collective-permute-done((bf16[4,97,256]{2,0,1:T(4,128)(2,1)S(1)}, bf16[4,97,256]{2,0,1:T(4,128)(2,1)S(1)}, u32[]{:S(2)}, u32[]{:S(2)}) %collective-permute-start.11) | collective-permute-done | bytes 198688 | tf_op jit(solution)/shard_map/ppermute | solution.py:105
  47.0 3.1 %collective-permute-start.6 = (bf16[48,1024]{1,0:T(8,128)(2,1)S(1)}, bf16[48,1024]{1,0:T(8,128)(2,1)S(1)}, u32[]{:S(2)}, u32[]{:S(2)}) collective-permute-start(bf16[48,1024]{1,0:T(8,128)(2,1)S(1)} %divide_convert_fusion), channel_id=1, source_target_pairs={{0,3},{1,0},{2,1},{3,2},{4,7},{5,4},{6,5},{7,6},{8,11},{9,8},{10,9... | collective-permute-start | bytes 294920 | tf_op jit(solution)/shard_map/ppermute | solution.py:105
  50.1 4.3 %select_select_fusion = bf16[8,4,97,256]{3,1,2,0:T(4,128)(2,1)S(1)} fusion(pred[8]{0:T(512)(128)(4,1)S(1)} %get-tuple-element.44, pred[8]{0:T(512)(128)(4,1)S(1)} %get-tuple-element.45, pred[8]{0:T(512)(128)(4,1)S(1)} %get-tuple-element.46, pred[8]{0:T(512)(128)(4,1)S(1)} %get-tuple-element.47, pred[8]{0:T(512)(128)(4,1)S(1)} %get-tuple-element.48, ...), kind=kLoop, calls=%fused_computation.14 | loop fusion | flops 5562368 | bytes 3178552 | tf_op jit(solution)/shard_map/jit(_where)/select_n | solution.py:98
  55.1 0.7 fusion.31
  55.9 1.1 copy.15
  57.3 1.7 %fusion.32 = (f32[384]{0:T(512)S(1)}, f32[384,384]{0,1:T(8,128)S(1)}) fusion(bf16[384,1024]{1,0:T(8,128)(2,1)} %bitcast.51, bf16[384,1024]{1,0:T(8,128)(2,1)S(1)} %bitcast.46), kind=kOutput, calls=%fused_computation.111 | convolution fusion | flops 302284416 | bytes 2164224 | tf_op jit(solution)/shard_map/dot_general | solution.py:195
  60.0 0.7 copy-done.3
  61.3 0.7 fusion.18
  62.1 16.2 %all_gather.3 = f32[48,4096]{1,0:T(8,128)S(1)} all-gather(f32[48,1024]{1,0:T(8,128)S(1)} %fusion.18), channel_id=1, replica_groups=mesh['dp'=8,'fsdp'=4] {'fsdp'}, dimensions={1}, use_global_device_ids=true | all-gather | bytes 983040 | tf_op jit(solution)/shard_map/all_gather | solution.py:222
  78.3 1.6 %fusion.8 = (f32[4096]{0:T(1024)S(1)}, f32[128]{0:T(128)S(1)}, f32[128,4096]{1,0:T(8,128)S(1)}) fusion(bf16[128,4096]{1,0:T(8,128)(2,1)S(1)} %copy-done.1, f32[128]{0:T(128)S(1)} %copy-done.20, f32[4096]{0:T(1024)S(1)} %convert_element_type.85, f32[48,4096]{1,0:T(8,128)S(1)} %all_gather.3, f32[48]{0:T(128)S(1)} %convert_reduce_fusion, s32[128]{0:T(128)S(1)} %bitcast.63), kind=kOutput, calls=%fused_computation.13 | convolution fusion | flops 305858432 | bytes 3966656 | tf_op jit(solution)/shard_map/dot_general | solution.py:224
  80.3 2.4 %collective-permute-start.17 = (f32[4096]{0:T(1024)S(1)}, f32[4096]{0:T(1024)S(1)}, u32[]{:S(2)}, u32[]{:S(2)}) collective-permute-start(f32[4096]{0:T(1024)S(1)} %get-tuple-element.10), channel_id=1, source_target_pairs={{0,2},{1,3},{2,0},{3,1},{4,6},{5,7},{6,4},{7,5},{8,10},{9,11},{10,... | collective-permute-start | bytes 49160 | tf_op jit(solution)/shard_map/ppermute | solution.py:105
  82.7 1.2 %collective-permute-start.16 = (f32[4096]{0:T(1024)S(1)}, f32[4096]{0:T(1024)S(1)}, u32[]{:S(2)}, u32[]{:S(2)}) collective-permute-start(f32[4096]{0:T(1024)S(1)} %get-tuple-element.10), channel_id=1, source_target_pairs={{0,3},{1,0},{2,1},{3,2},{4,7},{5,4},{6,5},{7,6},{8,11},{9,8},{10,9... | collective-permute-start | bytes 49160 | tf_op jit(solution)/shard_map/ppermute | solution.py:105
  84.8 0.8 collective-permute-done.16
  85.9 7.3 %collective-permute-start.24 = (f32[28672]{0:T(1024)S(1)}, f32[28672]{0:T(1024)S(1)}, u32[]{:S(2)}, u32[]{:S(2)}) collective-permute-start(f32[28672]{0:T(1024)S(1)} %get-tuple-element.34), channel_id=1, source_target_pairs={{0,8},{4,12},{8,16},{12,20},{16,24},{20,28},{24,0},{28,4},{1,9},{5... | collective-permute-start | bytes 344072 | tf_op jit(solution)/shard_map/ppermute | solution.py:134
  93.2 1.6 %fusion.5 = bf16[128,4096]{1,0:T(8,128)(2,1)} fusion(bf16[128,4096]{1,0:T(8,128)(2,1)S(1)} %copy-done.1, f32[128,4096]{1,0:T(8,128)S(1)} %get-tuple-element.42, f32[128]{0:T(128)S(1)} %broadcast_multiply_fusion, f32[128]{0:T(128)S(1)} %copy-done.18, f32[4096]{0:T(1024)S(1)} %convert_element_type.85, f32[128]{0:T(128)S(1)} %copy-done.20), kind=kLoop, calls=%fused_computation.10 | loop fusion | flops 3670016 | bytes 4212224 | tf_op jit(solution)/shard_map/convert_element_type | solution.py:234
  95.0 1.8 %collective-permute-start.21 = (f32[28672]{0:T(1024)S(1)}, f32[28672]{0:T(1024)}, u32[]{:S(2)}, u32[]{:S(2)}) collective-permute-start(f32[28672]{0:T(1024)S(1)} %get-tuple-element.31), channel_id=1, source_target_pairs={{0,20},{4,24},{8,28},{12,0},{16,4},{20,8},{24,12},{28,16},{1,21},{... | collective-permute-start | bytes 344072 | tf_op jit(solution)/shard_map/ppermute | solution.py:134
  96.9 1.3 %collective-permute-start.20 = (f32[28672]{0:T(1024)S(1)}, f32[28672]{0:T(1024)}, u32[]{:S(2)}, u32[]{:S(2)}) collective-permute-start(f32[28672]{0:T(1024)S(1)} %get-tuple-element.30), channel_id=1, source_target_pairs={{0,24},{4,28},{8,0},{12,4},{16,8},{20,12},{24,16},{28,20},{1,25},{... | collective-permute-start | bytes 344072 | tf_op jit(solution)/shard_map/ppermute | solution.py:134
  99.6 1.7 %convolution_multiply_fusion.2 = f32[48,256]{1,0:T(8,128)} fusion(bf16[384,1024]{1,0:T(8,128)(2,1)} %bitcast.52, s32[]{:T(128)S(6)} %select_n.360, bf16[384,384]{0,1:T(8,128)(2,1)} %copy-done.3, s32[]{:T(128)S(6)} %select_n.359), kind=kOutput, calls=%fused_computation.17 | convolution fusion | flops 9449472 | bytes 282632 | tf_op jit(solution)/shard_map/dot_general | solution.py:215
  101.5 3.1 %collective-permute-done.22 = f32[28672]{0:T(1024)S(1)} collective-permute-done((f32[28672]{0:T(1024)S(1)}, f32[28672]{0:T(1024)S(1)}, u32[]{:S(2)}, u32[]{:S(2)}) %collective-permute-start.22) | collective-permute-done | bytes 114720 | tf_op jit(solution)/shard_map/ppermute | solution.py:134
  104.6 1.5 %collective-permute-done.21 = f32[28672]{0:T(1024)} collective-permute-done((f32[28672]{0:T(1024)S(1)}, f32[28672]{0:T(1024)}, u32[]{:S(2)}, u32[]{:S(2)}) %collective-permute-start.21) | collective-permute-done | bytes 114720 | tf_op jit(solution)/shard_map/ppermute | solution.py:134
  106.1 0.9 slice.160
  107.1 0.9 slice.159
  108.0 0.9 slice.158
  109.3 2.1 %fusion.16 = f32[512,256]{1,0:T(8,128)} fusion(bf16[384,512]{1,0:T(8,128)(2,1)S(1)} %bitcast.50, f32[384,1024]{1,0:T(8,128)} %copy-done.2, s32[]{:T(128)S(6)} %select_n.360), kind=kOutput, calls=%fused_computation.40 | convolution fusion | flops 100663296 | bytes 1114116 | tf_op jit(solution)/shard_map/dot_general | solution.py:239
  111.5 0.7 slice.153
  112.2 0.7 slice.152
  112.9 0.7 slice.151
  113.6 0.7 select_reduce_fusion.2
  (122 shorter events, 8.5 us)
Async XLA Ops:
  0.6 60.6 %copy-start = (bf16[1024,1024]{1,0:T(8,128)(2,1)S(1)}, bf16[1024,1024]{1,0:T(8,128)(2,1)}, u32[]{:S(2)}) copy-start(bf16[1024,1024]{1,0:T(8,128)(2,1)} %param.13) | copy-start | bytes 6291460
  3.7 12.5 %collective-permute-start.5 = (bf16[97,256]{1,0:T(8,128)(2,1)S(1)}, bf16[97,256]{1,0:T(8,128)(2,1)}, u32[]{:S(2)}, u32[]{:S(2)}) collective-permute-start(bf16[97,256]{1,0:T(8,128)(2,1)S(1)} %constant_dynamic-update-slice_fusion), channel_id=1, source_target_pairs={{0,1},{1,2},{2,3},{3,0},{4,5},{5,6},{6,7},{7,4},{8,9},{9,10},{10,1... | collective-permute-start | bytes 149000 | tf_op jit(solution)/shard_map/ppermute | solution.py:105
  5.0 11.3 %collective-permute-start.4 = (bf16[97,256]{1,0:T(8,128)(2,1)S(1)}, bf16[97,256]{1,0:T(8,128)(2,1)}, u32[]{:S(2)}, u32[]{:S(2)}) collective-permute-start(bf16[97,256]{1,0:T(8,128)(2,1)S(1)} %constant_dynamic-update-slice_fusion), channel_id=1, source_target_pairs={{0,2},{1,3},{2,0},{3,1},{4,6},{5,7},{6,4},{7,5},{8,10},{9,11},{10,... | collective-permute-start | bytes 149000 | tf_op jit(solution)/shard_map/ppermute | solution.py:105
  6.1 10.2 %collective-permute-start.3 = (bf16[97,256]{1,0:T(8,128)(2,1)S(1)}, bf16[97,256]{1,0:T(8,128)(2,1)}, u32[]{:S(2)}, u32[]{:S(2)}) collective-permute-start(bf16[97,256]{1,0:T(8,128)(2,1)S(1)} %constant_dynamic-update-slice_fusion), channel_id=1, source_target_pairs={{0,3},{1,0},{2,1},{3,2},{4,7},{5,4},{6,5},{7,6},{8,11},{9,8},{10,9... | collective-permute-start | bytes 149000 | tf_op jit(solution)/shard_map/ppermute | solution.py:105
  10.3 1.7 %copy-start.19 = (f32[128]{0:T(128)}, f32[128]{0:T(128)S(1)}, u32[]{:S(2)}) copy-start(f32[128]{0:T(128)S(1)} %get-tuple-element.37) | copy-start | bytes 1540
  12.8 9.3 %collective-permute-start.2 = (f32[48,1024]{1,0:T(8,128)}, f32[48,1024]{1,0:T(8,128)S(1)}, u32[]{:S(2)}, u32[]{:S(2)}) collective-permute-start(f32[48,1024]{1,0:T(8,128)} %get-tuple-element.27), channel_id=1, source_target_pairs={{0,1},{1,2},{2,3},{3,0},{4,5},{5,6},{6,7},{7,4},{8,9},{9,10},{10,1... | collective-permute-start | bytes 589832 | tf_op jit(solution)/shard_map/ppermute | solution.py:121
  12.9 16.2 %collective-permute-start.1 = (f32[48,1024]{1,0:T(8,128)S(1)}, f32[48,1024]{1,0:T(8,128)S(1)}, u32[]{:S(2)}, u32[]{:S(2)}) collective-permute-start(f32[48,1024]{1,0:T(8,128)S(1)} %get-tuple-element.28), channel_id=1, source_target_pairs={{0,2},{1,3},{2,0},{3,1},{4,6},{5,7},{6,4},{7,5},{8,10},{9,11},{10,... | collective-permute-start | bytes 589832 | tf_op jit(solution)/shard_map/ppermute | solution.py:121
  16.0 38.4 %copy-start.4 = (pred[8]{0:T(512)(128)(4,1)}, pred[8]{0:T(512)(128)(4,1)S(1)}, u32[]{:S(2)}) copy-start(pred[8]{0:T(512)(128)(4,1)S(1)} %get-tuple-element.43) | copy-start | bytes 28
  16.0 38.4 %copy-start.6 = (pred[8]{0:T(512)(128)(4,1)}, pred[8]{0:T(512)(128)(4,1)S(1)}, u32[]{:S(2)}) copy-start(pred[8]{0:T(512)(128)(4,1)S(1)} %get-tuple-element.44) | copy-start | bytes 28
  16.0 38.4 %copy-start.8 = (pred[8]{0:T(512)(128)(4,1)}, pred[8]{0:T(512)(128)(4,1)S(1)}, u32[]{:S(2)}) copy-start(pred[8]{0:T(512)(128)(4,1)S(1)} %get-tuple-element.45) | copy-start | bytes 28
  16.0 38.4 %copy-start.10 = (pred[8]{0:T(512)(128)(4,1)}, pred[8]{0:T(512)(128)(4,1)S(1)}, u32[]{:S(2)}) copy-start(pred[8]{0:T(512)(128)(4,1)S(1)} %get-tuple-element.46) | copy-start | bytes 28
  16.1 38.4 %copy-start.12 = (pred[8]{0:T(512)(128)(4,1)}, pred[8]{0:T(512)(128)(4,1)S(1)}, u32[]{:S(2)}) copy-start(pred[8]{0:T(512)(128)(4,1)S(1)} %get-tuple-element.47) | copy-start | bytes 28
  16.1 38.4 %copy-start.14 = (pred[8]{0:T(512)(128)(4,1)}, pred[8]{0:T(512)(128)(4,1)S(1)}, u32[]{:S(2)}) copy-start(pred[8]{0:T(512)(128)(4,1)S(1)} %get-tuple-element.48) | copy-start | bytes 28
  16.1 38.4 %copy-start.16 = (pred[8]{0:T(512)(128)(4,1)}, pred[8]{0:T(512)(128)(4,1)S(1)}, u32[]{:S(2)}) copy-start(pred[8]{0:T(512)(128)(4,1)S(1)} %broadcast_compare_fusion.6) | copy-start | bytes 28
  16.2 16.5 %collective-permute-start = (f32[48,1024]{1,0:T(8,128)S(1)}, f32[48,1024]{1,0:T(8,128)S(1)}, u32[]{:S(2)}, u32[]{:S(2)}) collective-permute-start(f32[48,1024]{1,0:T(8,128)S(1)} %get-tuple-element.25), channel_id=1, source_target_pairs={{0,3},{1,0},{2,1},{3,2},{4,7},{5,4},{6,5},{7,6},{8,11},{9,8},{10,9... | collective-permute-start | bytes 589832 | tf_op jit(solution)/shard_map/ppermute | solution.py:121
  17.4 17.5 %collective-permute-start.15 = (bf16[4,97,256]{2,0,1:T(4,128)(2,1)S(1)}, bf16[4,97,256]{2,0,1:T(4,128)(2,1)S(1)}, u32[]{:S(2)}, u32[]{:S(2)}) collective-permute-start(bf16[4,97,256]{2,0,1:T(4,128)(2,1)S(1)} %select_select_fusion.3), channel_id=1, source_target_pairs={{0,4},{4,8},{8,12},{12,16},{16,20},{20,24},{24,28},{28,0},{1,5},{5... | collective-permute-start | bytes 595976 | tf_op jit(solution)/shard_map/ppermute | solution.py:105
  20.7 16.5 %collective-permute-start.14 = (bf16[4,97,256]{2,0,1:T(4,128)(2,1)S(1)}, bf16[4,97,256]{2,0,1:T(4,128)(2,1)S(1)}, u32[]{:S(2)}, u32[]{:S(2)}) collective-permute-start(bf16[4,97,256]{2,0,1:T(4,128)(2,1)S(1)} %select_select_fusion.3), channel_id=1, source_target_pairs={{0,8},{4,12},{8,16},{12,20},{16,24},{20,28},{24,0},{28,4},{1,9},{5... | collective-permute-start | bytes 595976 | tf_op jit(solution)/shard_map/ppermute | solution.py:105
  22.1 15.2 %collective-permute-start.13 = (bf16[4,97,256]{2,0,1:T(4,128)(2,1)S(1)}, bf16[4,97,256]{2,0,1:T(4,128)(2,1)S(1)}, u32[]{:S(2)}, u32[]{:S(2)}) collective-permute-start(bf16[4,97,256]{2,0,1:T(4,128)(2,1)S(1)} %select_select_fusion.3), channel_id=1, source_target_pairs={{0,12},{4,16},{8,20},{12,24},{16,28},{20,0},{24,4},{28,8},{1,13},{... | collective-permute-start | bytes 595976 | tf_op jit(solution)/shard_map/ppermute | solution.py:105
  29.1 8.2 %collective-permute-start.12 = (bf16[4,97,256]{2,0,1:T(4,128)(2,1)S(1)}, bf16[4,97,256]{2,0,1:T(4,128)(2,1)S(1)}, u32[]{:S(2)}, u32[]{:S(2)}) collective-permute-start(bf16[4,97,256]{2,0,1:T(4,128)(2,1)S(1)} %select_select_fusion.3), channel_id=1, source_target_pairs={{0,16},{4,20},{8,24},{12,28},{16,0},{20,4},{24,8},{28,12},{1,17},{... | collective-permute-start | bytes 595976 | tf_op jit(solution)/shard_map/ppermute | solution.py:105
  32.7 14.3 %collective-permute-start.11 = (bf16[4,97,256]{2,0,1:T(4,128)(2,1)S(1)}, bf16[4,97,256]{2,0,1:T(4,128)(2,1)S(1)}, u32[]{:S(2)}, u32[]{:S(2)}) collective-permute-start(bf16[4,97,256]{2,0,1:T(4,128)(2,1)S(1)} %select_select_fusion.3), channel_id=1, source_target_pairs={{0,20},{4,24},{8,28},{12,0},{16,4},{20,8},{24,12},{28,16},{1,21},{... | collective-permute-start | bytes 595976 | tf_op jit(solution)/shard_map/ppermute | solution.py:105
  34.9 15.2 %collective-permute-start.10 = (bf16[4,97,256]{2,0,1:T(4,128)(2,1)S(1)}, bf16[4,97,256]{2,0,1:T(4,128)(2,1)S(1)}, u32[]{:S(2)}, u32[]{:S(2)}) collective-permute-start(bf16[4,97,256]{2,0,1:T(4,128)(2,1)S(1)} %select_select_fusion.3), channel_id=1, source_target_pairs={{0,24},{4,28},{8,0},{12,4},{16,8},{20,12},{24,16},{28,20},{1,25},{... | collective-permute-start | bytes 595976 | tf_op jit(solution)/shard_map/ppermute | solution.py:105
  37.2 13.0 %collective-permute-start.9 = (bf16[4,97,256]{2,0,1:T(4,128)(2,1)S(1)}, bf16[4,97,256]{2,0,1:T(4,128)(2,1)S(1)}, u32[]{:S(2)}, u32[]{:S(2)}) collective-permute-start(bf16[4,97,256]{2,0,1:T(4,128)(2,1)S(1)} %select_select_fusion.3), channel_id=1, source_target_pairs={{0,28},{4,0},{8,4},{12,8},{16,12},{20,16},{24,20},{28,24},{1,29},{... | collective-permute-start | bytes 595976 | tf_op jit(solution)/shard_map/ppermute | solution.py:105
  37.3 17.2 %collective-permute-start.8 = (bf16[48,1024]{1,0:T(8,128)(2,1)S(1)}, bf16[48,1024]{1,0:T(8,128)(2,1)S(1)}, u32[]{:S(2)}, u32[]{:S(2)}) collective-permute-start(bf16[48,1024]{1,0:T(8,128)(2,1)S(1)} %divide_convert_fusion), channel_id=1, source_target_pairs={{0,1},{1,2},{2,3},{3,0},{4,5},{5,6},{6,7},{7,4},{8,9},{9,10},{10,1... | collective-permute-start | bytes 294920 | tf_op jit(solution)/shard_map/ppermute | solution.py:105
  37.3 17.1 %collective-permute-start.7 = (bf16[48,1024]{1,0:T(8,128)(2,1)S(1)}, bf16[48,1024]{1,0:T(8,128)(2,1)S(1)}, u32[]{:S(2)}, u32[]{:S(2)}) collective-permute-start(bf16[48,1024]{1,0:T(8,128)(2,1)S(1)} %divide_convert_fusion), channel_id=1, source_target_pairs={{0,2},{1,3},{2,0},{3,1},{4,6},{5,7},{6,4},{7,5},{8,10},{9,11},{10,... | collective-permute-start | bytes 294920 | tf_op jit(solution)/shard_map/ppermute | solution.py:105
  47.0 7.5 %collective-permute-start.6 = (bf16[48,1024]{1,0:T(8,128)(2,1)S(1)}, bf16[48,1024]{1,0:T(8,128)(2,1)S(1)}, u32[]{:S(2)}, u32[]{:S(2)}) collective-permute-start(bf16[48,1024]{1,0:T(8,128)(2,1)S(1)} %divide_convert_fusion), channel_id=1, source_target_pairs={{0,3},{1,0},{2,1},{3,2},{4,7},{5,4},{6,5},{7,6},{8,11},{9,8},{10,9... | collective-permute-start | bytes 294920 | tf_op jit(solution)/shard_map/ppermute | solution.py:105
  60.0 0.7 copy-start.3
  61.3 37.0 %copy-start.2 = (f32[384,1024]{1,0:T(8,128)}, f32[384,1024]{1,0:T(8,128)S(1)}, u32[]{:S(2)}) copy-start(f32[384,1024]{1,0:T(8,128)S(1)} %convolution_multiply_fusion) | copy-start | bytes 4718596
  61.3 17.0 %copy-start.1 = (bf16[128,4096]{1,0:T(8,128)(2,1)S(1)}, bf16[128,4096]{1,0:T(8,128)(2,1)}, u32[]{:S(2)}) copy-start(bf16[128,4096]{1,0:T(8,128)(2,1)} %param.10) | copy-start | bytes 3145732
  61.3 17.0 %copy-start.20 = (f32[128]{0:T(128)S(1)}, f32[128]{0:T(128)}, u32[]{:S(2)}) copy-start(f32[128]{0:T(128)} %copy-done.19) | copy-start | bytes 1540
  61.3 17.0 %copy-start.21 = (s32[1,128]{1,0:T(1,128)S(1)}, s32[1,128]{1,0:T(1,128)}, u32[]{:S(2)}) copy-start(s32[1,128]{1,0:T(1,128)} %param.11) | copy-start | bytes 1540
  79.9 13.3 %copy-start.18 = (f32[128]{0:T(128)S(1)}, f32[128]{0:T(128)}, u32[]{:S(2)}) copy-start(f32[128]{0:T(128)} %get-tuple-element.36) | copy-start | bytes 1540
  80.0 4.8 %collective-permute-start.18 = (f32[4096]{0:T(1024)S(1)}, f32[4096]{0:T(1024)S(1)}, u32[]{:S(2)}, u32[]{:S(2)}) collective-permute-start(f32[4096]{0:T(1024)S(1)} %get-tuple-element.10), channel_id=1, source_target_pairs={{0,1},{1,2},{2,3},{3,0},{4,5},{5,6},{6,7},{7,4},{8,9},{9,10},{10,1... | collective-permute-start | bytes 49160 | tf_op jit(solution)/shard_map/ppermute | solution.py:105
  80.3 4.5 %collective-permute-start.17 = (f32[4096]{0:T(1024)S(1)}, f32[4096]{0:T(1024)S(1)}, u32[]{:S(2)}, u32[]{:S(2)}) collective-permute-start(f32[4096]{0:T(1024)S(1)} %get-tuple-element.10), channel_id=1, source_target_pairs={{0,2},{1,3},{2,0},{3,1},{4,6},{5,7},{6,4},{7,5},{8,10},{9,11},{10,... | collective-permute-start | bytes 49160 | tf_op jit(solution)/shard_map/ppermute | solution.py:105
  82.7 2.9 %collective-permute-start.16 = (f32[4096]{0:T(1024)S(1)}, f32[4096]{0:T(1024)S(1)}, u32[]{:S(2)}, u32[]{:S(2)}) collective-permute-start(f32[4096]{0:T(1024)S(1)} %get-tuple-element.10), channel_id=1, source_target_pairs={{0,3},{1,0},{2,1},{3,2},{4,7},{5,4},{6,5},{7,6},{8,11},{9,8},{10,9... | collective-permute-start | bytes 49160 | tf_op jit(solution)/shard_map/ppermute | solution.py:105
  85.8 11.0 %collective-permute-start.25 = (f32[28672]{0:T(1024)S(1)}, f32[28672]{0:T(1024)S(1)}, u32[]{:S(2)}, u32[]{:S(2)}) collective-permute-start(f32[28672]{0:T(1024)S(1)} %get-tuple-element.35), channel_id=1, source_target_pairs={{0,4},{4,8},{8,12},{12,16},{16,20},{20,24},{24,28},{28,0},{1,5},{5... | collective-permute-start | bytes 344072 | tf_op jit(solution)/shard_map/ppermute | solution.py:134
  85.9 12.3 %collective-permute-start.24 = (f32[28672]{0:T(1024)S(1)}, f32[28672]{0:T(1024)S(1)}, u32[]{:S(2)}, u32[]{:S(2)}) collective-permute-start(f32[28672]{0:T(1024)S(1)} %get-tuple-element.34), channel_id=1, source_target_pairs={{0,8},{4,12},{8,16},{12,20},{16,24},{20,28},{24,0},{28,4},{1,9},{5... | collective-permute-start | bytes 344072 | tf_op jit(solution)/shard_map/ppermute | solution.py:134
  94.8 14.1 %copy-start.5 = (pred[8]{0:T(512)(128)(4,1)S(1)}, pred[8]{0:T(512)(128)(4,1)}, u32[]{:S(2)}) copy-start(pred[8]{0:T(512)(128)(4,1)} %copy-done.4) | copy-start | bytes 28
  94.8 14.2 %copy-start.7 = (pred[8]{0:T(512)(128)(4,1)S(1)}, pred[8]{0:T(512)(128)(4,1)}, u32[]{:S(2)}) copy-start(pred[8]{0:T(512)(128)(4,1)} %copy-done.6) | copy-start | bytes 28
  94.8 14.2 %copy-start.9 = (pred[8]{0:T(512)(128)(4,1)S(1)}, pred[8]{0:T(512)(128)(4,1)}, u32[]{:S(2)}) copy-start(pred[8]{0:T(512)(128)(4,1)} %copy-done.8) | copy-start | bytes 28
  94.9 14.2 %copy-start.11 = (pred[8]{0:T(512)(128)(4,1)S(1)}, pred[8]{0:T(512)(128)(4,1)}, u32[]{:S(2)}) copy-start(pred[8]{0:T(512)(128)(4,1)} %copy-done.10) | copy-start | bytes 28
  94.9 14.2 %copy-start.13 = (pred[8]{0:T(512)(128)(4,1)S(1)}, pred[8]{0:T(512)(128)(4,1)}, u32[]{:S(2)}) copy-start(pred[8]{0:T(512)(128)(4,1)} %copy-done.12) | copy-start | bytes 28
  94.9 14.2 %copy-start.15 = (pred[8]{0:T(512)(128)(4,1)S(1)}, pred[8]{0:T(512)(128)(4,1)}, u32[]{:S(2)}) copy-start(pred[8]{0:T(512)(128)(4,1)} %copy-done.14) | copy-start | bytes 28
  94.9 14.2 %copy-start.17 = (pred[8]{0:T(512)(128)(4,1)S(1)}, pred[8]{0:T(512)(128)(4,1)}, u32[]{:S(2)}) copy-start(pred[8]{0:T(512)(128)(4,1)} %copy-done.16) | copy-start | bytes 28
  94.9 6.5 %collective-permute-start.23 = (f32[28672]{0:T(1024)S(1)}, f32[28672]{0:T(1024)S(1)}, u32[]{:S(2)}, u32[]{:S(2)}) collective-permute-start(f32[28672]{0:T(1024)S(1)} %get-tuple-element.33), channel_id=1, source_target_pairs={{0,12},{4,16},{8,20},{12,24},{16,28},{20,0},{24,4},{28,8},{1,13},{... | collective-permute-start | bytes 344072 | tf_op jit(solution)/shard_map/ppermute | solution.py:134
  95.0 9.6 %collective-permute-start.22 = (f32[28672]{0:T(1024)S(1)}, f32[28672]{0:T(1024)S(1)}, u32[]{:S(2)}, u32[]{:S(2)}) collective-permute-start(f32[28672]{0:T(1024)S(1)} %get-tuple-element.32), channel_id=1, source_target_pairs={{0,16},{4,20},{8,24},{12,28},{16,0},{20,4},{24,8},{28,12},{1,17},{... | collective-permute-start | bytes 344072 | tf_op jit(solution)/shard_map/ppermute | solution.py:134
  95.0 11.1 %collective-permute-start.21 = (f32[28672]{0:T(1024)S(1)}, f32[28672]{0:T(1024)}, u32[]{:S(2)}, u32[]{:S(2)}) collective-permute-start(f32[28672]{0:T(1024)S(1)} %get-tuple-element.31), channel_id=1, source_target_pairs={{0,20},{4,24},{8,28},{12,0},{16,4},{20,8},{24,12},{28,16},{1,21},{... | collective-permute-start | bytes 344072 | tf_op jit(solution)/shard_map/ppermute | solution.py:134
  96.9 10.2 %collective-permute-start.20 = (f32[28672]{0:T(1024)S(1)}, f32[28672]{0:T(1024)}, u32[]{:S(2)}, u32[]{:S(2)}) collective-permute-start(f32[28672]{0:T(1024)S(1)} %get-tuple-element.30), channel_id=1, source_target_pairs={{0,24},{4,28},{8,0},{12,4},{16,8},{20,12},{24,16},{28,20},{1,25},{... | collective-permute-start | bytes 344072 | tf_op jit(solution)/shard_map/ppermute | solution.py:134
  98.2 9.9 %collective-permute-start.19 = (f32[28672]{0:T(1024)S(1)}, f32[28672]{0:T(1024)}, u32[]{:S(2)}, u32[]{:S(2)}) collective-permute-start(f32[28672]{0:T(1024)S(1)} %get-tuple-element.29), channel_id=1, source_target_pairs={{0,28},{4,0},{8,4},{12,8},{16,12},{20,16},{24,20},{28,24},{1,29},{... | collective-permute-start | bytes 344072 | tf_op jit(solution)/shard_map/ppermute | solution.py:134

commit v16 on v14

--- a/solution.py
+++ b/solution.py
@@ -219,7 +219,8 @@
     mean_part = lax.dot_general(
         grad_low, proj_weight, contract_last, preferred_element_type=jnp.float32
     )
-    mean_grad = lax.all_gather(mean_part, "fsdp", axis=1, tiled=True)
+    mean_grad = lax.optimization_barrier(gather_blocks(mean_part, "fsdp"))
+    mean_grad = mean_grad.transpose(1, 0, 2).reshape(rows, model_width)
     pool_grad = mean_grad / counts[:, None]
     normed_grad = lax.dot_general(
         member.astype(jnp.float32),

time: 110 us -> 109 us (level)
  blocking collectives: 19 us -> 0 us
  waiting for transfers between devices: 11 us -> 20.8 us
  starting transfers between devices: 41.7 us -> 50.2 us
  other arithmetic: 15 us -> 16.5 us
  local copies, waits for them, and re-layouts: 8.89 us -> 7.71 us
    all_gather x1 -> x0, blocking collectives: 19 us -> none  [local_small(): mean_grad = lax.all_gather(mean_part, 'fsdp', axis=1, tiled=True)]
    ppermute x16 -> x19, waiting for transfers between devices: 1.68 us -> 10.8 us  [gather_blocks(): lax.ppermute(x, axis, [(i, (i + s) % n) for i in range(n)])]
    ppermute x16 -> x19, starting transfers between devices: 23.1 us -> 31.1 us  [gather_blocks(): lax.ppermute(x, axis, [(i, (i + s) % n) for i in range(n)])]
    select_n x4 -> x5, other arithmetic: 6.1 us -> 7.62 us  [arrange(): out = jnp.where(source == s, copies[s][None], out)]
    unnamed x51 -> x52, local copies, waits for them, and re-layouts: 3.91 us -> 4.35 us
  transfers between devices with their start and end apart: 26 -> 29, of which waited for: 5 -> 8; matrix products, arithmetic and copies ran while one was open for 18% -> 18% of each run, Pallas kernels for 0% -> 0%
where the time goes in v16:
time: 109 us
  starting transfers between devices  50.2 us (46%)
  waiting for transfers between devices  20.8 us (19%)
  other arithmetic  16.5 us (15%)
  matrix products  10.3 us (9%)
  local copies, waits for them, and re-layouts  7.71 us (7%)
  between operations  3.2 us (3%)
    ppermute x19, starting transfers between devices, gather_blocks(): lax.ppermute(x, axis, [(i, (i + s) % n) for i in range(n)])  31.1 us
    ppermute x7, starting transfers between devices, spread_with_sum(): arrived = lax.ppermute(payload, axis, [(i, (i + s) % n) for i in range(n)])  15.3 us
    ppermute x19, waiting for transfers between devices, gather_blocks(): lax.ppermute(x, axis, [(i, (i + s) % n) for i in range(n)])  10.8 us
    ppermute x3, waiting for transfers between devices, scatter_sum(): lax.ppermute(piece, axis, [(i, (i + s) % n) for i in range(n)])  9.34 us
    select_n x5, other arithmetic, arrange(): out = jnp.where(source == s, copies[s][None], out)  7.62 us
    unnamed x52, local copies, waits for them, and re-layouts  4.35 us
    ppermute x3, starting transfers between devices, scatter_sum(): lax.ppermute(piece, axis, [(i, (i + s) % n) for i in range(n)])  3.88 us
  transfers between devices with their start and end apart: 29, of which 8 were waited for; matrix products, arithmetic and copies ran while one was open for 18% of the time, Pallas kernels for 0%

profile of v16, /device:TPU:0, one launch (start us, length us, event | category | flops | bytes accessed | tf_op | source)
XLA Modules:
  0.0 108.8 jit_solution(17495249993971738209)
XLA Ops:
  0.6 0.9 constant_dynamic-update-slice_fusion.2
  2.2 0.7 constant_dynamic-update-slice_fusion.1
  2.9 0.7 fusion.28
  3.7 3.1 %collective-permute-start.5 = (bf16[97,256]{1,0:T(8,128)(2,1)S(1)}, bf16[97,256]{1,0:T(8,128)(2,1)}, u32[]{:S(2)}, u32[]{:S(2)}) collective-permute-start(bf16[97,256]{1,0:T(8,128)(2,1)S(1)} %constant_dynamic-update-slice_fusion), channel_id=1, source_target_pairs={{0,1},{1,2},{2,3},{3,0},{4,5},{5,6},{6,7},{7,4},{8,9},{9,10},{10,1... | collective-permute-start | bytes 149000 | tf_op jit(solution)/shard_map/ppermute | solution.py:105
  6.8 2.6 %collective-permute-start.4 = (bf16[97,256]{1,0:T(8,128)(2,1)S(1)}, bf16[97,256]{1,0:T(8,128)(2,1)}, u32[]{:S(2)}, u32[]{:S(2)}) collective-permute-start(bf16[97,256]{1,0:T(8,128)(2,1)S(1)} %constant_dynamic-update-slice_fusion), channel_id=1, source_target_pairs={{0,2},{1,3},{2,0},{3,1},{4,6},{5,7},{6,4},{7,5},{8,10},{9,11},{10,... | collective-permute-start | bytes 149000 | tf_op jit(solution)/shard_map/ppermute | solution.py:105
  9.4 1.3 %collective-permute-start.3 = (bf16[97,256]{1,0:T(8,128)(2,1)S(1)}, bf16[97,256]{1,0:T(8,128)(2,1)}, u32[]{:S(2)}, u32[]{:S(2)}) collective-permute-start(bf16[97,256]{1,0:T(8,128)(2,1)S(1)} %constant_dynamic-update-slice_fusion), channel_id=1, source_target_pairs={{0,3},{1,0},{2,1},{3,2},{4,7},{5,4},{6,5},{7,6},{8,11},{9,8},{10,9... | collective-permute-start | bytes 149000 | tf_op jit(solution)/shard_map/ppermute | solution.py:105
  10.7 0.7 convert_element_type.85
  11.4 1.5 %fusion = f32[128]{0:T(128)S(1)} fusion(bf16[128,4096]{1,0:T(8,128)(2,1)} %param.10), kind=kLoop, calls=%fused_computation.5 | loop fusion | flops 1572736 | bytes 1049088 | tf_op jit(solution)/shard_map/reduce_sum | solution.py:168
  13.4 1.7 %fusion.9 = f32[48,4096]{1,0:T(8,128)S(1)} fusion(bf16[128,4096]{1,0:T(8,128)(2,1)} %param.10, f32[4096]{0:T(1024)S(1)} %convert_element_type.85, f32[128]{0:T(128)S(1)} %get-tuple-element.37, s32[128]{0:T(128)} %bitcast.67), kind=kOutput, calls=%fused_computation.18 | convolution fusion | flops 52434944 | bytes 1852416 | tf_op jit(solution)/shard_map/dot_general | solution.py:172
  15.2 0.8 constant_dynamic-slice_fusion.11
  16.0 0.7 collective-permute-start.2
  17.3 2.9 %collective-permute-start = (f32[48,1024]{1,0:T(8,128)S(1)}, f32[48,1024]{1,0:T(8,128)S(1)}, u32[]{:S(2)}, u32[]{:S(2)}) collective-permute-start(f32[48,1024]{1,0:T(8,128)S(1)} %get-tuple-element.25), channel_id=1, source_target_pairs={{0,3},{1,0},{2,1},{3,2},{4,7},{5,4},{6,5},{7,6},{8,11},{9,8},{10,9... | collective-permute-start | bytes 589832 | tf_op jit(solution)/shard_map/ppermute | solution.py:121
  20.1 1.1 %select_select_fusion.4 = bf16[4,97,256]{2,0,1:T(4,128)(2,1)S(1)} fusion(pred[4]{0:T(512)(128)(4,1)S(1)} %get-tuple-element.50, pred[4]{0:T(512)(128)(4,1)S(1)} %broadcast_compare_fusion.9, pred[4]{0:T(512)(128)(4,1)S(1)} %get-tuple-element.49, bf16[97,256]{1,0:T(8,128)(2,1)S(1)} %constant_dynamic-update-slice_fusion, ...), kind=kLoop, calls=%fused_computation.40 | loop fusion | flops 297984 | bytes 397324 | tf_op jit(solution)/shard_map/jit(_where)/select_n | solution.py:98
  21.3 1.5 %collective-permute-start.14 = (bf16[4,97,256]{2,0,1:T(4,128)(2,1)S(1)}, bf16[4,97,256]{2,0,1:T(4,128)(2,1)S(1)}, u32[]{:S(2)}, u32[]{:S(2)}) collective-permute-start(bf16[4,97,256]{2,0,1:T(4,128)(2,1)S(1)} %select_select_fusion.4), channel_id=1, source_target_pairs={{0,8},{4,12},{8,16},{12,20},{16,24},{20,28},{24,0},{28,4},{1,9},{5... | collective-permute-start | bytes 595976 | tf_op jit(solution)/shard_map/ppermute | solution.py:105
  23.1 2.8 %collective-permute-done.2 = f32[48,1024]{1,0:T(8,128)S(1)} collective-permute-done((f32[48,1024]{1,0:T(8,128)}, f32[48,1024]{1,0:T(8,128)S(1)}, u32[]{:S(2)}, u32[]{:S(2)}) %collective-permute-start.2) | collective-permute-done | bytes 196640 | tf_op jit(solution)/shard_map/ppermute | solution.py:121
  25.9 6.5 %collective-permute-done.1 = f32[48,1024]{1,0:T(8,128)S(1)} collective-permute-done((f32[48,1024]{1,0:T(8,128)S(1)}, f32[48,1024]{1,0:T(8,128)S(1)}, u32[]{:S(2)}, u32[]{:S(2)}) %collective-permute-start.1) | collective-permute-done | bytes 196640 | tf_op jit(solution)/shard_map/ppermute | solution.py:121
  32.4 1.5 %collective-permute-start.12 = (bf16[4,97,256]{2,0,1:T(4,128)(2,1)S(1)}, bf16[4,97,256]{2,0,1:T(4,128)(2,1)S(1)}, u32[]{:S(2)}, u32[]{:S(2)}) collective-permute-start(bf16[4,97,256]{2,0,1:T(4,128)(2,1)S(1)} %select_select_fusion.4), channel_id=1, source_target_pairs={{0,16},{4,20},{8,24},{12,28},{16,0},{20,4},{24,8},{28,12},{1,17},{... | collective-permute-start | bytes 595976 | tf_op jit(solution)/shard_map/ppermute | solution.py:105
  33.9 0.8 select_reduce_fusion
  34.8 1.5 %collective-permute-start.10 = (bf16[4,97,256]{2,0,1:T(4,128)(2,1)S(1)}, bf16[4,97,256]{2,0,1:T(4,128)(2,1)S(1)}, u32[]{:S(2)}, u32[]{:S(2)}) collective-permute-start(bf16[4,97,256]{2,0,1:T(4,128)(2,1)S(1)} %select_select_fusion.4), channel_id=1, source_target_pairs={{0,24},{4,28},{8,0},{12,4},{16,8},{20,12},{24,16},{28,20},{1,25},{... | collective-permute-start | bytes 595976 | tf_op jit(solution)/shard_map/ppermute | solution.py:105
  36.2 2.4 %collective-permute-start.9 = (bf16[4,97,256]{2,0,1:T(4,128)(2,1)S(1)}, bf16[4,97,256]{2,0,1:T(4,128)(2,1)S(1)}, u32[]{:S(2)}, u32[]{:S(2)}) collective-permute-start(bf16[4,97,256]{2,0,1:T(4,128)(2,1)S(1)} %select_select_fusion.4), channel_id=1, source_target_pairs={{0,28},{4,0},{8,4},{12,8},{16,12},{20,16},{24,20},{28,24},{1,29},{... | collective-permute-start | bytes 595976 | tf_op jit(solution)/shard_map/ppermute | solution.py:105
  38.8 2.4 %collective-permute-start.8 = (bf16[48,1024]{1,0:T(8,128)(2,1)S(1)}, bf16[48,1024]{1,0:T(8,128)(2,1)S(1)}, u32[]{:S(2)}, u32[]{:S(2)}) collective-permute-start(bf16[48,1024]{1,0:T(8,128)(2,1)S(1)} %divide_convert_fusion), channel_id=1, source_target_pairs={{0,1},{1,2},{2,3},{3,0},{4,5},{5,6},{6,7},{7,4},{8,9},{9,10},{10,1... | collective-permute-start | bytes 294920 | tf_op jit(solution)/shard_map/ppermute | solution.py:105
  41.2 1.8 %collective-permute-start.7 = (bf16[48,1024]{1,0:T(8,128)(2,1)S(1)}, bf16[48,1024]{1,0:T(8,128)(2,1)S(1)}, u32[]{:S(2)}, u32[]{:S(2)}) collective-permute-start(bf16[48,1024]{1,0:T(8,128)(2,1)S(1)} %divide_convert_fusion), channel_id=1, source_target_pairs={{0,2},{1,3},{2,0},{3,1},{4,6},{5,7},{6,4},{7,5},{8,10},{9,11},{10,... | collective-permute-start | bytes 294920 | tf_op jit(solution)/shard_map/ppermute | solution.py:105
  43.0 1.0 collective-permute-start.6
  44.4 4.2 %select_select_fusion = bf16[8,4,97,256]{3,1,2,0:T(4,128)(2,1)S(1)} fusion(pred[8]{0:T(512)(128)(4,1)S(1)} %get-tuple-element.44, pred[8]{0:T(512)(128)(4,1)S(1)} %get-tuple-element.45, pred[8]{0:T(512)(128)(4,1)S(1)} %get-tuple-element.46, pred[8]{0:T(512)(128)(4,1)S(1)} %get-tuple-element.47, pred[8]{0:T(512)(128)(4,1)S(1)} %get-tuple-element.48, ...), kind=kLoop, calls=%fused_computation.14 | loop fusion | flops 5562368 | bytes 3178552 | tf_op jit(solution)/shard_map/jit(_where)/select_n | solution.py:98
  49.2 0.7 collective-permute-done.6
  50.6 0.7 fusion.31
  51.3 1.0 copy.15
  52.7 1.7 %fusion.32 = (f32[384]{0:T(512)S(1)}, f32[384,384]{0,1:T(8,128)S(1)}) fusion(bf16[384,1024]{1,0:T(8,128)(2,1)} %bitcast.55, bf16[384,1024]{1,0:T(8,128)(2,1)S(1)} %bitcast.50), kind=kOutput, calls=%fused_computation.112 | convolution fusion | flops 302284416 | bytes 2164224 | tf_op jit(solution)/shard_map/dot_general | solution.py:195
  55.4 0.7 copy-done.3
  56.7 0.7 fusion.18
  57.5 2.3 %collective-permute-start.18 = (f32[48,1024]{1,0:T(8,128)S(1)}, f32[48,1024]{1,0:T(8,128)}, u32[]{:S(2)}, u32[]{:S(2)}) collective-permute-start(f32[48,1024]{1,0:T(8,128)S(1)} %fusion.18), channel_id=1, source_target_pairs={{0,1},{1,2},{2,3},{3,0},{4,5},{5,6},{6,7},{7,4},{8,9},{9,10},{10,1... | collective-permute-start | bytes 589832 | tf_op jit(solution)/shard_map/ppermute | solution.py:105
  59.8 0.7 collective-permute-start.17
  60.5 1.7 %collective-permute-start.16 = (f32[48,1024]{1,0:T(8,128)S(1)}, f32[48,1024]{1,0:T(8,128)}, u32[]{:S(2)}, u32[]{:S(2)}) collective-permute-start(f32[48,1024]{1,0:T(8,128)S(1)} %fusion.18), channel_id=1, source_target_pairs={{0,3},{1,0},{2,1},{3,2},{4,7},{5,4},{6,5},{7,6},{8,11},{9,8},{10,9... | collective-permute-start | bytes 589832 | tf_op jit(solution)/shard_map/ppermute | solution.py:105
  63.8 1.7 %convolution_multiply_fusion.2 = f32[48,256]{1,0:T(8,128)} fusion(bf16[384,1024]{1,0:T(8,128)(2,1)} %bitcast.56, s32[]{:T(128)S(6)} %select_n.371, bf16[384,384]{0,1:T(8,128)(2,1)} %copy-done.3, s32[]{:T(128)S(6)} %select_n.370), kind=kOutput, calls=%fused_computation.17 | convolution fusion | flops 9449472 | bytes 282632 | tf_op jit(solution)/shard_map/dot_general | solution.py:215
  65.5 0.7 constant_dynamic-slice_fusion.7
  66.2 1.1 collective-permute-done.18
  67.3 8.1 %collective-permute-done.17 = f32[48,1024]{1,0:T(8,128)} collective-permute-done((f32[48,1024]{1,0:T(8,128)S(1)}, f32[48,1024]{1,0:T(8,128)}, u32[]{:S(2)}, u32[]{:S(2)}) %collective-permute-start.17) | collective-permute-done | bytes 196640 | tf_op jit(solution)/shard_map/ppermute | solution.py:105
  75.4 1.5 %select_select_fusion.2 = f32[4,48,1024]{2,0,1:T(4,128)S(1)} fusion(f32[48,1024]{1,0:T(8,128)S(1)} %fusion.18, f32[48,1024]{1,0:T(8,128)} %collective-permute-done.18, f32[48,1024]{1,0:T(8,128)} %collective-permute-done.17, f32[48,1024]{1,0:T(8,128)} %collective-permute-done.16, pred[4]{0:T(512)(128)(4,1)S(1)} %get-tuple-element.50, ...), kind=kLoop, calls=%fused_computation.24 | loop fusion | flops 589824 | bytes 1572876 | tf_op jit(solution)/shard_map/jit(_where)/select_n | solution.py:98
  77.4 1.7 %fusion.8 = (f32[4096]{0:T(1024)S(1)}, f32[128]{0:T(128)S(1)}, f32[128,4096]{1,0:T(8,128)S(1)}) fusion(bf16[128,4096]{1,0:T(8,128)(2,1)S(1)} %copy-done.1, f32[128]{0:T(128)S(1)} %copy-done.20, f32[4096]{0:T(1024)S(1)} %convert_element_type.85, f32[48,4096]{1,0:T(8,128)S(1)} %bitcast.57, f32[48]{0:T(128)S(1)} %convert_reduce_fusion, s32[128]{0:T(128)S(1)} %bitcast.68), kind=kOutput, calls=%fused_computation.13 | convolution fusion | flops 305858432 | bytes 3966656 | tf_op jit(solution)/shard_map/dot_general | solution.py:225
  79.2 7.3 %collective-permute-start.24 = (f32[28672]{0:T(1024)S(1)}, f32[28672]{0:T(1024)S(1)}, u32[]{:S(2)}, u32[]{:S(2)}) collective-permute-start(f32[28672]{0:T(1024)S(1)} %get-tuple-element.34), channel_id=1, source_target_pairs={{0,8},{4,12},{8,16},{12,20},{16,24},{20,28},{24,0},{28,4},{1,9},{5... | collective-permute-start | bytes 344072 | tf_op jit(solution)/shard_map/ppermute | solution.py:134
  86.5 2.4 %collective-permute-start.23 = (f32[28672]{0:T(1024)S(1)}, f32[28672]{0:T(1024)S(1)}, u32[]{:S(2)}, u32[]{:S(2)}) collective-permute-start(f32[28672]{0:T(1024)S(1)} %get-tuple-element.33), channel_id=1, source_target_pairs={{0,12},{4,16},{8,20},{12,24},{16,28},{20,0},{24,4},{28,8},{1,13},{... | collective-permute-start | bytes 344072 | tf_op jit(solution)/shard_map/ppermute | solution.py:134
  89.5 2.7 %collective-permute-start.20 = (f32[28672]{0:T(1024)S(1)}, f32[28672]{0:T(1024)S(1)}, u32[]{:S(2)}, u32[]{:S(2)}) collective-permute-start(f32[28672]{0:T(1024)S(1)} %get-tuple-element.30), channel_id=1, source_target_pairs={{0,24},{4,28},{8,0},{12,4},{16,8},{20,12},{24,16},{28,20},{1,25},{... | collective-permute-start | bytes 344072 | tf_op jit(solution)/shard_map/ppermute | solution.py:134
  92.2 2.2 %collective-permute-start.19 = (f32[28672]{0:T(1024)S(1)}, f32[28672]{0:T(1024)S(1)}, u32[]{:S(2)}, u32[]{:S(2)}) collective-permute-start(f32[28672]{0:T(1024)S(1)} %get-tuple-element.29), channel_id=1, source_target_pairs={{0,28},{4,0},{8,4},{12,8},{16,12},{20,16},{24,20},{28,24},{1,29},{... | collective-permute-start | bytes 344072 | tf_op jit(solution)/shard_map/ppermute | solution.py:134
  94.5 1.6 %fusion.5 = bf16[128,4096]{1,0:T(8,128)(2,1)} fusion(bf16[128,4096]{1,0:T(8,128)(2,1)S(1)} %copy-done.1, f32[128,4096]{1,0:T(8,128)S(1)} %get-tuple-element.42, f32[128]{0:T(128)S(1)} %broadcast_multiply_fusion, f32[128]{0:T(128)S(1)} %copy-done.18, f32[4096]{0:T(1024)S(1)} %convert_element_type.85, f32[128]{0:T(128)S(1)} %copy-done.20), kind=kLoop, calls=%fused_computation.10 | loop fusion | flops 3670016 | bytes 4212224 | tf_op jit(solution)/shard_map/convert_element_type | solution.py:235
  97.0 4.7 %collective-permute-start.28 = (f32[4096]{0:T(1024)S(1)}, f32[4096]{0:T(1024)S(1)}, u32[]{:S(2)}, u32[]{:S(2)}) collective-permute-start(f32[4096]{0:T(1024)S(1)} %select_reduce_fusion.2), channel_id=1, source_target_pairs={{0,1},{1,2},{2,3},{3,0},{4,5},{5,6},{6,7},{7,4},{8,9},{9,10},{10,1... | collective-permute-start | bytes 49160 | tf_op jit(solution)/shard_map/ppermute | solution.py:105
  101.7 2.4 %collective-permute-start.26 = (f32[4096]{0:T(1024)S(1)}, f32[4096]{0:T(1024)S(1)}, u32[]{:S(2)}, u32[]{:S(2)}) collective-permute-start(f32[4096]{0:T(1024)S(1)} %select_reduce_fusion.2), channel_id=1, source_target_pairs={{0,3},{1,0},{2,1},{3,2},{4,7},{5,4},{6,5},{7,6},{8,11},{9,8},{10,9... | collective-permute-start | bytes 49160 | tf_op jit(solution)/shard_map/ppermute | solution.py:105
  104.8 2.1 %fusion.16 = f32[512,256]{1,0:T(8,128)} fusion(bf16[384,512]{1,0:T(8,128)(2,1)S(1)} %bitcast.54, f32[384,1024]{1,0:T(8,128)} %copy-done.2, s32[]{:T(128)S(6)} %select_n.371), kind=kOutput, calls=%fused_computation.41 | convolution fusion | flops 100663296 | bytes 1114116 | tf_op jit(solution)/shard_map/dot_general | solution.py:239
  106.9 0.7 select_reduce_fusion.3
  (129 shorter events, 8.9 us)
Async XLA Ops:
  0.6 56.1 %copy-start = (bf16[1024,1024]{1,0:T(8,128)(2,1)S(1)}, bf16[1024,1024]{1,0:T(8,128)(2,1)}, u32[]{:S(2)}) copy-start(bf16[1024,1024]{1,0:T(8,128)(2,1)} %param.13) | copy-start | bytes 6291460
  3.7 13.6 %collective-permute-start.5 = (bf16[97,256]{1,0:T(8,128)(2,1)S(1)}, bf16[97,256]{1,0:T(8,128)(2,1)}, u32[]{:S(2)}, u32[]{:S(2)}) collective-permute-start(bf16[97,256]{1,0:T(8,128)(2,1)S(1)} %constant_dynamic-update-slice_fusion), channel_id=1, source_target_pairs={{0,1},{1,2},{2,3},{3,0},{4,5},{5,6},{6,7},{7,4},{8,9},{9,10},{10,1... | collective-permute-start | bytes 149000 | tf_op jit(solution)/shard_map/ppermute | solution.py:105
  6.8 13.4 %collective-permute-start.4 = (bf16[97,256]{1,0:T(8,128)(2,1)S(1)}, bf16[97,256]{1,0:T(8,128)(2,1)}, u32[]{:S(2)}, u32[]{:S(2)}) collective-permute-start(bf16[97,256]{1,0:T(8,128)(2,1)S(1)} %constant_dynamic-update-slice_fusion), channel_id=1, source_target_pairs={{0,2},{1,3},{2,0},{3,1},{4,6},{5,7},{6,4},{7,5},{8,10},{9,11},{10,... | collective-permute-start | bytes 149000 | tf_op jit(solution)/shard_map/ppermute | solution.py:105
  9.4 10.8 %collective-permute-start.3 = (bf16[97,256]{1,0:T(8,128)(2,1)S(1)}, bf16[97,256]{1,0:T(8,128)(2,1)}, u32[]{:S(2)}, u32[]{:S(2)}) collective-permute-start(bf16[97,256]{1,0:T(8,128)(2,1)S(1)} %constant_dynamic-update-slice_fusion), channel_id=1, source_target_pairs={{0,3},{1,0},{2,1},{3,2},{4,7},{5,4},{6,5},{7,6},{8,11},{9,8},{10,9... | collective-permute-start | bytes 149000 | tf_op jit(solution)/shard_map/ppermute | solution.py:105
  16.0 9.9 %collective-permute-start.2 = (f32[48,1024]{1,0:T(8,128)}, f32[48,1024]{1,0:T(8,128)S(1)}, u32[]{:S(2)}, u32[]{:S(2)}) collective-permute-start(f32[48,1024]{1,0:T(8,128)} %get-tuple-element.27), channel_id=1, source_target_pairs={{0,1},{1,2},{2,3},{3,0},{4,5},{5,6},{6,7},{7,4},{8,9},{9,10},{10,1... | collective-permute-start | bytes 589832 | tf_op jit(solution)/shard_map/ppermute | solution.py:121
  16.6 15.8 %collective-permute-start.1 = (f32[48,1024]{1,0:T(8,128)S(1)}, f32[48,1024]{1,0:T(8,128)S(1)}, u32[]{:S(2)}, u32[]{:S(2)}) collective-permute-start(f32[48,1024]{1,0:T(8,128)S(1)} %get-tuple-element.28), channel_id=1, source_target_pairs={{0,2},{1,3},{2,0},{3,1},{4,6},{5,7},{6,4},{7,5},{8,10},{9,11},{10,... | collective-permute-start | bytes 589832 | tf_op jit(solution)/shard_map/ppermute | solution.py:121
  17.0 31.7 %copy-start.4 = (pred[8]{0:T(512)(128)(4,1)}, pred[8]{0:T(512)(128)(4,1)S(1)}, u32[]{:S(2)}) copy-start(pred[8]{0:T(512)(128)(4,1)S(1)} %get-tuple-element.43) | copy-start | bytes 28
  17.0 31.7 %copy-start.6 = (pred[8]{0:T(512)(128)(4,1)}, pred[8]{0:T(512)(128)(4,1)S(1)}, u32[]{:S(2)}) copy-start(pred[8]{0:T(512)(128)(4,1)S(1)} %get-tuple-element.44) | copy-start | bytes 28
  17.1 31.6 %copy-start.8 = (pred[8]{0:T(512)(128)(4,1)}, pred[8]{0:T(512)(128)(4,1)S(1)}, u32[]{:S(2)}) copy-start(pred[8]{0:T(512)(128)(4,1)S(1)} %get-tuple-element.45) | copy-start | bytes 28
  17.1 31.6 %copy-start.10 = (pred[8]{0:T(512)(128)(4,1)}, pred[8]{0:T(512)(128)(4,1)S(1)}, u32[]{:S(2)}) copy-start(pred[8]{0:T(512)(128)(4,1)S(1)} %get-tuple-element.46) | copy-start | bytes 28
  17.1 31.6 %copy-start.12 = (pred[8]{0:T(512)(128)(4,1)}, pred[8]{0:T(512)(128)(4,1)S(1)}, u32[]{:S(2)}) copy-start(pred[8]{0:T(512)(128)(4,1)S(1)} %get-tuple-element.47) | copy-start | bytes 28
  17.1 31.6 %copy-start.14 = (pred[8]{0:T(512)(128)(4,1)}, pred[8]{0:T(512)(128)(4,1)S(1)}, u32[]{:S(2)}) copy-start(pred[8]{0:T(512)(128)(4,1)S(1)} %get-tuple-element.48) | copy-start | bytes 28
  17.1 31.6 %copy-start.16 = (pred[8]{0:T(512)(128)(4,1)}, pred[8]{0:T(512)(128)(4,1)S(1)}, u32[]{:S(2)}) copy-start(pred[8]{0:T(512)(128)(4,1)S(1)} %broadcast_compare_fusion.6) | copy-start | bytes 28
  17.3 16.7 %collective-permute-start = (f32[48,1024]{1,0:T(8,128)S(1)}, f32[48,1024]{1,0:T(8,128)S(1)}, u32[]{:S(2)}, u32[]{:S(2)}) collective-permute-start(f32[48,1024]{1,0:T(8,128)S(1)} %get-tuple-element.25), channel_id=1, source_target_pairs={{0,3},{1,0},{2,1},{3,2},{4,7},{5,4},{6,5},{7,6},{8,11},{9,8},{10,9... | collective-permute-start | bytes 589832 | tf_op jit(solution)/shard_map/ppermute | solution.py:121
  21.3 13.5 %collective-permute-start.15 = (bf16[4,97,256]{2,0,1:T(4,128)(2,1)S(1)}, bf16[4,97,256]{2,0,1:T(4,128)(2,1)S(1)}, u32[]{:S(2)}, u32[]{:S(2)}) collective-permute-start(bf16[4,97,256]{2,0,1:T(4,128)(2,1)S(1)} %select_select_fusion.4), channel_id=1, source_target_pairs={{0,4},{4,8},{8,12},{12,16},{16,20},{20,24},{24,28},{28,0},{1,5},{5... | collective-permute-start | bytes 595976 | tf_op jit(solution)/shard_map/ppermute | solution.py:105
  21.3 14.9 %collective-permute-start.14 = (bf16[4,97,256]{2,0,1:T(4,128)(2,1)S(1)}, bf16[4,97,256]{2,0,1:T(4,128)(2,1)S(1)}, u32[]{:S(2)}, u32[]{:S(2)}) collective-permute-start(bf16[4,97,256]{2,0,1:T(4,128)(2,1)S(1)} %select_select_fusion.4), channel_id=1, source_target_pairs={{0,8},{4,12},{8,16},{12,20},{16,24},{20,28},{24,0},{28,4},{1,9},{5... | collective-permute-start | bytes 595976 | tf_op jit(solution)/shard_map/ppermute | solution.py:105
  25.9 12.8 %collective-permute-start.13 = (bf16[4,97,256]{2,0,1:T(4,128)(2,1)S(1)}, bf16[4,97,256]{2,0,1:T(4,128)(2,1)S(1)}, u32[]{:S(2)}, u32[]{:S(2)}) collective-permute-start(bf16[4,97,256]{2,0,1:T(4,128)(2,1)S(1)} %select_select_fusion.4), channel_id=1, source_target_pairs={{0,12},{4,16},{8,20},{12,24},{16,28},{20,0},{24,4},{28,8},{1,13},{... | collective-permute-start | bytes 595976 | tf_op jit(solution)/shard_map/ppermute | solution.py:105
  32.4 8.8 %collective-permute-start.12 = (bf16[4,97,256]{2,0,1:T(4,128)(2,1)S(1)}, bf16[4,97,256]{2,0,1:T(4,128)(2,1)S(1)}, u32[]{:S(2)}, u32[]{:S(2)}) collective-permute-start(bf16[4,97,256]{2,0,1:T(4,128)(2,1)S(1)} %select_select_fusion.4), channel_id=1, source_target_pairs={{0,16},{4,20},{8,24},{12,28},{16,0},{20,4},{24,8},{28,12},{1,17},{... | collective-permute-start | bytes 595976 | tf_op jit(solution)/shard_map/ppermute | solution.py:105
  33.9 9.0 %collective-permute-start.11 = (bf16[4,97,256]{2,0,1:T(4,128)(2,1)S(1)}, bf16[4,97,256]{2,0,1:T(4,128)(2,1)S(1)}, u32[]{:S(2)}, u32[]{:S(2)}) collective-permute-start(bf16[4,97,256]{2,0,1:T(4,128)(2,1)S(1)} %select_select_fusion.4), channel_id=1, source_target_pairs={{0,20},{4,24},{8,28},{12,0},{16,4},{20,8},{24,12},{28,16},{1,21},{... | collective-permute-start | bytes 595976 | tf_op jit(solution)/shard_map/ppermute | solution.py:105
  34.8 9.2 %collective-permute-start.10 = (bf16[4,97,256]{2,0,1:T(4,128)(2,1)S(1)}, bf16[4,97,256]{2,0,1:T(4,128)(2,1)S(1)}, u32[]{:S(2)}, u32[]{:S(2)}) collective-permute-start(bf16[4,97,256]{2,0,1:T(4,128)(2,1)S(1)} %select_select_fusion.4), channel_id=1, source_target_pairs={{0,24},{4,28},{8,0},{12,4},{16,8},{20,12},{24,16},{28,20},{1,25},{... | collective-permute-start | bytes 595976 | tf_op jit(solution)/shard_map/ppermute | solution.py:105
  36.2 8.2 %collective-permute-start.9 = (bf16[4,97,256]{2,0,1:T(4,128)(2,1)S(1)}, bf16[4,97,256]{2,0,1:T(4,128)(2,1)S(1)}, u32[]{:S(2)}, u32[]{:S(2)}) collective-permute-start(bf16[4,97,256]{2,0,1:T(4,128)(2,1)S(1)} %select_select_fusion.4), channel_id=1, source_target_pairs={{0,28},{4,0},{8,4},{12,8},{16,12},{20,16},{24,20},{28,24},{1,29},{... | collective-permute-start | bytes 595976 | tf_op jit(solution)/shard_map/ppermute | solution.py:105
  38.8 10.0 %collective-permute-start.8 = (bf16[48,1024]{1,0:T(8,128)(2,1)S(1)}, bf16[48,1024]{1,0:T(8,128)(2,1)S(1)}, u32[]{:S(2)}, u32[]{:S(2)}) collective-permute-start(bf16[48,1024]{1,0:T(8,128)(2,1)S(1)} %divide_convert_fusion), channel_id=1, source_target_pairs={{0,1},{1,2},{2,3},{3,0},{4,5},{5,6},{6,7},{7,4},{8,9},{9,10},{10,1... | collective-permute-start | bytes 294920 | tf_op jit(solution)/shard_map/ppermute | solution.py:105
  41.2 8.0 %collective-permute-start.7 = (bf16[48,1024]{1,0:T(8,128)(2,1)S(1)}, bf16[48,1024]{1,0:T(8,128)(2,1)S(1)}, u32[]{:S(2)}, u32[]{:S(2)}) collective-permute-start(bf16[48,1024]{1,0:T(8,128)(2,1)S(1)} %divide_convert_fusion), channel_id=1, source_target_pairs={{0,2},{1,3},{2,0},{3,1},{4,6},{5,7},{6,4},{7,5},{8,10},{9,11},{10,... | collective-permute-start | bytes 294920 | tf_op jit(solution)/shard_map/ppermute | solution.py:105
  43.0 7.0 %collective-permute-start.6 = (bf16[48,1024]{1,0:T(8,128)(2,1)S(1)}, bf16[48,1024]{1,0:T(8,128)(2,1)S(1)}, u32[]{:S(2)}, u32[]{:S(2)}) collective-permute-start(bf16[48,1024]{1,0:T(8,128)(2,1)S(1)} %divide_convert_fusion), channel_id=1, source_target_pairs={{0,3},{1,0},{2,1},{3,2},{4,7},{5,4},{6,5},{7,6},{8,11},{9,8},{10,9... | collective-permute-start | bytes 294920 | tf_op jit(solution)/shard_map/ppermute | solution.py:105
  56.7 6.1 %copy-start.2 = (f32[384,1024]{1,0:T(8,128)}, f32[384,1024]{1,0:T(8,128)S(1)}, u32[]{:S(2)}) copy-start(f32[384,1024]{1,0:T(8,128)S(1)} %convolution_multiply_fusion) | copy-start | bytes 4718596
  57.5 9.8 %collective-permute-start.18 = (f32[48,1024]{1,0:T(8,128)S(1)}, f32[48,1024]{1,0:T(8,128)}, u32[]{:S(2)}, u32[]{:S(2)}) collective-permute-start(f32[48,1024]{1,0:T(8,128)S(1)} %fusion.18), channel_id=1, source_target_pairs={{0,1},{1,2},{2,3},{3,0},{4,5},{5,6},{6,7},{7,4},{8,9},{9,10},{10,1... | collective-permute-start | bytes 589832 | tf_op jit(solution)/shard_map/ppermute | solution.py:105
  59.8 15.6 %collective-permute-start.17 = (f32[48,1024]{1,0:T(8,128)S(1)}, f32[48,1024]{1,0:T(8,128)}, u32[]{:S(2)}, u32[]{:S(2)}) collective-permute-start(f32[48,1024]{1,0:T(8,128)S(1)} %fusion.18), channel_id=1, source_target_pairs={{0,2},{1,3},{2,0},{3,1},{4,6},{5,7},{6,4},{7,5},{8,10},{9,11},{10,... | collective-permute-start | bytes 589832 | tf_op jit(solution)/shard_map/ppermute | solution.py:105
  60.5 14.8 %collective-permute-start.16 = (f32[48,1024]{1,0:T(8,128)S(1)}, f32[48,1024]{1,0:T(8,128)}, u32[]{:S(2)}, u32[]{:S(2)}) collective-permute-start(f32[48,1024]{1,0:T(8,128)S(1)} %fusion.18), channel_id=1, source_target_pairs={{0,3},{1,0},{2,1},{3,2},{4,7},{5,4},{6,5},{7,6},{8,11},{9,8},{10,9... | collective-permute-start | bytes 589832 | tf_op jit(solution)/shard_map/ppermute | solution.py:105
  65.5 11.8 %copy-start.1 = (bf16[128,4096]{1,0:T(8,128)(2,1)S(1)}, bf16[128,4096]{1,0:T(8,128)(2,1)}, u32[]{:S(2)}) copy-start(bf16[128,4096]{1,0:T(8,128)(2,1)} %param.10) | copy-start | bytes 3145732
  65.5 11.9 %copy-start.20 = (f32[128]{0:T(128)S(1)}, f32[128]{0:T(128)}, u32[]{:S(2)}) copy-start(f32[128]{0:T(128)} %copy-done.19) | copy-start | bytes 1540
  65.5 11.9 %copy-start.21 = (s32[1,128]{1,0:T(1,128)S(1)}, s32[1,128]{1,0:T(1,128)}, u32[]{:S(2)}) copy-start(s32[1,128]{1,0:T(1,128)} %param.11) | copy-start | bytes 1540
  77.4 17.0 %copy-start.18 = (f32[128]{0:T(128)S(1)}, f32[128]{0:T(128)}, u32[]{:S(2)}) copy-start(f32[128]{0:T(128)} %get-tuple-element.36) | copy-start | bytes 1540
  79.1 10.4 %collective-permute-start.25 = (f32[28672]{0:T(1024)S(1)}, f32[28672]{0:T(1024)S(1)}, u32[]{:S(2)}, u32[]{:S(2)}) collective-permute-start(f32[28672]{0:T(1024)S(1)} %get-tuple-element.35), channel_id=1, source_target_pairs={{0,4},{4,8},{8,12},{12,16},{16,20},{20,24},{24,28},{28,0},{1,5},{5... | collective-permute-start | bytes 344072 | tf_op jit(solution)/shard_map/ppermute | solution.py:134
  79.2 13.1 %collective-permute-start.24 = (f32[28672]{0:T(1024)S(1)}, f32[28672]{0:T(1024)S(1)}, u32[]{:S(2)}, u32[]{:S(2)}) collective-permute-start(f32[28672]{0:T(1024)S(1)} %get-tuple-element.34), channel_id=1, source_target_pairs={{0,8},{4,12},{8,16},{12,20},{16,24},{20,28},{24,0},{28,4},{1,9},{5... | collective-permute-start | bytes 344072 | tf_op jit(solution)/shard_map/ppermute | solution.py:134
  86.5 9.6 %collective-permute-start.23 = (f32[28672]{0:T(1024)S(1)}, f32[28672]{0:T(1024)S(1)}, u32[]{:S(2)}, u32[]{:S(2)}) collective-permute-start(f32[28672]{0:T(1024)S(1)} %get-tuple-element.33), channel_id=1, source_target_pairs={{0,12},{4,16},{8,20},{12,24},{16,28},{20,0},{24,4},{28,8},{1,13},{... | collective-permute-start | bytes 344072 | tf_op jit(solution)/shard_map/ppermute | solution.py:134
  88.8 7.3 %collective-permute-start.22 = (f32[28672]{0:T(1024)S(1)}, f32[28672]{0:T(1024)S(1)}, u32[]{:S(2)}, u32[]{:S(2)}) collective-permute-start(f32[28672]{0:T(1024)S(1)} %get-tuple-element.32), channel_id=1, source_target_pairs={{0,16},{4,20},{8,24},{12,28},{16,0},{20,4},{24,8},{28,12},{1,17},{... | collective-permute-start | bytes 344072 | tf_op jit(solution)/shard_map/ppermute | solution.py:134
  89.3 6.8 %collective-permute-start.21 = (f32[28672]{0:T(1024)S(1)}, f32[28672]{0:T(1024)S(1)}, u32[]{:S(2)}, u32[]{:S(2)}) collective-permute-start(f32[28672]{0:T(1024)S(1)} %get-tuple-element.31), channel_id=1, source_target_pairs={{0,20},{4,24},{8,28},{12,0},{16,4},{20,8},{24,12},{28,16},{1,21},{... | collective-permute-start | bytes 344072 | tf_op jit(solution)/shard_map/ppermute | solution.py:134
  89.5 6.7 %collective-permute-start.20 = (f32[28672]{0:T(1024)S(1)}, f32[28672]{0:T(1024)S(1)}, u32[]{:S(2)}, u32[]{:S(2)}) collective-permute-start(f32[28672]{0:T(1024)S(1)} %get-tuple-element.30), channel_id=1, source_target_pairs={{0,24},{4,28},{8,0},{12,4},{16,8},{20,12},{24,16},{28,20},{1,25},{... | collective-permute-start | bytes 344072 | tf_op jit(solution)/shard_map/ppermute | solution.py:134
  92.2 4.6 %collective-permute-start.19 = (f32[28672]{0:T(1024)S(1)}, f32[28672]{0:T(1024)S(1)}, u32[]{:S(2)}, u32[]{:S(2)}) collective-permute-start(f32[28672]{0:T(1024)S(1)} %get-tuple-element.29), channel_id=1, source_target_pairs={{0,28},{4,0},{8,4},{12,8},{16,12},{20,16},{24,20},{28,24},{1,29},{... | collective-permute-start | bytes 344072 | tf_op jit(solution)/shard_map/ppermute | solution.py:134
  94.4 2.4 %copy-start.7 = (pred[8]{0:T(512)(128)(4,1)S(1)}, pred[8]{0:T(512)(128)(4,1)}, u32[]{:S(2)}) copy-start(pred[8]{0:T(512)(128)(4,1)} %copy-done.6) | copy-start | bytes 28
  94.4 2.4 %copy-start.9 = (pred[8]{0:T(512)(128)(4,1)S(1)}, pred[8]{0:T(512)(128)(4,1)}, u32[]{:S(2)}) copy-start(pred[8]{0:T(512)(128)(4,1)} %copy-done.8) | copy-start | bytes 28
  94.4 2.4 %copy-start.11 = (pred[8]{0:T(512)(128)(4,1)S(1)}, pred[8]{0:T(512)(128)(4,1)}, u32[]{:S(2)}) copy-start(pred[8]{0:T(512)(128)(4,1)} %copy-done.10) | copy-start | bytes 28
  94.4 2.4 %copy-start.13 = (pred[8]{0:T(512)(128)(4,1)S(1)}, pred[8]{0:T(512)(128)(4,1)}, u32[]{:S(2)}) copy-start(pred[8]{0:T(512)(128)(4,1)} %copy-done.12) | copy-start | bytes 28
  94.4 2.4 %copy-start.15 = (pred[8]{0:T(512)(128)(4,1)S(1)}, pred[8]{0:T(512)(128)(4,1)}, u32[]{:S(2)}) copy-start(pred[8]{0:T(512)(128)(4,1)} %copy-done.14) | copy-start | bytes 28
  94.4 2.4 %copy-start.17 = (pred[8]{0:T(512)(128)(4,1)S(1)}, pred[8]{0:T(512)(128)(4,1)}, u32[]{:S(2)}) copy-start(pred[8]{0:T(512)(128)(4,1)} %copy-done.16) | copy-start | bytes 28
  97.0 9.9 %collective-permute-start.28 = (f32[4096]{0:T(1024)S(1)}, f32[4096]{0:T(1024)S(1)}, u32[]{:S(2)}, u32[]{:S(2)}) collective-permute-start(f32[4096]{0:T(1024)S(1)} %select_reduce_fusion.2), channel_id=1, source_target_pairs={{0,1},{1,2},{2,3},{3,0},{4,5},{5,6},{6,7},{7,4},{8,9},{9,10},{10,1... | collective-permute-start | bytes 49160 | tf_op jit(solution)/shard_map/ppermute | solution.py:105
  101.7 5.3 %collective-permute-start.27 = (f32[4096]{0:T(1024)S(1)}, f32[4096]{0:T(1024)S(1)}, u32[]{:S(2)}, u32[]{:S(2)}) collective-permute-start(f32[4096]{0:T(1024)S(1)} %select_reduce_fusion.2), channel_id=1, source_target_pairs={{0,2},{1,3},{2,0},{3,1},{4,6},{5,7},{6,4},{7,5},{8,10},{9,11},{10,... | collective-permute-start | bytes 49160 | tf_op jit(solution)/shard_map/ppermute | solution.py:105
  101.7 5.3 %collective-permute-start.26 = (f32[4096]{0:T(1024)S(1)}, f32[4096]{0:T(1024)S(1)}, u32[]{:S(2)}, u32[]{:S(2)}) collective-permute-start(f32[4096]{0:T(1024)S(1)} %select_reduce_fusion.2), channel_id=1, source_target_pairs={{0,3},{1,0},{2,1},{3,2},{4,7},{5,4},{6,5},{7,6},{8,11},{9,8},{10,9... | collective-permute-start | bytes 49160 | tf_op jit(solution)/shard_map/ppermute | solution.py:105
  (3 other events, 4.9 us)

commit v17 on v14

--- a/solution.py
+++ b/solution.py
@@ -204,11 +204,14 @@
     grad_probs = (jnp.exp(scores - log_total[:, None]) - matched.astype(jnp.float32)).astype(
         jnp.bfloat16
     )
-    query_grad_all = logit_scale * jnp.dot(grad_probs, region_all, preferred_element_type=jnp.float32)
-    query_grad = lax.dynamic_slice(query_grad_all, (me_dp * rows, me_f * width), (rows, width))
-    grad_low = lax.dynamic_slice(query_grad_all, (me_dp * rows, 0), (rows, feature_count * width))
-    grad_low = grad_low.astype(jnp.bfloat16)
-    grad_low_cols = lax.dynamic_slice(query_grad_all, (0, me_f * width), (pair_count, width))
+    probs_rows = lax.dynamic_slice(grad_probs, (me_dp * rows, 0), (rows, pair_count))
+    query_grad_rows = logit_scale * jnp.dot(
+        probs_rows, region_all, preferred_element_type=jnp.float32
+    )
+    query_grad = lax.dynamic_slice(query_grad_rows, (0, me_f * width), (rows, width))
+    grad_low = query_grad_rows.astype(jnp.bfloat16)
+    region_cols = lax.dynamic_slice(region_all, (0, me_f * width), (pair_count, width))
+    grad_low_cols = logit_scale * jnp.dot(grad_probs, region_cols, preferred_element_type=jnp.float32)
     grad_low_cols = grad_low_cols.astype(jnp.bfloat16)
     probs_cols = lax.dynamic_slice(grad_probs, (0, me_dp * rows), (pair_count, rows))
     query_cols = lax.dynamic_slice(query_all, (0, me_f * width), (pair_count, width))
@@ -221,13 +224,7 @@
     )
     mean_grad = lax.all_gather(mean_part, "fsdp", axis=1, tiled=True)
     pool_grad = mean_grad / counts[:, None]
-    normed_grad = lax.dot_general(
-        member.astype(jnp.float32),
-        pool_grad,
-        contract_first,
-        precision=lax.Precision.HIGHEST,
-        preferred_element_type=jnp.float32,
-    )
+    normed_grad = jnp.take(pool_grad, segment_ids[0], axis=0)
     gain_part = jnp.sum(normed_grad * states * inv_rms, axis=0)
     scaled = gain * normed_grad
     inner = jnp.mean(scaled * states, axis=1, keepdims=True)

time: 110 us -> 123 us (1.12)
  local copies, waits for them, and re-layouts: 8.89 us -> 21.4 us
  other arithmetic: 15 us -> 20.4 us
  waiting for transfers between devices: 11 us -> 8.35 us
  starting transfers between devices: 41.7 us -> 40.1 us
  matrix products: 10.3 us -> 8.84 us
    slice x14, local copies, waits for them, and re-layouts: 1.24 us -> 6.59 us  [spread_with_sum(): got.append(arrived[size:].reshape(piece.shape))]
    ppermute x3, waiting for transfers between devices: 9.34 us -> 4.84 us  [scatter_sum(): lax.ppermute(piece, axis, [(i, (i + s) % n) for i in range(n)])]
    slice x7, local copies, waits for them, and re-layouts: 0.74 us -> 5.03 us  [spread_with_sum(): sums.append(arrived[:size])]
    gather x0 -> x1, local copies, waits for them, and re-layouts: none -> 2.82 us  [local_small(): normed_grad = jnp.take(pool_grad, segment_ids[0], axis=0)]
    reduce_sum x0 -> x1, other arithmetic: none -> 2.69 us  [local_small(): gain_part = jnp.sum(normed_grad * states * inv_rms, axis=0)]
    ppermute x7, starting transfers between devices: 14.7 us -> 12 us  [spread_with_sum(): arrived = lax.ppermute(payload, axis, [(i, (i + s) % n) for i in range(n)])]
    dot_general x2 -> x1, matrix products: 2.23 us -> 0.39 us  [local_small(): jnp.dot(probs_rows, region_all, preferred_element_type=jnp.float32)]
    ppermute x16, waiting for transfers between devices: 1.68 us -> 3.49 us  [gather_blocks(): lax.ppermute(x, axis, [(i, (i + s) % n) for i in range(n)])]
  transfers between devices with their start and end apart: 26 -> 26, of which waited for: 5 -> 5; matrix products, arithmetic and copies ran while one was open for 18% -> 26% of each run, Pallas kernels for 0% -> 0%
where the time goes in v17:
time: 123 us; the launch traced here: 122 us
  starting transfers between devices  40.1 us (33%)
  local copies, waits for them, and re-layouts  21.4 us (17%)
  other arithmetic  20.4 us (17%)
  blocking collectives  20.1 us (16%)
  matrix products  8.84 us (7%)
  waiting for transfers between devices  8.35 us (7%)
  between operations  3.14 us (3%)
    ppermute x16, starting transfers between devices, gather_blocks(): lax.ppermute(x, axis, [(i, (i + s) % n) for i in range(n)])  24.2 us
    all_gather x1, blocking collectives, local_small(): mean_grad = lax.all_gather(mean_part, 'fsdp', axis=1, tiled=True)  20.1 us
    ppermute x7, starting transfers between devices, spread_with_sum(): arrived = lax.ppermute(payload, axis, [(i, (i + s) % n) for i in range(n)])  12 us
    slice x14, local copies, waits for them, and re-layouts, spread_with_sum(): got.append(arrived[size:].reshape(piece.shape))  6.59 us
    select_n x4, other arithmetic, arrange(): out = jnp.where(source == s, copies[s][None], out)  6.1 us
    slice x7, local copies, waits for them, and re-layouts, spread_with_sum(): sums.append(arrived[:size])  5.03 us
    ppermute x3, waiting for transfers between devices, scatter_sum(): lax.ppermute(piece, axis, [(i, (i + s) % n) for i in range(n)])  4.84 us
    unnamed x59, local copies, waits for them, and re-layouts  3.94 us
  transfers between devices with their start and end apart: 26, of which 5 were waited for; matrix products, arithmetic and copies ran while one was open for 26% of the time, Pallas kernels for 0%

profile of v17, /device:TPU:0, one launch (start us, length us, event | category | flops | bytes accessed | tf_op | source)
XLA Modules:
  0.0 122.3 jit_solution(8139936658325409350)
XLA Ops:
  0.6 0.9 constant_dynamic-update-slice_fusion.2
  2.2 0.7 constant_dynamic-update-slice_fusion.1
  2.9 0.7 fusion.31
  3.7 3.1 %collective-permute-start.5 = (bf16[97,256]{1,0:T(8,128)(2,1)S(1)}, bf16[97,256]{1,0:T(8,128)(2,1)}, u32[]{:S(2)}, u32[]{:S(2)}) collective-permute-start(bf16[97,256]{1,0:T(8,128)(2,1)S(1)} %constant_dynamic-update-slice_fusion), channel_id=1, source_target_pairs={{0,1},{1,2},{2,3},{3,0},{4,5},{5,6},{6,7},{7,4},{8,9},{9,10},{10,1... | collective-permute-start | bytes 149000 | tf_op jit(solution)/shard_map/ppermute | solution.py:105
  6.8 2.6 %collective-permute-start.4 = (bf16[97,256]{1,0:T(8,128)(2,1)S(1)}, bf16[97,256]{1,0:T(8,128)(2,1)}, u32[]{:S(2)}, u32[]{:S(2)}) collective-permute-start(bf16[97,256]{1,0:T(8,128)(2,1)S(1)} %constant_dynamic-update-slice_fusion), channel_id=1, source_target_pairs={{0,2},{1,3},{2,0},{3,1},{4,6},{5,7},{6,4},{7,5},{8,10},{9,11},{10,... | collective-permute-start | bytes 149000 | tf_op jit(solution)/shard_map/ppermute | solution.py:105
  9.4 1.3 %collective-permute-start.3 = (bf16[97,256]{1,0:T(8,128)(2,1)S(1)}, bf16[97,256]{1,0:T(8,128)(2,1)}, u32[]{:S(2)}, u32[]{:S(2)}) collective-permute-start(bf16[97,256]{1,0:T(8,128)(2,1)S(1)} %constant_dynamic-update-slice_fusion), channel_id=1, source_target_pairs={{0,3},{1,0},{2,1},{3,2},{4,7},{5,4},{6,5},{7,6},{8,11},{9,8},{10,9... | collective-permute-start | bytes 149000 | tf_op jit(solution)/shard_map/ppermute | solution.py:105
  11.4 1.5 %fusion = f32[128]{0:T(128)S(1)} fusion(bf16[128,4096]{1,0:T(8,128)(2,1)} %param.10), kind=kLoop, calls=%fused_computation.6 | loop fusion | flops 1572736 | bytes 1049088 | tf_op jit(solution)/shard_map/reduce_sum | solution.py:168
  13.4 1.7 %fusion.11 = f32[48,4096]{1,0:T(8,128)S(1)} fusion(bf16[128,4096]{1,0:T(8,128)(2,1)} %param.10, f32[4096]{0:T(1024)S(1)} %convert_element_type.84, f32[128]{0:T(128)S(1)} %get-tuple-element.37, s32[128]{0:T(128)} %bitcast.68), kind=kOutput, calls=%fused_computation.22 | convolution fusion | flops 52434944 | bytes 1852416 | tf_op jit(solution)/shard_map/dot_general | solution.py:172
  15.2 0.8 constant_dynamic-slice_fusion.12
  17.8 1.2 compare_and_fusion
  19.7 2.9 %collective-permute-start = (f32[48,1024]{1,0:T(8,128)S(1)}, f32[48,1024]{1,0:T(8,128)S(1)}, u32[]{:S(2)}, u32[]{:S(2)}) collective-permute-start(f32[48,1024]{1,0:T(8,128)S(1)} %get-tuple-element.25), channel_id=1, source_target_pairs={{0,3},{1,0},{2,1},{3,2},{4,7},{5,4},{6,5},{7,6},{8,11},{9,8},{10,9... | collective-permute-start | bytes 589832 | tf_op jit(solution)/shard_map/ppermute | solution.py:121
  22.6 1.1 select_select_fusion.3
  23.8 1.5 %collective-permute-start.14 = (bf16[4,97,256]{2,0,1:T(4,128)(2,1)S(1)}, bf16[4,97,256]{2,0,1:T(4,128)(2,1)S(1)}, u32[]{:S(2)}, u32[]{:S(2)}) collective-permute-start(bf16[4,97,256]{2,0,1:T(4,128)(2,1)S(1)} %select_select_fusion.3), channel_id=1, source_target_pairs={{0,8},{4,12},{8,16},{12,20},{16,24},{20,28},{24,0},{28,4},{1,9},{5... | collective-permute-start | bytes 595976 | tf_op jit(solution)/shard_map/ppermute | solution.py:105
  25.9 2.0 %collective-permute-start.13 = (bf16[4,97,256]{2,0,1:T(4,128)(2,1)S(1)}, bf16[4,97,256]{2,0,1:T(4,128)(2,1)S(1)}, u32[]{:S(2)}, u32[]{:S(2)}) collective-permute-start(bf16[4,97,256]{2,0,1:T(4,128)(2,1)S(1)} %select_select_fusion.3), channel_id=1, source_target_pairs={{0,12},{4,16},{8,20},{12,24},{16,28},{20,0},{24,4},{28,8},{1,13},{... | collective-permute-start | bytes 595976 | tf_op jit(solution)/shard_map/ppermute | solution.py:105
  27.9 4.5 %collective-permute-done.1 = f32[48,1024]{1,0:T(8,128)S(1)} collective-permute-done((f32[48,1024]{1,0:T(8,128)S(1)}, f32[48,1024]{1,0:T(8,128)S(1)}, u32[]{:S(2)}, u32[]{:S(2)}) %collective-permute-start.1) | collective-permute-done | bytes 196640 | tf_op jit(solution)/shard_map/ppermute | solution.py:121
  32.4 1.5 %collective-permute-start.12 = (bf16[4,97,256]{2,0,1:T(4,128)(2,1)S(1)}, bf16[4,97,256]{2,0,1:T(4,128)(2,1)S(1)}, u32[]{:S(2)}, u32[]{:S(2)}) collective-permute-start(bf16[4,97,256]{2,0,1:T(4,128)(2,1)S(1)} %select_select_fusion.3), channel_id=1, source_target_pairs={{0,16},{4,20},{8,24},{12,28},{16,0},{20,4},{24,8},{28,12},{1,17},{... | collective-permute-start | bytes 595976 | tf_op jit(solution)/shard_map/ppermute | solution.py:105
  33.9 0.8 select_reduce_fusion
  34.7 1.5 %collective-permute-start.10 = (bf16[4,97,256]{2,0,1:T(4,128)(2,1)S(1)}, bf16[4,97,256]{2,0,1:T(4,128)(2,1)S(1)}, u32[]{:S(2)}, u32[]{:S(2)}) collective-permute-start(bf16[4,97,256]{2,0,1:T(4,128)(2,1)S(1)} %select_select_fusion.3), channel_id=1, source_target_pairs={{0,24},{4,28},{8,0},{12,4},{16,8},{20,12},{24,16},{28,20},{1,25},{... | collective-permute-start | bytes 595976 | tf_op jit(solution)/shard_map/ppermute | solution.py:105
  36.2 2.4 %collective-permute-start.9 = (bf16[4,97,256]{2,0,1:T(4,128)(2,1)S(1)}, bf16[4,97,256]{2,0,1:T(4,128)(2,1)S(1)}, u32[]{:S(2)}, u32[]{:S(2)}) collective-permute-start(bf16[4,97,256]{2,0,1:T(4,128)(2,1)S(1)} %select_select_fusion.3), channel_id=1, source_target_pairs={{0,28},{4,0},{8,4},{12,8},{16,12},{20,16},{24,20},{28,24},{1,29},{... | collective-permute-start | bytes 595976 | tf_op jit(solution)/shard_map/ppermute | solution.py:105
  38.7 1.6 %collective-permute-done.13 = bf16[4,97,256]{2,0,1:T(4,128)(2,1)S(1)} collective-permute-done((bf16[4,97,256]{2,0,1:T(4,128)(2,1)S(1)}, bf16[4,97,256]{2,0,1:T(4,128)(2,1)S(1)}, u32[]{:S(2)}, u32[]{:S(2)}) %collective-permute-start.13) | collective-permute-done | bytes 198688 | tf_op jit(solution)/shard_map/ppermute | solution.py:105
  40.3 0.9 collective-permute-start.8
  41.2 1.8 %collective-permute-start.7 = (bf16[48,1024]{1,0:T(8,128)(2,1)S(1)}, bf16[48,1024]{1,0:T(8,128)(2,1)S(1)}, u32[]{:S(2)}, u32[]{:S(2)}) collective-permute-start(bf16[48,1024]{1,0:T(8,128)(2,1)S(1)} %divide_convert_fusion), channel_id=1, source_target_pairs={{0,2},{1,3},{2,0},{3,1},{4,6},{5,7},{6,4},{7,5},{8,10},{9,11},{10,... | collective-permute-start | bytes 294920 | tf_op jit(solution)/shard_map/ppermute | solution.py:105
  43.7 1.6 %collective-permute-start.6 = (bf16[48,1024]{1,0:T(8,128)(2,1)S(1)}, bf16[48,1024]{1,0:T(8,128)(2,1)S(1)}, u32[]{:S(2)}, u32[]{:S(2)}) collective-permute-start(bf16[48,1024]{1,0:T(8,128)(2,1)S(1)} %divide_convert_fusion), channel_id=1, source_target_pairs={{0,3},{1,0},{2,1},{3,2},{4,7},{5,4},{6,5},{7,6},{8,11},{9,8},{10,9... | collective-permute-start | bytes 294920 | tf_op jit(solution)/shard_map/ppermute | solution.py:105
  45.3 4.3 %select_select_fusion = bf16[8,4,97,256]{3,1,2,0:T(4,128)(2,1)S(1)} fusion(pred[8]{0:T(512)(128)(4,1)S(1)} %get-tuple-element.43, pred[8]{0:T(512)(128)(4,1)S(1)} %get-tuple-element.44, pred[8]{0:T(512)(128)(4,1)S(1)} %get-tuple-element.45, pred[8]{0:T(512)(128)(4,1)S(1)} %get-tuple-element.46, pred[8]{0:T(512)(128)(4,1)S(1)} %get-tuple-element.47, ...), kind=kLoop, calls=%fused_computation.15 | loop fusion | flops 5562368 | bytes 3178552 | tf_op jit(solution)/shard_map/jit(_where)/select_n | solution.py:98
  49.6 1.1 collective-permute-done.7
  52.2 1.1 copy.15
  53.6 1.8 %fusion.37 = (f32[384]{0:T(512)S(1)}, f32[384,384]{0,1:T(8,128)S(1)}) fusion(bf16[384,1024]{1,0:T(8,128)(2,1)} %bitcast.56, bf16[384,1024]{1,0:T(8,128)(2,1)S(1)} %bitcast.49), kind=kOutput, calls=%fused_computation.120 | convolution fusion | flops 302284416 | bytes 2164224 | tf_op jit(solution)/shard_map/dot_general | solution.py:195
  57.5 0.7 fusion.19
  58.3 20.1 %all_gather.3 = f32[48,4096]{1,0:T(8,128)S(1)} all-gather(f32[48,1024]{1,0:T(8,128)S(1)} %fusion.19), channel_id=1, replica_groups=mesh['dp'=8,'fsdp'=4] {'fsdp'}, dimensions={1}, use_global_device_ids=true | all-gather | bytes 983040 | tf_op jit(solution)/shard_map/all_gather | solution.py:225
  78.5 2.8 %gather_fusion = f32[128,4096]{1,0:T(8,128)} fusion(f32[48,4096]{1,0:T(8,128)S(1)} %broadcast_divide_fusion, s32[1024]{0:T(1024)} %pad_clamp_fusion), kind=kCustom, calls=%fused_computation | custom fusion | bytes 4194816 | tf_op jit(solution)/shard_map/jit(_take)/gather | solution.py:227
  81.3 2.7 %fusion.8 = (f32[4096]{0:T(1024)S(1)}, f32[128]{0:T(128)S(1)}) fusion(bf16[128,4096]{1,0:T(8,128)(2,1)} %param.10, f32[128,4096]{1,0:T(8,128)} %gather_fusion, f32[128]{0:T(128)S(1)} %copy-done.23, pred[128]{0:T(512)(128)(4,1)S(1)} %copy-done.24, f32[4096]{0:T(1024)S(1)} %convert_element_type.84), kind=kLoop, calls=%fused_computation.14 | loop fusion | flops 4190080 | bytes 3179648 | tf_op jit(solution)/shard_map/reduce_sum | solution.py:228
  85.1 6.0 %collective-permute-start.21 = (f32[28672]{0:T(1024)S(1)}, f32[28672]{0:T(1024)S(1)}, u32[]{:S(2)}, u32[]{:S(2)}) collective-permute-start(f32[28672]{0:T(1024)S(1)} %get-tuple-element.34), channel_id=1, source_target_pairs={{0,8},{4,12},{8,16},{12,20},{16,24},{20,28},{24,0},{28,4},{1,9},{5... | collective-permute-start | bytes 344072 | tf_op jit(solution)/shard_map/ppermute | solution.py:134
  91.0 2.5 %collective-permute-start.20 = (f32[28672]{0:T(1024)S(1)}, f32[28672]{0:T(1024)}, u32[]{:S(2)}, u32[]{:S(2)}) collective-permute-start(f32[28672]{0:T(1024)S(1)} %get-tuple-element.33), channel_id=1, source_target_pairs={{0,12},{4,16},{8,20},{12,24},{16,28},{20,0},{24,4},{28,8},{1,13},{... | collective-permute-start | bytes 344072 | tf_op jit(solution)/shard_map/ppermute | solution.py:134
  94.4 1.8 %fusion.5 = bf16[128,4096]{1,0:T(8,128)(2,1)} fusion(bf16[128,4096]{1,0:T(8,128)(2,1)S(1)} %copy-done.2, f32[128,4096]{1,0:T(8,128)S(1)} %copy-done.1, f32[128]{0:T(128)S(1)} %broadcast_multiply_fusion, f32[128]{0:T(128)S(1)} %copy-done.25, f32[4096]{0:T(1024)S(1)} %convert_element_type.84, f32[128]{0:T(128)S(1)} %copy-done.23, pred[128]{0:T(512)(128)(4,1)S(1)} %copy-done.24), kind=kLoop, calls=%fused_computation.11 | loop fusion | flops 4194304 | bytes 4212352 | tf_op jit(solution)/shard_map/convert_element_type | solution.py:231
  96.3 1.0 collective-permute-start.17
  97.4 1.6 %collective-permute-start.16 = (f32[28672]{0:T(1024)S(1)}, f32[28672]{0:T(1024)}, u32[]{:S(2)}, u32[]{:S(2)}) collective-permute-start(f32[28672]{0:T(1024)S(1)} %get-tuple-element.29), channel_id=1, source_target_pairs={{0,28},{4,0},{8,4},{12,8},{16,12},{20,16},{24,20},{28,24},{1,29},{... | collective-permute-start | bytes 344072 | tf_op jit(solution)/shard_map/ppermute | solution.py:134
  100.3 1.7 %convolution_multiply_fusion.3 = f32[48,256]{1,0:T(8,128)} fusion(bf16[384,1024]{1,0:T(8,128)(2,1)} %bitcast.57, s32[]{:T(128)S(6)} %select_n.379, bf16[384,384]{0,1:T(8,128)(2,1)S(1)} %copy-done.5, s32[]{:T(128)S(6)} %select_n.378), kind=kOutput, calls=%fused_computation.21 | convolution fusion | flops 9449472 | bytes 282632 | tf_op jit(solution)/shard_map/dot_general | solution.py:218
  107.4 2.3 %collective-permute-start.24 = (f32[4096]{0:T(1024)S(1)}, f32[4096]{0:T(1024)S(1)}, u32[]{:S(2)}, u32[]{:S(2)}) collective-permute-start(f32[4096]{0:T(1024)S(1)} %select_reduce_fusion.2), channel_id=1, source_target_pairs={{0,2},{1,3},{2,0},{3,1},{4,6},{5,7},{6,4},{7,5},{8,10},{9,11},{10,... | collective-permute-start | bytes 49160 | tf_op jit(solution)/shard_map/ppermute | solution.py:105
  109.7 1.5 %collective-permute-start.23 = (f32[4096]{0:T(1024)S(1)}, f32[4096]{0:T(1024)S(1)}, u32[]{:S(2)}, u32[]{:S(2)}) collective-permute-start(f32[4096]{0:T(1024)S(1)} %select_reduce_fusion.2), channel_id=1, source_target_pairs={{0,3},{1,0},{2,1},{3,2},{4,7},{5,4},{6,5},{7,6},{8,11},{9,8},{10,9... | collective-permute-start | bytes 49160 | tf_op jit(solution)/shard_map/ppermute | solution.py:105
  111.2 0.9 slice.166
  112.1 0.9 slice.165
  113.1 0.9 slice.164
  114.0 0.9 slice.163
  115.0 0.9 slice.162
  115.9 0.9 slice.161
  116.8 0.9 slice.160
  118.0 2.4 %fusion.10 = f32[512,256]{1,0:T(8,128)} fusion(bf16[384,512]{1,0:T(8,128)(2,1)S(1)} %bitcast.65, bf16[384,384]{0,1:T(8,128)(2,1)S(1)} %copy-done.5, bf16[384,1024]{1,0:T(8,128)(2,1)} %bitcast.51, s32[]{:T(128)S(6)} %select_n.379), kind=kOutput, calls=%fused_computation.20 | convolution fusion | flops 176357376 | bytes 1409028 | tf_op jit(solution)/shard_map/dot_general | solution.py:235
  120.5 0.7 select_reduce_fusion.3
  (135 shorter events, 18.0 us)
Async XLA Ops:
  0.6 56.9 %copy-start = (bf16[1024,1024]{1,0:T(8,128)(2,1)S(1)}, bf16[1024,1024]{1,0:T(8,128)(2,1)}, u32[]{:S(2)}) copy-start(bf16[1024,1024]{1,0:T(8,128)(2,1)} %param.13) | copy-start | bytes 6291460
  3.7 16.0 %collective-permute-start.5 = (bf16[97,256]{1,0:T(8,128)(2,1)S(1)}, bf16[97,256]{1,0:T(8,128)(2,1)}, u32[]{:S(2)}, u32[]{:S(2)}) collective-permute-start(bf16[97,256]{1,0:T(8,128)(2,1)S(1)} %constant_dynamic-update-slice_fusion), channel_id=1, source_target_pairs={{0,1},{1,2},{2,3},{3,0},{4,5},{5,6},{6,7},{7,4},{8,9},{9,10},{10,1... | collective-permute-start | bytes 149000 | tf_op jit(solution)/shard_map/ppermute | solution.py:105
  6.8 15.8 %collective-permute-start.4 = (bf16[97,256]{1,0:T(8,128)(2,1)S(1)}, bf16[97,256]{1,0:T(8,128)(2,1)}, u32[]{:S(2)}, u32[]{:S(2)}) collective-permute-start(bf16[97,256]{1,0:T(8,128)(2,1)S(1)} %constant_dynamic-update-slice_fusion), channel_id=1, source_target_pairs={{0,2},{1,3},{2,0},{3,1},{4,6},{5,7},{6,4},{7,5},{8,10},{9,11},{10,... | collective-permute-start | bytes 149000 | tf_op jit(solution)/shard_map/ppermute | solution.py:105
  9.4 13.2 %collective-permute-start.3 = (bf16[97,256]{1,0:T(8,128)(2,1)S(1)}, bf16[97,256]{1,0:T(8,128)(2,1)}, u32[]{:S(2)}, u32[]{:S(2)}) collective-permute-start(bf16[97,256]{1,0:T(8,128)(2,1)S(1)} %constant_dynamic-update-slice_fusion), channel_id=1, source_target_pairs={{0,3},{1,0},{2,1},{3,2},{4,7},{5,4},{6,5},{7,6},{8,11},{9,8},{10,9... | collective-permute-start | bytes 149000 | tf_op jit(solution)/shard_map/ppermute | solution.py:105
  16.0 9.9 %collective-permute-start.2 = (f32[48,1024]{1,0:T(8,128)}, f32[48,1024]{1,0:T(8,128)S(1)}, u32[]{:S(2)}, u32[]{:S(2)}) collective-permute-start(f32[48,1024]{1,0:T(8,128)} %get-tuple-element.27), channel_id=1, source_target_pairs={{0,1},{1,2},{2,3},{3,0},{4,5},{5,6},{6,7},{7,4},{8,9},{9,10},{10,1... | collective-permute-start | bytes 589832 | tf_op jit(solution)/shard_map/ppermute | solution.py:121
  16.6 15.7 %collective-permute-start.1 = (f32[48,1024]{1,0:T(8,128)S(1)}, f32[48,1024]{1,0:T(8,128)S(1)}, u32[]{:S(2)}, u32[]{:S(2)}) collective-permute-start(f32[48,1024]{1,0:T(8,128)S(1)} %get-tuple-element.28), channel_id=1, source_target_pairs={{0,2},{1,3},{2,0},{3,1},{4,6},{5,7},{6,4},{7,5},{8,10},{9,11},{10,... | collective-permute-start | bytes 589832 | tf_op jit(solution)/shard_map/ppermute | solution.py:121
  17.0 32.5 %copy-start.8 = (pred[8]{0:T(512)(128)(4,1)}, pred[8]{0:T(512)(128)(4,1)S(1)}, u32[]{:S(2)}) copy-start(pred[8]{0:T(512)(128)(4,1)S(1)} %get-tuple-element.42) | copy-start | bytes 28
  17.0 32.5 %copy-start.10 = (pred[8]{0:T(512)(128)(4,1)}, pred[8]{0:T(512)(128)(4,1)S(1)}, u32[]{:S(2)}) copy-start(pred[8]{0:T(512)(128)(4,1)S(1)} %get-tuple-element.43) | copy-start | bytes 28
  17.1 32.5 %copy-start.12 = (pred[8]{0:T(512)(128)(4,1)}, pred[8]{0:T(512)(128)(4,1)S(1)}, u32[]{:S(2)}) copy-start(pred[8]{0:T(512)(128)(4,1)S(1)} %get-tuple-element.44) | copy-start | bytes 28
  17.1 32.5 %copy-start.14 = (pred[8]{0:T(512)(128)(4,1)}, pred[8]{0:T(512)(128)(4,1)S(1)}, u32[]{:S(2)}) copy-start(pred[8]{0:T(512)(128)(4,1)S(1)} %get-tuple-element.45) | copy-start | bytes 28
  17.1 32.5 %copy-start.16 = (pred[8]{0:T(512)(128)(4,1)}, pred[8]{0:T(512)(128)(4,1)S(1)}, u32[]{:S(2)}) copy-start(pred[8]{0:T(512)(128)(4,1)S(1)} %get-tuple-element.46) | copy-start | bytes 28
  17.1 32.5 %copy-start.18 = (pred[8]{0:T(512)(128)(4,1)}, pred[8]{0:T(512)(128)(4,1)S(1)}, u32[]{:S(2)}) copy-start(pred[8]{0:T(512)(128)(4,1)S(1)} %get-tuple-element.47) | copy-start | bytes 28
  19.6 30.1 %copy-start.20 = (pred[8]{0:T(512)(128)(4,1)}, pred[8]{0:T(512)(128)(4,1)S(1)}, u32[]{:S(2)}) copy-start(pred[8]{0:T(512)(128)(4,1)S(1)} %broadcast_compare_fusion.6) | copy-start | bytes 28
  19.7 14.2 %collective-permute-start = (f32[48,1024]{1,0:T(8,128)S(1)}, f32[48,1024]{1,0:T(8,128)S(1)}, u32[]{:S(2)}, u32[]{:S(2)}) collective-permute-start(f32[48,1024]{1,0:T(8,128)S(1)} %get-tuple-element.25), channel_id=1, source_target_pairs={{0,3},{1,0},{2,1},{3,2},{4,7},{5,4},{6,5},{7,6},{8,11},{9,8},{10,9... | collective-permute-start | bytes 589832 | tf_op jit(solution)/shard_map/ppermute | solution.py:121
  23.7 11.0 %collective-permute-start.15 = (bf16[4,97,256]{2,0,1:T(4,128)(2,1)S(1)}, bf16[4,97,256]{2,0,1:T(4,128)(2,1)S(1)}, u32[]{:S(2)}, u32[]{:S(2)}) collective-permute-start(bf16[4,97,256]{2,0,1:T(4,128)(2,1)S(1)} %select_select_fusion.3), channel_id=1, source_target_pairs={{0,4},{4,8},{8,12},{12,16},{16,20},{20,24},{24,28},{28,0},{1,5},{5... | collective-permute-start | bytes 595976 | tf_op jit(solution)/shard_map/ppermute | solution.py:105
  23.8 12.5 %collective-permute-start.14 = (bf16[4,97,256]{2,0,1:T(4,128)(2,1)S(1)}, bf16[4,97,256]{2,0,1:T(4,128)(2,1)S(1)}, u32[]{:S(2)}, u32[]{:S(2)}) collective-permute-start(bf16[4,97,256]{2,0,1:T(4,128)(2,1)S(1)} %select_select_fusion.3), channel_id=1, source_target_pairs={{0,8},{4,12},{8,16},{12,20},{16,24},{20,28},{24,0},{28,4},{1,9},{5... | collective-permute-start | bytes 595976 | tf_op jit(solution)/shard_map/ppermute | solution.py:105
  25.9 14.4 %collective-permute-start.13 = (bf16[4,97,256]{2,0,1:T(4,128)(2,1)S(1)}, bf16[4,97,256]{2,0,1:T(4,128)(2,1)S(1)}, u32[]{:S(2)}, u32[]{:S(2)}) collective-permute-start(bf16[4,97,256]{2,0,1:T(4,128)(2,1)S(1)} %select_select_fusion.3), channel_id=1, source_target_pairs={{0,12},{4,16},{8,20},{12,24},{16,28},{20,0},{24,4},{28,8},{1,13},{... | collective-permute-start | bytes 595976 | tf_op jit(solution)/shard_map/ppermute | solution.py:105
  32.4 8.8 %collective-permute-start.12 = (bf16[4,97,256]{2,0,1:T(4,128)(2,1)S(1)}, bf16[4,97,256]{2,0,1:T(4,128)(2,1)S(1)}, u32[]{:S(2)}, u32[]{:S(2)}) collective-permute-start(bf16[4,97,256]{2,0,1:T(4,128)(2,1)S(1)} %select_select_fusion.3), channel_id=1, source_target_pairs={{0,16},{4,20},{8,24},{12,28},{16,0},{20,4},{24,8},{28,12},{1,17},{... | collective-permute-start | bytes 595976 | tf_op jit(solution)/shard_map/ppermute | solution.py:105
  33.9 9.8 %collective-permute-start.11 = (bf16[4,97,256]{2,0,1:T(4,128)(2,1)S(1)}, bf16[4,97,256]{2,0,1:T(4,128)(2,1)S(1)}, u32[]{:S(2)}, u32[]{:S(2)}) collective-permute-start(bf16[4,97,256]{2,0,1:T(4,128)(2,1)S(1)} %select_select_fusion.3), channel_id=1, source_target_pairs={{0,20},{4,24},{8,28},{12,0},{16,4},{20,8},{24,12},{28,16},{1,21},{... | collective-permute-start | bytes 595976 | tf_op jit(solution)/shard_map/ppermute | solution.py:105
  34.7 10.6 %collective-permute-start.10 = (bf16[4,97,256]{2,0,1:T(4,128)(2,1)S(1)}, bf16[4,97,256]{2,0,1:T(4,128)(2,1)S(1)}, u32[]{:S(2)}, u32[]{:S(2)}) collective-permute-start(bf16[4,97,256]{2,0,1:T(4,128)(2,1)S(1)} %select_select_fusion.3), channel_id=1, source_target_pairs={{0,24},{4,28},{8,0},{12,4},{16,8},{20,12},{24,16},{28,20},{1,25},{... | collective-permute-start | bytes 595976 | tf_op jit(solution)/shard_map/ppermute | solution.py:105
  36.2 9.1 %collective-permute-start.9 = (bf16[4,97,256]{2,0,1:T(4,128)(2,1)S(1)}, bf16[4,97,256]{2,0,1:T(4,128)(2,1)S(1)}, u32[]{:S(2)}, u32[]{:S(2)}) collective-permute-start(bf16[4,97,256]{2,0,1:T(4,128)(2,1)S(1)} %select_select_fusion.3), channel_id=1, source_target_pairs={{0,28},{4,0},{8,4},{12,8},{16,12},{20,16},{24,20},{28,24},{1,29},{... | collective-permute-start | bytes 595976 | tf_op jit(solution)/shard_map/ppermute | solution.py:105
  40.3 9.3 %collective-permute-start.8 = (bf16[48,1024]{1,0:T(8,128)(2,1)S(1)}, bf16[48,1024]{1,0:T(8,128)(2,1)S(1)}, u32[]{:S(2)}, u32[]{:S(2)}) collective-permute-start(bf16[48,1024]{1,0:T(8,128)(2,1)S(1)} %divide_convert_fusion), channel_id=1, source_target_pairs={{0,1},{1,2},{2,3},{3,0},{4,5},{5,6},{6,7},{7,4},{8,9},{9,10},{10,1... | collective-permute-start | bytes 294920 | tf_op jit(solution)/shard_map/ppermute | solution.py:105
  41.2 9.6 %collective-permute-start.7 = (bf16[48,1024]{1,0:T(8,128)(2,1)S(1)}, bf16[48,1024]{1,0:T(8,128)(2,1)S(1)}, u32[]{:S(2)}, u32[]{:S(2)}) collective-permute-start(bf16[48,1024]{1,0:T(8,128)(2,1)S(1)} %divide_convert_fusion), channel_id=1, source_target_pairs={{0,2},{1,3},{2,0},{3,1},{4,6},{5,7},{6,4},{7,5},{8,10},{9,11},{10,... | collective-permute-start | bytes 294920 | tf_op jit(solution)/shard_map/ppermute | solution.py:105
  43.7 7.1 %collective-permute-start.6 = (bf16[48,1024]{1,0:T(8,128)(2,1)S(1)}, bf16[48,1024]{1,0:T(8,128)(2,1)S(1)}, u32[]{:S(2)}, u32[]{:S(2)}) collective-permute-start(bf16[48,1024]{1,0:T(8,128)(2,1)S(1)} %divide_convert_fusion), channel_id=1, source_target_pairs={{0,3},{1,0},{2,1},{3,2},{4,7},{5,4},{6,5},{7,6},{8,11},{9,8},{10,9... | collective-permute-start | bytes 294920 | tf_op jit(solution)/shard_map/ppermute | solution.py:105
  53.4 4.1 %copy-start.3 = (bf16[48,8,4,256]{3,1,2,0:T(8,128)(2,1)}, bf16[48,8,4,256]{3,1,2,0:T(8,128)(2,1)S(1)}, u32[]{:S(2)}) copy-start(bf16[48,8,4,256]{3,1,2,0:T(8,128)(2,1)S(1)} %copy.16) | copy-start | bytes 2359300
  78.5 2.9 %copy-start.23 = (f32[128]{0:T(128)S(1)}, f32[128]{0:T(128)}, u32[]{:S(2)}) copy-start(f32[128]{0:T(128)} %copy-done.22) | copy-start | bytes 1540
  84.0 10.3 %copy-start.1 = (f32[128,4096]{1,0:T(8,128)S(1)}, f32[128,4096]{1,0:T(8,128)}, u32[]{:S(2)}) copy-start(f32[128,4096]{1,0:T(8,128)} %gather_fusion) | copy-start | bytes 6291460
  84.0 10.3 %copy-start.2 = (bf16[128,4096]{1,0:T(8,128)(2,1)S(1)}, bf16[128,4096]{1,0:T(8,128)(2,1)}, u32[]{:S(2)}) copy-start(bf16[128,4096]{1,0:T(8,128)(2,1)} %param.10) | copy-start | bytes 3145732
  84.0 10.3 %copy-start.25 = (f32[128]{0:T(128)S(1)}, f32[128]{0:T(128)}, u32[]{:S(2)}) copy-start(f32[128]{0:T(128)} %get-tuple-element.36) | copy-start | bytes 1540
  85.0 11.3 %collective-permute-start.22 = (f32[28672]{0:T(1024)S(1)}, f32[28672]{0:T(1024)S(1)}, u32[]{:S(2)}, u32[]{:S(2)}) collective-permute-start(f32[28672]{0:T(1024)S(1)} %get-tuple-element.35), channel_id=1, source_target_pairs={{0,4},{4,8},{8,12},{12,16},{16,20},{20,24},{24,28},{28,0},{1,5},{5... | collective-permute-start | bytes 344072 | tf_op jit(solution)/shard_map/ppermute | solution.py:134
  85.1 12.3 %collective-permute-start.21 = (f32[28672]{0:T(1024)S(1)}, f32[28672]{0:T(1024)S(1)}, u32[]{:S(2)}, u32[]{:S(2)}) collective-permute-start(f32[28672]{0:T(1024)S(1)} %get-tuple-element.34), channel_id=1, source_target_pairs={{0,8},{4,12},{8,16},{12,20},{16,24},{20,28},{24,0},{28,4},{1,9},{5... | collective-permute-start | bytes 344072 | tf_op jit(solution)/shard_map/ppermute | solution.py:134
  91.0 12.4 %collective-permute-start.20 = (f32[28672]{0:T(1024)S(1)}, f32[28672]{0:T(1024)}, u32[]{:S(2)}, u32[]{:S(2)}) collective-permute-start(f32[28672]{0:T(1024)S(1)} %get-tuple-element.33), channel_id=1, source_target_pairs={{0,12},{4,16},{8,20},{12,24},{16,28},{20,0},{24,4},{28,8},{1,13},{... | collective-permute-start | bytes 344072 | tf_op jit(solution)/shard_map/ppermute | solution.py:134
  93.5 10.7 %collective-permute-start.19 = (f32[28672]{0:T(1024)S(1)}, f32[28672]{0:T(1024)}, u32[]{:S(2)}, u32[]{:S(2)}) collective-permute-start(f32[28672]{0:T(1024)S(1)} %get-tuple-element.32), channel_id=1, source_target_pairs={{0,16},{4,20},{8,24},{12,28},{16,0},{20,4},{24,8},{28,12},{1,17},{... | collective-permute-start | bytes 344072 | tf_op jit(solution)/shard_map/ppermute | solution.py:134
  93.7 11.2 %collective-permute-start.18 = (f32[28672]{0:T(1024)S(1)}, f32[28672]{0:T(1024)}, u32[]{:S(2)}, u32[]{:S(2)}) collective-permute-start(f32[28672]{0:T(1024)S(1)} %get-tuple-element.31), channel_id=1, source_target_pairs={{0,20},{4,24},{8,28},{12,0},{16,4},{20,8},{24,12},{28,16},{1,21},{... | collective-permute-start | bytes 344072 | tf_op jit(solution)/shard_map/ppermute | solution.py:134
  94.4 6.0 %copy-start.5 = (bf16[384,384]{0,1:T(8,128)(2,1)S(1)}, bf16[384,384]{0,1:T(8,128)(2,1)}, u32[]{:S(2)}) copy-start(bf16[384,384]{0,1:T(8,128)(2,1)} %copy-done.4) | copy-start | bytes 884740
  94.4 12.7 %copy-start.9 = (pred[8]{0:T(512)(128)(4,1)S(1)}, pred[8]{0:T(512)(128)(4,1)}, u32[]{:S(2)}) copy-start(pred[8]{0:T(512)(128)(4,1)} %copy-done.8) | copy-start | bytes 28
  94.4 12.7 %copy-start.11 = (pred[8]{0:T(512)(128)(4,1)S(1)}, pred[8]{0:T(512)(128)(4,1)}, u32[]{:S(2)}) copy-start(pred[8]{0:T(512)(128)(4,1)} %copy-done.10) | copy-start | bytes 28
  94.4 12.7 %copy-start.13 = (pred[8]{0:T(512)(128)(4,1)S(1)}, pred[8]{0:T(512)(128)(4,1)}, u32[]{:S(2)}) copy-start(pred[8]{0:T(512)(128)(4,1)} %copy-done.12) | copy-start | bytes 28
  94.4 12.7 %copy-start.15 = (pred[8]{0:T(512)(128)(4,1)S(1)}, pred[8]{0:T(512)(128)(4,1)}, u32[]{:S(2)}) copy-start(pred[8]{0:T(512)(128)(4,1)} %copy-done.14) | copy-start | bytes 28
  94.4 12.7 %copy-start.17 = (pred[8]{0:T(512)(128)(4,1)S(1)}, pred[8]{0:T(512)(128)(4,1)}, u32[]{:S(2)}) copy-start(pred[8]{0:T(512)(128)(4,1)} %copy-done.16) | copy-start | bytes 28
  94.4 12.7 %copy-start.19 = (pred[8]{0:T(512)(128)(4,1)S(1)}, pred[8]{0:T(512)(128)(4,1)}, u32[]{:S(2)}) copy-start(pred[8]{0:T(512)(128)(4,1)} %copy-done.18) | copy-start | bytes 28
  94.4 12.7 %copy-start.21 = (pred[8]{0:T(512)(128)(4,1)S(1)}, pred[8]{0:T(512)(128)(4,1)}, u32[]{:S(2)}) copy-start(pred[8]{0:T(512)(128)(4,1)} %copy-done.20) | copy-start | bytes 28
  96.3 3.3 %copy-start.6 = (f32[28672]{0:T(1024)}, f32[28672]{0:T(1024)S(1)}, u32[]{:S(2)}) copy-start(f32[28672]{0:T(1024)S(1)} %collective-permute-done.22) | copy-start | bytes 344068
  96.3 9.3 %collective-permute-start.17 = (f32[28672]{0:T(1024)S(1)}, f32[28672]{0:T(1024)}, u32[]{:S(2)}, u32[]{:S(2)}) collective-permute-start(f32[28672]{0:T(1024)S(1)} %get-tuple-element.30), channel_id=1, source_target_pairs={{0,24},{4,28},{8,0},{12,4},{16,8},{20,12},{24,16},{28,20},{1,25},{... | collective-permute-start | bytes 344072 | tf_op jit(solution)/shard_map/ppermute | solution.py:134
  97.4 9.0 %collective-permute-start.16 = (f32[28672]{0:T(1024)S(1)}, f32[28672]{0:T(1024)}, u32[]{:S(2)}, u32[]{:S(2)}) collective-permute-start(f32[28672]{0:T(1024)S(1)} %get-tuple-element.29), channel_id=1, source_target_pairs={{0,28},{4,0},{8,4},{12,8},{16,12},{20,16},{24,20},{28,24},{1,29},{... | collective-permute-start | bytes 344072 | tf_op jit(solution)/shard_map/ppermute | solution.py:134
  107.3 13.2 %collective-permute-start.25 = (f32[4096]{0:T(1024)S(1)}, f32[4096]{0:T(1024)S(1)}, u32[]{:S(2)}, u32[]{:S(2)}) collective-permute-start(f32[4096]{0:T(1024)S(1)} %select_reduce_fusion.2), channel_id=1, source_target_pairs={{0,1},{1,2},{2,3},{3,0},{4,5},{5,6},{6,7},{7,4},{8,9},{9,10},{10,1... | collective-permute-start | bytes 49160 | tf_op jit(solution)/shard_map/ppermute | solution.py:105
  107.4 13.1 %collective-permute-start.24 = (f32[4096]{0:T(1024)S(1)}, f32[4096]{0:T(1024)S(1)}, u32[]{:S(2)}, u32[]{:S(2)}) collective-permute-start(f32[4096]{0:T(1024)S(1)} %select_reduce_fusion.2), channel_id=1, source_target_pairs={{0,2},{1,3},{2,0},{3,1},{4,6},{5,7},{6,4},{7,5},{8,10},{9,11},{10,... | collective-permute-start | bytes 49160 | tf_op jit(solution)/shard_map/ppermute | solution.py:105
  109.7 10.8 %collective-permute-start.23 = (f32[4096]{0:T(1024)S(1)}, f32[4096]{0:T(1024)S(1)}, u32[]{:S(2)}, u32[]{:S(2)}) collective-permute-start(f32[4096]{0:T(1024)S(1)} %select_reduce_fusion.2), channel_id=1, source_target_pairs={{0,3},{1,0},{2,1},{3,2},{4,7},{5,4},{6,5},{7,6},{8,11},{9,8},{10,9... | collective-permute-start | bytes 49160 | tf_op jit(solution)/shard_map/ppermute | solution.py:105
  (4 other events, 7.6 us)

commit v18 on v17

--- a/solution.py
+++ b/solution.py
@@ -224,7 +224,13 @@
     )
     mean_grad = lax.all_gather(mean_part, "fsdp", axis=1, tiled=True)
     pool_grad = mean_grad / counts[:, None]
-    normed_grad = jnp.take(pool_grad, segment_ids[0], axis=0)
+    normed_grad = lax.dot_general(
+        member.astype(jnp.float32),
+        pool_grad,
+        contract_first,
+        precision=lax.Precision.HIGHEST,
+        preferred_element_type=jnp.float32,
+    )
     gain_part = jnp.sum(normed_grad * states * inv_rms, axis=0)
     scaled = gain * normed_grad
     inner = jnp.mean(scaled * states, axis=1, keepdims=True)

time: 123 us -> 125 us (1.016)
  waiting for transfers between devices: 8.35 us -> 11 us
  other arithmetic: 20.4 us -> 18.7 us
  starting transfers between devices: 40.1 us -> 41.7 us
  local copies, waits for them, and re-layouts: 21.4 us -> 19.8 us
  matrix products: 8.84 us -> 10.4 us
  blocking collectives: 20.1 us -> 18.7 us
    ppermute x3, waiting for transfers between devices: 4.84 us -> 9.31 us  [scatter_sum(): lax.ppermute(piece, axis, [(i, (i + s) % n) for i in range(n)])]
    gather x1 -> x0, local copies, waits for them, and re-layouts: 2.82 us -> none  [local_small(): normed_grad = jnp.take(pool_grad, segment_ids[0], axis=0)]
    reduce_sum x1 -> x0, other arithmetic: 2.69 us -> none  [local_small(): gain_part = jnp.sum(normed_grad * states * inv_rms, axis=0)]
    ppermute x7, starting transfers between devices: 12 us -> 14.7 us  [spread_with_sum(): arrived = lax.ppermute(payload, axis, [(i, (i + s) % n) for i in range(n)])]
    ppermute x16, waiting for transfers between devices: 3.49 us -> 1.68 us  [gather_blocks(): lax.ppermute(x, axis, [(i, (i + s) % n) for i in range(n)])]
    select_n x4, other arithmetic: 6.1 us -> 7.74 us  [arrange(): out = jnp.where(source == s, copies[s][None], out)]
    dot_general x0 -> x1, matrix products: none -> 1.63 us  [local_small(): lax.dot_general(member.astype(jnp.float32), pool_grad, contract_first, pr...]
    all_gather x1, blocking collectives: 20.1 us -> 18.7 us  [local_small(): mean_grad = lax.all_gather(mean_part, 'fsdp', axis=1, tiled=True)]
where the time goes in v18:
time: 125 us; the launch traced here: 123 us
  starting transfers between devices  41.7 us (33%)
  local copies, waits for them, and re-layouts  19.8 us (16%)
  other arithmetic  18.7 us (15%)
  blocking collectives  18.7 us (15%)
  waiting for transfers between devices  11 us (9%)
  matrix products  10.4 us (8%)
  between operations  3.02 us (2%)
    ppermute x16, starting transfers between devices, gather_blocks(): lax.ppermute(x, axis, [(i, (i + s) % n) for i in range(n)])  23.1 us
    all_gather x1, blocking collectives, local_small(): mean_grad = lax.all_gather(mean_part, 'fsdp', axis=1, tiled=True)  18.7 us
    ppermute x7, starting transfers between devices, spread_with_sum(): arrived = lax.ppermute(payload, axis, [(i, (i + s) % n) for i in range(n)])  14.7 us
    ppermute x3, waiting for transfers between devices, scatter_sum(): lax.ppermute(piece, axis, [(i, (i + s) % n) for i in range(n)])  9.31 us
    select_n x4, other arithmetic, arrange(): out = jnp.where(source == s, copies[s][None], out)  7.74 us
    slice x14, local copies, waits for them, and re-layouts, spread_with_sum(): got.append(arrived[size:].reshape(piece.shape))  7.2 us
    slice x7, local copies, waits for them, and re-layouts, spread_with_sum(): sums.append(arrived[:size])  5.03 us
    unnamed x53, local copies, waits for them, and re-layouts  4.52 us
  transfers between devices with their start and end apart: 26, of which 5 were waited for; matrix products, arithmetic and copies ran while one was open for 26% of the time, Pallas kernels for 0%

profile of v18, /device:TPU:0, one launch (start us, length us, event | category | flops | bytes accessed | tf_op | source)
XLA Modules:
  0.0 123.3 jit_solution(12567939038557089840)
XLA Ops:
  0.6 0.9 constant_dynamic-update-slice_fusion.2
  2.2 0.7 constant_dynamic-update-slice_fusion.1
  2.9 0.7 fusion.35
  3.7 3.1 %collective-permute-start.5 = (bf16[97,256]{1,0:T(8,128)(2,1)S(1)}, bf16[97,256]{1,0:T(8,128)(2,1)}, u32[]{:S(2)}, u32[]{:S(2)}) collective-permute-start(bf16[97,256]{1,0:T(8,128)(2,1)S(1)} %constant_dynamic-update-slice_fusion), channel_id=1, source_target_pairs={{0,1},{1,2},{2,3},{3,0},{4,5},{5,6},{6,7},{7,4},{8,9},{9,10},{10,1... | collective-permute-start | bytes 149000 | tf_op jit(solution)/shard_map/ppermute | solution.py:105
  6.8 2.6 %collective-permute-start.4 = (bf16[97,256]{1,0:T(8,128)(2,1)S(1)}, bf16[97,256]{1,0:T(8,128)(2,1)}, u32[]{:S(2)}, u32[]{:S(2)}) collective-permute-start(bf16[97,256]{1,0:T(8,128)(2,1)S(1)} %constant_dynamic-update-slice_fusion), channel_id=1, source_target_pairs={{0,2},{1,3},{2,0},{3,1},{4,6},{5,7},{6,4},{7,5},{8,10},{9,11},{10,... | collective-permute-start | bytes 149000 | tf_op jit(solution)/shard_map/ppermute | solution.py:105
  9.4 1.3 %collective-permute-start.3 = (bf16[97,256]{1,0:T(8,128)(2,1)S(1)}, bf16[97,256]{1,0:T(8,128)(2,1)}, u32[]{:S(2)}, u32[]{:S(2)}) collective-permute-start(bf16[97,256]{1,0:T(8,128)(2,1)S(1)} %constant_dynamic-update-slice_fusion), channel_id=1, source_target_pairs={{0,3},{1,0},{2,1},{3,2},{4,7},{5,4},{6,5},{7,6},{8,11},{9,8},{10,9... | collective-permute-start | bytes 149000 | tf_op jit(solution)/shard_map/ppermute | solution.py:105
  11.4 1.5 %fusion = f32[128]{0:T(128)S(1)} fusion(bf16[128,4096]{1,0:T(8,128)(2,1)} %param.10), kind=kLoop, calls=%fused_computation.5 | loop fusion | flops 1572736 | bytes 1049088 | tf_op jit(solution)/shard_map/reduce_sum | solution.py:168
  13.4 1.7 %fusion.11 = f32[48,4096]{1,0:T(8,128)S(1)} fusion(bf16[128,4096]{1,0:T(8,128)(2,1)} %param.10, f32[4096]{0:T(1024)S(1)} %convert_element_type.85, f32[128]{0:T(128)S(1)} %get-tuple-element.37, s32[128]{0:T(128)} %bitcast.63), kind=kOutput, calls=%fused_computation.21 | convolution fusion | flops 52434944 | bytes 1852416 | tf_op jit(solution)/shard_map/dot_general | solution.py:172
  15.2 0.8 constant_dynamic-slice_fusion.12
  17.3 2.9 %collective-permute-start = (f32[48,1024]{1,0:T(8,128)S(1)}, f32[48,1024]{1,0:T(8,128)S(1)}, u32[]{:S(2)}, u32[]{:S(2)}) collective-permute-start(f32[48,1024]{1,0:T(8,128)S(1)} %get-tuple-element.25), channel_id=1, source_target_pairs={{0,3},{1,0},{2,1},{3,2},{4,7},{5,4},{6,5},{7,6},{8,11},{9,8},{10,9... | collective-permute-start | bytes 589832 | tf_op jit(solution)/shard_map/ppermute | solution.py:121
  20.2 1.1 select_select_fusion.3
  21.4 1.5 %collective-permute-start.14 = (bf16[4,97,256]{2,0,1:T(4,128)(2,1)S(1)}, bf16[4,97,256]{2,0,1:T(4,128)(2,1)S(1)}, u32[]{:S(2)}, u32[]{:S(2)}) collective-permute-start(bf16[4,97,256]{2,0,1:T(4,128)(2,1)S(1)} %select_select_fusion.3), channel_id=1, source_target_pairs={{0,8},{4,12},{8,16},{12,20},{16,24},{20,28},{24,0},{28,4},{1,9},{5... | collective-permute-start | bytes 595976 | tf_op jit(solution)/shard_map/ppermute | solution.py:105
  23.1 2.8 %collective-permute-done.2 = f32[48,1024]{1,0:T(8,128)S(1)} collective-permute-done((f32[48,1024]{1,0:T(8,128)}, f32[48,1024]{1,0:T(8,128)S(1)}, u32[]{:S(2)}, u32[]{:S(2)}) %collective-permute-start.2) | collective-permute-done | bytes 196640 | tf_op jit(solution)/shard_map/ppermute | solution.py:121
  25.9 6.5 %collective-permute-done.1 = f32[48,1024]{1,0:T(8,128)S(1)} collective-permute-done((f32[48,1024]{1,0:T(8,128)S(1)}, f32[48,1024]{1,0:T(8,128)S(1)}, u32[]{:S(2)}, u32[]{:S(2)}) %collective-permute-start.1) | collective-permute-done | bytes 196640 | tf_op jit(solution)/shard_map/ppermute | solution.py:121
  32.4 1.5 %collective-permute-start.12 = (bf16[4,97,256]{2,0,1:T(4,128)(2,1)S(1)}, bf16[4,97,256]{2,0,1:T(4,128)(2,1)S(1)}, u32[]{:S(2)}, u32[]{:S(2)}) collective-permute-start(bf16[4,97,256]{2,0,1:T(4,128)(2,1)S(1)} %select_select_fusion.3), channel_id=1, source_target_pairs={{0,16},{4,20},{8,24},{12,28},{16,0},{20,4},{24,8},{28,12},{1,17},{... | collective-permute-start | bytes 595976 | tf_op jit(solution)/shard_map/ppermute | solution.py:105
  33.9 0.8 select_reduce_fusion
  34.8 1.5 %collective-permute-start.10 = (bf16[4,97,256]{2,0,1:T(4,128)(2,1)S(1)}, bf16[4,97,256]{2,0,1:T(4,128)(2,1)S(1)}, u32[]{:S(2)}, u32[]{:S(2)}) collective-permute-start(bf16[4,97,256]{2,0,1:T(4,128)(2,1)S(1)} %select_select_fusion.3), channel_id=1, source_target_pairs={{0,24},{4,28},{8,0},{12,4},{16,8},{20,12},{24,16},{28,20},{1,25},{... | collective-permute-start | bytes 595976 | tf_op jit(solution)/shard_map/ppermute | solution.py:105
  36.2 2.4 %collective-permute-start.9 = (bf16[4,97,256]{2,0,1:T(4,128)(2,1)S(1)}, bf16[4,97,256]{2,0,1:T(4,128)(2,1)S(1)}, u32[]{:S(2)}, u32[]{:S(2)}) collective-permute-start(bf16[4,97,256]{2,0,1:T(4,128)(2,1)S(1)} %select_select_fusion.3), channel_id=1, source_target_pairs={{0,28},{4,0},{8,4},{12,8},{16,12},{20,16},{24,20},{28,24},{1,29},{... | collective-permute-start | bytes 595976 | tf_op jit(solution)/shard_map/ppermute | solution.py:105
  38.8 2.4 %collective-permute-start.8 = (bf16[48,1024]{1,0:T(8,128)(2,1)S(1)}, bf16[48,1024]{1,0:T(8,128)(2,1)S(1)}, u32[]{:S(2)}, u32[]{:S(2)}) collective-permute-start(bf16[48,1024]{1,0:T(8,128)(2,1)S(1)} %divide_convert_fusion), channel_id=1, source_target_pairs={{0,1},{1,2},{2,3},{3,0},{4,5},{5,6},{6,7},{7,4},{8,9},{9,10},{10,1... | collective-permute-start | bytes 294920 | tf_op jit(solution)/shard_map/ppermute | solution.py:105
  41.2 1.8 %collective-permute-start.7 = (bf16[48,1024]{1,0:T(8,128)(2,1)S(1)}, bf16[48,1024]{1,0:T(8,128)(2,1)S(1)}, u32[]{:S(2)}, u32[]{:S(2)}) collective-permute-start(bf16[48,1024]{1,0:T(8,128)(2,1)S(1)} %divide_convert_fusion), channel_id=1, source_target_pairs={{0,2},{1,3},{2,0},{3,1},{4,6},{5,7},{6,4},{7,5},{8,10},{9,11},{10,... | collective-permute-start | bytes 294920 | tf_op jit(solution)/shard_map/ppermute | solution.py:105
  43.0 1.0 collective-permute-start.6
  44.4 4.2 %select_select_fusion = bf16[8,4,97,256]{3,1,2,0:T(4,128)(2,1)S(1)} fusion(pred[8]{0:T(512)(128)(4,1)S(1)} %get-tuple-element.44, pred[8]{0:T(512)(128)(4,1)S(1)} %get-tuple-element.45, pred[8]{0:T(512)(128)(4,1)S(1)} %get-tuple-element.46, pred[8]{0:T(512)(128)(4,1)S(1)} %get-tuple-element.47, pred[8]{0:T(512)(128)(4,1)S(1)} %get-tuple-element.48, ...), kind=kLoop, calls=%fused_computation.14 | loop fusion | flops 5562368 | bytes 3178552 | tf_op jit(solution)/shard_map/jit(_where)/select_n | solution.py:98
  49.2 0.7 collective-permute-done.6
  51.3 1.1 copy.15
  52.7 1.7 %fusion.40 = (f32[384]{0:T(512)S(1)}, f32[384,384]{0,1:T(8,128)S(1)}) fusion(bf16[384,1024]{1,0:T(8,128)(2,1)} %bitcast.51, bf16[384,1024]{1,0:T(8,128)(2,1)S(1)} %bitcast.44), kind=kOutput, calls=%fused_computation.117 | convolution fusion | flops 302284416 | bytes 2164224 | tf_op jit(solution)/shard_map/dot_general | solution.py:195
  56.5 0.7 fusion.22
  57.3 18.7 %all_gather.3 = f32[48,4096]{1,0:T(8,128)S(1)} all-gather(f32[48,1024]{1,0:T(8,128)S(1)} %fusion.22), channel_id=1, replica_groups=mesh['dp'=8,'fsdp'=4] {'fsdp'}, dimensions={1}, use_global_device_ids=true | all-gather | bytes 983040 | tf_op jit(solution)/shard_map/all_gather | solution.py:225
  76.0 1.6 %fusion.8 = (f32[4096]{0:T(1024)S(1)}, f32[128]{0:T(128)S(1)}, f32[128,4096]{1,0:T(8,128)S(1)}) fusion(bf16[128,4096]{1,0:T(8,128)(2,1)S(1)} %copy-done.1, f32[128]{0:T(128)S(1)} %copy-done.21, f32[4096]{0:T(1024)S(1)} %convert_element_type.85, f32[48,4096]{1,0:T(8,128)S(1)} %all_gather.3, f32[48]{0:T(128)S(1)} %convert_reduce_fusion, s32[128]{0:T(128)S(1)} %bitcast.64), kind=kOutput, calls=%fused_computation.13 | convolution fusion | flops 305858432 | bytes 3966656 | tf_op jit(solution)/shard_map/dot_general | solution.py:227
  78.5 0.8 pad_maximum_fusion.6
  79.2 8.0 %collective-permute-start.21 = (f32[28672]{0:T(1024)S(1)}, f32[28672]{0:T(1024)S(1)}, u32[]{:S(2)}, u32[]{:S(2)}) collective-permute-start(f32[28672]{0:T(1024)S(1)} %get-tuple-element.34), channel_id=1, source_target_pairs={{0,8},{4,12},{8,16},{12,20},{16,24},{20,28},{24,0},{28,4},{1,9},{5... | collective-permute-start | bytes 344072 | tf_op jit(solution)/shard_map/ppermute | solution.py:134
  87.3 2.7 %collective-permute-start.20 = (f32[28672]{0:T(1024)}, f32[28672]{0:T(1024)}, u32[]{:S(2)}, u32[]{:S(2)}) collective-permute-start(f32[28672]{0:T(1024)} %get-tuple-element.33), channel_id=1, source_target_pairs={{0,12},{4,16},{8,20},{12,24},{16,28},{20,0},{24,4},{28,8},{1,13},{... | collective-permute-start | bytes 344072 | tf_op jit(solution)/shard_map/ppermute | solution.py:134
  90.6 1.6 %fusion.5 = bf16[128,4096]{1,0:T(8,128)(2,1)} fusion(bf16[128,4096]{1,0:T(8,128)(2,1)S(1)} %copy-done.1, f32[128,4096]{1,0:T(8,128)S(1)} %get-tuple-element.42, f32[128]{0:T(128)S(1)} %broadcast_multiply_fusion, f32[128]{0:T(128)S(1)} %copy-done.19, f32[4096]{0:T(1024)S(1)} %convert_element_type.85, f32[128]{0:T(128)S(1)} %copy-done.21), kind=kLoop, calls=%fused_computation.10 | loop fusion | flops 3670016 | bytes 4212224 | tf_op jit(solution)/shard_map/convert_element_type | solution.py:237
  92.3 1.2 %collective-permute-start.17 = (f32[28672]{0:T(1024)S(1)}, f32[28672]{0:T(1024)}, u32[]{:S(2)}, u32[]{:S(2)}) collective-permute-start(f32[28672]{0:T(1024)S(1)} %get-tuple-element.30), channel_id=1, source_target_pairs={{0,24},{4,28},{8,0},{12,4},{16,8},{20,12},{24,16},{28,20},{1,25},{... | collective-permute-start | bytes 344072 | tf_op jit(solution)/shard_map/ppermute | solution.py:134
  93.6 2.1 %collective-permute-start.16 = (f32[28672]{0:T(1024)S(1)}, f32[28672]{0:T(1024)}, u32[]{:S(2)}, u32[]{:S(2)}) collective-permute-start(f32[28672]{0:T(1024)S(1)} %get-tuple-element.29), channel_id=1, source_target_pairs={{0,28},{4,0},{8,4},{12,8},{16,12},{20,16},{24,20},{28,24},{1,29},{... | collective-permute-start | bytes 344072 | tf_op jit(solution)/shard_map/ppermute | solution.py:134
  97.6 1.7 %convolution_multiply_fusion.3 = f32[48,256]{1,0:T(8,128)} fusion(bf16[384,1024]{1,0:T(8,128)(2,1)} %bitcast.52, s32[]{:T(128)S(6)} %select_n.359, bf16[384,384]{0,1:T(8,128)(2,1)S(1)} %copy-done.3, s32[]{:T(128)S(6)} %select_n.358), kind=kOutput, calls=%fused_computation.20 | convolution fusion | flops 9449472 | bytes 282632 | tf_op jit(solution)/shard_map/dot_general | solution.py:218
  104.4 0.8 select_reduce_fusion.2
  105.3 2.3 %collective-permute-start.24 = (f32[4096]{0:T(1024)S(1)}, f32[4096]{0:T(1024)}, u32[]{:S(2)}, u32[]{:S(2)}) collective-permute-start(f32[4096]{0:T(1024)S(1)} %select_reduce_fusion.2), channel_id=1, source_target_pairs={{0,2},{1,3},{2,0},{3,1},{4,6},{5,7},{6,4},{7,5},{8,10},{9,11},{10,... | collective-permute-start | bytes 49160 | tf_op jit(solution)/shard_map/ppermute | solution.py:105
  107.6 1.5 %collective-permute-start.23 = (f32[4096]{0:T(1024)S(1)}, f32[4096]{0:T(1024)}, u32[]{:S(2)}, u32[]{:S(2)}) collective-permute-start(f32[4096]{0:T(1024)S(1)} %select_reduce_fusion.2), channel_id=1, source_target_pairs={{0,3},{1,0},{2,1},{3,2},{4,7},{5,4},{6,5},{7,6},{8,11},{9,8},{10,9... | collective-permute-start | bytes 49160 | tf_op jit(solution)/shard_map/ppermute | solution.py:105
  109.1 0.9 slice.164
  110.0 0.9 slice.163
  111.0 0.9 slice.162
  111.9 0.9 slice.161
  112.9 0.9 slice.160
  113.8 0.9 slice.159
  114.8 0.9 slice.158
  116.3 1.9 %select_select_fusion.1 = bf16[8,48,512]{2,1,0:T(8,128)(2,1)} fusion(bf16[48,512]{1,0:T(8,128)(2,1)} %bitcast.61, bf16[48,512]{1,0:T(8,128)(2,1)S(1)} %slice.146, bf16[48,512]{1,0:T(8,128)(2,1)S(1)} %slice.144, bf16[48,512]{1,0:T(8,128)(2,1)S(1)} %slice.142, bf16[48,512]{1,0:T(8,128)(2,1)S(1)} %slice.140, bf16[48,512]{1,0:T(8,128)(2,1)S(1)} %slice.138, ...), kind=kLoop, calls=%fused_computation.24 | loop fusion | flops 1376256 | bytes 786488 | tf_op jit(solution)/shard_map/jit(_where)/select_n | solution.py:98
  118.2 2.5 %fusion.10 = f32[512,256]{1,0:T(8,128)} fusion(bf16[384,512]{1,0:T(8,128)(2,1)} %bitcast.60, bf16[384,384]{0,1:T(8,128)(2,1)S(1)} %copy-done.3, bf16[384,1024]{1,0:T(8,128)(2,1)S(1)} %bitcast.46, s32[]{:T(128)S(6)} %select_n.359), kind=kOutput, calls=%fused_computation.19 | convolution fusion | flops 176357376 | bytes 1409028 | tf_op jit(solution)/shard_map/dot_general | solution.py:241
  120.7 1.5 %select_reduce_fusion.3 = f32[4096]{0:T(1024)} fusion(f32[4096]{0:T(1024)S(1)} %select_reduce_fusion.2, f32[4096]{0:T(1024)S(1)} %collective-permute-done.25, f32[4096]{0:T(1024)} %collective-permute-done.24, f32[4096]{0:T(1024)} %collective-permute-done.23, pred[4]{0:T(512)(128)(4,1)S(1)} %copy-done.7, pred[4]{0:T(512)(128)(4,1)S(1)} %copy-done.9, ...), kind=kLoop, calls=%fused_computation.53 | loop fusion | flops 61440 | bytes 81932 | tf_op jit(solution)/shard_map/reduce_sum | solution.py:111
  (124 shorter events, 16.9 us)
Async XLA Ops:
  0.6 55.9 %copy-start = (bf16[1024,1024]{1,0:T(8,128)(2,1)S(1)}, bf16[1024,1024]{1,0:T(8,128)(2,1)}, u32[]{:S(2)}) copy-start(bf16[1024,1024]{1,0:T(8,128)(2,1)} %param.13) | copy-start | bytes 6291460
  3.7 13.6 %collective-permute-start.5 = (bf16[97,256]{1,0:T(8,128)(2,1)S(1)}, bf16[97,256]{1,0:T(8,128)(2,1)}, u32[]{:S(2)}, u32[]{:S(2)}) collective-permute-start(bf16[97,256]{1,0:T(8,128)(2,1)S(1)} %constant_dynamic-update-slice_fusion), channel_id=1, source_target_pairs={{0,1},{1,2},{2,3},{3,0},{4,5},{5,6},{6,7},{7,4},{8,9},{9,10},{10,1... | collective-permute-start | bytes 149000 | tf_op jit(solution)/shard_map/ppermute | solution.py:105
  6.8 13.4 %collective-permute-start.4 = (bf16[97,256]{1,0:T(8,128)(2,1)S(1)}, bf16[97,256]{1,0:T(8,128)(2,1)}, u32[]{:S(2)}, u32[]{:S(2)}) collective-permute-start(bf16[97,256]{1,0:T(8,128)(2,1)S(1)} %constant_dynamic-update-slice_fusion), channel_id=1, source_target_pairs={{0,2},{1,3},{2,0},{3,1},{4,6},{5,7},{6,4},{7,5},{8,10},{9,11},{10,... | collective-permute-start | bytes 149000 | tf_op jit(solution)/shard_map/ppermute | solution.py:105
  9.4 10.8 %collective-permute-start.3 = (bf16[97,256]{1,0:T(8,128)(2,1)S(1)}, bf16[97,256]{1,0:T(8,128)(2,1)}, u32[]{:S(2)}, u32[]{:S(2)}) collective-permute-start(bf16[97,256]{1,0:T(8,128)(2,1)S(1)} %constant_dynamic-update-slice_fusion), channel_id=1, source_target_pairs={{0,3},{1,0},{2,1},{3,2},{4,7},{5,4},{6,5},{7,6},{8,11},{9,8},{10,9... | collective-permute-start | bytes 149000 | tf_op jit(solution)/shard_map/ppermute | solution.py:105
  13.4 3.2 %copy-start.20 = (f32[128]{0:T(128)}, f32[128]{0:T(128)S(1)}, u32[]{:S(2)}) copy-start(f32[128]{0:T(128)S(1)} %get-tuple-element.37) | copy-start | bytes 1540
  16.0 9.9 %collective-permute-start.2 = (f32[48,1024]{1,0:T(8,128)}, f32[48,1024]{1,0:T(8,128)S(1)}, u32[]{:S(2)}, u32[]{:S(2)}) collective-permute-start(f32[48,1024]{1,0:T(8,128)} %get-tuple-element.27), channel_id=1, source_target_pairs={{0,1},{1,2},{2,3},{3,0},{4,5},{5,6},{6,7},{7,4},{8,9},{9,10},{10,1... | collective-permute-start | bytes 589832 | tf_op jit(solution)/shard_map/ppermute | solution.py:121
  16.6 15.8 %collective-permute-start.1 = (f32[48,1024]{1,0:T(8,128)S(1)}, f32[48,1024]{1,0:T(8,128)S(1)}, u32[]{:S(2)}, u32[]{:S(2)}) collective-permute-start(f32[48,1024]{1,0:T(8,128)S(1)} %get-tuple-element.28), channel_id=1, source_target_pairs={{0,2},{1,3},{2,0},{3,1},{4,6},{5,7},{6,4},{7,5},{8,10},{9,11},{10,... | collective-permute-start | bytes 589832 | tf_op jit(solution)/shard_map/ppermute | solution.py:121
  17.0 33.0 %copy-start.6 = (pred[4]{0:T(512)(128)(4,1)}, pred[4]{0:T(512)(128)(4,1)S(1)}, u32[]{:S(2)}) copy-start(pred[4]{0:T(512)(128)(4,1)S(1)} %get-tuple-element.49) | copy-start | bytes 16
  17.0 32.9 %copy-start.8 = (pred[4]{0:T(512)(128)(4,1)}, pred[4]{0:T(512)(128)(4,1)S(1)}, u32[]{:S(2)}) copy-start(pred[4]{0:T(512)(128)(4,1)S(1)} %get-tuple-element.50) | copy-start | bytes 16
  17.0 32.9 %copy-start.10 = (pred[4]{0:T(512)(128)(4,1)}, pred[4]{0:T(512)(128)(4,1)S(1)}, u32[]{:S(2)}) copy-start(pred[4]{0:T(512)(128)(4,1)S(1)} %broadcast_compare_fusion.9) | copy-start | bytes 16
  17.1 31.6 %copy-start.12 = (pred[8]{0:T(512)(128)(4,1)}, pred[8]{0:T(512)(128)(4,1)S(1)}, u32[]{:S(2)}) copy-start(pred[8]{0:T(512)(128)(4,1)S(1)} %get-tuple-element.43) | copy-start | bytes 28
  17.1 31.6 %copy-start.13 = (pred[8]{0:T(512)(128)(4,1)}, pred[8]{0:T(512)(128)(4,1)S(1)}, u32[]{:S(2)}) copy-start(pred[8]{0:T(512)(128)(4,1)S(1)} %get-tuple-element.44) | copy-start | bytes 28
  17.1 31.6 %copy-start.14 = (pred[8]{0:T(512)(128)(4,1)}, pred[8]{0:T(512)(128)(4,1)S(1)}, u32[]{:S(2)}) copy-start(pred[8]{0:T(512)(128)(4,1)S(1)} %get-tuple-element.45) | copy-start | bytes 28
  17.1 31.6 %copy-start.15 = (pred[8]{0:T(512)(128)(4,1)}, pred[8]{0:T(512)(128)(4,1)S(1)}, u32[]{:S(2)}) copy-start(pred[8]{0:T(512)(128)(4,1)S(1)} %get-tuple-element.46) | copy-start | bytes 28
  17.1 31.6 %copy-start.16 = (pred[8]{0:T(512)(128)(4,1)}, pred[8]{0:T(512)(128)(4,1)S(1)}, u32[]{:S(2)}) copy-start(pred[8]{0:T(512)(128)(4,1)S(1)} %get-tuple-element.47) | copy-start | bytes 28
  17.1 31.6 %copy-start.17 = (pred[8]{0:T(512)(128)(4,1)}, pred[8]{0:T(512)(128)(4,1)S(1)}, u32[]{:S(2)}) copy-start(pred[8]{0:T(512)(128)(4,1)S(1)} %get-tuple-element.48) | copy-start | bytes 28
  17.2 31.6 %copy-start.18 = (pred[8]{0:T(512)(128)(4,1)}, pred[8]{0:T(512)(128)(4,1)S(1)}, u32[]{:S(2)}) copy-start(pred[8]{0:T(512)(128)(4,1)S(1)} %broadcast_compare_fusion.6) | copy-start | bytes 28
  17.3 16.6 %collective-permute-start = (f32[48,1024]{1,0:T(8,128)S(1)}, f32[48,1024]{1,0:T(8,128)S(1)}, u32[]{:S(2)}, u32[]{:S(2)}) collective-permute-start(f32[48,1024]{1,0:T(8,128)S(1)} %get-tuple-element.25), channel_id=1, source_target_pairs={{0,3},{1,0},{2,1},{3,2},{4,7},{5,4},{6,5},{7,6},{8,11},{9,8},{10,9... | collective-permute-start | bytes 589832 | tf_op jit(solution)/shard_map/ppermute | solution.py:121
  21.3 13.5 %collective-permute-start.15 = (bf16[4,97,256]{2,0,1:T(4,128)(2,1)S(1)}, bf16[4,97,256]{2,0,1:T(4,128)(2,1)S(1)}, u32[]{:S(2)}, u32[]{:S(2)}) collective-permute-start(bf16[4,97,256]{2,0,1:T(4,128)(2,1)S(1)} %select_select_fusion.3), channel_id=1, source_target_pairs={{0,4},{4,8},{8,12},{12,16},{16,20},{20,24},{24,28},{28,0},{1,5},{5... | collective-permute-start | bytes 595976 | tf_op jit(solution)/shard_map/ppermute | solution.py:105
  21.4 14.9 %collective-permute-start.14 = (bf16[4,97,256]{2,0,1:T(4,128)(2,1)S(1)}, bf16[4,97,256]{2,0,1:T(4,128)(2,1)S(1)}, u32[]{:S(2)}, u32[]{:S(2)}) collective-permute-start(bf16[4,97,256]{2,0,1:T(4,128)(2,1)S(1)} %select_select_fusion.3), channel_id=1, source_target_pairs={{0,8},{4,12},{8,16},{12,20},{16,24},{20,28},{24,0},{28,4},{1,9},{5... | collective-permute-start | bytes 595976 | tf_op jit(solution)/shard_map/ppermute | solution.py:105
  25.9 12.8 %collective-permute-start.13 = (bf16[4,97,256]{2,0,1:T(4,128)(2,1)S(1)}, bf16[4,97,256]{2,0,1:T(4,128)(2,1)S(1)}, u32[]{:S(2)}, u32[]{:S(2)}) collective-permute-start(bf16[4,97,256]{2,0,1:T(4,128)(2,1)S(1)} %select_select_fusion.3), channel_id=1, source_target_pairs={{0,12},{4,16},{8,20},{12,24},{16,28},{20,0},{24,4},{28,8},{1,13},{... | collective-permute-start | bytes 595976 | tf_op jit(solution)/shard_map/ppermute | solution.py:105
  32.4 8.8 %collective-permute-start.12 = (bf16[4,97,256]{2,0,1:T(4,128)(2,1)S(1)}, bf16[4,97,256]{2,0,1:T(4,128)(2,1)S(1)}, u32[]{:S(2)}, u32[]{:S(2)}) collective-permute-start(bf16[4,97,256]{2,0,1:T(4,128)(2,1)S(1)} %select_select_fusion.3), channel_id=1, source_target_pairs={{0,16},{4,20},{8,24},{12,28},{16,0},{20,4},{24,8},{28,12},{1,17},{... | collective-permute-start | bytes 595976 | tf_op jit(solution)/shard_map/ppermute | solution.py:105
  33.9 9.0 %collective-permute-start.11 = (bf16[4,97,256]{2,0,1:T(4,128)(2,1)S(1)}, bf16[4,97,256]{2,0,1:T(4,128)(2,1)S(1)}, u32[]{:S(2)}, u32[]{:S(2)}) collective-permute-start(bf16[4,97,256]{2,0,1:T(4,128)(2,1)S(1)} %select_select_fusion.3), channel_id=1, source_target_pairs={{0,20},{4,24},{8,28},{12,0},{16,4},{20,8},{24,12},{28,16},{1,21},{... | collective-permute-start | bytes 595976 | tf_op jit(solution)/shard_map/ppermute | solution.py:105
  34.8 9.2 %collective-permute-start.10 = (bf16[4,97,256]{2,0,1:T(4,128)(2,1)S(1)}, bf16[4,97,256]{2,0,1:T(4,128)(2,1)S(1)}, u32[]{:S(2)}, u32[]{:S(2)}) collective-permute-start(bf16[4,97,256]{2,0,1:T(4,128)(2,1)S(1)} %select_select_fusion.3), channel_id=1, source_target_pairs={{0,24},{4,28},{8,0},{12,4},{16,8},{20,12},{24,16},{28,20},{1,25},{... | collective-permute-start | bytes 595976 | tf_op jit(solution)/shard_map/ppermute | solution.py:105
  36.2 8.2 %collective-permute-start.9 = (bf16[4,97,256]{2,0,1:T(4,128)(2,1)S(1)}, bf16[4,97,256]{2,0,1:T(4,128)(2,1)S(1)}, u32[]{:S(2)}, u32[]{:S(2)}) collective-permute-start(bf16[4,97,256]{2,0,1:T(4,128)(2,1)S(1)} %select_select_fusion.3), channel_id=1, source_target_pairs={{0,28},{4,0},{8,4},{12,8},{16,12},{20,16},{24,20},{28,24},{1,29},{... | collective-permute-start | bytes 595976 | tf_op jit(solution)/shard_map/ppermute | solution.py:105
  38.8 10.0 %collective-permute-start.8 = (bf16[48,1024]{1,0:T(8,128)(2,1)S(1)}, bf16[48,1024]{1,0:T(8,128)(2,1)S(1)}, u32[]{:S(2)}, u32[]{:S(2)}) collective-permute-start(bf16[48,1024]{1,0:T(8,128)(2,1)S(1)} %divide_convert_fusion), channel_id=1, source_target_pairs={{0,1},{1,2},{2,3},{3,0},{4,5},{5,6},{6,7},{7,4},{8,9},{9,10},{10,1... | collective-permute-start | bytes 294920 | tf_op jit(solution)/shard_map/ppermute | solution.py:105
  41.2 8.0 %collective-permute-start.7 = (bf16[48,1024]{1,0:T(8,128)(2,1)S(1)}, bf16[48,1024]{1,0:T(8,128)(2,1)S(1)}, u32[]{:S(2)}, u32[]{:S(2)}) collective-permute-start(bf16[48,1024]{1,0:T(8,128)(2,1)S(1)} %divide_convert_fusion), channel_id=1, source_target_pairs={{0,2},{1,3},{2,0},{3,1},{4,6},{5,7},{6,4},{7,5},{8,10},{9,11},{10,... | collective-permute-start | bytes 294920 | tf_op jit(solution)/shard_map/ppermute | solution.py:105
  43.0 7.0 %collective-permute-start.6 = (bf16[48,1024]{1,0:T(8,128)(2,1)S(1)}, bf16[48,1024]{1,0:T(8,128)(2,1)S(1)}, u32[]{:S(2)}, u32[]{:S(2)}) collective-permute-start(bf16[48,1024]{1,0:T(8,128)(2,1)S(1)} %divide_convert_fusion), channel_id=1, source_target_pairs={{0,3},{1,0},{2,1},{3,2},{4,7},{5,4},{6,5},{7,6},{8,11},{9,8},{10,9... | collective-permute-start | bytes 294920 | tf_op jit(solution)/shard_map/ppermute | solution.py:105
  56.1 19.9 %copy-start.1 = (bf16[128,4096]{1,0:T(8,128)(2,1)S(1)}, bf16[128,4096]{1,0:T(8,128)(2,1)}, u32[]{:S(2)}) copy-start(bf16[128,4096]{1,0:T(8,128)(2,1)} %param.10) | copy-start | bytes 3145732
  56.1 19.9 %copy-start.21 = (f32[128]{0:T(128)S(1)}, f32[128]{0:T(128)}, u32[]{:S(2)}) copy-start(f32[128]{0:T(128)} %copy-done.20) | copy-start | bytes 1540
  56.1 19.9 %copy-start.22 = (s32[1,128]{1,0:T(1,128)S(1)}, s32[1,128]{1,0:T(1,128)}, u32[]{:S(2)}) copy-start(s32[1,128]{1,0:T(1,128)} %param.11) | copy-start | bytes 1540
  77.6 13.0 %copy-start.19 = (f32[128]{0:T(128)S(1)}, f32[128]{0:T(128)}, u32[]{:S(2)}) copy-start(f32[128]{0:T(128)} %get-tuple-element.36) | copy-start | bytes 1540
  79.2 13.1 %collective-permute-start.22 = (f32[28672]{0:T(1024)S(1)}, f32[28672]{0:T(1024)S(1)}, u32[]{:S(2)}, u32[]{:S(2)}) collective-permute-start(f32[28672]{0:T(1024)S(1)} %get-tuple-element.35), channel_id=1, source_target_pairs={{0,4},{4,8},{8,12},{12,16},{16,20},{20,24},{24,28},{28,0},{1,5},{5... | collective-permute-start | bytes 344072 | tf_op jit(solution)/shard_map/ppermute | solution.py:134
  79.2 14.3 %collective-permute-start.21 = (f32[28672]{0:T(1024)S(1)}, f32[28672]{0:T(1024)S(1)}, u32[]{:S(2)}, u32[]{:S(2)}) collective-permute-start(f32[28672]{0:T(1024)S(1)} %get-tuple-element.34), channel_id=1, source_target_pairs={{0,8},{4,12},{8,16},{12,20},{16,24},{20,28},{24,0},{28,4},{1,9},{5... | collective-permute-start | bytes 344072 | tf_op jit(solution)/shard_map/ppermute | solution.py:134
  87.3 13.5 %collective-permute-start.20 = (f32[28672]{0:T(1024)}, f32[28672]{0:T(1024)}, u32[]{:S(2)}, u32[]{:S(2)}) collective-permute-start(f32[28672]{0:T(1024)} %get-tuple-element.33), channel_id=1, source_target_pairs={{0,12},{4,16},{8,20},{12,24},{16,28},{20,0},{24,4},{28,8},{1,13},{... | collective-permute-start | bytes 344072 | tf_op jit(solution)/shard_map/ppermute | solution.py:134
  90.0 11.5 %collective-permute-start.19 = (f32[28672]{0:T(1024)}, f32[28672]{0:T(1024)}, u32[]{:S(2)}, u32[]{:S(2)}) collective-permute-start(f32[28672]{0:T(1024)} %get-tuple-element.32), channel_id=1, source_target_pairs={{0,16},{4,20},{8,24},{12,28},{16,0},{20,4},{24,8},{28,12},{1,17},{... | collective-permute-start | bytes 344072 | tf_op jit(solution)/shard_map/ppermute | solution.py:134
  90.2 12.1 %collective-permute-start.18 = (f32[28672]{0:T(1024)S(1)}, f32[28672]{0:T(1024)}, u32[]{:S(2)}, u32[]{:S(2)}) collective-permute-start(f32[28672]{0:T(1024)S(1)} %get-tuple-element.31), channel_id=1, source_target_pairs={{0,20},{4,24},{8,28},{12,0},{16,4},{20,8},{24,12},{28,16},{1,21},{... | collective-permute-start | bytes 344072 | tf_op jit(solution)/shard_map/ppermute | solution.py:134
  90.6 7.0 %copy-start.3 = (bf16[384,384]{0,1:T(8,128)(2,1)S(1)}, bf16[384,384]{0,1:T(8,128)(2,1)}, u32[]{:S(2)}) copy-start(bf16[384,384]{0,1:T(8,128)(2,1)} %copy-done.2) | copy-start | bytes 884740
  92.3 4.6 %copy-start.4 = (f32[28672]{0:T(1024)}, f32[28672]{0:T(1024)S(1)}, u32[]{:S(2)}) copy-start(f32[28672]{0:T(1024)S(1)} %collective-permute-done.22) | copy-start | bytes 344068
  92.3 10.6 %collective-permute-start.17 = (f32[28672]{0:T(1024)S(1)}, f32[28672]{0:T(1024)}, u32[]{:S(2)}, u32[]{:S(2)}) collective-permute-start(f32[28672]{0:T(1024)S(1)} %get-tuple-element.30), channel_id=1, source_target_pairs={{0,24},{4,28},{8,0},{12,4},{16,8},{20,12},{24,16},{28,20},{1,25},{... | collective-permute-start | bytes 344072 | tf_op jit(solution)/shard_map/ppermute | solution.py:134
  93.6 3.4 %copy-start.5 = (f32[28672]{0:T(1024)}, f32[28672]{0:T(1024)S(1)}, u32[]{:S(2)}) copy-start(f32[28672]{0:T(1024)S(1)} %collective-permute-done.21) | copy-start | bytes 344068
  93.6 10.1 %collective-permute-start.16 = (f32[28672]{0:T(1024)S(1)}, f32[28672]{0:T(1024)}, u32[]{:S(2)}, u32[]{:S(2)}) collective-permute-start(f32[28672]{0:T(1024)S(1)} %get-tuple-element.29), channel_id=1, source_target_pairs={{0,28},{4,0},{8,4},{12,8},{16,12},{20,16},{24,20},{28,24},{1,29},{... | collective-permute-start | bytes 344072 | tf_op jit(solution)/shard_map/ppermute | solution.py:134
  105.2 15.5 %collective-permute-start.25 = (f32[4096]{0:T(1024)S(1)}, f32[4096]{0:T(1024)S(1)}, u32[]{:S(2)}, u32[]{:S(2)}) collective-permute-start(f32[4096]{0:T(1024)S(1)} %select_reduce_fusion.2), channel_id=1, source_target_pairs={{0,1},{1,2},{2,3},{3,0},{4,5},{5,6},{6,7},{7,4},{8,9},{9,10},{10,1... | collective-permute-start | bytes 49160 | tf_op jit(solution)/shard_map/ppermute | solution.py:105
  105.3 15.4 %collective-permute-start.24 = (f32[4096]{0:T(1024)S(1)}, f32[4096]{0:T(1024)}, u32[]{:S(2)}, u32[]{:S(2)}) collective-permute-start(f32[4096]{0:T(1024)S(1)} %select_reduce_fusion.2), channel_id=1, source_target_pairs={{0,2},{1,3},{2,0},{3,1},{4,6},{5,7},{6,4},{7,5},{8,10},{9,11},{10,... | collective-permute-start | bytes 49160 | tf_op jit(solution)/shard_map/ppermute | solution.py:105
  107.6 13.1 %collective-permute-start.23 = (f32[4096]{0:T(1024)S(1)}, f32[4096]{0:T(1024)}, u32[]{:S(2)}, u32[]{:S(2)}) collective-permute-start(f32[4096]{0:T(1024)S(1)} %select_reduce_fusion.2), channel_id=1, source_target_pairs={{0,3},{1,0},{2,1},{3,2},{4,7},{5,4},{6,5},{7,6},{8,11},{9,8},{10,9... | collective-permute-start | bytes 49160 | tf_op jit(solution)/shard_map/ppermute | solution.py:105
  116.3 4.4 %copy-start.7 = (pred[4]{0:T(512)(128)(4,1)S(1)}, pred[4]{0:T(512)(128)(4,1)}, u32[]{:S(2)}) copy-start(pred[4]{0:T(512)(128)(4,1)} %copy-done.6) | copy-start | bytes 16
  116.3 4.4 %copy-start.9 = (pred[4]{0:T(512)(128)(4,1)S(1)}, pred[4]{0:T(512)(128)(4,1)}, u32[]{:S(2)}) copy-start(pred[4]{0:T(512)(128)(4,1)} %copy-done.8) | copy-start | bytes 16
  116.3 4.4 %copy-start.11 = (pred[4]{0:T(512)(128)(4,1)S(1)}, pred[4]{0:T(512)(128)(4,1)}, u32[]{:S(2)}) copy-start(pred[4]{0:T(512)(128)(4,1)} %copy-done.10) | copy-start | bytes 16
  (1 other events, 0.7 us)

commit v19 on v14

--- a/solution.py
+++ b/solution.py
@@ -178,7 +178,6 @@
     mean_pooled = mean_blocks.transpose(1, 0, 2).reshape(rows, model_width)
 
     gathered = gather_blocks(group_blocks, "dp")
-    mean_pooled, gathered = lax.optimization_barrier((mean_pooled, gathered))
     slice_width = model_width // data_count
     pieces = mean_pooled.reshape(rows, data_count, slice_width).transpose(1, 0, 2)
 
@@ -219,6 +218,7 @@
     mean_part = lax.dot_general(
         grad_low, proj_weight, contract_last, preferred_element_type=jnp.float32
     )
+    mean_part, mean_pooled = lax.optimization_barrier((mean_part, mean_pooled))
     mean_grad = lax.all_gather(mean_part, "fsdp", axis=1, tiled=True)
     pool_grad = mean_grad / counts[:, None]
     normed_grad = lax.dot_general(

time: 110 us -> 125 us (1.14); the launches traced: 109 us -> 122 us
  local copies, waits for them, and re-layouts: 8.89 us -> 17.1 us
  other arithmetic: 15 us -> 18.9 us
  starting transfers between devices: 41.7 us -> 39.4 us
  matrix products: 10.3 us -> 12.1 us
    another operation x2, local copies, waits for them, and re-layouts: 0.78 us -> 5.11 us
    convert_element_type x0 -> x1, local copies, waits for them, and re-layouts: none -> 2.35 us  [local_small(): pieces.astype(jnp.float32)]
    ppermute x7, starting transfers between devices: 14.7 us -> 12.4 us  [spread_with_sum(): arrived = lax.ppermute(payload, axis, [(i, (i + s) % n) for i in range(n)])]
    dot_general x1, matrix products: 1.63 us -> 3.44 us  [local_small(): lax.dot_general(member.astype(jnp.float32), pool_grad, contract_first, pr...]
    concatenate x1, other arithmetic: 0.06 us -> 1.58 us  [spread_with_sum(): payload = jnp.concatenate([total, piece.reshape(-1)])]
    unnamed x51 -> x79, local copies, waits for them, and re-layouts: 3.91 us -> 3 us
  transfers between devices with their start and end apart: 26 -> 26, of which waited for: 5 -> 4; matrix products, arithmetic and copies ran while one was open for 18% -> 27% of each run, Pallas kernels for 0% -> 0%
where the time goes in v19:
time: 125 us; the launch traced here: 122 us
  starting transfers between devices  39.4 us (32%)
  blocking collectives  20 us (16%)
  other arithmetic  18.9 us (15%)
  local copies, waits for them, and re-layouts  17.1 us (14%)
  matrix products  12.1 us (10%)
  waiting for transfers between devices  11.5 us (9%)
  between operations  3.3 us (3%)
    ppermute x16, starting transfers between devices, gather_blocks(): lax.ppermute(x, axis, [(i, (i + s) % n) for i in range(n)])  23.2 us
    all_gather x1, blocking collectives, local_small(): mean_grad = lax.all_gather(mean_part, 'fsdp', axis=1, tiled=True)  20 us
    ppermute x7, starting transfers between devices, spread_with_sum(): arrived = lax.ppermute(payload, axis, [(i, (i + s) % n) for i in range(n)])  12.4 us
    ppermute x3, waiting for transfers between devices, scatter_sum(): lax.ppermute(piece, axis, [(i, (i + s) % n) for i in range(n)])  10.2 us
    select_n x4, other arithmetic, arrange(): out = jnp.where(source == s, copies[s][None], out)  6.19 us
    another operation x2, local copies, waits for them, and re-layouts  5.11 us
    ppermute x3, starting transfers between devices, scatter_sum(): lax.ppermute(piece, axis, [(i, (i + s) % n) for i in range(n)])  3.88 us
    dot_general x1, matrix products, local_small(): lax.dot_general(member.astype(jnp.float32), pool_grad, contract_first, pr...  3.44 us
  transfers between devices with their start and end apart: 26, of which 4 were waited for; matrix products, arithmetic and copies ran while one was open for 27% of the time, Pallas kernels for 0%

profile of v19, /device:TPU:0, one launch (start us, length us, event | category | flops | bytes accessed | tf_op | source)
XLA Modules:
  0.0 122.4 jit_solution(2637657691043970427)
XLA Ops:
  0.6 0.9 constant_dynamic-update-slice_fusion.2
  2.2 0.7 constant_dynamic-update-slice_fusion.1
  2.9 0.7 fusion.29
  3.7 3.1 %collective-permute-start.2 = (bf16[97,256]{1,0:T(8,128)(2,1)S(1)}, bf16[97,256]{1,0:T(8,128)(2,1)S(1)}, u32[]{:S(2)}, u32[]{:S(2)}) collective-permute-start(bf16[97,256]{1,0:T(8,128)(2,1)S(1)} %constant_dynamic-update-slice_fusion), channel_id=1, source_target_pairs={{0,1},{1,2},{2,3},{3,0},{4,5},{5,6},{6,7},{7,4},{8,9},{9,10},{10,1... | collective-permute-start | bytes 149000 | tf_op jit(solution)/shard_map/ppermute | solution.py:105
  6.8 2.6 %collective-permute-start.1 = (bf16[97,256]{1,0:T(8,128)(2,1)S(1)}, bf16[97,256]{1,0:T(8,128)(2,1)S(1)}, u32[]{:S(2)}, u32[]{:S(2)}) collective-permute-start(bf16[97,256]{1,0:T(8,128)(2,1)S(1)} %constant_dynamic-update-slice_fusion), channel_id=1, source_target_pairs={{0,2},{1,3},{2,0},{3,1},{4,6},{5,7},{6,4},{7,5},{8,10},{9,11},{10,... | collective-permute-start | bytes 149000 | tf_op jit(solution)/shard_map/ppermute | solution.py:105
  9.4 1.3 %collective-permute-start = (bf16[97,256]{1,0:T(8,128)(2,1)S(1)}, bf16[97,256]{1,0:T(8,128)(2,1)S(1)}, u32[]{:S(2)}, u32[]{:S(2)}) collective-permute-start(bf16[97,256]{1,0:T(8,128)(2,1)S(1)} %constant_dynamic-update-slice_fusion), channel_id=1, source_target_pairs={{0,3},{1,0},{2,1},{3,2},{4,7},{5,4},{6,5},{7,6},{8,11},{9,8},{10,9... | collective-permute-start | bytes 149000 | tf_op jit(solution)/shard_map/ppermute | solution.py:105
  10.7 1.5 %fusion = f32[128]{0:T(128)S(1)} fusion(bf16[128,4096]{1,0:T(8,128)(2,1)} %param.10), kind=kLoop, calls=%fused_computation.5 | loop fusion | flops 1572736 | bytes 1049088 | tf_op jit(solution)/shard_map/reduce_sum | solution.py:168
  13.5 1.7 %fusion.9 = f32[48,4096]{1,0:T(8,128)S(1)} fusion(bf16[128,4096]{1,0:T(8,128)(2,1)} %param.10, f32[4096]{0:T(1024)S(1)} %convert_element_type.96, f32[128]{0:T(128)S(1)} %get-tuple-element.33, s32[128]{0:T(128)} %bitcast.56), kind=kOutput, calls=%fused_computation.18 | convolution fusion | flops 52434944 | bytes 1852416 | tf_op jit(solution)/shard_map/dot_general | solution.py:172
  15.2 0.8 constant_dynamic-slice_fusion.11
  17.4 2.9 %collective-permute-start.10 = (f32[48,1024]{1,0:T(8,128)S(1)}, f32[48,1024]{1,0:T(8,128)S(1)}, u32[]{:S(2)}, u32[]{:S(2)}) collective-permute-start(f32[48,1024]{1,0:T(8,128)S(1)} %get-tuple-element.21), channel_id=1, source_target_pairs={{0,3},{1,0},{2,1},{3,2},{4,7},{5,4},{6,5},{7,6},{8,11},{9,8},{10,9... | collective-permute-start | bytes 589832 | tf_op jit(solution)/shard_map/ppermute | solution.py:121
  20.6 1.5 %collective-permute-start.8 = (bf16[4,97,256]{2,0,1:T(4,128)(2,1)S(1)}, bf16[4,97,256]{2,0,1:T(4,128)(2,1)S(1)}, u32[]{:S(2)}, u32[]{:S(2)}) collective-permute-start(bf16[4,97,256]{2,0,1:T(4,128)(2,1)S(1)} %select_select_fusion.3), channel_id=1, source_target_pairs={{0,8},{4,12},{8,16},{12,20},{16,24},{20,28},{24,0},{28,4},{1,9},{5... | collective-permute-start | bytes 595976 | tf_op jit(solution)/shard_map/ppermute | solution.py:105
  22.3 3.7 %collective-permute-done.12 = f32[48,1024]{1,0:T(8,128)S(1)} collective-permute-done((f32[48,1024]{1,0:T(8,128)}, f32[48,1024]{1,0:T(8,128)S(1)}, u32[]{:S(2)}, u32[]{:S(2)}) %collective-permute-start.12) | collective-permute-done | bytes 196640 | tf_op jit(solution)/shard_map/ppermute | solution.py:121
  26.0 6.5 %collective-permute-done.11 = f32[48,1024]{1,0:T(8,128)S(1)} collective-permute-done((f32[48,1024]{1,0:T(8,128)}, f32[48,1024]{1,0:T(8,128)S(1)}, u32[]{:S(2)}, u32[]{:S(2)}) %collective-permute-start.11) | collective-permute-done | bytes 196640 | tf_op jit(solution)/shard_map/ppermute | solution.py:121
  32.5 1.5 %collective-permute-start.6 = (bf16[4,97,256]{2,0,1:T(4,128)(2,1)S(1)}, bf16[4,97,256]{2,0,1:T(4,128)(2,1)S(1)}, u32[]{:S(2)}, u32[]{:S(2)}) collective-permute-start(bf16[4,97,256]{2,0,1:T(4,128)(2,1)S(1)} %select_select_fusion.3), channel_id=1, source_target_pairs={{0,16},{4,20},{8,24},{12,28},{16,0},{20,4},{24,8},{28,12},{1,17},{... | collective-permute-start | bytes 595976 | tf_op jit(solution)/shard_map/ppermute | solution.py:105
  34.0 0.8 select_reduce_fusion
  34.8 1.5 %collective-permute-start.4 = (bf16[4,97,256]{2,0,1:T(4,128)(2,1)S(1)}, bf16[4,97,256]{2,0,1:T(4,128)(2,1)S(1)}, u32[]{:S(2)}, u32[]{:S(2)}) collective-permute-start(bf16[4,97,256]{2,0,1:T(4,128)(2,1)S(1)} %select_select_fusion.3), channel_id=1, source_target_pairs={{0,24},{4,28},{8,0},{12,4},{16,8},{20,12},{24,16},{28,20},{1,25},{... | collective-permute-start | bytes 595976 | tf_op jit(solution)/shard_map/ppermute | solution.py:105
  36.3 2.5 %collective-permute-start.3 = (bf16[4,97,256]{2,0,1:T(4,128)(2,1)S(1)}, bf16[4,97,256]{2,0,1:T(4,128)(2,1)S(1)}, u32[]{:S(2)}, u32[]{:S(2)}) collective-permute-start(bf16[4,97,256]{2,0,1:T(4,128)(2,1)S(1)} %select_select_fusion.3), channel_id=1, source_target_pairs={{0,28},{4,0},{8,4},{12,8},{16,12},{20,16},{24,20},{28,24},{1,29},{... | collective-permute-start | bytes 595976 | tf_op jit(solution)/shard_map/ppermute | solution.py:105
  38.9 2.6 %collective-permute-start.15 = (bf16[48,1024]{1,0:T(8,128)(2,1)S(1)}, bf16[48,1024]{1,0:T(8,128)(2,1)}, u32[]{:S(2)}, u32[]{:S(2)}) collective-permute-start(bf16[48,1024]{1,0:T(8,128)(2,1)S(1)} %divide_convert_fusion), channel_id=1, source_target_pairs={{0,1},{1,2},{2,3},{3,0},{4,5},{5,6},{6,7},{7,4},{8,9},{9,10},{10,1... | collective-permute-start | bytes 294920 | tf_op jit(solution)/shard_map/ppermute | solution.py:105
  41.5 1.6 %collective-permute-start.14 = (bf16[48,1024]{1,0:T(8,128)(2,1)S(1)}, bf16[48,1024]{1,0:T(8,128)(2,1)}, u32[]{:S(2)}, u32[]{:S(2)}) collective-permute-start(bf16[48,1024]{1,0:T(8,128)(2,1)S(1)} %divide_convert_fusion), channel_id=1, source_target_pairs={{0,2},{1,3},{2,0},{3,1},{4,6},{5,7},{6,4},{7,5},{8,10},{9,11},{10,... | collective-permute-start | bytes 294920 | tf_op jit(solution)/shard_map/ppermute | solution.py:105
  43.1 0.9 collective-permute-start.13
  44.5 4.2 %select_select_fusion = bf16[8,4,97,256]{3,1,2,0:T(4,128)(2,1)S(1)} fusion(pred[8]{0:T(512)(128)(4,1)S(1)} %get-tuple-element.40, pred[8]{0:T(512)(128)(4,1)S(1)} %get-tuple-element.41, pred[8]{0:T(512)(128)(4,1)S(1)} %get-tuple-element.42, pred[8]{0:T(512)(128)(4,1)S(1)} %get-tuple-element.43, pred[8]{0:T(512)(128)(4,1)S(1)} %get-tuple-element.44, ...), kind=kLoop, calls=%fused_computation.14 | loop fusion | flops 5562368 | bytes 3178552 | tf_op jit(solution)/shard_map/jit(_where)/select_n | solution.py:98
  49.6 1.1 copy.14
  50.9 1.7 %fusion.33 = (f32[384]{0:T(512)S(1)}, f32[384,384]{0,1:T(8,128)S(1)}) fusion(bf16[384,1024]{1,0:T(8,128)(2,1)} %bitcast.45, bf16[384,1024]{1,0:T(8,128)(2,1)S(1)} %bitcast.42), kind=kOutput, calls=%fused_computation.113 | convolution fusion | flops 302284416 | bytes 2164224 | tf_op jit(solution)/shard_map/dot_general | solution.py:194
  54.3 0.7 fusion.18
  55.1 20.0 %all_gather.3 = f32[48,4096]{1,0:T(8,128)S(1)} all-gather(f32[48,1024]{1,0:T(8,128)S(1)} %fusion.18), channel_id=1, replica_groups=mesh['dp'=8,'fsdp'=4] {'fsdp'}, dimensions={1}, use_global_device_ids=true | all-gather | bytes 983040 | tf_op jit(solution)/shard_map/all_gather | solution.py:222
  75.2 3.4 %fusion.6 = (f32[4096]{0:T(1024)}, f32[128]{0:T(128)S(1)}, f32[128,4096]{1,0:T(8,128)}) fusion(bf16[128,4096]{1,0:T(8,128)(2,1)S(1)} %copy-done.1, f32[128]{0:T(128)S(1)} %copy-done.33, f32[4096]{0:T(1024)S(1)} %convert_element_type.96, f32[48,4096]{1,0:T(8,128)S(1)} %all_gather.3, f32[48]{0:T(128)S(1)} %copy-done.30, s32[128]{0:T(128)S(1)} %bitcast.57), kind=kOutput, calls=%fused_computation.11 | convolution fusion | flops 305858432 | bytes 3966656 | tf_op jit(solution)/shard_map/dot_general | solution.py:224
  79.2 1.5 %select_select_fusion.2 = bf16[4,48,1024]{2,0,1:T(4,128)(2,1)S(1)} fusion(pred[4]{0:T(512)(128)(4,1)S(1)} %copy-done.10, pred[4]{0:T(512)(128)(4,1)S(1)} %copy-done.13, pred[4]{0:T(512)(128)(4,1)S(1)} %copy-done.7, bf16[48,1024]{1,0:T(8,128)(2,1)S(1)} %divide_convert_fusion, bf16[48,1024]{1,0:T(8,128)(2,1)} %collective-permute-done.15, ...), kind=kLoop, calls=%fused_computation.31 | loop fusion | flops 589824 | bytes 786444 | tf_op jit(solution)/shard_map/jit(_where)/select_n | solution.py:98
  80.7 1.0 convert_bitcast_fusion
  81.7 2.3 %reshape.412 = f32[48,8,512]{2,1,0:T(8,128)} reshape(f32[48,4,1024]{2,1,0:T(4,128)} %convert_bitcast_fusion) | data formatting | bytes 1572864 | tf_op jit(solution)/shard_map/convert_element_type | solution.py:235
  84.0 3.9 %constant_dynamic-slice_fusion.7 = (f32[48,1,512]{2,1,0:T(1,128)S(1)}, f32[48,1,512]{2,1,0:T(1,128)S(1)}, f32[48,1,512]{2,1,0:T(1,128)S(1)}, f32[48,1,512]{2,1,0...) fusion(f32[48,8,512]{2,1,0:T(8,128)} %reshape.412, ...), kind=kLoop, calls=%fused_computation.72 | loop fusion | bytes 1376284 | tf_op jit(solution)/shard_map/dynamic-slice
  87.9 1.6 %pad_maximum_fusion.6 = (f32[28672]{0:T(1024)S(1)}, f32[28672]{0:T(1024)}, f32[28672]{0:T(1024)}, f32[28672]{0:T(1024)}, f32[28672]{0:T(1024)}, /*index=5*/f32[28672]{0:T(1024)}, f32[28672]{0:T(1024)}) fusion(f32[4096]{0:T(1024)} %get-tuple-element.6, f32[24576]{0:T(1024)S(1)} %bitcast.47, f32[24576]{0:T(1024)S(1)} %bitcast.53, f32[24576]{0:T(1024)S(1)} %bitcast.52, ...), kind=kLoop, calls=%fused_computation.39 | loop fusion | flops 200704 | bytes 1507328 | tf_op jit(solution)/shard_map/concatenate | solution.py:133
  89.5 6.8 %collective-permute-start.21 = (f32[28672]{0:T(1024)}, f32[28672]{0:T(1024)}, u32[]{:S(2)}, u32[]{:S(2)}) collective-permute-start(f32[28672]{0:T(1024)} %get-tuple-element.30), channel_id=1, source_target_pairs={{0,8},{4,12},{8,16},{12,20},{16,24},{20,28},{24,0},{28,4},{1,9},{5... | collective-permute-start | bytes 344072 | tf_op jit(solution)/shard_map/ppermute | solution.py:134
  96.4 1.6 %fusion.3 = bf16[128,4096]{1,0:T(8,128)(2,1)} fusion(bf16[128,4096]{1,0:T(8,128)(2,1)S(1)} %copy-done.1, f32[128,4096]{1,0:T(8,128)S(1)} %copy-done.3, f32[128]{0:T(128)S(1)} %copy-done.35, f32[128]{0:T(128)S(1)} %copy-done.31, f32[4096]{0:T(1024)S(1)} %copy-done.5, f32[128]{0:T(128)S(1)} %copy-done.34), kind=kLoop, calls=%fused_computation.8 | loop fusion | flops 3670016 | bytes 4212224 | tf_op jit(solution)/shard_map/convert_element_type | solution.py:234
  98.0 1.4 %dynamic_slice.36 = f32[48,256]{1,0:T(8,128)} dynamic-slice(f32[384,1024]{1,0:T(8,128)} %copy-done.2, s32[]{:T(128)S(6)} %select_n.346, s32[]{:T(128)S(6)} %select_n.347), dynamic_slice_sizes={48,256} | dynamic-slice | bytes 98308 | tf_op jit(solution)/shard_map/dynamic_slice | solution.py:207
  100.1 1.7 %convolution_multiply_fusion.2 = f32[48,256]{1,0:T(8,128)} fusion(bf16[384,1024]{1,0:T(8,128)(2,1)} %bitcast.46, s32[]{:T(128)S(6)} %select_n.347, bf16[384,384]{0,1:T(8,128)(2,1)S(1)} %subtract_convert_fusion, s32[]{:T(128)S(6)} %select_n.346), kind=kOutput, calls=%fused_computation.17 | convolution fusion | flops 9449472 | bytes 282632 | tf_op jit(solution)/shard_map/dot_general | solution.py:214
  101.9 1.6 %collective-permute-start.20 = (f32[28672]{0:T(1024)}, f32[28672]{0:T(1024)S(1)}, u32[]{:S(2)}, u32[]{:S(2)}) collective-permute-start(f32[28672]{0:T(1024)} %get-tuple-element.29), channel_id=1, source_target_pairs={{0,12},{4,16},{8,20},{12,24},{16,28},{20,0},{24,4},{28,8},{1,13},{... | collective-permute-start | bytes 344072 | tf_op jit(solution)/shard_map/ppermute | solution.py:134
  103.5 1.3 %collective-permute-start.19 = (f32[28672]{0:T(1024)}, f32[28672]{0:T(1024)S(1)}, u32[]{:S(2)}, u32[]{:S(2)}) collective-permute-start(f32[28672]{0:T(1024)} %get-tuple-element.28), channel_id=1, source_target_pairs={{0,16},{4,20},{8,24},{12,28},{16,0},{20,4},{24,8},{28,12},{1,17},{... | collective-permute-start | bytes 344072 | tf_op jit(solution)/shard_map/ppermute | solution.py:134
  104.8 1.2 collective-permute-start.17
  106.0 1.5 %collective-permute-start.16 = (f32[28672]{0:T(1024)S(1)}, f32[28672]{0:T(1024)S(1)}, u32[]{:S(2)}, u32[]{:S(2)}) collective-permute-start(f32[28672]{0:T(1024)S(1)} %get-tuple-element.25), channel_id=1, source_target_pairs={{0,28},{4,0},{8,4},{12,8},{16,12},{20,16},{24,20},{28,24},{1,29},{... | collective-permute-start | bytes 344072 | tf_op jit(solution)/shard_map/ppermute | solution.py:134
  107.4 1.2 constant_dynamic-slice_fusion
  110.2 0.8 collective-permute-done.17
  111.0 0.9 select_reduce_fusion.2
  111.9 2.5 %collective-permute-start.24 = (f32[4096]{0:T(1024)S(1)}, f32[4096]{0:T(1024)S(1)}, u32[]{:S(2)}, u32[]{:S(2)}) collective-permute-start(f32[4096]{0:T(1024)S(1)} %select_reduce_fusion.2), channel_id=1, source_target_pairs={{0,2},{1,3},{2,0},{3,1},{4,6},{5,7},{6,4},{7,5},{8,10},{9,11},{10,... | collective-permute-start | bytes 49160 | tf_op jit(solution)/shard_map/ppermute | solution.py:105
  114.4 1.5 %collective-permute-start.23 = (f32[4096]{0:T(1024)S(1)}, f32[4096]{0:T(1024)S(1)}, u32[]{:S(2)}, u32[]{:S(2)}) collective-permute-start(f32[4096]{0:T(1024)S(1)} %select_reduce_fusion.2), channel_id=1, source_target_pairs={{0,3},{1,0},{2,1},{3,2},{4,7},{5,4},{6,5},{7,6},{8,11},{9,8},{10,9... | collective-permute-start | bytes 49160 | tf_op jit(solution)/shard_map/ppermute | solution.py:105
  115.9 0.9 slice.167
  116.8 0.9 slice.166
  118.4 2.1 %fusion.16 = f32[512,256]{1,0:T(8,128)} fusion(bf16[384,512]{1,0:T(8,128)(2,1)S(1)} %bitcast.44, f32[384,1024]{1,0:T(8,128)} %copy-done.2, s32[]{:T(128)S(6)} %select_n.347), kind=kOutput, calls=%fused_computation.41 | convolution fusion | flops 100663296 | bytes 1114116 | tf_op jit(solution)/shard_map/dot_general | solution.py:238
  120.6 0.7 select_reduce_fusion.3
  (152 shorter events, 9.6 us)
Async XLA Ops:
  0.6 53.6 %copy-start = (bf16[1024,1024]{1,0:T(8,128)(2,1)S(1)}, bf16[1024,1024]{1,0:T(8,128)(2,1)}, u32[]{:S(2)}) copy-start(bf16[1024,1024]{1,0:T(8,128)(2,1)} %param.13) | copy-start | bytes 6291460
  3.7 13.7 %collective-permute-start.2 = (bf16[97,256]{1,0:T(8,128)(2,1)S(1)}, bf16[97,256]{1,0:T(8,128)(2,1)S(1)}, u32[]{:S(2)}, u32[]{:S(2)}) collective-permute-start(bf16[97,256]{1,0:T(8,128)(2,1)S(1)} %constant_dynamic-update-slice_fusion), channel_id=1, source_target_pairs={{0,1},{1,2},{2,3},{3,0},{4,5},{5,6},{6,7},{7,4},{8,9},{9,10},{10,1... | collective-permute-start | bytes 149000 | tf_op jit(solution)/shard_map/ppermute | solution.py:105
  6.8 13.5 %collective-permute-start.1 = (bf16[97,256]{1,0:T(8,128)(2,1)S(1)}, bf16[97,256]{1,0:T(8,128)(2,1)S(1)}, u32[]{:S(2)}, u32[]{:S(2)}) collective-permute-start(bf16[97,256]{1,0:T(8,128)(2,1)S(1)} %constant_dynamic-update-slice_fusion), channel_id=1, source_target_pairs={{0,2},{1,3},{2,0},{3,1},{4,6},{5,7},{6,4},{7,5},{8,10},{9,11},{10,... | collective-permute-start | bytes 149000 | tf_op jit(solution)/shard_map/ppermute | solution.py:105
  9.4 10.9 %collective-permute-start = (bf16[97,256]{1,0:T(8,128)(2,1)S(1)}, bf16[97,256]{1,0:T(8,128)(2,1)S(1)}, u32[]{:S(2)}, u32[]{:S(2)}) collective-permute-start(bf16[97,256]{1,0:T(8,128)(2,1)S(1)} %constant_dynamic-update-slice_fusion), channel_id=1, source_target_pairs={{0,3},{1,0},{2,1},{3,2},{4,7},{5,4},{6,5},{7,6},{8,11},{9,8},{10,9... | collective-permute-start | bytes 149000 | tf_op jit(solution)/shard_map/ppermute | solution.py:105
  13.4 61.6 %copy-start.4 = (f32[4096]{0:T(1024)}, f32[4096]{0:T(1024)S(1)}, u32[]{:S(2)}) copy-start(f32[4096]{0:T(1024)S(1)} %convert_element_type.96) | copy-start | bytes 49156
  16.0 9.9 %collective-permute-start.12 = (f32[48,1024]{1,0:T(8,128)}, f32[48,1024]{1,0:T(8,128)S(1)}, u32[]{:S(2)}, u32[]{:S(2)}) collective-permute-start(f32[48,1024]{1,0:T(8,128)} %get-tuple-element.23), channel_id=1, source_target_pairs={{0,1},{1,2},{2,3},{3,0},{4,5},{5,6},{6,7},{7,4},{8,9},{9,10},{10,1... | collective-permute-start | bytes 589832 | tf_op jit(solution)/shard_map/ppermute | solution.py:121
  16.7 15.8 %collective-permute-start.11 = (f32[48,1024]{1,0:T(8,128)}, f32[48,1024]{1,0:T(8,128)S(1)}, u32[]{:S(2)}, u32[]{:S(2)}) collective-permute-start(f32[48,1024]{1,0:T(8,128)} %get-tuple-element.24), channel_id=1, source_target_pairs={{0,2},{1,3},{2,0},{3,1},{4,6},{5,7},{6,4},{7,5},{8,10},{9,11},{10,... | collective-permute-start | bytes 589832 | tf_op jit(solution)/shard_map/ppermute | solution.py:121
  17.1 31.7 %copy-start.15 = (pred[8]{0:T(512)(128)(4,1)}, pred[8]{0:T(512)(128)(4,1)S(1)}, u32[]{:S(2)}) copy-start(pred[8]{0:T(512)(128)(4,1)S(1)} %get-tuple-element.39) | copy-start | bytes 28
  17.1 31.7 %copy-start.17 = (pred[8]{0:T(512)(128)(4,1)}, pred[8]{0:T(512)(128)(4,1)S(1)}, u32[]{:S(2)}) copy-start(pred[8]{0:T(512)(128)(4,1)S(1)} %get-tuple-element.40) | copy-start | bytes 28
  17.1 31.7 %copy-start.19 = (pred[8]{0:T(512)(128)(4,1)}, pred[8]{0:T(512)(128)(4,1)S(1)}, u32[]{:S(2)}) copy-start(pred[8]{0:T(512)(128)(4,1)S(1)} %get-tuple-element.41) | copy-start | bytes 28
  17.1 31.7 %copy-start.21 = (pred[8]{0:T(512)(128)(4,1)}, pred[8]{0:T(512)(128)(4,1)S(1)}, u32[]{:S(2)}) copy-start(pred[8]{0:T(512)(128)(4,1)S(1)} %get-tuple-element.42) | copy-start | bytes 28
  17.1 31.6 %copy-start.23 = (pred[8]{0:T(512)(128)(4,1)}, pred[8]{0:T(512)(128)(4,1)S(1)}, u32[]{:S(2)}) copy-start(pred[8]{0:T(512)(128)(4,1)S(1)} %get-tuple-element.43) | copy-start | bytes 28
  17.1 31.6 %copy-start.25 = (pred[8]{0:T(512)(128)(4,1)}, pred[8]{0:T(512)(128)(4,1)S(1)}, u32[]{:S(2)}) copy-start(pred[8]{0:T(512)(128)(4,1)S(1)} %get-tuple-element.44) | copy-start | bytes 28
  17.2 31.6 %copy-start.27 = (pred[8]{0:T(512)(128)(4,1)}, pred[8]{0:T(512)(128)(4,1)S(1)}, u32[]{:S(2)}) copy-start(pred[8]{0:T(512)(128)(4,1)S(1)} %broadcast_compare_fusion.9) | copy-start | bytes 28
  17.2 31.6 %copy-start.12 = (pred[4]{0:T(512)(128)(4,1)}, pred[4]{0:T(512)(128)(4,1)S(1)}, u32[]{:S(2)}) copy-start(pred[4]{0:T(512)(128)(4,1)S(1)} %broadcast_compare_fusion.8) | copy-start | bytes 16
  17.4 16.6 %collective-permute-start.10 = (f32[48,1024]{1,0:T(8,128)S(1)}, f32[48,1024]{1,0:T(8,128)S(1)}, u32[]{:S(2)}, u32[]{:S(2)}) collective-permute-start(f32[48,1024]{1,0:T(8,128)S(1)} %get-tuple-element.21), channel_id=1, source_target_pairs={{0,3},{1,0},{2,1},{3,2},{4,7},{5,4},{6,5},{7,6},{8,11},{9,8},{10,9... | collective-permute-start | bytes 589832 | tf_op jit(solution)/shard_map/ppermute | solution.py:121
  20.5 14.3 %collective-permute-start.9 = (bf16[4,97,256]{2,0,1:T(4,128)(2,1)S(1)}, bf16[4,97,256]{2,0,1:T(4,128)(2,1)S(1)}, u32[]{:S(2)}, u32[]{:S(2)}) collective-permute-start(bf16[4,97,256]{2,0,1:T(4,128)(2,1)S(1)} %select_select_fusion.3), channel_id=1, source_target_pairs={{0,4},{4,8},{8,12},{12,16},{16,20},{20,24},{24,28},{28,0},{1,5},{5... | collective-permute-start | bytes 595976 | tf_op jit(solution)/shard_map/ppermute | solution.py:105
  20.6 15.8 %collective-permute-start.8 = (bf16[4,97,256]{2,0,1:T(4,128)(2,1)S(1)}, bf16[4,97,256]{2,0,1:T(4,128)(2,1)S(1)}, u32[]{:S(2)}, u32[]{:S(2)}) collective-permute-start(bf16[4,97,256]{2,0,1:T(4,128)(2,1)S(1)} %select_select_fusion.3), channel_id=1, source_target_pairs={{0,8},{4,12},{8,16},{12,20},{16,24},{20,28},{24,0},{28,4},{1,9},{5... | collective-permute-start | bytes 595976 | tf_op jit(solution)/shard_map/ppermute | solution.py:105
  22.3 26.5 %copy-start.29 = (f32[48]{0:T(128)}, f32[48]{0:T(128)S(1)}, u32[]{:S(2)}) copy-start(f32[48]{0:T(128)S(1)} %convert_reduce_fusion) | copy-start | bytes 580
  26.0 12.9 %collective-permute-start.7 = (bf16[4,97,256]{2,0,1:T(4,128)(2,1)S(1)}, bf16[4,97,256]{2,0,1:T(4,128)(2,1)S(1)}, u32[]{:S(2)}, u32[]{:S(2)}) collective-permute-start(bf16[4,97,256]{2,0,1:T(4,128)(2,1)S(1)} %select_select_fusion.3), channel_id=1, source_target_pairs={{0,12},{4,16},{8,20},{12,24},{16,28},{20,0},{24,4},{28,8},{1,13},{... | collective-permute-start | bytes 595976 | tf_op jit(solution)/shard_map/ppermute | solution.py:105
  32.5 9.1 %collective-permute-start.6 = (bf16[4,97,256]{2,0,1:T(4,128)(2,1)S(1)}, bf16[4,97,256]{2,0,1:T(4,128)(2,1)S(1)}, u32[]{:S(2)}, u32[]{:S(2)}) collective-permute-start(bf16[4,97,256]{2,0,1:T(4,128)(2,1)S(1)} %select_select_fusion.3), channel_id=1, source_target_pairs={{0,16},{4,20},{8,24},{12,28},{16,0},{20,4},{24,8},{28,12},{1,17},{... | collective-permute-start | bytes 595976 | tf_op jit(solution)/shard_map/ppermute | solution.py:105
  34.0 9.1 %collective-permute-start.5 = (bf16[4,97,256]{2,0,1:T(4,128)(2,1)S(1)}, bf16[4,97,256]{2,0,1:T(4,128)(2,1)S(1)}, u32[]{:S(2)}, u32[]{:S(2)}) collective-permute-start(bf16[4,97,256]{2,0,1:T(4,128)(2,1)S(1)} %select_select_fusion.3), channel_id=1, source_target_pairs={{0,20},{4,24},{8,28},{12,0},{16,4},{20,8},{24,12},{28,16},{1,21},{... | collective-permute-start | bytes 595976 | tf_op jit(solution)/shard_map/ppermute | solution.py:105
  34.8 9.2 %collective-permute-start.4 = (bf16[4,97,256]{2,0,1:T(4,128)(2,1)S(1)}, bf16[4,97,256]{2,0,1:T(4,128)(2,1)S(1)}, u32[]{:S(2)}, u32[]{:S(2)}) collective-permute-start(bf16[4,97,256]{2,0,1:T(4,128)(2,1)S(1)} %select_select_fusion.3), channel_id=1, source_target_pairs={{0,24},{4,28},{8,0},{12,4},{16,8},{20,12},{24,16},{28,20},{1,25},{... | collective-permute-start | bytes 595976 | tf_op jit(solution)/shard_map/ppermute | solution.py:105
  36.3 8.2 %collective-permute-start.3 = (bf16[4,97,256]{2,0,1:T(4,128)(2,1)S(1)}, bf16[4,97,256]{2,0,1:T(4,128)(2,1)S(1)}, u32[]{:S(2)}, u32[]{:S(2)}) collective-permute-start(bf16[4,97,256]{2,0,1:T(4,128)(2,1)S(1)} %select_select_fusion.3), channel_id=1, source_target_pairs={{0,28},{4,0},{8,4},{12,8},{16,12},{20,16},{24,20},{28,24},{1,29},{... | collective-permute-start | bytes 595976 | tf_op jit(solution)/shard_map/ppermute | solution.py:105
  38.9 40.3 %collective-permute-start.15 = (bf16[48,1024]{1,0:T(8,128)(2,1)S(1)}, bf16[48,1024]{1,0:T(8,128)(2,1)}, u32[]{:S(2)}, u32[]{:S(2)}) collective-permute-start(bf16[48,1024]{1,0:T(8,128)(2,1)S(1)} %divide_convert_fusion), channel_id=1, source_target_pairs={{0,1},{1,2},{2,3},{3,0},{4,5},{5,6},{6,7},{7,4},{8,9},{9,10},{10,1... | collective-permute-start | bytes 294920 | tf_op jit(solution)/shard_map/ppermute | solution.py:105
  41.5 37.6 %collective-permute-start.14 = (bf16[48,1024]{1,0:T(8,128)(2,1)S(1)}, bf16[48,1024]{1,0:T(8,128)(2,1)}, u32[]{:S(2)}, u32[]{:S(2)}) collective-permute-start(bf16[48,1024]{1,0:T(8,128)(2,1)S(1)} %divide_convert_fusion), channel_id=1, source_target_pairs={{0,2},{1,3},{2,0},{3,1},{4,6},{5,7},{6,4},{7,5},{8,10},{9,11},{10,... | collective-permute-start | bytes 294920 | tf_op jit(solution)/shard_map/ppermute | solution.py:105
  43.1 36.1 %collective-permute-start.13 = (bf16[48,1024]{1,0:T(8,128)(2,1)S(1)}, bf16[48,1024]{1,0:T(8,128)(2,1)}, u32[]{:S(2)}, u32[]{:S(2)}) collective-permute-start(bf16[48,1024]{1,0:T(8,128)(2,1)S(1)} %divide_convert_fusion), channel_id=1, source_target_pairs={{0,3},{1,0},{2,1},{3,2},{4,7},{5,4},{6,5},{7,6},{8,11},{9,8},{10,9... | collective-permute-start | bytes 294920 | tf_op jit(solution)/shard_map/ppermute | solution.py:105
  54.2 24.4 %copy-start.2 = (f32[384,1024]{1,0:T(8,128)}, f32[384,1024]{1,0:T(8,128)S(1)}, u32[]{:S(2)}) copy-start(f32[384,1024]{1,0:T(8,128)S(1)} %convolution_multiply_fusion) | copy-start | bytes 4718596
  54.3 20.8 %copy-start.1 = (bf16[128,4096]{1,0:T(8,128)(2,1)S(1)}, bf16[128,4096]{1,0:T(8,128)(2,1)}, u32[]{:S(2)}) copy-start(bf16[128,4096]{1,0:T(8,128)(2,1)} %param.10) | copy-start | bytes 3145732
  54.3 20.8 %copy-start.30 = (f32[48]{0:T(128)S(1)}, f32[48]{0:T(128)}, u32[]{:S(2)}) copy-start(f32[48]{0:T(128)} %copy-done.29) | copy-start | bytes 580
  54.3 20.8 %copy-start.33 = (f32[128]{0:T(128)S(1)}, f32[128]{0:T(128)}, u32[]{:S(2)}) copy-start(f32[128]{0:T(128)} %copy-done.32) | copy-start | bytes 1540
  54.3 20.8 %copy-start.36 = (s32[1,128]{1,0:T(1,128)S(1)}, s32[1,128]{1,0:T(1,128)}, u32[]{:S(2)}) copy-start(s32[1,128]{1,0:T(1,128)} %param.11) | copy-start | bytes 1540
  89.5 15.3 %collective-permute-start.22 = (f32[28672]{0:T(1024)}, f32[28672]{0:T(1024)}, u32[]{:S(2)}, u32[]{:S(2)}) collective-permute-start(f32[28672]{0:T(1024)} %get-tuple-element.31), channel_id=1, source_target_pairs={{0,4},{4,8},{8,12},{12,16},{16,20},{20,24},{24,28},{28,0},{1,5},{5... | collective-permute-start | bytes 344072 | tf_op jit(solution)/shard_map/ppermute | solution.py:134
  89.5 16.4 %collective-permute-start.21 = (f32[28672]{0:T(1024)}, f32[28672]{0:T(1024)}, u32[]{:S(2)}, u32[]{:S(2)}) collective-permute-start(f32[28672]{0:T(1024)} %get-tuple-element.30), channel_id=1, source_target_pairs={{0,8},{4,12},{8,16},{12,20},{16,24},{20,28},{24,0},{28,4},{1,9},{5... | collective-permute-start | bytes 344072 | tf_op jit(solution)/shard_map/ppermute | solution.py:134
  98.0 20.1 %copy-start.24 = (pred[8]{0:T(512)(128)(4,1)S(1)}, pred[8]{0:T(512)(128)(4,1)}, u32[]{:S(2)}) copy-start(pred[8]{0:T(512)(128)(4,1)} %copy-done.23) | copy-start | bytes 28
  98.0 20.1 %copy-start.26 = (pred[8]{0:T(512)(128)(4,1)S(1)}, pred[8]{0:T(512)(128)(4,1)}, u32[]{:S(2)}) copy-start(pred[8]{0:T(512)(128)(4,1)} %copy-done.25) | copy-start | bytes 28
  98.0 20.1 %copy-start.28 = (pred[8]{0:T(512)(128)(4,1)S(1)}, pred[8]{0:T(512)(128)(4,1)}, u32[]{:S(2)}) copy-start(pred[8]{0:T(512)(128)(4,1)} %copy-done.27) | copy-start | bytes 28
  100.1 20.4 %copy-start.8 = (pred[4]{0:T(512)(128)(4,1)S(1)}, pred[4]{0:T(512)(128)(4,1)}, u32[]{:S(2)}) copy-start(pred[4]{0:T(512)(128)(4,1)} %copy-done.6) | copy-start | bytes 16
  100.1 20.4 %copy-start.11 = (pred[4]{0:T(512)(128)(4,1)S(1)}, pred[4]{0:T(512)(128)(4,1)}, u32[]{:S(2)}) copy-start(pred[4]{0:T(512)(128)(4,1)} %copy-done.9) | copy-start | bytes 16
  100.1 20.4 %copy-start.14 = (pred[4]{0:T(512)(128)(4,1)S(1)}, pred[4]{0:T(512)(128)(4,1)}, u32[]{:S(2)}) copy-start(pred[4]{0:T(512)(128)(4,1)} %copy-done.12) | copy-start | bytes 16
  101.9 8.2 %collective-permute-start.20 = (f32[28672]{0:T(1024)}, f32[28672]{0:T(1024)S(1)}, u32[]{:S(2)}, u32[]{:S(2)}) collective-permute-start(f32[28672]{0:T(1024)} %get-tuple-element.29), channel_id=1, source_target_pairs={{0,12},{4,16},{8,20},{12,24},{16,28},{20,0},{24,4},{28,8},{1,13},{... | collective-permute-start | bytes 344072 | tf_op jit(solution)/shard_map/ppermute | solution.py:134
  103.5 6.6 %collective-permute-start.19 = (f32[28672]{0:T(1024)}, f32[28672]{0:T(1024)S(1)}, u32[]{:S(2)}, u32[]{:S(2)}) collective-permute-start(f32[28672]{0:T(1024)} %get-tuple-element.28), channel_id=1, source_target_pairs={{0,16},{4,20},{8,24},{12,28},{16,0},{20,4},{24,8},{28,12},{1,17},{... | collective-permute-start | bytes 344072 | tf_op jit(solution)/shard_map/ppermute | solution.py:134
  104.8 5.4 %collective-permute-start.18 = (f32[28672]{0:T(1024)}, f32[28672]{0:T(1024)S(1)}, u32[]{:S(2)}, u32[]{:S(2)}) collective-permute-start(f32[28672]{0:T(1024)} %get-tuple-element.27), channel_id=1, source_target_pairs={{0,20},{4,24},{8,28},{12,0},{16,4},{20,8},{24,12},{28,16},{1,21},{... | collective-permute-start | bytes 344072 | tf_op jit(solution)/shard_map/ppermute | solution.py:134
  104.8 6.2 %collective-permute-start.17 = (f32[28672]{0:T(1024)}, f32[28672]{0:T(1024)S(1)}, u32[]{:S(2)}, u32[]{:S(2)}) collective-permute-start(f32[28672]{0:T(1024)} %get-tuple-element.26), channel_id=1, source_target_pairs={{0,24},{4,28},{8,0},{12,4},{16,8},{20,12},{24,16},{28,20},{1,25},{... | collective-permute-start | bytes 344072 | tf_op jit(solution)/shard_map/ppermute | solution.py:134
  106.0 5.0 %collective-permute-start.16 = (f32[28672]{0:T(1024)S(1)}, f32[28672]{0:T(1024)S(1)}, u32[]{:S(2)}, u32[]{:S(2)}) collective-permute-start(f32[28672]{0:T(1024)S(1)} %get-tuple-element.25), channel_id=1, source_target_pairs={{0,28},{4,0},{8,4},{12,8},{16,12},{20,16},{24,20},{28,24},{1,29},{... | collective-permute-start | bytes 344072 | tf_op jit(solution)/shard_map/ppermute | solution.py:134
  111.9 8.7 %collective-permute-start.25 = (f32[4096]{0:T(1024)S(1)}, f32[4096]{0:T(1024)S(1)}, u32[]{:S(2)}, u32[]{:S(2)}) collective-permute-start(f32[4096]{0:T(1024)S(1)} %select_reduce_fusion.2), channel_id=1, source_target_pairs={{0,1},{1,2},{2,3},{3,0},{4,5},{5,6},{6,7},{7,4},{8,9},{9,10},{10,1... | collective-permute-start | bytes 49160 | tf_op jit(solution)/shard_map/ppermute | solution.py:105
  111.9 8.6 %collective-permute-start.24 = (f32[4096]{0:T(1024)S(1)}, f32[4096]{0:T(1024)S(1)}, u32[]{:S(2)}, u32[]{:S(2)}) collective-permute-start(f32[4096]{0:T(1024)S(1)} %select_reduce_fusion.2), channel_id=1, source_target_pairs={{0,2},{1,3},{2,0},{3,1},{4,6},{5,7},{6,4},{7,5},{8,10},{9,11},{10,... | collective-permute-start | bytes 49160 | tf_op jit(solution)/shard_map/ppermute | solution.py:105
  114.4 6.1 %collective-permute-start.23 = (f32[4096]{0:T(1024)S(1)}, f32[4096]{0:T(1024)S(1)}, u32[]{:S(2)}, u32[]{:S(2)}) collective-permute-start(f32[4096]{0:T(1024)S(1)} %select_reduce_fusion.2), channel_id=1, source_target_pairs={{0,3},{1,0},{2,1},{3,2},{4,7},{5,4},{6,5},{7,6},{8,11},{9,8},{10,9... | collective-permute-start | bytes 49160 | tf_op jit(solution)/shard_map/ppermute | solution.py:105
  (15 other events, 196.8 us)

commit v20 on v14

--- a/solution.py
+++ b/solution.py
@@ -158,7 +158,7 @@
     packed = jnp.concatenate(
         [query_cache, region_cache, extra.reshape(extra_rows, width).astype(jnp.bfloat16)], axis=0
     )
-    group_blocks = gather_blocks(packed, "fsdp")
+    group_blocks = lax.optimization_barrier(gather_blocks(packed, "fsdp"))
     group_side = group_blocks[:, 2 * rows :].reshape(feature_count, extra_rows * width)
     group_ids = group_side[:, 2 * rows : 2 * rows + tokens].reshape(feature_count * tokens)
     group_ids = group_ids.astype(jnp.int32)
@@ -177,7 +177,7 @@
     mean_blocks = lax.optimization_barrier(gather_blocks(mean_chunk, "fsdp"))
     mean_pooled = mean_blocks.transpose(1, 0, 2).reshape(rows, model_width)
 
-    gathered = gather_blocks(group_blocks, "dp")
+    gathered = lax.optimization_barrier(gather_blocks(group_blocks, "dp"))
     mean_pooled, gathered = lax.optimization_barrier((mean_pooled, gathered))
     slice_width = model_width // data_count
     pieces = mean_pooled.reshape(rows, data_count, slice_width).transpose(1, 0, 2)

time: 110 us -> 110 us (level)
  no operation moved by 1% of the time
where the time goes in v20:
time: 110 us; the launch traced here: 109 us
  starting transfers between devices  41.7 us (38%)
  blocking collectives  19 us (17%)
  other arithmetic  15 us (14%)
  waiting for transfers between devices  11 us (10%)
  matrix products  10.3 us (9%)
  local copies, waits for them, and re-layouts  8.89 us (8%)
  between operations  3.2 us (3%)
    ppermute x16, starting transfers between devices, gather_blocks(): lax.ppermute(x, axis, [(i, (i + s) % n) for i in range(n)])  23.1 us
    all_gather x1, blocking collectives, local_small(): mean_grad = lax.all_gather(mean_part, 'fsdp', axis=1, tiled=True)  19 us
    ppermute x7, starting transfers between devices, spread_with_sum(): arrived = lax.ppermute(payload, axis, [(i, (i + s) % n) for i in range(n)])  14.7 us
    ppermute x3, waiting for transfers between devices, scatter_sum(): lax.ppermute(piece, axis, [(i, (i + s) % n) for i in range(n)])  9.34 us
    select_n x4, other arithmetic, arrange(): out = jnp.where(source == s, copies[s][None], out)  6.1 us
    unnamed x51, local copies, waits for them, and re-layouts  3.91 us
    ppermute x3, starting transfers between devices, scatter_sum(): lax.ppermute(piece, axis, [(i, (i + s) % n) for i in range(n)])  3.88 us
  transfers between devices with their start and end apart: 26, of which 5 were waited for; matrix products, arithmetic and copies ran while one was open for 18% of the time, Pallas kernels for 0%

profile of v20, /device:TPU:0, one launch (start us, length us, event | category | flops | bytes accessed | tf_op | source)
XLA Modules:
  0.0 109.1 jit_solution(16302946568854262447)
XLA Ops:
  0.6 0.9 constant_dynamic-update-slice_fusion.2
  1.5 0.7 and_select_fusion.2
  2.2 0.7 constant_dynamic-update-slice_fusion.1
  2.9 0.7 fusion.28
  3.7 3.1 %collective-permute-start.5 = (bf16[97,256]{1,0:T(8,128)(2,1)S(1)}, bf16[97,256]{1,0:T(8,128)(2,1)}, u32[]{:S(2)}, u32[]{:S(2)}) collective-permute-start(bf16[97,256]{1,0:T(8,128)(2,1)S(1)} %constant_dynamic-update-slice_fusion), channel_id=1, source_target_pairs={{0,1},{1,2},{2,3},{3,0},{4,5},{5,6},{6,7},{7,4},{8,9},{9,10},{10,1... | collective-permute-start | bytes 149000 | tf_op jit(solution)/shard_map/ppermute | solution.py:105
  6.8 2.6 %collective-permute-start.4 = (bf16[97,256]{1,0:T(8,128)(2,1)S(1)}, bf16[97,256]{1,0:T(8,128)(2,1)}, u32[]{:S(2)}, u32[]{:S(2)}) collective-permute-start(bf16[97,256]{1,0:T(8,128)(2,1)S(1)} %constant_dynamic-update-slice_fusion), channel_id=1, source_target_pairs={{0,2},{1,3},{2,0},{3,1},{4,6},{5,7},{6,4},{7,5},{8,10},{9,11},{10,... | collective-permute-start | bytes 149000 | tf_op jit(solution)/shard_map/ppermute | solution.py:105
  9.4 1.3 %collective-permute-start.3 = (bf16[97,256]{1,0:T(8,128)(2,1)S(1)}, bf16[97,256]{1,0:T(8,128)(2,1)}, u32[]{:S(2)}, u32[]{:S(2)}) collective-permute-start(bf16[97,256]{1,0:T(8,128)(2,1)S(1)} %constant_dynamic-update-slice_fusion), channel_id=1, source_target_pairs={{0,3},{1,0},{2,1},{3,2},{4,7},{5,4},{6,5},{7,6},{8,11},{9,8},{10,9... | collective-permute-start | bytes 149000 | tf_op jit(solution)/shard_map/ppermute | solution.py:105
  10.7 0.7 convert_element_type.85
  11.4 1.5 %fusion = f32[128]{0:T(128)S(1)} fusion(bf16[128,4096]{1,0:T(8,128)(2,1)} %param.10), kind=kLoop, calls=%fused_computation.5 | loop fusion | flops 1572736 | bytes 1049088 | tf_op jit(solution)/shard_map/reduce_sum | solution.py:168
  13.4 1.7 %fusion.9 = f32[48,4096]{1,0:T(8,128)S(1)} fusion(bf16[128,4096]{1,0:T(8,128)(2,1)} %param.10, f32[4096]{0:T(1024)S(1)} %convert_element_type.85, f32[128]{0:T(128)S(1)} %get-tuple-element.37, s32[128]{0:T(128)} %bitcast.62), kind=kOutput, calls=%fused_computation.18 | convolution fusion | flops 52434944 | bytes 1852416 | tf_op jit(solution)/shard_map/dot_general | solution.py:172
  15.2 0.8 constant_dynamic-slice_fusion.11
  16.0 0.7 collective-permute-start.2
  17.3 2.9 %collective-permute-start = (f32[48,1024]{1,0:T(8,128)S(1)}, f32[48,1024]{1,0:T(8,128)S(1)}, u32[]{:S(2)}, u32[]{:S(2)}) collective-permute-start(f32[48,1024]{1,0:T(8,128)S(1)} %get-tuple-element.25), channel_id=1, source_target_pairs={{0,3},{1,0},{2,1},{3,2},{4,7},{5,4},{6,5},{7,6},{8,11},{9,8},{10,9... | collective-permute-start | bytes 589832 | tf_op jit(solution)/shard_map/ppermute | solution.py:121
  20.1 1.1 %select_select_fusion.3 = bf16[4,97,256]{2,0,1:T(4,128)(2,1)S(1)} fusion(pred[4]{0:T(512)(128)(4,1)S(1)} %get-tuple-element.50, pred[4]{0:T(512)(128)(4,1)S(1)} %broadcast_compare_fusion.9, pred[4]{0:T(512)(128)(4,1)S(1)} %get-tuple-element.49, bf16[97,256]{1,0:T(8,128)(2,1)S(1)} %constant_dynamic-update-slice_fusion, ...), kind=kLoop, calls=%fused_computation.39 | loop fusion | flops 297984 | bytes 397324 | tf_op jit(solution)/shard_map/jit(_where)/select_n | solution.py:98
  21.3 1.5 %collective-permute-start.14 = (bf16[4,97,256]{2,0,1:T(4,128)(2,1)S(1)}, bf16[4,97,256]{2,0,1:T(4,128)(2,1)S(1)}, u32[]{:S(2)}, u32[]{:S(2)}) collective-permute-start(bf16[4,97,256]{2,0,1:T(4,128)(2,1)S(1)} %select_select_fusion.3), channel_id=1, source_target_pairs={{0,8},{4,12},{8,16},{12,20},{16,24},{20,28},{24,0},{28,4},{1,9},{5... | collective-permute-start | bytes 595976 | tf_op jit(solution)/shard_map/ppermute | solution.py:105
  23.1 2.8 %collective-permute-done.2 = f32[48,1024]{1,0:T(8,128)S(1)} collective-permute-done((f32[48,1024]{1,0:T(8,128)}, f32[48,1024]{1,0:T(8,128)S(1)}, u32[]{:S(2)}, u32[]{:S(2)}) %collective-permute-start.2) | collective-permute-done | bytes 196640 | tf_op jit(solution)/shard_map/ppermute | solution.py:121
  25.9 6.5 %collective-permute-done.1 = f32[48,1024]{1,0:T(8,128)S(1)} collective-permute-done((f32[48,1024]{1,0:T(8,128)S(1)}, f32[48,1024]{1,0:T(8,128)S(1)}, u32[]{:S(2)}, u32[]{:S(2)}) %collective-permute-start.1) | collective-permute-done | bytes 196640 | tf_op jit(solution)/shard_map/ppermute | solution.py:121
  32.4 1.5 %collective-permute-start.12 = (bf16[4,97,256]{2,0,1:T(4,128)(2,1)S(1)}, bf16[4,97,256]{2,0,1:T(4,128)(2,1)S(1)}, u32[]{:S(2)}, u32[]{:S(2)}) collective-permute-start(bf16[4,97,256]{2,0,1:T(4,128)(2,1)S(1)} %select_select_fusion.3), channel_id=1, source_target_pairs={{0,16},{4,20},{8,24},{12,28},{16,0},{20,4},{24,8},{28,12},{1,17},{... | collective-permute-start | bytes 595976 | tf_op jit(solution)/shard_map/ppermute | solution.py:105
  33.9 0.8 select_reduce_fusion
  34.8 1.5 %collective-permute-start.10 = (bf16[4,97,256]{2,0,1:T(4,128)(2,1)S(1)}, bf16[4,97,256]{2,0,1:T(4,128)(2,1)S(1)}, u32[]{:S(2)}, u32[]{:S(2)}) collective-permute-start(bf16[4,97,256]{2,0,1:T(4,128)(2,1)S(1)} %select_select_fusion.3), channel_id=1, source_target_pairs={{0,24},{4,28},{8,0},{12,4},{16,8},{20,12},{24,16},{28,20},{1,25},{... | collective-permute-start | bytes 595976 | tf_op jit(solution)/shard_map/ppermute | solution.py:105
  36.2 2.4 %collective-permute-start.9 = (bf16[4,97,256]{2,0,1:T(4,128)(2,1)S(1)}, bf16[4,97,256]{2,0,1:T(4,128)(2,1)S(1)}, u32[]{:S(2)}, u32[]{:S(2)}) collective-permute-start(bf16[4,97,256]{2,0,1:T(4,128)(2,1)S(1)} %select_select_fusion.3), channel_id=1, source_target_pairs={{0,28},{4,0},{8,4},{12,8},{16,12},{20,16},{24,20},{28,24},{1,29},{... | collective-permute-start | bytes 595976 | tf_op jit(solution)/shard_map/ppermute | solution.py:105
  38.8 2.4 %collective-permute-start.8 = (bf16[48,1024]{1,0:T(8,128)(2,1)S(1)}, bf16[48,1024]{1,0:T(8,128)(2,1)S(1)}, u32[]{:S(2)}, u32[]{:S(2)}) collective-permute-start(bf16[48,1024]{1,0:T(8,128)(2,1)S(1)} %divide_convert_fusion), channel_id=1, source_target_pairs={{0,1},{1,2},{2,3},{3,0},{4,5},{5,6},{6,7},{7,4},{8,9},{9,10},{10,1... | collective-permute-start | bytes 294920 | tf_op jit(solution)/shard_map/ppermute | solution.py:105
  41.2 1.8 %collective-permute-start.7 = (bf16[48,1024]{1,0:T(8,128)(2,1)S(1)}, bf16[48,1024]{1,0:T(8,128)(2,1)S(1)}, u32[]{:S(2)}, u32[]{:S(2)}) collective-permute-start(bf16[48,1024]{1,0:T(8,128)(2,1)S(1)} %divide_convert_fusion), channel_id=1, source_target_pairs={{0,2},{1,3},{2,0},{3,1},{4,6},{5,7},{6,4},{7,5},{8,10},{9,11},{10,... | collective-permute-start | bytes 294920 | tf_op jit(solution)/shard_map/ppermute | solution.py:105
  43.0 1.0 collective-permute-start.6
  44.4 4.2 %select_select_fusion = bf16[8,4,97,256]{3,1,2,0:T(4,128)(2,1)S(1)} fusion(pred[8]{0:T(512)(128)(4,1)S(1)} %get-tuple-element.44, pred[8]{0:T(512)(128)(4,1)S(1)} %get-tuple-element.45, pred[8]{0:T(512)(128)(4,1)S(1)} %get-tuple-element.46, pred[8]{0:T(512)(128)(4,1)S(1)} %get-tuple-element.47, pred[8]{0:T(512)(128)(4,1)S(1)} %get-tuple-element.48, ...), kind=kLoop, calls=%fused_computation.14 | loop fusion | flops 5562368 | bytes 3178552 | tf_op jit(solution)/shard_map/jit(_where)/select_n | solution.py:98
  49.2 0.7 collective-permute-done.6
  50.6 0.7 fusion.31
  51.3 1.1 copy.15
  52.7 1.7 %fusion.32 = (f32[384]{0:T(512)S(1)}, f32[384,384]{0,1:T(8,128)S(1)}) fusion(bf16[384,1024]{1,0:T(8,128)(2,1)} %bitcast.51, bf16[384,1024]{1,0:T(8,128)(2,1)S(1)} %bitcast.46), kind=kOutput, calls=%fused_computation.111 | convolution fusion | flops 302284416 | bytes 2164224 | tf_op jit(solution)/shard_map/dot_general | solution.py:195
  54.6 0.6 subtract_reduce_fusion
  55.4 0.7 copy-done.3
  56.8 0.7 fusion.18
  57.5 19.0 %all_gather.3 = f32[48,4096]{1,0:T(8,128)S(1)} all-gather(f32[48,1024]{1,0:T(8,128)S(1)} %fusion.18), channel_id=1, replica_groups=mesh['dp'=8,'fsdp'=4] {'fsdp'}, dimensions={1}, use_global_device_ids=true | all-gather | bytes 983040 | tf_op jit(solution)/shard_map/all_gather | solution.py:222
  76.5 1.6 %fusion.8 = (f32[4096]{0:T(1024)S(1)}, f32[128]{0:T(128)S(1)}, f32[128,4096]{1,0:T(8,128)S(1)}) fusion(bf16[128,4096]{1,0:T(8,128)(2,1)S(1)} %copy-done.1, f32[128]{0:T(128)S(1)} %copy-done.20, f32[4096]{0:T(1024)S(1)} %convert_element_type.85, f32[48,4096]{1,0:T(8,128)S(1)} %all_gather.3, f32[48]{0:T(128)S(1)} %convert_reduce_fusion, s32[128]{0:T(128)S(1)} %bitcast.63), kind=kOutput, calls=%fused_computation.13 | convolution fusion | flops 305858432 | bytes 3966656 | tf_op jit(solution)/shard_map/dot_general | solution.py:224
  78.3 0.7 constant_dynamic-slice_fusion.7
  79.2 8.1 %collective-permute-start.21 = (f32[28672]{0:T(1024)S(1)}, f32[28672]{0:T(1024)S(1)}, u32[]{:S(2)}, u32[]{:S(2)}) collective-permute-start(f32[28672]{0:T(1024)S(1)} %get-tuple-element.34), channel_id=1, source_target_pairs={{0,8},{4,12},{8,16},{12,20},{16,24},{20,28},{24,0},{28,4},{1,9},{5... | collective-permute-start | bytes 344072 | tf_op jit(solution)/shard_map/ppermute | solution.py:134
  87.2 2.7 %collective-permute-start.20 = (f32[28672]{0:T(1024)S(1)}, f32[28672]{0:T(1024)S(1)}, u32[]{:S(2)}, u32[]{:S(2)}) collective-permute-start(f32[28672]{0:T(1024)S(1)} %get-tuple-element.33), channel_id=1, source_target_pairs={{0,12},{4,16},{8,20},{12,24},{16,28},{20,0},{24,4},{28,8},{1,13},{... | collective-permute-start | bytes 344072 | tf_op jit(solution)/shard_map/ppermute | solution.py:134
  90.6 1.6 %fusion.5 = bf16[128,4096]{1,0:T(8,128)(2,1)} fusion(bf16[128,4096]{1,0:T(8,128)(2,1)S(1)} %copy-done.1, f32[128,4096]{1,0:T(8,128)S(1)} %get-tuple-element.42, f32[128]{0:T(128)S(1)} %broadcast_multiply_fusion, f32[128]{0:T(128)S(1)} %copy-done.18, f32[4096]{0:T(1024)S(1)} %convert_element_type.85, f32[128]{0:T(128)S(1)} %copy-done.20), kind=kLoop, calls=%fused_computation.10 | loop fusion | flops 3670016 | bytes 4212224 | tf_op jit(solution)/shard_map/convert_element_type | solution.py:234
  92.2 1.2 %collective-permute-start.17 = (f32[28672]{0:T(1024)S(1)}, f32[28672]{0:T(1024)S(1)}, u32[]{:S(2)}, u32[]{:S(2)}) collective-permute-start(f32[28672]{0:T(1024)S(1)} %get-tuple-element.30), channel_id=1, source_target_pairs={{0,24},{4,28},{8,0},{12,4},{16,8},{20,12},{24,16},{28,20},{1,25},{... | collective-permute-start | bytes 344072 | tf_op jit(solution)/shard_map/ppermute | solution.py:134
  93.4 2.1 %collective-permute-start.16 = (f32[28672]{0:T(1024)S(1)}, f32[28672]{0:T(1024)}, u32[]{:S(2)}, u32[]{:S(2)}) collective-permute-start(f32[28672]{0:T(1024)S(1)} %get-tuple-element.29), channel_id=1, source_target_pairs={{0,28},{4,0},{8,4},{12,8},{16,12},{20,16},{24,20},{28,24},{1,29},{... | collective-permute-start | bytes 344072 | tf_op jit(solution)/shard_map/ppermute | solution.py:134
  95.6 0.6 dynamic_slice.40
  96.9 1.7 %convolution_multiply_fusion.2 = f32[48,256]{1,0:T(8,128)} fusion(bf16[384,1024]{1,0:T(8,128)(2,1)} %bitcast.52, s32[]{:T(128)S(6)} %select_n.348, bf16[384,384]{0,1:T(8,128)(2,1)} %copy-done.3, s32[]{:T(128)S(6)} %select_n.347), kind=kOutput, calls=%fused_computation.17 | convolution fusion | flops 9449472 | bytes 282632 | tf_op jit(solution)/shard_map/dot_general | solution.py:215
  98.7 0.7 slice.151
  99.7 2.3 %collective-permute-start.24 = (f32[4096]{0:T(1024)S(1)}, f32[4096]{0:T(1024)S(1)}, u32[]{:S(2)}, u32[]{:S(2)}) collective-permute-start(f32[4096]{0:T(1024)S(1)} %select_reduce_fusion.2), channel_id=1, source_target_pairs={{0,2},{1,3},{2,0},{3,1},{4,6},{5,7},{6,4},{7,5},{8,10},{9,11},{10,... | collective-permute-start | bytes 49160 | tf_op jit(solution)/shard_map/ppermute | solution.py:105
  102.0 1.6 %collective-permute-start.23 = (f32[4096]{0:T(1024)S(1)}, f32[4096]{0:T(1024)S(1)}, u32[]{:S(2)}, u32[]{:S(2)}) collective-permute-start(f32[4096]{0:T(1024)S(1)} %select_reduce_fusion.2), channel_id=1, source_target_pairs={{0,3},{1,0},{2,1},{3,2},{4,7},{5,4},{6,5},{7,6},{8,11},{9,8},{10,9... | collective-permute-start | bytes 49160 | tf_op jit(solution)/shard_map/ppermute | solution.py:105
  103.9 0.9 slice.158
  105.1 2.1 %fusion.16 = f32[512,256]{1,0:T(8,128)} fusion(bf16[384,512]{1,0:T(8,128)(2,1)S(1)} %bitcast.50, f32[384,1024]{1,0:T(8,128)} %copy-done.2, s32[]{:T(128)S(6)} %select_n.348), kind=kOutput, calls=%fused_computation.40 | convolution fusion | flops 100663296 | bytes 1114116 | tf_op jit(solution)/shard_map/dot_general | solution.py:238
  107.2 0.7 select_reduce_fusion.3
  (122 shorter events, 6.0 us)
Async XLA Ops:
  0.6 56.1 %copy-start = (bf16[1024,1024]{1,0:T(8,128)(2,1)S(1)}, bf16[1024,1024]{1,0:T(8,128)(2,1)}, u32[]{:S(2)}) copy-start(bf16[1024,1024]{1,0:T(8,128)(2,1)} %param.13) | copy-start | bytes 6291460
  3.7 13.6 %collective-permute-start.5 = (bf16[97,256]{1,0:T(8,128)(2,1)S(1)}, bf16[97,256]{1,0:T(8,128)(2,1)}, u32[]{:S(2)}, u32[]{:S(2)}) collective-permute-start(bf16[97,256]{1,0:T(8,128)(2,1)S(1)} %constant_dynamic-update-slice_fusion), channel_id=1, source_target_pairs={{0,1},{1,2},{2,3},{3,0},{4,5},{5,6},{6,7},{7,4},{8,9},{9,10},{10,1... | collective-permute-start | bytes 149000 | tf_op jit(solution)/shard_map/ppermute | solution.py:105
  6.8 13.4 %collective-permute-start.4 = (bf16[97,256]{1,0:T(8,128)(2,1)S(1)}, bf16[97,256]{1,0:T(8,128)(2,1)}, u32[]{:S(2)}, u32[]{:S(2)}) collective-permute-start(bf16[97,256]{1,0:T(8,128)(2,1)S(1)} %constant_dynamic-update-slice_fusion), channel_id=1, source_target_pairs={{0,2},{1,3},{2,0},{3,1},{4,6},{5,7},{6,4},{7,5},{8,10},{9,11},{10,... | collective-permute-start | bytes 149000 | tf_op jit(solution)/shard_map/ppermute | solution.py:105
  9.4 10.8 %collective-permute-start.3 = (bf16[97,256]{1,0:T(8,128)(2,1)S(1)}, bf16[97,256]{1,0:T(8,128)(2,1)}, u32[]{:S(2)}, u32[]{:S(2)}) collective-permute-start(bf16[97,256]{1,0:T(8,128)(2,1)S(1)} %constant_dynamic-update-slice_fusion), channel_id=1, source_target_pairs={{0,3},{1,0},{2,1},{3,2},{4,7},{5,4},{6,5},{7,6},{8,11},{9,8},{10,9... | collective-permute-start | bytes 149000 | tf_op jit(solution)/shard_map/ppermute | solution.py:105
  13.4 1.7 %copy-start.19 = (f32[128]{0:T(128)}, f32[128]{0:T(128)S(1)}, u32[]{:S(2)}) copy-start(f32[128]{0:T(128)S(1)} %get-tuple-element.37) | copy-start | bytes 1540
  16.0 9.9 %collective-permute-start.2 = (f32[48,1024]{1,0:T(8,128)}, f32[48,1024]{1,0:T(8,128)S(1)}, u32[]{:S(2)}, u32[]{:S(2)}) collective-permute-start(f32[48,1024]{1,0:T(8,128)} %get-tuple-element.27), channel_id=1, source_target_pairs={{0,1},{1,2},{2,3},{3,0},{4,5},{5,6},{6,7},{7,4},{8,9},{9,10},{10,1... | collective-permute-start | bytes 589832 | tf_op jit(solution)/shard_map/ppermute | solution.py:121
  16.6 15.8 %collective-permute-start.1 = (f32[48,1024]{1,0:T(8,128)S(1)}, f32[48,1024]{1,0:T(8,128)S(1)}, u32[]{:S(2)}, u32[]{:S(2)}) collective-permute-start(f32[48,1024]{1,0:T(8,128)S(1)} %get-tuple-element.28), channel_id=1, source_target_pairs={{0,2},{1,3},{2,0},{3,1},{4,6},{5,7},{6,4},{7,5},{8,10},{9,11},{10,... | collective-permute-start | bytes 589832 | tf_op jit(solution)/shard_map/ppermute | solution.py:121
  17.0 31.7 %copy-start.4 = (pred[8]{0:T(512)(128)(4,1)}, pred[8]{0:T(512)(128)(4,1)S(1)}, u32[]{:S(2)}) copy-start(pred[8]{0:T(512)(128)(4,1)S(1)} %get-tuple-element.43) | copy-start | bytes 28
  17.0 31.7 %copy-start.6 = (pred[8]{0:T(512)(128)(4,1)}, pred[8]{0:T(512)(128)(4,1)S(1)}, u32[]{:S(2)}) copy-start(pred[8]{0:T(512)(128)(4,1)S(1)} %get-tuple-element.44) | copy-start | bytes 28
  17.1 31.6 %copy-start.8 = (pred[8]{0:T(512)(128)(4,1)}, pred[8]{0:T(512)(128)(4,1)S(1)}, u32[]{:S(2)}) copy-start(pred[8]{0:T(512)(128)(4,1)S(1)} %get-tuple-element.45) | copy-start | bytes 28
  17.1 31.6 %copy-start.10 = (pred[8]{0:T(512)(128)(4,1)}, pred[8]{0:T(512)(128)(4,1)S(1)}, u32[]{:S(2)}) copy-start(pred[8]{0:T(512)(128)(4,1)S(1)} %get-tuple-element.46) | copy-start | bytes 28
  17.1 31.6 %copy-start.12 = (pred[8]{0:T(512)(128)(4,1)}, pred[8]{0:T(512)(128)(4,1)S(1)}, u32[]{:S(2)}) copy-start(pred[8]{0:T(512)(128)(4,1)S(1)} %get-tuple-element.47) | copy-start | bytes 28
  17.1 31.6 %copy-start.14 = (pred[8]{0:T(512)(128)(4,1)}, pred[8]{0:T(512)(128)(4,1)S(1)}, u32[]{:S(2)}) copy-start(pred[8]{0:T(512)(128)(4,1)S(1)} %get-tuple-element.48) | copy-start | bytes 28
  17.1 31.6 %copy-start.16 = (pred[8]{0:T(512)(128)(4,1)}, pred[8]{0:T(512)(128)(4,1)S(1)}, u32[]{:S(2)}) copy-start(pred[8]{0:T(512)(128)(4,1)S(1)} %broadcast_compare_fusion.6) | copy-start | bytes 28
  17.3 16.7 %collective-permute-start = (f32[48,1024]{1,0:T(8,128)S(1)}, f32[48,1024]{1,0:T(8,128)S(1)}, u32[]{:S(2)}, u32[]{:S(2)}) collective-permute-start(f32[48,1024]{1,0:T(8,128)S(1)} %get-tuple-element.25), channel_id=1, source_target_pairs={{0,3},{1,0},{2,1},{3,2},{4,7},{5,4},{6,5},{7,6},{8,11},{9,8},{10,9... | collective-permute-start | bytes 589832 | tf_op jit(solution)/shard_map/ppermute | solution.py:121
  21.3 13.5 %collective-permute-start.15 = (bf16[4,97,256]{2,0,1:T(4,128)(2,1)S(1)}, bf16[4,97,256]{2,0,1:T(4,128)(2,1)S(1)}, u32[]{:S(2)}, u32[]{:S(2)}) collective-permute-start(bf16[4,97,256]{2,0,1:T(4,128)(2,1)S(1)} %select_select_fusion.3), channel_id=1, source_target_pairs={{0,4},{4,8},{8,12},{12,16},{16,20},{20,24},{24,28},{28,0},{1,5},{5... | collective-permute-start | bytes 595976 | tf_op jit(solution)/shard_map/ppermute | solution.py:105
  21.3 14.9 %collective-permute-start.14 = (bf16[4,97,256]{2,0,1:T(4,128)(2,1)S(1)}, bf16[4,97,256]{2,0,1:T(4,128)(2,1)S(1)}, u32[]{:S(2)}, u32[]{:S(2)}) collective-permute-start(bf16[4,97,256]{2,0,1:T(4,128)(2,1)S(1)} %select_select_fusion.3), channel_id=1, source_target_pairs={{0,8},{4,12},{8,16},{12,20},{16,24},{20,28},{24,0},{28,4},{1,9},{5... | collective-permute-start | bytes 595976 | tf_op jit(solution)/shard_map/ppermute | solution.py:105
  25.9 12.8 %collective-permute-start.13 = (bf16[4,97,256]{2,0,1:T(4,128)(2,1)S(1)}, bf16[4,97,256]{2,0,1:T(4,128)(2,1)S(1)}, u32[]{:S(2)}, u32[]{:S(2)}) collective-permute-start(bf16[4,97,256]{2,0,1:T(4,128)(2,1)S(1)} %select_select_fusion.3), channel_id=1, source_target_pairs={{0,12},{4,16},{8,20},{12,24},{16,28},{20,0},{24,4},{28,8},{1,13},{... | collective-permute-start | bytes 595976 | tf_op jit(solution)/shard_map/ppermute | solution.py:105
  32.4 8.8 %collective-permute-start.12 = (bf16[4,97,256]{2,0,1:T(4,128)(2,1)S(1)}, bf16[4,97,256]{2,0,1:T(4,128)(2,1)S(1)}, u32[]{:S(2)}, u32[]{:S(2)}) collective-permute-start(bf16[4,97,256]{2,0,1:T(4,128)(2,1)S(1)} %select_select_fusion.3), channel_id=1, source_target_pairs={{0,16},{4,20},{8,24},{12,28},{16,0},{20,4},{24,8},{28,12},{1,17},{... | collective-permute-start | bytes 595976 | tf_op jit(solution)/shard_map/ppermute | solution.py:105
  33.9 9.0 %collective-permute-start.11 = (bf16[4,97,256]{2,0,1:T(4,128)(2,1)S(1)}, bf16[4,97,256]{2,0,1:T(4,128)(2,1)S(1)}, u32[]{:S(2)}, u32[]{:S(2)}) collective-permute-start(bf16[4,97,256]{2,0,1:T(4,128)(2,1)S(1)} %select_select_fusion.3), channel_id=1, source_target_pairs={{0,20},{4,24},{8,28},{12,0},{16,4},{20,8},{24,12},{28,16},{1,21},{... | collective-permute-start | bytes 595976 | tf_op jit(solution)/shard_map/ppermute | solution.py:105
  34.8 9.2 %collective-permute-start.10 = (bf16[4,97,256]{2,0,1:T(4,128)(2,1)S(1)}, bf16[4,97,256]{2,0,1:T(4,128)(2,1)S(1)}, u32[]{:S(2)}, u32[]{:S(2)}) collective-permute-start(bf16[4,97,256]{2,0,1:T(4,128)(2,1)S(1)} %select_select_fusion.3), channel_id=1, source_target_pairs={{0,24},{4,28},{8,0},{12,4},{16,8},{20,12},{24,16},{28,20},{1,25},{... | collective-permute-start | bytes 595976 | tf_op jit(solution)/shard_map/ppermute | solution.py:105
  36.2 8.2 %collective-permute-start.9 = (bf16[4,97,256]{2,0,1:T(4,128)(2,1)S(1)}, bf16[4,97,256]{2,0,1:T(4,128)(2,1)S(1)}, u32[]{:S(2)}, u32[]{:S(2)}) collective-permute-start(bf16[4,97,256]{2,0,1:T(4,128)(2,1)S(1)} %select_select_fusion.3), channel_id=1, source_target_pairs={{0,28},{4,0},{8,4},{12,8},{16,12},{20,16},{24,20},{28,24},{1,29},{... | collective-permute-start | bytes 595976 | tf_op jit(solution)/shard_map/ppermute | solution.py:105
  38.8 10.0 %collective-permute-start.8 = (bf16[48,1024]{1,0:T(8,128)(2,1)S(1)}, bf16[48,1024]{1,0:T(8,128)(2,1)S(1)}, u32[]{:S(2)}, u32[]{:S(2)}) collective-permute-start(bf16[48,1024]{1,0:T(8,128)(2,1)S(1)} %divide_convert_fusion), channel_id=1, source_target_pairs={{0,1},{1,2},{2,3},{3,0},{4,5},{5,6},{6,7},{7,4},{8,9},{9,10},{10,1... | collective-permute-start | bytes 294920 | tf_op jit(solution)/shard_map/ppermute | solution.py:105
  41.2 8.0 %collective-permute-start.7 = (bf16[48,1024]{1,0:T(8,128)(2,1)S(1)}, bf16[48,1024]{1,0:T(8,128)(2,1)S(1)}, u32[]{:S(2)}, u32[]{:S(2)}) collective-permute-start(bf16[48,1024]{1,0:T(8,128)(2,1)S(1)} %divide_convert_fusion), channel_id=1, source_target_pairs={{0,2},{1,3},{2,0},{3,1},{4,6},{5,7},{6,4},{7,5},{8,10},{9,11},{10,... | collective-permute-start | bytes 294920 | tf_op jit(solution)/shard_map/ppermute | solution.py:105
  43.0 7.0 %collective-permute-start.6 = (bf16[48,1024]{1,0:T(8,128)(2,1)S(1)}, bf16[48,1024]{1,0:T(8,128)(2,1)S(1)}, u32[]{:S(2)}, u32[]{:S(2)}) collective-permute-start(bf16[48,1024]{1,0:T(8,128)(2,1)S(1)} %divide_convert_fusion), channel_id=1, source_target_pairs={{0,3},{1,0},{2,1},{3,2},{4,7},{5,4},{6,5},{7,6},{8,11},{9,8},{10,9... | collective-permute-start | bytes 294920 | tf_op jit(solution)/shard_map/ppermute | solution.py:105
  55.4 0.7 copy-start.3
  56.7 38.8 %copy-start.2 = (f32[384,1024]{1,0:T(8,128)}, f32[384,1024]{1,0:T(8,128)S(1)}, u32[]{:S(2)}) copy-start(f32[384,1024]{1,0:T(8,128)S(1)} %convolution_multiply_fusion) | copy-start | bytes 4718596
  56.7 19.8 %copy-start.1 = (bf16[128,4096]{1,0:T(8,128)(2,1)S(1)}, bf16[128,4096]{1,0:T(8,128)(2,1)}, u32[]{:S(2)}) copy-start(bf16[128,4096]{1,0:T(8,128)(2,1)} %param.10) | copy-start | bytes 3145732
  56.8 19.8 %copy-start.20 = (f32[128]{0:T(128)S(1)}, f32[128]{0:T(128)}, u32[]{:S(2)}) copy-start(f32[128]{0:T(128)} %copy-done.19) | copy-start | bytes 1540
  56.8 19.7 %copy-start.21 = (s32[1,128]{1,0:T(1,128)S(1)}, s32[1,128]{1,0:T(1,128)}, u32[]{:S(2)}) copy-start(s32[1,128]{1,0:T(1,128)} %param.11) | copy-start | bytes 1540
  78.2 12.4 %copy-start.18 = (f32[128]{0:T(128)S(1)}, f32[128]{0:T(128)}, u32[]{:S(2)}) copy-start(f32[128]{0:T(128)} %get-tuple-element.36) | copy-start | bytes 1540
  79.1 13.1 %collective-permute-start.22 = (f32[28672]{0:T(1024)S(1)}, f32[28672]{0:T(1024)S(1)}, u32[]{:S(2)}, u32[]{:S(2)}) collective-permute-start(f32[28672]{0:T(1024)S(1)} %get-tuple-element.35), channel_id=1, source_target_pairs={{0,4},{4,8},{8,12},{12,16},{16,20},{20,24},{24,28},{28,0},{1,5},{5... | collective-permute-start | bytes 344072 | tf_op jit(solution)/shard_map/ppermute | solution.py:134
  79.2 14.2 %collective-permute-start.21 = (f32[28672]{0:T(1024)S(1)}, f32[28672]{0:T(1024)S(1)}, u32[]{:S(2)}, u32[]{:S(2)}) collective-permute-start(f32[28672]{0:T(1024)S(1)} %get-tuple-element.34), channel_id=1, source_target_pairs={{0,8},{4,12},{8,16},{12,20},{16,24},{20,28},{24,0},{28,4},{1,9},{5... | collective-permute-start | bytes 344072 | tf_op jit(solution)/shard_map/ppermute | solution.py:134
  87.2 11.4 %collective-permute-start.20 = (f32[28672]{0:T(1024)S(1)}, f32[28672]{0:T(1024)S(1)}, u32[]{:S(2)}, u32[]{:S(2)}) collective-permute-start(f32[28672]{0:T(1024)S(1)} %get-tuple-element.33), channel_id=1, source_target_pairs={{0,12},{4,16},{8,20},{12,24},{16,28},{20,0},{24,4},{28,8},{1,13},{... | collective-permute-start | bytes 344072 | tf_op jit(solution)/shard_map/ppermute | solution.py:134
  89.9 8.7 %collective-permute-start.19 = (f32[28672]{0:T(1024)S(1)}, f32[28672]{0:T(1024)S(1)}, u32[]{:S(2)}, u32[]{:S(2)}) collective-permute-start(f32[28672]{0:T(1024)S(1)} %get-tuple-element.32), channel_id=1, source_target_pairs={{0,16},{4,20},{8,24},{12,28},{16,0},{20,4},{24,8},{28,12},{1,17},{... | collective-permute-start | bytes 344072 | tf_op jit(solution)/shard_map/ppermute | solution.py:134
  90.1 8.6 %collective-permute-start.18 = (f32[28672]{0:T(1024)S(1)}, f32[28672]{0:T(1024)S(1)}, u32[]{:S(2)}, u32[]{:S(2)}) collective-permute-start(f32[28672]{0:T(1024)S(1)} %get-tuple-element.31), channel_id=1, source_target_pairs={{0,20},{4,24},{8,28},{12,0},{16,4},{20,8},{24,12},{28,16},{1,21},{... | collective-permute-start | bytes 344072 | tf_op jit(solution)/shard_map/ppermute | solution.py:134
  90.5 8.9 %copy-start.5 = (pred[8]{0:T(512)(128)(4,1)S(1)}, pred[8]{0:T(512)(128)(4,1)}, u32[]{:S(2)}) copy-start(pred[8]{0:T(512)(128)(4,1)} %copy-done.4) | copy-start | bytes 28
  90.5 8.9 %copy-start.7 = (pred[8]{0:T(512)(128)(4,1)S(1)}, pred[8]{0:T(512)(128)(4,1)}, u32[]{:S(2)}) copy-start(pred[8]{0:T(512)(128)(4,1)} %copy-done.6) | copy-start | bytes 28
  90.5 8.9 %copy-start.9 = (pred[8]{0:T(512)(128)(4,1)S(1)}, pred[8]{0:T(512)(128)(4,1)}, u32[]{:S(2)}) copy-start(pred[8]{0:T(512)(128)(4,1)} %copy-done.8) | copy-start | bytes 28
  90.6 8.9 %copy-start.11 = (pred[8]{0:T(512)(128)(4,1)S(1)}, pred[8]{0:T(512)(128)(4,1)}, u32[]{:S(2)}) copy-start(pred[8]{0:T(512)(128)(4,1)} %copy-done.10) | copy-start | bytes 28
  90.6 8.9 %copy-start.13 = (pred[8]{0:T(512)(128)(4,1)S(1)}, pred[8]{0:T(512)(128)(4,1)}, u32[]{:S(2)}) copy-start(pred[8]{0:T(512)(128)(4,1)} %copy-done.12) | copy-start | bytes 28
  90.6 8.9 %copy-start.15 = (pred[8]{0:T(512)(128)(4,1)S(1)}, pred[8]{0:T(512)(128)(4,1)}, u32[]{:S(2)}) copy-start(pred[8]{0:T(512)(128)(4,1)} %copy-done.14) | copy-start | bytes 28
  90.6 8.9 %copy-start.17 = (pred[8]{0:T(512)(128)(4,1)S(1)}, pred[8]{0:T(512)(128)(4,1)}, u32[]{:S(2)}) copy-start(pred[8]{0:T(512)(128)(4,1)} %copy-done.16) | copy-start | bytes 28
  92.2 6.5 %collective-permute-start.17 = (f32[28672]{0:T(1024)S(1)}, f32[28672]{0:T(1024)S(1)}, u32[]{:S(2)}, u32[]{:S(2)}) collective-permute-start(f32[28672]{0:T(1024)S(1)} %get-tuple-element.30), channel_id=1, source_target_pairs={{0,24},{4,28},{8,0},{12,4},{16,8},{20,12},{24,16},{28,20},{1,25},{... | collective-permute-start | bytes 344072 | tf_op jit(solution)/shard_map/ppermute | solution.py:134
  93.4 5.3 %collective-permute-start.16 = (f32[28672]{0:T(1024)S(1)}, f32[28672]{0:T(1024)}, u32[]{:S(2)}, u32[]{:S(2)}) collective-permute-start(f32[28672]{0:T(1024)S(1)} %get-tuple-element.29), channel_id=1, source_target_pairs={{0,28},{4,0},{8,4},{12,8},{16,12},{20,16},{24,20},{28,24},{1,29},{... | collective-permute-start | bytes 344072 | tf_op jit(solution)/shard_map/ppermute | solution.py:134
  99.6 7.6 %collective-permute-start.25 = (f32[4096]{0:T(1024)S(1)}, f32[4096]{0:T(1024)S(1)}, u32[]{:S(2)}, u32[]{:S(2)}) collective-permute-start(f32[4096]{0:T(1024)S(1)} %select_reduce_fusion.2), channel_id=1, source_target_pairs={{0,1},{1,2},{2,3},{3,0},{4,5},{5,6},{6,7},{7,4},{8,9},{9,10},{10,1... | collective-permute-start | bytes 49160 | tf_op jit(solution)/shard_map/ppermute | solution.py:105
  99.7 7.5 %collective-permute-start.24 = (f32[4096]{0:T(1024)S(1)}, f32[4096]{0:T(1024)S(1)}, u32[]{:S(2)}, u32[]{:S(2)}) collective-permute-start(f32[4096]{0:T(1024)S(1)} %select_reduce_fusion.2), channel_id=1, source_target_pairs={{0,2},{1,3},{2,0},{3,1},{4,6},{5,7},{6,4},{7,5},{8,10},{9,11},{10,... | collective-permute-start | bytes 49160 | tf_op jit(solution)/shard_map/ppermute | solution.py:105
  102.0 5.3 %collective-permute-start.23 = (f32[4096]{0:T(1024)S(1)}, f32[4096]{0:T(1024)S(1)}, u32[]{:S(2)}, u32[]{:S(2)}) collective-permute-start(f32[4096]{0:T(1024)S(1)} %select_reduce_fusion.2), channel_id=1, source_target_pairs={{0,3},{1,0},{2,1},{3,2},{4,7},{5,4},{6,5},{7,6},{8,11},{9,8},{10,9... | collective-permute-start | bytes 49160 | tf_op jit(solution)/shard_map/ppermute | solution.py:105
